TPU v7x, 32 devices: a whole 2x2x4 slice. The times are simulated.
32 devices in a mesh: seq: 8 (over z, y), batch: 4 (over x, core).
Axes of the slice: x: 2, y: 2, z: 4, core: 2. Of those that a mesh axis runs over, the one named last changes fastest.
Arguments:
- query_rows: bfloat16 [8192, 2048], P(('batch', 'seq')), parts along dimension 0, may hold values from -6 to 6
- key_rows: bfloat16 [8192, 2048], P(('batch', 'seq')), parts along dimension 0, may hold values from -6 to 6
- value_rows: bfloat16 [8192, 2048], P(('batch', 'seq')), parts along dimension 0, may hold values from -6 to 6
- out_grad: bfloat16 [8192, 2048], P(('batch', 'seq')), parts along dimension 0, may hold values from -6 to 6
Outputs:
- attended: bfloat16 [8192, 2048], P(('batch', 'seq')), parts along dimension 0
- query_grad: bfloat16 [8192, 2048], P(('batch', 'seq')), parts along dimension 0
- key_grad: bfloat16 [8192, 2048], P(('batch', 'seq')), parts along dimension 0
- value_grad: bfloat16 [8192, 2048], P(('batch', 'seq')), parts along dimension 0
There are 4 independent parts, one for each index of `batch`. A program takes and returns all parts, laid end to end along the dimension named above; each array names one. Nothing has to cross between parts.
All inputs are finite; a program needn't handle non-finite values.
Results may differ from a plain program's by a relative error of at most 0.025.
Values may be sent and summed in bfloat16 or wider, within the bound.
No kernel may reach another device: no remote copies, remote signals or barrier semaphores. Data moves between devices by JAX's collectives and lax.ppermute only.
A program may use at most 128 MiB of HBM per device.

v0:
```python
import math

import jax
import jax.numpy as jnp
from jax import lax
from jax.sharding import PartitionSpec as P

HEAD_DIM = 128
POOLED = 128
HGROUP = 4


def partner_2(block, axis, stride):
    count = lax.axis_size(axis)
    route = []
    for low in range(count):
        high = low | 1 << stride
        if high != low and high < count:
            route += [(low, high), (high, low)]
    return lax.ppermute(block, axis, route)


def combine_halves(mine, other, bit_level, position):
    upper_bit = position // 2**bit_level % 2 == 1
    lower_half = jnp.where(upper_bit, other, mine)
    upper_half = jnp.where(upper_bit, mine, other)
    joined = jnp.concatenate((lower_half, upper_half), axis=1)
    return jnp.mean(joined.reshape(mine.shape[0], mine.shape[1], 2, mine.shape[2]), axis=2)


def head_group(query_part, grad_part, key_part, value_part, key_bias, near_last, score_scale):
    leaf_rows = query_part.shape[0]
    key_count = key_part.shape[0]
    group_heads = query_part.shape[1] // HEAD_DIM
    far_first = 2 * leaf_rows
    query_heads = query_part.reshape(leaf_rows, group_heads, HEAD_DIM)
    grad_heads = grad_part.reshape(leaf_rows, group_heads, HEAD_DIM)
    key_heads = key_part.reshape(key_count, group_heads, HEAD_DIM)
    value_heads = value_part.reshape(key_count, group_heads, HEAD_DIM)
    scores = (
        jnp.einsum("qhd,khd->hqk", query_heads, key_heads, preferred_element_type=jnp.float32)
        * score_scale
        + key_bias
    )
    row_max = jnp.max(scores, axis=-1, keepdims=True)
    log_total = row_max + jnp.log(jnp.sum(jnp.exp(scores - row_max), axis=-1, keepdims=True))
    weights = jnp.exp(scores - log_total)
    weights_low = weights.astype(jnp.bfloat16)
    attended = jnp.einsum(
        "hqk,khd->qhd", weights_low, value_heads, preferred_element_type=jnp.float32
    ).astype(jnp.bfloat16)
    row_dot = jnp.einsum("qhd,qhd->hq", grad_heads, attended, preferred_element_type=jnp.float32)[
        ..., None
    ]
    weight_grad = jnp.einsum(
        "qhd,khd->hqk", grad_heads, value_heads, preferred_element_type=jnp.float32
    )
    score_grad = (weights * (weight_grad - row_dot)).astype(jnp.bfloat16)
    query_grad = (
        jnp.einsum("hqk,khd->qhd", score_grad, key_heads, preferred_element_type=jnp.float32)
        * score_scale
    ).astype(jnp.bfloat16)
    key_all = (
        jnp.einsum("hqk,qhd->khd", score_grad, query_heads, preferred_element_type=jnp.float32)
        * score_scale
    )
    value_all = jnp.einsum(
        "hqk,qhd->khd", weights_low, grad_heads, preferred_element_type=jnp.float32
    )
    far_count = key_count - far_first
    return (
        attended.reshape(leaf_rows, -1),
        query_grad.reshape(leaf_rows, -1),
        key_all[:near_last].reshape(near_last, -1),
        key_all[far_first:].reshape(far_count, -1),
        value_all[:near_last].reshape(near_last, -1),
        value_all[far_first:].reshape(far_count, -1),
        log_total[..., 0],
        row_dot[..., 0],
    )


def body(query_rows, key_rows, value_rows, out_grad):
    leaf_rows = query_rows.shape[0]
    model_width = query_rows.shape[1]
    seq_count = lax.axis_size("seq")
    levels = seq_count.bit_length() - 1
    position = lax.axis_index("seq")
    pool_ratio = leaf_rows // POOLED
    head_count = model_width // HEAD_DIM
    group_width = HGROUP * HEAD_DIM
    score_scale = HEAD_DIM ** (-0.5)
    paired = jnp.stack((key_rows, value_rows))
    sibling = partner_2(paired, "seq", 0)
    own_summary = jnp.mean(
        paired.reshape(2, POOLED, pool_ratio, model_width), axis=2, dtype=jnp.float32
    )
    sibling_summary = jnp.mean(
        sibling.reshape(2, POOLED, pool_ratio, model_width), axis=2, dtype=jnp.float32
    )
    summary = combine_halves(own_summary, sibling_summary, 0, position)
    far_parts = []
    for step_level in range(1, levels):
        partner = partner_2(summary.astype(jnp.bfloat16), "seq", step_level).astype(summary.dtype)
        far_parts.append(partner)
        if step_level + 1 < levels:
            summary = combine_halves(summary, partner, step_level, position)
    far_rows = jnp.concatenate(far_parts, axis=1).astype(jnp.bfloat16)
    all_keys = jnp.concatenate((key_rows, sibling[0], far_rows[0]), axis=0)
    all_values = jnp.concatenate((value_rows, sibling[1], far_rows[1]), axis=0)
    bias_parts = [jnp.zeros((2 * leaf_rows,), jnp.float32)]
    for step_level in range(1, levels):
        bias_parts.append(jnp.full((POOLED,), math.log(pool_ratio * 2**step_level), jnp.float32))
    key_bias = jnp.concatenate(bias_parts, axis=0)
    near_last = 2 * leaf_rows
    outputs = [[], [], [], [], [], [], [], []]
    for group_index in range(head_count // HGROUP):
        columns = slice(group_index * group_width, (group_index + 1) * group_width)
        results = head_group(
            query_rows[:, columns],
            out_grad[:, columns],
            all_keys[:, columns],
            all_values[:, columns],
            key_bias,
            near_last,
            score_scale,
        )
        for slot_index in range(8):
            outputs[slot_index].append(results[slot_index])
    attended = jnp.concatenate(outputs[0], axis=1)
    query_grad = jnp.concatenate(outputs[1], axis=1)
    near_key = jnp.concatenate(outputs[2], axis=1)
    far_key = jnp.concatenate(outputs[3], axis=1)
    near_value = jnp.concatenate(outputs[4], axis=1)
    far_value = jnp.concatenate(outputs[5], axis=1)
    to_sibling = jnp.stack((near_key[leaf_rows:], near_value[leaf_rows:])).astype(jnp.bfloat16)
    from_sibling = partner_2(to_sibling, "seq", 0)
    own_terms = jnp.stack((near_key[:leaf_rows], near_value[:leaf_rows]))
    near_total = own_terms + from_sibling.astype(jnp.float32)
    far_grads = jnp.stack((far_key, far_value)).reshape(2, levels - 1, POOLED, model_width)
    summary_grad = jnp.zeros((2, POOLED, model_width), jnp.float32)
    for step_level in reversed(range(levels)):
        spread = jnp.broadcast_to(
            0.5 * summary_grad[:, :, None, :], (2, POOLED, 2, model_width)
        ).reshape(2, 2 * POOLED, model_width)
        upper_bit = position // 2**step_level % 2 == 1
        lower_half = spread[:, :POOLED]
        upper_half = spread[:, POOLED:]
        own_share = jnp.where(upper_bit, upper_half, lower_half)
        other_share = jnp.where(upper_bit, lower_half, upper_half)
        outgoing = other_share + far_grads[:, step_level - 1] if step_level >= 1 else other_share
        returned = partner_2(outgoing.astype(jnp.bfloat16), "seq", step_level).astype(
            outgoing.dtype
        )
        summary_grad = own_share + returned
    far_tokens = jnp.broadcast_to(
        summary_grad[:, :, None, :] / pool_ratio, (2, POOLED, pool_ratio, model_width)
    ).reshape(2, leaf_rows, model_width)
    grads_total = near_total + far_tokens
    return (
        attended,
        query_grad,
        grads_total[0].astype(jnp.bfloat16),
        grads_total[1].astype(jnp.bfloat16),
    )


def solution(mesh):
    return jax.shard_map(
        body,
        mesh=mesh,
        in_specs=(
            P(("batch", "seq"), None),
            P(("batch", "seq"), None),
            P(("batch", "seq"), None),
            P(("batch", "seq"), None),
        ),
        out_specs=(
            P(("batch", "seq"), None),
            P(("batch", "seq"), None),
            P(("batch", "seq"), None),
            P(("batch", "seq"), None),
        ),
        check_vma=False,
    )
```

profile of v0, /device:TPU:0, one launch (start us, length us, event | category | flops | bytes accessed | tf_op | source)
XLA Modules:
  0.0 417.8 jit_solution(5383415935953819843)
XLA Ops:
  0.7 3.2 pad_maximum_fusion.6
  3.9 3.0 collective-permute-start
  9.8 7.3 %convert_reduce_fusion = f32[2,128,2048]{2,1,0:T(8,128)S(1)} fusion(bf16[1,128,2,2048]{3,2,1,0:T(2,128)(2,1)} %stack.45, bf16[1,128,2,2048]{3,2,1,0:T(2,128)(2,1)} %stack.44), kind=kLoop, calls=%fused_computation.11 | loop fusion | flops 2621440 | bytes 4194304 | tf_op jit(solution)/shard_map/reduce_sum | solution.py:95
  17.1 35.7 %collective-permute-done = bf16[2,256,2048]{2,1,0:T(8,128)(2,1)} collective-permute-done((bf16[2,256,2048]{2,1,0:T(8,128)(2,1)}, bf16[2,256,2048]{2,1,0:T(8,128)(2,1)}, u32[]{:S(2)}, u32[]{:S(2)}) %collective-permute-start) | collective-permute-done | bytes 2097184 | tf_op jit(solution)/shard_map/ppermute | solution.py:20
  54.9 4.9 %bitcast_reduce_fusion.2 = f32[2,128,2048]{2,0,1:T(2,128)S(1)} fusion(f32[2,256,2048]{2,1,0:T(8,128)S(1)} %convert_element_type.162), kind=kLoop, calls=%fused_computation.10 | loop fusion | flops 524288 | bytes 6291456 | tf_op jit(solution)/shard_map/reduce_sum | solution.py:98
  59.8 4.0 broadcast_select_fusion.1
  63.8 3.9 bitcast_reduce_fusion.1
  71.6 22.9 %collective-permute-done.1 = bf16[2,128,2048]{2,0,1:T(2,128)(2,1)} collective-permute-done((bf16[2,128,2048]{2,0,1:T(2,128)(2,1)}, bf16[2,128,2048]{2,0,1:T(2,128)(2,1)}, u32[]{:S(2)}, u32[]{:S(2)}) %collective-permute-start.1) | collective-permute-done | bytes 1048608 | tf_op jit(solution)/shard_map/ppermute | solution.py:20
  94.4 3.6 convert_select_fusion.1
  98.0 4.2 %bitcast_reduce_fusion = f32[2,128,2048]{2,0,1:T(2,128)S(1)} fusion(f32[2,128,2048]{2,0,1:T(2,128)S(1)} %get-tuple-element.22, f32[2,128,2048]{2,0,1:T(2,128)S(1)} %get-tuple-element.21), kind=kLoop, calls=%fused_computation.8 | loop fusion | flops 1572864 | bytes 6291456 | tf_op jit(solution)/shard_map/reduce_sum | solution.py:28
  102.2 12.0 %multiply_convert_fusion = bf16[2,128,2048]{2,0,1:T(2,128)(2,1)S(1)} fusion(f32[2,128,2048]{2,0,1:T(2,128)S(1)} %bitcast_reduce_fusion), kind=kLoop, calls=%fused_computation.71 | loop fusion | flops 1048576 | bytes 3145728 | tf_op jit(solution)/shard_map/convert_element_type | solution.py:104
  127.8 2.8 slice_bitcast_fusion.5
  132.6 28.6 %collective-permute-done.2 = bf16[2,128,2048]{2,0,1:T(2,128)(2,1)} collective-permute-done((bf16[2,128,2048]{2,0,1:T(2,128)(2,1)S(1)}, bf16[2,128,2048]{2,0,1:T(2,128)(2,1)}, u32[]{:S(2)}, u32[]{:S(2)}) %collective-permute-start.2) | collective-permute-done | bytes 1048608 | tf_op jit(solution)/shard_map/ppermute | solution.py:20
  163.2 3.0 fusion.45
  172.9 2.6 copy.375
  182.6 2.7 fusion.48
  186.5 3.5 fusion.16
  198.9 4.6 %fusion.13 = (f32[4,256]{1,0:T(4,128)S(1)}, f32[4,256]{1,0:T(4,128)S(1)}, f32[4,256]{1,0:T(4,128)S(1)}) fusion(f32[4,768,256]{2,1,0:T(8,128)} %get-tuple-element.39, f32[4,256]{1,0:T(4,128)S(1)} %get-tuple-element.5, f32[768]{0:T(1024)S(1)} %copy-done.56, f32[4,256]{1,0:T(4,128)S(1)} %get-tuple-element.6, f32[4,768,256]{2,1,0:T(8,128)S(1)} %fusion.48, ...), kind=kLoop, calls=%fused_computation.38 | loop fusion | flops 9434112 | bytes 9464832 | tf_op jit(solution)/shard_map/reduce_sum | solution.py:46
  213.3 3.9 fusion.33
  225.6 2.8 fusion.32
  246.3 2.6 copy.423
  253.1 2.6 copy.421
  264.8 6.4 %maximum_maximum_fusion = f32[2,2,128,2048]{3,0,2,1:T(2,128)S(1)} fusion(f32[1,2,128,512]{3,0,2,1:T(1,128)} %bitcast.311, f32[1,2,128,512]{3,0,2,1:T(1,128)} %bitcast.315, f32[1,2,128,512]{3,0,2,1:T(1,128)} %bitcast.313, f32[1,2,128,512]{3,0,2,1:T(1,128)} %bitcast.309, f32[1,2,128,512]{3,0,2,1:T(1,128)} %bitcast.310, f32[1,2,128,512]{3,0,2,1:T(1,128)S(1)} %bitcast.314, ...), kind=kLoop, calls=%fused_computation.7 | loop fusion | flops 7340032 | bytes 8388608 | tf_op jit(solution)/shard_map/stack | solution.py:140
  275.4 44.6 %collective-permute-done.4 = bf16[2,128,2048]{2,0,1:T(2,128)(2,1)S(1)} collective-permute-done((bf16[2,128,2048]{2,0,1:T(2,128)(2,1)S(1)}, bf16[2,128,2048]{2,0,1:T(2,128)(2,1)S(1)}, u32[]{:S(2)}, u32[]{:S(2)}) %collective-permute-start.4) | collective-permute-done | bytes 1048608 | tf_op jit(solution)/shard_map/ppermute | solution.py:20
  321.2 2.6 broadcast_in_dim.6
  323.9 2.8 fusion.23
  331.4 19.3 %collective-permute-done.5 = bf16[2,128,2048]{2,0,1:T(2,128)(2,1)S(1)} collective-permute-done((bf16[2,128,2048]{2,0,1:T(2,128)(2,1)S(1)}, bf16[2,128,2048]{2,0,1:T(2,128)(2,1)S(1)}, u32[]{:S(2)}, u32[]{:S(2)}) %collective-permute-start.5) | collective-permute-done | bytes 1048608 | tf_op jit(solution)/shard_map/ppermute | solution.py:20
  353.0 2.6 broadcast_in_dim.7
  358.5 39.1 %collective-permute-done.6 = bf16[2,128,2048]{2,0,1:T(2,128)(2,1)S(1)} collective-permute-done((bf16[2,128,2048]{2,0,1:T(2,128)(2,1)S(1)}, bf16[2,128,2048]{2,0,1:T(2,128)(2,1)S(1)}, u32[]{:S(2)}, u32[]{:S(2)}) %collective-permute-start.6) | collective-permute-done | bytes 1048608 | tf_op jit(solution)/shard_map/ppermute | solution.py:20
  401.0 4.4 %broadcast_in_dim.8 = f32[2,128,2,2048]{3,2,1,0:T(2,128)} broadcast(f32[2,128,2048]{2,1,0:T(8,128)S(1)} %copy.440), dimensions={0,1,3} | broadcast | bytes 6291456 | tf_op jit(solution)/shard_map/broadcast_in_dim | solution.py:156
  405.4 6.0 %reshape.241 = f32[2,256,2048]{2,1,0:T(8,128)} reshape(f32[2,128,2,2048]{3,2,1,0:T(2,128)} %broadcast_in_dim.8) | data formatting | bytes 8388608 | tf_op jit(solution)/shard_map/reshape | solution.py:158
  411.4 4.6 %fusion.1 = bf16[2,256,2048]{2,1,0:T(8,128)(2,1)S(1)} fusion(f32[2,256,2048]{2,1,0:T(8,128)} %reshape.241, f32[1,256,2048]{2,1,0:T(8,128)S(1)} %slice_bitcast_fusion.1, f32[1,256,2048]{2,1,0:T(8,128)} %slice_bitcast_fusion.2, bf16[2,256,2048]{2,1,0:T(8,128)(2,1)} %collective-permute-done.3), kind=kLoop, calls=%fused_computation.6 | loop fusion | flops 5242880 | bytes 12582912 | tf_op jit(solution)/shard_map/convert.2
  (244 shorter events, 119.3 us)
Async XLA Ops:
  0.6 6.2 %copy-start.3 = (bf16[256,2048]{1,0:T(8,128)(2,1)S(1)}, bf16[256,2048]{1,0:T(8,128)(2,1)}, u32[]{:S(2)}) copy-start(bf16[256,2048]{1,0:T(8,128)(2,1)} %param.5) | copy-start | bytes 3145732
  0.6 7.7 %copy-start.4 = (bf16[256,2048]{1,0:T(8,128)(2,1)S(1)}, bf16[256,2048]{1,0:T(8,128)(2,1)}, u32[]{:S(2)}) copy-start(bf16[256,2048]{1,0:T(8,128)(2,1)} %param.6) | copy-start | bytes 3145732
  3.9 48.9 %collective-permute-start = (bf16[2,256,2048]{2,1,0:T(8,128)(2,1)}, bf16[2,256,2048]{2,1,0:T(8,128)(2,1)}, u32[]{:S(2)}, u32[]{:S(2)}) collective-permute-start(bf16[2,256,2048]{2,1,0:T(8,128)(2,1)} %pad_maximum_fusion.6), channel_id=1, source_target_pairs={{0,4},{4,0},{8,12},{12,8},{16,20},{20,16},{24,28},{28,24},{1,5},{5... | collective-permute-start | bytes 6291464 | tf_op jit(solution)/shard_map/ppermute | solution.py:20
  69.8 24.7 %collective-permute-start.1 = (bf16[2,128,2048]{2,0,1:T(2,128)(2,1)}, bf16[2,128,2048]{2,0,1:T(2,128)(2,1)}, u32[]{:S(2)}, u32[]{:S(2)}) collective-permute-start(bf16[2,128,2048]{2,0,1:T(2,128)(2,1)} %multiply_convert_fusion.1), channel_id=1, source_target_pairs={{0,8},{8,0},{4,12},{12,4},{16,24},{24,16},{20,28},{28,20},{1,9},{9... | collective-permute-start | bytes 3145736 | tf_op jit(solution)/shard_map/ppermute | solution.py:20
  102.2 14.5 %copy-start.47 = (bf16[256,2048]{1,0:T(8,128)(2,1)S(1)}, bf16[256,2048]{1,0:T(8,128)(2,1)}, u32[]{:S(2)}) copy-start(bf16[256,2048]{1,0:T(8,128)(2,1)} %param.4) | copy-start | bytes 3145732
  114.2 47.0 %collective-permute-start.2 = (bf16[2,128,2048]{2,0,1:T(2,128)(2,1)S(1)}, bf16[2,128,2048]{2,0,1:T(2,128)(2,1)}, u32[]{:S(2)}, u32[]{:S(2)}) collective-permute-start(bf16[2,128,2048]{2,0,1:T(2,128)(2,1)S(1)} %multiply_convert_fusion), channel_id=1, source_target_pairs={{0,16},{16,0},{4,20},{20,4},{8,24},{24,8},{12,28},{28,12},{1,17},{... | collective-permute-start | bytes 3145736 | tf_op jit(solution)/shard_map/ppermute | solution.py:20
  170.3 7.5 %copy-start.5 = (bf16[256,2048]{1,0:T(8,128)(2,1)S(1)}, bf16[256,2048]{1,0:T(8,128)(2,1)}, u32[]{:S(2)}) copy-start(bf16[256,2048]{1,0:T(8,128)(2,1)} %param.6) | copy-start | bytes 3145732
  170.3 7.5 %copy-start.21 = (bf16[256,2048]{1,0:T(8,128)(2,1)S(1)}, bf16[256,2048]{1,0:T(8,128)(2,1)}, u32[]{:S(2)}) copy-start(bf16[256,2048]{1,0:T(8,128)(2,1)} %get-tuple-element.26) | copy-start | bytes 3145732
  172.9 9.0 %copy-start.9 = (bf16[768,512]{0,1:T(8,128)(2,1)}, bf16[768,512]{0,1:T(8,128)(2,1)S(1)}, u32[]{:S(2)}) copy-start(bf16[768,512]{0,1:T(8,128)(2,1)S(1)} %copy.387) | copy-start | bytes 2359300
  233.9 5.9 %copy-start.43 = (bf16[4,128,256]{2,1,0:T(8,128)(2,1)S(1)}, bf16[4,128,256]{2,1,0:T(8,128)(2,1)}, u32[]{:S(2)}) copy-start(bf16[4,128,256]{2,1,0:T(8,128)(2,1)} %fusion.24) | copy-start | bytes 786436
  233.9 6.8 %slice-start.9 = ((f32[768,4,128]{0,2,1:T(8,128)}), f32[512,4,128]{0,2,1:T(8,128)S(1)}, s32[]{:S(2)}) async-start(f32[768,4,128]{0,2,1:T(8,128)} %copy-done.16), calls=%async_computation.9 | async-start | bytes 2097152 | tf_op jit(solution)/shard_map/slice | solution.py:74
  233.9 8.1 %slice-start.8 = ((f32[768,4,128]{0,2,1:T(8,128)}), f32[256,4,128]{0,2,1:T(8,128)S(1)}, s32[]{:S(2)}) async-start(f32[768,4,128]{0,2,1:T(8,128)} %copy-done.16), calls=%async_computation.8 | async-start | bytes 1048576 | tf_op jit(solution)/shard_map/slice | solution.py:75
  234.3 8.9 %slice-start.3 = ((f32[768,4,128]{0,2,1:T(8,128)}), f32[512,4,128]{0,2,1:T(8,128)S(1)}, s32[]{:S(2)}) async-start(f32[768,4,128]{0,2,1:T(8,128)} %copy-done.13), calls=%async_computation.3 | async-start | bytes 2097152 | tf_op jit(solution)/shard_map/slice | solution.py:76
  237.9 6.5 %slice-start.2 = ((f32[768,4,128]{0,2,1:T(8,128)}), f32[256,4,128]{0,2,1:T(8,128)S(1)}, s32[]{:S(2)}) async-start(f32[768,4,128]{0,2,1:T(8,128)} %copy-done.13), calls=%async_computation.2 | async-start | bytes 1048576 | tf_op jit(solution)/shard_map/slice | solution.py:77
  243.2 5.7 %slice-start.10 = ((f32[768,4,128]{0,2,1:T(8,128)}), f32[256,4,128]{0,2,1:T(8,128)S(1)}, s32[]{:S(2)}) async-start(f32[768,4,128]{0,2,1:T(8,128)} %copy-done.17), calls=%async_computation.10 | async-start | bytes 1048576 | tf_op jit(solution)/shard_map/slice | solution.py:75
  243.2 6.7 %slice-start.5 = ((f32[768,4,128]{0,2,1:T(8,128)}), f32[512,4,128]{0,2,1:T(8,128)S(1)}, s32[]{:S(2)}) async-start(f32[768,4,128]{0,2,1:T(8,128)} %copy-done.14), calls=%async_computation.5 | async-start | bytes 2097152 | tf_op jit(solution)/shard_map/slice | solution.py:76
  245.5 5.7 %slice-start.4 = ((f32[768,4,128]{0,2,1:T(8,128)}), f32[256,4,128]{0,2,1:T(8,128)S(1)}, s32[]{:S(2)}) async-start(f32[768,4,128]{0,2,1:T(8,128)} %copy-done.14), calls=%async_computation.4 | async-start | bytes 1048576 | tf_op jit(solution)/shard_map/slice | solution.py:77
  246.3 5.9 %copy-start.45 = (bf16[4,128,256]{2,1,0:T(8,128)(2,1)S(1)}, bf16[4,128,256]{2,1,0:T(8,128)(2,1)}, u32[]{:S(2)}) copy-start(bf16[4,128,256]{2,1,0:T(8,128)(2,1)} %fusion.25) | copy-start | bytes 786436
  249.9 5.7 %slice-start.11 = ((f32[768,4,128]{0,2,1:T(8,128)}), f32[256,4,128]{0,2,1:T(8,128)S(1)}, s32[]{:S(2)}) async-start(f32[768,4,128]{0,2,1:T(8,128)} %copy-done.18), calls=%async_computation.11 | async-start | bytes 1048576 | tf_op jit(solution)/shard_map/slice | solution.py:75
  251.2 5.4 %slice-start.7 = ((f32[768,4,128]{0,2,1:T(8,128)}), f32[512,4,128]{0,2,1:T(8,128)S(1)}, s32[]{:S(2)}) async-start(f32[768,4,128]{0,2,1:T(8,128)} %copy-done.15), calls=%async_computation.7 | async-start | bytes 2097152 | tf_op jit(solution)/shard_map/slice | solution.py:76
  252.2 5.7 %slice-start.6 = ((f32[768,4,128]{0,2,1:T(8,128)}), f32[256,4,128]{0,2,1:T(8,128)S(1)}, s32[]{:S(2)}) async-start(f32[768,4,128]{0,2,1:T(8,128)} %copy-done.15), calls=%async_computation.6 | async-start | bytes 1048576 | tf_op jit(solution)/shard_map/slice | solution.py:77
  253.1 5.9 %copy-start.46 = (bf16[4,128,256]{2,1,0:T(8,128)(2,1)S(1)}, bf16[4,128,256]{2,1,0:T(8,128)(2,1)}, u32[]{:S(2)}) copy-start(bf16[4,128,256]{2,1,0:T(8,128)(2,1)} %fusion.26) | copy-start | bytes 786436
  256.6 5.7 %slice-start.12 = ((f32[768,4,128]{0,2,1:T(8,128)}), f32[256,4,128]{0,2,1:T(8,128)S(1)}, s32[]{:S(2)}) async-start(f32[768,4,128]{0,2,1:T(8,128)} %copy-done.19), calls=%async_computation.12 | async-start | bytes 1048576 | tf_op jit(solution)/shard_map/slice | solution.py:75
  256.7 6.7 %slice-start.1 = ((f32[768,4,128]{0,2,1:T(8,128)}), f32[512,4,128]{0,2,1:T(8,128)S(1)}, s32[]{:S(2)}) async-start(f32[768,4,128]{0,2,1:T(8,128)} %copy-done.12), calls=%async_computation.1 | async-start | bytes 2097152 | tf_op jit(solution)/shard_map/slice | solution.py:76
  264.8 7.5 %copy-start.23 = (f32[512,512]{1,0:T(8,128)S(1)}, f32[512,512]{1,0:T(8,128)}, u32[]{:S(2)}) copy-start(f32[512,512]{1,0:T(8,128)} %copy.420) | copy-start | bytes 3145732
  264.8 7.5 %copy-start.25 = (f32[512,512]{1,0:T(8,128)S(1)}, f32[512,512]{1,0:T(8,128)}, u32[]{:S(2)}) copy-start(f32[512,512]{1,0:T(8,128)} %copy.423) | copy-start | bytes 3145732
  264.8 7.5 %copy-start.27 = (f32[512,512]{1,0:T(8,128)S(1)}, f32[512,512]{1,0:T(8,128)}, u32[]{:S(2)}) copy-start(f32[512,512]{1,0:T(8,128)} %copy.421) | copy-start | bytes 3145732
  264.8 7.5 %copy-start.28 = (f32[512,512]{1,0:T(8,128)S(1)}, f32[512,512]{1,0:T(8,128)}, u32[]{:S(2)}) copy-start(f32[512,512]{1,0:T(8,128)} %copy.422) | copy-start | bytes 3145732
  272.2 47.8 %collective-permute-start.4 = (bf16[2,128,2048]{2,0,1:T(2,128)(2,1)S(1)}, bf16[2,128,2048]{2,0,1:T(2,128)(2,1)S(1)}, u32[]{:S(2)}, u32[]{:S(2)}) collective-permute-start(bf16[2,128,2048]{2,0,1:T(2,128)(2,1)S(1)} %fusion.30), channel_id=1, source_target_pairs={{0,16},{16,0},{4,20},{20,4},{8,24},{24,8},{12,28},{28,12},{1,17},{... | collective-permute-start | bytes 3145736 | tf_op jit(solution)/shard_map/ppermute | solution.py:20
  326.7 24.0 %collective-permute-start.5 = (bf16[2,128,2048]{2,0,1:T(2,128)(2,1)S(1)}, bf16[2,128,2048]{2,0,1:T(2,128)(2,1)S(1)}, u32[]{:S(2)}, u32[]{:S(2)}) collective-permute-start(bf16[2,128,2048]{2,0,1:T(2,128)(2,1)S(1)} %fusion.23), channel_id=1, source_target_pairs={{0,8},{8,0},{4,12},{12,4},{16,24},{24,16},{20,28},{28,20},{1,9},{9... | collective-permute-start | bytes 3145736 | tf_op jit(solution)/shard_map/ppermute | solution.py:20
  328.5 82.9 %collective-permute-start.3 = (bf16[2,256,2048]{2,1,0:T(8,128)(2,1)}, bf16[2,256,2048]{2,1,0:T(8,128)(2,1)}, u32[]{:S(2)}, u32[]{:S(2)}) collective-permute-start(bf16[2,256,2048]{2,1,0:T(8,128)(2,1)} %pad_maximum_fusion.7), channel_id=1, source_target_pairs={{0,4},{4,0},{8,12},{12,8},{16,20},{20,16},{24,28},{28,24},{1,5},{5... | collective-permute-start | bytes 6291464 | tf_op jit(solution)/shard_map/ppermute | solution.py:20
  356.8 40.7 %collective-permute-start.6 = (bf16[2,128,2048]{2,0,1:T(2,128)(2,1)S(1)}, bf16[2,128,2048]{2,0,1:T(2,128)(2,1)S(1)}, u32[]{:S(2)}, u32[]{:S(2)}) collective-permute-start(bf16[2,128,2048]{2,0,1:T(2,128)(2,1)S(1)} %select_convert_fusion), channel_id=1, source_target_pairs={{0,4},{4,0},{8,12},{12,8},{16,20},{20,16},{24,28},{28,24},{1,5},{5... | collective-permute-start | bytes 3145736 | tf_op jit(solution)/shard_map/ppermute | solution.py:20
  (47 other events, 133.8 us)
where the time goes:
time: 423 us; the launch traced here: 418 us
  waiting for transfers between devices  190 us (45%)
  local copies, waits for them, and re-layouts  106 us (25%)
  other arithmetic  78.7 us (19%)
  matrix products  32.7 us (8%)
  starting transfers between devices  8.24 us (2%)
    ppermute x7, waiting for transfers between devices, partner_2(): return lax.ppermute(block, axis, route)  190 us
    unnamed x128, local copies, waits for them, and re-layouts  18.7 us
    convert_element_type x2, other arithmetic, body(): summary.astype(jnp.bfloat16)  14 us
    dot_general x4, matrix products, head_group(): jnp.einsum('hqk,khd->qhd', weights_low, value_heads, preferred_element_ty...  9.9 us
    slice x5, local copies, waits for them, and re-layouts, body(): all_values[:, columns]  9.49 us
    reshape x4, local copies, waits for them, and re-layouts, head_group(): key_all[:near_last].reshape(near_last, -1)  9 us
    slice x5, local copies, waits for them, and re-layouts, body(): all_keys[:, columns]  8.97 us
  transfers between devices with their start and end apart: 7, of which 6 were waited for; matrix products, arithmetic and copies ran while one was open for 13% of the time, Pallas kernels for 0%

commit v1 on v0

--- a/solution.py
+++ b/solution.py
@@ -1,13 +1,14 @@
+import functools
 import math
 
 import jax
 import jax.numpy as jnp
 from jax import lax
+from jax.experimental import pallas as pl
 from jax.sharding import PartitionSpec as P
 
 HEAD_DIM = 128
 POOLED = 128
-HGROUP = 4
 
 
 def partner_2(block, axis, stride):
@@ -28,56 +29,62 @@
     return jnp.mean(joined.reshape(mine.shape[0], mine.shape[1], 2, mine.shape[2]), axis=2)
 
 
-def head_group(query_part, grad_part, key_part, value_part, key_bias, near_last, score_scale):
-    leaf_rows = query_part.shape[0]
-    key_count = key_part.shape[0]
-    group_heads = query_part.shape[1] // HEAD_DIM
-    far_first = 2 * leaf_rows
-    query_heads = query_part.reshape(leaf_rows, group_heads, HEAD_DIM)
-    grad_heads = grad_part.reshape(leaf_rows, group_heads, HEAD_DIM)
-    key_heads = key_part.reshape(key_count, group_heads, HEAD_DIM)
-    value_heads = value_part.reshape(key_count, group_heads, HEAD_DIM)
+def attention_kernel(bias_ref, q_ref, do_ref, k_ref, v_ref, o_ref, dq_ref, dk_ref, dv_ref, *, scale):
+    q = q_ref[...]
+    do = do_ref[...]
+    k = k_ref[...]
+    v = v_ref[...]
     scores = (
-        jnp.einsum("qhd,khd->hqk", query_heads, key_heads, preferred_element_type=jnp.float32)
-        * score_scale
-        + key_bias
+        lax.dot_general(q, k, (((1,), (1,)), ((), ())), preferred_element_type=jnp.float32) * scale
+        + bias_ref[...]
     )
     row_max = jnp.max(scores, axis=-1, keepdims=True)
     log_total = row_max + jnp.log(jnp.sum(jnp.exp(scores - row_max), axis=-1, keepdims=True))
     weights = jnp.exp(scores - log_total)
     weights_low = weights.astype(jnp.bfloat16)
-    attended = jnp.einsum(
-        "hqk,khd->qhd", weights_low, value_heads, preferred_element_type=jnp.float32
+    attended = jnp.dot(weights_low, v, preferred_element_type=jnp.float32).astype(jnp.bfloat16)
+    o_ref[...] = attended
+    row_dot = jnp.sum(
+        do.astype(jnp.float32) * attended.astype(jnp.float32), axis=-1, keepdims=True
+    )
+    weight_grad = lax.dot_general(do, v, (((1,), (1,)), ((), ())), preferred_element_type=jnp.float32)
+    score_grad = (weights * (weight_grad - row_dot)).astype(jnp.bfloat16)
+    dq_ref[...] = (
+        jnp.dot(score_grad, k, preferred_element_type=jnp.float32) * scale
     ).astype(jnp.bfloat16)
-    row_dot = jnp.einsum("qhd,qhd->hq", grad_heads, attended, preferred_element_type=jnp.float32)[
-        ..., None
-    ]
-    weight_grad = jnp.einsum(
-        "qhd,khd->hqk", grad_heads, value_heads, preferred_element_type=jnp.float32
-    )
-    score_grad = (weights * (weight_grad - row_dot)).astype(jnp.bfloat16)
-    query_grad = (
-        jnp.einsum("hqk,khd->qhd", score_grad, key_heads, preferred_element_type=jnp.float32)
-        * score_scale
-    ).astype(jnp.bfloat16)
-    key_all = (
-        jnp.einsum("hqk,qhd->khd", score_grad, query_heads, preferred_element_type=jnp.float32)
-        * score_scale
-    )
-    value_all = jnp.einsum(
-        "hqk,qhd->khd", weights_low, grad_heads, preferred_element_type=jnp.float32
-    )
-    far_count = key_count - far_first
-    return (
-        attended.reshape(leaf_rows, -1),
-        query_grad.reshape(leaf_rows, -1),
-        key_all[:near_last].reshape(near_last, -1),
-        key_all[far_first:].reshape(far_count, -1),
-        value_all[:near_last].reshape(near_last, -1),
-        value_all[far_first:].reshape(far_count, -1),
-        log_total[..., 0],
-        row_dot[..., 0],
-    )
+    dk_ref[...] = jnp.dot(score_grad.T, q, preferred_element_type=jnp.float32) * scale
+    dv_ref[...] = jnp.dot(weights_low.T, do, preferred_element_type=jnp.float32)
+
+
+def attention(query_rows, out_grad, all_keys, all_values, key_bias, score_scale):
+    leaf_rows, model_width = query_rows.shape
+    key_count = all_keys.shape[0]
+    heads = model_width // HEAD_DIM
+    row_block = pl.BlockSpec((leaf_rows, HEAD_DIM), lambda h: (0, h))
+    key_block = pl.BlockSpec((key_count, HEAD_DIM), lambda h: (0, h))
+    flops = 12 * leaf_rows * key_count * model_width
+    io_bytes = 2 * (4 * leaf_rows + 2 * key_count) * model_width + 8 * key_count * model_width
+    return pl.pallas_call(
+        functools.partial(attention_kernel, scale=score_scale),
+        grid=(heads,),
+        in_specs=[
+            pl.BlockSpec((1, key_count), lambda h: (0, 0)),
+            row_block,
+            row_block,
+            key_block,
+            key_block,
+        ],
+        out_specs=[row_block, row_block, key_block, key_block],
+        out_shape=[
+            jax.ShapeDtypeStruct((leaf_rows, model_width), jnp.bfloat16),
+            jax.ShapeDtypeStruct((leaf_rows, model_width), jnp.bfloat16),
+            jax.ShapeDtypeStruct((key_count, model_width), jnp.float32),
+            jax.ShapeDtypeStruct((key_count, model_width), jnp.float32),
+        ],
+        cost_estimate=pl.CostEstimate(
+            flops=flops, transcendentals=2 * leaf_rows * key_count * heads, bytes_accessed=io_bytes
+        ),
+    )(key_bias.reshape(1, key_count), query_rows, out_grad, all_keys, all_values)
 
 
 def body(query_rows, key_rows, value_rows, out_grad):
@@ -88,7 +95,6 @@
     position = lax.axis_index("seq")
     pool_ratio = leaf_rows // POOLED
     head_count = model_width // HEAD_DIM
-    group_width = HGROUP * HEAD_DIM
     score_scale = HEAD_DIM ** (-0.5)
     paired = jnp.stack((key_rows, value_rows))
     sibling = partner_2(paired, "seq", 0)
@@ -113,26 +119,13 @@
         bias_parts.append(jnp.full((POOLED,), math.log(pool_ratio * 2**step_level), jnp.float32))
     key_bias = jnp.concatenate(bias_parts, axis=0)
     near_last = 2 * leaf_rows
-    outputs = [[], [], [], [], [], [], [], []]
-    for group_index in range(head_count // HGROUP):
-        columns = slice(group_index * group_width, (group_index + 1) * group_width)
-        results = head_group(
-            query_rows[:, columns],
-            out_grad[:, columns],
-            all_keys[:, columns],
-            all_values[:, columns],
-            key_bias,
-            near_last,
-            score_scale,
-        )
-        for slot_index in range(8):
-            outputs[slot_index].append(results[slot_index])
-    attended = jnp.concatenate(outputs[0], axis=1)
-    query_grad = jnp.concatenate(outputs[1], axis=1)
-    near_key = jnp.concatenate(outputs[2], axis=1)
-    far_key = jnp.concatenate(outputs[3], axis=1)
-    near_value = jnp.concatenate(outputs[4], axis=1)
-    far_value = jnp.concatenate(outputs[5], axis=1)
+    attended, query_grad, key_all, value_all = attention(
+        query_rows, out_grad, all_keys, all_values, key_bias, score_scale
+    )
+    near_key = key_all[:near_last]
+    far_key = key_all[near_last:]
+    near_value = value_all[:near_last]
+    far_value = value_all[near_last:]
     to_sibling = jnp.stack((near_key[leaf_rows:], near_value[leaf_rows:])).astype(jnp.bfloat16)
     from_sibling = partner_2(to_sibling, "seq", 0)
     own_terms = jnp.stack((near_key[:leaf_rows], near_value[:leaf_rows]))

time: 423 us -> 372 us (0.88)
  local copies, waits for them, and re-layouts: 106 us -> 68.2 us
  matrix products: 32.7 us -> 0 us
  Pallas kernels: 0 us -> 23 us
  other arithmetic: 78.7 us -> 60.3 us
  waiting for transfers between devices: 190 us -> 204 us
    dot_general x24 -> x0, matrix products: 32.7 us -> none  [the longest x4 9.9 us: head_group(): jnp.einsum('hqk,khd->qhd', weights_low, value_heads, preferred_element_ty...]
    slice x42 -> x0, local copies, waits for them, and re-layouts: 27.2 us -> none  [the longest x5 9.49 us: body(): all_values[:, columns]]
    pallas_call x0 -> x1, Pallas kernels: none -> 23 us  [attention(): pl.pallas_call(functools.partial(attention_kernel, scale=score_scale), gr...]
    unnamed x128 -> x15, local copies, waits for them, and re-layouts: 18.7 us -> 4.19 us
    ppermute x7, waiting for transfers between devices: 190 us -> 204 us  [partner_2(): return lax.ppermute(block, axis, route)]
    convert_element_type x2, other arithmetic: 14 us -> 1.29 us  [body(): summary.astype(jnp.bfloat16)]
    concatenate x8 -> x0, local copies, waits for them, and re-layouts: 8.14 us -> none  [the longest x4 4.07 us: body(): far_key = jnp.concatenate(outputs[3], axis=1)]
    reduce_sum x2, other arithmetic: 8.16 us -> 14.7 us  [combine_halves(): jnp.mean(joined.reshape(mine.shape[0], mine.shape[1], 2, mine.shape[2]),...]
  transfers between devices with their start and end apart: 7 -> 7, of which waited for: 6 -> 6; matrix products, arithmetic and copies ran while one was open for 13% -> 12% of each run, Pallas kernels for 0% -> 0%
where the time goes in v1:
time: 372 us; the launch traced here: 365 us
  waiting for transfers between devices  204 us (55%)
  local copies, waits for them, and re-layouts  68.2 us (18%)
  other arithmetic  60.3 us (16%)
  Pallas kernels  23 us (6%)
  starting transfers between devices  8.17 us (2%)
    ppermute x7, waiting for transfers between devices, partner_2(): return lax.ppermute(block, axis, route)  204 us
    pallas_call x1, Pallas kernels, attention(): pl.pallas_call(functools.partial(attention_kernel, scale=score_scale), gr...  23 us
    reduce_sum x2, other arithmetic, combine_halves(): jnp.mean(joined.reshape(mine.shape[0], mine.shape[1], 2, mine.shape[2]),...  14.7 us
    reshape x2, local copies, waits for them, and re-layouts, body(): spread = jnp.broadcast_to(0.5 * summary_grad[:, :, None, :], (2, POOLED,...  12.4 us
    reshape x2, local copies, waits for them, and re-layouts, combine_halves(): joined.reshape(mine.shape[0], mine.shape[1], 2, mine.shape[2])  12 us
    broadcast_in_dim x2, local copies, waits for them, and re-layouts, body(): jnp.broadcast_to(0.5 * summary_grad[:, :, None, :], (2, POOLED, 2, model_...  8.7 us
    ppermute x7, starting transfers between devices, partner_2(): return lax.ppermute(block, axis, route)  8.17 us
  transfers between devices with their start and end apart: 7, of which 6 were waited for; matrix products, arithmetic and copies ran while one was open for 12% of the time, Pallas kernels for 0%

profile of v1, /device:TPU:0, one launch (start us, length us, event | category | flops | bytes accessed | tf_op | source)
XLA Modules:
  0.0 365.1 jit_solution(3916350652180163216)
XLA Ops:
  0.6 3.2 pad_maximum_fusion.5
  3.8 3.0 collective-permute-start
  8.2 7.0 %convert_reduce_fusion = f32[2,128,2048]{2,1,0:T(8,128)} fusion(bf16[1,128,2,2048]{3,2,1,0:T(2,128)(2,1)S(1)} %stack.49, bf16[1,128,2,2048]{3,2,1,0:T(2,128)(2,1)S(1)} %stack.48), kind=kLoop, calls=%fused_computation.7 | loop fusion | flops 2621440 | bytes 4194304 | tf_op jit(solution)/shard_map/reduce_sum | solution.py:101
  15.2 37.5 %collective-permute-done = bf16[2,256,2048]{2,1,0:T(8,128)(2,1)} collective-permute-done((bf16[2,256,2048]{2,1,0:T(8,128)(2,1)}, bf16[2,256,2048]{2,1,0:T(8,128)(2,1)}, u32[]{:S(2)}, u32[]{:S(2)}) %collective-permute-start) | collective-permute-done | bytes 2097184 | tf_op jit(solution)/shard_map/ppermute | solution.py:21
  52.7 6.0 %reshape.50 = f32[2,128,2,2048]{3,2,1,0:T(2,128)} reshape(bf16[2,256,2048]{2,1,0:T(8,128)(2,1)} %collective-permute-done) | data formatting | bytes 6291456 | tf_op jit(solution)/shard_map/convert_element_type | solution.py:104
  58.7 7.4 %reduce_sum.36 = f32[2,128,2048]{2,1,0:T(8,128)S(1)} reduce(f32[2,128,2,2048]{3,2,1,0:T(2,128)} %reshape.50, f32[]{:T(128)} %constant.71.clone.1), dimensions={2}, to_apply=%region_0.0 | reduce | flops 524288 | bytes 6291460 | tf_op jit(solution)/shard_map/reduce_sum | solution.py:104
  66.1 2.0 multiply_select_fusion.1
  68.1 2.5 pad_maximum_fusion
  70.6 6.0 %reshape.45 = f32[2,128,2,2048]{3,2,1,0:T(2,128)} reshape(f32[2,256,2048]{2,1,0:T(8,128)} %pad_maximum_fusion) | data formatting | bytes 8388608 | tf_op jit(solution)/shard_map/reshape | solution.py:29
  76.6 7.4 %reduce_sum.38 = f32[2,128,2048]{2,1,0:T(8,128)S(1)} reduce(f32[2,128,2,2048]{3,2,1,0:T(2,128)} %reshape.45, f32[]{:T(128)} %constant.71.clone.1), dimensions={2}, to_apply=%region_2.3 | reduce | flops 524288 | bytes 6291460 | tf_op jit(solution)/shard_map/reduce_sum | solution.py:29
  86.9 22.9 %collective-permute-done.1 = bf16[2,128,2048]{2,1,0:T(8,128)(2,1)} collective-permute-done((bf16[2,128,2048]{2,1,0:T(8,128)(2,1)}, bf16[2,128,2048]{2,1,0:T(8,128)(2,1)}, u32[]{:S(2)}, u32[]{:S(2)}) %collective-permute-start.1) | collective-permute-done | bytes 1048608 | tf_op jit(solution)/shard_map/ppermute | solution.py:21
  111.5 2.5 pad_maximum_fusion.1
  113.9 6.0 %reshape.46 = f32[2,128,2,2048]{3,2,1,0:T(2,128)} reshape(f32[2,256,2048]{2,1,0:T(8,128)} %pad_maximum_fusion.1) | data formatting | bytes 8388608 | tf_op jit(solution)/shard_map/reshape | solution.py:29
  120.0 7.4 %reduce_sum.39 = f32[2,128,2048]{2,1,0:T(8,128)S(1)} reduce(f32[2,128,2,2048]{3,2,1,0:T(2,128)} %reshape.46, f32[]{:T(128)} %constant.71.clone.1), dimensions={2}, to_apply=%region_3.4 | reduce | flops 524288 | bytes 6291460 | tf_op jit(solution)/shard_map/reduce_sum | solution.py:29
  127.5 2.6 collective-permute-start.2
  133.2 41.2 %collective-permute-done.2 = bf16[2,128,2048]{2,1,0:T(8,128)(2,1)S(1)} collective-permute-done((bf16[2,128,2048]{2,1,0:T(8,128)(2,1)S(1)}, bf16[2,128,2048]{2,1,0:T(8,128)(2,1)S(1)}, u32[]{:S(2)}, u32[]{:S(2)}) %collective-permute-start.2) | collective-permute-done | bytes 1048608 | tf_op jit(solution)/shard_map/ppermute | solution.py:21
  175.7 3.0 pad_maximum_fusion.2
  178.7 23.0 %shard_map.75 = (bf16[256,2048]{1,0:T(8,128)(2,1)}, bf16[256,2048]{1,0:T(8,128)(2,1)}, f32[768,2048]{1,0:T(8,128)}, f32[768,2048]{1,0:T(8,128)}) custom-call(f32[1,768]{1,0:T(1,128)} %constant.65.clone.1.bias_ref, bf16[256,2048]{1,0:T(8,128)(2,1)} %q_ref.1, bf16[256,2048]{1,0:T(8,128)(2,1)} %do_ref.1, bf16[768,2048]{1,0:T(8,128)(2,1)} %get-tuple-element.26.k_ref, ...), custom_call_target="tpu_custom_call" | custom-call | flops 4831838208 | bytes 23068672 | tf_op jit(solution)/shard_map/pallas_call | solution.py:67
  201.8 4.1 %slice_bitcast_fusion.1 = (f32[1,256,2048]{2,1,0:T(8,128)}, f32[256,2048]{1,0:T(8,128)S(1)}) fusion(f32[768,2048]{1,0:T(8,128)} %get-tuple-element.10), kind=kLoop, calls=%fused_computation.27 | loop fusion | bytes 8388608 | tf_op jit(solution)/shard_map/stack | solution.py:131
  209.6 47.8 %collective-permute-done.4 = bf16[2,128,2048]{2,1,0:T(8,128)(2,1)S(1)} collective-permute-done((bf16[2,128,2048]{2,1,0:T(8,128)(2,1)S(1)}, bf16[2,128,2048]{2,1,0:T(8,128)(2,1)S(1)}, u32[]{:S(2)}, u32[]{:S(2)}) %collective-permute-start.4) | collective-permute-done | bytes 1048608 | tf_op jit(solution)/shard_map/ppermute | solution.py:21
  257.6 4.3 %broadcast_in_dim.6 = f32[2,128,2,2048]{3,2,1,0:T(2,128)} broadcast(f32[2,128,2048]{2,1,0:T(8,128)S(1)} %convert_multiply_fusion), dimensions={0,1,3} | broadcast | bytes 6291456 | tf_op jit(solution)/shard_map/broadcast_in_dim | solution.py:136
  262.0 6.3 %reshape.47 = f32[2,256,2048]{2,1,0:T(8,128)} reshape(f32[2,128,2,2048]{3,2,1,0:T(2,128)} %broadcast_in_dim.6) | data formatting | bytes 8388608 | tf_op jit(solution)/shard_map/reshape | solution.py:138
  268.2 3.0 fusion.6
  277.0 18.2 %collective-permute-done.5 = bf16[2,128,2048]{2,1,0:T(8,128)(2,1)S(1)} collective-permute-done((bf16[2,128,2048]{2,1,0:T(8,128)(2,1)S(1)}, bf16[2,128,2048]{2,1,0:T(8,128)(2,1)S(1)}, u32[]{:S(2)}, u32[]{:S(2)}) %collective-permute-start.5) | collective-permute-done | bytes 1048608 | tf_op jit(solution)/shard_map/ppermute | solution.py:21
  295.7 4.4 %broadcast_in_dim.7 = f32[2,128,2,2048]{3,2,1,0:T(2,128)} broadcast(f32[2,128,2048]{2,1,0:T(8,128)S(1)} %add_multiply_fusion.1), dimensions={0,1,3} | broadcast | bytes 6291456 | tf_op jit(solution)/shard_map/broadcast_in_dim | solution.py:136
  300.0 6.1 %reshape.48 = f32[2,256,2048]{2,1,0:T(8,128)} reshape(f32[2,128,2,2048]{3,2,1,0:T(2,128)} %broadcast_in_dim.7) | data formatting | bytes 8388608 | tf_op jit(solution)/shard_map/reshape | solution.py:138
  306.1 2.4 select_convert_fusion
  308.6 36.8 %collective-permute-done.6 = bf16[2,128,2048]{2,1,0:T(8,128)(2,1)S(1)} collective-permute-done((bf16[2,128,2048]{2,1,0:T(8,128)(2,1)S(1)}, bf16[2,128,2048]{2,1,0:T(8,128)(2,1)S(1)}, u32[]{:S(2)}, u32[]{:S(2)}) %collective-permute-start.6) | collective-permute-done | bytes 1048608 | tf_op jit(solution)/shard_map/ppermute | solution.py:21
  345.3 2.7 add_multiply_fusion
  348.1 4.4 %broadcast_in_dim.8 = f32[2,128,2,2048]{3,2,1,0:T(2,128)} broadcast(f32[2,128,2048]{2,1,0:T(8,128)S(1)} %add_multiply_fusion), dimensions={0,1,3} | broadcast | bytes 6291456 | tf_op jit(solution)/shard_map/broadcast_in_dim | solution.py:149
  352.5 6.2 %reshape.49 = f32[2,256,2048]{2,1,0:T(8,128)} reshape(f32[2,128,2,2048]{3,2,1,0:T(2,128)} %broadcast_in_dim.8) | data formatting | bytes 8388608 | tf_op jit(solution)/shard_map/reshape | solution.py:151
  358.7 4.6 %fusion.1 = bf16[2,256,2048]{2,1,0:T(8,128)(2,1)S(1)} fusion(f32[2,256,2048]{2,1,0:T(8,128)} %reshape.49, f32[1,256,2048]{2,1,0:T(8,128)} %get-tuple-element.14, f32[1,256,2048]{2,1,0:T(8,128)S(1)} %copy-done.5, bf16[2,256,2048]{2,1,0:T(8,128)(2,1)} %collective-permute-done.3), kind=kLoop, calls=%fused_computation.4 | loop fusion | flops 5242880 | bytes 12582912 | tf_op jit(solution)/shard_map/convert.2
  (37 shorter events, 22.5 us)
Async XLA Ops:
  0.6 6.1 %copy-start.3 = (bf16[256,2048]{1,0:T(8,128)(2,1)S(1)}, bf16[256,2048]{1,0:T(8,128)(2,1)}, u32[]{:S(2)}) copy-start(bf16[256,2048]{1,0:T(8,128)(2,1)} %param.5) | copy-start | bytes 3145732
  3.8 3.7 %copy-start.2 = (bf16[256,2048]{1,0:T(8,128)(2,1)S(1)}, bf16[256,2048]{1,0:T(8,128)(2,1)}, u32[]{:S(2)}) copy-start(bf16[256,2048]{1,0:T(8,128)(2,1)} %param.6) | copy-start | bytes 3145732
  3.8 48.9 %collective-permute-start = (bf16[2,256,2048]{2,1,0:T(8,128)(2,1)}, bf16[2,256,2048]{2,1,0:T(8,128)(2,1)}, u32[]{:S(2)}, u32[]{:S(2)}) collective-permute-start(bf16[2,256,2048]{2,1,0:T(8,128)(2,1)} %pad_maximum_fusion.5), channel_id=1, source_target_pairs={{0,4},{4,0},{8,12},{12,8},{16,20},{20,16},{24,28},{28,24},{1,5},{5... | collective-permute-start | bytes 6291464 | tf_op jit(solution)/shard_map/ppermute | solution.py:21
  85.1 24.7 %collective-permute-start.1 = (bf16[2,128,2048]{2,1,0:T(8,128)(2,1)}, bf16[2,128,2048]{2,1,0:T(8,128)(2,1)}, u32[]{:S(2)}, u32[]{:S(2)}) collective-permute-start(bf16[2,128,2048]{2,1,0:T(8,128)(2,1)} %multiply_convert_fusion.1), channel_id=1, source_target_pairs={{0,8},{8,0},{4,12},{12,4},{16,24},{24,16},{20,28},{28,20},{1,9},{9... | collective-permute-start | bytes 3145736 | tf_op jit(solution)/shard_map/ppermute | solution.py:21
  127.5 46.9 %collective-permute-start.2 = (bf16[2,128,2048]{2,1,0:T(8,128)(2,1)S(1)}, bf16[2,128,2048]{2,1,0:T(8,128)(2,1)S(1)}, u32[]{:S(2)}, u32[]{:S(2)}) collective-permute-start(bf16[2,128,2048]{2,1,0:T(8,128)(2,1)S(1)} %multiply_convert_fusion), channel_id=1, source_target_pairs={{0,16},{16,0},{4,20},{20,4},{8,24},{24,8},{12,28},{28,12},{1,17},{... | collective-permute-start | bytes 3145736 | tf_op jit(solution)/shard_map/ppermute | solution.py:21
  174.5 1.2 copy-start.4
  201.7 4.8 %copy-start.6 = (f32[768,2048]{1,0:T(8,128)S(1)}, f32[768,2048]{1,0:T(8,128)}, u32[]{:S(2)}) copy-start(f32[768,2048]{1,0:T(8,128)} %get-tuple-element.11) | copy-start | bytes 18874372
  208.2 1.4 copy-start.1
  209.6 47.8 %collective-permute-start.4 = (bf16[2,128,2048]{2,1,0:T(8,128)(2,1)S(1)}, bf16[2,128,2048]{2,1,0:T(8,128)(2,1)S(1)}, u32[]{:S(2)}, u32[]{:S(2)}) collective-permute-start(bf16[2,128,2048]{2,1,0:T(8,128)(2,1)S(1)} %fusion.9), channel_id=1, source_target_pairs={{0,16},{16,0},{4,20},{20,4},{8,24},{24,8},{12,28},{28,12},{1,17},{... | collective-permute-start | bytes 3145736 | tf_op jit(solution)/shard_map/ppermute | solution.py:21
  271.2 24.0 %collective-permute-start.5 = (bf16[2,128,2048]{2,1,0:T(8,128)(2,1)S(1)}, bf16[2,128,2048]{2,1,0:T(8,128)(2,1)S(1)}, u32[]{:S(2)}, u32[]{:S(2)}) collective-permute-start(bf16[2,128,2048]{2,1,0:T(8,128)(2,1)S(1)} %fusion.6), channel_id=1, source_target_pairs={{0,8},{8,0},{4,12},{12,4},{16,24},{24,16},{20,28},{28,20},{1,9},{9... | collective-permute-start | bytes 3145736 | tf_op jit(solution)/shard_map/ppermute | solution.py:21
  274.8 20.4 %copy-start = (f32[2,256,2048]{2,1,0:T(8,128)S(1)}, f32[2,256,2048]{2,1,0:T(8,128)}, u32[]{:S(2)}) copy-start(f32[2,256,2048]{2,1,0:T(8,128)} %reshape.47) | copy-start | bytes 12582916
  276.3 82.4 %collective-permute-start.3 = (bf16[2,256,2048]{2,1,0:T(8,128)(2,1)}, bf16[2,256,2048]{2,1,0:T(8,128)(2,1)}, u32[]{:S(2)}, u32[]{:S(2)}) collective-permute-start(bf16[2,256,2048]{2,1,0:T(8,128)(2,1)} %pad_maximum_fusion.6), channel_id=1, source_target_pairs={{0,4},{4,0},{8,12},{12,8},{16,20},{20,16},{24,28},{28,24},{1,5},{5... | collective-permute-start | bytes 6291464 | tf_op jit(solution)/shard_map/ppermute | solution.py:21
  308.5 36.8 %collective-permute-start.6 = (bf16[2,128,2048]{2,1,0:T(8,128)(2,1)S(1)}, bf16[2,128,2048]{2,1,0:T(8,128)(2,1)S(1)}, u32[]{:S(2)}, u32[]{:S(2)}) collective-permute-start(bf16[2,128,2048]{2,1,0:T(8,128)(2,1)S(1)} %select_convert_fusion), channel_id=1, source_target_pairs={{0,4},{4,0},{8,12},{12,8},{16,20},{20,16},{24,28},{28,24},{1,5},{5... | collective-permute-start | bytes 3145736 | tf_op jit(solution)/shard_map/ppermute | solution.py:21
  352.4 6.2 %copy-start.5 = (f32[1,256,2048]{2,1,0:T(8,128)S(1)}, f32[1,256,2048]{2,1,0:T(8,128)}, u32[]{:S(2)}) copy-start(f32[1,256,2048]{2,1,0:T(8,128)} %get-tuple-element.12) | copy-start | bytes 6291460

commit v2 on v1

v2 whole, which is shorter than its diff:
```python
import functools
import math

import jax
import jax.numpy as jnp
from jax import lax
from jax.experimental import pallas as pl
from jax.sharding import PartitionSpec as P

HEAD_DIM = 128
POOLED = 128
CHUNKS = 4


def partner_2(block, axis, stride):
    count = lax.axis_size(axis)
    route = []
    for low in range(count):
        high = low | 1 << stride
        if high != low and high < count:
            route += [(low, high), (high, low)]
    return lax.ppermute(block, axis, route)


def attention_kernel(bias_ref, q_ref, do_ref, k_ref, v_ref, o_ref, dq_ref, dk_ref, dv_ref, *, scale):
    q = q_ref[...]
    do = do_ref[...]
    k = k_ref[...]
    v = v_ref[...]
    scores = (
        lax.dot_general(q, k, (((1,), (1,)), ((), ())), preferred_element_type=jnp.float32) * scale
        + bias_ref[...]
    )
    row_max = jnp.max(scores, axis=-1, keepdims=True)
    log_total = row_max + jnp.log(jnp.sum(jnp.exp(scores - row_max), axis=-1, keepdims=True))
    weights = jnp.exp(scores - log_total)
    weights_low = weights.astype(jnp.bfloat16)
    attended = jnp.dot(weights_low, v, preferred_element_type=jnp.float32).astype(jnp.bfloat16)
    o_ref[...] = attended
    row_dot = jnp.sum(
        do.astype(jnp.float32) * attended.astype(jnp.float32), axis=-1, keepdims=True
    )
    weight_grad = lax.dot_general(do, v, (((1,), (1,)), ((), ())), preferred_element_type=jnp.float32)
    score_grad = (weights * (weight_grad - row_dot)).astype(jnp.bfloat16)
    dq_ref[...] = (
        jnp.dot(score_grad, k, preferred_element_type=jnp.float32) * scale
    ).astype(jnp.bfloat16)
    dk_ref[...] = jnp.dot(score_grad.T, q, preferred_element_type=jnp.float32) * scale
    dv_ref[...] = jnp.dot(weights_low.T, do, preferred_element_type=jnp.float32)


def attention(query_rows, out_grad, keys, values, key_bias, score_scale, head_offset):
    leaf_rows = query_rows.shape[0]
    key_count, width = keys.shape
    heads = width // HEAD_DIM
    row_in = pl.BlockSpec((leaf_rows, HEAD_DIM), lambda h: (0, h + head_offset))
    row_out = pl.BlockSpec((leaf_rows, HEAD_DIM), lambda h: (0, h))
    key_block = pl.BlockSpec((key_count, HEAD_DIM), lambda h: (0, h))
    flops = 12 * leaf_rows * key_count * width
    io_bytes = 2 * (4 * leaf_rows + 2 * key_count) * width + 8 * key_count * width
    return pl.pallas_call(
        functools.partial(attention_kernel, scale=score_scale),
        grid=(heads,),
        in_specs=[
            pl.BlockSpec((1, key_count), lambda h: (0, 0)),
            row_in,
            row_in,
            key_block,
            key_block,
        ],
        out_specs=[row_out, row_out, key_block, key_block],
        out_shape=[
            jax.ShapeDtypeStruct((leaf_rows, width), jnp.bfloat16),
            jax.ShapeDtypeStruct((leaf_rows, width), jnp.bfloat16),
            jax.ShapeDtypeStruct((key_count, width), jnp.float32),
            jax.ShapeDtypeStruct((key_count, width), jnp.float32),
        ],
        cost_estimate=pl.CostEstimate(
            flops=flops, transcendentals=2 * leaf_rows * key_count * heads, bytes_accessed=io_bytes
        ),
    )(key_bias.reshape(1, key_count), query_rows, out_grad, keys, values)


def placed_pool(rows_in, upper):
    run = rows_in // (POOLED // 2)
    out_row = lax.broadcasted_iota(jnp.int32, (POOLED, rows_in), 0)
    in_row = lax.broadcasted_iota(jnp.int32, (POOLED, rows_in), 1)
    offset = upper * (POOLED // 2)
    return jnp.where(out_row - offset == in_row // run, 1.0 / run, 0.0).astype(jnp.float32)


def apply(matrix, rows):
    return jnp.dot(
        matrix, rows.astype(jnp.float32), precision=lax.Precision.HIGHEST,
        preferred_element_type=jnp.float32,
    )


def body(query_rows, key_rows, value_rows, out_grad):
    leaf_rows, model_width = query_rows.shape
    seq_count = lax.axis_size("seq")
    levels = seq_count.bit_length() - 1
    position = lax.axis_index("seq")
    pool_ratio = leaf_rows // POOLED
    score_scale = HEAD_DIM ** (-0.5)
    chunk_width = model_width // CHUNKS
    bias_parts = [jnp.zeros((2 * leaf_rows,), jnp.float32)]
    for step_level in range(1, levels):
        bias_parts.append(jnp.full((POOLED,), math.log(pool_ratio * 2**step_level), jnp.float32))
    key_bias = jnp.concatenate(bias_parts, axis=0)
    bits = [position // 2**step_level % 2 for step_level in range(levels)]
    mine = [placed_pool(leaf_rows if s == 0 else POOLED, bits[s]) for s in range(levels)]
    other = [placed_pool(leaf_rows if s == 0 else POOLED, 1 - bits[s]) for s in range(levels)]
    far_first = 2 * leaf_rows
    pieces = [[], [], [], []]
    for chunk in range(CHUNKS):
        columns = slice(chunk * chunk_width, (chunk + 1) * chunk_width)
        own = (key_rows[:, columns], value_rows[:, columns])
        sibling = partner_2(own, "seq", 0)
        summary = [apply(mine[0], own[i]) + apply(other[0], sibling[i]) for i in range(2)]
        far = []
        for step_level in range(1, levels):
            partner = partner_2(tuple(x.astype(jnp.bfloat16) for x in summary), "seq", step_level)
            far.append(partner)
            if step_level + 1 < levels:
                summary = [
                    apply(mine[step_level], summary[i]) + apply(other[step_level], partner[i])
                    for i in range(2)
                ]
        keys = jnp.concatenate([own[0], sibling[0]] + [f[0] for f in far], axis=0)
        values = jnp.concatenate([own[1], sibling[1]] + [f[1] for f in far], axis=0)
        attended, query_grad, key_all, value_all = attention(
            query_rows, out_grad, keys, values, key_bias, score_scale,
            chunk * (chunk_width // HEAD_DIM),
        )
        terms = (key_all, value_all)
        grad = None
        for step_level in reversed(range(1, levels)):
            first = far_first + (step_level - 1) * POOLED
            outgoing = [terms[i][first:first + POOLED] for i in range(2)]
            if grad is not None:
                outgoing = [outgoing[i] + apply(other[step_level].T, grad[i]) for i in range(2)]
            returned = partner_2(tuple(x.astype(jnp.bfloat16) for x in outgoing), "seq", step_level)
            if grad is None:
                grad = [returned[i].astype(jnp.float32) for i in range(2)]
            else:
                grad = [apply(mine[step_level].T, grad[i]) + returned[i] for i in range(2)]
        to_sibling = [terms[i][leaf_rows:far_first] for i in range(2)]
        own_total = [terms[i][:leaf_rows] for i in range(2)]
        if grad is not None:
            to_sibling = [to_sibling[i] + apply(other[0].T, grad[i]) for i in range(2)]
            own_total = [own_total[i] + apply(mine[0].T, grad[i]) for i in range(2)]
        from_sibling = partner_2(tuple(x.astype(jnp.bfloat16) for x in to_sibling), "seq", 0)
        totals = [own_total[i] + from_sibling[i].astype(jnp.float32) for i in range(2)]
        for slot, piece in enumerate((attended, query_grad, totals[0], totals[1])):
            pieces[slot].append(piece)
    return tuple(jnp.concatenate(p, axis=1).astype(jnp.bfloat16) for p in pieces)


def solution(mesh):
    spec = P(("batch", "seq"), None)
    return jax.shard_map(
        body, mesh=mesh, in_specs=(spec, spec, spec, spec), out_specs=(spec, spec, spec, spec),
        check_vma=False,
    )
```

time: 372 us -> 235 us (0.63); the launches traced: 365 us -> 234 us
  waiting for transfers between devices: 204 us -> 60.1 us
  starting transfers between devices: 8.17 us -> 63.7 us
  local copies, waits for them, and re-layouts: 68.2 us -> 15.2 us
  matrix products: 0 us -> 43.5 us
  other arithmetic: 60.3 us -> 20.4 us
  Pallas kernels: 23 us -> 29.2 us
    ppermute x7 -> x48, waiting for transfers between devices: 204 us -> 60.1 us  [partner_2(): return lax.ppermute(block, axis, route)]
    ppermute x7 -> x48, starting transfers between devices: 8.17 us -> 63.7 us  [partner_2(): return lax.ppermute(block, axis, route)]
    dot_general x0 -> x64, matrix products: none -> 43.5 us  [apply(): jnp.dot(matrix, rows.astype(jnp.float32), precision=lax.Precision.HIGHEST...]
    reshape x5 -> x0, local copies, waits for them, and re-layouts: 30.6 us -> none  [the longest x2 12.4 us: body(): spread = jnp.broadcast_to(0.5 * summary_grad[:, :, None, :], (2, POOLED,...]
    reduce_sum x4 -> x0, other arithmetic: 29.1 us -> none  [the longest x2 14.7 us: combine_halves(): jnp.mean(joined.reshape(mine.shape[0], mine.shape[1], 2, mine.shape[2]),...]
    slice x0 -> x10, local copies, waits for them, and re-layouts: none -> 15.1 us  [the longest x8 11.8 us: body(): outgoing = [terms[i][first:first + POOLED] for i in range(2)]]
    broadcast_in_dim x3 -> x0, local copies, waits for them, and re-layouts: 13.1 us -> none  [the longest x2 8.7 us: body(): jnp.broadcast_to(0.5 * summary_grad[:, :, None, :], (2, POOLED, 2, model_...]
    concatenate x3 -> x12, other arithmetic: 7.89 us -> 19.2 us  [the longest x4 7.84 us: body(): keys = jnp.concatenate([own[0], sibling[0]] + [f[0] for f in far], axis=0)]
  transfers between devices with their start and end apart: 7 -> 48, of which waited for: 6 -> 17; matrix products, arithmetic and copies ran while one was open for 12% -> 32% of each run, Pallas kernels for 0% -> 12%
where the time goes in v2:
time: 235 us; the launch traced here: 234 us
  starting transfers between devices  63.7 us (27%)
  waiting for transfers between devices  60.1 us (26%)
  matrix products  43.5 us (19%)
  Pallas kernels  29.2 us (12%)
  other arithmetic  20.4 us (9%)
  local copies, waits for them, and re-layouts  15.2 us (6%)
    ppermute x48, starting transfers between devices, partner_2(): return lax.ppermute(block, axis, route)  63.7 us
    ppermute x48, waiting for transfers between devices, partner_2(): return lax.ppermute(block, axis, route)  60.1 us
    dot_general x64, matrix products, apply(): jnp.dot(matrix, rows.astype(jnp.float32), precision=lax.Precision.HIGHEST...  43.5 us
    pallas_call x4, Pallas kernels, attention(): pl.pallas_call(functools.partial(attention_kernel, scale=score_scale), gr...  29.2 us
    slice x8, local copies, waits for them, and re-layouts, body(): outgoing = [terms[i][first:first + POOLED] for i in range(2)]  11.8 us
    concatenate x4, other arithmetic, body(): keys = jnp.concatenate([own[0], sibling[0]] + [f[0] for f in far], axis=0)  7.84 us
    concatenate x4, other arithmetic, body(): values = jnp.concatenate([own[1], sibling[1]] + [f[1] for f in far], axis=0)  5.7 us
    concatenate x4, other arithmetic, body(): jnp.concatenate(p, axis=1).astype(jnp.bfloat16)  5.68 us
  transfers between devices with their start and end apart: 48, of which 17 were waited for; matrix products, arithmetic and copies ran while one was open for 32% of the time, Pallas kernels for 12%

profile of v2, /device:TPU:0, one launch (start us, length us, event | category | flops | bytes accessed | tf_op | source)
XLA Modules:
  0.0 233.6 jit_solution(11413826215892806130)
XLA Ops:
  0.6 2.3 fusion.665
  2.9 3.0 %collective-permute-start = (bf16[256,512]{1,0:T(8,128)(2,1)}, bf16[256,512]{1,0:T(8,128)(2,1)}, u32[]{:S(2)}, u32[]{:S(2)}) collective-permute-start(bf16[256,512]{1,0:T(8,128)(2,1)} %get-tuple-element.40), channel_id=1, source_target_pairs={{0,4},{4,0},{8,12},{12,8},{16,20},{20,16},{24,28},{28,24},{1,5},{5... | collective-permute-start | bytes 786440 | tf_op jit(solution)/shard_map/ppermute | solution.py:22
  5.9 2.0 collective-permute-start.18
  9.0 2.0 collective-permute-start.3
  18.9 2.1 collective-permute-start.21
  22.4 2.2 collective-permute-done.18
  24.6 2.1 collective-permute-start.15
  30.2 2.1 collective-permute-start.1
  33.6 2.2 collective-permute-done.3
  35.8 2.1 collective-permute-start.7
  41.3 2.1 collective-permute-start.19
  43.7 3.2 %collective-permute-done.21 = bf16[256,512]{1,0:T(8,128)(2,1)S(1)} collective-permute-done((bf16[256,512]{1,0:T(8,128)(2,1)}, bf16[256,512]{1,0:T(8,128)(2,1)S(1)}, u32[]{:S(2)}, u32[]{:S(2)}) %collective-permute-start.21) | collective-permute-done | bytes 262176 | tf_op jit(solution)/shard_map/ppermute | solution.py:22
  46.9 2.1 collective-permute-start.13
  58.9 2.9 %collective-permute-start.2 = (bf16[128,512]{1,0:T(8,128)(2,1)}, bf16[128,512]{1,0:T(8,128)(2,1)S(1)}, u32[]{:S(2)}, u32[]{:S(2)}) collective-permute-start(bf16[128,512]{1,0:T(8,128)(2,1)} %fusion), channel_id=1, source_target_pairs={{0,16},{16,0},{4,20},{20,4},{8,24},{24,8},{12,28},{28,12},{1,17},{... | collective-permute-start | bytes 393224 | tf_op jit(solution)/shard_map/ppermute | solution.py:22
  62.6 2.9 %collective-permute-start.20 = (bf16[128,512]{1,0:T(8,128)(2,1)S(1)}, bf16[128,512]{1,0:T(8,128)(2,1)S(1)}, u32[]{:S(2)}, u32[]{:S(2)}) collective-permute-start(bf16[128,512]{1,0:T(8,128)(2,1)S(1)} %fusion.6), channel_id=1, source_target_pairs={{0,16},{16,0},{4,20},{20,4},{8,24},{24,8},{12,28},{28,12},{1,17},{... | collective-permute-start | bytes 393224 | tf_op jit(solution)/shard_map/ppermute | solution.py:22
  65.8 3.2 %collective-permute-done.22 = bf16[128,512]{1,0:T(8,128)(2,1)S(1)} collective-permute-done((bf16[128,512]{1,0:T(8,128)(2,1)S(1)}, bf16[128,512]{1,0:T(8,128)(2,1)S(1)}, u32[]{:S(2)}, u32[]{:S(2)}) %collective-permute-start.22) | collective-permute-done | bytes 131104 | tf_op jit(solution)/shard_map/ppermute | solution.py:22
  72.6 17.7 %collective-permute-done.14 = bf16[128,512]{1,0:T(8,128)(2,1)S(1)} collective-permute-done((bf16[128,512]{1,0:T(8,128)(2,1)S(1)}, bf16[128,512]{1,0:T(8,128)(2,1)S(1)}, u32[]{:S(2)}, u32[]{:S(2)}) %collective-permute-start.14) | collective-permute-done | bytes 131104 | tf_op jit(solution)/shard_map/ppermute | solution.py:22
  90.3 2.0 pad_maximum_fusion.8.k_ref
  92.3 7.5 %collective-permute-done.17 = bf16[128,512]{1,0:T(8,128)(2,1)S(1)} collective-permute-done((bf16[128,512]{1,0:T(8,128)(2,1)S(1)}, bf16[128,512]{1,0:T(8,128)(2,1)S(1)}, u32[]{:S(2)}, u32[]{:S(2)}) %collective-permute-start.17) | collective-permute-done | bytes 131104 | tf_op jit(solution)/shard_map/ppermute | solution.py:22
  101.7 7.3 %shard_map.77 = (bf16[256,512]{1,0:T(8,128)(2,1)}, bf16[256,512]{1,0:T(8,128)(2,1)}, f32[768,512]{1,0:T(8,128)}, f32[768,512]{1,0:T(8,128)}) custom-call(f32[1,768]{1,0:T(1,128)} %constant.74.clone.1.bias_ref, bf16[256,2048]{1,0:T(8,128)(2,1)} %q_ref.7, bf16[256,2048]{1,0:T(8,128)(2,1)} %do_ref.7, bf16[768,512]{1,0:T(8,128)(2,1)} %pad_maximum_fusion.8.k_ref, ...), custom_call_target="tpu_custom_call" | custom-call | flops 1207959552 | bytes 5767168 | tf_op jit(solution)/shard_map/pallas_call | solution.py:61
  112.2 2.9 %collective-permute-start.23 = (bf16[128,512]{1,0:T(8,128)(2,1)S(1)}, bf16[128,512]{1,0:T(8,128)(2,1)S(1)}, u32[]{:S(2)}, u32[]{:S(2)}) collective-permute-start(bf16[128,512]{1,0:T(8,128)(2,1)S(1)} %fusion.7), channel_id=1, source_target_pairs={{0,16},{16,0},{4,20},{20,4},{8,24},{24,8},{12,28},{28,12},{1,17},{... | collective-permute-start | bytes 393224 | tf_op jit(solution)/shard_map/ppermute | solution.py:22
  115.1 2.0 pad_maximum_fusion.10.k_ref
  117.1 2.7 %collective-permute-done.23 = bf16[128,512]{1,0:T(8,128)(2,1)S(1)} collective-permute-done((bf16[128,512]{1,0:T(8,128)(2,1)S(1)}, bf16[128,512]{1,0:T(8,128)(2,1)S(1)}, u32[]{:S(2)}, u32[]{:S(2)}) %collective-permute-start.23) | collective-permute-done | bytes 131104 | tf_op jit(solution)/shard_map/ppermute | solution.py:22
  121.9 7.3 %shard_map.78 = (bf16[256,512]{1,0:T(8,128)(2,1)}, bf16[256,512]{1,0:T(8,128)(2,1)}, f32[768,512]{1,0:T(8,128)}, f32[768,512]{1,0:T(8,128)}) custom-call(f32[1,768]{1,0:T(1,128)} %constant.74.clone.1.bias_ref, bf16[256,2048]{1,0:T(8,128)(2,1)} %q_ref.7, bf16[256,2048]{1,0:T(8,128)(2,1)} %do_ref.7, bf16[768,512]{1,0:T(8,128)(2,1)} %pad_maximum_fusion.10.k_ref, ...), custom_call_target="tpu_custom_call" | custom-call | flops 1207959552 | bytes 5767168 | tf_op jit(solution)/shard_map/pallas_call | solution.py:61
  134.2 2.0 pad_maximum_fusion.6.k_ref
  138.3 7.3 %shard_map.76 = (bf16[256,512]{1,0:T(8,128)(2,1)}, bf16[256,512]{1,0:T(8,128)(2,1)}, f32[768,512]{1,0:T(8,128)}, f32[768,512]{1,0:T(8,128)}) custom-call(f32[1,768]{1,0:T(1,128)} %constant.74.clone.1.bias_ref, bf16[256,2048]{1,0:T(8,128)(2,1)} %q_ref.7, bf16[256,2048]{1,0:T(8,128)(2,1)} %do_ref.7, bf16[768,512]{1,0:T(8,128)(2,1)} %pad_maximum_fusion.6.k_ref, ...), custom_call_target="tpu_custom_call" | custom-call | flops 1207959552 | bytes 5767168 | tf_op jit(solution)/shard_map/pallas_call | solution.py:61
  150.6 2.0 pad_maximum_fusion.4.k_ref
  155.7 7.3 %shard_map.75 = (bf16[256,512]{1,0:T(8,128)(2,1)}, bf16[256,512]{1,0:T(8,128)(2,1)}, f32[768,512]{1,0:T(8,128)}, f32[768,512]{1,0:T(8,128)}) custom-call(f32[1,768]{1,0:T(1,128)} %constant.74.clone.1.bias_ref, bf16[256,2048]{1,0:T(8,128)(2,1)} %q_ref.7, bf16[256,2048]{1,0:T(8,128)(2,1)} %do_ref.7, bf16[768,512]{1,0:T(8,128)(2,1)} %pad_maximum_fusion.4.k_ref, ...), custom_call_target="tpu_custom_call" | custom-call | flops 1207959552 | bytes 5767168 | tf_op jit(solution)/shard_map/pallas_call | solution.py:61
  165.2 2.4 %pad_maximum_fusion = bf16[256,2048]{1,0:T(8,128)(2,1)} fusion(bf16[256,512]{1,0:T(8,128)(2,1)} %get-tuple-element.23, bf16[256,512]{1,0:T(8,128)(2,1)} %get-tuple-element.22, bf16[256,512]{1,0:T(8,128)(2,1)} %get-tuple-element.21, bf16[256,512]{1,0:T(8,128)(2,1)} %get-tuple-element.20), kind=kLoop, calls=%fused_computation.32 | loop fusion | flops 4194304 | bytes 2097152 | tf_op jit(solution)/shard_map/concatenate | solution.py:157
  214.6 3.7 %collective-permute-done.47 = bf16[256,512]{1,0:T(8,128)(2,1)S(1)} collective-permute-done((bf16[256,512]{1,0:T(8,128)(2,1)S(1)}, bf16[256,512]{1,0:T(8,128)(2,1)S(1)}, u32[]{:S(2)}, u32[]{:S(2)}) %collective-permute-start.47) | collective-permute-done | bytes 262176 | tf_op jit(solution)/shard_map/ppermute | solution.py:22
  219.7 4.3 %collective-permute-done.41 = bf16[256,512]{1,0:T(8,128)(2,1)S(1)} collective-permute-done((bf16[256,512]{1,0:T(8,128)(2,1)S(1)}, bf16[256,512]{1,0:T(8,128)(2,1)S(1)}, u32[]{:S(2)}, u32[]{:S(2)}) %collective-permute-start.41) | collective-permute-done | bytes 262176 | tf_op jit(solution)/shard_map/ppermute | solution.py:22
  225.3 4.3 %collective-permute-done.38 = bf16[256,512]{1,0:T(8,128)(2,1)S(1)} collective-permute-done((bf16[256,512]{1,0:T(8,128)(2,1)S(1)}, bf16[256,512]{1,0:T(8,128)(2,1)S(1)}, u32[]{:S(2)}, u32[]{:S(2)}) %collective-permute-start.38) | collective-permute-done | bytes 262176 | tf_op jit(solution)/shard_map/ppermute | solution.py:22
  (230 shorter events, 111.2 us)
Async XLA Ops:
  5.9 18.6 %collective-permute-start.18 = (bf16[256,512]{1,0:T(8,128)(2,1)}, bf16[256,512]{1,0:T(8,128)(2,1)}, u32[]{:S(2)}, u32[]{:S(2)}) collective-permute-start(bf16[256,512]{1,0:T(8,128)(2,1)} %get-tuple-element.42), channel_id=1, source_target_pairs={{0,4},{4,0},{8,12},{12,8},{16,20},{20,16},{24,28},{28,24},{1,5},{5... | collective-permute-start | bytes 786440 | tf_op jit(solution)/shard_map/ppermute | solution.py:22
  7.9 22.3 %collective-permute-start.12 = (bf16[256,512]{1,0:T(8,128)(2,1)}, bf16[256,512]{1,0:T(8,128)(2,1)}, u32[]{:S(2)}, u32[]{:S(2)}) collective-permute-start(bf16[256,512]{1,0:T(8,128)(2,1)} %get-tuple-element.43), channel_id=1, source_target_pairs={{0,4},{4,0},{8,12},{12,8},{16,20},{20,16},{24,28},{28,24},{1,5},{5... | collective-permute-start | bytes 786440 | tf_op jit(solution)/shard_map/ppermute | solution.py:22
  9.0 26.8 %collective-permute-start.3 = (bf16[256,512]{1,0:T(8,128)(2,1)}, bf16[256,512]{1,0:T(8,128)(2,1)}, u32[]{:S(2)}, u32[]{:S(2)}) collective-permute-start(bf16[256,512]{1,0:T(8,128)(2,1)} %get-tuple-element.36), channel_id=1, source_target_pairs={{0,4},{4,0},{8,12},{12,8},{16,20},{20,16},{24,28},{28,24},{1,5},{5... | collective-permute-start | bytes 786440 | tf_op jit(solution)/shard_map/ppermute | solution.py:22
  15.2 26.1 %collective-permute-start.9 = (bf16[256,512]{1,0:T(8,128)(2,1)}, bf16[256,512]{1,0:T(8,128)(2,1)S(1)}, u32[]{:S(2)}, u32[]{:S(2)}) collective-permute-start(bf16[256,512]{1,0:T(8,128)(2,1)} %get-tuple-element.37), channel_id=1, source_target_pairs={{0,4},{4,0},{8,12},{12,8},{16,20},{20,16},{24,28},{28,24},{1,5},{5... | collective-permute-start | bytes 786440 | tf_op jit(solution)/shard_map/ppermute | solution.py:22
  18.9 28.0 %collective-permute-start.21 = (bf16[256,512]{1,0:T(8,128)(2,1)}, bf16[256,512]{1,0:T(8,128)(2,1)S(1)}, u32[]{:S(2)}, u32[]{:S(2)}) collective-permute-start(bf16[256,512]{1,0:T(8,128)(2,1)} %get-tuple-element.38), channel_id=1, source_target_pairs={{0,4},{4,0},{8,12},{12,8},{16,20},{20,16},{24,28},{28,24},{1,5},{5... | collective-permute-start | bytes 786440 | tf_op jit(solution)/shard_map/ppermute | solution.py:22
  24.6 27.2 %collective-permute-start.15 = (bf16[256,512]{1,0:T(8,128)(2,1)}, bf16[256,512]{1,0:T(8,128)(2,1)S(1)}, u32[]{:S(2)}, u32[]{:S(2)}) collective-permute-start(bf16[256,512]{1,0:T(8,128)(2,1)} %get-tuple-element.39), channel_id=1, source_target_pairs={{0,4},{4,0},{8,12},{12,8},{16,20},{20,16},{24,28},{28,24},{1,5},{5... | collective-permute-start | bytes 786440 | tf_op jit(solution)/shard_map/ppermute | solution.py:22
  30.2 24.1 %collective-permute-start.1 = (bf16[128,512]{1,0:T(8,128)(2,1)S(1)}, bf16[128,512]{1,0:T(8,128)(2,1)S(1)}, u32[]{:S(2)}, u32[]{:S(2)}) collective-permute-start(bf16[128,512]{1,0:T(8,128)(2,1)S(1)} %get-tuple-element.56), channel_id=1, source_target_pairs={{0,8},{8,0},{4,12},{12,4},{16,24},{24,16},{20,28},{28,20},{1,9},{9... | collective-permute-start | bytes 393224 | tf_op jit(solution)/shard_map/ppermute | solution.py:22
  35.8 19.8 %collective-permute-start.7 = (bf16[128,512]{1,0:T(8,128)(2,1)S(1)}, bf16[128,512]{1,0:T(8,128)(2,1)S(1)}, u32[]{:S(2)}, u32[]{:S(2)}) collective-permute-start(bf16[128,512]{1,0:T(8,128)(2,1)S(1)} %get-tuple-element.52), channel_id=1, source_target_pairs={{0,8},{8,0},{4,12},{12,4},{16,24},{24,16},{20,28},{28,20},{1,9},{9... | collective-permute-start | bytes 393224 | tf_op jit(solution)/shard_map/ppermute | solution.py:22
  41.3 17.0 %collective-permute-start.19 = (bf16[128,512]{1,0:T(8,128)(2,1)S(1)}, bf16[128,512]{1,0:T(8,128)(2,1)S(1)}, u32[]{:S(2)}, u32[]{:S(2)}) collective-permute-start(bf16[128,512]{1,0:T(8,128)(2,1)S(1)} %get-tuple-element.44), channel_id=1, source_target_pairs={{0,8},{8,0},{4,12},{12,4},{16,24},{24,16},{20,28},{28,20},{1,9},{9... | collective-permute-start | bytes 393224 | tf_op jit(solution)/shard_map/ppermute | solution.py:22
  55.6 13.4 %collective-permute-start.22 = (bf16[128,512]{1,0:T(8,128)(2,1)S(1)}, bf16[128,512]{1,0:T(8,128)(2,1)S(1)}, u32[]{:S(2)}, u32[]{:S(2)}) collective-permute-start(bf16[128,512]{1,0:T(8,128)(2,1)S(1)} %get-tuple-element.46), channel_id=1, source_target_pairs={{0,8},{8,0},{4,12},{12,4},{16,24},{24,16},{20,28},{28,20},{1,9},{9... | collective-permute-start | bytes 393224 | tf_op jit(solution)/shard_map/ppermute | solution.py:22
  58.9 90.0 %collective-permute-start.2 = (bf16[128,512]{1,0:T(8,128)(2,1)}, bf16[128,512]{1,0:T(8,128)(2,1)S(1)}, u32[]{:S(2)}, u32[]{:S(2)}) collective-permute-start(bf16[128,512]{1,0:T(8,128)(2,1)} %fusion), channel_id=1, source_target_pairs={{0,16},{16,0},{4,20},{20,4},{8,24},{24,8},{12,28},{28,12},{1,17},{... | collective-permute-start | bytes 393224 | tf_op jit(solution)/shard_map/ppermute | solution.py:22
  62.1 70.4 %collective-permute-start.8 = (bf16[128,512]{1,0:T(8,128)(2,1)}, bf16[128,512]{1,0:T(8,128)(2,1)S(1)}, u32[]{:S(2)}, u32[]{:S(2)}) collective-permute-start(bf16[128,512]{1,0:T(8,128)(2,1)} %fusion.2), channel_id=1, source_target_pairs={{0,16},{16,0},{4,20},{20,4},{8,24},{24,8},{12,28},{28,12},{1,17},{... | collective-permute-start | bytes 393224 | tf_op jit(solution)/shard_map/ppermute | solution.py:22
  62.6 49.6 %collective-permute-start.20 = (bf16[128,512]{1,0:T(8,128)(2,1)S(1)}, bf16[128,512]{1,0:T(8,128)(2,1)S(1)}, u32[]{:S(2)}, u32[]{:S(2)}) collective-permute-start(bf16[128,512]{1,0:T(8,128)(2,1)S(1)} %fusion.6), channel_id=1, source_target_pairs={{0,16},{16,0},{4,20},{20,4},{8,24},{24,8},{12,28},{28,12},{1,17},{... | collective-permute-start | bytes 393224 | tf_op jit(solution)/shard_map/ppermute | solution.py:22
  69.0 21.3 %collective-permute-start.14 = (bf16[128,512]{1,0:T(8,128)(2,1)S(1)}, bf16[128,512]{1,0:T(8,128)(2,1)S(1)}, u32[]{:S(2)}, u32[]{:S(2)}) collective-permute-start(bf16[128,512]{1,0:T(8,128)(2,1)S(1)} %fusion.4), channel_id=1, source_target_pairs={{0,16},{16,0},{4,20},{20,4},{8,24},{24,8},{12,28},{28,12},{1,17},{... | collective-permute-start | bytes 393224 | tf_op jit(solution)/shard_map/ppermute | solution.py:22
  70.5 82.0 %collective-permute-start.5 = (bf16[128,512]{1,0:T(8,128)(2,1)S(1)}, bf16[128,512]{1,0:T(8,128)(2,1)S(1)}, u32[]{:S(2)}, u32[]{:S(2)}) collective-permute-start(bf16[128,512]{1,0:T(8,128)(2,1)S(1)} %fusion.1), channel_id=1, source_target_pairs={{0,16},{16,0},{4,20},{20,4},{8,24},{24,8},{12,28},{28,12},{1,17},{... | collective-permute-start | bytes 393224 | tf_op jit(solution)/shard_map/ppermute | solution.py:22
  99.8 36.4 %collective-permute-start.11 = (bf16[128,512]{1,0:T(8,128)(2,1)S(1)}, bf16[128,512]{1,0:T(8,128)(2,1)S(1)}, u32[]{:S(2)}, u32[]{:S(2)}) collective-permute-start(bf16[128,512]{1,0:T(8,128)(2,1)S(1)} %fusion.3), channel_id=1, source_target_pairs={{0,16},{16,0},{4,20},{20,4},{8,24},{24,8},{12,28},{28,12},{1,17},{... | collective-permute-start | bytes 393224 | tf_op jit(solution)/shard_map/ppermute | solution.py:22
  119.8 48.9 %collective-permute-start.42 = (bf16[128,512]{1,0:T(8,128)(2,1)}, bf16[128,512]{1,0:T(8,128)(2,1)}, u32[]{:S(2)}, u32[]{:S(2)}) collective-permute-start(bf16[128,512]{1,0:T(8,128)(2,1)} %slice.225), channel_id=1, source_target_pairs={{0,16},{16,0},{4,20},{20,4},{8,24},{24,8},{12,28},{28,12},{1,17},{... | collective-permute-start | bytes 393224 | tf_op jit(solution)/shard_map/ppermute | solution.py:22
  132.5 39.2 %collective-permute-start.30 = (bf16[128,512]{1,0:T(8,128)(2,1)}, bf16[128,512]{1,0:T(8,128)(2,1)}, u32[]{:S(2)}, u32[]{:S(2)}) collective-permute-start(bf16[128,512]{1,0:T(8,128)(2,1)} %slice.229), channel_id=1, source_target_pairs={{0,16},{16,0},{4,20},{20,4},{8,24},{24,8},{12,28},{28,12},{1,17},{... | collective-permute-start | bytes 393224 | tf_op jit(solution)/shard_map/ppermute | solution.py:22
  136.2 38.2 %collective-permute-start.45 = (bf16[128,512]{1,0:T(8,128)(2,1)}, bf16[128,512]{1,0:T(8,128)(2,1)S(1)}, u32[]{:S(2)}, u32[]{:S(2)}) collective-permute-start(bf16[128,512]{1,0:T(8,128)(2,1)} %slice.224), channel_id=1, source_target_pairs={{0,16},{16,0},{4,20},{20,4},{8,24},{24,8},{12,28},{28,12},{1,17},{... | collective-permute-start | bytes 393224 | tf_op jit(solution)/shard_map/ppermute | solution.py:22
  148.9 27.6 %collective-permute-start.33 = (bf16[128,512]{1,0:T(8,128)(2,1)}, bf16[128,512]{1,0:T(8,128)(2,1)}, u32[]{:S(2)}, u32[]{:S(2)}) collective-permute-start(bf16[128,512]{1,0:T(8,128)(2,1)} %slice.228), channel_id=1, source_target_pairs={{0,16},{16,0},{4,20},{20,4},{8,24},{24,8},{12,28},{28,12},{1,17},{... | collective-permute-start | bytes 393224 | tf_op jit(solution)/shard_map/ppermute | solution.py:22
  152.5 25.6 %collective-permute-start.39 = (bf16[128,512]{1,0:T(8,128)(2,1)}, bf16[128,512]{1,0:T(8,128)(2,1)S(1)}, u32[]{:S(2)}, u32[]{:S(2)}) collective-permute-start(bf16[128,512]{1,0:T(8,128)(2,1)} %slice.226), channel_id=1, source_target_pairs={{0,16},{16,0},{4,20},{20,4},{8,24},{24,8},{12,28},{28,12},{1,17},{... | collective-permute-start | bytes 393224 | tf_op jit(solution)/shard_map/ppermute | solution.py:22
  176.5 14.5 %collective-permute-start.43 = (bf16[128,512]{1,0:T(8,128)(2,1)S(1)}, bf16[128,512]{1,0:T(8,128)(2,1)S(1)}, u32[]{:S(2)}, u32[]{:S(2)}) collective-permute-start(bf16[128,512]{1,0:T(8,128)(2,1)S(1)} %add_convert_fusion.17), channel_id=1, source_target_pairs={{0,8},{8,0},{4,12},{12,4},{16,24},{24,16},{20,28},{28,20},{1,9},{9... | collective-permute-start | bytes 393224 | tf_op jit(solution)/shard_map/ppermute | solution.py:22
  180.4 18.2 %collective-permute-start.46 = (bf16[128,512]{1,0:T(8,128)(2,1)S(1)}, bf16[128,512]{1,0:T(8,128)(2,1)S(1)}, u32[]{:S(2)}, u32[]{:S(2)}) collective-permute-start(bf16[128,512]{1,0:T(8,128)(2,1)S(1)} %add_convert_fusion.16), channel_id=1, source_target_pairs={{0,8},{8,0},{4,12},{12,4},{16,24},{24,16},{20,28},{28,20},{1,9},{9... | collective-permute-start | bytes 393224 | tf_op jit(solution)/shard_map/ppermute | solution.py:22
  184.3 20.1 %collective-permute-start.40 = (bf16[128,512]{1,0:T(8,128)(2,1)S(1)}, bf16[128,512]{1,0:T(8,128)(2,1)S(1)}, u32[]{:S(2)}, u32[]{:S(2)}) collective-permute-start(bf16[128,512]{1,0:T(8,128)(2,1)S(1)} %add_convert_fusion.18), channel_id=1, source_target_pairs={{0,8},{8,0},{4,12},{12,4},{16,24},{24,16},{20,28},{28,20},{1,9},{9... | collective-permute-start | bytes 393224 | tf_op jit(solution)/shard_map/ppermute | solution.py:22
  186.7 15.1 %collective-permute-start.28 = (bf16[128,512]{1,0:T(8,128)(2,1)S(1)}, bf16[128,512]{1,0:T(8,128)(2,1)S(1)}, u32[]{:S(2)}, u32[]{:S(2)}) collective-permute-start(bf16[128,512]{1,0:T(8,128)(2,1)S(1)} %add_convert_fusion.22), channel_id=1, source_target_pairs={{0,8},{8,0},{4,12},{12,4},{16,24},{24,16},{20,28},{28,20},{1,9},{9... | collective-permute-start | bytes 393224 | tf_op jit(solution)/shard_map/ppermute | solution.py:22
  191.0 19.5 %collective-permute-start.37 = (bf16[128,512]{1,0:T(8,128)(2,1)S(1)}, bf16[128,512]{1,0:T(8,128)(2,1)S(1)}, u32[]{:S(2)}, u32[]{:S(2)}) collective-permute-start(bf16[128,512]{1,0:T(8,128)(2,1)S(1)} %add_convert_fusion.19), channel_id=1, source_target_pairs={{0,8},{8,0},{4,12},{12,4},{16,24},{24,16},{20,28},{28,20},{1,9},{9... | collective-permute-start | bytes 393224 | tf_op jit(solution)/shard_map/ppermute | solution.py:22
  198.6 15.1 %collective-permute-start.44 = (bf16[256,512]{1,0:T(8,128)(2,1)S(1)}, bf16[256,512]{1,0:T(8,128)(2,1)S(1)}, u32[]{:S(2)}, u32[]{:S(2)}) collective-permute-start(bf16[256,512]{1,0:T(8,128)(2,1)S(1)} %add_convert_fusion.3), channel_id=1, source_target_pairs={{0,4},{4,0},{8,12},{12,8},{16,20},{20,16},{24,28},{28,24},{1,5},{5... | collective-permute-start | bytes 786440 | tf_op jit(solution)/shard_map/ppermute | solution.py:22
  201.8 29.0 %collective-permute-start.32 = (bf16[256,512]{1,0:T(8,128)(2,1)S(1)}, bf16[256,512]{1,0:T(8,128)(2,1)S(1)}, u32[]{:S(2)}, u32[]{:S(2)}) collective-permute-start(bf16[256,512]{1,0:T(8,128)(2,1)S(1)} %add_convert_fusion.11), channel_id=1, source_target_pairs={{0,4},{4,0},{8,12},{12,8},{16,20},{20,16},{24,28},{28,24},{1,5},{5... | collective-permute-start | bytes 786440 | tf_op jit(solution)/shard_map/ppermute | solution.py:22
  204.4 14.0 %collective-permute-start.47 = (bf16[256,512]{1,0:T(8,128)(2,1)S(1)}, bf16[256,512]{1,0:T(8,128)(2,1)S(1)}, u32[]{:S(2)}, u32[]{:S(2)}) collective-permute-start(bf16[256,512]{1,0:T(8,128)(2,1)S(1)} %add_convert_fusion.1), channel_id=1, source_target_pairs={{0,4},{4,0},{8,12},{12,8},{16,20},{20,16},{24,28},{28,24},{1,5},{5... | collective-permute-start | bytes 786440 | tf_op jit(solution)/shard_map/ppermute | solution.py:22
  207.6 23.4 %collective-permute-start.35 = (bf16[256,512]{1,0:T(8,128)(2,1)S(1)}, bf16[256,512]{1,0:T(8,128)(2,1)S(1)}, u32[]{:S(2)}, u32[]{:S(2)}) collective-permute-start(bf16[256,512]{1,0:T(8,128)(2,1)S(1)} %add_convert_fusion.9), channel_id=1, source_target_pairs={{0,4},{4,0},{8,12},{12,8},{16,20},{20,16},{24,28},{28,24},{1,5},{5... | collective-permute-start | bytes 786440 | tf_op jit(solution)/shard_map/ppermute | solution.py:22
  210.5 13.5 %collective-permute-start.41 = (bf16[256,512]{1,0:T(8,128)(2,1)S(1)}, bf16[256,512]{1,0:T(8,128)(2,1)S(1)}, u32[]{:S(2)}, u32[]{:S(2)}) collective-permute-start(bf16[256,512]{1,0:T(8,128)(2,1)S(1)} %add_convert_fusion.5), channel_id=1, source_target_pairs={{0,4},{4,0},{8,12},{12,8},{16,20},{20,16},{24,28},{28,24},{1,5},{5... | collective-permute-start | bytes 786440 | tf_op jit(solution)/shard_map/ppermute | solution.py:22
  213.7 17.4 %collective-permute-start.29 = (bf16[256,512]{1,0:T(8,128)(2,1)S(1)}, bf16[256,512]{1,0:T(8,128)(2,1)S(1)}, u32[]{:S(2)}, u32[]{:S(2)}) collective-permute-start(bf16[256,512]{1,0:T(8,128)(2,1)S(1)} %add_convert_fusion.13), channel_id=1, source_target_pairs={{0,4},{4,0},{8,12},{12,8},{16,20},{20,16},{24,28},{28,24},{1,5},{5... | collective-permute-start | bytes 786440 | tf_op jit(solution)/shard_map/ppermute | solution.py:22
  (46 other events, 591.9 us)

commit v3 on v2

v3 whole, which is shorter than its diff:
```python
import functools
import math

import jax
import jax.numpy as jnp
from jax import lax
from jax.experimental import pallas as pl
from jax.sharding import PartitionSpec as P

HEAD_DIM = 128
POOLED = 128
CHUNKS = 4


def partner_2(block, axis, stride):
    count = lax.axis_size(axis)
    route = []
    for low in range(count):
        high = low | 1 << stride
        if high != low and high < count:
            route += [(low, high), (high, low)]
    return lax.ppermute(block, axis, route)


def attention_kernel(bias_ref, q_ref, do_ref, *refs, scale, parts):
    part_refs = refs[:parts]
    o_ref, dq_ref = refs[parts:parts + 2]
    grad_refs = refs[parts + 2:]
    q = q_ref[...]
    do = do_ref[...]
    k = jnp.concatenate([r[0] for r in part_refs], axis=0)
    v = jnp.concatenate([r[1] for r in part_refs], axis=0)
    scores = (
        lax.dot_general(q, k, (((1,), (1,)), ((), ())), preferred_element_type=jnp.float32) * scale
        + bias_ref[...]
    )
    row_max = jnp.max(scores, axis=-1, keepdims=True)
    log_total = row_max + jnp.log(jnp.sum(jnp.exp(scores - row_max), axis=-1, keepdims=True))
    weights = jnp.exp(scores - log_total)
    weights_low = weights.astype(jnp.bfloat16)
    attended = jnp.dot(weights_low, v, preferred_element_type=jnp.float32).astype(jnp.bfloat16)
    o_ref[...] = attended
    row_dot = jnp.sum(
        do.astype(jnp.float32) * attended.astype(jnp.float32), axis=-1, keepdims=True
    )
    weight_grad = lax.dot_general(do, v, (((1,), (1,)), ((), ())), preferred_element_type=jnp.float32)
    score_grad = (weights * (weight_grad - row_dot)).astype(jnp.bfloat16)
    dq_ref[...] = (
        jnp.dot(score_grad, k, preferred_element_type=jnp.float32) * scale
    ).astype(jnp.bfloat16)
    dk = jnp.dot(score_grad.T, q, preferred_element_type=jnp.float32) * scale
    dv = jnp.dot(weights_low.T, do, preferred_element_type=jnp.float32)
    first = 0
    for r in grad_refs:
        rows = r.shape[1]
        r[0] = dk[first:first + rows]
        r[1] = dv[first:first + rows]
        first += rows


def attention(query_rows, out_grad, parts, key_bias, score_scale, head_offset):
    leaf_rows = query_rows.shape[0]
    width = parts[0].shape[2]
    key_count = sum(p.shape[1] for p in parts)
    heads = width // HEAD_DIM
    row_in = pl.BlockSpec((leaf_rows, HEAD_DIM), lambda h: (0, h + head_offset))
    row_out = pl.BlockSpec((leaf_rows, HEAD_DIM), lambda h: (0, h))
    part_specs = [pl.BlockSpec((2, p.shape[1], HEAD_DIM), lambda h: (0, 0, h)) for p in parts]
    flops = 12 * leaf_rows * key_count * width
    io_bytes = 2 * (4 * leaf_rows + 2 * key_count) * width + 8 * key_count * width
    return pl.pallas_call(
        functools.partial(attention_kernel, scale=score_scale, parts=len(parts)),
        grid=(heads,),
        in_specs=[pl.BlockSpec((1, key_count), lambda h: (0, 0)), row_in, row_in] + part_specs,
        out_specs=[row_out, row_out] + part_specs,
        out_shape=[
            jax.ShapeDtypeStruct((leaf_rows, width), jnp.bfloat16),
            jax.ShapeDtypeStruct((leaf_rows, width), jnp.bfloat16),
        ] + [jax.ShapeDtypeStruct(p.shape, jnp.float32) for p in parts],
        cost_estimate=pl.CostEstimate(
            flops=flops, transcendentals=2 * leaf_rows * key_count * heads, bytes_accessed=io_bytes
        ),
    )(key_bias.reshape(1, key_count), query_rows, out_grad, *parts)


def placed_pool(rows_in, upper):
    run = rows_in // (POOLED // 2)
    out_row = lax.broadcasted_iota(jnp.int32, (POOLED, rows_in), 0)
    in_row = lax.broadcasted_iota(jnp.int32, (POOLED, rows_in), 1)
    offset = upper * (POOLED // 2)
    return jnp.where(out_row - offset == in_row // run, 1.0 / run, 0.0).astype(jnp.float32)


def apply(matrix, rows):
    return jnp.einsum(
        "pr,krw->kpw", matrix, rows.astype(jnp.float32), precision=lax.Precision.HIGHEST,
        preferred_element_type=jnp.float32,
    )


def body(query_rows, key_rows, value_rows, out_grad):
    leaf_rows, model_width = query_rows.shape
    seq_count = lax.axis_size("seq")
    levels = seq_count.bit_length() - 1
    position = lax.axis_index("seq")
    pool_ratio = leaf_rows // POOLED
    score_scale = HEAD_DIM ** (-0.5)
    chunk_width = model_width // CHUNKS
    bias_parts = [jnp.zeros((2 * leaf_rows,), jnp.float32)]
    for step_level in range(1, levels):
        bias_parts.append(jnp.full((POOLED,), math.log(pool_ratio * 2**step_level), jnp.float32))
    key_bias = jnp.concatenate(bias_parts, axis=0)
    bits = [position // 2**step_level % 2 for step_level in range(levels)]
    mine = [placed_pool(leaf_rows if s == 0 else POOLED, bits[s]) for s in range(levels)]
    other = [placed_pool(leaf_rows if s == 0 else POOLED, 1 - bits[s]) for s in range(levels)]
    pieces = [[], [], [], []]
    for chunk in range(CHUNKS):
        columns = slice(chunk * chunk_width, (chunk + 1) * chunk_width)
        own = jnp.stack((key_rows[:, columns], value_rows[:, columns]))
        sibling = partner_2(own, "seq", 0)
        summary = apply(mine[0], own) + apply(other[0], sibling)
        far = []
        for step_level in range(1, levels):
            partner = partner_2(summary.astype(jnp.bfloat16), "seq", step_level)
            far.append(partner)
            if step_level + 1 < levels:
                summary = apply(mine[step_level], summary) + apply(other[step_level], partner)
        outs = attention(
            query_rows, out_grad, [own, sibling] + far, key_bias, score_scale,
            chunk * (chunk_width // HEAD_DIM),
        )
        attended, query_grad, terms = outs[0], outs[1], outs[2:]
        grad = None
        for step_level in reversed(range(1, levels)):
            outgoing = terms[1 + step_level]
            if grad is not None:
                outgoing = outgoing + apply(other[step_level].T, grad)
            returned = partner_2(outgoing.astype(jnp.bfloat16), "seq", step_level)
            if grad is None:
                grad = returned.astype(jnp.float32)
            else:
                grad = apply(mine[step_level].T, grad) + returned
        to_sibling = terms[1]
        own_total = terms[0]
        if grad is not None:
            to_sibling = to_sibling + apply(other[0].T, grad)
            own_total = own_total + apply(mine[0].T, grad)
        from_sibling = partner_2(to_sibling.astype(jnp.bfloat16), "seq", 0)
        totals = own_total + from_sibling.astype(jnp.float32)
        for slot, piece in enumerate((attended, query_grad, totals[0], totals[1])):
            pieces[slot].append(piece)
    return tuple(jnp.concatenate(p, axis=1).astype(jnp.bfloat16) for p in pieces)


def solution(mesh):
    spec = P(("batch", "seq"), None)
    return jax.shard_map(
        body, mesh=mesh, in_specs=(spec, spec, spec, spec), out_specs=(spec, spec, spec, spec),
        check_vma=False,
    )
```

time: 235 us -> 200 us (0.85)
  waiting for transfers between devices: 60.1 us -> 91.2 us
  starting transfers between devices: 63.7 us -> 33.1 us
  matrix products: 43.5 us -> 24.3 us
  local copies, waits for them, and re-layouts: 15.2 us -> 5.73 us
  other arithmetic: 20.4 us -> 14.9 us
    ppermute x48 -> x24, waiting for transfers between devices: 60.1 us -> 91.2 us  [partner_2(): return lax.ppermute(block, axis, route)]
    ppermute x48 -> x24, starting transfers between devices: 63.7 us -> 33.1 us  [partner_2(): return lax.ppermute(block, axis, route)]
    dot_general x64 -> x32, matrix products: 43.5 us -> 24.3 us  [apply(): jnp.einsum('pr,krw->kpw', matrix, rows.astype(jnp.float32), precision=lax...]
    slice x10 -> x0, local copies, waits for them, and re-layouts: 15.1 us -> none  [the longest x8 11.8 us: body(): outgoing = [terms[i][first:first + POOLED] for i in range(2)]]
    concatenate x8 -> x0, other arithmetic: 13.5 us -> none  [the longest x4 7.84 us: body(): keys = jnp.concatenate([own[0], sibling[0]] + [f[0] for f in far], axis=0)]
    convert_element_type x0 -> x12, other arithmetic: none -> 5.69 us  [the longest x8 4.67 us: body(): returned = partner_2(outgoing.astype(jnp.bfloat16), 'seq', step_level)]
    unnamed x60 -> x56, local copies, waits for them, and re-layouts: 0.12 us -> 3.84 us
    another operation x8, other arithmetic: 1.14 us -> 3.76 us  [the longest x4 2.57 us: body(): own = jnp.stack((key_rows[:, columns], value_rows[:, columns]))]
  transfers between devices with their start and end apart: 48 -> 24, of which waited for: 17 -> 14; matrix products, arithmetic and copies ran while one was open for 32% -> 18% of each run, Pallas kernels for 12% -> 14%
where the time goes in v3:
time: 200 us; the launch traced here: 199 us
  waiting for transfers between devices  91.2 us (46%)
  starting transfers between devices  33.1 us (17%)
  Pallas kernels  28.8 us (14%)
  matrix products  24.3 us (12%)
  other arithmetic  14.9 us (7%)
  local copies, waits for them, and re-layouts  5.73 us (3%)
    ppermute x24, waiting for transfers between devices, partner_2(): return lax.ppermute(block, axis, route)  91.2 us
    ppermute x24, starting transfers between devices, partner_2(): return lax.ppermute(block, axis, route)  33.1 us
    pallas_call x4, Pallas kernels, attention(): pl.pallas_call(functools.partial(attention_kernel, scale=score_scale, par...  28.8 us
    dot_general x32, matrix products, apply(): jnp.einsum('pr,krw->kpw', matrix, rows.astype(jnp.float32), precision=lax...  24.3 us
    concatenate x4, other arithmetic, body(): jnp.concatenate(p, axis=1).astype(jnp.bfloat16)  5.42 us
    convert_element_type x8, other arithmetic, body(): returned = partner_2(outgoing.astype(jnp.bfloat16), 'seq', step_level)  4.67 us
  transfers between devices with their start and end apart: 24, of which 14 were waited for; matrix products, arithmetic and copies ran while one was open for 18% of the time, Pallas kernels for 14%

profile of v3, /device:TPU:0, one launch (start us, length us, event | category | flops | bytes accessed | tf_op | source)
XLA Modules:
  0.0 199.4 jit_solution(3189818381937373199)
XLA Ops:
  0.6 1.7 slice_bitcast_fusion.14
  3.2 3.0 %collective-permute-start = (bf16[2,256,512]{2,1,0:T(8,128)(2,1)}, bf16[2,256,512]{2,1,0:T(8,128)(2,1)}, u32[]{:S(2)}, u32[]{:S(2)}) collective-permute-start(bf16[2,256,512]{2,1,0:T(8,128)(2,1)} %pad_maximum_fusion.4.refs_0_), channel_id=1, source_target_pairs={{0,4},{4,0},{8,12},{12,8},{16,20},{20,16},{24,28},{28,24},{1,5},{5... | collective-permute-start | bytes 1572872 | tf_op jit(solution)/shard_map/ppermute | solution.py:22
  7.9 2.0 %collective-permute-start.6 = (bf16[2,256,512]{2,1,0:T(8,128)(2,1)}, bf16[2,256,512]{2,1,0:T(8,128)(2,1)}, u32[]{:S(2)}, u32[]{:S(2)}) collective-permute-start(bf16[2,256,512]{2,1,0:T(8,128)(2,1)} %pad_maximum_fusion.6.refs_0_), channel_id=1, source_target_pairs={{0,4},{4,0},{8,12},{12,8},{16,20},{20,16},{24,28},{28,24},{1,5},{5... | collective-permute-start | bytes 1572872 | tf_op jit(solution)/shard_map/ppermute | solution.py:22
  11.9 7.4 %collective-permute-done.refs_1_ = bf16[2,256,512]{2,1,0:T(8,128)(2,1)} collective-permute-done((bf16[2,256,512]{2,1,0:T(8,128)(2,1)}, bf16[2,256,512]{2,1,0:T(8,128)(2,1)}, u32[]{:S(2)}, u32[]{:S(2)}) %collective-permute-start) | collective-permute-done | bytes 524320 | tf_op jit(solution)/shard_map/ppermute | solution.py:22
  20.7 2.2 %collective-permute-start.1 = (bf16[2,128,512]{2,1,0:T(8,128)(2,1)S(1)}, bf16[2,128,512]{2,1,0:T(8,128)(2,1)S(1)}, u32[]{:S(2)}, u32[]{:S(2)}) collective-permute-start(bf16[2,128,512]{2,1,0:T(8,128)(2,1)S(1)} %get-tuple-element.74), channel_id=1, source_target_pairs={{0,8},{8,0},{4,12},{12,4},{16,24},{24,16},{20,28},{28,20},{1,9},{9... | collective-permute-start | bytes 786440 | tf_op jit(solution)/shard_map/ppermute | solution.py:22
  22.9 7.6 %collective-permute-done.3.refs_1_ = bf16[2,256,512]{2,1,0:T(8,128)(2,1)} collective-permute-done((bf16[2,256,512]{2,1,0:T(8,128)(2,1)}, bf16[2,256,512]{2,1,0:T(8,128)(2,1)}, u32[]{:S(2)}, u32[]{:S(2)}) %collective-permute-start.3) | collective-permute-done | bytes 524320 | tf_op jit(solution)/shard_map/ppermute | solution.py:22
  32.0 2.2 %collective-permute-start.4 = (bf16[2,128,512]{2,1,0:T(8,128)(2,1)S(1)}, bf16[2,128,512]{2,1,0:T(8,128)(2,1)S(1)}, u32[]{:S(2)}, u32[]{:S(2)}) collective-permute-start(bf16[2,128,512]{2,1,0:T(8,128)(2,1)S(1)} %get-tuple-element.72), channel_id=1, source_target_pairs={{0,8},{8,0},{4,12},{12,4},{16,24},{24,16},{20,28},{28,20},{1,9},{9... | collective-permute-start | bytes 786440 | tf_op jit(solution)/shard_map/ppermute | solution.py:22
  34.2 7.6 %collective-permute-done.6.refs_1_ = bf16[2,256,512]{2,1,0:T(8,128)(2,1)} collective-permute-done((bf16[2,256,512]{2,1,0:T(8,128)(2,1)}, bf16[2,256,512]{2,1,0:T(8,128)(2,1)}, u32[]{:S(2)}, u32[]{:S(2)}) %collective-permute-start.6) | collective-permute-done | bytes 524320 | tf_op jit(solution)/shard_map/ppermute | solution.py:22
  43.2 2.2 %collective-permute-start.7 = (bf16[2,128,512]{2,1,0:T(8,128)(2,1)S(1)}, bf16[2,128,512]{2,1,0:T(8,128)(2,1)S(1)}, u32[]{:S(2)}, u32[]{:S(2)}) collective-permute-start(bf16[2,128,512]{2,1,0:T(8,128)(2,1)S(1)} %get-tuple-element.70), channel_id=1, source_target_pairs={{0,8},{8,0},{4,12},{12,4},{16,24},{24,16},{20,28},{28,20},{1,9},{9... | collective-permute-start | bytes 786440 | tf_op jit(solution)/shard_map/ppermute | solution.py:22
  47.2 4.9 %collective-permute-done.9.refs_1_ = bf16[2,256,512]{2,1,0:T(8,128)(2,1)} collective-permute-done((bf16[2,256,512]{2,1,0:T(8,128)(2,1)S(1)}, bf16[2,256,512]{2,1,0:T(8,128)(2,1)}, u32[]{:S(2)}, u32[]{:S(2)}) %collective-permute-start.9) | collective-permute-done | bytes 524320 | tf_op jit(solution)/shard_map/ppermute | solution.py:22
  54.2 1.9 collective-permute-start.10
  56.5 2.7 %collective-permute-start.2 = (bf16[2,128,512]{2,1,0:T(8,128)(2,1)S(1)}, bf16[2,128,512]{2,1,0:T(8,128)(2,1)S(1)}, u32[]{:S(2)}, u32[]{:S(2)}) collective-permute-start(bf16[2,128,512]{2,1,0:T(8,128)(2,1)S(1)} %fusion.15), channel_id=1, source_target_pairs={{0,16},{16,0},{4,20},{20,4},{8,24},{24,8},{12,28},{28,12},{1,17},{... | collective-permute-start | bytes 786440 | tf_op jit(solution)/shard_map/ppermute | solution.py:22
  60.5 2.7 %collective-permute-start.8 = (bf16[2,128,512]{2,1,0:T(8,128)(2,1)S(1)}, bf16[2,128,512]{2,1,0:T(8,128)(2,1)S(1)}, u32[]{:S(2)}, u32[]{:S(2)}) collective-permute-start(bf16[2,128,512]{2,1,0:T(8,128)(2,1)S(1)} %fusion.13), channel_id=1, source_target_pairs={{0,16},{16,0},{4,20},{20,4},{8,24},{24,8},{12,28},{28,12},{1,17},{... | collective-permute-start | bytes 786440 | tf_op jit(solution)/shard_map/ppermute | solution.py:22
  63.1 3.7 %collective-permute-done.10.refs_2_ = bf16[2,128,512]{2,1,0:T(8,128)(2,1)S(1)} collective-permute-done((bf16[2,128,512]{2,1,0:T(8,128)(2,1)S(1)}, bf16[2,128,512]{2,1,0:T(8,128)(2,1)S(1)}, u32[]{:S(2)}, u32[]{:S(2)}) %collective-permute-start.10) | collective-permute-done | bytes 262176 | tf_op jit(solution)/shard_map/ppermute | solution.py:22
  67.8 24.3 %collective-permute-done.2.refs_3_ = bf16[2,128,512]{2,1,0:T(8,128)(2,1)S(1)} collective-permute-done((bf16[2,128,512]{2,1,0:T(8,128)(2,1)S(1)}, bf16[2,128,512]{2,1,0:T(8,128)(2,1)S(1)}, u32[]{:S(2)}, u32[]{:S(2)}) %collective-permute-start.2) | collective-permute-done | bytes 262176 | tf_op jit(solution)/shard_map/ppermute | solution.py:22
  92.7 7.3 %shard_map.75 = (bf16[256,512]{1,0:T(8,128)(2,1)}, bf16[256,512]{1,0:T(8,128)(2,1)}, f32[2,256,512]{2,1,0:T(8,128)}, f32[2,256,512]{2,1,0:T(8,128)}, f32[2,128,512]{2,1,0:T(8,128)}, /*index=5*/f32[2,128,512]{2,1,0:T(8,128)}) custom-call(f32[1,768]{1,0:T(1,128)} %constant.74.clone.1.bias_ref, bf16[256,2048]{1,0:T(8,128)(2,1)} %q_ref.7, ...), custom_call_target="tpu_custom_call" | custom-call | flops 1207959552 | bytes 5767168 | tf_op jit(solution)/shard_map/pallas_call | solution.py:71
  102.0 7.2 %shard_map.76 = (bf16[256,512]{1,0:T(8,128)(2,1)}, bf16[256,512]{1,0:T(8,128)(2,1)}, f32[2,256,512]{2,1,0:T(8,128)}, f32[2,256,512]{2,1,0:T(8,128)}, f32[2,128,512]{2,1,0:T(8,128)}, /*index=5*/f32[2,128,512]{2,1,0:T(8,128)}) custom-call(f32[1,768]{1,0:T(1,128)} %constant.74.clone.1.bias_ref, bf16[256,2048]{1,0:T(8,128)(2,1)} %q_ref.7, ...), custom_call_target="tpu_custom_call" | custom-call | flops 1207959552 | bytes 5767168 | tf_op jit(solution)/shard_map/pallas_call | solution.py:71
  110.2 3.0 %collective-permute-start.15 = (bf16[2,128,512]{2,1,0:T(8,128)(2,1)S(1)}, bf16[2,128,512]{2,1,0:T(8,128)(2,1)S(1)}, u32[]{:S(2)}, u32[]{:S(2)}) collective-permute-start(bf16[2,128,512]{2,1,0:T(8,128)(2,1)S(1)} %convert_element_type.131), channel_id=1, source_target_pairs={{0,16},{16,0},{4,20},{20,4},{8,24},{24,8},{12,28},{28,12},{1,17},{... | collective-permute-start | bytes 786440 | tf_op jit(solution)/shard_map/ppermute | solution.py:22
  113.9 7.2 %shard_map.77 = (bf16[256,512]{1,0:T(8,128)(2,1)}, bf16[256,512]{1,0:T(8,128)(2,1)}, f32[2,256,512]{2,1,0:T(8,128)}, f32[2,256,512]{2,1,0:T(8,128)}, f32[2,128,512]{2,1,0:T(8,128)}, /*index=5*/f32[2,128,512]{2,1,0:T(8,128)}) custom-call(f32[1,768]{1,0:T(1,128)} %constant.74.clone.1.bias_ref, bf16[256,2048]{1,0:T(8,128)(2,1)} %q_ref.7, ...), custom_call_target="tpu_custom_call" | custom-call | flops 1207959552 | bytes 5767168 | tf_op jit(solution)/shard_map/pallas_call | solution.py:71
  123.0 7.1 %shard_map.78 = (bf16[256,512]{1,0:T(8,128)(2,1)}, bf16[256,512]{1,0:T(8,128)(2,1)}, f32[2,256,512]{2,1,0:T(8,128)}, f32[2,256,512]{2,1,0:T(8,128)}, f32[2,128,512]{2,1,0:T(8,128)}, /*index=5*/f32[2,128,512]{2,1,0:T(8,128)}) custom-call(f32[1,768]{1,0:T(1,128)} %constant.74.clone.1.bias_ref, bf16[256,2048]{1,0:T(8,128)(2,1)} %q_ref.7, ...), custom_call_target="tpu_custom_call" | custom-call | flops 1207959552 | bytes 5767168 | tf_op jit(solution)/shard_map/pallas_call | solution.py:71
  131.2 3.0 %collective-permute-start.21 = (bf16[2,128,512]{2,1,0:T(8,128)(2,1)S(1)}, bf16[2,128,512]{2,1,0:T(8,128)(2,1)S(1)}, u32[]{:S(2)}, u32[]{:S(2)}) collective-permute-start(bf16[2,128,512]{2,1,0:T(8,128)(2,1)S(1)} %convert_element_type.141), channel_id=1, source_target_pairs={{0,16},{16,0},{4,20},{20,4},{8,24},{24,8},{12,28},{28,12},{1,17},{... | collective-permute-start | bytes 786440 | tf_op jit(solution)/shard_map/ppermute | solution.py:22
  134.2 2.1 %pad_maximum_fusion.1 = bf16[256,2048]{1,0:T(8,128)(2,1)} fusion(bf16[256,512]{1,0:T(8,128)(2,1)} %get-tuple-element.35, bf16[256,512]{1,0:T(8,128)(2,1)S(1)} %copy-done.22, bf16[256,512]{1,0:T(8,128)(2,1)S(1)} %copy-done.20, bf16[256,512]{1,0:T(8,128)(2,1)S(1)} %copy-done.18), kind=kLoop, calls=%fused_computation.41 | loop fusion | flops 4194304 | bytes 2097152 | tf_op jit(solution)/shard_map/concatenate | solution.py:152
  139.1 1.7 collective-permute-start.16
  140.8 4.7 %collective-permute-done.18 = bf16[2,128,512]{2,1,0:T(8,128)(2,1)S(1)} collective-permute-done((bf16[2,128,512]{2,1,0:T(8,128)(2,1)S(1)}, bf16[2,128,512]{2,1,0:T(8,128)(2,1)S(1)}, u32[]{:S(2)}, u32[]{:S(2)}) %collective-permute-start.18) | collective-permute-done | bytes 262176 | tf_op jit(solution)/shard_map/ppermute | solution.py:22
  146.2 2.6 %collective-permute-done.21 = bf16[2,128,512]{2,1,0:T(8,128)(2,1)S(1)} collective-permute-done((bf16[2,128,512]{2,1,0:T(8,128)(2,1)S(1)}, bf16[2,128,512]{2,1,0:T(8,128)(2,1)S(1)}, u32[]{:S(2)}, u32[]{:S(2)}) %collective-permute-start.21) | collective-permute-done | bytes 262176 | tf_op jit(solution)/shard_map/ppermute | solution.py:22
  149.5 4.1 %collective-permute-done.13 = bf16[2,128,512]{2,1,0:T(8,128)(2,1)S(1)} collective-permute-done((bf16[2,128,512]{2,1,0:T(8,128)(2,1)S(1)}, bf16[2,128,512]{2,1,0:T(8,128)(2,1)S(1)}, u32[]{:S(2)}, u32[]{:S(2)}) %collective-permute-start.13) | collective-permute-done | bytes 262176 | tf_op jit(solution)/shard_map/ppermute | solution.py:22
  155.6 1.6 collective-permute-start.14
  157.2 2.1 %collective-permute-done.16 = bf16[2,128,512]{2,1,0:T(8,128)(2,1)S(1)} collective-permute-done((bf16[2,128,512]{2,1,0:T(8,128)(2,1)S(1)}, bf16[2,128,512]{2,1,0:T(8,128)(2,1)S(1)}, u32[]{:S(2)}, u32[]{:S(2)}) %collective-permute-start.16) | collective-permute-done | bytes 262176 | tf_op jit(solution)/shard_map/ppermute | solution.py:22
  166.2 1.6 collective-permute-start.20
  174.1 7.6 %collective-permute-done.17 = bf16[2,256,512]{2,1,0:T(8,128)(2,1)S(1)} collective-permute-done((bf16[2,256,512]{2,1,0:T(8,128)(2,1)S(1)}, bf16[2,256,512]{2,1,0:T(8,128)(2,1)S(1)}, u32[]{:S(2)}, u32[]{:S(2)}) %collective-permute-start.17) | collective-permute-done | bytes 524320 | tf_op jit(solution)/shard_map/ppermute | solution.py:22
  182.1 9.1 %collective-permute-done.20 = bf16[2,256,512]{2,1,0:T(8,128)(2,1)S(1)} collective-permute-done((bf16[2,256,512]{2,1,0:T(8,128)(2,1)S(1)}, bf16[2,256,512]{2,1,0:T(8,128)(2,1)S(1)}, u32[]{:S(2)}, u32[]{:S(2)}) %collective-permute-start.20) | collective-permute-done | bytes 524320 | tf_op jit(solution)/shard_map/ppermute | solution.py:22
  191.6 5.3 %collective-permute-done.23 = bf16[2,256,512]{2,1,0:T(8,128)(2,1)S(1)} collective-permute-done((bf16[2,256,512]{2,1,0:T(8,128)(2,1)S(1)}, bf16[2,256,512]{2,1,0:T(8,128)(2,1)S(1)}, u32[]{:S(2)}, u32[]{:S(2)}) %collective-permute-start.23) | collective-permute-done | bytes 524320 | tf_op jit(solution)/shard_map/ppermute | solution.py:22
  (145 shorter events, 44.9 us)
Async XLA Ops:
  3.2 16.0 %collective-permute-start = (bf16[2,256,512]{2,1,0:T(8,128)(2,1)}, bf16[2,256,512]{2,1,0:T(8,128)(2,1)}, u32[]{:S(2)}, u32[]{:S(2)}) collective-permute-start(bf16[2,256,512]{2,1,0:T(8,128)(2,1)} %pad_maximum_fusion.4.refs_0_), channel_id=1, source_target_pairs={{0,4},{4,0},{8,12},{12,8},{16,20},{20,16},{24,28},{28,24},{1,5},{5... | collective-permute-start | bytes 1572872 | tf_op jit(solution)/shard_map/ppermute | solution.py:22
  7.0 23.5 %collective-permute-start.3 = (bf16[2,256,512]{2,1,0:T(8,128)(2,1)}, bf16[2,256,512]{2,1,0:T(8,128)(2,1)}, u32[]{:S(2)}, u32[]{:S(2)}) collective-permute-start(bf16[2,256,512]{2,1,0:T(8,128)(2,1)} %pad_maximum_fusion.5.refs_0_), channel_id=1, source_target_pairs={{0,4},{4,0},{8,12},{12,8},{16,20},{20,16},{24,28},{28,24},{1,5},{5... | collective-permute-start | bytes 1572872 | tf_op jit(solution)/shard_map/ppermute | solution.py:22
  7.9 33.9 %collective-permute-start.6 = (bf16[2,256,512]{2,1,0:T(8,128)(2,1)}, bf16[2,256,512]{2,1,0:T(8,128)(2,1)}, u32[]{:S(2)}, u32[]{:S(2)}) collective-permute-start(bf16[2,256,512]{2,1,0:T(8,128)(2,1)} %pad_maximum_fusion.6.refs_0_), channel_id=1, source_target_pairs={{0,4},{4,0},{8,12},{12,8},{16,20},{20,16},{24,28},{28,24},{1,5},{5... | collective-permute-start | bytes 1572872 | tf_op jit(solution)/shard_map/ppermute | solution.py:22
  10.0 42.2 %collective-permute-start.9 = (bf16[2,256,512]{2,1,0:T(8,128)(2,1)S(1)}, bf16[2,256,512]{2,1,0:T(8,128)(2,1)}, u32[]{:S(2)}, u32[]{:S(2)}) collective-permute-start(bf16[2,256,512]{2,1,0:T(8,128)(2,1)S(1)} %pad_maximum_fusion.7.refs_0_), channel_id=1, source_target_pairs={{0,4},{4,0},{8,12},{12,8},{16,20},{20,16},{24,28},{28,24},{1,5},{5... | collective-permute-start | bytes 1572872 | tf_op jit(solution)/shard_map/ppermute | solution.py:22
  20.7 35.4 %collective-permute-start.1 = (bf16[2,128,512]{2,1,0:T(8,128)(2,1)S(1)}, bf16[2,128,512]{2,1,0:T(8,128)(2,1)S(1)}, u32[]{:S(2)}, u32[]{:S(2)}) collective-permute-start(bf16[2,128,512]{2,1,0:T(8,128)(2,1)S(1)} %get-tuple-element.74), channel_id=1, source_target_pairs={{0,8},{8,0},{4,12},{12,4},{16,24},{24,16},{20,28},{28,20},{1,9},{9... | collective-permute-start | bytes 786440 | tf_op jit(solution)/shard_map/ppermute | solution.py:22
  32.0 27.2 %collective-permute-start.4 = (bf16[2,128,512]{2,1,0:T(8,128)(2,1)S(1)}, bf16[2,128,512]{2,1,0:T(8,128)(2,1)S(1)}, u32[]{:S(2)}, u32[]{:S(2)}) collective-permute-start(bf16[2,128,512]{2,1,0:T(8,128)(2,1)S(1)} %get-tuple-element.72), channel_id=1, source_target_pairs={{0,8},{8,0},{4,12},{12,4},{16,24},{24,16},{20,28},{28,20},{1,9},{9... | collective-permute-start | bytes 786440 | tf_op jit(solution)/shard_map/ppermute | solution.py:22
  43.2 16.8 %collective-permute-start.7 = (bf16[2,128,512]{2,1,0:T(8,128)(2,1)S(1)}, bf16[2,128,512]{2,1,0:T(8,128)(2,1)S(1)}, u32[]{:S(2)}, u32[]{:S(2)}) collective-permute-start(bf16[2,128,512]{2,1,0:T(8,128)(2,1)S(1)} %get-tuple-element.70), channel_id=1, source_target_pairs={{0,8},{8,0},{4,12},{12,4},{16,24},{24,16},{20,28},{28,20},{1,9},{9... | collective-permute-start | bytes 786440 | tf_op jit(solution)/shard_map/ppermute | solution.py:22
  54.2 12.6 %collective-permute-start.10 = (bf16[2,128,512]{2,1,0:T(8,128)(2,1)S(1)}, bf16[2,128,512]{2,1,0:T(8,128)(2,1)S(1)}, u32[]{:S(2)}, u32[]{:S(2)}) collective-permute-start(bf16[2,128,512]{2,1,0:T(8,128)(2,1)S(1)} %get-tuple-element.68), channel_id=1, source_target_pairs={{0,8},{8,0},{4,12},{12,4},{16,24},{24,16},{20,28},{28,20},{1,9},{9... | collective-permute-start | bytes 786440 | tf_op jit(solution)/shard_map/ppermute | solution.py:22
  56.5 35.5 %collective-permute-start.2 = (bf16[2,128,512]{2,1,0:T(8,128)(2,1)S(1)}, bf16[2,128,512]{2,1,0:T(8,128)(2,1)S(1)}, u32[]{:S(2)}, u32[]{:S(2)}) collective-permute-start(bf16[2,128,512]{2,1,0:T(8,128)(2,1)S(1)} %fusion.15), channel_id=1, source_target_pairs={{0,16},{16,0},{4,20},{20,4},{8,24},{24,8},{12,28},{28,12},{1,17},{... | collective-permute-start | bytes 786440 | tf_op jit(solution)/shard_map/ppermute | solution.py:22
  59.6 41.6 %collective-permute-start.5 = (bf16[2,128,512]{2,1,0:T(8,128)(2,1)S(1)}, bf16[2,128,512]{2,1,0:T(8,128)(2,1)S(1)}, u32[]{:S(2)}, u32[]{:S(2)}) collective-permute-start(bf16[2,128,512]{2,1,0:T(8,128)(2,1)S(1)} %fusion.14), channel_id=1, source_target_pairs={{0,16},{16,0},{4,20},{20,4},{8,24},{24,8},{12,28},{28,12},{1,17},{... | collective-permute-start | bytes 786440 | tf_op jit(solution)/shard_map/ppermute | solution.py:22
  60.0 7.2 %copy-start.13 = (bf16[2,128,512]{2,1,0:T(8,128)(2,1)}, bf16[2,128,512]{2,1,0:T(8,128)(2,1)S(1)}, u32[]{:S(2)}) copy-start(bf16[2,128,512]{2,1,0:T(8,128)(2,1)S(1)} %collective-permute-done.7.refs_2_) | copy-start | bytes 786436
  60.5 52.7 %collective-permute-start.8 = (bf16[2,128,512]{2,1,0:T(8,128)(2,1)S(1)}, bf16[2,128,512]{2,1,0:T(8,128)(2,1)S(1)}, u32[]{:S(2)}, u32[]{:S(2)}) collective-permute-start(bf16[2,128,512]{2,1,0:T(8,128)(2,1)S(1)} %fusion.13), channel_id=1, source_target_pairs={{0,16},{16,0},{4,20},{20,4},{8,24},{24,8},{12,28},{28,12},{1,17},{... | collective-permute-start | bytes 786440 | tf_op jit(solution)/shard_map/ppermute | solution.py:22
  66.8 33.3 %copy-start.14 = (bf16[2,128,512]{2,1,0:T(8,128)(2,1)}, bf16[2,128,512]{2,1,0:T(8,128)(2,1)S(1)}, u32[]{:S(2)}) copy-start(bf16[2,128,512]{2,1,0:T(8,128)(2,1)S(1)} %collective-permute-done.10.refs_2_) | copy-start | bytes 786436
  67.2 55.0 %collective-permute-start.11 = (bf16[2,128,512]{2,1,0:T(8,128)(2,1)S(1)}, bf16[2,128,512]{2,1,0:T(8,128)(2,1)S(1)}, u32[]{:S(2)}, u32[]{:S(2)}) collective-permute-start(bf16[2,128,512]{2,1,0:T(8,128)(2,1)S(1)} %fusion.12), channel_id=1, source_target_pairs={{0,16},{16,0},{4,20},{20,4},{8,24},{24,8},{12,28},{28,12},{1,17},{... | collective-permute-start | bytes 786440 | tf_op jit(solution)/shard_map/ppermute | solution.py:22
  101.2 36.3 %collective-permute-start.12 = (bf16[2,128,512]{2,1,0:T(8,128)(2,1)S(1)}, bf16[2,128,512]{2,1,0:T(8,128)(2,1)S(1)}, u32[]{:S(2)}, u32[]{:S(2)}) collective-permute-start(bf16[2,128,512]{2,1,0:T(8,128)(2,1)S(1)} %convert_element_type.126), channel_id=1, source_target_pairs={{0,16},{16,0},{4,20},{20,4},{8,24},{24,8},{12,28},{28,12},{1,17},{... | collective-permute-start | bytes 786440 | tf_op jit(solution)/shard_map/ppermute | solution.py:22
  110.2 27.9 %collective-permute-start.15 = (bf16[2,128,512]{2,1,0:T(8,128)(2,1)S(1)}, bf16[2,128,512]{2,1,0:T(8,128)(2,1)S(1)}, u32[]{:S(2)}, u32[]{:S(2)}) collective-permute-start(bf16[2,128,512]{2,1,0:T(8,128)(2,1)S(1)} %convert_element_type.131), channel_id=1, source_target_pairs={{0,16},{16,0},{4,20},{20,4},{8,24},{24,8},{12,28},{28,12},{1,17},{... | collective-permute-start | bytes 786440 | tf_op jit(solution)/shard_map/ppermute | solution.py:22
  122.1 12.0 %copy-start.18 = (bf16[256,512]{1,0:T(8,128)(2,1)S(1)}, bf16[256,512]{1,0:T(8,128)(2,1)}, u32[]{:S(2)}) copy-start(bf16[256,512]{1,0:T(8,128)(2,1)} %get-tuple-element.32) | copy-start | bytes 786436
  122.1 12.0 %copy-start.20 = (bf16[256,512]{1,0:T(8,128)(2,1)S(1)}, bf16[256,512]{1,0:T(8,128)(2,1)}, u32[]{:S(2)}) copy-start(bf16[256,512]{1,0:T(8,128)(2,1)} %get-tuple-element.33) | copy-start | bytes 786436
  122.2 12.0 %copy-start.22 = (bf16[256,512]{1,0:T(8,128)(2,1)S(1)}, bf16[256,512]{1,0:T(8,128)(2,1)}, u32[]{:S(2)}) copy-start(bf16[256,512]{1,0:T(8,128)(2,1)} %get-tuple-element.34) | copy-start | bytes 786436
  122.2 23.4 %collective-permute-start.18 = (bf16[2,128,512]{2,1,0:T(8,128)(2,1)S(1)}, bf16[2,128,512]{2,1,0:T(8,128)(2,1)S(1)}, u32[]{:S(2)}, u32[]{:S(2)}) collective-permute-start(bf16[2,128,512]{2,1,0:T(8,128)(2,1)S(1)} %convert_element_type.136), channel_id=1, source_target_pairs={{0,16},{16,0},{4,20},{20,4},{8,24},{24,8},{12,28},{28,12},{1,17},{... | collective-permute-start | bytes 786440 | tf_op jit(solution)/shard_map/ppermute | solution.py:22
  131.2 17.7 %collective-permute-start.21 = (bf16[2,128,512]{2,1,0:T(8,128)(2,1)S(1)}, bf16[2,128,512]{2,1,0:T(8,128)(2,1)S(1)}, u32[]{:S(2)}, u32[]{:S(2)}) collective-permute-start(bf16[2,128,512]{2,1,0:T(8,128)(2,1)S(1)} %convert_element_type.141), channel_id=1, source_target_pairs={{0,16},{16,0},{4,20},{20,4},{8,24},{24,8},{12,28},{28,12},{1,17},{... | collective-permute-start | bytes 786440 | tf_op jit(solution)/shard_map/ppermute | solution.py:22
  138.1 15.6 %collective-permute-start.13 = (bf16[2,128,512]{2,1,0:T(8,128)(2,1)S(1)}, bf16[2,128,512]{2,1,0:T(8,128)(2,1)S(1)}, u32[]{:S(2)}, u32[]{:S(2)}) collective-permute-start(bf16[2,128,512]{2,1,0:T(8,128)(2,1)S(1)} %add_convert_fusion.11), channel_id=1, source_target_pairs={{0,8},{8,0},{4,12},{12,4},{16,24},{24,16},{20,28},{28,20},{1,9},{9... | collective-permute-start | bytes 786440 | tf_op jit(solution)/shard_map/ppermute | solution.py:22
  139.0 7.0 %copy-start.11 = (f32[2,128,512]{2,1,0:T(8,128)S(1)}, f32[2,128,512]{2,1,0:T(8,128)}, u32[]{:S(2)}) copy-start(f32[2,128,512]{2,1,0:T(8,128)} %get-tuple-element.46) | copy-start | bytes 1572868
  139.1 20.2 %collective-permute-start.16 = (bf16[2,128,512]{2,1,0:T(8,128)(2,1)S(1)}, bf16[2,128,512]{2,1,0:T(8,128)(2,1)S(1)}, u32[]{:S(2)}, u32[]{:S(2)}) collective-permute-start(bf16[2,128,512]{2,1,0:T(8,128)(2,1)S(1)} %add_convert_fusion.10), channel_id=1, source_target_pairs={{0,8},{8,0},{4,12},{12,4},{16,24},{24,16},{20,28},{28,20},{1,9},{9... | collective-permute-start | bytes 786440 | tf_op jit(solution)/shard_map/ppermute | solution.py:22
  146.1 18.1 %collective-permute-start.19 = (bf16[2,128,512]{2,1,0:T(8,128)(2,1)S(1)}, bf16[2,128,512]{2,1,0:T(8,128)(2,1)S(1)}, u32[]{:S(2)}, u32[]{:S(2)}) collective-permute-start(bf16[2,128,512]{2,1,0:T(8,128)(2,1)S(1)} %add_convert_fusion.9), channel_id=1, source_target_pairs={{0,8},{8,0},{4,12},{12,4},{16,24},{24,16},{20,28},{28,20},{1,9},{9... | collective-permute-start | bytes 786440 | tf_op jit(solution)/shard_map/ppermute | solution.py:22
  149.4 19.5 %collective-permute-start.22 = (bf16[2,128,512]{2,1,0:T(8,128)(2,1)S(1)}, bf16[2,128,512]{2,1,0:T(8,128)(2,1)S(1)}, u32[]{:S(2)}, u32[]{:S(2)}) collective-permute-start(bf16[2,128,512]{2,1,0:T(8,128)(2,1)S(1)} %add_convert_fusion.8), channel_id=1, source_target_pairs={{0,8},{8,0},{4,12},{12,4},{16,24},{24,16},{20,28},{28,20},{1,9},{9... | collective-permute-start | bytes 786440 | tf_op jit(solution)/shard_map/ppermute | solution.py:22
  155.6 18.1 %collective-permute-start.14 = (bf16[2,256,512]{2,1,0:T(8,128)(2,1)S(1)}, bf16[2,256,512]{2,1,0:T(8,128)(2,1)S(1)}, u32[]{:S(2)}, u32[]{:S(2)}) collective-permute-start(bf16[2,256,512]{2,1,0:T(8,128)(2,1)S(1)} %add_convert_fusion.7), channel_id=1, source_target_pairs={{0,4},{4,0},{8,12},{12,8},{16,20},{20,16},{24,28},{28,24},{1,5},{5... | collective-permute-start | bytes 1572872 | tf_op jit(solution)/shard_map/ppermute | solution.py:22
  161.2 20.5 %collective-permute-start.17 = (bf16[2,256,512]{2,1,0:T(8,128)(2,1)S(1)}, bf16[2,256,512]{2,1,0:T(8,128)(2,1)S(1)}, u32[]{:S(2)}, u32[]{:S(2)}) collective-permute-start(bf16[2,256,512]{2,1,0:T(8,128)(2,1)S(1)} %add_convert_fusion.5), channel_id=1, source_target_pairs={{0,4},{4,0},{8,12},{12,8},{16,20},{20,16},{24,28},{28,24},{1,5},{5... | collective-permute-start | bytes 1572872 | tf_op jit(solution)/shard_map/ppermute | solution.py:22
  166.2 25.0 %collective-permute-start.20 = (bf16[2,256,512]{2,1,0:T(8,128)(2,1)S(1)}, bf16[2,256,512]{2,1,0:T(8,128)(2,1)S(1)}, u32[]{:S(2)}, u32[]{:S(2)}) collective-permute-start(bf16[2,256,512]{2,1,0:T(8,128)(2,1)S(1)} %add_convert_fusion.3), channel_id=1, source_target_pairs={{0,4},{4,0},{8,12},{12,8},{16,20},{20,16},{24,28},{28,24},{1,5},{5... | collective-permute-start | bytes 1572872 | tf_op jit(solution)/shard_map/ppermute | solution.py:22
  170.9 25.9 %collective-permute-start.23 = (bf16[2,256,512]{2,1,0:T(8,128)(2,1)S(1)}, bf16[2,256,512]{2,1,0:T(8,128)(2,1)S(1)}, u32[]{:S(2)}, u32[]{:S(2)}) collective-permute-start(bf16[2,256,512]{2,1,0:T(8,128)(2,1)S(1)} %add_convert_fusion.1), channel_id=1, source_target_pairs={{0,4},{4,0},{8,12},{12,8},{16,20},{20,16},{24,28},{28,24},{1,5},{5... | collective-permute-start | bytes 1572872 | tf_op jit(solution)/shard_map/ppermute | solution.py:22
  174.1 7.7 %copy-start.1 = (f32[2,256,512]{2,1,0:T(8,128)S(1)}, f32[2,256,512]{2,1,0:T(8,128)}, u32[]{:S(2)}) copy-start(f32[2,256,512]{2,1,0:T(8,128)} %get-tuple-element.40) | copy-start | bytes 3145732
  182.1 9.2 %copy-start.2 = (f32[2,256,512]{2,1,0:T(8,128)S(1)}, f32[2,256,512]{2,1,0:T(8,128)}, u32[]{:S(2)}) copy-start(f32[2,256,512]{2,1,0:T(8,128)} %get-tuple-element.44) | copy-start | bytes 3145732
  (20 other events, 34.8 us)

commit v4 on v3

--- a/solution.py
+++ b/solution.py
@@ -83,6 +83,12 @@
     )(key_bias.reshape(1, key_count), query_rows, out_grad, *parts)
 
 
+def after(value, earlier):
+    if earlier is None:
+        return value
+    return lax.optimization_barrier((value, earlier))[0]
+
+
 def placed_pool(rows_in, upper):
     run = rows_in // (POOLED // 2)
     out_row = lax.broadcasted_iota(jnp.int32, (POOLED, rows_in), 0)
@@ -114,6 +120,7 @@
     mine = [placed_pool(leaf_rows if s == 0 else POOLED, bits[s]) for s in range(levels)]
     other = [placed_pool(leaf_rows if s == 0 else POOLED, 1 - bits[s]) for s in range(levels)]
     pieces = [[], [], [], []]
+    last = {}
     for chunk in range(CHUNKS):
         columns = slice(chunk * chunk_width, (chunk + 1) * chunk_width)
         own = jnp.stack((key_rows[:, columns], value_rows[:, columns]))
@@ -121,7 +128,9 @@
         summary = apply(mine[0], own) + apply(other[0], sibling)
         far = []
         for step_level in range(1, levels):
-            partner = partner_2(summary.astype(jnp.bfloat16), "seq", step_level)
+            send = after(summary.astype(jnp.bfloat16), last.get(("fwd", step_level)))
+            partner = partner_2(send, "seq", step_level)
+            last[("fwd", step_level)] = partner
             far.append(partner)
             if step_level + 1 < levels:
                 summary = apply(mine[step_level], summary) + apply(other[step_level], partner)
@@ -135,7 +144,9 @@
             outgoing = terms[1 + step_level]
             if grad is not None:
                 outgoing = outgoing + apply(other[step_level].T, grad)
-            returned = partner_2(outgoing.astype(jnp.bfloat16), "seq", step_level)
+            send = after(outgoing.astype(jnp.bfloat16), last.get(("bwd", step_level)))
+            returned = partner_2(send, "seq", step_level)
+            last[("bwd", step_level)] = returned
             if grad is None:
                 grad = returned.astype(jnp.float32)
             else:
@@ -145,7 +156,9 @@
         if grad is not None:
             to_sibling = to_sibling + apply(other[0].T, grad)
             own_total = own_total + apply(mine[0].T, grad)
-        from_sibling = partner_2(to_sibling.astype(jnp.bfloat16), "seq", 0)
+        send = after(to_sibling.astype(jnp.bfloat16), last.get(("bwd", 0)))
+        from_sibling = partner_2(send, "seq", 0)
+        last[("bwd", 0)] = from_sibling
         totals = own_total + from_sibling.astype(jnp.float32)
         for slot, piece in enumerate((attended, query_grad, totals[0], totals[1])):
             pieces[slot].append(piece)

time: 200 us -> 223 us (1.11)
  waiting for transfers between devices: 91.2 us -> 115 us
  starting transfers between devices: 33.1 us -> 27.2 us
  other arithmetic: 14.9 us -> 17.6 us
  matrix products: 24.3 us -> 26.9 us
    ppermute x24, waiting for transfers between devices: 91.2 us -> 115 us  [partner_2(): return lax.ppermute(block, axis, route)]
    ppermute x24, starting transfers between devices: 33.1 us -> 27.2 us  [partner_2(): return lax.ppermute(block, axis, route)]
    dot_general x32, matrix products: 24.3 us -> 26.9 us  [apply(): jnp.einsum('pr,krw->kpw', matrix, rows.astype(jnp.float32), precision=lax...]
  transfers between devices with their start and end apart: 24 -> 24, of which waited for: 14 -> 15; matrix products, arithmetic and copies ran while one was open for 18% -> 19% of each run, Pallas kernels for 14% -> 13%
where the time goes in v4:
time: 223 us; the launch traced here: 222 us
  waiting for transfers between devices  115 us (52%)
  Pallas kernels  28.9 us (13%)
  starting transfers between devices  27.2 us (12%)
  matrix products  26.9 us (12%)
  other arithmetic  17.6 us (8%)
  local copies, waits for them, and re-layouts  4.12 us (2%)
    ppermute x24, waiting for transfers between devices, partner_2(): return lax.ppermute(block, axis, route)  115 us
    pallas_call x4, Pallas kernels, attention(): pl.pallas_call(functools.partial(attention_kernel, scale=score_scale, par...  28.9 us
    ppermute x24, starting transfers between devices, partner_2(): return lax.ppermute(block, axis, route)  27.2 us
    dot_general x32, matrix products, apply(): jnp.einsum('pr,krw->kpw', matrix, rows.astype(jnp.float32), precision=lax...  26.9 us
    concatenate x4, other arithmetic, body(): jnp.concatenate(p, axis=1).astype(jnp.bfloat16)  5.64 us
    convert_element_type x8, other arithmetic, body(): send = after(outgoing.astype(jnp.bfloat16), last.get(('bwd', step_level)))  5.35 us
  transfers between devices with their start and end apart: 24, of which 15 were waited for; matrix products, arithmetic and copies ran while one was open for 19% of the time, Pallas kernels for 13%

profile of v4, /device:TPU:0, one launch (start us, length us, event | category | flops | bytes accessed | tf_op | source)
XLA Modules:
  0.0 221.5 jit_solution(9244682903333040528)
XLA Ops:
  0.6 1.7 slice_bitcast_fusion.14
  3.2 3.0 %collective-permute-start = (bf16[2,256,512]{2,1,0:T(8,128)(2,1)}, bf16[2,256,512]{2,1,0:T(8,128)(2,1)}, u32[]{:S(2)}, u32[]{:S(2)}) collective-permute-start(bf16[2,256,512]{2,1,0:T(8,128)(2,1)} %pad_maximum_fusion.4.refs_0_), channel_id=1, source_target_pairs={{0,4},{4,0},{8,12},{12,8},{16,20},{20,16},{24,28},{28,24},{1,5},{5... | collective-permute-start | bytes 1572872 | tf_op jit(solution)/shard_map/ppermute | solution.py:22
  7.9 2.0 collective-permute-start.6
  11.9 7.4 %collective-permute-done.refs_1_ = bf16[2,256,512]{2,1,0:T(8,128)(2,1)} collective-permute-done((bf16[2,256,512]{2,1,0:T(8,128)(2,1)}, bf16[2,256,512]{2,1,0:T(8,128)(2,1)}, u32[]{:S(2)}, u32[]{:S(2)}) %collective-permute-start) | collective-permute-done | bytes 524320 | tf_op jit(solution)/shard_map/ppermute | solution.py:22
  20.7 2.2 collective-permute-start.1
  23.5 7.0 %collective-permute-done.3.refs_1_ = bf16[2,256,512]{2,1,0:T(8,128)(2,1)} collective-permute-done((bf16[2,256,512]{2,1,0:T(8,128)(2,1)}, bf16[2,256,512]{2,1,0:T(8,128)(2,1)}, u32[]{:S(2)}, u32[]{:S(2)}) %collective-permute-start.3) | collective-permute-done | bytes 524320 | tf_op jit(solution)/shard_map/ppermute | solution.py:22
  30.5 2.2 fusion.346
  32.7 9.1 %collective-permute-done.6.refs_1_ = bf16[2,256,512]{2,1,0:T(8,128)(2,1)} collective-permute-done((bf16[2,256,512]{2,1,0:T(8,128)(2,1)}, bf16[2,256,512]{2,1,0:T(8,128)(2,1)}, u32[]{:S(2)}, u32[]{:S(2)}) %collective-permute-start.6) | collective-permute-done | bytes 524320 | tf_op jit(solution)/shard_map/ppermute | solution.py:22
  41.7 1.5 fusion.345
  44.9 3.2 %collective-permute-start.2 = (bf16[2,128,512]{2,1,0:T(8,128)(2,1)S(1)}, bf16[2,128,512]{2,1,0:T(8,128)(2,1)S(1)}, u32[]{:S(2)}, u32[]{:S(2)}) collective-permute-start(bf16[2,128,512]{2,1,0:T(8,128)(2,1)S(1)} %fusion.15), channel_id=1, source_target_pairs={{0,16},{16,0},{4,20},{20,4},{8,24},{24,8},{12,28},{28,12},{1,17},{... | collective-permute-start | bytes 786440 | tf_op jit(solution)/shard_map/ppermute | solution.py:22
  48.1 4.0 %collective-permute-done.9.refs_1_ = bf16[2,256,512]{2,1,0:T(8,128)(2,1)} collective-permute-done((bf16[2,256,512]{2,1,0:T(8,128)(2,1)S(1)}, bf16[2,256,512]{2,1,0:T(8,128)(2,1)}, u32[]{:S(2)}, u32[]{:S(2)}) %collective-permute-start.9) | collective-permute-done | bytes 524320 | tf_op jit(solution)/shard_map/ppermute | solution.py:22
  52.1 1.5 fusion.344
  53.6 1.9 collective-permute-start.4
  55.5 2.7 %collective-permute-done.2.refs_3_ = bf16[2,128,512]{2,1,0:T(8,128)(2,1)S(1)} collective-permute-done((bf16[2,128,512]{2,1,0:T(8,128)(2,1)S(1)}, bf16[2,128,512]{2,1,0:T(8,128)(2,1)S(1)}, u32[]{:S(2)}, u32[]{:S(2)}) %collective-permute-start.2) | collective-permute-done | bytes 262176 | tf_op jit(solution)/shard_map/ppermute | solution.py:22
  59.0 7.3 %shard_map.75 = (bf16[256,512]{1,0:T(8,128)(2,1)}, bf16[256,512]{1,0:T(8,128)(2,1)}, f32[2,256,512]{2,1,0:T(8,128)}, f32[2,256,512]{2,1,0:T(8,128)}, f32[2,128,512]{2,1,0:T(8,128)}, /*index=5*/f32[2,128,512]{2,1,0:T(8,128)}) custom-call(f32[1,768]{1,0:T(1,128)} %constant.74.clone.1.bias_ref, bf16[256,2048]{1,0:T(8,128)(2,1)} %q_ref.7, ...), custom_call_target="tpu_custom_call" | custom-call | flops 1207959552 | bytes 5767168 | tf_op jit(solution)/shard_map/pallas_call | solution.py:71
  68.5 3.0 %collective-permute-start.5 = (bf16[2,128,512]{2,1,0:T(8,128)(2,1)S(1)}, bf16[2,128,512]{2,1,0:T(8,128)(2,1)S(1)}, u32[]{:S(2)}, u32[]{:S(2)}) collective-permute-start(bf16[2,128,512]{2,1,0:T(8,128)(2,1)S(1)} %fusion.14), channel_id=1, source_target_pairs={{0,16},{16,0},{4,20},{20,4},{8,24},{24,8},{12,28},{28,12},{1,17},{... | collective-permute-start | bytes 786440 | tf_op jit(solution)/shard_map/ppermute | solution.py:22
  72.6 15.8 %collective-permute-done.12 = bf16[2,128,512]{2,1,0:T(8,128)(2,1)S(1)} collective-permute-done((bf16[2,128,512]{2,1,0:T(8,128)(2,1)S(1)}, bf16[2,128,512]{2,1,0:T(8,128)(2,1)S(1)}, u32[]{:S(2)}, u32[]{:S(2)}) %collective-permute-start.12) | collective-permute-done | bytes 262176 | tf_op jit(solution)/shard_map/ppermute | solution.py:22
  89.0 3.3 %collective-permute-done.5.refs_3_ = bf16[2,128,512]{2,1,0:T(8,128)(2,1)S(1)} collective-permute-done((bf16[2,128,512]{2,1,0:T(8,128)(2,1)S(1)}, bf16[2,128,512]{2,1,0:T(8,128)(2,1)S(1)}, u32[]{:S(2)}, u32[]{:S(2)}) %collective-permute-start.5) | collective-permute-done | bytes 262176 | tf_op jit(solution)/shard_map/ppermute | solution.py:22
  93.1 7.2 %shard_map.76 = (bf16[256,512]{1,0:T(8,128)(2,1)}, bf16[256,512]{1,0:T(8,128)(2,1)}, f32[2,256,512]{2,1,0:T(8,128)}, f32[2,256,512]{2,1,0:T(8,128)}, f32[2,128,512]{2,1,0:T(8,128)}, /*index=5*/f32[2,128,512]{2,1,0:T(8,128)}) custom-call(f32[1,768]{1,0:T(1,128)} %constant.74.clone.1.bias_ref, bf16[256,2048]{1,0:T(8,128)(2,1)} %q_ref.7, ...), custom_call_target="tpu_custom_call" | custom-call | flops 1207959552 | bytes 5767168 | tf_op jit(solution)/shard_map/pallas_call | solution.py:71
  101.8 3.0 %collective-permute-start.8 = (bf16[2,128,512]{2,1,0:T(8,128)(2,1)S(1)}, bf16[2,128,512]{2,1,0:T(8,128)(2,1)}, u32[]{:S(2)}, u32[]{:S(2)}) collective-permute-start(bf16[2,128,512]{2,1,0:T(8,128)(2,1)S(1)} %fusion.13), channel_id=1, source_target_pairs={{0,16},{16,0},{4,20},{20,4},{8,24},{24,8},{12,28},{28,12},{1,17},{... | collective-permute-start | bytes 786440 | tf_op jit(solution)/shard_map/ppermute | solution.py:22
  108.9 11.5 %collective-permute-done.15 = bf16[2,128,512]{2,1,0:T(8,128)(2,1)S(1)} collective-permute-done((bf16[2,128,512]{2,1,0:T(8,128)(2,1)S(1)}, bf16[2,128,512]{2,1,0:T(8,128)(2,1)S(1)}, u32[]{:S(2)}, u32[]{:S(2)}) %collective-permute-start.15) | collective-permute-done | bytes 262176 | tf_op jit(solution)/shard_map/ppermute | solution.py:22
  121.0 4.9 %collective-permute-done.8.refs_3_ = bf16[2,128,512]{2,1,0:T(8,128)(2,1)} collective-permute-done((bf16[2,128,512]{2,1,0:T(8,128)(2,1)S(1)}, bf16[2,128,512]{2,1,0:T(8,128)(2,1)}, u32[]{:S(2)}, u32[]{:S(2)}) %collective-permute-start.8) | collective-permute-done | bytes 262176 | tf_op jit(solution)/shard_map/ppermute | solution.py:22
  125.9 7.1 %shard_map.77 = (bf16[256,512]{1,0:T(8,128)(2,1)}, bf16[256,512]{1,0:T(8,128)(2,1)}, f32[2,256,512]{2,1,0:T(8,128)}, f32[2,256,512]{2,1,0:T(8,128)}, f32[2,128,512]{2,1,0:T(8,128)}, /*index=5*/f32[2,128,512]{2,1,0:T(8,128)}) custom-call(f32[1,768]{1,0:T(1,128)} %constant.74.clone.1.bias_ref, bf16[256,2048]{1,0:T(8,128)(2,1)} %q_ref.7, ...), custom_call_target="tpu_custom_call" | custom-call | flops 1207959552 | bytes 5767168 | tf_op jit(solution)/shard_map/pallas_call | solution.py:71
  134.6 3.0 %collective-permute-start.11 = (bf16[2,128,512]{2,1,0:T(8,128)(2,1)S(1)}, bf16[2,128,512]{2,1,0:T(8,128)(2,1)}, u32[]{:S(2)}, u32[]{:S(2)}) collective-permute-start(bf16[2,128,512]{2,1,0:T(8,128)(2,1)S(1)} %fusion.12), channel_id=1, source_target_pairs={{0,16},{16,0},{4,20},{20,4},{8,24},{24,8},{12,28},{28,12},{1,17},{... | collective-permute-start | bytes 786440 | tf_op jit(solution)/shard_map/ppermute | solution.py:22
  141.3 11.8 %collective-permute-done.18 = bf16[2,128,512]{2,1,0:T(8,128)(2,1)S(1)} collective-permute-done((bf16[2,128,512]{2,1,0:T(8,128)(2,1)S(1)}, bf16[2,128,512]{2,1,0:T(8,128)(2,1)S(1)}, u32[]{:S(2)}, u32[]{:S(2)}) %collective-permute-start.18) | collective-permute-done | bytes 262176 | tf_op jit(solution)/shard_map/ppermute | solution.py:22
  155.5 3.4 %collective-permute-done.11.refs_3_ = bf16[2,128,512]{2,1,0:T(8,128)(2,1)} collective-permute-done((bf16[2,128,512]{2,1,0:T(8,128)(2,1)S(1)}, bf16[2,128,512]{2,1,0:T(8,128)(2,1)}, u32[]{:S(2)}, u32[]{:S(2)}) %collective-permute-start.11) | collective-permute-done | bytes 262176 | tf_op jit(solution)/shard_map/ppermute | solution.py:22
  158.9 7.3 %shard_map.78 = (bf16[256,512]{1,0:T(8,128)(2,1)}, bf16[256,512]{1,0:T(8,128)(2,1)}, f32[2,256,512]{2,1,0:T(8,128)}, f32[2,256,512]{2,1,0:T(8,128)}, f32[2,128,512]{2,1,0:T(8,128)}, /*index=5*/f32[2,128,512]{2,1,0:T(8,128)}) custom-call(f32[1,768]{1,0:T(1,128)} %constant.74.clone.1.bias_ref, bf16[256,2048]{1,0:T(8,128)(2,1)} %q_ref.7, ...), custom_call_target="tpu_custom_call" | custom-call | flops 1207959552 | bytes 5767168 | tf_op jit(solution)/shard_map/pallas_call | solution.py:71
  167.4 2.4 %pad_maximum_fusion.1 = bf16[256,2048]{1,0:T(8,128)(2,1)} fusion(bf16[256,512]{1,0:T(8,128)(2,1)} %get-tuple-element.56, bf16[256,512]{1,0:T(8,128)(2,1)} %get-tuple-element.55, bf16[256,512]{1,0:T(8,128)(2,1)} %get-tuple-element.54, bf16[256,512]{1,0:T(8,128)(2,1)} %get-tuple-element.53), kind=kLoop, calls=%fused_computation.41 | loop fusion | flops 4194304 | bytes 2097152 | tf_op jit(solution)/shard_map/concatenate | solution.py:165
  176.9 5.0 %collective-permute-done.21 = bf16[2,128,512]{2,1,0:T(8,128)(2,1)S(1)} collective-permute-done((bf16[2,128,512]{2,1,0:T(8,128)(2,1)S(1)}, bf16[2,128,512]{2,1,0:T(8,128)(2,1)S(1)}, u32[]{:S(2)}, u32[]{:S(2)}) %collective-permute-start.21) | collective-permute-done | bytes 262176 | tf_op jit(solution)/shard_map/ppermute | solution.py:22
  183.9 6.8 %collective-permute-done.22 = bf16[2,128,512]{2,1,0:T(8,128)(2,1)S(1)} collective-permute-done((bf16[2,128,512]{2,1,0:T(8,128)(2,1)S(1)}, bf16[2,128,512]{2,1,0:T(8,128)(2,1)S(1)}, u32[]{:S(2)}, u32[]{:S(2)}) %collective-permute-start.22) | collective-permute-done | bytes 262176 | tf_op jit(solution)/shard_map/ppermute | solution.py:22
  195.1 11.7 %collective-permute-done.20 = bf16[2,256,512]{2,1,0:T(8,128)(2,1)S(1)} collective-permute-done((bf16[2,256,512]{2,1,0:T(8,128)(2,1)S(1)}, bf16[2,256,512]{2,1,0:T(8,128)(2,1)S(1)}, u32[]{:S(2)}, u32[]{:S(2)}) %collective-permute-start.20) | collective-permute-done | bytes 524320 | tf_op jit(solution)/shard_map/ppermute | solution.py:22
  208.1 10.9 %collective-permute-done.23 = bf16[2,256,512]{2,1,0:T(8,128)(2,1)S(1)} collective-permute-done((bf16[2,256,512]{2,1,0:T(8,128)(2,1)S(1)}, bf16[2,256,512]{2,1,0:T(8,128)(2,1)S(1)}, u32[]{:S(2)}, u32[]{:S(2)}) %collective-permute-start.23) | collective-permute-done | bytes 524320 | tf_op jit(solution)/shard_map/ppermute | solution.py:22
  (135 shorter events, 45.5 us)
Async XLA Ops:
  3.2 16.0 %collective-permute-start = (bf16[2,256,512]{2,1,0:T(8,128)(2,1)}, bf16[2,256,512]{2,1,0:T(8,128)(2,1)}, u32[]{:S(2)}, u32[]{:S(2)}) collective-permute-start(bf16[2,256,512]{2,1,0:T(8,128)(2,1)} %pad_maximum_fusion.4.refs_0_), channel_id=1, source_target_pairs={{0,4},{4,0},{8,12},{12,8},{16,20},{20,16},{24,28},{28,24},{1,5},{5... | collective-permute-start | bytes 1572872 | tf_op jit(solution)/shard_map/ppermute | solution.py:22
  7.0 23.5 %collective-permute-start.3 = (bf16[2,256,512]{2,1,0:T(8,128)(2,1)}, bf16[2,256,512]{2,1,0:T(8,128)(2,1)}, u32[]{:S(2)}, u32[]{:S(2)}) collective-permute-start(bf16[2,256,512]{2,1,0:T(8,128)(2,1)} %pad_maximum_fusion.5.refs_0_), channel_id=1, source_target_pairs={{0,4},{4,0},{8,12},{12,8},{16,20},{20,16},{24,28},{28,24},{1,5},{5... | collective-permute-start | bytes 1572872 | tf_op jit(solution)/shard_map/ppermute | solution.py:22
  7.9 33.9 %collective-permute-start.6 = (bf16[2,256,512]{2,1,0:T(8,128)(2,1)}, bf16[2,256,512]{2,1,0:T(8,128)(2,1)}, u32[]{:S(2)}, u32[]{:S(2)}) collective-permute-start(bf16[2,256,512]{2,1,0:T(8,128)(2,1)} %pad_maximum_fusion.6.refs_0_), channel_id=1, source_target_pairs={{0,4},{4,0},{8,12},{12,8},{16,20},{20,16},{24,28},{28,24},{1,5},{5... | collective-permute-start | bytes 1572872 | tf_op jit(solution)/shard_map/ppermute | solution.py:22
  10.0 42.2 %collective-permute-start.9 = (bf16[2,256,512]{2,1,0:T(8,128)(2,1)S(1)}, bf16[2,256,512]{2,1,0:T(8,128)(2,1)}, u32[]{:S(2)}, u32[]{:S(2)}) collective-permute-start(bf16[2,256,512]{2,1,0:T(8,128)(2,1)S(1)} %pad_maximum_fusion.7.refs_0_), channel_id=1, source_target_pairs={{0,4},{4,0},{8,12},{12,8},{16,20},{20,16},{24,28},{28,24},{1,5},{5... | collective-permute-start | bytes 1572872 | tf_op jit(solution)/shard_map/ppermute | solution.py:22
  20.7 23.7 %collective-permute-start.1 = (bf16[2,128,512]{2,1,0:T(8,128)(2,1)S(1)}, bf16[2,128,512]{2,1,0:T(8,128)(2,1)S(1)}, u32[]{:S(2)}, u32[]{:S(2)}) collective-permute-start(bf16[2,128,512]{2,1,0:T(8,128)(2,1)S(1)} %get-tuple-element.104), channel_id=1, source_target_pairs={{0,8},{8,0},{4,12},{12,4},{16,24},{24,16},{20,28},{28,20},{1,9},{9... | collective-permute-start | bytes 786440 | tf_op jit(solution)/shard_map/ppermute | solution.py:22
  44.5 9.2 %copy-start.16 = (bf16[2,128,512]{2,1,0:T(8,128)(2,1)}, bf16[2,128,512]{2,1,0:T(8,128)(2,1)S(1)}, u32[]{:S(2)}) copy-start(bf16[2,128,512]{2,1,0:T(8,128)(2,1)S(1)} %collective-permute-done.1.refs_2_) | copy-start | bytes 786436
  44.9 13.4 %collective-permute-start.2 = (bf16[2,128,512]{2,1,0:T(8,128)(2,1)S(1)}, bf16[2,128,512]{2,1,0:T(8,128)(2,1)S(1)}, u32[]{:S(2)}, u32[]{:S(2)}) collective-permute-start(bf16[2,128,512]{2,1,0:T(8,128)(2,1)S(1)} %fusion.15), channel_id=1, source_target_pairs={{0,16},{16,0},{4,20},{20,4},{8,24},{24,8},{12,28},{28,12},{1,17},{... | collective-permute-start | bytes 786440 | tf_op jit(solution)/shard_map/ppermute | solution.py:22
  53.6 14.4 %collective-permute-start.4 = (bf16[2,128,512]{2,1,0:T(8,128)(2,1)}, bf16[2,128,512]{2,1,0:T(8,128)(2,1)S(1)}, u32[]{:S(2)}, u32[]{:S(2)}) collective-permute-start(bf16[2,128,512]{2,1,0:T(8,128)(2,1)} %get-tuple-element.44), channel_id=1, source_target_pairs={{0,8},{8,0},{4,12},{12,4},{16,24},{24,16},{20,28},{28,20},{1,9},{9... | collective-permute-start | bytes 786440 | tf_op jit(solution)/shard_map/ppermute | solution.py:22
  67.3 21.0 %collective-permute-start.12 = (bf16[2,128,512]{2,1,0:T(8,128)(2,1)S(1)}, bf16[2,128,512]{2,1,0:T(8,128)(2,1)S(1)}, u32[]{:S(2)}, u32[]{:S(2)}) collective-permute-start(bf16[2,128,512]{2,1,0:T(8,128)(2,1)S(1)} %convert_element_type.126), channel_id=1, source_target_pairs={{0,16},{16,0},{4,20},{20,4},{8,24},{24,8},{12,28},{28,12},{1,17},{... | collective-permute-start | bytes 786440 | tf_op jit(solution)/shard_map/ppermute | solution.py:22
  68.0 20.8 %copy-start.12 = (f32[2,128,512]{2,1,0:T(8,128)S(1)}, f32[2,128,512]{2,1,0:T(8,128)}, u32[]{:S(2)}) copy-start(f32[2,128,512]{2,1,0:T(8,128)} %get-tuple-element.59) | copy-start | bytes 1572868
  68.0 20.9 %copy-start.15 = (bf16[2,128,512]{2,1,0:T(8,128)(2,1)}, bf16[2,128,512]{2,1,0:T(8,128)(2,1)S(1)}, u32[]{:S(2)}) copy-start(bf16[2,128,512]{2,1,0:T(8,128)(2,1)S(1)} %collective-permute-done.4.refs_2_) | copy-start | bytes 786436
  68.5 23.9 %collective-permute-start.5 = (bf16[2,128,512]{2,1,0:T(8,128)(2,1)S(1)}, bf16[2,128,512]{2,1,0:T(8,128)(2,1)S(1)}, u32[]{:S(2)}, u32[]{:S(2)}) collective-permute-start(bf16[2,128,512]{2,1,0:T(8,128)(2,1)S(1)} %fusion.14), channel_id=1, source_target_pairs={{0,16},{16,0},{4,20},{20,4},{8,24},{24,8},{12,28},{28,12},{1,17},{... | collective-permute-start | bytes 786440 | tf_op jit(solution)/shard_map/ppermute | solution.py:22
  71.4 30.0 %collective-permute-start.7 = (bf16[2,128,512]{2,1,0:T(8,128)(2,1)S(1)}, bf16[2,128,512]{2,1,0:T(8,128)(2,1)S(1)}, u32[]{:S(2)}, u32[]{:S(2)}) collective-permute-start(bf16[2,128,512]{2,1,0:T(8,128)(2,1)S(1)} %get-tuple-element.47), channel_id=1, source_target_pairs={{0,8},{8,0},{4,12},{12,4},{16,24},{24,16},{20,28},{28,20},{1,9},{9... | collective-permute-start | bytes 786440 | tf_op jit(solution)/shard_map/ppermute | solution.py:22
  88.9 15.9 %collective-permute-start.13 = (bf16[2,128,512]{2,1,0:T(8,128)(2,1)S(1)}, bf16[2,128,512]{2,1,0:T(8,128)(2,1)S(1)}, u32[]{:S(2)}, u32[]{:S(2)}) collective-permute-start(bf16[2,128,512]{2,1,0:T(8,128)(2,1)S(1)} %add_convert_fusion.11), channel_id=1, source_target_pairs={{0,8},{8,0},{4,12},{12,4},{16,24},{24,16},{20,28},{28,20},{1,9},{9... | collective-permute-start | bytes 786440 | tf_op jit(solution)/shard_map/ppermute | solution.py:22
  101.3 19.0 %collective-permute-start.15 = (bf16[2,128,512]{2,1,0:T(8,128)(2,1)S(1)}, bf16[2,128,512]{2,1,0:T(8,128)(2,1)S(1)}, u32[]{:S(2)}, u32[]{:S(2)}) collective-permute-start(bf16[2,128,512]{2,1,0:T(8,128)(2,1)S(1)} %convert_element_type.131), channel_id=1, source_target_pairs={{0,16},{16,0},{4,20},{20,4},{8,24},{24,8},{12,28},{28,12},{1,17},{... | collective-permute-start | bytes 786440 | tf_op jit(solution)/shard_map/ppermute | solution.py:22
  101.8 24.1 %collective-permute-start.8 = (bf16[2,128,512]{2,1,0:T(8,128)(2,1)S(1)}, bf16[2,128,512]{2,1,0:T(8,128)(2,1)}, u32[]{:S(2)}, u32[]{:S(2)}) collective-permute-start(bf16[2,128,512]{2,1,0:T(8,128)(2,1)S(1)} %fusion.13), channel_id=1, source_target_pairs={{0,16},{16,0},{4,20},{20,4},{8,24},{24,8},{12,28},{28,12},{1,17},{... | collective-permute-start | bytes 786440 | tf_op jit(solution)/shard_map/ppermute | solution.py:22
  104.8 29.4 %collective-permute-start.10 = (bf16[2,128,512]{2,1,0:T(8,128)(2,1)S(1)}, bf16[2,128,512]{2,1,0:T(8,128)(2,1)S(1)}, u32[]{:S(2)}, u32[]{:S(2)}) collective-permute-start(bf16[2,128,512]{2,1,0:T(8,128)(2,1)S(1)} %get-tuple-element.50), channel_id=1, source_target_pairs={{0,8},{8,0},{4,12},{12,4},{16,24},{24,16},{20,28},{28,20},{1,9},{9... | collective-permute-start | bytes 786440 | tf_op jit(solution)/shard_map/ppermute | solution.py:22
  107.5 13.3 %copy-start.10 = (f32[2,128,512]{2,1,0:T(8,128)S(1)}, f32[2,128,512]{2,1,0:T(8,128)}, u32[]{:S(2)}) copy-start(f32[2,128,512]{2,1,0:T(8,128)} %get-tuple-element.64) | copy-start | bytes 1572868
  107.5 64.1 %collective-permute-start.14 = (bf16[2,256,512]{2,1,0:T(8,128)(2,1)}, bf16[2,256,512]{2,1,0:T(8,128)(2,1)}, u32[]{:S(2)}, u32[]{:S(2)}) collective-permute-start(bf16[2,256,512]{2,1,0:T(8,128)(2,1)} %add_convert_fusion.7), channel_id=1, source_target_pairs={{0,4},{4,0},{8,12},{12,8},{16,20},{20,16},{24,28},{28,24},{1,5},{5... | collective-permute-start | bytes 1572872 | tf_op jit(solution)/shard_map/ppermute | solution.py:22
  120.9 17.8 %collective-permute-start.16 = (bf16[2,128,512]{2,1,0:T(8,128)(2,1)S(1)}, bf16[2,128,512]{2,1,0:T(8,128)(2,1)}, u32[]{:S(2)}, u32[]{:S(2)}) collective-permute-start(bf16[2,128,512]{2,1,0:T(8,128)(2,1)S(1)} %add_convert_fusion.10), channel_id=1, source_target_pairs={{0,8},{8,0},{4,12},{12,4},{16,24},{24,16},{20,28},{28,20},{1,9},{9... | collective-permute-start | bytes 786440 | tf_op jit(solution)/shard_map/ppermute | solution.py:22
  134.1 19.0 %collective-permute-start.18 = (bf16[2,128,512]{2,1,0:T(8,128)(2,1)S(1)}, bf16[2,128,512]{2,1,0:T(8,128)(2,1)S(1)}, u32[]{:S(2)}, u32[]{:S(2)}) collective-permute-start(bf16[2,128,512]{2,1,0:T(8,128)(2,1)S(1)} %convert_element_type.136), channel_id=1, source_target_pairs={{0,16},{16,0},{4,20},{20,4},{8,24},{24,8},{12,28},{28,12},{1,17},{... | collective-permute-start | bytes 786440 | tf_op jit(solution)/shard_map/ppermute | solution.py:22
  134.6 24.2 %collective-permute-start.11 = (bf16[2,128,512]{2,1,0:T(8,128)(2,1)S(1)}, bf16[2,128,512]{2,1,0:T(8,128)(2,1)}, u32[]{:S(2)}, u32[]{:S(2)}) collective-permute-start(bf16[2,128,512]{2,1,0:T(8,128)(2,1)S(1)} %fusion.12), channel_id=1, source_target_pairs={{0,16},{16,0},{4,20},{20,4},{8,24},{24,8},{12,28},{28,12},{1,17},{... | collective-permute-start | bytes 786440 | tf_op jit(solution)/shard_map/ppermute | solution.py:22
  140.2 13.4 %copy-start.11 = (f32[2,128,512]{2,1,0:T(8,128)S(1)}, f32[2,128,512]{2,1,0:T(8,128)}, u32[]{:S(2)}) copy-start(f32[2,128,512]{2,1,0:T(8,128)} %get-tuple-element.71) | copy-start | bytes 1572868
  154.4 19.9 %collective-permute-start.19 = (bf16[2,128,512]{2,1,0:T(8,128)(2,1)}, bf16[2,128,512]{2,1,0:T(8,128)(2,1)}, u32[]{:S(2)}, u32[]{:S(2)}) collective-permute-start(bf16[2,128,512]{2,1,0:T(8,128)(2,1)} %add_convert_fusion.9), channel_id=1, source_target_pairs={{0,8},{8,0},{4,12},{12,4},{16,24},{24,16},{20,28},{28,20},{1,9},{9... | collective-permute-start | bytes 786440 | tf_op jit(solution)/shard_map/ppermute | solution.py:22
  167.3 14.6 %collective-permute-start.21 = (bf16[2,128,512]{2,1,0:T(8,128)(2,1)S(1)}, bf16[2,128,512]{2,1,0:T(8,128)(2,1)S(1)}, u32[]{:S(2)}, u32[]{:S(2)}) collective-permute-start(bf16[2,128,512]{2,1,0:T(8,128)(2,1)S(1)} %convert_element_type.141), channel_id=1, source_target_pairs={{0,16},{16,0},{4,20},{20,4},{8,24},{24,8},{12,28},{28,12},{1,17},{... | collective-permute-start | bytes 786440 | tf_op jit(solution)/shard_map/ppermute | solution.py:22
  171.7 22.2 %collective-permute-start.17 = (bf16[2,256,512]{2,1,0:T(8,128)(2,1)S(1)}, bf16[2,256,512]{2,1,0:T(8,128)(2,1)S(1)}, u32[]{:S(2)}, u32[]{:S(2)}) collective-permute-start(bf16[2,256,512]{2,1,0:T(8,128)(2,1)S(1)} %add_convert_fusion.5), channel_id=1, source_target_pairs={{0,4},{4,0},{8,12},{12,8},{16,20},{20,16},{24,28},{28,24},{1,5},{5... | collective-permute-start | bytes 1572872 | tf_op jit(solution)/shard_map/ppermute | solution.py:22
  175.7 6.6 %copy-start.9 = (f32[2,128,512]{2,1,0:T(8,128)S(1)}, f32[2,128,512]{2,1,0:T(8,128)}, u32[]{:S(2)}) copy-start(f32[2,128,512]{2,1,0:T(8,128)} %get-tuple-element.78) | copy-start | bytes 1572868
  182.4 8.3 %collective-permute-start.22 = (bf16[2,128,512]{2,1,0:T(8,128)(2,1)S(1)}, bf16[2,128,512]{2,1,0:T(8,128)(2,1)S(1)}, u32[]{:S(2)}, u32[]{:S(2)}) collective-permute-start(bf16[2,128,512]{2,1,0:T(8,128)(2,1)S(1)} %add_convert_fusion.8), channel_id=1, source_target_pairs={{0,8},{8,0},{4,12},{12,4},{16,24},{24,16},{20,28},{28,20},{1,9},{9... | collective-permute-start | bytes 786440 | tf_op jit(solution)/shard_map/ppermute | solution.py:22
  193.8 13.1 %collective-permute-start.20 = (bf16[2,256,512]{2,1,0:T(8,128)(2,1)S(1)}, bf16[2,256,512]{2,1,0:T(8,128)(2,1)S(1)}, u32[]{:S(2)}, u32[]{:S(2)}) collective-permute-start(bf16[2,256,512]{2,1,0:T(8,128)(2,1)S(1)} %add_convert_fusion.3), channel_id=1, source_target_pairs={{0,4},{4,0},{8,12},{12,8},{16,20},{20,16},{24,28},{28,24},{1,5},{5... | collective-permute-start | bytes 1572872 | tf_op jit(solution)/shard_map/ppermute | solution.py:22
  195.1 12.7 %copy-start.2 = (f32[2,256,512]{2,1,0:T(8,128)S(1)}, f32[2,256,512]{2,1,0:T(8,128)}, u32[]{:S(2)}) copy-start(f32[2,256,512]{2,1,0:T(8,128)} %get-tuple-element.68) | copy-start | bytes 3145732
  206.9 12.1 %collective-permute-start.23 = (bf16[2,256,512]{2,1,0:T(8,128)(2,1)S(1)}, bf16[2,256,512]{2,1,0:T(8,128)(2,1)S(1)}, u32[]{:S(2)}, u32[]{:S(2)}) collective-permute-start(bf16[2,256,512]{2,1,0:T(8,128)(2,1)S(1)} %add_convert_fusion.1), channel_id=1, source_target_pairs={{0,4},{4,0},{8,12},{12,8},{16,20},{20,16},{24,28},{28,24},{1,5},{5... | collective-permute-start | bytes 1572872 | tf_op jit(solution)/shard_map/ppermute | solution.py:22
  208.1 10.9 %copy-start.3 = (f32[2,256,512]{2,1,0:T(8,128)S(1)}, f32[2,256,512]{2,1,0:T(8,128)}, u32[]{:S(2)}) copy-start(f32[2,256,512]{2,1,0:T(8,128)} %get-tuple-element.75) | copy-start | bytes 3145732
  (15 other events, 32.4 us)

commit v5 on v3

--- a/solution.py
+++ b/solution.py
@@ -83,6 +83,15 @@
     )(key_bias.reshape(1, key_count), query_rows, out_grad, *parts)
 
 
+def inner_pairs(count, level):
+    mask = (1 << level) | (1 << (level - 1))
+    return [(b, b ^ mask) for b in range(count) if (b >> level & 1) != (b >> (level - 1) & 1)]
+
+
+def outer_pairs(count, level):
+    return [(b, b ^ (1 << (level - 1))) for b in range(count) if (b >> level & 1) != (b >> (level - 1) & 1)]
+
+
 def placed_pool(rows_in, upper):
     run = rows_in // (POOLED // 2)
     out_row = lax.broadcasted_iota(jnp.int32, (POOLED, rows_in), 0)
@@ -111,6 +120,7 @@
         bias_parts.append(jnp.full((POOLED,), math.log(pool_ratio * 2**step_level), jnp.float32))
     key_bias = jnp.concatenate(bias_parts, axis=0)
     bits = [position // 2**step_level % 2 for step_level in range(levels)]
+    inner = [None] + [bits[s] != bits[s - 1] for s in range(1, levels)]
     mine = [placed_pool(leaf_rows if s == 0 else POOLED, bits[s]) for s in range(levels)]
     other = [placed_pool(leaf_rows if s == 0 else POOLED, 1 - bits[s]) for s in range(levels)]
     pieces = [[], [], [], []]
@@ -121,7 +131,12 @@
         summary = apply(mine[0], own) + apply(other[0], sibling)
         far = []
         for step_level in range(1, levels):
-            partner = partner_2(summary.astype(jnp.bfloat16), "seq", step_level)
+            if step_level == 1:
+                partner = partner_2(summary.astype(jnp.bfloat16), "seq", step_level)
+            else:
+                crossed = lax.ppermute(summary.astype(jnp.bfloat16), "seq", inner_pairs(seq_count, step_level))
+                passed = lax.ppermute(crossed, "seq", outer_pairs(seq_count, step_level))
+                partner = jnp.where(inner[step_level], crossed, passed)
             far.append(partner)
             if step_level + 1 < levels:
                 summary = apply(mine[step_level], summary) + apply(other[step_level], partner)
@@ -135,7 +150,13 @@
             outgoing = terms[1 + step_level]
             if grad is not None:
                 outgoing = outgoing + apply(other[step_level].T, grad)
-            returned = partner_2(outgoing.astype(jnp.bfloat16), "seq", step_level)
+            if step_level == 1:
+                returned = partner_2(outgoing.astype(jnp.bfloat16), "seq", step_level)
+            else:
+                back = [(t, s) for s, t in outer_pairs(seq_count, step_level)]
+                gathered = lax.ppermute(outgoing.astype(jnp.bfloat16), "seq", back)
+                total = outgoing + gathered.astype(jnp.float32)
+                returned = lax.ppermute(total.astype(jnp.bfloat16), "seq", inner_pairs(seq_count, step_level))
             if grad is None:
                 grad = returned.astype(jnp.float32)
             else:

time: 200 us -> 207 us (1.035)
  starting transfers between devices: 33.1 us -> 60 us
  waiting for transfers between devices: 91.2 us -> 69.9 us
  other arithmetic: 14.9 us -> 18.2 us
  local copies, waits for them, and re-layouts: 5.73 us -> 2.49 us
    ppermute x24 -> x16, waiting for transfers between devices: 91.2 us -> 58.7 us  [partner_2(): return lax.ppermute(block, axis, route)]
    ppermute x0 -> x16, starting transfers between devices: none -> 22.5 us  [the longest x4 11.6 us: body(): gathered = lax.ppermute(outgoing.astype(jnp.bfloat16), 'seq', back)]
    ppermute x0 -> x16, waiting for transfers between devices: none -> 11.1 us  [the longest x4 11.1 us: body(): passed = lax.ppermute(crossed, 'seq', outer_pairs(seq_count, step_level))]
    convert_element_type x0 -> x8, other arithmetic: none -> 4.62 us  [the longest x4 4.3 us: body(): gathered = lax.ppermute(outgoing.astype(jnp.bfloat16), 'seq', back)]
    ppermute x24 -> x16, starting transfers between devices: 33.1 us -> 37.5 us  [partner_2(): return lax.ppermute(block, axis, route)]
    convert_element_type x8 -> x4, other arithmetic: 4.67 us -> 0.4 us  [body(): returned = partner_2(outgoing.astype(jnp.bfloat16), 'seq', step_level)]
    unnamed x56, local copies, waits for them, and re-layouts: 3.84 us -> 0.6 us
    select_n x0 -> x4, other arithmetic: none -> 2.92 us  [body(): partner = jnp.where(inner[step_level], crossed, passed)]
  transfers between devices with their start and end apart: 24 -> 32, of which waited for: 14 -> 10; matrix products, arithmetic and copies ran while one was open for 18% -> 19% of each run, Pallas kernels for 14% -> 14%
where the time goes in v5:
time: 207 us; the launch traced here: 205 us
  waiting for transfers between devices  69.9 us (34%)
  starting transfers between devices  60 us (29%)
  Pallas kernels  28.8 us (14%)
  matrix products  24.3 us (12%)
  other arithmetic  18.2 us (9%)
  local copies, waits for them, and re-layouts  2.49 us (1%)
    ppermute x16, waiting for transfers between devices, partner_2(): return lax.ppermute(block, axis, route)  58.7 us
    ppermute x16, starting transfers between devices, partner_2(): return lax.ppermute(block, axis, route)  37.5 us
    pallas_call x4, Pallas kernels, attention(): pl.pallas_call(functools.partial(attention_kernel, scale=score_scale, par...  28.8 us
    dot_general x32, matrix products, apply(): jnp.einsum('pr,krw->kpw', matrix, rows.astype(jnp.float32), precision=lax...  24.3 us
    ppermute x4, starting transfers between devices, body(): gathered = lax.ppermute(outgoing.astype(jnp.bfloat16), 'seq', back)  11.6 us
    ppermute x4, waiting for transfers between devices, body(): passed = lax.ppermute(crossed, 'seq', outer_pairs(seq_count, step_level))  11.1 us
    concatenate x4, other arithmetic, body(): jnp.concatenate(p, axis=1).astype(jnp.bfloat16)  5.42 us
    ppermute x4, starting transfers between devices, body(): passed = lax.ppermute(crossed, 'seq', outer_pairs(seq_count, step_level))  5.17 us
  transfers between devices with their start and end apart: 32, of which 10 were waited for; matrix products, arithmetic and copies ran while one was open for 19% of the time, Pallas kernels for 14%

profile of v5, /device:TPU:0, one launch (start us, length us, event | category | flops | bytes accessed | tf_op | source)
XLA Modules:
  0.0 205.3 jit_solution(4958404424874613603)
XLA Ops:
  0.6 1.7 slice_bitcast_fusion.14
  3.2 3.0 %collective-permute-start = (bf16[2,256,512]{2,1,0:T(8,128)(2,1)}, bf16[2,256,512]{2,1,0:T(8,128)(2,1)}, u32[]{:S(2)}, u32[]{:S(2)}) collective-permute-start(bf16[2,256,512]{2,1,0:T(8,128)(2,1)} %pad_maximum_fusion.4.refs_0_), channel_id=1, source_target_pairs={{0,4},{4,0},{8,12},{12,8},{16,20},{20,16},{24,28},{28,24},{1,5},{5... | collective-permute-start | bytes 1572872 | tf_op jit(solution)/shard_map/ppermute | solution.py:22
  7.9 2.0 collective-permute-start.8
  11.9 7.4 %collective-permute-done.refs_1_ = bf16[2,256,512]{2,1,0:T(8,128)(2,1)} collective-permute-done((bf16[2,256,512]{2,1,0:T(8,128)(2,1)}, bf16[2,256,512]{2,1,0:T(8,128)(2,1)}, u32[]{:S(2)}, u32[]{:S(2)}) %collective-permute-start) | collective-permute-done | bytes 524320 | tf_op jit(solution)/shard_map/ppermute | solution.py:22
  19.3 1.5 fusion.347
  20.7 2.2 %collective-permute-start.1 = (bf16[2,128,512]{2,1,0:T(8,128)(2,1)S(1)}, bf16[2,128,512]{2,1,0:T(8,128)(2,1)S(1)}, u32[]{:S(2)}, u32[]{:S(2)}) collective-permute-start(bf16[2,128,512]{2,1,0:T(8,128)(2,1)S(1)} %get-tuple-element.74), channel_id=1, source_target_pairs={{0,8},{8,0},{4,12},{12,4},{16,24},{24,16},{20,28},{28,20},{1,9},{9... | collective-permute-start | bytes 786440 | tf_op jit(solution)/shard_map/ppermute | solution.py:22
  22.9 7.6 %collective-permute-done.4.refs_1_ = bf16[2,256,512]{2,1,0:T(8,128)(2,1)} collective-permute-done((bf16[2,256,512]{2,1,0:T(8,128)(2,1)}, bf16[2,256,512]{2,1,0:T(8,128)(2,1)}, u32[]{:S(2)}, u32[]{:S(2)}) %collective-permute-start.4) | collective-permute-done | bytes 524320 | tf_op jit(solution)/shard_map/ppermute | solution.py:22
  30.5 1.5 fusion.346
  32.0 2.2 %collective-permute-start.5 = (bf16[2,128,512]{2,1,0:T(8,128)(2,1)S(1)}, bf16[2,128,512]{2,1,0:T(8,128)(2,1)S(1)}, u32[]{:S(2)}, u32[]{:S(2)}) collective-permute-start(bf16[2,128,512]{2,1,0:T(8,128)(2,1)S(1)} %get-tuple-element.72), channel_id=1, source_target_pairs={{0,8},{8,0},{4,12},{12,4},{16,24},{24,16},{20,28},{28,20},{1,9},{9... | collective-permute-start | bytes 786440 | tf_op jit(solution)/shard_map/ppermute | solution.py:22
  34.1 7.6 %collective-permute-done.8.refs_1_ = bf16[2,256,512]{2,1,0:T(8,128)(2,1)} collective-permute-done((bf16[2,256,512]{2,1,0:T(8,128)(2,1)}, bf16[2,256,512]{2,1,0:T(8,128)(2,1)}, u32[]{:S(2)}, u32[]{:S(2)}) %collective-permute-start.8) | collective-permute-done | bytes 524320 | tf_op jit(solution)/shard_map/ppermute | solution.py:22
  41.7 1.5 fusion.345
  43.2 2.2 %collective-permute-start.9 = (bf16[2,128,512]{2,1,0:T(8,128)(2,1)S(1)}, bf16[2,128,512]{2,1,0:T(8,128)(2,1)S(1)}, u32[]{:S(2)}, u32[]{:S(2)}) collective-permute-start(bf16[2,128,512]{2,1,0:T(8,128)(2,1)S(1)} %get-tuple-element.70), channel_id=1, source_target_pairs={{0,8},{8,0},{4,12},{12,4},{16,24},{24,16},{20,28},{28,20},{1,9},{9... | collective-permute-start | bytes 786440 | tf_op jit(solution)/shard_map/ppermute | solution.py:22
  47.2 4.9 %collective-permute-done.12.refs_1_ = bf16[2,256,512]{2,1,0:T(8,128)(2,1)} collective-permute-done((bf16[2,256,512]{2,1,0:T(8,128)(2,1)S(1)}, bf16[2,256,512]{2,1,0:T(8,128)(2,1)}, u32[]{:S(2)}, u32[]{:S(2)}) %collective-permute-start.12) | collective-permute-done | bytes 524320 | tf_op jit(solution)/shard_map/ppermute | solution.py:22
  54.2 1.9 collective-permute-start.13
  59.5 2.3 %collective-permute-done.13.refs_2_ = bf16[2,128,512]{2,1,0:T(8,128)(2,1)S(1)} collective-permute-done((bf16[2,128,512]{2,1,0:T(8,128)(2,1)S(1)}, bf16[2,128,512]{2,1,0:T(8,128)(2,1)S(1)}, u32[]{:S(2)}, u32[]{:S(2)}) %collective-permute-start.13) | collective-permute-done | bytes 262176 | tf_op jit(solution)/shard_map/ppermute | solution.py:22
  68.2 11.1 %collective-permute-done.3 = bf16[2,128,512]{2,1,0:T(8,128)(2,1)S(1)} collective-permute-done((bf16[2,128,512]{2,1,0:T(8,128)(2,1)S(1)}, bf16[2,128,512]{2,1,0:T(8,128)(2,1)S(1)}, u32[]{:S(2)}, u32[]{:S(2)}) %collective-permute-start.3) | collective-permute-done | bytes 262176 | tf_op jit(solution)/shard_map/ppermute | solution.py:138
  80.0 7.2 %shard_map.75 = (bf16[256,512]{1,0:T(8,128)(2,1)}, bf16[256,512]{1,0:T(8,128)(2,1)}, f32[2,256,512]{2,1,0:T(8,128)}, f32[2,256,512]{2,1,0:T(8,128)}, f32[2,128,512]{2,1,0:T(8,128)}, /*index=5*/f32[2,128,512]{2,1,0:T(8,128)}) custom-call(f32[1,768]{1,0:T(1,128)} %constant.85.clone.1.bias_ref, bf16[256,2048]{1,0:T(8,128)(2,1)} %q_ref.7, ...), custom_call_target="tpu_custom_call" | custom-call | flops 1207959552 | bytes 5767168 | tf_op jit(solution)/shard_map/pallas_call | solution.py:71
  88.3 7.5 %collective-permute-start.16 = (bf16[2,128,512]{2,1,0:T(8,128)(2,1)S(1)}, bf16[2,128,512]{2,1,0:T(8,128)(2,1)S(1)}, u32[]{:S(2)}, u32[]{:S(2)}) collective-permute-start(bf16[2,128,512]{2,1,0:T(8,128)(2,1)S(1)} %convert_element_type.150), channel_id=1, source_target_pairs={{0,8},{4,12},{24,16},{28,20},{1,9},{5,13},{25,17},{29,21},{2,10},{... | collective-permute-start | bytes 786440 | tf_op jit(solution)/shard_map/ppermute | solution.py:157
  96.6 7.2 %shard_map.76 = (bf16[256,512]{1,0:T(8,128)(2,1)}, bf16[256,512]{1,0:T(8,128)(2,1)}, f32[2,256,512]{2,1,0:T(8,128)}, f32[2,256,512]{2,1,0:T(8,128)}, f32[2,128,512]{2,1,0:T(8,128)}, /*index=5*/f32[2,128,512]{2,1,0:T(8,128)}) custom-call(f32[1,768]{1,0:T(1,128)} %constant.85.clone.1.bias_ref, bf16[256,2048]{1,0:T(8,128)(2,1)} %q_ref.7, ...), custom_call_target="tpu_custom_call" | custom-call | flops 1207959552 | bytes 5767168 | tf_op jit(solution)/shard_map/pallas_call | solution.py:71
  104.9 1.5 collective-permute-start.20
  107.1 7.2 %shard_map.77 = (bf16[256,512]{1,0:T(8,128)(2,1)}, bf16[256,512]{1,0:T(8,128)(2,1)}, f32[2,256,512]{2,1,0:T(8,128)}, f32[2,256,512]{2,1,0:T(8,128)}, f32[2,128,512]{2,1,0:T(8,128)}, /*index=5*/f32[2,128,512]{2,1,0:T(8,128)}) custom-call(f32[1,768]{1,0:T(1,128)} %constant.85.clone.1.bias_ref, bf16[256,2048]{1,0:T(8,128)(2,1)} %q_ref.7, ...), custom_call_target="tpu_custom_call" | custom-call | flops 1207959552 | bytes 5767168 | tf_op jit(solution)/shard_map/pallas_call | solution.py:71
  117.5 7.2 %shard_map.78 = (bf16[256,512]{1,0:T(8,128)(2,1)}, bf16[256,512]{1,0:T(8,128)(2,1)}, f32[2,256,512]{2,1,0:T(8,128)}, f32[2,256,512]{2,1,0:T(8,128)}, f32[2,128,512]{2,1,0:T(8,128)}, /*index=5*/f32[2,128,512]{2,1,0:T(8,128)}) custom-call(f32[1,768]{1,0:T(1,128)} %constant.85.clone.1.bias_ref, bf16[256,2048]{1,0:T(8,128)(2,1)} %q_ref.7, ...), custom_call_target="tpu_custom_call" | custom-call | flops 1207959552 | bytes 5767168 | tf_op jit(solution)/shard_map/pallas_call | solution.py:71
  127.1 2.1 %pad_maximum_fusion.1 = bf16[256,2048]{1,0:T(8,128)(2,1)} fusion(bf16[256,512]{1,0:T(8,128)(2,1)} %get-tuple-element.35, bf16[256,512]{1,0:T(8,128)(2,1)S(1)} %copy-done.26, bf16[256,512]{1,0:T(8,128)(2,1)S(1)} %copy-done.24, bf16[256,512]{1,0:T(8,128)(2,1)S(1)} %copy-done.22), kind=kLoop, calls=%fused_computation.41 | loop fusion | flops 4194304 | bytes 2097152 | tf_op jit(solution)/shard_map/concatenate | solution.py:173
  134.4 8.4 %collective-permute-start.18 = (bf16[2,128,512]{2,1,0:T(8,128)(2,1)S(1)}, bf16[2,128,512]{2,1,0:T(8,128)(2,1)S(1)}, u32[]{:S(2)}, u32[]{:S(2)}) collective-permute-start(bf16[2,128,512]{2,1,0:T(8,128)(2,1)S(1)} %add_convert_fusion.14), channel_id=1, source_target_pairs={{0,8},{8,0},{4,12},{12,4},{16,24},{24,16},{20,28},{28,20},{1,9},{9... | collective-permute-start | bytes 786440 | tf_op jit(solution)/shard_map/ppermute | solution.py:22
  143.4 4.0 %collective-permute-start.22 = (bf16[2,128,512]{2,1,0:T(8,128)(2,1)S(1)}, bf16[2,128,512]{2,1,0:T(8,128)(2,1)S(1)}, u32[]{:S(2)}, u32[]{:S(2)}) collective-permute-start(bf16[2,128,512]{2,1,0:T(8,128)(2,1)S(1)} %add_convert_fusion.12), channel_id=1, source_target_pairs={{0,8},{8,0},{4,12},{12,4},{16,24},{24,16},{20,28},{28,20},{1,9},{9... | collective-permute-start | bytes 786440 | tf_op jit(solution)/shard_map/ppermute | solution.py:22
  148.0 5.0 %collective-permute-start.26 = (bf16[2,128,512]{2,1,0:T(8,128)(2,1)S(1)}, bf16[2,128,512]{2,1,0:T(8,128)(2,1)S(1)}, u32[]{:S(2)}, u32[]{:S(2)}) collective-permute-start(bf16[2,128,512]{2,1,0:T(8,128)(2,1)S(1)} %add_convert_fusion.10), channel_id=1, source_target_pairs={{0,8},{8,0},{4,12},{12,4},{16,24},{24,16},{20,28},{28,20},{1,9},{9... | collective-permute-start | bytes 786440 | tf_op jit(solution)/shard_map/ppermute | solution.py:22
  153.6 2.4 %collective-permute-start.30 = (bf16[2,128,512]{2,1,0:T(8,128)(2,1)S(1)}, bf16[2,128,512]{2,1,0:T(8,128)(2,1)S(1)}, u32[]{:S(2)}, u32[]{:S(2)}) collective-permute-start(bf16[2,128,512]{2,1,0:T(8,128)(2,1)S(1)} %add_convert_fusion.8), channel_id=1, source_target_pairs={{0,8},{8,0},{4,12},{12,4},{16,24},{24,16},{20,28},{28,20},{1,9},{9... | collective-permute-start | bytes 786440 | tf_op jit(solution)/shard_map/ppermute | solution.py:22
  158.0 1.6 collective-permute-start.19
  165.2 1.6 collective-permute-start.27
  173.3 10.9 %collective-permute-done.23 = bf16[2,256,512]{2,1,0:T(8,128)(2,1)S(1)} collective-permute-done((bf16[2,256,512]{2,1,0:T(8,128)(2,1)S(1)}, bf16[2,256,512]{2,1,0:T(8,128)(2,1)S(1)}, u32[]{:S(2)}, u32[]{:S(2)}) %collective-permute-start.23) | collective-permute-done | bytes 524320 | tf_op jit(solution)/shard_map/ppermute | solution.py:22
  184.5 10.9 %collective-permute-done.27 = bf16[2,256,512]{2,1,0:T(8,128)(2,1)S(1)} collective-permute-done((bf16[2,256,512]{2,1,0:T(8,128)(2,1)S(1)}, bf16[2,256,512]{2,1,0:T(8,128)(2,1)S(1)}, u32[]{:S(2)}, u32[]{:S(2)}) %collective-permute-start.27) | collective-permute-done | bytes 524320 | tf_op jit(solution)/shard_map/ppermute | solution.py:22
  195.7 7.0 %collective-permute-done.31 = bf16[2,256,512]{2,1,0:T(8,128)(2,1)S(1)} collective-permute-done((bf16[2,256,512]{2,1,0:T(8,128)(2,1)S(1)}, bf16[2,256,512]{2,1,0:T(8,128)(2,1)S(1)}, u32[]{:S(2)}, u32[]{:S(2)}) %collective-permute-start.31) | collective-permute-done | bytes 524320 | tf_op jit(solution)/shard_map/ppermute | solution.py:22
  (169 shorter events, 51.6 us)
Async XLA Ops:
  3.2 16.0 %collective-permute-start = (bf16[2,256,512]{2,1,0:T(8,128)(2,1)}, bf16[2,256,512]{2,1,0:T(8,128)(2,1)}, u32[]{:S(2)}, u32[]{:S(2)}) collective-permute-start(bf16[2,256,512]{2,1,0:T(8,128)(2,1)} %pad_maximum_fusion.4.refs_0_), channel_id=1, source_target_pairs={{0,4},{4,0},{8,12},{12,8},{16,20},{20,16},{24,28},{28,24},{1,5},{5... | collective-permute-start | bytes 1572872 | tf_op jit(solution)/shard_map/ppermute | solution.py:22
  7.0 23.5 %collective-permute-start.4 = (bf16[2,256,512]{2,1,0:T(8,128)(2,1)}, bf16[2,256,512]{2,1,0:T(8,128)(2,1)}, u32[]{:S(2)}, u32[]{:S(2)}) collective-permute-start(bf16[2,256,512]{2,1,0:T(8,128)(2,1)} %pad_maximum_fusion.5.refs_0_), channel_id=1, source_target_pairs={{0,4},{4,0},{8,12},{12,8},{16,20},{20,16},{24,28},{28,24},{1,5},{5... | collective-permute-start | bytes 1572872 | tf_op jit(solution)/shard_map/ppermute | solution.py:22
  7.9 33.9 %collective-permute-start.8 = (bf16[2,256,512]{2,1,0:T(8,128)(2,1)}, bf16[2,256,512]{2,1,0:T(8,128)(2,1)}, u32[]{:S(2)}, u32[]{:S(2)}) collective-permute-start(bf16[2,256,512]{2,1,0:T(8,128)(2,1)} %pad_maximum_fusion.6.refs_0_), channel_id=1, source_target_pairs={{0,4},{4,0},{8,12},{12,8},{16,20},{20,16},{24,28},{28,24},{1,5},{5... | collective-permute-start | bytes 1572872 | tf_op jit(solution)/shard_map/ppermute | solution.py:22
  10.0 42.2 %collective-permute-start.12 = (bf16[2,256,512]{2,1,0:T(8,128)(2,1)S(1)}, bf16[2,256,512]{2,1,0:T(8,128)(2,1)}, u32[]{:S(2)}, u32[]{:S(2)}) collective-permute-start(bf16[2,256,512]{2,1,0:T(8,128)(2,1)S(1)} %pad_maximum_fusion.7.refs_0_), channel_id=1, source_target_pairs={{0,4},{4,0},{8,12},{12,8},{16,20},{20,16},{24,28},{28,24},{1,5},{5... | collective-permute-start | bytes 1572872 | tf_op jit(solution)/shard_map/ppermute | solution.py:22
  20.7 35.4 %collective-permute-start.1 = (bf16[2,128,512]{2,1,0:T(8,128)(2,1)S(1)}, bf16[2,128,512]{2,1,0:T(8,128)(2,1)S(1)}, u32[]{:S(2)}, u32[]{:S(2)}) collective-permute-start(bf16[2,128,512]{2,1,0:T(8,128)(2,1)S(1)} %get-tuple-element.74), channel_id=1, source_target_pairs={{0,8},{8,0},{4,12},{12,4},{16,24},{24,16},{20,28},{28,20},{1,9},{9... | collective-permute-start | bytes 786440 | tf_op jit(solution)/shard_map/ppermute | solution.py:22
  32.0 25.2 %collective-permute-start.5 = (bf16[2,128,512]{2,1,0:T(8,128)(2,1)S(1)}, bf16[2,128,512]{2,1,0:T(8,128)(2,1)S(1)}, u32[]{:S(2)}, u32[]{:S(2)}) collective-permute-start(bf16[2,128,512]{2,1,0:T(8,128)(2,1)S(1)} %get-tuple-element.72), channel_id=1, source_target_pairs={{0,8},{8,0},{4,12},{12,4},{16,24},{24,16},{20,28},{28,20},{1,9},{9... | collective-permute-start | bytes 786440 | tf_op jit(solution)/shard_map/ppermute | solution.py:22
  43.2 15.2 %collective-permute-start.9 = (bf16[2,128,512]{2,1,0:T(8,128)(2,1)S(1)}, bf16[2,128,512]{2,1,0:T(8,128)(2,1)S(1)}, u32[]{:S(2)}, u32[]{:S(2)}) collective-permute-start(bf16[2,128,512]{2,1,0:T(8,128)(2,1)S(1)} %get-tuple-element.70), channel_id=1, source_target_pairs={{0,8},{8,0},{4,12},{12,4},{16,24},{24,16},{20,28},{28,20},{1,9},{9... | collective-permute-start | bytes 786440 | tf_op jit(solution)/shard_map/ppermute | solution.py:22
  54.2 7.6 %collective-permute-start.13 = (bf16[2,128,512]{2,1,0:T(8,128)(2,1)S(1)}, bf16[2,128,512]{2,1,0:T(8,128)(2,1)S(1)}, u32[]{:S(2)}, u32[]{:S(2)}) collective-permute-start(bf16[2,128,512]{2,1,0:T(8,128)(2,1)S(1)} %get-tuple-element.68), channel_id=1, source_target_pairs={{0,8},{8,0},{4,12},{12,4},{16,24},{24,16},{20,28},{28,20},{1,9},{9... | collective-permute-start | bytes 786440 | tf_op jit(solution)/shard_map/ppermute | solution.py:22
  56.5 6.4 %collective-permute-start.2 = (bf16[2,128,512]{2,1,0:T(8,128)(2,1)S(1)}, bf16[2,128,512]{2,1,0:T(8,128)(2,1)S(1)}, u32[]{:S(2)}, u32[]{:S(2)}) collective-permute-start(bf16[2,128,512]{2,1,0:T(8,128)(2,1)S(1)} %fusion.15), channel_id=1, source_target_pairs={{8,16},{12,20},{16,8},{20,12},{9,17},{13,21},{17,9},{21,13},{10,18... | collective-permute-start | bytes 786440 | tf_op jit(solution)/shard_map/ppermute | solution.py:137
  57.7 6.6 %collective-permute-start.6 = (bf16[2,128,512]{2,1,0:T(8,128)(2,1)S(1)}, bf16[2,128,512]{2,1,0:T(8,128)(2,1)S(1)}, u32[]{:S(2)}, u32[]{:S(2)}) collective-permute-start(bf16[2,128,512]{2,1,0:T(8,128)(2,1)S(1)} %fusion.14), channel_id=1, source_target_pairs={{8,16},{12,20},{16,8},{20,12},{9,17},{13,21},{17,9},{21,13},{10,18... | collective-permute-start | bytes 786440 | tf_op jit(solution)/shard_map/ppermute | solution.py:137
  58.8 6.7 %collective-permute-start.10 = (bf16[2,128,512]{2,1,0:T(8,128)(2,1)S(1)}, bf16[2,128,512]{2,1,0:T(8,128)(2,1)S(1)}, u32[]{:S(2)}, u32[]{:S(2)}) collective-permute-start(bf16[2,128,512]{2,1,0:T(8,128)(2,1)S(1)} %fusion.13), channel_id=1, source_target_pairs={{8,16},{12,20},{16,8},{20,12},{9,17},{13,21},{17,9},{21,13},{10,18... | collective-permute-start | bytes 786440 | tf_op jit(solution)/shard_map/ppermute | solution.py:137
  62.2 4.7 %collective-permute-start.14 = (bf16[2,128,512]{2,1,0:T(8,128)(2,1)S(1)}, bf16[2,128,512]{2,1,0:T(8,128)(2,1)S(1)}, u32[]{:S(2)}, u32[]{:S(2)}) collective-permute-start(bf16[2,128,512]{2,1,0:T(8,128)(2,1)S(1)} %fusion.12), channel_id=1, source_target_pairs={{8,16},{12,20},{16,8},{20,12},{9,17},{13,21},{17,9},{21,13},{10,18... | collective-permute-start | bytes 786440 | tf_op jit(solution)/shard_map/ppermute | solution.py:137
  62.9 16.4 %collective-permute-start.3 = (bf16[2,128,512]{2,1,0:T(8,128)(2,1)S(1)}, bf16[2,128,512]{2,1,0:T(8,128)(2,1)S(1)}, u32[]{:S(2)}, u32[]{:S(2)}) collective-permute-start(bf16[2,128,512]{2,1,0:T(8,128)(2,1)S(1)} %collective-permute-done.2), channel_id=1, source_target_pairs={{8,0},{12,4},{16,24},{20,28},{9,1},{13,5},{17,25},{21,29},{10,2},{... | collective-permute-start | bytes 786440 | tf_op jit(solution)/shard_map/ppermute | solution.py:138
  64.3 31.6 %collective-permute-start.7 = (bf16[2,128,512]{2,1,0:T(8,128)(2,1)S(1)}, bf16[2,128,512]{2,1,0:T(8,128)(2,1)S(1)}, u32[]{:S(2)}, u32[]{:S(2)}) collective-permute-start(bf16[2,128,512]{2,1,0:T(8,128)(2,1)S(1)} %collective-permute-done.6), channel_id=1, source_target_pairs={{8,0},{12,4},{16,24},{20,28},{9,1},{13,5},{17,25},{21,29},{10,2},{... | collective-permute-start | bytes 786440 | tf_op jit(solution)/shard_map/ppermute | solution.py:138
  65.6 40.8 %collective-permute-start.11 = (bf16[2,128,512]{2,1,0:T(8,128)(2,1)S(1)}, bf16[2,128,512]{2,1,0:T(8,128)(2,1)S(1)}, u32[]{:S(2)}, u32[]{:S(2)}) collective-permute-start(bf16[2,128,512]{2,1,0:T(8,128)(2,1)S(1)} %collective-permute-done.10), channel_id=1, source_target_pairs={{8,0},{12,4},{16,24},{20,28},{9,1},{13,5},{17,25},{21,29},{10,2},{... | collective-permute-start | bytes 786440 | tf_op jit(solution)/shard_map/ppermute | solution.py:138
  66.9 49.8 %collective-permute-start.15 = (bf16[2,128,512]{2,1,0:T(8,128)(2,1)S(1)}, bf16[2,128,512]{2,1,0:T(8,128)(2,1)S(1)}, u32[]{:S(2)}, u32[]{:S(2)}) collective-permute-start(bf16[2,128,512]{2,1,0:T(8,128)(2,1)S(1)} %collective-permute-done.14), channel_id=1, source_target_pairs={{8,0},{12,4},{16,24},{20,28},{9,1},{13,5},{17,25},{21,29},{10,2},{... | collective-permute-start | bytes 786440 | tf_op jit(solution)/shard_map/ppermute | solution.py:138
  88.3 42.1 %collective-permute-start.16 = (bf16[2,128,512]{2,1,0:T(8,128)(2,1)S(1)}, bf16[2,128,512]{2,1,0:T(8,128)(2,1)S(1)}, u32[]{:S(2)}, u32[]{:S(2)}) collective-permute-start(bf16[2,128,512]{2,1,0:T(8,128)(2,1)S(1)} %convert_element_type.150), channel_id=1, source_target_pairs={{0,8},{4,12},{24,16},{28,20},{1,9},{5,13},{25,17},{29,21},{2,10},{... | collective-permute-start | bytes 786440 | tf_op jit(solution)/shard_map/ppermute | solution.py:157
  104.9 26.5 %collective-permute-start.20 = (bf16[2,128,512]{2,1,0:T(8,128)(2,1)S(1)}, bf16[2,128,512]{2,1,0:T(8,128)(2,1)S(1)}, u32[]{:S(2)}, u32[]{:S(2)}) collective-permute-start(bf16[2,128,512]{2,1,0:T(8,128)(2,1)S(1)} %convert_element_type.157), channel_id=1, source_target_pairs={{0,8},{4,12},{24,16},{28,20},{1,9},{5,13},{25,17},{29,21},{2,10},{... | collective-permute-start | bytes 786440 | tf_op jit(solution)/shard_map/ppermute | solution.py:157
  115.4 16.7 %collective-permute-start.24 = (bf16[2,128,512]{2,1,0:T(8,128)(2,1)S(1)}, bf16[2,128,512]{2,1,0:T(8,128)(2,1)S(1)}, u32[]{:S(2)}, u32[]{:S(2)}) collective-permute-start(bf16[2,128,512]{2,1,0:T(8,128)(2,1)S(1)} %convert_element_type.164), channel_id=1, source_target_pairs={{0,8},{4,12},{24,16},{28,20},{1,9},{5,13},{25,17},{29,21},{2,10},{... | collective-permute-start | bytes 786440 | tf_op jit(solution)/shard_map/ppermute | solution.py:157
  125.7 7.3 %collective-permute-start.28 = (bf16[2,128,512]{2,1,0:T(8,128)(2,1)S(1)}, bf16[2,128,512]{2,1,0:T(8,128)(2,1)S(1)}, u32[]{:S(2)}, u32[]{:S(2)}) collective-permute-start(bf16[2,128,512]{2,1,0:T(8,128)(2,1)S(1)} %convert_element_type.171), channel_id=1, source_target_pairs={{0,8},{4,12},{24,16},{28,20},{1,9},{5,13},{25,17},{29,21},{2,10},{... | collective-permute-start | bytes 786440 | tf_op jit(solution)/shard_map/ppermute | solution.py:157
  130.5 3.3 %collective-permute-start.17 = (bf16[2,128,512]{2,1,0:T(8,128)(2,1)S(1)}, bf16[2,128,512]{2,1,0:T(8,128)(2,1)S(1)}, u32[]{:S(2)}, u32[]{:S(2)}) collective-permute-start(bf16[2,128,512]{2,1,0:T(8,128)(2,1)S(1)} %add_convert_fusion.15), channel_id=1, source_target_pairs={{8,16},{12,20},{16,8},{20,12},{9,17},{13,21},{17,9},{21,13},{10,18... | collective-permute-start | bytes 786440 | tf_op jit(solution)/shard_map/ppermute | solution.py:159
  131.4 11.4 %collective-permute-start.21 = (bf16[2,128,512]{2,1,0:T(8,128)(2,1)S(1)}, bf16[2,128,512]{2,1,0:T(8,128)(2,1)S(1)}, u32[]{:S(2)}, u32[]{:S(2)}) collective-permute-start(bf16[2,128,512]{2,1,0:T(8,128)(2,1)S(1)} %add_convert_fusion.13), channel_id=1, source_target_pairs={{8,16},{12,20},{16,8},{20,12},{9,17},{13,21},{17,9},{21,13},{10,18... | collective-permute-start | bytes 786440 | tf_op jit(solution)/shard_map/ppermute | solution.py:159
  132.2 15.2 %collective-permute-start.25 = (bf16[2,128,512]{2,1,0:T(8,128)(2,1)S(1)}, bf16[2,128,512]{2,1,0:T(8,128)(2,1)S(1)}, u32[]{:S(2)}, u32[]{:S(2)}) collective-permute-start(bf16[2,128,512]{2,1,0:T(8,128)(2,1)S(1)} %add_convert_fusion.11), channel_id=1, source_target_pairs={{8,16},{12,20},{16,8},{20,12},{9,17},{13,21},{17,9},{21,13},{10,18... | collective-permute-start | bytes 786440 | tf_op jit(solution)/shard_map/ppermute | solution.py:159
  133.1 19.9 %collective-permute-start.29 = (bf16[2,128,512]{2,1,0:T(8,128)(2,1)S(1)}, bf16[2,128,512]{2,1,0:T(8,128)(2,1)S(1)}, u32[]{:S(2)}, u32[]{:S(2)}) collective-permute-start(bf16[2,128,512]{2,1,0:T(8,128)(2,1)S(1)} %add_convert_fusion.9), channel_id=1, source_target_pairs={{8,16},{12,20},{16,8},{20,12},{9,17},{13,21},{17,9},{21,13},{10,18... | collective-permute-start | bytes 786440 | tf_op jit(solution)/shard_map/ppermute | solution.py:159
  134.4 21.5 %collective-permute-start.18 = (bf16[2,128,512]{2,1,0:T(8,128)(2,1)S(1)}, bf16[2,128,512]{2,1,0:T(8,128)(2,1)S(1)}, u32[]{:S(2)}, u32[]{:S(2)}) collective-permute-start(bf16[2,128,512]{2,1,0:T(8,128)(2,1)S(1)} %add_convert_fusion.14), channel_id=1, source_target_pairs={{0,8},{8,0},{4,12},{12,4},{16,24},{24,16},{20,28},{28,20},{1,9},{9... | collective-permute-start | bytes 786440 | tf_op jit(solution)/shard_map/ppermute | solution.py:22
  143.4 16.1 %collective-permute-start.22 = (bf16[2,128,512]{2,1,0:T(8,128)(2,1)S(1)}, bf16[2,128,512]{2,1,0:T(8,128)(2,1)S(1)}, u32[]{:S(2)}, u32[]{:S(2)}) collective-permute-start(bf16[2,128,512]{2,1,0:T(8,128)(2,1)S(1)} %add_convert_fusion.12), channel_id=1, source_target_pairs={{0,8},{8,0},{4,12},{12,4},{16,24},{24,16},{20,28},{28,20},{1,9},{9... | collective-permute-start | bytes 786440 | tf_op jit(solution)/shard_map/ppermute | solution.py:22
  148.0 15.2 %collective-permute-start.26 = (bf16[2,128,512]{2,1,0:T(8,128)(2,1)S(1)}, bf16[2,128,512]{2,1,0:T(8,128)(2,1)S(1)}, u32[]{:S(2)}, u32[]{:S(2)}) collective-permute-start(bf16[2,128,512]{2,1,0:T(8,128)(2,1)S(1)} %add_convert_fusion.10), channel_id=1, source_target_pairs={{0,8},{8,0},{4,12},{12,4},{16,24},{24,16},{20,28},{28,20},{1,9},{9... | collective-permute-start | bytes 786440 | tf_op jit(solution)/shard_map/ppermute | solution.py:22
  153.6 14.3 %collective-permute-start.30 = (bf16[2,128,512]{2,1,0:T(8,128)(2,1)S(1)}, bf16[2,128,512]{2,1,0:T(8,128)(2,1)S(1)}, u32[]{:S(2)}, u32[]{:S(2)}) collective-permute-start(bf16[2,128,512]{2,1,0:T(8,128)(2,1)S(1)} %add_convert_fusion.8), channel_id=1, source_target_pairs={{0,8},{8,0},{4,12},{12,4},{16,24},{24,16},{20,28},{28,20},{1,9},{9... | collective-permute-start | bytes 786440 | tf_op jit(solution)/shard_map/ppermute | solution.py:22
  158.0 14.9 %collective-permute-start.19 = (bf16[2,256,512]{2,1,0:T(8,128)(2,1)S(1)}, bf16[2,256,512]{2,1,0:T(8,128)(2,1)S(1)}, u32[]{:S(2)}, u32[]{:S(2)}) collective-permute-start(bf16[2,256,512]{2,1,0:T(8,128)(2,1)S(1)} %add_convert_fusion.7), channel_id=1, source_target_pairs={{0,4},{4,0},{8,12},{12,8},{16,20},{20,16},{24,28},{28,24},{1,5},{5... | collective-permute-start | bytes 1572872 | tf_op jit(solution)/shard_map/ppermute | solution.py:22
  161.5 22.6 %collective-permute-start.23 = (bf16[2,256,512]{2,1,0:T(8,128)(2,1)S(1)}, bf16[2,256,512]{2,1,0:T(8,128)(2,1)S(1)}, u32[]{:S(2)}, u32[]{:S(2)}) collective-permute-start(bf16[2,256,512]{2,1,0:T(8,128)(2,1)S(1)} %add_convert_fusion.5), channel_id=1, source_target_pairs={{0,4},{4,0},{8,12},{12,8},{16,20},{20,16},{24,28},{28,24},{1,5},{5... | collective-permute-start | bytes 1572872 | tf_op jit(solution)/shard_map/ppermute | solution.py:22
  165.2 30.2 %collective-permute-start.27 = (bf16[2,256,512]{2,1,0:T(8,128)(2,1)S(1)}, bf16[2,256,512]{2,1,0:T(8,128)(2,1)S(1)}, u32[]{:S(2)}, u32[]{:S(2)}) collective-permute-start(bf16[2,256,512]{2,1,0:T(8,128)(2,1)S(1)} %add_convert_fusion.3), channel_id=1, source_target_pairs={{0,4},{4,0},{8,12},{12,8},{16,20},{20,16},{24,28},{28,24},{1,5},{5... | collective-permute-start | bytes 1572872 | tf_op jit(solution)/shard_map/ppermute | solution.py:22
  169.9 32.9 %collective-permute-start.31 = (bf16[2,256,512]{2,1,0:T(8,128)(2,1)S(1)}, bf16[2,256,512]{2,1,0:T(8,128)(2,1)S(1)}, u32[]{:S(2)}, u32[]{:S(2)}) collective-permute-start(bf16[2,256,512]{2,1,0:T(8,128)(2,1)S(1)} %add_convert_fusion.1), channel_id=1, source_target_pairs={{0,4},{4,0},{8,12},{12,8},{16,20},{20,16},{24,28},{28,24},{1,5},{5... | collective-permute-start | bytes 1572872 | tf_op jit(solution)/shard_map/ppermute | solution.py:22
  (28 other events, 134.9 us)

commit v6 on v3

--- a/solution.py
+++ b/solution.py
@@ -83,6 +83,10 @@
     )(key_bias.reshape(1, key_count), query_rows, out_grad, *parts)
 
 
+def after(value, earlier):
+    return lax.optimization_barrier((value, earlier))[0]
+
+
 def placed_pool(rows_in, upper):
     run = rows_in // (POOLED // 2)
     out_row = lax.broadcasted_iota(jnp.int32, (POOLED, rows_in), 0)
@@ -113,12 +117,19 @@
     bits = [position // 2**step_level % 2 for step_level in range(levels)]
     mine = [placed_pool(leaf_rows if s == 0 else POOLED, bits[s]) for s in range(levels)]
     other = [placed_pool(leaf_rows if s == 0 else POOLED, 1 - bits[s]) for s in range(levels)]
+    pool_own = placed_pool(leaf_rows, 0)[: POOLED // 2]
+    own_pooled = apply(pool_own, jnp.stack((key_rows, value_rows)))
+    sibling_pooled = partner_2(own_pooled.astype(jnp.bfloat16), "seq", 0)
+    place_mine = placed_pool(POOLED // 2, bits[0])
+    place_other = placed_pool(POOLED // 2, 1 - bits[0])
     pieces = [[], [], [], []]
     for chunk in range(CHUNKS):
         columns = slice(chunk * chunk_width, (chunk + 1) * chunk_width)
         own = jnp.stack((key_rows[:, columns], value_rows[:, columns]))
-        sibling = partner_2(own, "seq", 0)
-        summary = apply(mine[0], own) + apply(other[0], sibling)
+        sibling = partner_2(after(own, sibling_pooled), "seq", 0)
+        summary = apply(place_mine, own_pooled[:, :, columns]) + apply(
+            place_other, sibling_pooled[:, :, columns]
+        )
         far = []
         for step_level in range(1, levels):
             partner = partner_2(summary.astype(jnp.bfloat16), "seq", step_level)

time: 200 us -> 188 us (0.940)
  waiting for transfers between devices: 91.2 us -> 70.4 us
  starting transfers between devices: 33.1 us -> 38.3 us
  matrix products: 24.3 us -> 28.3 us
  local copies, waits for them, and re-layouts: 5.73 us -> 2.11 us
    ppermute x24 -> x25, waiting for transfers between devices: 91.2 us -> 70.4 us  [partner_2(): return lax.ppermute(block, axis, route)]
    ppermute x24 -> x25, starting transfers between devices: 33.1 us -> 38.3 us  [partner_2(): return lax.ppermute(block, axis, route)]
    dot_general x32 -> x33, matrix products: 24.3 us -> 28.3 us  [apply(): jnp.einsum('pr,krw->kpw', matrix, rows.astype(jnp.float32), precision=lax...]
    unnamed x56 -> x72, local copies, waits for them, and re-layouts: 3.84 us -> 0.73 us
  transfers between devices with their start and end apart: 24 -> 25, of which waited for: 14 -> 13; matrix products, arithmetic and copies ran while one was open for 18% -> 21% of each run, Pallas kernels for 14% -> 16%
where the time goes in v6:
time: 188 us; the launch traced here: 186 us
  waiting for transfers between devices  70.4 us (37%)
  starting transfers between devices  38.3 us (20%)
  Pallas kernels  28.9 us (15%)
  matrix products  28.3 us (15%)
  other arithmetic  16.3 us (9%)
  local copies, waits for them, and re-layouts  2.11 us (1%)
    ppermute x25, waiting for transfers between devices, partner_2(): return lax.ppermute(block, axis, route)  70.4 us
    ppermute x25, starting transfers between devices, partner_2(): return lax.ppermute(block, axis, route)  38.3 us
    pallas_call x4, Pallas kernels, attention(): pl.pallas_call(functools.partial(attention_kernel, scale=score_scale, par...  28.9 us
    dot_general x33, matrix products, apply(): jnp.einsum('pr,krw->kpw', matrix, rows.astype(jnp.float32), precision=lax...  28.3 us
    concatenate x4, other arithmetic, body(): jnp.concatenate(p, axis=1).astype(jnp.bfloat16)  5.42 us
    convert_element_type x8, other arithmetic, body(): returned = partner_2(outgoing.astype(jnp.bfloat16), 'seq', step_level)  4.67 us
    another operation x4, other arithmetic, body(): own = jnp.stack((key_rows[:, columns], value_rows[:, columns]))  3.94 us
  transfers between devices with their start and end apart: 25, of which 13 were waited for; matrix products, arithmetic and copies ran while one was open for 21% of the time, Pallas kernels for 16%

profile of v6, /device:TPU:0, one launch (start us, length us, event | category | flops | bytes accessed | tf_op | source)
XLA Modules:
  0.0 185.8 jit_solution(10365700402954235427)
XLA Ops:
  0.7 3.7 %fusion.340 = (bf16[2,64,2048]{2,1,0:T(8,128)(2,1)}, f32[2,64,2048]{2,1,0:T(8,128)S(1)}) fusion(s32[128,256]{1,0:T(8,128)S(1)} %broadcast_select_fusion, bf16[1,256,2048]{2,1,0:T(8,128)(2,1)} %bitcast.199, bf16[1,256,2048]{2,1,0:T(8,128)(2,1)} %bitcast.200), kind=kOutput, calls=%fused_computation.423 | convolution fusion | flops 806666240 | bytes 3735552 | tf_op jit(solution)/shard_map/pr,krw->kpw/dot_general | solution.py:99
  4.4 3.0 %collective-permute-start = (bf16[2,64,2048]{2,1,0:T(8,128)(2,1)}, bf16[2,64,2048]{2,1,0:T(8,128)(2,1)}, u32[]{:S(2)}, u32[]{:S(2)}) collective-permute-start(bf16[2,64,2048]{2,1,0:T(8,128)(2,1)} %get-tuple-element.76), channel_id=1, source_target_pairs={{0,4},{4,0},{8,12},{12,8},{16,20},{20,16},{24,28},{28,24},{1,5},{5... | collective-permute-start | bytes 1572872 | tf_op jit(solution)/shard_map/ppermute | solution.py:22
  11.1 2.0 %pad_maximum_fusion.5.refs_0_ = bf16[2,256,512]{2,1,0:T(8,128)(2,1)} fusion(bf16[1,256,512]{2,1,0:T(8,128)(2,1)S(1)} %copy-done.13, bf16[1,256,512]{2,1,0:T(8,128)(2,1)} %get-tuple-element.88), kind=kLoop, calls=%fused_computation.57 | loop fusion | flops 262144 | bytes 1048576 | tf_op jit(solution)/shard_map/stack | solution.py:128
  15.3 4.3 %collective-permute-done = bf16[2,64,2048]{2,1,0:T(8,128)(2,1)} collective-permute-done((bf16[2,64,2048]{2,1,0:T(8,128)(2,1)}, bf16[2,64,2048]{2,1,0:T(8,128)(2,1)}, u32[]{:S(2)}, u32[]{:S(2)}) %collective-permute-start) | collective-permute-done | bytes 524320 | tf_op jit(solution)/shard_map/ppermute | solution.py:22
  19.6 1.3 fusion.344
  20.9 1.9 %collective-permute-start.2 = (bf16[2,128,512]{2,1,0:T(8,128)(2,1)S(1)}, bf16[2,128,512]{2,1,0:T(8,128)(2,1)S(1)}, u32[]{:S(2)}, u32[]{:S(2)}) collective-permute-start(bf16[2,128,512]{2,1,0:T(8,128)(2,1)S(1)} %get-tuple-element.84), channel_id=1, source_target_pairs={{0,8},{8,0},{4,12},{12,4},{16,24},{24,16},{20,28},{28,20},{1,9},{9... | collective-permute-start | bytes 786440 | tf_op jit(solution)/shard_map/ppermute | solution.py:22
  22.8 1.5 collective-permute-start.1
  24.9 1.3 fusion.343
  29.7 1.9 %collective-permute-start.8 = (bf16[2,128,512]{2,1,0:T(8,128)(2,1)S(1)}, bf16[2,128,512]{2,1,0:T(8,128)(2,1)S(1)}, u32[]{:S(2)}, u32[]{:S(2)}) collective-permute-start(bf16[2,128,512]{2,1,0:T(8,128)(2,1)S(1)} %get-tuple-element.80), channel_id=1, source_target_pairs={{0,8},{8,0},{4,12},{12,4},{16,24},{24,16},{20,28},{28,20},{1,9},{9... | collective-permute-start | bytes 786440 | tf_op jit(solution)/shard_map/ppermute | solution.py:22
  31.5 1.3 fusion.341
  34.2 4.8 %collective-permute-done.5.refs_2_ = bf16[2,128,512]{2,1,0:T(8,128)(2,1)S(1)} collective-permute-done((bf16[2,128,512]{2,1,0:T(8,128)(2,1)S(1)}, bf16[2,128,512]{2,1,0:T(8,128)(2,1)S(1)}, u32[]{:S(2)}, u32[]{:S(2)}) %collective-permute-start.5) | collective-permute-done | bytes 262176 | tf_op jit(solution)/shard_map/ppermute | solution.py:22
  39.5 7.8 %collective-permute-done.8.refs_2_ = bf16[2,128,512]{2,1,0:T(8,128)(2,1)S(1)} collective-permute-done((bf16[2,128,512]{2,1,0:T(8,128)(2,1)S(1)}, bf16[2,128,512]{2,1,0:T(8,128)(2,1)S(1)}, u32[]{:S(2)}, u32[]{:S(2)}) %collective-permute-start.8) | collective-permute-done | bytes 262176 | tf_op jit(solution)/shard_map/ppermute | solution.py:22
  48.2 2.8 %collective-permute-done.11.refs_2_ = bf16[2,128,512]{2,1,0:T(8,128)(2,1)S(1)} collective-permute-done((bf16[2,128,512]{2,1,0:T(8,128)(2,1)S(1)}, bf16[2,128,512]{2,1,0:T(8,128)(2,1)S(1)}, u32[]{:S(2)}, u32[]{:S(2)}) %collective-permute-start.11) | collective-permute-done | bytes 262176 | tf_op jit(solution)/shard_map/ppermute | solution.py:22
  51.0 1.6 collective-permute-start.6
  53.8 2.1 %collective-permute-start.9 = (bf16[2,128,512]{2,1,0:T(8,128)(2,1)S(1)}, bf16[2,128,512]{2,1,0:T(8,128)(2,1)}, u32[]{:S(2)}, u32[]{:S(2)}) collective-permute-start(bf16[2,128,512]{2,1,0:T(8,128)(2,1)S(1)} %fusion.16), channel_id=1, source_target_pairs={{0,16},{16,0},{4,20},{20,4},{8,24},{24,8},{12,28},{28,12},{1,17},{... | collective-permute-start | bytes 786440 | tf_op jit(solution)/shard_map/ppermute | solution.py:22
  56.3 11.8 %collective-permute-done.6.refs_3_ = bf16[2,128,512]{2,1,0:T(8,128)(2,1)S(1)} collective-permute-done((bf16[2,128,512]{2,1,0:T(8,128)(2,1)S(1)}, bf16[2,128,512]{2,1,0:T(8,128)(2,1)S(1)}, u32[]{:S(2)}, u32[]{:S(2)}) %collective-permute-start.6) | collective-permute-done | bytes 262176 | tf_op jit(solution)/shard_map/ppermute | solution.py:22
  68.2 7.3 %shard_map.75 = (bf16[256,512]{1,0:T(8,128)(2,1)}, bf16[256,512]{1,0:T(8,128)(2,1)}, f32[2,256,512]{2,1,0:T(8,128)}, f32[2,256,512]{2,1,0:T(8,128)}, f32[2,128,512]{2,1,0:T(8,128)}, /*index=5*/f32[2,128,512]{2,1,0:T(8,128)}) custom-call(f32[1,768]{1,0:T(1,128)} %constant.88.clone.1.bias_ref, bf16[256,2048]{1,0:T(8,128)(2,1)} %q_ref.7, ...), custom_call_target="tpu_custom_call" | custom-call | flops 1207959552 | bytes 5767168 | tf_op jit(solution)/shard_map/pallas_call | solution.py:71
  76.7 3.0 %collective-permute-start.13 = (bf16[2,128,512]{2,1,0:T(8,128)(2,1)S(1)}, bf16[2,128,512]{2,1,0:T(8,128)(2,1)S(1)}, u32[]{:S(2)}, u32[]{:S(2)}) collective-permute-start(bf16[2,128,512]{2,1,0:T(8,128)(2,1)S(1)} %convert_element_type.127), channel_id=1, source_target_pairs={{0,16},{16,0},{4,20},{20,4},{8,24},{24,8},{12,28},{28,12},{1,17},{... | collective-permute-start | bytes 786440 | tf_op jit(solution)/shard_map/ppermute | solution.py:22
  79.6 7.2 %shard_map.76 = (bf16[256,512]{1,0:T(8,128)(2,1)}, bf16[256,512]{1,0:T(8,128)(2,1)}, f32[2,256,512]{2,1,0:T(8,128)}, f32[2,256,512]{2,1,0:T(8,128)}, f32[2,128,512]{2,1,0:T(8,128)}, /*index=5*/f32[2,128,512]{2,1,0:T(8,128)}) custom-call(f32[1,768]{1,0:T(1,128)} %constant.88.clone.1.bias_ref, bf16[256,2048]{1,0:T(8,128)(2,1)} %q_ref.7, ...), custom_call_target="tpu_custom_call" | custom-call | flops 1207959552 | bytes 5767168 | tf_op jit(solution)/shard_map/pallas_call | solution.py:71
  88.8 7.2 %shard_map.77 = (bf16[256,512]{1,0:T(8,128)(2,1)}, bf16[256,512]{1,0:T(8,128)(2,1)}, f32[2,256,512]{2,1,0:T(8,128)}, f32[2,256,512]{2,1,0:T(8,128)}, f32[2,128,512]{2,1,0:T(8,128)}, /*index=5*/f32[2,128,512]{2,1,0:T(8,128)}) custom-call(f32[1,768]{1,0:T(1,128)} %constant.88.clone.1.bias_ref, bf16[256,2048]{1,0:T(8,128)(2,1)} %q_ref.7, ...), custom_call_target="tpu_custom_call" | custom-call | flops 1207959552 | bytes 5767168 | tf_op jit(solution)/shard_map/pallas_call | solution.py:71
  97.0 2.3 %collective-permute-start.19 = (bf16[2,128,512]{2,1,0:T(8,128)(2,1)S(1)}, bf16[2,128,512]{2,1,0:T(8,128)(2,1)S(1)}, u32[]{:S(2)}, u32[]{:S(2)}) collective-permute-start(bf16[2,128,512]{2,1,0:T(8,128)(2,1)S(1)} %convert_element_type.137), channel_id=1, source_target_pairs={{0,16},{16,0},{4,20},{20,4},{8,24},{24,8},{12,28},{28,12},{1,17},{... | collective-permute-start | bytes 786440 | tf_op jit(solution)/shard_map/ppermute | solution.py:22
  99.3 7.1 %shard_map.78 = (bf16[256,512]{1,0:T(8,128)(2,1)}, bf16[256,512]{1,0:T(8,128)(2,1)}, f32[2,256,512]{2,1,0:T(8,128)}, f32[2,256,512]{2,1,0:T(8,128)}, f32[2,128,512]{2,1,0:T(8,128)}, /*index=5*/f32[2,128,512]{2,1,0:T(8,128)}) custom-call(f32[1,768]{1,0:T(1,128)} %constant.88.clone.1.bias_ref, bf16[256,2048]{1,0:T(8,128)(2,1)} %q_ref.7, ...), custom_call_target="tpu_custom_call" | custom-call | flops 1207959552 | bytes 5767168 | tf_op jit(solution)/shard_map/pallas_call | solution.py:71
  108.3 2.1 %pad_maximum_fusion.1 = bf16[256,2048]{1,0:T(8,128)(2,1)} fusion(bf16[256,512]{1,0:T(8,128)(2,1)} %get-tuple-element.43, bf16[256,512]{1,0:T(8,128)(2,1)S(1)} %copy-done.30, bf16[256,512]{1,0:T(8,128)(2,1)S(1)} %copy-done.28, bf16[256,512]{1,0:T(8,128)(2,1)S(1)} %copy-done.26), kind=kLoop, calls=%fused_computation.45 | loop fusion | flops 4194304 | bytes 2097152 | tf_op jit(solution)/shard_map/concatenate | solution.py:163
  112.2 9.9 %collective-permute-start.14 = (bf16[2,128,512]{2,1,0:T(8,128)(2,1)S(1)}, bf16[2,128,512]{2,1,0:T(8,128)(2,1)S(1)}, u32[]{:S(2)}, u32[]{:S(2)}) collective-permute-start(bf16[2,128,512]{2,1,0:T(8,128)(2,1)S(1)} %add_convert_fusion.11), channel_id=1, source_target_pairs={{0,8},{8,0},{4,12},{12,4},{16,24},{24,16},{20,28},{28,20},{1,9},{9... | collective-permute-start | bytes 786440 | tf_op jit(solution)/shard_map/ppermute | solution.py:22
  123.2 4.1 %collective-permute-done.19 = bf16[2,128,512]{2,1,0:T(8,128)(2,1)S(1)} collective-permute-done((bf16[2,128,512]{2,1,0:T(8,128)(2,1)S(1)}, bf16[2,128,512]{2,1,0:T(8,128)(2,1)S(1)}, u32[]{:S(2)}, u32[]{:S(2)}) %collective-permute-start.19) | collective-permute-done | bytes 262176 | tf_op jit(solution)/shard_map/ppermute | solution.py:22
  127.9 3.7 %collective-permute-done.22 = bf16[2,128,512]{2,1,0:T(8,128)(2,1)S(1)} collective-permute-done((bf16[2,128,512]{2,1,0:T(8,128)(2,1)S(1)}, bf16[2,128,512]{2,1,0:T(8,128)(2,1)S(1)}, u32[]{:S(2)}, u32[]{:S(2)}) %collective-permute-start.22) | collective-permute-done | bytes 262176 | tf_op jit(solution)/shard_map/ppermute | solution.py:22
  132.3 4.1 %collective-permute-done.14 = bf16[2,128,512]{2,1,0:T(8,128)(2,1)S(1)} collective-permute-done((bf16[2,128,512]{2,1,0:T(8,128)(2,1)S(1)}, bf16[2,128,512]{2,1,0:T(8,128)(2,1)S(1)}, u32[]{:S(2)}, u32[]{:S(2)}) %collective-permute-start.14) | collective-permute-done | bytes 262176 | tf_op jit(solution)/shard_map/ppermute | solution.py:22
  138.4 2.5 %collective-permute-start.15 = (bf16[2,256,512]{2,1,0:T(8,128)(2,1)S(1)}, bf16[2,256,512]{2,1,0:T(8,128)(2,1)S(1)}, u32[]{:S(2)}, u32[]{:S(2)}) collective-permute-start(bf16[2,256,512]{2,1,0:T(8,128)(2,1)S(1)} %add_convert_fusion.7), channel_id=1, source_target_pairs={{0,4},{4,0},{8,12},{12,8},{16,20},{20,16},{24,28},{28,24},{1,5},{5... | collective-permute-start | bytes 1572872 | tf_op jit(solution)/shard_map/ppermute | solution.py:22
  144.1 2.5 %collective-permute-start.18 = (bf16[2,256,512]{2,1,0:T(8,128)(2,1)S(1)}, bf16[2,256,512]{2,1,0:T(8,128)(2,1)S(1)}, u32[]{:S(2)}, u32[]{:S(2)}) collective-permute-start(bf16[2,256,512]{2,1,0:T(8,128)(2,1)S(1)} %add_convert_fusion.5), channel_id=1, source_target_pairs={{0,4},{4,0},{8,12},{12,8},{16,20},{20,16},{24,28},{28,24},{1,5},{5... | collective-permute-start | bytes 1572872 | tf_op jit(solution)/shard_map/ppermute | solution.py:22
  157.6 7.4 %collective-permute-done.18 = bf16[2,256,512]{2,1,0:T(8,128)(2,1)S(1)} collective-permute-done((bf16[2,256,512]{2,1,0:T(8,128)(2,1)S(1)}, bf16[2,256,512]{2,1,0:T(8,128)(2,1)S(1)}, u32[]{:S(2)}, u32[]{:S(2)}) %collective-permute-start.18) | collective-permute-done | bytes 524320 | tf_op jit(solution)/shard_map/ppermute | solution.py:22
  165.4 10.9 %collective-permute-done.21 = bf16[2,256,512]{2,1,0:T(8,128)(2,1)S(1)} collective-permute-done((bf16[2,256,512]{2,1,0:T(8,128)(2,1)S(1)}, bf16[2,256,512]{2,1,0:T(8,128)(2,1)S(1)}, u32[]{:S(2)}, u32[]{:S(2)}) %collective-permute-start.21) | collective-permute-done | bytes 524320 | tf_op jit(solution)/shard_map/ppermute | solution.py:22
  176.6 6.6 %collective-permute-done.24 = bf16[2,256,512]{2,1,0:T(8,128)(2,1)S(1)} collective-permute-done((bf16[2,256,512]{2,1,0:T(8,128)(2,1)S(1)}, bf16[2,256,512]{2,1,0:T(8,128)(2,1)S(1)}, u32[]{:S(2)}, u32[]{:S(2)}) %collective-permute-start.24) | collective-permute-done | bytes 524320 | tf_op jit(solution)/shard_map/ppermute | solution.py:22
  (165 shorter events, 43.1 us)
Async XLA Ops:
  4.4 15.2 %collective-permute-start = (bf16[2,64,2048]{2,1,0:T(8,128)(2,1)}, bf16[2,64,2048]{2,1,0:T(8,128)(2,1)}, u32[]{:S(2)}, u32[]{:S(2)}) collective-permute-start(bf16[2,64,2048]{2,1,0:T(8,128)(2,1)} %get-tuple-element.76), channel_id=1, source_target_pairs={{0,4},{4,0},{8,12},{12,8},{16,20},{20,16},{24,28},{28,24},{1,5},{5... | collective-permute-start | bytes 1572872 | tf_op jit(solution)/shard_map/ppermute | solution.py:22
  11.1 11.7 %copy-start.16 = (bf16[2,256,512]{2,1,0:T(8,128)(2,1)}, bf16[2,256,512]{2,1,0:T(8,128)(2,1)S(1)}, u32[]{:S(2)}) copy-start(bf16[2,256,512]{2,1,0:T(8,128)(2,1)S(1)} %pad_maximum_fusion.4.refs_0_) | copy-start | bytes 1572868
  14.0 39.0 %copy-start.15 = (bf16[2,256,512]{2,1,0:T(8,128)(2,1)}, bf16[2,256,512]{2,1,0:T(8,128)(2,1)S(1)}, u32[]{:S(2)}) copy-start(bf16[2,256,512]{2,1,0:T(8,128)(2,1)S(1)} %pad_maximum_fusion.7.refs_0_) | copy-start | bytes 1572868
  20.9 12.5 %collective-permute-start.2 = (bf16[2,128,512]{2,1,0:T(8,128)(2,1)S(1)}, bf16[2,128,512]{2,1,0:T(8,128)(2,1)S(1)}, u32[]{:S(2)}, u32[]{:S(2)}) collective-permute-start(bf16[2,128,512]{2,1,0:T(8,128)(2,1)S(1)} %get-tuple-element.84), channel_id=1, source_target_pairs={{0,8},{8,0},{4,12},{12,4},{16,24},{24,16},{20,28},{28,20},{1,9},{9... | collective-permute-start | bytes 786440 | tf_op jit(solution)/shard_map/ppermute | solution.py:22
  22.8 31.0 %collective-permute-start.1 = (bf16[2,256,512]{2,1,0:T(8,128)(2,1)S(1)}, bf16[2,256,512]{2,1,0:T(8,128)(2,1)S(1)}, u32[]{:S(2)}, u32[]{:S(2)}) collective-permute-start(bf16[2,256,512]{2,1,0:T(8,128)(2,1)S(1)} %pad_maximum_fusion.4.refs_0_), channel_id=1, source_target_pairs={{0,4},{4,0},{8,12},{12,8},{16,20},{20,16},{24,28},{28,24},{1,5},{5... | collective-permute-start | bytes 1572872 | tf_op jit(solution)/shard_map/ppermute | solution.py:22
  26.9 12.1 %collective-permute-start.5 = (bf16[2,128,512]{2,1,0:T(8,128)(2,1)S(1)}, bf16[2,128,512]{2,1,0:T(8,128)(2,1)S(1)}, u32[]{:S(2)}, u32[]{:S(2)}) collective-permute-start(bf16[2,128,512]{2,1,0:T(8,128)(2,1)S(1)} %get-tuple-element.82), channel_id=1, source_target_pairs={{0,8},{8,0},{4,12},{12,4},{16,24},{24,16},{20,28},{28,20},{1,9},{9... | collective-permute-start | bytes 786440 | tf_op jit(solution)/shard_map/ppermute | solution.py:22
  27.4 49.2 %collective-permute-start.4 = (bf16[2,256,512]{2,1,0:T(8,128)(2,1)}, bf16[2,256,512]{2,1,0:T(8,128)(2,1)S(1)}, u32[]{:S(2)}, u32[]{:S(2)}) collective-permute-start(bf16[2,256,512]{2,1,0:T(8,128)(2,1)} %pad_maximum_fusion.5.refs_0_), channel_id=1, source_target_pairs={{0,4},{4,0},{8,12},{12,8},{16,20},{20,16},{24,28},{28,24},{1,5},{5... | collective-permute-start | bytes 1572872 | tf_op jit(solution)/shard_map/ppermute | solution.py:22
  29.7 17.6 %collective-permute-start.8 = (bf16[2,128,512]{2,1,0:T(8,128)(2,1)S(1)}, bf16[2,128,512]{2,1,0:T(8,128)(2,1)S(1)}, u32[]{:S(2)}, u32[]{:S(2)}) collective-permute-start(bf16[2,128,512]{2,1,0:T(8,128)(2,1)S(1)} %get-tuple-element.80), channel_id=1, source_target_pairs={{0,8},{8,0},{4,12},{12,4},{16,24},{24,16},{20,28},{28,20},{1,9},{9... | collective-permute-start | bytes 786440 | tf_op jit(solution)/shard_map/ppermute | solution.py:22
  33.5 17.5 %collective-permute-start.11 = (bf16[2,128,512]{2,1,0:T(8,128)(2,1)S(1)}, bf16[2,128,512]{2,1,0:T(8,128)(2,1)S(1)}, u32[]{:S(2)}, u32[]{:S(2)}) collective-permute-start(bf16[2,128,512]{2,1,0:T(8,128)(2,1)S(1)} %get-tuple-element.78), channel_id=1, source_target_pairs={{0,8},{8,0},{4,12},{12,4},{16,24},{24,16},{20,28},{28,20},{1,9},{9... | collective-permute-start | bytes 786440 | tf_op jit(solution)/shard_map/ppermute | solution.py:22
  39.0 14.0 %copy-start.23 = (bf16[2,128,512]{2,1,0:T(8,128)(2,1)}, bf16[2,128,512]{2,1,0:T(8,128)(2,1)S(1)}, u32[]{:S(2)}) copy-start(bf16[2,128,512]{2,1,0:T(8,128)(2,1)S(1)} %collective-permute-done.5.refs_2_) | copy-start | bytes 786436
  39.0 14.0 %collective-permute-start.3 = (bf16[2,128,512]{2,1,0:T(8,128)(2,1)S(1)}, bf16[2,128,512]{2,1,0:T(8,128)(2,1)S(1)}, u32[]{:S(2)}, u32[]{:S(2)}) collective-permute-start(bf16[2,128,512]{2,1,0:T(8,128)(2,1)S(1)} %fusion.18), channel_id=1, source_target_pairs={{0,16},{16,0},{4,20},{20,4},{8,24},{24,8},{12,28},{28,12},{1,17},{... | collective-permute-start | bytes 786440 | tf_op jit(solution)/shard_map/ppermute | solution.py:22
  47.3 41.5 %collective-permute-start.7 = (bf16[2,256,512]{2,1,0:T(8,128)(2,1)}, bf16[2,256,512]{2,1,0:T(8,128)(2,1)}, u32[]{:S(2)}, u32[]{:S(2)}) collective-permute-start(bf16[2,256,512]{2,1,0:T(8,128)(2,1)} %pad_maximum_fusion.6.refs_0_), channel_id=1, source_target_pairs={{0,4},{4,0},{8,12},{12,8},{16,20},{20,16},{24,28},{28,24},{1,5},{5... | collective-permute-start | bytes 1572872 | tf_op jit(solution)/shard_map/ppermute | solution.py:22
  51.0 17.2 %collective-permute-start.6 = (bf16[2,128,512]{2,1,0:T(8,128)(2,1)S(1)}, bf16[2,128,512]{2,1,0:T(8,128)(2,1)S(1)}, u32[]{:S(2)}, u32[]{:S(2)}) collective-permute-start(bf16[2,128,512]{2,1,0:T(8,128)(2,1)S(1)} %fusion.17), channel_id=1, source_target_pairs={{0,16},{16,0},{4,20},{20,4},{8,24},{24,8},{12,28},{28,12},{1,17},{... | collective-permute-start | bytes 786440 | tf_op jit(solution)/shard_map/ppermute | solution.py:22
  53.0 15.1 %copy-start.35 = (bf16[2,128,512]{2,1,0:T(8,128)(2,1)}, bf16[2,128,512]{2,1,0:T(8,128)(2,1)S(1)}, u32[]{:S(2)}) copy-start(bf16[2,128,512]{2,1,0:T(8,128)(2,1)S(1)} %collective-permute-done.3.refs_3_) | copy-start | bytes 786436
  53.0 46.3 %collective-permute-start.10 = (bf16[2,256,512]{2,1,0:T(8,128)(2,1)S(1)}, bf16[2,256,512]{2,1,0:T(8,128)(2,1)}, u32[]{:S(2)}, u32[]{:S(2)}) collective-permute-start(bf16[2,256,512]{2,1,0:T(8,128)(2,1)S(1)} %pad_maximum_fusion.7.refs_0_), channel_id=1, source_target_pairs={{0,4},{4,0},{8,12},{12,8},{16,20},{20,16},{24,28},{28,24},{1,5},{5... | collective-permute-start | bytes 1572872 | tf_op jit(solution)/shard_map/ppermute | solution.py:22
  53.8 14.4 %copy-start.33 = (bf16[2,256,512]{2,1,0:T(8,128)(2,1)}, bf16[2,256,512]{2,1,0:T(8,128)(2,1)S(1)}, u32[]{:S(2)}) copy-start(bf16[2,256,512]{2,1,0:T(8,128)(2,1)S(1)} %collective-permute-done.1.refs_1_) | copy-start | bytes 1572868
  53.8 34.2 %collective-permute-start.9 = (bf16[2,128,512]{2,1,0:T(8,128)(2,1)S(1)}, bf16[2,128,512]{2,1,0:T(8,128)(2,1)}, u32[]{:S(2)}, u32[]{:S(2)}) collective-permute-start(bf16[2,128,512]{2,1,0:T(8,128)(2,1)S(1)} %fusion.16), channel_id=1, source_target_pairs={{0,16},{16,0},{4,20},{20,4},{8,24},{24,8},{12,28},{28,12},{1,17},{... | collective-permute-start | bytes 786440 | tf_op jit(solution)/shard_map/ppermute | solution.py:22
  68.2 31.2 %collective-permute-start.12 = (bf16[2,128,512]{2,1,0:T(8,128)(2,1)S(1)}, bf16[2,128,512]{2,1,0:T(8,128)(2,1)}, u32[]{:S(2)}, u32[]{:S(2)}) collective-permute-start(bf16[2,128,512]{2,1,0:T(8,128)(2,1)S(1)} %fusion.15), channel_id=1, source_target_pairs={{0,16},{16,0},{4,20},{20,4},{8,24},{24,8},{12,28},{28,12},{1,17},{... | collective-permute-start | bytes 786440 | tf_op jit(solution)/shard_map/ppermute | solution.py:22
  76.7 34.9 %collective-permute-start.13 = (bf16[2,128,512]{2,1,0:T(8,128)(2,1)S(1)}, bf16[2,128,512]{2,1,0:T(8,128)(2,1)S(1)}, u32[]{:S(2)}, u32[]{:S(2)}) collective-permute-start(bf16[2,128,512]{2,1,0:T(8,128)(2,1)S(1)} %convert_element_type.127), channel_id=1, source_target_pairs={{0,16},{16,0},{4,20},{20,4},{8,24},{24,8},{12,28},{28,12},{1,17},{... | collective-permute-start | bytes 786440 | tf_op jit(solution)/shard_map/ppermute | solution.py:22
  88.0 34.2 %collective-permute-start.16 = (bf16[2,128,512]{2,1,0:T(8,128)(2,1)S(1)}, bf16[2,128,512]{2,1,0:T(8,128)(2,1)S(1)}, u32[]{:S(2)}, u32[]{:S(2)}) collective-permute-start(bf16[2,128,512]{2,1,0:T(8,128)(2,1)S(1)} %convert_element_type.132), channel_id=1, source_target_pairs={{0,16},{16,0},{4,20},{20,4},{8,24},{24,8},{12,28},{28,12},{1,17},{... | collective-permute-start | bytes 786440 | tf_op jit(solution)/shard_map/ppermute | solution.py:22
  97.0 11.3 %copy-start.26 = (bf16[256,512]{1,0:T(8,128)(2,1)S(1)}, bf16[256,512]{1,0:T(8,128)(2,1)}, u32[]{:S(2)}) copy-start(bf16[256,512]{1,0:T(8,128)(2,1)} %get-tuple-element.40) | copy-start | bytes 786436
  97.0 11.3 %copy-start.28 = (bf16[256,512]{1,0:T(8,128)(2,1)S(1)}, bf16[256,512]{1,0:T(8,128)(2,1)}, u32[]{:S(2)}) copy-start(bf16[256,512]{1,0:T(8,128)(2,1)} %get-tuple-element.41) | copy-start | bytes 786436
  97.0 30.2 %collective-permute-start.19 = (bf16[2,128,512]{2,1,0:T(8,128)(2,1)S(1)}, bf16[2,128,512]{2,1,0:T(8,128)(2,1)S(1)}, u32[]{:S(2)}, u32[]{:S(2)}) collective-permute-start(bf16[2,128,512]{2,1,0:T(8,128)(2,1)S(1)} %convert_element_type.137), channel_id=1, source_target_pairs={{0,16},{16,0},{4,20},{20,4},{8,24},{24,8},{12,28},{28,12},{1,17},{... | collective-permute-start | bytes 786440 | tf_op jit(solution)/shard_map/ppermute | solution.py:22
  107.5 24.1 %collective-permute-start.22 = (bf16[2,128,512]{2,1,0:T(8,128)(2,1)S(1)}, bf16[2,128,512]{2,1,0:T(8,128)(2,1)S(1)}, u32[]{:S(2)}, u32[]{:S(2)}) collective-permute-start(bf16[2,128,512]{2,1,0:T(8,128)(2,1)S(1)} %convert_element_type.142), channel_id=1, source_target_pairs={{0,16},{16,0},{4,20},{20,4},{8,24},{24,8},{12,28},{28,12},{1,17},{... | collective-permute-start | bytes 786440 | tf_op jit(solution)/shard_map/ppermute | solution.py:22
  112.2 24.2 %collective-permute-start.14 = (bf16[2,128,512]{2,1,0:T(8,128)(2,1)S(1)}, bf16[2,128,512]{2,1,0:T(8,128)(2,1)S(1)}, u32[]{:S(2)}, u32[]{:S(2)}) collective-permute-start(bf16[2,128,512]{2,1,0:T(8,128)(2,1)S(1)} %add_convert_fusion.11), channel_id=1, source_target_pairs={{0,8},{8,0},{4,12},{12,4},{16,24},{24,16},{20,28},{28,20},{1,9},{9... | collective-permute-start | bytes 786440 | tf_op jit(solution)/shard_map/ppermute | solution.py:22
  122.7 19.3 %collective-permute-start.17 = (bf16[2,128,512]{2,1,0:T(8,128)(2,1)S(1)}, bf16[2,128,512]{2,1,0:T(8,128)(2,1)S(1)}, u32[]{:S(2)}, u32[]{:S(2)}) collective-permute-start(bf16[2,128,512]{2,1,0:T(8,128)(2,1)S(1)} %add_convert_fusion.10), channel_id=1, source_target_pairs={{0,8},{8,0},{4,12},{12,4},{16,24},{24,16},{20,28},{28,20},{1,9},{9... | collective-permute-start | bytes 786440 | tf_op jit(solution)/shard_map/ppermute | solution.py:22
  127.8 19.8 %collective-permute-start.20 = (bf16[2,128,512]{2,1,0:T(8,128)(2,1)S(1)}, bf16[2,128,512]{2,1,0:T(8,128)(2,1)S(1)}, u32[]{:S(2)}, u32[]{:S(2)}) collective-permute-start(bf16[2,128,512]{2,1,0:T(8,128)(2,1)S(1)} %add_convert_fusion.9), channel_id=1, source_target_pairs={{0,8},{8,0},{4,12},{12,4},{16,24},{24,16},{20,28},{28,20},{1,9},{9... | collective-permute-start | bytes 786440 | tf_op jit(solution)/shard_map/ppermute | solution.py:22
  132.2 19.6 %collective-permute-start.23 = (bf16[2,128,512]{2,1,0:T(8,128)(2,1)S(1)}, bf16[2,128,512]{2,1,0:T(8,128)(2,1)S(1)}, u32[]{:S(2)}, u32[]{:S(2)}) collective-permute-start(bf16[2,128,512]{2,1,0:T(8,128)(2,1)S(1)} %add_convert_fusion.8), channel_id=1, source_target_pairs={{0,8},{8,0},{4,12},{12,4},{16,24},{24,16},{20,28},{28,20},{1,9},{9... | collective-permute-start | bytes 786440 | tf_op jit(solution)/shard_map/ppermute | solution.py:22
  138.4 18.7 %collective-permute-start.15 = (bf16[2,256,512]{2,1,0:T(8,128)(2,1)S(1)}, bf16[2,256,512]{2,1,0:T(8,128)(2,1)S(1)}, u32[]{:S(2)}, u32[]{:S(2)}) collective-permute-start(bf16[2,256,512]{2,1,0:T(8,128)(2,1)S(1)} %add_convert_fusion.7), channel_id=1, source_target_pairs={{0,4},{4,0},{8,12},{12,8},{16,20},{20,16},{24,28},{28,24},{1,5},{5... | collective-permute-start | bytes 1572872 | tf_op jit(solution)/shard_map/ppermute | solution.py:22
  144.1 21.0 %collective-permute-start.18 = (bf16[2,256,512]{2,1,0:T(8,128)(2,1)S(1)}, bf16[2,256,512]{2,1,0:T(8,128)(2,1)S(1)}, u32[]{:S(2)}, u32[]{:S(2)}) collective-permute-start(bf16[2,256,512]{2,1,0:T(8,128)(2,1)S(1)} %add_convert_fusion.5), channel_id=1, source_target_pairs={{0,4},{4,0},{8,12},{12,8},{16,20},{20,16},{24,28},{28,24},{1,5},{5... | collective-permute-start | bytes 1572872 | tf_op jit(solution)/shard_map/ppermute | solution.py:22
  149.7 26.6 %collective-permute-start.21 = (bf16[2,256,512]{2,1,0:T(8,128)(2,1)S(1)}, bf16[2,256,512]{2,1,0:T(8,128)(2,1)S(1)}, u32[]{:S(2)}, u32[]{:S(2)}) collective-permute-start(bf16[2,256,512]{2,1,0:T(8,128)(2,1)S(1)} %add_convert_fusion.3), channel_id=1, source_target_pairs={{0,4},{4,0},{8,12},{12,8},{16,20},{20,16},{24,28},{28,24},{1,5},{5... | collective-permute-start | bytes 1572872 | tf_op jit(solution)/shard_map/ppermute | solution.py:22
  153.9 29.4 %collective-permute-start.24 = (bf16[2,256,512]{2,1,0:T(8,128)(2,1)S(1)}, bf16[2,256,512]{2,1,0:T(8,128)(2,1)S(1)}, u32[]{:S(2)}, u32[]{:S(2)}) collective-permute-start(bf16[2,256,512]{2,1,0:T(8,128)(2,1)S(1)} %add_convert_fusion.1), channel_id=1, source_target_pairs={{0,4},{4,0},{8,12},{12,8},{16,20},{20,16},{24,28},{28,24},{1,5},{5... | collective-permute-start | bytes 1572872 | tf_op jit(solution)/shard_map/ppermute | solution.py:22
  (29 other events, 129.1 us)

commit v7 on v6

--- a/solution.py
+++ b/solution.py
@@ -118,11 +118,15 @@
     mine = [placed_pool(leaf_rows if s == 0 else POOLED, bits[s]) for s in range(levels)]
     other = [placed_pool(leaf_rows if s == 0 else POOLED, 1 - bits[s]) for s in range(levels)]
     pool_own = placed_pool(leaf_rows, 0)[: POOLED // 2]
-    own_pooled = apply(pool_own, jnp.stack((key_rows, value_rows)))
+    own_pooled = jnp.einsum(
+        "pr,krw->kpw", pool_own.astype(jnp.bfloat16), jnp.stack((key_rows, value_rows)),
+        preferred_element_type=jnp.float32,
+    )
     sibling_pooled = partner_2(own_pooled.astype(jnp.bfloat16), "seq", 0)
     place_mine = placed_pool(POOLED // 2, bits[0])
     place_other = placed_pool(POOLED // 2, 1 - bits[0])
     pieces = [[], [], [], []]
+    late = []
     for chunk in range(CHUNKS):
         columns = slice(chunk * chunk_width, (chunk + 1) * chunk_width)
         own = jnp.stack((key_rows[:, columns], value_rows[:, columns]))
@@ -136,17 +140,24 @@
             far.append(partner)
             if step_level + 1 < levels:
                 summary = apply(mine[step_level], summary) + apply(other[step_level], partner)
+        held = own
+        if chunk >= 2:
+            held = after(held, late[chunk - 2][1])
+        if chunk >= 3:
+            held = after(held, late[chunk - 3][0])
         outs = attention(
-            query_rows, out_grad, [own, sibling] + far, key_bias, score_scale,
+            query_rows, out_grad, [held, sibling] + far, key_bias, score_scale,
             chunk * (chunk_width // HEAD_DIM),
         )
         attended, query_grad, terms = outs[0], outs[1], outs[2:]
         grad = None
+        sends = {}
         for step_level in reversed(range(1, levels)):
             outgoing = terms[1 + step_level]
             if grad is not None:
                 outgoing = outgoing + apply(other[step_level].T, grad)
-            returned = partner_2(outgoing.astype(jnp.bfloat16), "seq", step_level)
+            sends[step_level] = outgoing.astype(jnp.bfloat16)
+            returned = partner_2(sends[step_level], "seq", step_level)
             if grad is None:
                 grad = returned.astype(jnp.float32)
             else:
@@ -156,7 +167,9 @@
         if grad is not None:
             to_sibling = to_sibling + apply(other[0].T, grad)
             own_total = own_total + apply(mine[0].T, grad)
-        from_sibling = partner_2(to_sibling.astype(jnp.bfloat16), "seq", 0)
+        sibling_send = to_sibling.astype(jnp.bfloat16)
+        late.append((sibling_send, sends.get(1, sibling_send)))
+        from_sibling = partner_2(sibling_send, "seq", 0)
         totals = own_total + from_sibling.astype(jnp.float32)
         for slot, piece in enumerate((attended, query_grad, totals[0], totals[1])):
             pieces[slot].append(piece)

time: 188 us -> 181 us (0.963)
  waiting for transfers between devices: 70.4 us -> 64.9 us
  starting transfers between devices: 38.3 us -> 33.6 us
  local copies, waits for them, and re-layouts: 2.11 us -> 5.1 us
  matrix products: 28.3 us -> 30.6 us
    ppermute x25, waiting for transfers between devices: 70.4 us -> 64.9 us  [partner_2(): return lax.ppermute(block, axis, route)]
    ppermute x25, starting transfers between devices: 38.3 us -> 33.6 us  [partner_2(): return lax.ppermute(block, axis, route)]
    unnamed x72 -> x78, local copies, waits for them, and re-layouts: 0.73 us -> 3.71 us
    dot_general x0 -> x1, matrix products: none -> 2.91 us  [body(): jnp.einsum('pr,krw->kpw', pool_own.astype(jnp.bfloat16), jnp.stack((key_r...]
    another operation x4, other arithmetic: 1.19 us -> 3.34 us
    dot_general x33 -> x32, matrix products: 28.3 us -> 27.7 us  [apply(): jnp.einsum('pr,krw->kpw', matrix, rows.astype(jnp.float32), precision=lax...]
  transfers between devices with their start and end apart: 25 -> 25, of which waited for: 13 -> 11; matrix products, arithmetic and copies ran while one was open for 21% -> 23% of each run, Pallas kernels for 16% -> 16%
where the time goes in v7:
time: 181 us; the launch traced here: 180 us
  waiting for transfers between devices  64.9 us (36%)
  starting transfers between devices  33.6 us (19%)
  matrix products  30.6 us (17%)
  Pallas kernels  28.8 us (16%)
  other arithmetic  15.7 us (9%)
  local copies, waits for them, and re-layouts  5.1 us (3%)
    ppermute x25, waiting for transfers between devices, partner_2(): return lax.ppermute(block, axis, route)  64.9 us
    ppermute x25, starting transfers between devices, partner_2(): return lax.ppermute(block, axis, route)  33.6 us
    pallas_call x4, Pallas kernels, attention(): pl.pallas_call(functools.partial(attention_kernel, scale=score_scale, par...  28.8 us
    dot_general x32, matrix products, apply(): jnp.einsum('pr,krw->kpw', matrix, rows.astype(jnp.float32), precision=lax...  27.7 us
    convert_element_type x8, other arithmetic, body(): sends[step_level] = outgoing.astype(jnp.bfloat16)  4.77 us
    concatenate x4, other arithmetic, body(): jnp.concatenate(p, axis=1).astype(jnp.bfloat16)  4.39 us
    unnamed x78, local copies, waits for them, and re-layouts  3.71 us
  transfers between devices with their start and end apart: 25, of which 11 were waited for; matrix products, arithmetic and copies ran while one was open for 23% of the time, Pallas kernels for 16%

profile of v7, /device:TPU:0, one launch (start us, length us, event | category | flops | bytes accessed | tf_op | source)
XLA Modules:
  0.0 180.1 jit_solution(16002526747122857786)
XLA Ops:
  0.7 2.9 %fusion.340 = (bf16[2,64,2048]{2,1,0:T(8,128)(2,1)}, f32[2,64,2048]{2,1,0:T(8,128)S(1)}) fusion(bf16[1,256,2048]{2,1,0:T(8,128)(2,1)} %bitcast.199, bf16[1,256,2048]{2,1,0:T(8,128)(2,1)} %bitcast.200, s32[128,256]{1,0:T(8,128)S(1)} %broadcast_select_fusion), kind=kOutput, calls=%fused_computation.423 | convolution fusion | flops 138739712 | bytes 3735552 | tf_op jit(solution)/shard_map/pr,krw->kpw/dot_general | solution.py:121
  3.6 3.0 %collective-permute-start = (bf16[2,64,2048]{2,1,0:T(8,128)(2,1)}, bf16[2,64,2048]{2,1,0:T(8,128)(2,1)}, u32[]{:S(2)}, u32[]{:S(2)}) collective-permute-start(bf16[2,64,2048]{2,1,0:T(8,128)(2,1)} %get-tuple-element.82), channel_id=1, source_target_pairs={{0,4},{4,0},{8,12},{12,8},{16,20},{20,16},{24,28},{28,24},{1,5},{5... | collective-permute-start | bytes 1572872 | tf_op jit(solution)/shard_map/ppermute | solution.py:22
  6.6 1.4 fusion.21
  8.0 1.4 fusion.23
  10.7 2.0 %pad_maximum_fusion.6.refs_0_ = bf16[2,256,512]{2,1,0:T(8,128)(2,1)} fusion(bf16[1,256,512]{2,1,0:T(8,128)(2,1)} %get-tuple-element.70, bf16[1,256,512]{2,1,0:T(8,128)(2,1)} %get-tuple-element.95), kind=kLoop, calls=%fused_computation.58 | loop fusion | flops 262144 | bytes 1048576 | tf_op jit(solution)/shard_map/stack | solution.py:132
  15.0 3.8 %collective-permute-done = bf16[2,64,2048]{2,1,0:T(8,128)(2,1)} collective-permute-done((bf16[2,64,2048]{2,1,0:T(8,128)(2,1)}, bf16[2,64,2048]{2,1,0:T(8,128)(2,1)}, u32[]{:S(2)}, u32[]{:S(2)}) %collective-permute-start) | collective-permute-done | bytes 524320 | tf_op jit(solution)/shard_map/ppermute | solution.py:22
  20.1 1.9 %collective-permute-start.2 = (bf16[2,128,512]{2,1,0:T(8,128)(2,1)S(1)}, bf16[2,128,512]{2,1,0:T(8,128)(2,1)S(1)}, u32[]{:S(2)}, u32[]{:S(2)}) collective-permute-start(bf16[2,128,512]{2,1,0:T(8,128)(2,1)S(1)} %get-tuple-element.86), channel_id=1, source_target_pairs={{0,8},{8,0},{4,12},{12,4},{16,24},{24,16},{20,28},{28,20},{1,9},{9... | collective-permute-start | bytes 786440 | tf_op jit(solution)/shard_map/ppermute | solution.py:22
  25.0 1.9 %collective-permute-start.9 = (bf16[2,128,512]{2,1,0:T(8,128)(2,1)S(1)}, bf16[2,128,512]{2,1,0:T(8,128)(2,1)S(1)}, u32[]{:S(2)}, u32[]{:S(2)}) collective-permute-start(bf16[2,128,512]{2,1,0:T(8,128)(2,1)S(1)} %get-tuple-element.90), channel_id=1, source_target_pairs={{0,8},{8,0},{4,12},{12,4},{16,24},{24,16},{20,28},{28,20},{1,9},{9... | collective-permute-start | bytes 786440 | tf_op jit(solution)/shard_map/ppermute | solution.py:22
  30.9 1.8 %collective-permute-start.13 = (bf16[2,256,512]{2,1,0:T(8,128)(2,1)S(1)}, bf16[2,256,512]{2,1,0:T(8,128)(2,1)}, u32[]{:S(2)}, u32[]{:S(2)}) collective-permute-start(bf16[2,256,512]{2,1,0:T(8,128)(2,1)S(1)} %pad_maximum_fusion.7.refs_0_), channel_id=1, source_target_pairs={{0,4},{4,0},{8,12},{12,8},{16,20},{20,16},{24,28},{28,24},{1,5},{5... | collective-permute-start | bytes 1572872 | tf_op jit(solution)/shard_map/ppermute | solution.py:22
  32.7 2.3 %collective-permute-done.5.refs_2_ = bf16[2,128,512]{2,1,0:T(8,128)(2,1)S(1)} collective-permute-done((bf16[2,128,512]{2,1,0:T(8,128)(2,1)S(1)}, bf16[2,128,512]{2,1,0:T(8,128)(2,1)S(1)}, u32[]{:S(2)}, u32[]{:S(2)}) %collective-permute-start.5) | collective-permute-done | bytes 262176 | tf_op jit(solution)/shard_map/ppermute | solution.py:22
  35.1 1.7 collective-permute-start.4
  37.3 2.6 %collective-permute-start.6 = (bf16[2,128,512]{2,1,0:T(8,128)(2,1)S(1)}, bf16[2,128,512]{2,1,0:T(8,128)(2,1)S(1)}, u32[]{:S(2)}, u32[]{:S(2)}) collective-permute-start(bf16[2,128,512]{2,1,0:T(8,128)(2,1)S(1)} %fusion.17), channel_id=1, source_target_pairs={{0,16},{16,0},{4,20},{20,4},{8,24},{24,8},{12,28},{28,12},{1,17},{... | collective-permute-start | bytes 786440 | tf_op jit(solution)/shard_map/ppermute | solution.py:22
  40.4 9.8 %collective-permute-done.14.refs_2_ = bf16[2,128,512]{2,1,0:T(8,128)(2,1)S(1)} collective-permute-done((bf16[2,128,512]{2,1,0:T(8,128)(2,1)S(1)}, bf16[2,128,512]{2,1,0:T(8,128)(2,1)S(1)}, u32[]{:S(2)}, u32[]{:S(2)}) %collective-permute-start.14) | collective-permute-done | bytes 262176 | tf_op jit(solution)/shard_map/ppermute | solution.py:22
  50.2 1.4 collective-permute-start.1
  53.4 3.7 %collective-permute-done.4.refs_1_ = bf16[2,256,512]{2,1,0:T(8,128)(2,1)S(1)} collective-permute-done((bf16[2,256,512]{2,1,0:T(8,128)(2,1)S(1)}, bf16[2,256,512]{2,1,0:T(8,128)(2,1)S(1)}, u32[]{:S(2)}, u32[]{:S(2)}) %collective-permute-start.4) | collective-permute-done | bytes 524320 | tf_op jit(solution)/shard_map/ppermute | solution.py:22
  57.9 2.8 %collective-permute-start.3 = (bf16[2,128,512]{2,1,0:T(8,128)(2,1)S(1)}, bf16[2,128,512]{2,1,0:T(8,128)(2,1)S(1)}, u32[]{:S(2)}, u32[]{:S(2)}) collective-permute-start(bf16[2,128,512]{2,1,0:T(8,128)(2,1)S(1)} %fusion.18), channel_id=1, source_target_pairs={{0,16},{16,0},{4,20},{20,4},{8,24},{24,8},{12,28},{28,12},{1,17},{... | collective-permute-start | bytes 786440 | tf_op jit(solution)/shard_map/ppermute | solution.py:22
  60.7 7.3 %shard_map.76 = (bf16[256,512]{1,0:T(8,128)(2,1)}, bf16[256,512]{1,0:T(8,128)(2,1)}, f32[2,256,512]{2,1,0:T(8,128)}, f32[2,256,512]{2,1,0:T(8,128)}, f32[2,128,512]{2,1,0:T(8,128)}, /*index=5*/f32[2,128,512]{2,1,0:T(8,128)}) custom-call(f32[1,768]{1,0:T(1,128)} %constant.88.clone.1.bias_ref, bf16[256,2048]{1,0:T(8,128)(2,1)} %q_ref.7, ...), custom_call_target="tpu_custom_call" | custom-call | flops 1207959552 | bytes 5767168 | tf_op jit(solution)/shard_map/pallas_call | solution.py:71
  69.7 10.9 %collective-permute-done.3.refs_3_ = bf16[2,128,512]{2,1,0:T(8,128)(2,1)S(1)} collective-permute-done((bf16[2,128,512]{2,1,0:T(8,128)(2,1)S(1)}, bf16[2,128,512]{2,1,0:T(8,128)(2,1)S(1)}, u32[]{:S(2)}, u32[]{:S(2)}) %collective-permute-start.3) | collective-permute-done | bytes 262176 | tf_op jit(solution)/shard_map/ppermute | solution.py:22
  80.6 2.9 %collective-permute-start.15 = (bf16[2,128,512]{2,1,0:T(8,128)(2,1)}, bf16[2,128,512]{2,1,0:T(8,128)(2,1)}, u32[]{:S(2)}, u32[]{:S(2)}) collective-permute-start(bf16[2,128,512]{2,1,0:T(8,128)(2,1)} %fusion.15), channel_id=1, source_target_pairs={{0,16},{16,0},{4,20},{20,4},{8,24},{24,8},{12,28},{28,12},{1,17},{... | collective-permute-start | bytes 786440 | tf_op jit(solution)/shard_map/ppermute | solution.py:22
  83.5 7.1 %shard_map.75 = (bf16[256,512]{1,0:T(8,128)(2,1)}, bf16[256,512]{1,0:T(8,128)(2,1)}, f32[2,256,512]{2,1,0:T(8,128)}, f32[2,256,512]{2,1,0:T(8,128)}, f32[2,128,512]{2,1,0:T(8,128)}, /*index=5*/f32[2,128,512]{2,1,0:T(8,128)}) custom-call(f32[1,768]{1,0:T(1,128)} %constant.88.clone.1.bias_ref, bf16[256,2048]{1,0:T(8,128)(2,1)} %q_ref.7, ...), custom_call_target="tpu_custom_call" | custom-call | flops 1207959552 | bytes 5767168 | tf_op jit(solution)/shard_map/pallas_call | solution.py:71
  92.6 20.3 %collective-permute-done.7 = bf16[2,128,512]{2,1,0:T(8,128)(2,1)S(1)} collective-permute-done((bf16[2,128,512]{2,1,0:T(8,128)(2,1)S(1)}, bf16[2,128,512]{2,1,0:T(8,128)(2,1)S(1)}, u32[]{:S(2)}, u32[]{:S(2)}) %collective-permute-start.7) | collective-permute-done | bytes 262176 | tf_op jit(solution)/shard_map/ppermute | solution.py:22
  115.6 7.2 %shard_map.77 = (bf16[256,512]{1,0:T(8,128)(2,1)}, bf16[256,512]{1,0:T(8,128)(2,1)}, f32[2,256,512]{2,1,0:T(8,128)}, f32[2,256,512]{2,1,0:T(8,128)}, f32[2,128,512]{2,1,0:T(8,128)}, /*index=5*/f32[2,128,512]{2,1,0:T(8,128)}) custom-call(f32[1,768]{1,0:T(1,128)} %constant.88.clone.1.bias_ref, bf16[256,2048]{1,0:T(8,128)(2,1)} %q_ref.7, ...), custom_call_target="tpu_custom_call" | custom-call | flops 1207959552 | bytes 5767168 | tf_op jit(solution)/shard_map/pallas_call | solution.py:71
  123.9 2.4 %collective-permute-start.19 = (bf16[2,128,512]{2,1,0:T(8,128)(2,1)S(1)}, bf16[2,128,512]{2,1,0:T(8,128)(2,1)S(1)}, u32[]{:S(2)}, u32[]{:S(2)}) collective-permute-start(bf16[2,128,512]{2,1,0:T(8,128)(2,1)S(1)} %convert_element_type.137), channel_id=1, source_target_pairs={{0,16},{16,0},{4,20},{20,4},{8,24},{24,8},{12,28},{28,12},{1,17},{... | collective-permute-start | bytes 786440 | tf_op jit(solution)/shard_map/ppermute | solution.py:22
  126.3 1.4 fusion.8
  129.2 1.6 collective-permute-start.18
  133.4 7.1 %shard_map.78 = (bf16[256,512]{1,0:T(8,128)(2,1)}, bf16[256,512]{1,0:T(8,128)(2,1)}, f32[2,256,512]{2,1,0:T(8,128)}, f32[2,256,512]{2,1,0:T(8,128)}, f32[2,128,512]{2,1,0:T(8,128)}, /*index=5*/f32[2,128,512]{2,1,0:T(8,128)}) custom-call(f32[1,768]{1,0:T(1,128)} %constant.88.clone.1.bias_ref, bf16[256,2048]{1,0:T(8,128)(2,1)} %q_ref.7, ...), custom_call_target="tpu_custom_call" | custom-call | flops 1207959552 | bytes 5767168 | tf_op jit(solution)/shard_map/pallas_call | solution.py:71
  144.0 1.4 collective-permute-start.20
  149.2 3.6 %collective-permute-done.22 = bf16[2,128,512]{2,1,0:T(8,128)(2,1)S(1)} collective-permute-done((bf16[2,128,512]{2,1,0:T(8,128)(2,1)S(1)}, bf16[2,128,512]{2,1,0:T(8,128)(2,1)S(1)}, u32[]{:S(2)}, u32[]{:S(2)}) %collective-permute-start.22) | collective-permute-done | bytes 262176 | tf_op jit(solution)/shard_map/ppermute | solution.py:22
  156.6 1.5 collective-permute-start.21
  161.9 1.6 collective-permute-start.24
  168.6 2.9 %collective-permute-done.21 = bf16[2,256,512]{2,1,0:T(8,128)(2,1)S(1)} collective-permute-done((bf16[2,256,512]{2,1,0:T(8,128)(2,1)S(1)}, bf16[2,256,512]{2,1,0:T(8,128)(2,1)S(1)}, u32[]{:S(2)}, u32[]{:S(2)}) %collective-permute-start.21) | collective-permute-done | bytes 524320 | tf_op jit(solution)/shard_map/ppermute | solution.py:22
  171.9 5.7 %collective-permute-done.24 = bf16[2,256,512]{2,1,0:T(8,128)(2,1)S(1)} collective-permute-done((bf16[2,256,512]{2,1,0:T(8,128)(2,1)S(1)}, bf16[2,256,512]{2,1,0:T(8,128)(2,1)S(1)}, u32[]{:S(2)}, u32[]{:S(2)}) %collective-permute-start.24) | collective-permute-done | bytes 524320 | tf_op jit(solution)/shard_map/ppermute | solution.py:22
  (171 shorter events, 49.1 us)
Async XLA Ops:
  3.6 15.2 %collective-permute-start = (bf16[2,64,2048]{2,1,0:T(8,128)(2,1)}, bf16[2,64,2048]{2,1,0:T(8,128)(2,1)}, u32[]{:S(2)}, u32[]{:S(2)}) collective-permute-start(bf16[2,64,2048]{2,1,0:T(8,128)(2,1)} %get-tuple-element.82), channel_id=1, source_target_pairs={{0,4},{4,0},{8,12},{12,8},{16,20},{20,16},{24,28},{28,24},{1,5},{5... | collective-permute-start | bytes 1572872 | tf_op jit(solution)/shard_map/ppermute | solution.py:22
  12.7 22.3 %copy-start.19 = (bf16[2,256,512]{2,1,0:T(8,128)(2,1)}, bf16[2,256,512]{2,1,0:T(8,128)(2,1)S(1)}, u32[]{:S(2)}) copy-start(bf16[2,256,512]{2,1,0:T(8,128)(2,1)S(1)} %pad_maximum_fusion.5.refs_0_) | copy-start | bytes 1572868
  12.8 37.4 %copy-start.18 = (bf16[2,256,512]{2,1,0:T(8,128)(2,1)}, bf16[2,256,512]{2,1,0:T(8,128)(2,1)S(1)}, u32[]{:S(2)}) copy-start(bf16[2,256,512]{2,1,0:T(8,128)(2,1)S(1)} %pad_maximum_fusion.4.refs_0_) | copy-start | bytes 1572868
  13.7 17.2 %copy-start.17 = (bf16[2,256,512]{2,1,0:T(8,128)(2,1)}, bf16[2,256,512]{2,1,0:T(8,128)(2,1)S(1)}, u32[]{:S(2)}) copy-start(bf16[2,256,512]{2,1,0:T(8,128)(2,1)S(1)} %pad_maximum_fusion.7.refs_0_) | copy-start | bytes 1572868
  20.1 17.1 %collective-permute-start.2 = (bf16[2,128,512]{2,1,0:T(8,128)(2,1)S(1)}, bf16[2,128,512]{2,1,0:T(8,128)(2,1)S(1)}, u32[]{:S(2)}, u32[]{:S(2)}) collective-permute-start(bf16[2,128,512]{2,1,0:T(8,128)(2,1)S(1)} %get-tuple-element.86), channel_id=1, source_target_pairs={{0,8},{8,0},{4,12},{12,4},{16,24},{24,16},{20,28},{28,20},{1,9},{9... | collective-permute-start | bytes 786440 | tf_op jit(solution)/shard_map/ppermute | solution.py:22
  23.3 11.7 %collective-permute-start.5 = (bf16[2,128,512]{2,1,0:T(8,128)(2,1)S(1)}, bf16[2,128,512]{2,1,0:T(8,128)(2,1)S(1)}, u32[]{:S(2)}, u32[]{:S(2)}) collective-permute-start(bf16[2,128,512]{2,1,0:T(8,128)(2,1)S(1)} %get-tuple-element.84), channel_id=1, source_target_pairs={{0,8},{8,0},{4,12},{12,4},{16,24},{24,16},{20,28},{28,20},{1,9},{9... | collective-permute-start | bytes 786440 | tf_op jit(solution)/shard_map/ppermute | solution.py:22
  25.0 44.2 %collective-permute-start.9 = (bf16[2,128,512]{2,1,0:T(8,128)(2,1)S(1)}, bf16[2,128,512]{2,1,0:T(8,128)(2,1)S(1)}, u32[]{:S(2)}, u32[]{:S(2)}) collective-permute-start(bf16[2,128,512]{2,1,0:T(8,128)(2,1)S(1)} %get-tuple-element.90), channel_id=1, source_target_pairs={{0,8},{8,0},{4,12},{12,4},{16,24},{24,16},{20,28},{28,20},{1,9},{9... | collective-permute-start | bytes 786440 | tf_op jit(solution)/shard_map/ppermute | solution.py:22
  28.2 22.0 %collective-permute-start.14 = (bf16[2,128,512]{2,1,0:T(8,128)(2,1)S(1)}, bf16[2,128,512]{2,1,0:T(8,128)(2,1)S(1)}, u32[]{:S(2)}, u32[]{:S(2)}) collective-permute-start(bf16[2,128,512]{2,1,0:T(8,128)(2,1)S(1)} %get-tuple-element.88), channel_id=1, source_target_pairs={{0,8},{8,0},{4,12},{12,4},{16,24},{24,16},{20,28},{28,20},{1,9},{9... | collective-permute-start | bytes 786440 | tf_op jit(solution)/shard_map/ppermute | solution.py:22
  30.9 102.5 %collective-permute-start.13 = (bf16[2,256,512]{2,1,0:T(8,128)(2,1)S(1)}, bf16[2,256,512]{2,1,0:T(8,128)(2,1)}, u32[]{:S(2)}, u32[]{:S(2)}) collective-permute-start(bf16[2,256,512]{2,1,0:T(8,128)(2,1)S(1)} %pad_maximum_fusion.7.refs_0_), channel_id=1, source_target_pairs={{0,4},{4,0},{8,12},{12,8},{16,20},{20,16},{24,28},{28,24},{1,5},{5... | collective-permute-start | bytes 1572872 | tf_op jit(solution)/shard_map/ppermute | solution.py:22
  35.1 22.0 %collective-permute-start.4 = (bf16[2,256,512]{2,1,0:T(8,128)(2,1)S(1)}, bf16[2,256,512]{2,1,0:T(8,128)(2,1)S(1)}, u32[]{:S(2)}, u32[]{:S(2)}) collective-permute-start(bf16[2,256,512]{2,1,0:T(8,128)(2,1)S(1)} %pad_maximum_fusion.5.refs_0_), channel_id=1, source_target_pairs={{0,4},{4,0},{8,12},{12,8},{16,20},{20,16},{24,28},{28,24},{1,5},{5... | collective-permute-start | bytes 1572872 | tf_op jit(solution)/shard_map/ppermute | solution.py:22
  37.3 15.5 %copy-start.26 = (bf16[2,128,512]{2,1,0:T(8,128)(2,1)}, bf16[2,128,512]{2,1,0:T(8,128)(2,1)S(1)}, u32[]{:S(2)}) copy-start(bf16[2,128,512]{2,1,0:T(8,128)(2,1)S(1)} %collective-permute-done.2.refs_2_) | copy-start | bytes 786436
  37.3 15.4 %collective-permute-start.6 = (bf16[2,128,512]{2,1,0:T(8,128)(2,1)S(1)}, bf16[2,128,512]{2,1,0:T(8,128)(2,1)S(1)}, u32[]{:S(2)}, u32[]{:S(2)}) collective-permute-start(bf16[2,128,512]{2,1,0:T(8,128)(2,1)S(1)} %fusion.17), channel_id=1, source_target_pairs={{0,16},{16,0},{4,20},{20,4},{8,24},{24,8},{12,28},{28,12},{1,17},{... | collective-permute-start | bytes 786440 | tf_op jit(solution)/shard_map/ppermute | solution.py:22
  50.2 17.9 %copy-start.24 = (bf16[2,128,512]{2,1,0:T(8,128)(2,1)}, bf16[2,128,512]{2,1,0:T(8,128)(2,1)S(1)}, u32[]{:S(2)}) copy-start(bf16[2,128,512]{2,1,0:T(8,128)(2,1)S(1)} %collective-permute-done.14.refs_2_) | copy-start | bytes 786436
  50.2 30.4 %collective-permute-start.1 = (bf16[2,256,512]{2,1,0:T(8,128)(2,1)S(1)}, bf16[2,256,512]{2,1,0:T(8,128)(2,1)}, u32[]{:S(2)}, u32[]{:S(2)}) collective-permute-start(bf16[2,256,512]{2,1,0:T(8,128)(2,1)S(1)} %pad_maximum_fusion.4.refs_0_), channel_id=1, source_target_pairs={{0,4},{4,0},{8,12},{12,8},{16,20},{20,16},{24,28},{28,24},{1,5},{5... | collective-permute-start | bytes 1572872 | tf_op jit(solution)/shard_map/ppermute | solution.py:22
  52.7 62.9 %collective-permute-start.8 = (bf16[2,256,512]{2,1,0:T(8,128)(2,1)}, bf16[2,256,512]{2,1,0:T(8,128)(2,1)}, u32[]{:S(2)}, u32[]{:S(2)}) collective-permute-start(bf16[2,256,512]{2,1,0:T(8,128)(2,1)} %pad_maximum_fusion.6.refs_0_), channel_id=1, source_target_pairs={{0,4},{4,0},{8,12},{12,8},{16,20},{20,16},{24,28},{28,24},{1,5},{5... | collective-permute-start | bytes 1572872 | tf_op jit(solution)/shard_map/ppermute | solution.py:22
  57.9 22.7 %collective-permute-start.3 = (bf16[2,128,512]{2,1,0:T(8,128)(2,1)S(1)}, bf16[2,128,512]{2,1,0:T(8,128)(2,1)S(1)}, u32[]{:S(2)}, u32[]{:S(2)}) collective-permute-start(bf16[2,128,512]{2,1,0:T(8,128)(2,1)S(1)} %fusion.18), channel_id=1, source_target_pairs={{0,16},{16,0},{4,20},{20,4},{8,24},{24,8},{12,28},{28,12},{1,17},{... | collective-permute-start | bytes 786440 | tf_op jit(solution)/shard_map/ppermute | solution.py:22
  69.1 21.5 %copy-start.25 = (bf16[2,128,512]{2,1,0:T(8,128)(2,1)}, bf16[2,128,512]{2,1,0:T(8,128)(2,1)S(1)}, u32[]{:S(2)}) copy-start(bf16[2,128,512]{2,1,0:T(8,128)(2,1)S(1)} %collective-permute-done.9.refs_2_) | copy-start | bytes 786436
  69.2 22.7 %collective-permute-start.11 = (bf16[2,128,512]{2,1,0:T(8,128)(2,1)S(1)}, bf16[2,128,512]{2,1,0:T(8,128)(2,1)S(1)}, u32[]{:S(2)}, u32[]{:S(2)}) collective-permute-start(bf16[2,128,512]{2,1,0:T(8,128)(2,1)S(1)} %convert_element_type.126), channel_id=1, source_target_pairs={{0,16},{16,0},{4,20},{20,4},{8,24},{24,8},{12,28},{28,12},{1,17},{... | collective-permute-start | bytes 786440 | tf_op jit(solution)/shard_map/ppermute | solution.py:22
  80.6 33.8 %collective-permute-start.10 = (bf16[2,128,512]{2,1,0:T(8,128)(2,1)S(1)}, bf16[2,128,512]{2,1,0:T(8,128)(2,1)}, u32[]{:S(2)}, u32[]{:S(2)}) collective-permute-start(bf16[2,128,512]{2,1,0:T(8,128)(2,1)S(1)} %fusion.16), channel_id=1, source_target_pairs={{0,16},{16,0},{4,20},{20,4},{8,24},{24,8},{12,28},{28,12},{1,17},{... | collective-permute-start | bytes 786440 | tf_op jit(solution)/shard_map/ppermute | solution.py:22
  80.6 52.8 %collective-permute-start.15 = (bf16[2,128,512]{2,1,0:T(8,128)(2,1)}, bf16[2,128,512]{2,1,0:T(8,128)(2,1)}, u32[]{:S(2)}, u32[]{:S(2)}) collective-permute-start(bf16[2,128,512]{2,1,0:T(8,128)(2,1)} %fusion.15), channel_id=1, source_target_pairs={{0,16},{16,0},{4,20},{20,4},{8,24},{24,8},{12,28},{28,12},{1,17},{... | collective-permute-start | bytes 786440 | tf_op jit(solution)/shard_map/ppermute | solution.py:22
  91.8 21.1 %collective-permute-start.7 = (bf16[2,128,512]{2,1,0:T(8,128)(2,1)S(1)}, bf16[2,128,512]{2,1,0:T(8,128)(2,1)S(1)}, u32[]{:S(2)}, u32[]{:S(2)}) collective-permute-start(bf16[2,128,512]{2,1,0:T(8,128)(2,1)S(1)} %convert_element_type.121), channel_id=1, source_target_pairs={{0,16},{16,0},{4,20},{20,4},{8,24},{24,8},{12,28},{28,12},{1,17},{... | collective-permute-start | bytes 786440 | tf_op jit(solution)/shard_map/ppermute | solution.py:22
  92.5 21.9 %copy-start.23 = (f32[2,128,512]{2,1,0:T(8,128)S(1)}, f32[2,128,512]{2,1,0:T(8,128)}, u32[]{:S(2)}) copy-start(f32[2,128,512]{2,1,0:T(8,128)} %get-tuple-element.39) | copy-start | bytes 1572868
  112.9 13.4 %collective-permute-start.17 = (bf16[2,128,512]{2,1,0:T(8,128)(2,1)S(1)}, bf16[2,128,512]{2,1,0:T(8,128)(2,1)}, u32[]{:S(2)}, u32[]{:S(2)}) collective-permute-start(bf16[2,128,512]{2,1,0:T(8,128)(2,1)S(1)} %add_convert_fusion.10), channel_id=1, source_target_pairs={{0,8},{8,0},{4,12},{12,4},{16,24},{24,16},{20,28},{28,20},{1,9},{9... | collective-permute-start | bytes 786440 | tf_op jit(solution)/shard_map/ppermute | solution.py:22
  114.4 16.4 %collective-permute-start.12 = (bf16[2,128,512]{2,1,0:T(8,128)(2,1)S(1)}, bf16[2,128,512]{2,1,0:T(8,128)(2,1)S(1)}, u32[]{:S(2)}, u32[]{:S(2)}) collective-permute-start(bf16[2,128,512]{2,1,0:T(8,128)(2,1)S(1)} %add_convert_fusion.11), channel_id=1, source_target_pairs={{0,8},{8,0},{4,12},{12,4},{16,24},{24,16},{20,28},{28,20},{1,9},{9... | collective-permute-start | bytes 786440 | tf_op jit(solution)/shard_map/ppermute | solution.py:22
  123.9 19.5 %collective-permute-start.19 = (bf16[2,128,512]{2,1,0:T(8,128)(2,1)S(1)}, bf16[2,128,512]{2,1,0:T(8,128)(2,1)S(1)}, u32[]{:S(2)}, u32[]{:S(2)}) collective-permute-start(bf16[2,128,512]{2,1,0:T(8,128)(2,1)S(1)} %convert_element_type.137), channel_id=1, source_target_pairs={{0,16},{16,0},{4,20},{20,4},{8,24},{24,8},{12,28},{28,12},{1,17},{... | collective-permute-start | bytes 786440 | tf_op jit(solution)/shard_map/ppermute | solution.py:22
  129.2 34.2 %collective-permute-start.18 = (bf16[2,256,512]{2,1,0:T(8,128)(2,1)S(1)}, bf16[2,256,512]{2,1,0:T(8,128)(2,1)}, u32[]{:S(2)}, u32[]{:S(2)}) collective-permute-start(bf16[2,256,512]{2,1,0:T(8,128)(2,1)S(1)} %add_convert_fusion.5), channel_id=1, source_target_pairs={{0,4},{4,0},{8,12},{12,8},{16,20},{20,16},{24,28},{28,24},{1,5},{5... | collective-permute-start | bytes 1572872 | tf_op jit(solution)/shard_map/ppermute | solution.py:22
  132.8 32.1 %collective-permute-start.16 = (bf16[2,256,512]{2,1,0:T(8,128)(2,1)S(1)}, bf16[2,256,512]{2,1,0:T(8,128)(2,1)}, u32[]{:S(2)}, u32[]{:S(2)}) collective-permute-start(bf16[2,256,512]{2,1,0:T(8,128)(2,1)S(1)} %add_convert_fusion.7), channel_id=1, source_target_pairs={{0,4},{4,0},{8,12},{12,8},{16,20},{20,16},{24,28},{28,24},{1,5},{5... | collective-permute-start | bytes 1572872 | tf_op jit(solution)/shard_map/ppermute | solution.py:22
  141.6 11.2 %collective-permute-start.22 = (bf16[2,128,512]{2,1,0:T(8,128)(2,1)S(1)}, bf16[2,128,512]{2,1,0:T(8,128)(2,1)S(1)}, u32[]{:S(2)}, u32[]{:S(2)}) collective-permute-start(bf16[2,128,512]{2,1,0:T(8,128)(2,1)S(1)} %convert_element_type.142), channel_id=1, source_target_pairs={{0,16},{16,0},{4,20},{20,4},{8,24},{24,8},{12,28},{28,12},{1,17},{... | collective-permute-start | bytes 786440 | tf_op jit(solution)/shard_map/ppermute | solution.py:22
  144.0 10.6 %collective-permute-start.20 = (bf16[2,128,512]{2,1,0:T(8,128)(2,1)S(1)}, bf16[2,128,512]{2,1,0:T(8,128)(2,1)S(1)}, u32[]{:S(2)}, u32[]{:S(2)}) collective-permute-start(bf16[2,128,512]{2,1,0:T(8,128)(2,1)S(1)} %add_convert_fusion.9), channel_id=1, source_target_pairs={{0,8},{8,0},{4,12},{12,4},{16,24},{24,16},{20,28},{28,20},{1,9},{9... | collective-permute-start | bytes 786440 | tf_op jit(solution)/shard_map/ppermute | solution.py:22
  153.4 6.4 %collective-permute-start.23 = (bf16[2,128,512]{2,1,0:T(8,128)(2,1)S(1)}, bf16[2,128,512]{2,1,0:T(8,128)(2,1)S(1)}, u32[]{:S(2)}, u32[]{:S(2)}) collective-permute-start(bf16[2,128,512]{2,1,0:T(8,128)(2,1)S(1)} %add_convert_fusion.8), channel_id=1, source_target_pairs={{0,8},{8,0},{4,12},{12,4},{16,24},{24,16},{20,28},{28,20},{1,9},{9... | collective-permute-start | bytes 786440 | tf_op jit(solution)/shard_map/ppermute | solution.py:22
  156.6 14.9 %collective-permute-start.21 = (bf16[2,256,512]{2,1,0:T(8,128)(2,1)S(1)}, bf16[2,256,512]{2,1,0:T(8,128)(2,1)S(1)}, u32[]{:S(2)}, u32[]{:S(2)}) collective-permute-start(bf16[2,256,512]{2,1,0:T(8,128)(2,1)S(1)} %add_convert_fusion.3), channel_id=1, source_target_pairs={{0,4},{4,0},{8,12},{12,8},{16,20},{20,16},{24,28},{28,24},{1,5},{5... | collective-permute-start | bytes 1572872 | tf_op jit(solution)/shard_map/ppermute | solution.py:22
  161.9 15.7 %collective-permute-start.24 = (bf16[2,256,512]{2,1,0:T(8,128)(2,1)S(1)}, bf16[2,256,512]{2,1,0:T(8,128)(2,1)S(1)}, u32[]{:S(2)}, u32[]{:S(2)}) collective-permute-start(bf16[2,256,512]{2,1,0:T(8,128)(2,1)S(1)} %add_convert_fusion.1), channel_id=1, source_target_pairs={{0,4},{4,0},{8,12},{12,8},{16,20},{20,16},{24,28},{28,24},{1,5},{5... | collective-permute-start | bytes 1572872 | tf_op jit(solution)/shard_map/ppermute | solution.py:22
  (32 other events, 92.3 us)

commit v8 on v7

--- a/solution.py
+++ b/solution.py
@@ -87,6 +87,15 @@
     return lax.optimization_barrier((value, earlier))[0]
 
 
+def inner_pairs(count, level):
+    mask = (1 << level) | (1 << (level - 1))
+    return [(b, b ^ mask) for b in range(count) if (b >> level & 1) != (b >> (level - 1) & 1)]
+
+
+def outer_pairs(count, level):
+    return [(b, b ^ (1 << (level - 1))) for b in range(count) if (b >> level & 1) != (b >> (level - 1) & 1)]
+
+
 def placed_pool(rows_in, upper):
     run = rows_in // (POOLED // 2)
     out_row = lax.broadcasted_iota(jnp.int32, (POOLED, rows_in), 0)
@@ -115,6 +124,7 @@
         bias_parts.append(jnp.full((POOLED,), math.log(pool_ratio * 2**step_level), jnp.float32))
     key_bias = jnp.concatenate(bias_parts, axis=0)
     bits = [position // 2**step_level % 2 for step_level in range(levels)]
+    inner = [None] + [bits[s] != bits[s - 1] for s in range(1, levels)]
     mine = [placed_pool(leaf_rows if s == 0 else POOLED, bits[s]) for s in range(levels)]
     other = [placed_pool(leaf_rows if s == 0 else POOLED, 1 - bits[s]) for s in range(levels)]
     pool_own = placed_pool(leaf_rows, 0)[: POOLED // 2]
@@ -136,7 +146,12 @@
         )
         far = []
         for step_level in range(1, levels):
-            partner = partner_2(summary.astype(jnp.bfloat16), "seq", step_level)
+            if step_level == 1:
+                partner = partner_2(summary.astype(jnp.bfloat16), "seq", step_level)
+            else:
+                crossed = lax.ppermute(summary.astype(jnp.bfloat16), "seq", inner_pairs(seq_count, step_level))
+                passed = lax.ppermute(crossed, "seq", outer_pairs(seq_count, step_level))
+                partner = jnp.where(inner[step_level], crossed, passed)
             far.append(partner)
             if step_level + 1 < levels:
                 summary = apply(mine[step_level], summary) + apply(other[step_level], partner)
@@ -157,7 +172,13 @@
             if grad is not None:
                 outgoing = outgoing + apply(other[step_level].T, grad)
             sends[step_level] = outgoing.astype(jnp.bfloat16)
-            returned = partner_2(sends[step_level], "seq", step_level)
+            if step_level == 1:
+                returned = partner_2(sends[step_level], "seq", step_level)
+            else:
+                back = [(t, s) for s, t in outer_pairs(seq_count, step_level)]
+                gathered = lax.ppermute(sends[step_level], "seq", back)
+                total = outgoing + gathered.astype(jnp.float32)
+                returned = lax.ppermute(total.astype(jnp.bfloat16), "seq", inner_pairs(seq_count, step_level))
             if grad is None:
                 grad = returned.astype(jnp.float32)
             else:

time: 181 us -> 175 us (0.967)
  waiting for transfers between devices: 64.9 us -> 31.1 us
  starting transfers between devices: 33.6 us -> 57.6 us
  other arithmetic: 15.7 us -> 20.9 us
  local copies, waits for them, and re-layouts: 5.1 us -> 3.27 us
    ppermute x25 -> x17, waiting for transfers between devices: 64.9 us -> 22.7 us  [partner_2(): return lax.ppermute(block, axis, route)]
    ppermute x0 -> x16, starting transfers between devices: none -> 23 us  [the longest x4 12.1 us: body(): gathered = lax.ppermute(sends[step_level], 'seq', back)]
    ppermute x0 -> x16, waiting for transfers between devices: none -> 8.38 us  [the longest x4 5.37 us: body(): passed = lax.ppermute(crossed, 'seq', outer_pairs(seq_count, step_level))]
    select_n x0 -> x4, other arithmetic: none -> 3.03 us  [body(): partner = jnp.where(inner[step_level], crossed, passed)]
    unnamed x78 -> x84, local copies, waits for them, and re-layouts: 3.71 us -> 1.88 us
    ppermute x25 -> x17, starting transfers between devices: 33.6 us -> 34.6 us  [partner_2(): return lax.ppermute(block, axis, route)]
  transfers between devices with their start and end apart: 25 -> 33, of which waited for: 11 -> 10; matrix products, arithmetic and copies ran while one was open for 23% -> 26% of each run, Pallas kernels for 16% -> 16%
where the time goes in v8:
time: 175 us; the launch traced here: 174 us
  starting transfers between devices  57.6 us (33%)
  waiting for transfers between devices  31.1 us (18%)
  matrix products  30.4 us (17%)
  Pallas kernels  28.6 us (16%)
  other arithmetic  20.9 us (12%)
  local copies, waits for them, and re-layouts  3.27 us (2%)
    ppermute x17, starting transfers between devices, partner_2(): return lax.ppermute(block, axis, route)  34.6 us
    pallas_call x4, Pallas kernels, attention(): pl.pallas_call(functools.partial(attention_kernel, scale=score_scale, par...  28.6 us
    dot_general x32, matrix products, apply(): jnp.einsum('pr,krw->kpw', matrix, rows.astype(jnp.float32), precision=lax...  27.5 us
    ppermute x17, waiting for transfers between devices, partner_2(): return lax.ppermute(block, axis, route)  22.7 us
    ppermute x4, starting transfers between devices, body(): gathered = lax.ppermute(sends[step_level], 'seq', back)  12.1 us
    ppermute x4, waiting for transfers between devices, body(): passed = lax.ppermute(crossed, 'seq', outer_pairs(seq_count, step_level))  5.37 us
    ppermute x4, starting transfers between devices, body(): passed = lax.ppermute(crossed, 'seq', outer_pairs(seq_count, step_level))  5.15 us
    convert_element_type x8, other arithmetic, body(): sends[step_level] = outgoing.astype(jnp.bfloat16)  4.82 us
  transfers between devices with their start and end apart: 33, of which 10 were waited for; matrix products, arithmetic and copies ran while one was open for 26% of the time, Pallas kernels for 16%

profile of v8, /device:TPU:0, one launch (start us, length us, event | category | flops | bytes accessed | tf_op | source)
XLA Modules:
  0.0 173.5 jit_solution(1286101539661886992)
XLA Ops:
  0.7 2.9 %fusion.340 = (bf16[2,64,2048]{2,1,0:T(8,128)(2,1)}, f32[2,64,2048]{2,1,0:T(8,128)S(1)}) fusion(bf16[1,256,2048]{2,1,0:T(8,128)(2,1)} %bitcast.199, bf16[1,256,2048]{2,1,0:T(8,128)(2,1)} %bitcast.200, s32[128,256]{1,0:T(8,128)S(1)} %broadcast_select_fusion.4), kind=kOutput, calls=%fused_computation.431 | convolution fusion | flops 138739712 | bytes 3735552 | tf_op jit(solution)/shard_map/pr,krw->kpw/dot_general | solution.py:131
  3.6 3.0 %collective-permute-start = (bf16[2,64,2048]{2,1,0:T(8,128)(2,1)}, bf16[2,64,2048]{2,1,0:T(8,128)(2,1)}, u32[]{:S(2)}, u32[]{:S(2)}) collective-permute-start(bf16[2,64,2048]{2,1,0:T(8,128)(2,1)} %get-tuple-element.82), channel_id=1, source_target_pairs={{0,4},{4,0},{8,12},{12,8},{16,20},{20,16},{24,28},{28,24},{1,5},{5... | collective-permute-start | bytes 1572872 | tf_op jit(solution)/shard_map/ppermute | solution.py:22
  6.6 1.4 fusion.21
  8.0 1.4 fusion.23
  10.7 2.0 %pad_maximum_fusion.6.refs_0_ = bf16[2,256,512]{2,1,0:T(8,128)(2,1)} fusion(bf16[1,256,512]{2,1,0:T(8,128)(2,1)} %get-tuple-element.70, bf16[1,256,512]{2,1,0:T(8,128)(2,1)} %get-tuple-element.95), kind=kLoop, calls=%fused_computation.58 | loop fusion | flops 262144 | bytes 1048576 | tf_op jit(solution)/shard_map/stack | solution.py:142
  15.1 3.7 %collective-permute-done = bf16[2,64,2048]{2,1,0:T(8,128)(2,1)} collective-permute-done((bf16[2,64,2048]{2,1,0:T(8,128)(2,1)}, bf16[2,64,2048]{2,1,0:T(8,128)(2,1)}, u32[]{:S(2)}, u32[]{:S(2)}) %collective-permute-start) | collective-permute-done | bytes 524320 | tf_op jit(solution)/shard_map/ppermute | solution.py:22
  20.1 1.9 %collective-permute-start.2 = (bf16[2,128,512]{2,1,0:T(8,128)(2,1)S(1)}, bf16[2,128,512]{2,1,0:T(8,128)(2,1)S(1)}, u32[]{:S(2)}, u32[]{:S(2)}) collective-permute-start(bf16[2,128,512]{2,1,0:T(8,128)(2,1)S(1)} %get-tuple-element.86), channel_id=1, source_target_pairs={{0,8},{8,0},{4,12},{12,4},{16,24},{24,16},{20,28},{28,20},{1,9},{9... | collective-permute-start | bytes 786440 | tf_op jit(solution)/shard_map/ppermute | solution.py:22
  25.0 1.9 %collective-permute-start.12 = (bf16[2,128,512]{2,1,0:T(8,128)(2,1)S(1)}, bf16[2,128,512]{2,1,0:T(8,128)(2,1)S(1)}, u32[]{:S(2)}, u32[]{:S(2)}) collective-permute-start(bf16[2,128,512]{2,1,0:T(8,128)(2,1)S(1)} %get-tuple-element.90), channel_id=1, source_target_pairs={{0,8},{8,0},{4,12},{12,4},{16,24},{24,16},{20,28},{28,20},{1,9},{9... | collective-permute-start | bytes 786440 | tf_op jit(solution)/shard_map/ppermute | solution.py:22
  30.3 4.8 %collective-permute-done.6.refs_2_ = bf16[2,128,512]{2,1,0:T(8,128)(2,1)S(1)} collective-permute-done((bf16[2,128,512]{2,1,0:T(8,128)(2,1)S(1)}, bf16[2,128,512]{2,1,0:T(8,128)(2,1)S(1)}, u32[]{:S(2)}, u32[]{:S(2)}) %collective-permute-start.6) | collective-permute-done | bytes 262176 | tf_op jit(solution)/shard_map/ppermute | solution.py:22
  36.8 1.8 %collective-permute-start.1 = (bf16[2,256,512]{2,1,0:T(8,128)(2,1)S(1)}, bf16[2,256,512]{2,1,0:T(8,128)(2,1)}, u32[]{:S(2)}, u32[]{:S(2)}) collective-permute-start(bf16[2,256,512]{2,1,0:T(8,128)(2,1)S(1)} %pad_maximum_fusion.4.refs_0_), channel_id=1, source_target_pairs={{0,4},{4,0},{8,12},{12,8},{16,20},{20,16},{24,28},{28,24},{1,5},{5... | collective-permute-start | bytes 1572872 | tf_op jit(solution)/shard_map/ppermute | solution.py:22
  43.8 1.4 collective-permute-done.19.refs_2_
  47.7 5.4 %collective-permute-done.8 = bf16[2,128,512]{2,1,0:T(8,128)(2,1)S(1)} collective-permute-done((bf16[2,128,512]{2,1,0:T(8,128)(2,1)S(1)}, bf16[2,128,512]{2,1,0:T(8,128)(2,1)S(1)}, u32[]{:S(2)}, u32[]{:S(2)}) %collective-permute-start.8) | collective-permute-done | bytes 262176 | tf_op jit(solution)/shard_map/ppermute | solution.py:153
  55.2 4.2 %collective-permute-done.5.refs_1_ = bf16[2,256,512]{2,1,0:T(8,128)(2,1)S(1)} collective-permute-done((bf16[2,256,512]{2,1,0:T(8,128)(2,1)S(1)}, bf16[2,256,512]{2,1,0:T(8,128)(2,1)S(1)}, u32[]{:S(2)}, u32[]{:S(2)}) %collective-permute-start.5) | collective-permute-done | bytes 524320 | tf_op jit(solution)/shard_map/ppermute | solution.py:22
  60.2 1.7 %collective-permute-start.18 = (bf16[2,256,512]{2,1,0:T(8,128)(2,1)S(1)}, bf16[2,256,512]{2,1,0:T(8,128)(2,1)}, u32[]{:S(2)}, u32[]{:S(2)}) collective-permute-start(bf16[2,256,512]{2,1,0:T(8,128)(2,1)S(1)} %pad_maximum_fusion.7.refs_0_), channel_id=1, source_target_pairs={{0,4},{4,0},{8,12},{12,8},{16,20},{20,16},{24,28},{28,24},{1,5},{5... | collective-permute-start | bytes 1572872 | tf_op jit(solution)/shard_map/ppermute | solution.py:22
  62.0 7.2 %shard_map.76 = (bf16[256,512]{1,0:T(8,128)(2,1)}, bf16[256,512]{1,0:T(8,128)(2,1)}, f32[2,256,512]{2,1,0:T(8,128)}, f32[2,256,512]{2,1,0:T(8,128)}, f32[2,128,512]{2,1,0:T(8,128)}, /*index=5*/f32[2,128,512]{2,1,0:T(8,128)}) custom-call(f32[1,768]{1,0:T(1,128)} %constant.99.clone.1.bias_ref, bf16[256,2048]{1,0:T(8,128)(2,1)} %q_ref.7, ...), custom_call_target="tpu_custom_call" | custom-call | flops 1207959552 | bytes 5767168 | tf_op jit(solution)/shard_map/pallas_call | solution.py:71
  73.9 6.5 %collective-permute-start.15 = (bf16[2,128,512]{2,1,0:T(8,128)(2,1)S(1)}, bf16[2,128,512]{2,1,0:T(8,128)(2,1)S(1)}, u32[]{:S(2)}, u32[]{:S(2)}) collective-permute-start(bf16[2,128,512]{2,1,0:T(8,128)(2,1)S(1)} %convert_element_type.152), channel_id=1, source_target_pairs={{0,8},{4,12},{24,16},{28,20},{1,9},{5,13},{25,17},{29,21},{2,10},{... | collective-permute-start | bytes 786440 | tf_op jit(solution)/shard_map/ppermute | solution.py:179
  80.4 7.1 %shard_map.75 = (bf16[256,512]{1,0:T(8,128)(2,1)}, bf16[256,512]{1,0:T(8,128)(2,1)}, f32[2,256,512]{2,1,0:T(8,128)}, f32[2,256,512]{2,1,0:T(8,128)}, f32[2,128,512]{2,1,0:T(8,128)}, /*index=5*/f32[2,128,512]{2,1,0:T(8,128)}) custom-call(f32[1,768]{1,0:T(1,128)} %constant.99.clone.1.bias_ref, bf16[256,2048]{1,0:T(8,128)(2,1)} %q_ref.7, ...), custom_call_target="tpu_custom_call" | custom-call | flops 1207959552 | bytes 5767168 | tf_op jit(solution)/shard_map/pallas_call | solution.py:71
  88.7 1.5 collective-permute-start.9
  92.6 2.2 %collective-permute-done.9 = bf16[2,128,512]{2,1,0:T(8,128)(2,1)S(1)} collective-permute-done((bf16[2,128,512]{2,1,0:T(8,128)(2,1)S(1)}, bf16[2,128,512]{2,1,0:T(8,128)(2,1)S(1)}, u32[]{:S(2)}, u32[]{:S(2)}) %collective-permute-start.9) | collective-permute-done | bytes 262176 | tf_op jit(solution)/shard_map/ppermute | solution.py:179
  96.2 4.6 %collective-permute-start.23 = (bf16[2,128,512]{2,1,0:T(8,128)(2,1)S(1)}, bf16[2,128,512]{2,1,0:T(8,128)(2,1)S(1)}, u32[]{:S(2)}, u32[]{:S(2)}) collective-permute-start(bf16[2,128,512]{2,1,0:T(8,128)(2,1)S(1)} %add_convert_fusion.12), channel_id=1, source_target_pairs={{0,8},{8,0},{4,12},{12,4},{16,24},{24,16},{20,28},{28,20},{1,9},{9... | collective-permute-start | bytes 786440 | tf_op jit(solution)/shard_map/ppermute | solution.py:22
  101.4 4.9 %collective-permute-start.17 = (bf16[2,128,512]{2,1,0:T(8,128)(2,1)S(1)}, bf16[2,128,512]{2,1,0:T(8,128)(2,1)S(1)}, u32[]{:S(2)}, u32[]{:S(2)}) collective-permute-start(bf16[2,128,512]{2,1,0:T(8,128)(2,1)S(1)} %add_convert_fusion.14), channel_id=1, source_target_pairs={{0,8},{8,0},{4,12},{12,4},{16,24},{24,16},{20,28},{28,20},{1,9},{9... | collective-permute-start | bytes 786440 | tf_op jit(solution)/shard_map/ppermute | solution.py:22
  106.3 7.2 %shard_map.77 = (bf16[256,512]{1,0:T(8,128)(2,1)}, bf16[256,512]{1,0:T(8,128)(2,1)}, f32[2,256,512]{2,1,0:T(8,128)}, f32[2,256,512]{2,1,0:T(8,128)}, f32[2,128,512]{2,1,0:T(8,128)}, /*index=5*/f32[2,128,512]{2,1,0:T(8,128)}) custom-call(f32[1,768]{1,0:T(1,128)} %constant.99.clone.1.bias_ref, bf16[256,2048]{1,0:T(8,128)(2,1)} %q_ref.7, ...), custom_call_target="tpu_custom_call" | custom-call | flops 1207959552 | bytes 5767168 | tf_op jit(solution)/shard_map/pallas_call | solution.py:71
  114.5 2.7 %collective-permute-start.25 = (bf16[2,128,512]{2,1,0:T(8,128)(2,1)S(1)}, bf16[2,128,512]{2,1,0:T(8,128)(2,1)}, u32[]{:S(2)}, u32[]{:S(2)}) collective-permute-start(bf16[2,128,512]{2,1,0:T(8,128)(2,1)S(1)} %convert_element_type.165), channel_id=1, source_target_pairs={{0,8},{4,12},{24,16},{28,20},{1,9},{5,13},{25,17},{29,21},{2,10},{... | collective-permute-start | bytes 786440 | tf_op jit(solution)/shard_map/ppermute | solution.py:179
  119.2 1.6 collective-permute-start.24
  124.4 7.2 %shard_map.78 = (bf16[256,512]{1,0:T(8,128)(2,1)}, bf16[256,512]{1,0:T(8,128)(2,1)}, f32[2,256,512]{2,1,0:T(8,128)}, f32[2,256,512]{2,1,0:T(8,128)}, f32[2,128,512]{2,1,0:T(8,128)}, /*index=5*/f32[2,128,512]{2,1,0:T(8,128)}) custom-call(f32[1,768]{1,0:T(1,128)} %constant.99.clone.1.bias_ref, bf16[256,2048]{1,0:T(8,128)(2,1)} %q_ref.7, ...), custom_call_target="tpu_custom_call" | custom-call | flops 1207959552 | bytes 5767168 | tf_op jit(solution)/shard_map/pallas_call | solution.py:71
  132.8 1.4 collective-permute-start.29
  142.2 4.5 %collective-permute-start.27 = (bf16[2,128,512]{2,1,0:T(8,128)(2,1)S(1)}, bf16[2,128,512]{2,1,0:T(8,128)(2,1)S(1)}, u32[]{:S(2)}, u32[]{:S(2)}) collective-permute-start(bf16[2,128,512]{2,1,0:T(8,128)(2,1)S(1)} %add_convert_fusion.10), channel_id=1, source_target_pairs={{0,8},{8,0},{4,12},{12,4},{16,24},{24,16},{20,28},{28,20},{1,9},{9... | collective-permute-start | bytes 786440 | tf_op jit(solution)/shard_map/ppermute | solution.py:22
  147.3 4.7 %collective-permute-start.31 = (bf16[2,128,512]{2,1,0:T(8,128)(2,1)S(1)}, bf16[2,128,512]{2,1,0:T(8,128)(2,1)S(1)}, u32[]{:S(2)}, u32[]{:S(2)}) collective-permute-start(bf16[2,128,512]{2,1,0:T(8,128)(2,1)S(1)} %add_convert_fusion.8), channel_id=1, source_target_pairs={{0,8},{8,0},{4,12},{12,4},{16,24},{24,16},{20,28},{28,20},{1,9},{9... | collective-permute-start | bytes 786440 | tf_op jit(solution)/shard_map/ppermute | solution.py:22
  154.1 1.6 collective-permute-start.28
  156.8 1.4 add_convert_fusion.4
  158.2 1.4 add_convert_fusion.6
  164.6 6.3 %collective-permute-done.32 = bf16[2,256,512]{2,1,0:T(8,128)(2,1)S(1)} collective-permute-done((bf16[2,256,512]{2,1,0:T(8,128)(2,1)S(1)}, bf16[2,256,512]{2,1,0:T(8,128)(2,1)S(1)}, u32[]{:S(2)}, u32[]{:S(2)}) %collective-permute-start.32) | collective-permute-done | bytes 524320 | tf_op jit(solution)/shard_map/ppermute | solution.py:22
  (201 shorter events, 60.4 us)
Async XLA Ops:
  3.6 15.2 %collective-permute-start = (bf16[2,64,2048]{2,1,0:T(8,128)(2,1)}, bf16[2,64,2048]{2,1,0:T(8,128)(2,1)}, u32[]{:S(2)}, u32[]{:S(2)}) collective-permute-start(bf16[2,64,2048]{2,1,0:T(8,128)(2,1)} %get-tuple-element.82), channel_id=1, source_target_pairs={{0,4},{4,0},{8,12},{12,8},{16,20},{20,16},{24,28},{28,24},{1,5},{5... | collective-permute-start | bytes 1572872 | tf_op jit(solution)/shard_map/ppermute | solution.py:22
  20.1 18.5 %collective-permute-start.2 = (bf16[2,128,512]{2,1,0:T(8,128)(2,1)S(1)}, bf16[2,128,512]{2,1,0:T(8,128)(2,1)S(1)}, u32[]{:S(2)}, u32[]{:S(2)}) collective-permute-start(bf16[2,128,512]{2,1,0:T(8,128)(2,1)S(1)} %get-tuple-element.86), channel_id=1, source_target_pairs={{0,8},{8,0},{4,12},{12,4},{16,24},{24,16},{20,28},{28,20},{1,9},{9... | collective-permute-start | bytes 786440 | tf_op jit(solution)/shard_map/ppermute | solution.py:22
  23.3 11.7 %collective-permute-start.6 = (bf16[2,128,512]{2,1,0:T(8,128)(2,1)S(1)}, bf16[2,128,512]{2,1,0:T(8,128)(2,1)S(1)}, u32[]{:S(2)}, u32[]{:S(2)}) collective-permute-start(bf16[2,128,512]{2,1,0:T(8,128)(2,1)S(1)} %get-tuple-element.84), channel_id=1, source_target_pairs={{0,8},{8,0},{4,12},{12,4},{16,24},{24,16},{20,28},{28,20},{1,9},{9... | collective-permute-start | bytes 786440 | tf_op jit(solution)/shard_map/ppermute | solution.py:22
  25.0 15.7 %collective-permute-start.12 = (bf16[2,128,512]{2,1,0:T(8,128)(2,1)S(1)}, bf16[2,128,512]{2,1,0:T(8,128)(2,1)S(1)}, u32[]{:S(2)}, u32[]{:S(2)}) collective-permute-start(bf16[2,128,512]{2,1,0:T(8,128)(2,1)S(1)} %get-tuple-element.90), channel_id=1, source_target_pairs={{0,8},{8,0},{4,12},{12,4},{16,24},{24,16},{20,28},{28,20},{1,9},{9... | collective-permute-start | bytes 786440 | tf_op jit(solution)/shard_map/ppermute | solution.py:22
  28.2 17.1 %collective-permute-start.19 = (bf16[2,128,512]{2,1,0:T(8,128)(2,1)S(1)}, bf16[2,128,512]{2,1,0:T(8,128)(2,1)S(1)}, u32[]{:S(2)}, u32[]{:S(2)}) collective-permute-start(bf16[2,128,512]{2,1,0:T(8,128)(2,1)S(1)} %get-tuple-element.88), channel_id=1, source_target_pairs={{0,8},{8,0},{4,12},{12,4},{16,24},{24,16},{20,28},{28,20},{1,9},{9... | collective-permute-start | bytes 786440 | tf_op jit(solution)/shard_map/ppermute | solution.py:22
  35.5 5.9 %collective-permute-start.7 = (bf16[2,128,512]{2,1,0:T(8,128)(2,1)S(1)}, bf16[2,128,512]{2,1,0:T(8,128)(2,1)S(1)}, u32[]{:S(2)}, u32[]{:S(2)}) collective-permute-start(bf16[2,128,512]{2,1,0:T(8,128)(2,1)S(1)} %fusion.17), channel_id=1, source_target_pairs={{8,16},{12,20},{16,8},{20,12},{9,17},{13,21},{17,9},{21,13},{10,18... | collective-permute-start | bytes 786440 | tf_op jit(solution)/shard_map/ppermute | solution.py:152
  36.8 37.1 %collective-permute-start.1 = (bf16[2,256,512]{2,1,0:T(8,128)(2,1)S(1)}, bf16[2,256,512]{2,1,0:T(8,128)(2,1)}, u32[]{:S(2)}, u32[]{:S(2)}) collective-permute-start(bf16[2,256,512]{2,1,0:T(8,128)(2,1)S(1)} %pad_maximum_fusion.4.refs_0_), channel_id=1, source_target_pairs={{0,4},{4,0},{8,12},{12,8},{16,20},{20,16},{24,28},{28,24},{1,5},{5... | collective-permute-start | bytes 1572872 | tf_op jit(solution)/shard_map/ppermute | solution.py:22
  38.6 20.8 %collective-permute-start.5 = (bf16[2,256,512]{2,1,0:T(8,128)(2,1)S(1)}, bf16[2,256,512]{2,1,0:T(8,128)(2,1)S(1)}, u32[]{:S(2)}, u32[]{:S(2)}) collective-permute-start(bf16[2,256,512]{2,1,0:T(8,128)(2,1)S(1)} %copy-done.24), channel_id=1, source_target_pairs={{0,4},{4,0},{8,12},{12,8},{16,20},{20,16},{24,28},{28,24},{1,5},{5... | collective-permute-start | bytes 1572872 | tf_op jit(solution)/shard_map/ppermute | solution.py:22
  40.7 6.4 %collective-permute-start.3 = (bf16[2,128,512]{2,1,0:T(8,128)(2,1)S(1)}, bf16[2,128,512]{2,1,0:T(8,128)(2,1)S(1)}, u32[]{:S(2)}, u32[]{:S(2)}) collective-permute-start(bf16[2,128,512]{2,1,0:T(8,128)(2,1)S(1)} %fusion.18), channel_id=1, source_target_pairs={{8,16},{12,20},{16,8},{20,12},{9,17},{13,21},{17,9},{21,13},{10,18... | collective-permute-start | bytes 786440 | tf_op jit(solution)/shard_map/ppermute | solution.py:152
  41.4 11.7 %collective-permute-start.8 = (bf16[2,128,512]{2,1,0:T(8,128)(2,1)S(1)}, bf16[2,128,512]{2,1,0:T(8,128)(2,1)S(1)}, u32[]{:S(2)}, u32[]{:S(2)}) collective-permute-start(bf16[2,128,512]{2,1,0:T(8,128)(2,1)S(1)} %collective-permute-done.7), channel_id=1, source_target_pairs={{8,0},{12,4},{16,24},{20,28},{9,1},{13,5},{17,25},{21,29},{10,2},{... | collective-permute-start | bytes 786440 | tf_op jit(solution)/shard_map/ppermute | solution.py:153
  45.3 24.9 %collective-permute-start.13 = (bf16[2,128,512]{2,1,0:T(8,128)(2,1)}, bf16[2,128,512]{2,1,0:T(8,128)(2,1)S(1)}, u32[]{:S(2)}, u32[]{:S(2)}) collective-permute-start(bf16[2,128,512]{2,1,0:T(8,128)(2,1)} %fusion.16), channel_id=1, source_target_pairs={{8,16},{12,20},{16,8},{20,12},{9,17},{13,21},{17,9},{21,13},{10,18... | collective-permute-start | bytes 786440 | tf_op jit(solution)/shard_map/ppermute | solution.py:152
  47.1 23.5 %collective-permute-start.20 = (bf16[2,128,512]{2,1,0:T(8,128)(2,1)}, bf16[2,128,512]{2,1,0:T(8,128)(2,1)S(1)}, u32[]{:S(2)}, u32[]{:S(2)}) collective-permute-start(bf16[2,128,512]{2,1,0:T(8,128)(2,1)} %fusion.15), channel_id=1, source_target_pairs={{8,16},{12,20},{16,8},{20,12},{9,17},{13,21},{17,9},{21,13},{10,18... | collective-permute-start | bytes 786440 | tf_op jit(solution)/shard_map/ppermute | solution.py:152
  53.1 18.7 %collective-permute-start.4 = (bf16[2,128,512]{2,1,0:T(8,128)(2,1)S(1)}, bf16[2,128,512]{2,1,0:T(8,128)(2,1)S(1)}, u32[]{:S(2)}, u32[]{:S(2)}) collective-permute-start(bf16[2,128,512]{2,1,0:T(8,128)(2,1)S(1)} %collective-permute-done.3), channel_id=1, source_target_pairs={{8,0},{12,4},{16,24},{20,28},{9,1},{13,5},{17,25},{21,29},{10,2},{... | collective-permute-start | bytes 786440 | tf_op jit(solution)/shard_map/ppermute | solution.py:153
  60.2 64.2 %collective-permute-start.18 = (bf16[2,256,512]{2,1,0:T(8,128)(2,1)S(1)}, bf16[2,256,512]{2,1,0:T(8,128)(2,1)}, u32[]{:S(2)}, u32[]{:S(2)}) collective-permute-start(bf16[2,256,512]{2,1,0:T(8,128)(2,1)S(1)} %pad_maximum_fusion.7.refs_0_), channel_id=1, source_target_pairs={{0,4},{4,0},{8,12},{12,8},{16,20},{20,16},{24,28},{28,24},{1,5},{5... | collective-permute-start | bytes 1572872 | tf_op jit(solution)/shard_map/ppermute | solution.py:22
  70.2 36.1 %collective-permute-start.11 = (bf16[2,256,512]{2,1,0:T(8,128)(2,1)S(1)}, bf16[2,256,512]{2,1,0:T(8,128)(2,1)}, u32[]{:S(2)}, u32[]{:S(2)}) collective-permute-start(bf16[2,256,512]{2,1,0:T(8,128)(2,1)S(1)} %copy-done.22), channel_id=1, source_target_pairs={{0,4},{4,0},{8,12},{12,8},{16,20},{20,16},{24,28},{28,24},{1,5},{5... | collective-permute-start | bytes 1572872 | tf_op jit(solution)/shard_map/ppermute | solution.py:22
  70.6 18.1 %collective-permute-start.14 = (bf16[2,128,512]{2,1,0:T(8,128)(2,1)S(1)}, bf16[2,128,512]{2,1,0:T(8,128)(2,1)S(1)}, u32[]{:S(2)}, u32[]{:S(2)}) collective-permute-start(bf16[2,128,512]{2,1,0:T(8,128)(2,1)S(1)} %collective-permute-done.13), channel_id=1, source_target_pairs={{8,0},{12,4},{16,24},{20,28},{9,1},{13,5},{17,25},{21,29},{10,2},{... | collective-permute-start | bytes 786440 | tf_op jit(solution)/shard_map/ppermute | solution.py:153
  71.9 20.0 %collective-permute-start.21 = (bf16[2,128,512]{2,1,0:T(8,128)(2,1)S(1)}, bf16[2,128,512]{2,1,0:T(8,128)(2,1)S(1)}, u32[]{:S(2)}, u32[]{:S(2)}) collective-permute-start(bf16[2,128,512]{2,1,0:T(8,128)(2,1)S(1)} %collective-permute-done.20), channel_id=1, source_target_pairs={{8,0},{12,4},{16,24},{20,28},{9,1},{13,5},{17,25},{21,29},{10,2},{... | collective-permute-start | bytes 786440 | tf_op jit(solution)/shard_map/ppermute | solution.py:153
  73.9 17.1 %collective-permute-start.15 = (bf16[2,128,512]{2,1,0:T(8,128)(2,1)S(1)}, bf16[2,128,512]{2,1,0:T(8,128)(2,1)S(1)}, u32[]{:S(2)}, u32[]{:S(2)}) collective-permute-start(bf16[2,128,512]{2,1,0:T(8,128)(2,1)S(1)} %convert_element_type.152), channel_id=1, source_target_pairs={{0,8},{4,12},{24,16},{28,20},{1,9},{5,13},{25,17},{29,21},{2,10},{... | collective-permute-start | bytes 786440 | tf_op jit(solution)/shard_map/ppermute | solution.py:179
  88.7 6.1 %collective-permute-start.9 = (bf16[2,128,512]{2,1,0:T(8,128)(2,1)S(1)}, bf16[2,128,512]{2,1,0:T(8,128)(2,1)S(1)}, u32[]{:S(2)}, u32[]{:S(2)}) collective-permute-start(bf16[2,128,512]{2,1,0:T(8,128)(2,1)S(1)} %convert_element_type.145), channel_id=1, source_target_pairs={{0,8},{4,12},{24,16},{28,20},{1,9},{5,13},{25,17},{29,21},{2,10},{... | collective-permute-start | bytes 786440 | tf_op jit(solution)/shard_map/ppermute | solution.py:179
  94.9 6.0 %collective-permute-start.10 = (bf16[2,128,512]{2,1,0:T(8,128)(2,1)S(1)}, bf16[2,128,512]{2,1,0:T(8,128)(2,1)S(1)}, u32[]{:S(2)}, u32[]{:S(2)}) collective-permute-start(bf16[2,128,512]{2,1,0:T(8,128)(2,1)S(1)} %add_convert_fusion.15), channel_id=1, source_target_pairs={{8,16},{12,20},{16,8},{20,12},{9,17},{13,21},{17,9},{21,13},{10,18... | collective-permute-start | bytes 786440 | tf_op jit(solution)/shard_map/ppermute | solution.py:181
  96.2 21.0 %collective-permute-start.23 = (bf16[2,128,512]{2,1,0:T(8,128)(2,1)S(1)}, bf16[2,128,512]{2,1,0:T(8,128)(2,1)S(1)}, u32[]{:S(2)}, u32[]{:S(2)}) collective-permute-start(bf16[2,128,512]{2,1,0:T(8,128)(2,1)S(1)} %add_convert_fusion.12), channel_id=1, source_target_pairs={{0,8},{8,0},{4,12},{12,4},{16,24},{24,16},{20,28},{28,20},{1,9},{9... | collective-permute-start | bytes 786440 | tf_op jit(solution)/shard_map/ppermute | solution.py:22
  101.4 19.3 %collective-permute-start.17 = (bf16[2,128,512]{2,1,0:T(8,128)(2,1)S(1)}, bf16[2,128,512]{2,1,0:T(8,128)(2,1)S(1)}, u32[]{:S(2)}, u32[]{:S(2)}) collective-permute-start(bf16[2,128,512]{2,1,0:T(8,128)(2,1)S(1)} %add_convert_fusion.14), channel_id=1, source_target_pairs={{0,8},{8,0},{4,12},{12,4},{16,24},{24,16},{20,28},{28,20},{1,9},{9... | collective-permute-start | bytes 786440 | tf_op jit(solution)/shard_map/ppermute | solution.py:22
  114.5 20.8 %collective-permute-start.25 = (bf16[2,128,512]{2,1,0:T(8,128)(2,1)S(1)}, bf16[2,128,512]{2,1,0:T(8,128)(2,1)}, u32[]{:S(2)}, u32[]{:S(2)}) collective-permute-start(bf16[2,128,512]{2,1,0:T(8,128)(2,1)S(1)} %convert_element_type.165), channel_id=1, source_target_pairs={{0,8},{4,12},{24,16},{28,20},{1,9},{5,13},{25,17},{29,21},{2,10},{... | collective-permute-start | bytes 786440 | tf_op jit(solution)/shard_map/ppermute | solution.py:179
  119.2 37.6 %collective-permute-start.24 = (bf16[2,256,512]{2,1,0:T(8,128)(2,1)S(1)}, bf16[2,256,512]{2,1,0:T(8,128)(2,1)}, u32[]{:S(2)}, u32[]{:S(2)}) collective-permute-start(bf16[2,256,512]{2,1,0:T(8,128)(2,1)S(1)} %add_convert_fusion.5), channel_id=1, source_target_pairs={{0,4},{4,0},{8,12},{12,8},{16,20},{20,16},{24,28},{28,24},{1,5},{5... | collective-permute-start | bytes 1572872 | tf_op jit(solution)/shard_map/ppermute | solution.py:22
  122.7 35.5 %collective-permute-start.22 = (bf16[2,256,512]{2,1,0:T(8,128)(2,1)S(1)}, bf16[2,256,512]{2,1,0:T(8,128)(2,1)}, u32[]{:S(2)}, u32[]{:S(2)}) collective-permute-start(bf16[2,256,512]{2,1,0:T(8,128)(2,1)S(1)} %add_convert_fusion.7), channel_id=1, source_target_pairs={{0,4},{4,0},{8,12},{12,8},{16,20},{20,16},{24,28},{28,24},{1,5},{5... | collective-permute-start | bytes 1572872 | tf_op jit(solution)/shard_map/ppermute | solution.py:22
  132.8 7.8 %collective-permute-start.29 = (bf16[2,128,512]{2,1,0:T(8,128)(2,1)S(1)}, bf16[2,128,512]{2,1,0:T(8,128)(2,1)S(1)}, u32[]{:S(2)}, u32[]{:S(2)}) collective-permute-start(bf16[2,128,512]{2,1,0:T(8,128)(2,1)S(1)} %convert_element_type.172), channel_id=1, source_target_pairs={{0,8},{4,12},{24,16},{28,20},{1,9},{5,13},{25,17},{29,21},{2,10},{... | collective-permute-start | bytes 786440 | tf_op jit(solution)/shard_map/ppermute | solution.py:179
  136.4 5.2 %collective-permute-start.26 = (bf16[2,128,512]{2,1,0:T(8,128)(2,1)S(1)}, bf16[2,128,512]{2,1,0:T(8,128)(2,1)S(1)}, u32[]{:S(2)}, u32[]{:S(2)}) collective-permute-start(bf16[2,128,512]{2,1,0:T(8,128)(2,1)S(1)} %add_convert_fusion.11), channel_id=1, source_target_pairs={{8,16},{12,20},{16,8},{20,12},{9,17},{13,21},{17,9},{21,13},{10,18... | collective-permute-start | bytes 786440 | tf_op jit(solution)/shard_map/ppermute | solution.py:181
  140.7 6.1 %collective-permute-start.30 = (bf16[2,128,512]{2,1,0:T(8,128)(2,1)S(1)}, bf16[2,128,512]{2,1,0:T(8,128)(2,1)S(1)}, u32[]{:S(2)}, u32[]{:S(2)}) collective-permute-start(bf16[2,128,512]{2,1,0:T(8,128)(2,1)S(1)} %add_convert_fusion.9), channel_id=1, source_target_pairs={{8,16},{12,20},{16,8},{20,12},{9,17},{13,21},{17,9},{21,13},{10,18... | collective-permute-start | bytes 786440 | tf_op jit(solution)/shard_map/ppermute | solution.py:181
  142.2 9.9 %collective-permute-start.27 = (bf16[2,128,512]{2,1,0:T(8,128)(2,1)S(1)}, bf16[2,128,512]{2,1,0:T(8,128)(2,1)S(1)}, u32[]{:S(2)}, u32[]{:S(2)}) collective-permute-start(bf16[2,128,512]{2,1,0:T(8,128)(2,1)S(1)} %add_convert_fusion.10), channel_id=1, source_target_pairs={{0,8},{8,0},{4,12},{12,4},{16,24},{24,16},{20,28},{28,20},{1,9},{9... | collective-permute-start | bytes 786440 | tf_op jit(solution)/shard_map/ppermute | solution.py:22
  147.3 12.4 %collective-permute-start.31 = (bf16[2,128,512]{2,1,0:T(8,128)(2,1)S(1)}, bf16[2,128,512]{2,1,0:T(8,128)(2,1)S(1)}, u32[]{:S(2)}, u32[]{:S(2)}) collective-permute-start(bf16[2,128,512]{2,1,0:T(8,128)(2,1)S(1)} %add_convert_fusion.8), channel_id=1, source_target_pairs={{0,8},{8,0},{4,12},{12,4},{16,24},{24,16},{20,28},{28,20},{1,9},{9... | collective-permute-start | bytes 786440 | tf_op jit(solution)/shard_map/ppermute | solution.py:22
  154.1 10.2 %collective-permute-start.28 = (bf16[2,256,512]{2,1,0:T(8,128)(2,1)S(1)}, bf16[2,256,512]{2,1,0:T(8,128)(2,1)S(1)}, u32[]{:S(2)}, u32[]{:S(2)}) collective-permute-start(bf16[2,256,512]{2,1,0:T(8,128)(2,1)S(1)} %add_convert_fusion.3), channel_id=1, source_target_pairs={{0,4},{4,0},{8,12},{12,8},{16,20},{20,16},{24,28},{28,24},{1,5},{5... | collective-permute-start | bytes 1572872 | tf_op jit(solution)/shard_map/ppermute | solution.py:22
  161.7 9.2 %collective-permute-start.32 = (bf16[2,256,512]{2,1,0:T(8,128)(2,1)S(1)}, bf16[2,256,512]{2,1,0:T(8,128)(2,1)S(1)}, u32[]{:S(2)}, u32[]{:S(2)}) collective-permute-start(bf16[2,256,512]{2,1,0:T(8,128)(2,1)S(1)} %add_convert_fusion.1), channel_id=1, source_target_pairs={{0,4},{4,0},{8,12},{12,8},{16,20},{20,16},{24,28},{28,24},{1,5},{5... | collective-permute-start | bytes 1572872 | tf_op jit(solution)/shard_map/ppermute | solution.py:22
  (43 other events, 225.7 us)

commit v9 on v8

--- a/solution.py
+++ b/solution.py
@@ -35,8 +35,8 @@
         + bias_ref[...]
     )
     row_max = jnp.max(scores, axis=-1, keepdims=True)
-    log_total = row_max + jnp.log(jnp.sum(jnp.exp(scores - row_max), axis=-1, keepdims=True))
-    weights = jnp.exp(scores - log_total)
+    shifted = jnp.exp(scores - row_max)
+    weights = shifted * (1.0 / jnp.sum(shifted, axis=-1, keepdims=True))
     weights_low = weights.astype(jnp.bfloat16)
     attended = jnp.dot(weights_low, v, preferred_element_type=jnp.float32).astype(jnp.bfloat16)
     o_ref[...] = attended
@@ -48,8 +48,9 @@
     dq_ref[...] = (
         jnp.dot(score_grad, k, preferred_element_type=jnp.float32) * scale
     ).astype(jnp.bfloat16)
-    dk = jnp.dot(score_grad.T, q, preferred_element_type=jnp.float32) * scale
-    dv = jnp.dot(weights_low.T, do, preferred_element_type=jnp.float32)
+    by_query = (((0,), (0,)), ((), ()))
+    dk = lax.dot_general(score_grad, q, by_query, preferred_element_type=jnp.float32) * scale
+    dv = lax.dot_general(weights_low, do, by_query, preferred_element_type=jnp.float32)
     first = 0
     for r in grad_refs:
         rows = r.shape[1]

time: 175 us -> 175 us (level)
  no operation moved by 1% of the time
where the time goes in v9:
time: 175 us; the launch traced here: 174 us
  starting transfers between devices  57.6 us (33%)
  waiting for transfers between devices  31.1 us (18%)
  matrix products  30.4 us (17%)
  Pallas kernels  28.6 us (16%)
  other arithmetic  20.9 us (12%)
  local copies, waits for them, and re-layouts  3.28 us (2%)
    ppermute x17, starting transfers between devices, partner_2(): return lax.ppermute(block, axis, route)  34.6 us
    pallas_call x4, Pallas kernels, attention(): pl.pallas_call(functools.partial(attention_kernel, scale=score_scale, par...  28.6 us
    dot_general x32, matrix products, apply(): jnp.einsum('pr,krw->kpw', matrix, rows.astype(jnp.float32), precision=lax...  27.5 us
    ppermute x17, waiting for transfers between devices, partner_2(): return lax.ppermute(block, axis, route)  22.7 us
    ppermute x4, starting transfers between devices, body(): gathered = lax.ppermute(sends[step_level], 'seq', back)  12.1 us
    ppermute x4, waiting for transfers between devices, body(): passed = lax.ppermute(crossed, 'seq', outer_pairs(seq_count, step_level))  5.37 us
    ppermute x4, starting transfers between devices, body(): passed = lax.ppermute(crossed, 'seq', outer_pairs(seq_count, step_level))  5.15 us
    convert_element_type x8, other arithmetic, body(): sends[step_level] = outgoing.astype(jnp.bfloat16)  4.82 us
  transfers between devices with their start and end apart: 33, of which 10 were waited for; matrix products, arithmetic and copies ran while one was open for 26% of the time, Pallas kernels for 16%

profile of v9, /device:TPU:0, one launch (start us, length us, event | category | flops | bytes accessed | tf_op | source)
XLA Modules:
  0.0 173.5 jit_solution(16582441100114422829)
XLA Ops:
  0.7 2.9 %fusion.340 = (bf16[2,64,2048]{2,1,0:T(8,128)(2,1)}, f32[2,64,2048]{2,1,0:T(8,128)S(1)}) fusion(bf16[1,256,2048]{2,1,0:T(8,128)(2,1)} %bitcast.199, bf16[1,256,2048]{2,1,0:T(8,128)(2,1)} %bitcast.200, s32[128,256]{1,0:T(8,128)S(1)} %broadcast_select_fusion.4), kind=kOutput, calls=%fused_computation.431 | convolution fusion | flops 138739712 | bytes 3735552 | tf_op jit(solution)/shard_map/pr,krw->kpw/dot_general | solution.py:132
  3.6 3.0 %collective-permute-start = (bf16[2,64,2048]{2,1,0:T(8,128)(2,1)}, bf16[2,64,2048]{2,1,0:T(8,128)(2,1)}, u32[]{:S(2)}, u32[]{:S(2)}) collective-permute-start(bf16[2,64,2048]{2,1,0:T(8,128)(2,1)} %get-tuple-element.82), channel_id=1, source_target_pairs={{0,4},{4,0},{8,12},{12,8},{16,20},{20,16},{24,28},{28,24},{1,5},{5... | collective-permute-start | bytes 1572872 | tf_op jit(solution)/shard_map/ppermute | solution.py:22
  6.6 1.4 fusion.21
  8.0 1.4 fusion.23
  10.7 2.0 %pad_maximum_fusion.6.refs_0_ = bf16[2,256,512]{2,1,0:T(8,128)(2,1)} fusion(bf16[1,256,512]{2,1,0:T(8,128)(2,1)} %get-tuple-element.70, bf16[1,256,512]{2,1,0:T(8,128)(2,1)} %get-tuple-element.95), kind=kLoop, calls=%fused_computation.58 | loop fusion | flops 262144 | bytes 1048576 | tf_op jit(solution)/shard_map/stack | solution.py:143
  15.1 3.7 %collective-permute-done = bf16[2,64,2048]{2,1,0:T(8,128)(2,1)} collective-permute-done((bf16[2,64,2048]{2,1,0:T(8,128)(2,1)}, bf16[2,64,2048]{2,1,0:T(8,128)(2,1)}, u32[]{:S(2)}, u32[]{:S(2)}) %collective-permute-start) | collective-permute-done | bytes 524320 | tf_op jit(solution)/shard_map/ppermute | solution.py:22
  20.1 1.9 %collective-permute-start.2 = (bf16[2,128,512]{2,1,0:T(8,128)(2,1)S(1)}, bf16[2,128,512]{2,1,0:T(8,128)(2,1)S(1)}, u32[]{:S(2)}, u32[]{:S(2)}) collective-permute-start(bf16[2,128,512]{2,1,0:T(8,128)(2,1)S(1)} %get-tuple-element.86), channel_id=1, source_target_pairs={{0,8},{8,0},{4,12},{12,4},{16,24},{24,16},{20,28},{28,20},{1,9},{9... | collective-permute-start | bytes 786440 | tf_op jit(solution)/shard_map/ppermute | solution.py:22
  25.0 1.9 %collective-permute-start.12 = (bf16[2,128,512]{2,1,0:T(8,128)(2,1)S(1)}, bf16[2,128,512]{2,1,0:T(8,128)(2,1)S(1)}, u32[]{:S(2)}, u32[]{:S(2)}) collective-permute-start(bf16[2,128,512]{2,1,0:T(8,128)(2,1)S(1)} %get-tuple-element.90), channel_id=1, source_target_pairs={{0,8},{8,0},{4,12},{12,4},{16,24},{24,16},{20,28},{28,20},{1,9},{9... | collective-permute-start | bytes 786440 | tf_op jit(solution)/shard_map/ppermute | solution.py:22
  30.3 4.8 %collective-permute-done.6.refs_2_ = bf16[2,128,512]{2,1,0:T(8,128)(2,1)S(1)} collective-permute-done((bf16[2,128,512]{2,1,0:T(8,128)(2,1)S(1)}, bf16[2,128,512]{2,1,0:T(8,128)(2,1)S(1)}, u32[]{:S(2)}, u32[]{:S(2)}) %collective-permute-start.6) | collective-permute-done | bytes 262176 | tf_op jit(solution)/shard_map/ppermute | solution.py:22
  36.8 1.8 %collective-permute-start.1 = (bf16[2,256,512]{2,1,0:T(8,128)(2,1)S(1)}, bf16[2,256,512]{2,1,0:T(8,128)(2,1)}, u32[]{:S(2)}, u32[]{:S(2)}) collective-permute-start(bf16[2,256,512]{2,1,0:T(8,128)(2,1)S(1)} %pad_maximum_fusion.4.refs_0_), channel_id=1, source_target_pairs={{0,4},{4,0},{8,12},{12,8},{16,20},{20,16},{24,28},{28,24},{1,5},{5... | collective-permute-start | bytes 1572872 | tf_op jit(solution)/shard_map/ppermute | solution.py:22
  43.8 1.4 collective-permute-done.19.refs_2_
  47.7 5.4 %collective-permute-done.8 = bf16[2,128,512]{2,1,0:T(8,128)(2,1)S(1)} collective-permute-done((bf16[2,128,512]{2,1,0:T(8,128)(2,1)S(1)}, bf16[2,128,512]{2,1,0:T(8,128)(2,1)S(1)}, u32[]{:S(2)}, u32[]{:S(2)}) %collective-permute-start.8) | collective-permute-done | bytes 262176 | tf_op jit(solution)/shard_map/ppermute | solution.py:154
  55.2 4.2 %collective-permute-done.5.refs_1_ = bf16[2,256,512]{2,1,0:T(8,128)(2,1)S(1)} collective-permute-done((bf16[2,256,512]{2,1,0:T(8,128)(2,1)S(1)}, bf16[2,256,512]{2,1,0:T(8,128)(2,1)S(1)}, u32[]{:S(2)}, u32[]{:S(2)}) %collective-permute-start.5) | collective-permute-done | bytes 524320 | tf_op jit(solution)/shard_map/ppermute | solution.py:22
  60.2 1.7 %collective-permute-start.18 = (bf16[2,256,512]{2,1,0:T(8,128)(2,1)S(1)}, bf16[2,256,512]{2,1,0:T(8,128)(2,1)}, u32[]{:S(2)}, u32[]{:S(2)}) collective-permute-start(bf16[2,256,512]{2,1,0:T(8,128)(2,1)S(1)} %pad_maximum_fusion.7.refs_0_), channel_id=1, source_target_pairs={{0,4},{4,0},{8,12},{12,8},{16,20},{20,16},{24,28},{28,24},{1,5},{5... | collective-permute-start | bytes 1572872 | tf_op jit(solution)/shard_map/ppermute | solution.py:22
  62.0 7.1 %shard_map.76 = (bf16[256,512]{1,0:T(8,128)(2,1)}, bf16[256,512]{1,0:T(8,128)(2,1)}, f32[2,256,512]{2,1,0:T(8,128)}, f32[2,256,512]{2,1,0:T(8,128)}, f32[2,128,512]{2,1,0:T(8,128)}, /*index=5*/f32[2,128,512]{2,1,0:T(8,128)}) custom-call(f32[1,768]{1,0:T(1,128)} %constant.99.clone.1.bias_ref, bf16[256,2048]{1,0:T(8,128)(2,1)} %q_ref.7, ...), custom_call_target="tpu_custom_call" | custom-call | flops 1207959552 | bytes 5767168 | tf_op jit(solution)/shard_map/pallas_call | solution.py:72
  73.9 6.5 %collective-permute-start.15 = (bf16[2,128,512]{2,1,0:T(8,128)(2,1)S(1)}, bf16[2,128,512]{2,1,0:T(8,128)(2,1)S(1)}, u32[]{:S(2)}, u32[]{:S(2)}) collective-permute-start(bf16[2,128,512]{2,1,0:T(8,128)(2,1)S(1)} %convert_element_type.152), channel_id=1, source_target_pairs={{0,8},{4,12},{24,16},{28,20},{1,9},{5,13},{25,17},{29,21},{2,10},{... | collective-permute-start | bytes 786440 | tf_op jit(solution)/shard_map/ppermute | solution.py:180
  80.4 7.1 %shard_map.75 = (bf16[256,512]{1,0:T(8,128)(2,1)}, bf16[256,512]{1,0:T(8,128)(2,1)}, f32[2,256,512]{2,1,0:T(8,128)}, f32[2,256,512]{2,1,0:T(8,128)}, f32[2,128,512]{2,1,0:T(8,128)}, /*index=5*/f32[2,128,512]{2,1,0:T(8,128)}) custom-call(f32[1,768]{1,0:T(1,128)} %constant.99.clone.1.bias_ref, bf16[256,2048]{1,0:T(8,128)(2,1)} %q_ref.7, ...), custom_call_target="tpu_custom_call" | custom-call | flops 1207959552 | bytes 5767168 | tf_op jit(solution)/shard_map/pallas_call | solution.py:72
  88.7 1.5 collective-permute-start.9
  92.6 2.1 %collective-permute-done.9 = bf16[2,128,512]{2,1,0:T(8,128)(2,1)S(1)} collective-permute-done((bf16[2,128,512]{2,1,0:T(8,128)(2,1)S(1)}, bf16[2,128,512]{2,1,0:T(8,128)(2,1)S(1)}, u32[]{:S(2)}, u32[]{:S(2)}) %collective-permute-start.9) | collective-permute-done | bytes 262176 | tf_op jit(solution)/shard_map/ppermute | solution.py:180
  96.2 4.7 %collective-permute-start.23 = (bf16[2,128,512]{2,1,0:T(8,128)(2,1)S(1)}, bf16[2,128,512]{2,1,0:T(8,128)(2,1)S(1)}, u32[]{:S(2)}, u32[]{:S(2)}) collective-permute-start(bf16[2,128,512]{2,1,0:T(8,128)(2,1)S(1)} %add_convert_fusion.12), channel_id=1, source_target_pairs={{0,8},{8,0},{4,12},{12,4},{16,24},{24,16},{20,28},{28,20},{1,9},{9... | collective-permute-start | bytes 786440 | tf_op jit(solution)/shard_map/ppermute | solution.py:22
  101.4 4.8 %collective-permute-start.17 = (bf16[2,128,512]{2,1,0:T(8,128)(2,1)S(1)}, bf16[2,128,512]{2,1,0:T(8,128)(2,1)S(1)}, u32[]{:S(2)}, u32[]{:S(2)}) collective-permute-start(bf16[2,128,512]{2,1,0:T(8,128)(2,1)S(1)} %add_convert_fusion.14), channel_id=1, source_target_pairs={{0,8},{8,0},{4,12},{12,4},{16,24},{24,16},{20,28},{28,20},{1,9},{9... | collective-permute-start | bytes 786440 | tf_op jit(solution)/shard_map/ppermute | solution.py:22
  106.3 7.2 %shard_map.77 = (bf16[256,512]{1,0:T(8,128)(2,1)}, bf16[256,512]{1,0:T(8,128)(2,1)}, f32[2,256,512]{2,1,0:T(8,128)}, f32[2,256,512]{2,1,0:T(8,128)}, f32[2,128,512]{2,1,0:T(8,128)}, /*index=5*/f32[2,128,512]{2,1,0:T(8,128)}) custom-call(f32[1,768]{1,0:T(1,128)} %constant.99.clone.1.bias_ref, bf16[256,2048]{1,0:T(8,128)(2,1)} %q_ref.7, ...), custom_call_target="tpu_custom_call" | custom-call | flops 1207959552 | bytes 5767168 | tf_op jit(solution)/shard_map/pallas_call | solution.py:72
  114.5 2.7 %collective-permute-start.25 = (bf16[2,128,512]{2,1,0:T(8,128)(2,1)S(1)}, bf16[2,128,512]{2,1,0:T(8,128)(2,1)}, u32[]{:S(2)}, u32[]{:S(2)}) collective-permute-start(bf16[2,128,512]{2,1,0:T(8,128)(2,1)S(1)} %convert_element_type.165), channel_id=1, source_target_pairs={{0,8},{4,12},{24,16},{28,20},{1,9},{5,13},{25,17},{29,21},{2,10},{... | collective-permute-start | bytes 786440 | tf_op jit(solution)/shard_map/ppermute | solution.py:180
  119.2 1.6 collective-permute-start.24
  124.4 7.2 %shard_map.78 = (bf16[256,512]{1,0:T(8,128)(2,1)}, bf16[256,512]{1,0:T(8,128)(2,1)}, f32[2,256,512]{2,1,0:T(8,128)}, f32[2,256,512]{2,1,0:T(8,128)}, f32[2,128,512]{2,1,0:T(8,128)}, /*index=5*/f32[2,128,512]{2,1,0:T(8,128)}) custom-call(f32[1,768]{1,0:T(1,128)} %constant.99.clone.1.bias_ref, bf16[256,2048]{1,0:T(8,128)(2,1)} %q_ref.7, ...), custom_call_target="tpu_custom_call" | custom-call | flops 1207959552 | bytes 5767168 | tf_op jit(solution)/shard_map/pallas_call | solution.py:72
  132.8 1.4 collective-permute-start.29
  142.2 4.5 %collective-permute-start.27 = (bf16[2,128,512]{2,1,0:T(8,128)(2,1)S(1)}, bf16[2,128,512]{2,1,0:T(8,128)(2,1)S(1)}, u32[]{:S(2)}, u32[]{:S(2)}) collective-permute-start(bf16[2,128,512]{2,1,0:T(8,128)(2,1)S(1)} %add_convert_fusion.10), channel_id=1, source_target_pairs={{0,8},{8,0},{4,12},{12,4},{16,24},{24,16},{20,28},{28,20},{1,9},{9... | collective-permute-start | bytes 786440 | tf_op jit(solution)/shard_map/ppermute | solution.py:22
  147.3 4.8 %collective-permute-start.31 = (bf16[2,128,512]{2,1,0:T(8,128)(2,1)S(1)}, bf16[2,128,512]{2,1,0:T(8,128)(2,1)S(1)}, u32[]{:S(2)}, u32[]{:S(2)}) collective-permute-start(bf16[2,128,512]{2,1,0:T(8,128)(2,1)S(1)} %add_convert_fusion.8), channel_id=1, source_target_pairs={{0,8},{8,0},{4,12},{12,4},{16,24},{24,16},{20,28},{28,20},{1,9},{9... | collective-permute-start | bytes 786440 | tf_op jit(solution)/shard_map/ppermute | solution.py:22
  154.1 1.6 collective-permute-start.28
  156.8 1.4 add_convert_fusion.4
  158.3 1.4 add_convert_fusion.6
  164.6 6.3 %collective-permute-done.32 = bf16[2,256,512]{2,1,0:T(8,128)(2,1)S(1)} collective-permute-done((bf16[2,256,512]{2,1,0:T(8,128)(2,1)S(1)}, bf16[2,256,512]{2,1,0:T(8,128)(2,1)S(1)}, u32[]{:S(2)}, u32[]{:S(2)}) %collective-permute-start.32) | collective-permute-done | bytes 524320 | tf_op jit(solution)/shard_map/ppermute | solution.py:22
  (201 shorter events, 60.4 us)
Async XLA Ops:
  3.6 15.2 %collective-permute-start = (bf16[2,64,2048]{2,1,0:T(8,128)(2,1)}, bf16[2,64,2048]{2,1,0:T(8,128)(2,1)}, u32[]{:S(2)}, u32[]{:S(2)}) collective-permute-start(bf16[2,64,2048]{2,1,0:T(8,128)(2,1)} %get-tuple-element.82), channel_id=1, source_target_pairs={{0,4},{4,0},{8,12},{12,8},{16,20},{20,16},{24,28},{28,24},{1,5},{5... | collective-permute-start | bytes 1572872 | tf_op jit(solution)/shard_map/ppermute | solution.py:22
  20.1 18.5 %collective-permute-start.2 = (bf16[2,128,512]{2,1,0:T(8,128)(2,1)S(1)}, bf16[2,128,512]{2,1,0:T(8,128)(2,1)S(1)}, u32[]{:S(2)}, u32[]{:S(2)}) collective-permute-start(bf16[2,128,512]{2,1,0:T(8,128)(2,1)S(1)} %get-tuple-element.86), channel_id=1, source_target_pairs={{0,8},{8,0},{4,12},{12,4},{16,24},{24,16},{20,28},{28,20},{1,9},{9... | collective-permute-start | bytes 786440 | tf_op jit(solution)/shard_map/ppermute | solution.py:22
  23.3 11.7 %collective-permute-start.6 = (bf16[2,128,512]{2,1,0:T(8,128)(2,1)S(1)}, bf16[2,128,512]{2,1,0:T(8,128)(2,1)S(1)}, u32[]{:S(2)}, u32[]{:S(2)}) collective-permute-start(bf16[2,128,512]{2,1,0:T(8,128)(2,1)S(1)} %get-tuple-element.84), channel_id=1, source_target_pairs={{0,8},{8,0},{4,12},{12,4},{16,24},{24,16},{20,28},{28,20},{1,9},{9... | collective-permute-start | bytes 786440 | tf_op jit(solution)/shard_map/ppermute | solution.py:22
  25.0 15.7 %collective-permute-start.12 = (bf16[2,128,512]{2,1,0:T(8,128)(2,1)S(1)}, bf16[2,128,512]{2,1,0:T(8,128)(2,1)S(1)}, u32[]{:S(2)}, u32[]{:S(2)}) collective-permute-start(bf16[2,128,512]{2,1,0:T(8,128)(2,1)S(1)} %get-tuple-element.90), channel_id=1, source_target_pairs={{0,8},{8,0},{4,12},{12,4},{16,24},{24,16},{20,28},{28,20},{1,9},{9... | collective-permute-start | bytes 786440 | tf_op jit(solution)/shard_map/ppermute | solution.py:22
  28.2 17.1 %collective-permute-start.19 = (bf16[2,128,512]{2,1,0:T(8,128)(2,1)S(1)}, bf16[2,128,512]{2,1,0:T(8,128)(2,1)S(1)}, u32[]{:S(2)}, u32[]{:S(2)}) collective-permute-start(bf16[2,128,512]{2,1,0:T(8,128)(2,1)S(1)} %get-tuple-element.88), channel_id=1, source_target_pairs={{0,8},{8,0},{4,12},{12,4},{16,24},{24,16},{20,28},{28,20},{1,9},{9... | collective-permute-start | bytes 786440 | tf_op jit(solution)/shard_map/ppermute | solution.py:22
  35.5 5.9 %collective-permute-start.7 = (bf16[2,128,512]{2,1,0:T(8,128)(2,1)S(1)}, bf16[2,128,512]{2,1,0:T(8,128)(2,1)S(1)}, u32[]{:S(2)}, u32[]{:S(2)}) collective-permute-start(bf16[2,128,512]{2,1,0:T(8,128)(2,1)S(1)} %fusion.17), channel_id=1, source_target_pairs={{8,16},{12,20},{16,8},{20,12},{9,17},{13,21},{17,9},{21,13},{10,18... | collective-permute-start | bytes 786440 | tf_op jit(solution)/shard_map/ppermute | solution.py:153
  36.8 37.1 %collective-permute-start.1 = (bf16[2,256,512]{2,1,0:T(8,128)(2,1)S(1)}, bf16[2,256,512]{2,1,0:T(8,128)(2,1)}, u32[]{:S(2)}, u32[]{:S(2)}) collective-permute-start(bf16[2,256,512]{2,1,0:T(8,128)(2,1)S(1)} %pad_maximum_fusion.4.refs_0_), channel_id=1, source_target_pairs={{0,4},{4,0},{8,12},{12,8},{16,20},{20,16},{24,28},{28,24},{1,5},{5... | collective-permute-start | bytes 1572872 | tf_op jit(solution)/shard_map/ppermute | solution.py:22
  38.6 20.8 %collective-permute-start.5 = (bf16[2,256,512]{2,1,0:T(8,128)(2,1)S(1)}, bf16[2,256,512]{2,1,0:T(8,128)(2,1)S(1)}, u32[]{:S(2)}, u32[]{:S(2)}) collective-permute-start(bf16[2,256,512]{2,1,0:T(8,128)(2,1)S(1)} %copy-done.24), channel_id=1, source_target_pairs={{0,4},{4,0},{8,12},{12,8},{16,20},{20,16},{24,28},{28,24},{1,5},{5... | collective-permute-start | bytes 1572872 | tf_op jit(solution)/shard_map/ppermute | solution.py:22
  40.7 6.4 %collective-permute-start.3 = (bf16[2,128,512]{2,1,0:T(8,128)(2,1)S(1)}, bf16[2,128,512]{2,1,0:T(8,128)(2,1)S(1)}, u32[]{:S(2)}, u32[]{:S(2)}) collective-permute-start(bf16[2,128,512]{2,1,0:T(8,128)(2,1)S(1)} %fusion.18), channel_id=1, source_target_pairs={{8,16},{12,20},{16,8},{20,12},{9,17},{13,21},{17,9},{21,13},{10,18... | collective-permute-start | bytes 786440 | tf_op jit(solution)/shard_map/ppermute | solution.py:153
  41.4 11.7 %collective-permute-start.8 = (bf16[2,128,512]{2,1,0:T(8,128)(2,1)S(1)}, bf16[2,128,512]{2,1,0:T(8,128)(2,1)S(1)}, u32[]{:S(2)}, u32[]{:S(2)}) collective-permute-start(bf16[2,128,512]{2,1,0:T(8,128)(2,1)S(1)} %collective-permute-done.7), channel_id=1, source_target_pairs={{8,0},{12,4},{16,24},{20,28},{9,1},{13,5},{17,25},{21,29},{10,2},{... | collective-permute-start | bytes 786440 | tf_op jit(solution)/shard_map/ppermute | solution.py:154
  45.3 24.9 %collective-permute-start.13 = (bf16[2,128,512]{2,1,0:T(8,128)(2,1)}, bf16[2,128,512]{2,1,0:T(8,128)(2,1)S(1)}, u32[]{:S(2)}, u32[]{:S(2)}) collective-permute-start(bf16[2,128,512]{2,1,0:T(8,128)(2,1)} %fusion.16), channel_id=1, source_target_pairs={{8,16},{12,20},{16,8},{20,12},{9,17},{13,21},{17,9},{21,13},{10,18... | collective-permute-start | bytes 786440 | tf_op jit(solution)/shard_map/ppermute | solution.py:153
  47.1 23.5 %collective-permute-start.20 = (bf16[2,128,512]{2,1,0:T(8,128)(2,1)}, bf16[2,128,512]{2,1,0:T(8,128)(2,1)S(1)}, u32[]{:S(2)}, u32[]{:S(2)}) collective-permute-start(bf16[2,128,512]{2,1,0:T(8,128)(2,1)} %fusion.15), channel_id=1, source_target_pairs={{8,16},{12,20},{16,8},{20,12},{9,17},{13,21},{17,9},{21,13},{10,18... | collective-permute-start | bytes 786440 | tf_op jit(solution)/shard_map/ppermute | solution.py:153
  53.1 18.7 %collective-permute-start.4 = (bf16[2,128,512]{2,1,0:T(8,128)(2,1)S(1)}, bf16[2,128,512]{2,1,0:T(8,128)(2,1)S(1)}, u32[]{:S(2)}, u32[]{:S(2)}) collective-permute-start(bf16[2,128,512]{2,1,0:T(8,128)(2,1)S(1)} %collective-permute-done.3), channel_id=1, source_target_pairs={{8,0},{12,4},{16,24},{20,28},{9,1},{13,5},{17,25},{21,29},{10,2},{... | collective-permute-start | bytes 786440 | tf_op jit(solution)/shard_map/ppermute | solution.py:154
  60.2 64.2 %collective-permute-start.18 = (bf16[2,256,512]{2,1,0:T(8,128)(2,1)S(1)}, bf16[2,256,512]{2,1,0:T(8,128)(2,1)}, u32[]{:S(2)}, u32[]{:S(2)}) collective-permute-start(bf16[2,256,512]{2,1,0:T(8,128)(2,1)S(1)} %pad_maximum_fusion.7.refs_0_), channel_id=1, source_target_pairs={{0,4},{4,0},{8,12},{12,8},{16,20},{20,16},{24,28},{28,24},{1,5},{5... | collective-permute-start | bytes 1572872 | tf_op jit(solution)/shard_map/ppermute | solution.py:22
  70.2 36.1 %collective-permute-start.11 = (bf16[2,256,512]{2,1,0:T(8,128)(2,1)S(1)}, bf16[2,256,512]{2,1,0:T(8,128)(2,1)}, u32[]{:S(2)}, u32[]{:S(2)}) collective-permute-start(bf16[2,256,512]{2,1,0:T(8,128)(2,1)S(1)} %copy-done.22), channel_id=1, source_target_pairs={{0,4},{4,0},{8,12},{12,8},{16,20},{20,16},{24,28},{28,24},{1,5},{5... | collective-permute-start | bytes 1572872 | tf_op jit(solution)/shard_map/ppermute | solution.py:22
  70.5 18.1 %collective-permute-start.14 = (bf16[2,128,512]{2,1,0:T(8,128)(2,1)S(1)}, bf16[2,128,512]{2,1,0:T(8,128)(2,1)S(1)}, u32[]{:S(2)}, u32[]{:S(2)}) collective-permute-start(bf16[2,128,512]{2,1,0:T(8,128)(2,1)S(1)} %collective-permute-done.13), channel_id=1, source_target_pairs={{8,0},{12,4},{16,24},{20,28},{9,1},{13,5},{17,25},{21,29},{10,2},{... | collective-permute-start | bytes 786440 | tf_op jit(solution)/shard_map/ppermute | solution.py:154
  71.8 20.0 %collective-permute-start.21 = (bf16[2,128,512]{2,1,0:T(8,128)(2,1)S(1)}, bf16[2,128,512]{2,1,0:T(8,128)(2,1)S(1)}, u32[]{:S(2)}, u32[]{:S(2)}) collective-permute-start(bf16[2,128,512]{2,1,0:T(8,128)(2,1)S(1)} %collective-permute-done.20), channel_id=1, source_target_pairs={{8,0},{12,4},{16,24},{20,28},{9,1},{13,5},{17,25},{21,29},{10,2},{... | collective-permute-start | bytes 786440 | tf_op jit(solution)/shard_map/ppermute | solution.py:154
  73.9 17.1 %collective-permute-start.15 = (bf16[2,128,512]{2,1,0:T(8,128)(2,1)S(1)}, bf16[2,128,512]{2,1,0:T(8,128)(2,1)S(1)}, u32[]{:S(2)}, u32[]{:S(2)}) collective-permute-start(bf16[2,128,512]{2,1,0:T(8,128)(2,1)S(1)} %convert_element_type.152), channel_id=1, source_target_pairs={{0,8},{4,12},{24,16},{28,20},{1,9},{5,13},{25,17},{29,21},{2,10},{... | collective-permute-start | bytes 786440 | tf_op jit(solution)/shard_map/ppermute | solution.py:180
  88.7 6.1 %collective-permute-start.9 = (bf16[2,128,512]{2,1,0:T(8,128)(2,1)S(1)}, bf16[2,128,512]{2,1,0:T(8,128)(2,1)S(1)}, u32[]{:S(2)}, u32[]{:S(2)}) collective-permute-start(bf16[2,128,512]{2,1,0:T(8,128)(2,1)S(1)} %convert_element_type.145), channel_id=1, source_target_pairs={{0,8},{4,12},{24,16},{28,20},{1,9},{5,13},{25,17},{29,21},{2,10},{... | collective-permute-start | bytes 786440 | tf_op jit(solution)/shard_map/ppermute | solution.py:180
  94.8 6.0 %collective-permute-start.10 = (bf16[2,128,512]{2,1,0:T(8,128)(2,1)S(1)}, bf16[2,128,512]{2,1,0:T(8,128)(2,1)S(1)}, u32[]{:S(2)}, u32[]{:S(2)}) collective-permute-start(bf16[2,128,512]{2,1,0:T(8,128)(2,1)S(1)} %add_convert_fusion.15), channel_id=1, source_target_pairs={{8,16},{12,20},{16,8},{20,12},{9,17},{13,21},{17,9},{21,13},{10,18... | collective-permute-start | bytes 786440 | tf_op jit(solution)/shard_map/ppermute | solution.py:182
  96.2 21.0 %collective-permute-start.23 = (bf16[2,128,512]{2,1,0:T(8,128)(2,1)S(1)}, bf16[2,128,512]{2,1,0:T(8,128)(2,1)S(1)}, u32[]{:S(2)}, u32[]{:S(2)}) collective-permute-start(bf16[2,128,512]{2,1,0:T(8,128)(2,1)S(1)} %add_convert_fusion.12), channel_id=1, source_target_pairs={{0,8},{8,0},{4,12},{12,4},{16,24},{24,16},{20,28},{28,20},{1,9},{9... | collective-permute-start | bytes 786440 | tf_op jit(solution)/shard_map/ppermute | solution.py:22
  101.4 19.3 %collective-permute-start.17 = (bf16[2,128,512]{2,1,0:T(8,128)(2,1)S(1)}, bf16[2,128,512]{2,1,0:T(8,128)(2,1)S(1)}, u32[]{:S(2)}, u32[]{:S(2)}) collective-permute-start(bf16[2,128,512]{2,1,0:T(8,128)(2,1)S(1)} %add_convert_fusion.14), channel_id=1, source_target_pairs={{0,8},{8,0},{4,12},{12,4},{16,24},{24,16},{20,28},{28,20},{1,9},{9... | collective-permute-start | bytes 786440 | tf_op jit(solution)/shard_map/ppermute | solution.py:22
  114.5 20.8 %collective-permute-start.25 = (bf16[2,128,512]{2,1,0:T(8,128)(2,1)S(1)}, bf16[2,128,512]{2,1,0:T(8,128)(2,1)}, u32[]{:S(2)}, u32[]{:S(2)}) collective-permute-start(bf16[2,128,512]{2,1,0:T(8,128)(2,1)S(1)} %convert_element_type.165), channel_id=1, source_target_pairs={{0,8},{4,12},{24,16},{28,20},{1,9},{5,13},{25,17},{29,21},{2,10},{... | collective-permute-start | bytes 786440 | tf_op jit(solution)/shard_map/ppermute | solution.py:180
  119.2 37.6 %collective-permute-start.24 = (bf16[2,256,512]{2,1,0:T(8,128)(2,1)S(1)}, bf16[2,256,512]{2,1,0:T(8,128)(2,1)}, u32[]{:S(2)}, u32[]{:S(2)}) collective-permute-start(bf16[2,256,512]{2,1,0:T(8,128)(2,1)S(1)} %add_convert_fusion.5), channel_id=1, source_target_pairs={{0,4},{4,0},{8,12},{12,8},{16,20},{20,16},{24,28},{28,24},{1,5},{5... | collective-permute-start | bytes 1572872 | tf_op jit(solution)/shard_map/ppermute | solution.py:22
  122.7 35.5 %collective-permute-start.22 = (bf16[2,256,512]{2,1,0:T(8,128)(2,1)S(1)}, bf16[2,256,512]{2,1,0:T(8,128)(2,1)}, u32[]{:S(2)}, u32[]{:S(2)}) collective-permute-start(bf16[2,256,512]{2,1,0:T(8,128)(2,1)S(1)} %add_convert_fusion.7), channel_id=1, source_target_pairs={{0,4},{4,0},{8,12},{12,8},{16,20},{20,16},{24,28},{28,24},{1,5},{5... | collective-permute-start | bytes 1572872 | tf_op jit(solution)/shard_map/ppermute | solution.py:22
  132.8 7.8 %collective-permute-start.29 = (bf16[2,128,512]{2,1,0:T(8,128)(2,1)S(1)}, bf16[2,128,512]{2,1,0:T(8,128)(2,1)S(1)}, u32[]{:S(2)}, u32[]{:S(2)}) collective-permute-start(bf16[2,128,512]{2,1,0:T(8,128)(2,1)S(1)} %convert_element_type.172), channel_id=1, source_target_pairs={{0,8},{4,12},{24,16},{28,20},{1,9},{5,13},{25,17},{29,21},{2,10},{... | collective-permute-start | bytes 786440 | tf_op jit(solution)/shard_map/ppermute | solution.py:180
  136.3 5.2 %collective-permute-start.26 = (bf16[2,128,512]{2,1,0:T(8,128)(2,1)S(1)}, bf16[2,128,512]{2,1,0:T(8,128)(2,1)S(1)}, u32[]{:S(2)}, u32[]{:S(2)}) collective-permute-start(bf16[2,128,512]{2,1,0:T(8,128)(2,1)S(1)} %add_convert_fusion.11), channel_id=1, source_target_pairs={{8,16},{12,20},{16,8},{20,12},{9,17},{13,21},{17,9},{21,13},{10,18... | collective-permute-start | bytes 786440 | tf_op jit(solution)/shard_map/ppermute | solution.py:182
  140.6 6.1 %collective-permute-start.30 = (bf16[2,128,512]{2,1,0:T(8,128)(2,1)S(1)}, bf16[2,128,512]{2,1,0:T(8,128)(2,1)S(1)}, u32[]{:S(2)}, u32[]{:S(2)}) collective-permute-start(bf16[2,128,512]{2,1,0:T(8,128)(2,1)S(1)} %add_convert_fusion.9), channel_id=1, source_target_pairs={{8,16},{12,20},{16,8},{20,12},{9,17},{13,21},{17,9},{21,13},{10,18... | collective-permute-start | bytes 786440 | tf_op jit(solution)/shard_map/ppermute | solution.py:182
  142.2 9.9 %collective-permute-start.27 = (bf16[2,128,512]{2,1,0:T(8,128)(2,1)S(1)}, bf16[2,128,512]{2,1,0:T(8,128)(2,1)S(1)}, u32[]{:S(2)}, u32[]{:S(2)}) collective-permute-start(bf16[2,128,512]{2,1,0:T(8,128)(2,1)S(1)} %add_convert_fusion.10), channel_id=1, source_target_pairs={{0,8},{8,0},{4,12},{12,4},{16,24},{24,16},{20,28},{28,20},{1,9},{9... | collective-permute-start | bytes 786440 | tf_op jit(solution)/shard_map/ppermute | solution.py:22
  147.3 12.4 %collective-permute-start.31 = (bf16[2,128,512]{2,1,0:T(8,128)(2,1)S(1)}, bf16[2,128,512]{2,1,0:T(8,128)(2,1)S(1)}, u32[]{:S(2)}, u32[]{:S(2)}) collective-permute-start(bf16[2,128,512]{2,1,0:T(8,128)(2,1)S(1)} %add_convert_fusion.8), channel_id=1, source_target_pairs={{0,8},{8,0},{4,12},{12,4},{16,24},{24,16},{20,28},{28,20},{1,9},{9... | collective-permute-start | bytes 786440 | tf_op jit(solution)/shard_map/ppermute | solution.py:22
  154.1 10.2 %collective-permute-start.28 = (bf16[2,256,512]{2,1,0:T(8,128)(2,1)S(1)}, bf16[2,256,512]{2,1,0:T(8,128)(2,1)S(1)}, u32[]{:S(2)}, u32[]{:S(2)}) collective-permute-start(bf16[2,256,512]{2,1,0:T(8,128)(2,1)S(1)} %add_convert_fusion.3), channel_id=1, source_target_pairs={{0,4},{4,0},{8,12},{12,8},{16,20},{20,16},{24,28},{28,24},{1,5},{5... | collective-permute-start | bytes 1572872 | tf_op jit(solution)/shard_map/ppermute | solution.py:22
  161.7 9.2 %collective-permute-start.32 = (bf16[2,256,512]{2,1,0:T(8,128)(2,1)S(1)}, bf16[2,256,512]{2,1,0:T(8,128)(2,1)S(1)}, u32[]{:S(2)}, u32[]{:S(2)}) collective-permute-start(bf16[2,256,512]{2,1,0:T(8,128)(2,1)S(1)} %add_convert_fusion.1), channel_id=1, source_target_pairs={{0,4},{4,0},{8,12},{12,8},{16,20},{20,16},{24,28},{28,24},{1,5},{5... | collective-permute-start | bytes 1572872 | tf_op jit(solution)/shard_map/ppermute | solution.py:22
  (43 other events, 225.7 us)

commit v10 on v9

--- a/solution.py
+++ b/solution.py
@@ -9,7 +9,7 @@
 
 HEAD_DIM = 128
 POOLED = 128
-CHUNKS = 4
+CHUNKS = 2
 
 
 def partner_2(block, axis, stride):

time: 175 us -> 175 us (level)
  waiting for transfers between devices: 31.1 us -> 70.8 us
  starting transfers between devices: 57.6 us -> 37.4 us
  matrix products: 30.4 us -> 22.1 us
  other arithmetic: 20.9 us -> 16.3 us
  Pallas kernels: 28.6 us -> 24.8 us
    ppermute x17 -> x9, waiting for transfers between devices: 22.7 us -> 55.3 us  [partner_2(): return lax.ppermute(block, axis, route)]
    ppermute x4 -> x2, starting transfers between devices: 12.1 us -> 3.56 us  [body(): gathered = lax.ppermute(sends[step_level], 'seq', back)]
    dot_general x32 -> x16, matrix products: 27.5 us -> 19.1 us  [apply(): jnp.einsum('pr,krw->kpw', matrix, rows.astype(jnp.float32), precision=lax...]
    ppermute x4 -> x2, waiting for transfers between devices: 5.37 us -> 13.1 us  [body(): passed = lax.ppermute(crossed, 'seq', outer_pairs(seq_count, step_level))]
    ppermute x17 -> x9, starting transfers between devices: 34.6 us -> 27.5 us  [partner_2(): return lax.ppermute(block, axis, route)]
    pallas_call x4 -> x2, Pallas kernels: 28.6 us -> 24.8 us  [attention(): pl.pallas_call(functools.partial(attention_kernel, scale=score_scale, par...]
    ppermute x4 -> x2, starting transfers between devices: 5.15 us -> 2.57 us  [body(): passed = lax.ppermute(crossed, 'seq', outer_pairs(seq_count, step_level))]
    another operation x4 -> x2, other arithmetic: 3.42 us -> 1.26 us
  transfers between devices with their start and end apart: 33 -> 17, of which waited for: 10 -> 9; matrix products, arithmetic and copies ran while one was open for 26% -> 19% of each run, Pallas kernels for 16% -> 14%
where the time goes in v10:
time: 175 us; the launch traced here: 174 us
  waiting for transfers between devices  70.8 us (40%)
  starting transfers between devices  37.4 us (21%)
  Pallas kernels  24.8 us (14%)
  matrix products  22.1 us (13%)
  other arithmetic  16.3 us (9%)
    ppermute x9, waiting for transfers between devices, partner_2(): return lax.ppermute(block, axis, route)  55.3 us
    ppermute x9, starting transfers between devices, partner_2(): return lax.ppermute(block, axis, route)  27.5 us
    pallas_call x2, Pallas kernels, attention(): pl.pallas_call(functools.partial(attention_kernel, scale=score_scale, par...  24.8 us
    dot_general x16, matrix products, apply(): jnp.einsum('pr,krw->kpw', matrix, rows.astype(jnp.float32), precision=lax...  19.1 us
    ppermute x2, waiting for transfers between devices, body(): passed = lax.ppermute(crossed, 'seq', outer_pairs(seq_count, step_level))  13.1 us
    concatenate x4, other arithmetic, body(): jnp.concatenate(p, axis=1).astype(jnp.bfloat16)  5.37 us
    ppermute x2, starting transfers between devices, body(): gathered = lax.ppermute(sends[step_level], 'seq', back)  3.56 us
  transfers between devices with their start and end apart: 17, of which 9 were waited for; matrix products, arithmetic and copies ran while one was open for 19% of the time, Pallas kernels for 14%

profile of v10, /device:TPU:0, one launch (start us, length us, event | category | flops | bytes accessed | tf_op | source)
XLA Modules:
  0.0 174.2 jit_solution(16356472817588452361)
XLA Ops:
  0.7 3.0 %fusion.186 = (bf16[2,64,2048]{2,1,0:T(8,128)(2,1)}, f32[2,64,2048]{2,1,0:T(8,128)S(1)}) fusion(bf16[1,256,2048]{2,1,0:T(8,128)(2,1)} %bitcast.119, bf16[1,256,2048]{2,1,0:T(8,128)(2,1)} %bitcast.120, s32[128,256]{1,0:T(8,128)S(1)} %broadcast_select_fusion.2), kind=kOutput, calls=%fused_computation.241 | convolution fusion | flops 138739712 | bytes 3735552 | tf_op jit(solution)/shard_map/pr,krw->kpw/dot_general | solution.py:132
  3.7 3.0 %collective-permute-start = (bf16[2,64,2048]{2,1,0:T(8,128)(2,1)}, bf16[2,64,2048]{2,1,0:T(8,128)(2,1)}, u32[]{:S(2)}, u32[]{:S(2)}) collective-permute-start(bf16[2,64,2048]{2,1,0:T(8,128)(2,1)} %get-tuple-element.40), channel_id=1, source_target_pairs={{0,4},{4,0},{8,12},{12,8},{16,20},{20,16},{24,28},{28,24},{1,5},{5... | collective-permute-start | bytes 1572872 | tf_op jit(solution)/shard_map/ppermute | solution.py:22
  6.7 1.4 slice_bitcast_fusion.6
  11.5 7.4 %collective-permute-done = bf16[2,64,2048]{2,1,0:T(8,128)(2,1)} collective-permute-done((bf16[2,64,2048]{2,1,0:T(8,128)(2,1)}, bf16[2,64,2048]{2,1,0:T(8,128)(2,1)}, u32[]{:S(2)}, u32[]{:S(2)}) %collective-permute-start) | collective-permute-done | bytes 524320 | tf_op jit(solution)/shard_map/ppermute | solution.py:22
  18.9 1.6 fusion.188
  20.5 1.9 %collective-permute-start.2 = (bf16[2,128,1024]{2,1,0:T(8,128)(2,1)S(1)}, bf16[2,128,1024]{2,1,0:T(8,128)(2,1)S(1)}, u32[]{:S(2)}, u32[]{:S(2)}) collective-permute-start(bf16[2,128,1024]{2,1,0:T(8,128)(2,1)S(1)} %get-tuple-element.44), channel_id=1, source_target_pairs={{0,8},{8,0},{4,12},{12,4},{16,24},{24,16},{20,28},{28,20},{1,9},{9... | collective-permute-start | bytes 1572872 | tf_op jit(solution)/shard_map/ppermute | solution.py:22
  22.4 1.5 collective-permute-start.1
  23.9 1.6 fusion.187
  27.1 8.3 %collective-permute-done.2.refs_2_ = bf16[2,128,1024]{2,1,0:T(8,128)(2,1)S(1)} collective-permute-done((bf16[2,128,1024]{2,1,0:T(8,128)(2,1)S(1)}, bf16[2,128,1024]{2,1,0:T(8,128)(2,1)S(1)}, u32[]{:S(2)}, u32[]{:S(2)}) %collective-permute-start.2) | collective-permute-done | bytes 524320 | tf_op jit(solution)/shard_map/ppermute | solution.py:22
  36.1 1.5 collective-permute-start.3
  38.6 6.3 %collective-permute-done.6.refs_2_ = bf16[2,128,1024]{2,1,0:T(8,128)(2,1)S(1)} collective-permute-done((bf16[2,128,1024]{2,1,0:T(8,128)(2,1)S(1)}, bf16[2,128,1024]{2,1,0:T(8,128)(2,1)S(1)}, u32[]{:S(2)}, u32[]{:S(2)}) %collective-permute-start.6) | collective-permute-done | bytes 524320 | tf_op jit(solution)/shard_map/ppermute | solution.py:22
  47.7 1.5 collective-permute-start.5
  50.5 13.1 %collective-permute-done.4 = bf16[2,128,1024]{2,1,0:T(8,128)(2,1)} collective-permute-done((bf16[2,128,1024]{2,1,0:T(8,128)(2,1)}, bf16[2,128,1024]{2,1,0:T(8,128)(2,1)}, u32[]{:S(2)}, u32[]{:S(2)}) %collective-permute-start.4) | collective-permute-done | bytes 524320 | tf_op jit(solution)/shard_map/ppermute | solution.py:154
  63.6 1.9 %broadcast_select_fusion.1.refs_3_ = bf16[2,128,1024]{2,1,0:T(8,128)(2,1)} fusion(bf16[2,128,1024]{2,1,0:T(8,128)(2,1)} %collective-permute-done.3, bf16[2,128,1024]{2,1,0:T(8,128)(2,1)} %collective-permute-done.4, pred[]{:T(512)S(6)} %ne.113), kind=kLoop, calls=%fused_computation.53 | loop fusion | flops 262144 | bytes 1572865 | tf_op jit(solution)/shard_map/jit(_where)/select_n | solution.py:155
  65.5 12.3 %shard_map.75 = (bf16[256,1024]{1,0:T(8,128)(2,1)}, bf16[256,1024]{1,0:T(8,128)(2,1)}, f32[2,256,1024]{2,1,0:T(8,128)}, f32[2,256,1024]{2,1,0:T(8,128)}, f32[2,1...) custom-call(f32[1,768]{1,0:T(1,128)} %constant.99.clone.1.bias_ref, bf16[256,2048]{1,0:T(8,128)(2,1)} %q_ref.3, ...), custom_call_target="tpu_custom_call" | custom-call | flops 2415919104 | bytes 11534336 | tf_op jit(solution)/shard_map/pallas_call | solution.py:72
  79.2 2.2 %collective-permute-start.9 = (bf16[2,128,1024]{2,1,0:T(8,128)(2,1)S(1)}, bf16[2,128,1024]{2,1,0:T(8,128)(2,1)}, u32[]{:S(2)}, u32[]{:S(2)}) collective-permute-start(bf16[2,128,1024]{2,1,0:T(8,128)(2,1)S(1)} %convert_element_type.79), channel_id=1, source_target_pairs={{0,8},{4,12},{24,16},{28,20},{1,9},{5,13},{25,17},{29,21},{2,10},{... | collective-permute-start | bytes 1572872 | tf_op jit(solution)/shard_map/ppermute | solution.py:180
  82.3 12.4 %shard_map.76 = (bf16[256,1024]{1,0:T(8,128)(2,1)}, bf16[256,1024]{1,0:T(8,128)(2,1)}, f32[2,256,1024]{2,1,0:T(8,128)}, f32[2,256,1024]{2,1,0:T(8,128)}, f32[2,1...) custom-call(f32[1,768]{1,0:T(1,128)} %constant.99.clone.1.bias_ref, bf16[256,2048]{1,0:T(8,128)(2,1)} %q_ref.3, ...), custom_call_target="tpu_custom_call" | custom-call | flops 2415919104 | bytes 11534336 | tf_op jit(solution)/shard_map/pallas_call | solution.py:72
  94.7 1.4 convert_element_type.86
  96.1 1.3 collective-permute-start.13
  97.5 2.2 %pad_maximum_fusion.3 = bf16[256,2048]{1,0:T(8,128)(2,1)} fusion(bf16[256,1024]{1,0:T(8,128)(2,1)} %get-tuple-element.23, bf16[256,1024]{1,0:T(8,128)(2,1)S(1)} %copy-done.17), kind=kLoop, calls=%fused_computation.33 | loop fusion | flops 2097152 | bytes 2097152 | tf_op jit(solution)/shard_map/concatenate | solution.py:198
  102.8 2.4 %collective-permute-done.13 = bf16[2,128,1024]{2,1,0:T(8,128)(2,1)S(1)} collective-permute-done((bf16[2,128,1024]{2,1,0:T(8,128)(2,1)S(1)}, bf16[2,128,1024]{2,1,0:T(8,128)(2,1)S(1)}, u32[]{:S(2)}, u32[]{:S(2)}) %collective-permute-start.13) | collective-permute-done | bytes 524320 | tf_op jit(solution)/shard_map/ppermute | solution.py:180
  107.1 8.7 %collective-permute-start.11 = (bf16[2,128,1024]{2,1,0:T(8,128)(2,1)S(1)}, bf16[2,128,1024]{2,1,0:T(8,128)(2,1)S(1)}, u32[]{:S(2)}, u32[]{:S(2)}) collective-permute-start(bf16[2,128,1024]{2,1,0:T(8,128)(2,1)S(1)} %add_convert_fusion.2), channel_id=1, source_target_pairs={{0,8},{8,0},{4,12},{12,4},{16,24},{24,16},{20,28},{28,20},{1,9},{9... | collective-permute-start | bytes 1572872 | tf_op jit(solution)/shard_map/ppermute | solution.py:22
  116.7 7.2 %collective-permute-start.15 = (bf16[2,128,1024]{2,1,0:T(8,128)(2,1)S(1)}, bf16[2,128,1024]{2,1,0:T(8,128)(2,1)S(1)}, u32[]{:S(2)}, u32[]{:S(2)}) collective-permute-start(bf16[2,128,1024]{2,1,0:T(8,128)(2,1)S(1)} %add_convert_fusion), channel_id=1, source_target_pairs={{0,8},{8,0},{4,12},{12,4},{16,24},{24,16},{20,28},{28,20},{1,9},{9... | collective-permute-start | bytes 1572872 | tf_op jit(solution)/shard_map/ppermute | solution.py:22
  124.8 1.9 %fusion.25 = f32[2,1024,256]{1,2,0:T(8,128)S(1)} fusion(f32[2,128,1024]{2,1,0:T(8,128)S(1)} %fusion.9, s32[128]{0:T(128)S(1)} %iota_subtract_fusion.2, s32[256]{0:T(256)S(1)} %get-tuple-element.48, s32[256]{0:T(256)S(1)} %get-tuple-element.49, pred[256]{0:T(512)(128)(4,1)S(1)} %compare_and_fusion.1), kind=kOutput, calls=%fused_computation.58 | convolution fusion | flops 805404672 | bytes 3148544 | tf_op jit(solution)/shard_map/pr,krw->kpw/dot_general | solution.py:109
  127.2 1.6 collective-permute-start.12
  128.9 5.3 %collective-permute-done.15 = bf16[2,128,1024]{2,1,0:T(8,128)(2,1)S(1)} collective-permute-done((bf16[2,128,1024]{2,1,0:T(8,128)(2,1)S(1)}, bf16[2,128,1024]{2,1,0:T(8,128)(2,1)S(1)}, u32[]{:S(2)}, u32[]{:S(2)}) %collective-permute-start.15) | collective-permute-done | bytes 524320 | tf_op jit(solution)/shard_map/ppermute | solution.py:22
  134.9 1.9 %fusion.23 = f32[2,1024,256]{1,2,0:T(8,128)S(1)} fusion(f32[2,128,1024]{2,1,0:T(8,128)S(1)} %fusion.10, s32[128]{0:T(128)S(1)} %iota_subtract_fusion.2, s32[256]{0:T(256)S(1)} %get-tuple-element.48, s32[256]{0:T(256)S(1)} %get-tuple-element.49, pred[256]{0:T(512)(128)(4,1)S(1)} %compare_and_fusion.1), kind=kOutput, calls=%fused_computation.56 | convolution fusion | flops 805404672 | bytes 3148544 | tf_op jit(solution)/shard_map/pr,krw->kpw/dot_general | solution.py:109
  137.3 1.6 collective-permute-start.16
  139.0 1.9 %fusion.31 = f32[2,1024,256]{1,2,0:T(8,128)S(1)} fusion(f32[2,128,1024]{2,1,0:T(8,128)S(1)} %fusion.9, s32[128]{0:T(128)S(1)} %iota_subtract_fusion.3, s32[256]{0:T(256)S(1)} %get-tuple-element.48, s32[256]{0:T(256)S(1)} %get-tuple-element.49, pred[256]{0:T(512)(128)(4,1)S(1)} %compare_and_fusion.1), kind=kOutput, calls=%fused_computation.64 | convolution fusion | flops 805404672 | bytes 3148544 | tf_op jit(solution)/shard_map/pr,krw->kpw/dot_general | solution.py:109
  140.9 1.9 %fusion.29 = f32[2,1024,256]{1,2,0:T(8,128)S(1)} fusion(f32[2,128,1024]{2,1,0:T(8,128)S(1)} %fusion.10, s32[128]{0:T(128)S(1)} %iota_subtract_fusion.3, s32[256]{0:T(256)S(1)} %get-tuple-element.48, s32[256]{0:T(256)S(1)} %get-tuple-element.49, pred[256]{0:T(512)(128)(4,1)S(1)} %compare_and_fusion.1), kind=kOutput, calls=%fused_computation.62 | convolution fusion | flops 805404672 | bytes 3148544 | tf_op jit(solution)/shard_map/pr,krw->kpw/dot_general | solution.py:109
  142.8 10.6 %collective-permute-done.12 = bf16[2,256,1024]{2,1,0:T(8,128)(2,1)S(1)} collective-permute-done((bf16[2,256,1024]{2,1,0:T(8,128)(2,1)S(1)}, bf16[2,256,1024]{2,1,0:T(8,128)(2,1)S(1)}, u32[]{:S(2)}, u32[]{:S(2)}) %collective-permute-start.12) | collective-permute-done | bytes 1048608 | tf_op jit(solution)/shard_map/ppermute | solution.py:22
  154.1 17.3 %collective-permute-done.16 = bf16[2,256,1024]{2,1,0:T(8,128)(2,1)S(1)} collective-permute-done((bf16[2,256,1024]{2,1,0:T(8,128)(2,1)S(1)}, bf16[2,256,1024]{2,1,0:T(8,128)(2,1)S(1)}, u32[]{:S(2)}, u32[]{:S(2)}) %collective-permute-start.16) | collective-permute-done | bytes 1048608 | tf_op jit(solution)/shard_map/ppermute | solution.py:22
  (89 shorter events, 24.9 us)
Async XLA Ops:
  0.6 6.1 %copy-start.1 = (bf16[256,2048]{1,0:T(8,128)(2,1)S(1)}, bf16[256,2048]{1,0:T(8,128)(2,1)}, u32[]{:S(2)}) copy-start(bf16[256,2048]{1,0:T(8,128)(2,1)} %param.5) | copy-start | bytes 3145732
  0.6 6.1 %copy-start = (bf16[256,2048]{1,0:T(8,128)(2,1)S(1)}, bf16[256,2048]{1,0:T(8,128)(2,1)}, u32[]{:S(2)}) copy-start(bf16[256,2048]{1,0:T(8,128)(2,1)} %param.6) | copy-start | bytes 3145732
  3.7 15.2 %collective-permute-start = (bf16[2,64,2048]{2,1,0:T(8,128)(2,1)}, bf16[2,64,2048]{2,1,0:T(8,128)(2,1)}, u32[]{:S(2)}, u32[]{:S(2)}) collective-permute-start(bf16[2,64,2048]{2,1,0:T(8,128)(2,1)} %get-tuple-element.40), channel_id=1, source_target_pairs={{0,4},{4,0},{8,12},{12,8},{16,20},{20,16},{24,28},{28,24},{1,5},{5... | collective-permute-start | bytes 1572872 | tf_op jit(solution)/shard_map/ppermute | solution.py:22
  9.4 13.0 %copy-start.10 = (bf16[2,256,1024]{2,1,0:T(8,128)(2,1)}, bf16[2,256,1024]{2,1,0:T(8,128)(2,1)S(1)}, u32[]{:S(2)}) copy-start(bf16[2,256,1024]{2,1,0:T(8,128)(2,1)S(1)} %pad_maximum_fusion.refs_0_) | copy-start | bytes 3145732
  20.5 14.9 %collective-permute-start.2 = (bf16[2,128,1024]{2,1,0:T(8,128)(2,1)S(1)}, bf16[2,128,1024]{2,1,0:T(8,128)(2,1)S(1)}, u32[]{:S(2)}, u32[]{:S(2)}) collective-permute-start(bf16[2,128,1024]{2,1,0:T(8,128)(2,1)S(1)} %get-tuple-element.44), channel_id=1, source_target_pairs={{0,8},{8,0},{4,12},{12,4},{16,24},{24,16},{20,28},{28,20},{1,9},{9... | collective-permute-start | bytes 1572872 | tf_op jit(solution)/shard_map/ppermute | solution.py:22
  22.4 43.2 %collective-permute-start.1 = (bf16[2,256,1024]{2,1,0:T(8,128)(2,1)S(1)}, bf16[2,256,1024]{2,1,0:T(8,128)(2,1)}, u32[]{:S(2)}, u32[]{:S(2)}) collective-permute-start(bf16[2,256,1024]{2,1,0:T(8,128)(2,1)S(1)} %pad_maximum_fusion.refs_0_), channel_id=1, source_target_pairs={{0,4},{4,0},{8,12},{12,8},{16,20},{20,16},{24,28},{28,24},{1,5},{5... | collective-permute-start | bytes 3145736 | tf_op jit(solution)/shard_map/ppermute | solution.py:22
  25.5 19.4 %collective-permute-start.6 = (bf16[2,128,1024]{2,1,0:T(8,128)(2,1)S(1)}, bf16[2,128,1024]{2,1,0:T(8,128)(2,1)S(1)}, u32[]{:S(2)}, u32[]{:S(2)}) collective-permute-start(bf16[2,128,1024]{2,1,0:T(8,128)(2,1)S(1)} %get-tuple-element.42), channel_id=1, source_target_pairs={{0,8},{8,0},{4,12},{12,4},{16,24},{24,16},{20,28},{28,20},{1,9},{9... | collective-permute-start | bytes 1572872 | tf_op jit(solution)/shard_map/ppermute | solution.py:22
  36.1 10.2 %collective-permute-start.3 = (bf16[2,128,1024]{2,1,0:T(8,128)(2,1)S(1)}, bf16[2,128,1024]{2,1,0:T(8,128)(2,1)}, u32[]{:S(2)}, u32[]{:S(2)}) collective-permute-start(bf16[2,128,1024]{2,1,0:T(8,128)(2,1)S(1)} %fusion.16), channel_id=1, source_target_pairs={{8,16},{12,20},{16,8},{20,12},{9,17},{13,21},{17,9},{21,13},{10,18... | collective-permute-start | bytes 1572872 | tf_op jit(solution)/shard_map/ppermute | solution.py:153
  37.5 10.0 %copy-start.8 = (bf16[1,256,1024]{2,1,0:T(8,128)(2,1)S(1)}, bf16[1,256,1024]{2,1,0:T(8,128)(2,1)}, u32[]{:S(2)}) copy-start(bf16[1,256,1024]{2,1,0:T(8,128)(2,1)} %get-tuple-element.39) | copy-start | bytes 1572868
  37.5 10.0 %copy-start.9 = (bf16[1,256,1024]{2,1,0:T(8,128)(2,1)S(1)}, bf16[1,256,1024]{2,1,0:T(8,128)(2,1)}, u32[]{:S(2)}) copy-start(bf16[1,256,1024]{2,1,0:T(8,128)(2,1)} %get-tuple-element.46) | copy-start | bytes 1572868
  45.5 3.7 %collective-permute-start.7 = (bf16[2,128,1024]{2,1,0:T(8,128)(2,1)S(1)}, bf16[2,128,1024]{2,1,0:T(8,128)(2,1)S(1)}, u32[]{:S(2)}, u32[]{:S(2)}) collective-permute-start(bf16[2,128,1024]{2,1,0:T(8,128)(2,1)S(1)} %fusion.15), channel_id=1, source_target_pairs={{8,16},{12,20},{16,8},{20,12},{9,17},{13,21},{17,9},{21,13},{10,18... | collective-permute-start | bytes 1572872 | tf_op jit(solution)/shard_map/ppermute | solution.py:153
  46.3 17.4 %collective-permute-start.4 = (bf16[2,128,1024]{2,1,0:T(8,128)(2,1)}, bf16[2,128,1024]{2,1,0:T(8,128)(2,1)}, u32[]{:S(2)}, u32[]{:S(2)}) collective-permute-start(bf16[2,128,1024]{2,1,0:T(8,128)(2,1)} %collective-permute-done.3), channel_id=1, source_target_pairs={{8,0},{12,4},{16,24},{20,28},{9,1},{13,5},{17,25},{21,29},{10,2},{... | collective-permute-start | bytes 1572872 | tf_op jit(solution)/shard_map/ppermute | solution.py:154
  47.7 30.2 %copy-start.11 = (bf16[2,256,1024]{2,1,0:T(8,128)(2,1)}, bf16[2,256,1024]{2,1,0:T(8,128)(2,1)S(1)}, u32[]{:S(2)}) copy-start(bf16[2,256,1024]{2,1,0:T(8,128)(2,1)S(1)} %pad_maximum_fusion.1.refs_0_) | copy-start | bytes 3145732
  47.7 34.6 %collective-permute-start.5 = (bf16[2,256,1024]{2,1,0:T(8,128)(2,1)S(1)}, bf16[2,256,1024]{2,1,0:T(8,128)(2,1)}, u32[]{:S(2)}, u32[]{:S(2)}) collective-permute-start(bf16[2,256,1024]{2,1,0:T(8,128)(2,1)S(1)} %pad_maximum_fusion.1.refs_0_), channel_id=1, source_target_pairs={{0,4},{4,0},{8,12},{12,8},{16,20},{20,16},{24,28},{28,24},{1,5},{5... | collective-permute-start | bytes 3145736 | tf_op jit(solution)/shard_map/ppermute | solution.py:22
  49.2 32.2 %collective-permute-start.8 = (bf16[2,128,1024]{2,1,0:T(8,128)(2,1)S(1)}, bf16[2,128,1024]{2,1,0:T(8,128)(2,1)S(1)}, u32[]{:S(2)}, u32[]{:S(2)}) collective-permute-start(bf16[2,128,1024]{2,1,0:T(8,128)(2,1)S(1)} %collective-permute-done.7), channel_id=1, source_target_pairs={{8,0},{12,4},{16,24},{20,28},{9,1},{13,5},{17,25},{21,29},{10,2},{... | collective-permute-start | bytes 1572872 | tf_op jit(solution)/shard_map/ppermute | solution.py:154
  79.2 20.5 %collective-permute-start.9 = (bf16[2,128,1024]{2,1,0:T(8,128)(2,1)S(1)}, bf16[2,128,1024]{2,1,0:T(8,128)(2,1)}, u32[]{:S(2)}, u32[]{:S(2)}) collective-permute-start(bf16[2,128,1024]{2,1,0:T(8,128)(2,1)S(1)} %convert_element_type.79), channel_id=1, source_target_pairs={{0,8},{4,12},{24,16},{28,20},{1,9},{5,13},{25,17},{29,21},{2,10},{... | collective-permute-start | bytes 1572872 | tf_op jit(solution)/shard_map/ppermute | solution.py:180
  82.3 15.2 %copy-start.17 = (bf16[256,1024]{1,0:T(8,128)(2,1)S(1)}, bf16[256,1024]{1,0:T(8,128)(2,1)}, u32[]{:S(2)}) copy-start(bf16[256,1024]{1,0:T(8,128)(2,1)} %get-tuple-element.22) | copy-start | bytes 1572868
  94.7 5.0 %copy-start.2 = (f32[2,128,1024]{2,1,0:T(8,128)S(1)}, f32[2,128,1024]{2,1,0:T(8,128)}, u32[]{:S(2)}) copy-start(f32[2,128,1024]{2,1,0:T(8,128)} %get-tuple-element.25) | copy-start | bytes 3145732
  96.1 9.0 %collective-permute-start.13 = (bf16[2,128,1024]{2,1,0:T(8,128)(2,1)S(1)}, bf16[2,128,1024]{2,1,0:T(8,128)(2,1)S(1)}, u32[]{:S(2)}, u32[]{:S(2)}) collective-permute-start(bf16[2,128,1024]{2,1,0:T(8,128)(2,1)S(1)} %convert_element_type.86), channel_id=1, source_target_pairs={{0,8},{4,12},{24,16},{28,20},{1,9},{5,13},{25,17},{29,21},{2,10},{... | collective-permute-start | bytes 1572872 | tf_op jit(solution)/shard_map/ppermute | solution.py:180
  97.5 4.2 %copy-start.16 = (bf16[256,1024]{1,0:T(8,128)(2,1)S(1)}, bf16[256,1024]{1,0:T(8,128)(2,1)}, u32[]{:S(2)}) copy-start(bf16[256,1024]{1,0:T(8,128)(2,1)} %get-tuple-element.19) | copy-start | bytes 1572868
  97.5 4.2 %copy-start.18 = (bf16[256,1024]{1,0:T(8,128)(2,1)S(1)}, bf16[256,1024]{1,0:T(8,128)(2,1)}, u32[]{:S(2)}) copy-start(bf16[256,1024]{1,0:T(8,128)(2,1)} %get-tuple-element.21) | copy-start | bytes 1572868
  99.7 5.5 %copy-start.3 = (f32[2,128,1024]{2,1,0:T(8,128)S(1)}, f32[2,128,1024]{2,1,0:T(8,128)}, u32[]{:S(2)}) copy-start(f32[2,128,1024]{2,1,0:T(8,128)} %get-tuple-element.29) | copy-start | bytes 3145732
  101.0 5.2 %collective-permute-start.10 = (bf16[2,128,1024]{2,1,0:T(8,128)(2,1)S(1)}, bf16[2,128,1024]{2,1,0:T(8,128)(2,1)S(1)}, u32[]{:S(2)}, u32[]{:S(2)}) collective-permute-start(bf16[2,128,1024]{2,1,0:T(8,128)(2,1)S(1)} %add_convert_fusion.3), channel_id=1, source_target_pairs={{8,16},{12,20},{16,8},{20,12},{9,17},{13,21},{17,9},{21,13},{10,18... | collective-permute-start | bytes 1572872 | tf_op jit(solution)/shard_map/ppermute | solution.py:182
  102.8 4.1 %copy-start.12 = (f32[2,128,1024]{2,1,0:T(8,128)S(1)}, f32[2,128,1024]{2,1,0:T(8,128)}, u32[]{:S(2)}) copy-start(f32[2,128,1024]{2,1,0:T(8,128)} %get-tuple-element.26) | copy-start | bytes 3145732
  105.3 10.5 %collective-permute-start.14 = (bf16[2,128,1024]{2,1,0:T(8,128)(2,1)S(1)}, bf16[2,128,1024]{2,1,0:T(8,128)(2,1)S(1)}, u32[]{:S(2)}, u32[]{:S(2)}) collective-permute-start(bf16[2,128,1024]{2,1,0:T(8,128)(2,1)S(1)} %add_convert_fusion.1), channel_id=1, source_target_pairs={{8,16},{12,20},{16,8},{20,12},{9,17},{13,21},{17,9},{21,13},{10,18... | collective-permute-start | bytes 1572872 | tf_op jit(solution)/shard_map/ppermute | solution.py:182
  106.9 9.6 %copy-start.13 = (f32[2,128,1024]{2,1,0:T(8,128)S(1)}, f32[2,128,1024]{2,1,0:T(8,128)}, u32[]{:S(2)}) copy-start(f32[2,128,1024]{2,1,0:T(8,128)} %get-tuple-element.30) | copy-start | bytes 3145732
  107.1 16.9 %collective-permute-start.11 = (bf16[2,128,1024]{2,1,0:T(8,128)(2,1)S(1)}, bf16[2,128,1024]{2,1,0:T(8,128)(2,1)S(1)}, u32[]{:S(2)}, u32[]{:S(2)}) collective-permute-start(bf16[2,128,1024]{2,1,0:T(8,128)(2,1)S(1)} %add_convert_fusion.2), channel_id=1, source_target_pairs={{0,8},{8,0},{4,12},{12,4},{16,24},{24,16},{20,28},{28,20},{1,9},{9... | collective-permute-start | bytes 1572872 | tf_op jit(solution)/shard_map/ppermute | solution.py:22
  116.7 17.5 %collective-permute-start.15 = (bf16[2,128,1024]{2,1,0:T(8,128)(2,1)S(1)}, bf16[2,128,1024]{2,1,0:T(8,128)(2,1)S(1)}, u32[]{:S(2)}, u32[]{:S(2)}) collective-permute-start(bf16[2,128,1024]{2,1,0:T(8,128)(2,1)S(1)} %add_convert_fusion), channel_id=1, source_target_pairs={{0,8},{8,0},{4,12},{12,4},{16,24},{24,16},{20,28},{28,20},{1,9},{9... | collective-permute-start | bytes 1572872 | tf_op jit(solution)/shard_map/ppermute | solution.py:22
  127.2 26.2 %collective-permute-start.12 = (bf16[2,256,1024]{2,1,0:T(8,128)(2,1)S(1)}, bf16[2,256,1024]{2,1,0:T(8,128)(2,1)S(1)}, u32[]{:S(2)}, u32[]{:S(2)}) collective-permute-start(bf16[2,256,1024]{2,1,0:T(8,128)(2,1)S(1)} %fusion.6), channel_id=1, source_target_pairs={{0,4},{4,0},{8,12},{12,8},{16,20},{20,16},{24,28},{28,24},{1,5},{5... | collective-permute-start | bytes 3145736 | tf_op jit(solution)/shard_map/ppermute | solution.py:22
  137.3 34.0 %collective-permute-start.16 = (bf16[2,256,1024]{2,1,0:T(8,128)(2,1)S(1)}, bf16[2,256,1024]{2,1,0:T(8,128)(2,1)S(1)}, u32[]{:S(2)}, u32[]{:S(2)}) collective-permute-start(bf16[2,256,1024]{2,1,0:T(8,128)(2,1)S(1)} %fusion.3), channel_id=1, source_target_pairs={{0,4},{4,0},{8,12},{12,8},{16,20},{20,16},{24,28},{28,24},{1,5},{5... | collective-permute-start | bytes 3145736 | tf_op jit(solution)/shard_map/ppermute | solution.py:22
  140.9 12.5 %copy-start.4 = (f32[2,256,1024]{2,1,0:T(8,128)S(1)}, f32[2,256,1024]{2,1,0:T(8,128)}, u32[]{:S(2)}) copy-start(f32[2,256,1024]{2,1,0:T(8,128)} %get-tuple-element.24) | copy-start | bytes 6291460
  154.0 17.4 %copy-start.5 = (f32[2,256,1024]{2,1,0:T(8,128)S(1)}, f32[2,256,1024]{2,1,0:T(8,128)}, u32[]{:S(2)}) copy-start(f32[2,256,1024]{2,1,0:T(8,128)} %get-tuple-element.28) | copy-start | bytes 6291460
  (4 other events, 9.8 us)

commit v11 on v10

--- a/solution.py
+++ b/solution.py
@@ -9,7 +9,7 @@
 
 HEAD_DIM = 128
 POOLED = 128
-CHUNKS = 2
+CHUNKS_MIDDLE = 2
 
 
 def partner_2(block, axis, stride):
@@ -119,7 +119,11 @@
     position = lax.axis_index("seq")
     pool_ratio = leaf_rows // POOLED
     score_scale = HEAD_DIM ** (-0.5)
-    chunk_width = model_width // CHUNKS
+    head_count = model_width // HEAD_DIM
+    edge = max(1, head_count * 3 // 16)
+    middle = (head_count - 2 * edge) // CHUNKS_MIDDLE
+    chunk_heads = [edge] + [middle] * (CHUNKS_MIDDLE - 1) + [head_count - 2 * edge - middle * (CHUNKS_MIDDLE - 1), edge]
+    chunk_first = [sum(chunk_heads[:i]) for i in range(len(chunk_heads))]
     bias_parts = [jnp.zeros((2 * leaf_rows,), jnp.float32)]
     for step_level in range(1, levels):
         bias_parts.append(jnp.full((POOLED,), math.log(pool_ratio * 2**step_level), jnp.float32))
@@ -138,8 +142,8 @@
     place_other = placed_pool(POOLED // 2, 1 - bits[0])
     pieces = [[], [], [], []]
     late = []
-    for chunk in range(CHUNKS):
-        columns = slice(chunk * chunk_width, (chunk + 1) * chunk_width)
+    for chunk in range(len(chunk_heads)):
+        columns = slice(chunk_first[chunk] * HEAD_DIM, (chunk_first[chunk] + chunk_heads[chunk]) * HEAD_DIM)
         own = jnp.stack((key_rows[:, columns], value_rows[:, columns]))
         sibling = partner_2(after(own, sibling_pooled), "seq", 0)
         summary = apply(place_mine, own_pooled[:, :, columns]) + apply(
@@ -163,7 +167,7 @@
             held = after(held, late[chunk - 3][0])
         outs = attention(
             query_rows, out_grad, [held, sibling] + far, key_bias, score_scale,
-            chunk * (chunk_width // HEAD_DIM),
+            chunk_first[chunk],
         )
         attended, query_grad, terms = outs[0], outs[1], outs[2:]
         grad = None

time: 175 us -> 178 us (1.017)
  waiting for transfers between devices: 70.8 us -> 45.1 us
  starting transfers between devices: 37.4 us -> 47.5 us
  matrix products: 22.1 us -> 29.1 us
  Pallas kernels: 24.8 us -> 28.5 us
  local copies, waits for them, and re-layouts: 1.59 us -> 4.81 us
  other arithmetic: 16.3 us -> 19.1 us
    ppermute x9 -> x17, waiting for transfers between devices: 55.3 us -> 30.3 us  [partner_2(): return lax.ppermute(block, axis, route)]
    ppermute x2 -> x4, starting transfers between devices: 3.56 us -> 17.4 us  [body(): gathered = lax.ppermute(sends[step_level], 'seq', back)]
    ppermute x9 -> x17, starting transfers between devices: 27.5 us -> 17.7 us  [partner_2(): return lax.ppermute(block, axis, route)]
    dot_general x16 -> x32, matrix products: 19.1 us -> 26.1 us  [apply(): jnp.einsum('pr,krw->kpw', matrix, rows.astype(jnp.float32), precision=lax...]
    pallas_call x2 -> x4, Pallas kernels: 24.8 us -> 28.5 us  [attention(): pl.pallas_call(functools.partial(attention_kernel, scale=score_scale, par...]
    another operation x2 -> x4, other arithmetic: 1.4 us -> 4.6 us  [body(): own = jnp.stack((key_rows[:, columns], value_rows[:, columns]))]
    unnamed x38 -> x76, local copies, waits for them, and re-layouts: 0.09 us -> 2.72 us
    ppermute x2 -> x4, starting transfers between devices: 2.57 us -> 5.13 us  [body(): passed = lax.ppermute(crossed, 'seq', outer_pairs(seq_count, step_level))]
  transfers between devices with their start and end apart: 17 -> 33, of which waited for: 9 -> 12; matrix products, arithmetic and copies ran while one was open for 19% -> 25% of each run, Pallas kernels for 14% -> 16%
where the time goes in v11:
time: 178 us; the launch traced here: 176 us
  starting transfers between devices  47.5 us (27%)
  waiting for transfers between devices  45.1 us (25%)
  matrix products  29.1 us (16%)
  Pallas kernels  28.5 us (16%)
  other arithmetic  19.1 us (11%)
  local copies, waits for them, and re-layouts  4.81 us (3%)
    ppermute x17, waiting for transfers between devices, partner_2(): return lax.ppermute(block, axis, route)  30.3 us
    pallas_call x4, Pallas kernels, attention(): pl.pallas_call(functools.partial(attention_kernel, scale=score_scale, par...  28.5 us
    dot_general x32, matrix products, apply(): jnp.einsum('pr,krw->kpw', matrix, rows.astype(jnp.float32), precision=lax...  26.1 us
    ppermute x17, starting transfers between devices, partner_2(): return lax.ppermute(block, axis, route)  17.7 us
    ppermute x4, starting transfers between devices, body(): gathered = lax.ppermute(sends[step_level], 'seq', back)  17.4 us
    ppermute x4, waiting for transfers between devices, body(): passed = lax.ppermute(crossed, 'seq', outer_pairs(seq_count, step_level))  11.8 us
    concatenate x4, other arithmetic, body(): jnp.concatenate(p, axis=1).astype(jnp.bfloat16)  5.37 us
    ppermute x4, starting transfers between devices, body(): passed = lax.ppermute(crossed, 'seq', outer_pairs(seq_count, step_level))  5.13 us
  transfers between devices with their start and end apart: 33, of which 12 were waited for; matrix products, arithmetic and copies ran while one was open for 25% of the time, Pallas kernels for 16%

profile of v11, /device:TPU:0, one launch (start us, length us, event | category | flops | bytes accessed | tf_op | source)
XLA Modules:
  0.0 175.8 jit_solution(2057992405527489685)
XLA Ops:
  0.7 3.0 %fusion.340 = (bf16[2,64,2048]{2,1,0:T(8,128)(2,1)}, f32[2,64,2048]{2,1,0:T(8,128)S(1)}) fusion(bf16[1,256,2048]{2,1,0:T(8,128)(2,1)} %bitcast.199, bf16[1,256,2048]{2,1,0:T(8,128)(2,1)} %bitcast.200, s32[128,256]{1,0:T(8,128)S(1)} %broadcast_select_fusion.4), kind=kOutput, calls=%fused_computation.431 | convolution fusion | flops 138739712 | bytes 3735552 | tf_op jit(solution)/shard_map/pr,krw->kpw/dot_general | solution.py:136
  3.7 3.0 %collective-permute-start = (bf16[2,64,2048]{2,1,0:T(8,128)(2,1)}, bf16[2,64,2048]{2,1,0:T(8,128)(2,1)}, u32[]{:S(2)}, u32[]{:S(2)}) collective-permute-start(bf16[2,64,2048]{2,1,0:T(8,128)(2,1)} %get-tuple-element.82), channel_id=1, source_target_pairs={{0,4},{4,0},{8,12},{12,8},{16,20},{20,16},{24,28},{28,24},{1,5},{5... | collective-permute-start | bytes 1572872 | tf_op jit(solution)/shard_map/ppermute | solution.py:22
  9.7 1.9 %pad_maximum_fusion.6.refs_0_ = bf16[2,256,384]{2,1,0:T(8,128)(2,1)} fusion(bf16[1,256,384]{2,1,0:T(8,128)(2,1)} %get-tuple-element.72, bf16[1,256,384]{2,1,0:T(8,128)(2,1)} %get-tuple-element.93), kind=kLoop, calls=%fused_computation.62 | loop fusion | flops 196608 | bytes 786432 | tf_op jit(solution)/shard_map/stack | solution.py:147
  11.6 1.7 pad_maximum_fusion.7.refs_0_
  15.8 3.0 %collective-permute-done = bf16[2,64,2048]{2,1,0:T(8,128)(2,1)} collective-permute-done((bf16[2,64,2048]{2,1,0:T(8,128)(2,1)}, bf16[2,64,2048]{2,1,0:T(8,128)(2,1)}, u32[]{:S(2)}, u32[]{:S(2)}) %collective-permute-start) | collective-permute-done | bytes 524320 | tf_op jit(solution)/shard_map/ppermute | solution.py:22
  20.1 1.9 %collective-permute-start.2 = (bf16[2,128,384]{2,1,0:T(8,128)(2,1)S(1)}, bf16[2,128,384]{2,1,0:T(8,128)(2,1)S(1)}, u32[]{:S(2)}, u32[]{:S(2)}) collective-permute-start(bf16[2,128,384]{2,1,0:T(8,128)(2,1)S(1)} %get-tuple-element.86), channel_id=1, source_target_pairs={{0,8},{8,0},{4,12},{12,4},{16,24},{24,16},{20,28},{28,20},{1,9},{9... | collective-permute-start | bytes 589832 | tf_op jit(solution)/shard_map/ppermute | solution.py:22
  23.6 1.7 collective-permute-start.1
  27.0 1.9 %collective-permute-start.6 = (bf16[2,128,640]{2,1,0:T(8,128)(2,1)S(1)}, bf16[2,128,640]{2,1,0:T(8,128)(2,1)S(1)}, u32[]{:S(2)}, u32[]{:S(2)}) collective-permute-start(bf16[2,128,640]{2,1,0:T(8,128)(2,1)S(1)} %get-tuple-element.84), channel_id=1, source_target_pairs={{0,8},{8,0},{4,12},{12,4},{16,24},{24,16},{20,28},{28,20},{1,9},{9... | collective-permute-start | bytes 983048 | tf_op jit(solution)/shard_map/ppermute | solution.py:22
  30.1 1.4 fusion.344
  35.5 3.7 %collective-permute-done.6.refs_2_ = bf16[2,128,640]{2,1,0:T(8,128)(2,1)S(1)} collective-permute-done((bf16[2,128,640]{2,1,0:T(8,128)(2,1)S(1)}, bf16[2,128,640]{2,1,0:T(8,128)(2,1)S(1)}, u32[]{:S(2)}, u32[]{:S(2)}) %collective-permute-start.6) | collective-permute-done | bytes 327712 | tf_op jit(solution)/shard_map/ppermute | solution.py:22
  41.1 3.4 %collective-permute-done.12.refs_2_ = bf16[2,128,640]{2,1,0:T(8,128)(2,1)S(1)} collective-permute-done((bf16[2,128,640]{2,1,0:T(8,128)(2,1)S(1)}, bf16[2,128,640]{2,1,0:T(8,128)(2,1)S(1)}, u32[]{:S(2)}, u32[]{:S(2)}) %collective-permute-start.12) | collective-permute-done | bytes 327712 | tf_op jit(solution)/shard_map/ppermute | solution.py:22
  44.6 1.4 collective-permute-start.7
  48.5 1.4 collective-permute-start.13
  49.9 4.5 %collective-permute-done.4 = bf16[2,128,384]{2,1,0:T(8,128)(2,1)S(1)} collective-permute-done((bf16[2,128,384]{2,1,0:T(8,128)(2,1)S(1)}, bf16[2,128,384]{2,1,0:T(8,128)(2,1)S(1)}, u32[]{:S(2)}, u32[]{:S(2)}) %collective-permute-start.4) | collective-permute-done | bytes 196640 | tf_op jit(solution)/shard_map/ppermute | solution.py:158
  57.2 1.5 collective-permute-start.5
  58.7 5.8 %shard_map.75 = (bf16[256,384]{1,0:T(8,128)(2,1)}, bf16[256,384]{1,0:T(8,128)(2,1)}, f32[2,256,384]{2,1,0:T(8,128)}, f32[2,256,384]{2,1,0:T(8,128)}, f32[2,128,384]{2,1,0:T(8,128)}, /*index=5*/f32[2,128,384]{2,1,0:T(8,128)}) custom-call(f32[1,768]{1,0:T(1,128)} %constant.99.clone.1.bias_ref, bf16[256,2048]{1,0:T(8,128)(2,1)} %q_ref.7, ...), custom_call_target="tpu_custom_call" | custom-call | flops 905969664 | bytes 4325376 | tf_op jit(solution)/shard_map/pallas_call | solution.py:72
  65.6 4.6 %collective-permute-start.9 = (bf16[2,128,384]{2,1,0:T(8,128)(2,1)S(1)}, bf16[2,128,384]{2,1,0:T(8,128)(2,1)S(1)}, u32[]{:S(2)}, u32[]{:S(2)}) collective-permute-start(bf16[2,128,384]{2,1,0:T(8,128)(2,1)S(1)} %convert_element_type.145), channel_id=1, source_target_pairs={{0,8},{4,12},{24,16},{28,20},{1,9},{5,13},{25,17},{29,21},{2,10},{... | collective-permute-start | bytes 589832 | tf_op jit(solution)/shard_map/ppermute | solution.py:184
  74.7 7.2 %collective-permute-done.8 = bf16[2,128,640]{2,1,0:T(8,128)(2,1)S(1)} collective-permute-done((bf16[2,128,640]{2,1,0:T(8,128)(2,1)}, bf16[2,128,640]{2,1,0:T(8,128)(2,1)S(1)}, u32[]{:S(2)}, u32[]{:S(2)}) %collective-permute-start.8) | collective-permute-done | bytes 327712 | tf_op jit(solution)/shard_map/ppermute | solution.py:158
  83.6 8.5 %shard_map.76 = (bf16[256,640]{1,0:T(8,128)(2,1)}, bf16[256,640]{1,0:T(8,128)(2,1)}, f32[2,256,640]{2,1,0:T(8,128)}, f32[2,256,640]{2,1,0:T(8,128)}, f32[2,128,640]{2,1,0:T(8,128)}, /*index=5*/f32[2,128,640]{2,1,0:T(8,128)}) custom-call(f32[1,768]{1,0:T(1,128)} %constant.99.clone.1.bias_ref, bf16[256,2048]{1,0:T(8,128)(2,1)} %q_ref.7, ...), custom_call_target="tpu_custom_call" | custom-call | flops 1509949440 | bytes 7208960 | tf_op jit(solution)/shard_map/pallas_call | solution.py:72
  93.3 5.0 %collective-permute-start.15 = (bf16[2,128,640]{2,1,0:T(8,128)(2,1)S(1)}, bf16[2,128,640]{2,1,0:T(8,128)(2,1)S(1)}, u32[]{:S(2)}, u32[]{:S(2)}) collective-permute-start(bf16[2,128,640]{2,1,0:T(8,128)(2,1)S(1)} %convert_element_type.152), channel_id=1, source_target_pairs={{0,8},{4,12},{24,16},{28,20},{1,9},{5,13},{25,17},{29,21},{2,10},{... | collective-permute-start | bytes 983048 | tf_op jit(solution)/shard_map/ppermute | solution.py:184
  99.7 8.5 %shard_map.77 = (bf16[256,640]{1,0:T(8,128)(2,1)}, bf16[256,640]{1,0:T(8,128)(2,1)}, f32[2,256,640]{2,1,0:T(8,128)}, f32[2,256,640]{2,1,0:T(8,128)}, f32[2,128,640]{2,1,0:T(8,128)}, /*index=5*/f32[2,128,640]{2,1,0:T(8,128)}) custom-call(f32[1,768]{1,0:T(1,128)} %constant.99.clone.1.bias_ref, bf16[256,2048]{1,0:T(8,128)(2,1)} %q_ref.7, ...), custom_call_target="tpu_custom_call" | custom-call | flops 1509949440 | bytes 7208960 | tf_op jit(solution)/shard_map/pallas_call | solution.py:72
  109.3 4.9 %collective-permute-start.25 = (bf16[2,128,640]{2,1,0:T(8,128)(2,1)S(1)}, bf16[2,128,640]{2,1,0:T(8,128)(2,1)S(1)}, u32[]{:S(2)}, u32[]{:S(2)}) collective-permute-start(bf16[2,128,640]{2,1,0:T(8,128)(2,1)S(1)} %convert_element_type.165), channel_id=1, source_target_pairs={{0,8},{4,12},{24,16},{28,20},{1,9},{5,13},{25,17},{29,21},{2,10},{... | collective-permute-start | bytes 983048 | tf_op jit(solution)/shard_map/ppermute | solution.py:184
  117.9 2.3 %collective-permute-done.25 = bf16[2,128,640]{2,1,0:T(8,128)(2,1)S(1)} collective-permute-done((bf16[2,128,640]{2,1,0:T(8,128)(2,1)S(1)}, bf16[2,128,640]{2,1,0:T(8,128)(2,1)S(1)}, u32[]{:S(2)}, u32[]{:S(2)}) %collective-permute-start.25) | collective-permute-done | bytes 327712 | tf_op jit(solution)/shard_map/ppermute | solution.py:184
  121.0 3.4 %collective-permute-done.22 = bf16[2,256,384]{2,1,0:T(8,128)(2,1)S(1)} collective-permute-done((bf16[2,256,384]{2,1,0:T(8,128)(2,1)S(1)}, bf16[2,256,384]{2,1,0:T(8,128)(2,1)S(1)}, u32[]{:S(2)}, u32[]{:S(2)}) %collective-permute-start.22) | collective-permute-done | bytes 393248 | tf_op jit(solution)/shard_map/ppermute | solution.py:22
  126.9 5.8 %shard_map.78 = (bf16[256,384]{1,0:T(8,128)(2,1)}, bf16[256,384]{1,0:T(8,128)(2,1)}, f32[2,256,384]{2,1,0:T(8,128)}, f32[2,256,384]{2,1,0:T(8,128)}, f32[2,128,384]{2,1,0:T(8,128)}, /*index=5*/f32[2,128,384]{2,1,0:T(8,128)}) custom-call(f32[1,768]{1,0:T(1,128)} %constant.99.clone.1.bias_ref, bf16[256,2048]{1,0:T(8,128)(2,1)} %q_ref.7, ...), custom_call_target="tpu_custom_call" | custom-call | flops 905969664 | bytes 4325376 | tf_op jit(solution)/shard_map/pallas_call | solution.py:72
  133.9 2.9 %collective-permute-start.29 = (bf16[2,128,384]{2,1,0:T(8,128)(2,1)S(1)}, bf16[2,128,384]{2,1,0:T(8,128)(2,1)S(1)}, u32[]{:S(2)}, u32[]{:S(2)}) collective-permute-start(bf16[2,128,384]{2,1,0:T(8,128)(2,1)S(1)} %convert_element_type.172), channel_id=1, source_target_pairs={{0,8},{4,12},{24,16},{28,20},{1,9},{5,13},{25,17},{29,21},{2,10},{... | collective-permute-start | bytes 589832 | tf_op jit(solution)/shard_map/ppermute | solution.py:184
  136.8 2.0 %pad_maximum_fusion = bf16[256,2048]{1,0:T(8,128)(2,1)} fusion(bf16[256,384]{1,0:T(8,128)(2,1)} %get-tuple-element.50, bf16[256,640]{1,0:T(8,128)(2,1)S(1)} %copy-done.31, bf16[256,640]{1,0:T(8,128)(2,1)S(1)} %copy-done.29, bf16[256,384]{1,0:T(8,128)(2,1)S(1)} %copy-done.33), kind=kLoop, calls=%fused_computation.48 | loop fusion | flops 4194304 | bytes 2097152 | tf_op jit(solution)/shard_map/concatenate | solution.py:202
  145.8 4.0 %collective-permute-done.27 = bf16[2,128,640]{2,1,0:T(8,128)(2,1)S(1)} collective-permute-done((bf16[2,128,640]{2,1,0:T(8,128)(2,1)S(1)}, bf16[2,128,640]{2,1,0:T(8,128)(2,1)S(1)}, u32[]{:S(2)}, u32[]{:S(2)}) %collective-permute-start.27) | collective-permute-done | bytes 327712 | tf_op jit(solution)/shard_map/ppermute | solution.py:22
  155.1 3.6 %collective-permute-done.31 = bf16[2,128,384]{2,1,0:T(8,128)(2,1)S(1)} collective-permute-done((bf16[2,128,384]{2,1,0:T(8,128)(2,1)S(1)}, bf16[2,128,384]{2,1,0:T(8,128)(2,1)S(1)}, u32[]{:S(2)}, u32[]{:S(2)}) %collective-permute-start.31) | collective-permute-done | bytes 196640 | tf_op jit(solution)/shard_map/ppermute | solution.py:22
  160.1 1.6 collective-permute-start.32
  162.6 6.6 %collective-permute-done.28 = bf16[2,256,640]{2,1,0:T(8,128)(2,1)S(1)} collective-permute-done((bf16[2,256,640]{2,1,0:T(8,128)(2,1)S(1)}, bf16[2,256,640]{2,1,0:T(8,128)(2,1)S(1)}, u32[]{:S(2)}, u32[]{:S(2)}) %collective-permute-start.28) | collective-permute-done | bytes 655392 | tf_op jit(solution)/shard_map/ppermute | solution.py:22
  170.8 2.6 %collective-permute-done.32 = bf16[2,256,384]{2,1,0:T(8,128)(2,1)S(1)} collective-permute-done((bf16[2,256,384]{2,1,0:T(8,128)(2,1)S(1)}, bf16[2,256,384]{2,1,0:T(8,128)(2,1)S(1)}, u32[]{:S(2)}, u32[]{:S(2)}) %collective-permute-start.32) | collective-permute-done | bytes 393248 | tf_op jit(solution)/shard_map/ppermute | solution.py:22
  (194 shorter events, 59.4 us)
Async XLA Ops:
  3.7 15.2 %collective-permute-start = (bf16[2,64,2048]{2,1,0:T(8,128)(2,1)}, bf16[2,64,2048]{2,1,0:T(8,128)(2,1)}, u32[]{:S(2)}, u32[]{:S(2)}) collective-permute-start(bf16[2,64,2048]{2,1,0:T(8,128)(2,1)} %get-tuple-element.82), channel_id=1, source_target_pairs={{0,4},{4,0},{8,12},{12,8},{16,20},{20,16},{24,28},{28,24},{1,5},{5... | collective-permute-start | bytes 1572872 | tf_op jit(solution)/shard_map/ppermute | solution.py:22
  20.1 14.3 %collective-permute-start.2 = (bf16[2,128,384]{2,1,0:T(8,128)(2,1)S(1)}, bf16[2,128,384]{2,1,0:T(8,128)(2,1)S(1)}, u32[]{:S(2)}, u32[]{:S(2)}) collective-permute-start(bf16[2,128,384]{2,1,0:T(8,128)(2,1)S(1)} %get-tuple-element.86), channel_id=1, source_target_pairs={{0,8},{8,0},{4,12},{12,4},{16,24},{24,16},{20,28},{28,20},{1,9},{9... | collective-permute-start | bytes 589832 | tf_op jit(solution)/shard_map/ppermute | solution.py:22
  23.3 9.5 %collective-permute-start.19 = (bf16[2,128,384]{2,1,0:T(8,128)(2,1)S(1)}, bf16[2,128,384]{2,1,0:T(8,128)(2,1)S(1)}, u32[]{:S(2)}, u32[]{:S(2)}) collective-permute-start(bf16[2,128,384]{2,1,0:T(8,128)(2,1)S(1)} %get-tuple-element.88), channel_id=1, source_target_pairs={{0,8},{8,0},{4,12},{12,4},{16,24},{24,16},{20,28},{28,20},{1,9},{9... | collective-permute-start | bytes 589832 | tf_op jit(solution)/shard_map/ppermute | solution.py:22
  23.6 32.9 %collective-permute-start.1 = (bf16[2,256,384]{2,1,0:T(8,128)(2,1)S(1)}, bf16[2,256,384]{2,1,0:T(8,128)(2,1)S(1)}, u32[]{:S(2)}, u32[]{:S(2)}) collective-permute-start(bf16[2,256,384]{2,1,0:T(8,128)(2,1)S(1)} %copy-done.23), channel_id=1, source_target_pairs={{0,4},{4,0},{8,12},{12,8},{16,20},{20,16},{24,28},{28,24},{1,5},{5... | collective-permute-start | bytes 1179656 | tf_op jit(solution)/shard_map/ppermute | solution.py:22
  25.3 101.6 %collective-permute-start.18 = (bf16[2,256,384]{2,1,0:T(8,128)(2,1)S(1)}, bf16[2,256,384]{2,1,0:T(8,128)(2,1)}, u32[]{:S(2)}, u32[]{:S(2)}) collective-permute-start(bf16[2,256,384]{2,1,0:T(8,128)(2,1)S(1)} %copy-done.22), channel_id=1, source_target_pairs={{0,4},{4,0},{8,12},{12,8},{16,20},{20,16},{24,28},{28,24},{1,5},{5... | collective-permute-start | bytes 1179656 | tf_op jit(solution)/shard_map/ppermute | solution.py:22
  27.0 12.2 %collective-permute-start.6 = (bf16[2,128,640]{2,1,0:T(8,128)(2,1)S(1)}, bf16[2,128,640]{2,1,0:T(8,128)(2,1)S(1)}, u32[]{:S(2)}, u32[]{:S(2)}) collective-permute-start(bf16[2,128,640]{2,1,0:T(8,128)(2,1)S(1)} %get-tuple-element.84), channel_id=1, source_target_pairs={{0,8},{8,0},{4,12},{12,4},{16,24},{24,16},{20,28},{28,20},{1,9},{9... | collective-permute-start | bytes 983048 | tf_op jit(solution)/shard_map/ppermute | solution.py:22
  32.8 11.8 %collective-permute-start.12 = (bf16[2,128,640]{2,1,0:T(8,128)(2,1)S(1)}, bf16[2,128,640]{2,1,0:T(8,128)(2,1)S(1)}, u32[]{:S(2)}, u32[]{:S(2)}) collective-permute-start(bf16[2,128,640]{2,1,0:T(8,128)(2,1)S(1)} %get-tuple-element.90), channel_id=1, source_target_pairs={{0,8},{8,0},{4,12},{12,4},{16,24},{24,16},{20,28},{28,20},{1,9},{9... | collective-permute-start | bytes 983048 | tf_op jit(solution)/shard_map/ppermute | solution.py:22
  34.5 14.1 %collective-permute-start.20 = (bf16[2,128,384]{2,1,0:T(8,128)(2,1)S(1)}, bf16[2,128,384]{2,1,0:T(8,128)(2,1)S(1)}, u32[]{:S(2)}, u32[]{:S(2)}) collective-permute-start(bf16[2,128,384]{2,1,0:T(8,128)(2,1)S(1)} %fusion.17), channel_id=1, source_target_pairs={{8,16},{12,20},{16,8},{20,12},{9,17},{13,21},{17,9},{21,13},{10,18... | collective-permute-start | bytes 589832 | tf_op jit(solution)/shard_map/ppermute | solution.py:157
  39.2 6.8 %collective-permute-start.3 = (bf16[2,128,384]{2,1,0:T(8,128)(2,1)S(1)}, bf16[2,128,384]{2,1,0:T(8,128)(2,1)S(1)}, u32[]{:S(2)}, u32[]{:S(2)}) collective-permute-start(bf16[2,128,384]{2,1,0:T(8,128)(2,1)S(1)} %fusion.18), channel_id=1, source_target_pairs={{8,16},{12,20},{16,8},{20,12},{9,17},{13,21},{17,9},{21,13},{10,18... | collective-permute-start | bytes 589832 | tf_op jit(solution)/shard_map/ppermute | solution.py:157
  44.6 25.6 %collective-permute-start.7 = (bf16[2,128,640]{2,1,0:T(8,128)(2,1)}, bf16[2,128,640]{2,1,0:T(8,128)(2,1)}, u32[]{:S(2)}, u32[]{:S(2)}) collective-permute-start(bf16[2,128,640]{2,1,0:T(8,128)(2,1)} %fusion.14), channel_id=1, source_target_pairs={{8,16},{12,20},{16,8},{20,12},{9,17},{13,21},{17,9},{21,13},{10,18... | collective-permute-start | bytes 983048 | tf_op jit(solution)/shard_map/ppermute | solution.py:157
  46.0 8.5 %collective-permute-start.4 = (bf16[2,128,384]{2,1,0:T(8,128)(2,1)S(1)}, bf16[2,128,384]{2,1,0:T(8,128)(2,1)S(1)}, u32[]{:S(2)}, u32[]{:S(2)}) collective-permute-start(bf16[2,128,384]{2,1,0:T(8,128)(2,1)S(1)} %collective-permute-done.3), channel_id=1, source_target_pairs={{8,0},{12,4},{16,24},{20,28},{9,1},{13,5},{17,25},{21,29},{10,2},{... | collective-permute-start | bytes 589832 | tf_op jit(solution)/shard_map/ppermute | solution.py:158
  48.5 23.7 %collective-permute-start.13 = (bf16[2,128,640]{2,1,0:T(8,128)(2,1)}, bf16[2,128,640]{2,1,0:T(8,128)(2,1)}, u32[]{:S(2)}, u32[]{:S(2)}) collective-permute-start(bf16[2,128,640]{2,1,0:T(8,128)(2,1)} %fusion.13), channel_id=1, source_target_pairs={{8,16},{12,20},{16,8},{20,12},{9,17},{13,21},{17,9},{21,13},{10,18... | collective-permute-start | bytes 983048 | tf_op jit(solution)/shard_map/ppermute | solution.py:157
  54.5 11.1 %collective-permute-start.21 = (bf16[2,128,384]{2,1,0:T(8,128)(2,1)S(1)}, bf16[2,128,384]{2,1,0:T(8,128)(2,1)S(1)}, u32[]{:S(2)}, u32[]{:S(2)}) collective-permute-start(bf16[2,128,384]{2,1,0:T(8,128)(2,1)S(1)} %collective-permute-done.20), channel_id=1, source_target_pairs={{8,0},{12,4},{16,24},{20,28},{9,1},{13,5},{17,25},{21,29},{10,2},{... | collective-permute-start | bytes 589832 | tf_op jit(solution)/shard_map/ppermute | solution.py:158
  57.2 26.4 %collective-permute-start.5 = (bf16[2,256,640]{2,1,0:T(8,128)(2,1)S(1)}, bf16[2,256,640]{2,1,0:T(8,128)(2,1)}, u32[]{:S(2)}, u32[]{:S(2)}) collective-permute-start(bf16[2,256,640]{2,1,0:T(8,128)(2,1)S(1)} %pad_maximum_fusion.4.refs_0_), channel_id=1, source_target_pairs={{0,4},{4,0},{8,12},{12,8},{16,20},{20,16},{24,28},{28,24},{1,5},{5... | collective-permute-start | bytes 1966088 | tf_op jit(solution)/shard_map/ppermute | solution.py:22
  65.6 7.7 %collective-permute-start.9 = (bf16[2,128,384]{2,1,0:T(8,128)(2,1)S(1)}, bf16[2,128,384]{2,1,0:T(8,128)(2,1)S(1)}, u32[]{:S(2)}, u32[]{:S(2)}) collective-permute-start(bf16[2,128,384]{2,1,0:T(8,128)(2,1)S(1)} %convert_element_type.145), channel_id=1, source_target_pairs={{0,8},{4,12},{24,16},{28,20},{1,9},{5,13},{25,17},{29,21},{2,10},{... | collective-permute-start | bytes 589832 | tf_op jit(solution)/shard_map/ppermute | solution.py:184
  70.2 11.7 %collective-permute-start.8 = (bf16[2,128,640]{2,1,0:T(8,128)(2,1)}, bf16[2,128,640]{2,1,0:T(8,128)(2,1)S(1)}, u32[]{:S(2)}, u32[]{:S(2)}) collective-permute-start(bf16[2,128,640]{2,1,0:T(8,128)(2,1)} %collective-permute-done.7), channel_id=1, source_target_pairs={{8,0},{12,4},{16,24},{20,28},{9,1},{13,5},{17,25},{21,29},{10,2},{... | collective-permute-start | bytes 983048 | tf_op jit(solution)/shard_map/ppermute | solution.py:158
  72.2 27.4 %collective-permute-start.11 = (bf16[2,256,640]{2,1,0:T(8,128)(2,1)S(1)}, bf16[2,256,640]{2,1,0:T(8,128)(2,1)}, u32[]{:S(2)}, u32[]{:S(2)}) collective-permute-start(bf16[2,256,640]{2,1,0:T(8,128)(2,1)S(1)} %copy-done.20), channel_id=1, source_target_pairs={{0,4},{4,0},{8,12},{12,8},{16,20},{20,16},{24,28},{28,24},{1,5},{5... | collective-permute-start | bytes 1966088 | tf_op jit(solution)/shard_map/ppermute | solution.py:22
  73.3 25.5 %collective-permute-start.14 = (bf16[2,128,640]{2,1,0:T(8,128)(2,1)}, bf16[2,128,640]{2,1,0:T(8,128)(2,1)S(1)}, u32[]{:S(2)}, u32[]{:S(2)}) collective-permute-start(bf16[2,128,640]{2,1,0:T(8,128)(2,1)} %collective-permute-done.13), channel_id=1, source_target_pairs={{8,0},{12,4},{16,24},{20,28},{9,1},{13,5},{17,25},{21,29},{10,2},{... | collective-permute-start | bytes 983048 | tf_op jit(solution)/shard_map/ppermute | solution.py:158
  81.9 16.4 %collective-permute-start.10 = (bf16[2,128,384]{2,1,0:T(8,128)(2,1)S(1)}, bf16[2,128,384]{2,1,0:T(8,128)(2,1)S(1)}, u32[]{:S(2)}, u32[]{:S(2)}) collective-permute-start(bf16[2,128,384]{2,1,0:T(8,128)(2,1)S(1)} %add_convert_fusion.15), channel_id=1, source_target_pairs={{8,16},{12,20},{16,8},{20,12},{9,17},{13,21},{17,9},{21,13},{10,18... | collective-permute-start | bytes 589832 | tf_op jit(solution)/shard_map/ppermute | solution.py:186
  93.3 23.9 %collective-permute-start.15 = (bf16[2,128,640]{2,1,0:T(8,128)(2,1)S(1)}, bf16[2,128,640]{2,1,0:T(8,128)(2,1)S(1)}, u32[]{:S(2)}, u32[]{:S(2)}) collective-permute-start(bf16[2,128,640]{2,1,0:T(8,128)(2,1)S(1)} %convert_element_type.152), channel_id=1, source_target_pairs={{0,8},{4,12},{24,16},{28,20},{1,9},{5,13},{25,17},{29,21},{2,10},{... | collective-permute-start | bytes 983048 | tf_op jit(solution)/shard_map/ppermute | solution.py:184
  98.8 15.4 %collective-permute-start.17 = (bf16[2,128,384]{2,1,0:T(8,128)(2,1)S(1)}, bf16[2,128,384]{2,1,0:T(8,128)(2,1)S(1)}, u32[]{:S(2)}, u32[]{:S(2)}) collective-permute-start(bf16[2,128,384]{2,1,0:T(8,128)(2,1)S(1)} %add_convert_fusion.14), channel_id=1, source_target_pairs={{0,8},{8,0},{4,12},{12,4},{16,24},{24,16},{20,28},{28,20},{1,9},{9... | collective-permute-start | bytes 589832 | tf_op jit(solution)/shard_map/ppermute | solution.py:22
  109.3 10.9 %collective-permute-start.25 = (bf16[2,128,640]{2,1,0:T(8,128)(2,1)S(1)}, bf16[2,128,640]{2,1,0:T(8,128)(2,1)S(1)}, u32[]{:S(2)}, u32[]{:S(2)}) collective-permute-start(bf16[2,128,640]{2,1,0:T(8,128)(2,1)S(1)} %convert_element_type.165), channel_id=1, source_target_pairs={{0,8},{4,12},{24,16},{28,20},{1,9},{5,13},{25,17},{29,21},{2,10},{... | collective-permute-start | bytes 983048 | tf_op jit(solution)/shard_map/ppermute | solution.py:184
  116.6 7.8 %collective-permute-start.22 = (bf16[2,256,384]{2,1,0:T(8,128)(2,1)S(1)}, bf16[2,256,384]{2,1,0:T(8,128)(2,1)S(1)}, u32[]{:S(2)}, u32[]{:S(2)}) collective-permute-start(bf16[2,256,384]{2,1,0:T(8,128)(2,1)S(1)} %add_convert_fusion.7), channel_id=1, source_target_pairs={{0,4},{4,0},{8,12},{12,8},{16,20},{20,16},{24,28},{28,24},{1,5},{5... | collective-permute-start | bytes 1179656 | tf_op jit(solution)/shard_map/ppermute | solution.py:22
  117.3 7.4 %collective-permute-start.16 = (bf16[2,128,640]{2,1,0:T(8,128)(2,1)S(1)}, bf16[2,128,640]{2,1,0:T(8,128)(2,1)S(1)}, u32[]{:S(2)}, u32[]{:S(2)}) collective-permute-start(bf16[2,128,640]{2,1,0:T(8,128)(2,1)S(1)} %add_convert_fusion.11), channel_id=1, source_target_pairs={{8,16},{12,20},{16,8},{20,12},{9,17},{13,21},{17,9},{21,13},{10,18... | collective-permute-start | bytes 983048 | tf_op jit(solution)/shard_map/ppermute | solution.py:186
  120.3 19.6 %collective-permute-start.26 = (bf16[2,128,640]{2,1,0:T(8,128)(2,1)S(1)}, bf16[2,128,640]{2,1,0:T(8,128)(2,1)S(1)}, u32[]{:S(2)}, u32[]{:S(2)}) collective-permute-start(bf16[2,128,640]{2,1,0:T(8,128)(2,1)S(1)} %add_convert_fusion.9), channel_id=1, source_target_pairs={{8,16},{12,20},{16,8},{20,12},{9,17},{13,21},{17,9},{21,13},{10,18... | collective-permute-start | bytes 983048 | tf_op jit(solution)/shard_map/ppermute | solution.py:186
  125.8 16.1 %collective-permute-start.23 = (bf16[2,128,640]{2,1,0:T(8,128)(2,1)S(1)}, bf16[2,128,640]{2,1,0:T(8,128)(2,1)S(1)}, u32[]{:S(2)}, u32[]{:S(2)}) collective-permute-start(bf16[2,128,640]{2,1,0:T(8,128)(2,1)S(1)} %add_convert_fusion.10), channel_id=1, source_target_pairs={{0,8},{8,0},{4,12},{12,4},{16,24},{24,16},{20,28},{28,20},{1,9},{9... | collective-permute-start | bytes 983048 | tf_op jit(solution)/shard_map/ppermute | solution.py:22
  133.9 6.8 %collective-permute-start.29 = (bf16[2,128,384]{2,1,0:T(8,128)(2,1)S(1)}, bf16[2,128,384]{2,1,0:T(8,128)(2,1)S(1)}, u32[]{:S(2)}, u32[]{:S(2)}) collective-permute-start(bf16[2,128,384]{2,1,0:T(8,128)(2,1)S(1)} %convert_element_type.172), channel_id=1, source_target_pairs={{0,8},{4,12},{24,16},{28,20},{1,9},{5,13},{25,17},{29,21},{2,10},{... | collective-permute-start | bytes 589832 | tf_op jit(solution)/shard_map/ppermute | solution.py:184
  140.6 9.2 %collective-permute-start.27 = (bf16[2,128,640]{2,1,0:T(8,128)(2,1)S(1)}, bf16[2,128,640]{2,1,0:T(8,128)(2,1)S(1)}, u32[]{:S(2)}, u32[]{:S(2)}) collective-permute-start(bf16[2,128,640]{2,1,0:T(8,128)(2,1)S(1)} %add_convert_fusion.8), channel_id=1, source_target_pairs={{0,8},{8,0},{4,12},{12,4},{16,24},{24,16},{20,28},{28,20},{1,9},{9... | collective-permute-start | bytes 983048 | tf_op jit(solution)/shard_map/ppermute | solution.py:22
  141.0 11.4 %collective-permute-start.30 = (bf16[2,128,384]{2,1,0:T(8,128)(2,1)S(1)}, bf16[2,128,384]{2,1,0:T(8,128)(2,1)S(1)}, u32[]{:S(2)}, u32[]{:S(2)}) collective-permute-start(bf16[2,128,384]{2,1,0:T(8,128)(2,1)S(1)} %add_convert_fusion.13), channel_id=1, source_target_pairs={{8,16},{12,20},{16,8},{20,12},{9,17},{13,21},{17,9},{21,13},{10,18... | collective-permute-start | bytes 589832 | tf_op jit(solution)/shard_map/ppermute | solution.py:186
  144.0 25.5 %collective-permute-start.24 = (bf16[2,256,640]{2,1,0:T(8,128)(2,1)S(1)}, bf16[2,256,640]{2,1,0:T(8,128)(2,1)S(1)}, u32[]{:S(2)}, u32[]{:S(2)}) collective-permute-start(bf16[2,256,640]{2,1,0:T(8,128)(2,1)S(1)} %add_convert_fusion.3), channel_id=1, source_target_pairs={{0,4},{4,0},{8,12},{12,8},{16,20},{20,16},{24,28},{28,24},{1,5},{5... | collective-permute-start | bytes 1966088 | tf_op jit(solution)/shard_map/ppermute | solution.py:22
  151.9 17.3 %collective-permute-start.28 = (bf16[2,256,640]{2,1,0:T(8,128)(2,1)S(1)}, bf16[2,256,640]{2,1,0:T(8,128)(2,1)S(1)}, u32[]{:S(2)}, u32[]{:S(2)}) collective-permute-start(bf16[2,256,640]{2,1,0:T(8,128)(2,1)S(1)} %add_convert_fusion.1), channel_id=1, source_target_pairs={{0,4},{4,0},{8,12},{12,8},{16,20},{20,16},{24,28},{28,24},{1,5},{5... | collective-permute-start | bytes 1966088 | tf_op jit(solution)/shard_map/ppermute | solution.py:22
  160.1 13.3 %collective-permute-start.32 = (bf16[2,256,384]{2,1,0:T(8,128)(2,1)S(1)}, bf16[2,256,384]{2,1,0:T(8,128)(2,1)S(1)}, u32[]{:S(2)}, u32[]{:S(2)}) collective-permute-start(bf16[2,256,384]{2,1,0:T(8,128)(2,1)S(1)} %add_convert_fusion.5), channel_id=1, source_target_pairs={{0,4},{4,0},{8,12},{12,8},{16,20},{20,16},{24,28},{28,24},{1,5},{5... | collective-permute-start | bytes 1179656 | tf_op jit(solution)/shard_map/ppermute | solution.py:22
  (39 other events, 283.7 us)

commit v12 on v9

--- a/solution.py
+++ b/solution.py
@@ -134,6 +134,12 @@
         preferred_element_type=jnp.float32,
     )
     sibling_pooled = partner_2(own_pooled.astype(jnp.bfloat16), "seq", 0)
+    pick_row = lax.broadcasted_iota(jnp.int32, (POOLED // 2, POOLED), 0)
+    pick_col = lax.broadcasted_iota(jnp.int32, (POOLED // 2, POOLED), 1)
+    pick_other = jnp.where(
+        pick_col == pick_row + (1 - bits[0]) * (POOLED // 2), 1.0, 0.0
+    ).astype(jnp.float32)
+    spread_own = pool_own.T
     place_mine = placed_pool(POOLED // 2, bits[0])
     place_other = placed_pool(POOLED // 2, 1 - bits[0])
     pieces = [[], [], [], []]
@@ -184,14 +190,14 @@
                 grad = returned.astype(jnp.float32)
             else:
                 grad = apply(mine[step_level].T, grad) + returned
-        to_sibling = terms[1]
         own_total = terms[0]
-        if grad is not None:
-            to_sibling = to_sibling + apply(other[0].T, grad)
-            own_total = own_total + apply(mine[0].T, grad)
-        sibling_send = to_sibling.astype(jnp.bfloat16)
+        sibling_send = terms[1].astype(jnp.bfloat16)
         late.append((sibling_send, sends.get(1, sibling_send)))
         from_sibling = partner_2(sibling_send, "seq", 0)
+        if grad is not None:
+            own_total = own_total + apply(mine[0].T, grad)
+            pooled_back = partner_2(apply(pick_other, grad).astype(jnp.bfloat16), "seq", 0)
+            own_total = own_total + apply(spread_own, pooled_back)
         totals = own_total + from_sibling.astype(jnp.float32)
         for slot, piece in enumerate((attended, query_grad, totals[0], totals[1])):
             pieces[slot].append(piece)

time: 175 us -> 194 us (1.11)
  waiting for transfers between devices: 31.1 us -> 41.7 us
  other arithmetic: 20.9 us -> 24.5 us
  starting transfers between devices: 57.6 us -> 59.7 us
    ppermute x17 -> x21, waiting for transfers between devices: 22.7 us -> 33.9 us  [partner_2(): return lax.ppermute(block, axis, route)]
    dot_general x32 -> x36, matrix products: 27.5 us -> 28.6 us  [apply(): jnp.einsum('pr,krw->kpw', matrix, rows.astype(jnp.float32), precision=lax...]
    ppermute x17 -> x21, starting transfers between devices: 34.6 us -> 35.3 us  [partner_2(): return lax.ppermute(block, axis, route)]
  transfers between devices with their start and end apart: 33 -> 37, of which waited for: 10 -> 11; matrix products, arithmetic and copies ran while one was open for 26% -> 26% of each run, Pallas kernels for 16% -> 15%
where the time goes in v12:
time: 194 us; the launch traced here: 193 us
  starting transfers between devices  59.7 us (31%)
  waiting for transfers between devices  41.7 us (21%)
  matrix products  31.5 us (16%)
  Pallas kernels  28.5 us (15%)
  other arithmetic  24.5 us (13%)
  local copies, waits for them, and re-layouts  4.93 us (3%)
    ppermute x21, starting transfers between devices, partner_2(): return lax.ppermute(block, axis, route)  35.3 us
    ppermute x21, waiting for transfers between devices, partner_2(): return lax.ppermute(block, axis, route)  33.9 us
    dot_general x36, matrix products, apply(): jnp.einsum('pr,krw->kpw', matrix, rows.astype(jnp.float32), precision=lax...  28.6 us
    pallas_call x4, Pallas kernels, attention(): pl.pallas_call(functools.partial(attention_kernel, scale=score_scale, par...  28.5 us
    ppermute x4, starting transfers between devices, body(): gathered = lax.ppermute(sends[step_level], 'seq', back)  13.4 us
    ppermute x4, waiting for transfers between devices, body(): passed = lax.ppermute(crossed, 'seq', outer_pairs(seq_count, step_level))  5.63 us
    concatenate x4, other arithmetic, body(): jnp.concatenate(p, axis=1).astype(jnp.bfloat16)  5.42 us
    ppermute x4, starting transfers between devices, body(): passed = lax.ppermute(crossed, 'seq', outer_pairs(seq_count, step_level))  5.13 us
  transfers between devices with their start and end apart: 37, of which 11 were waited for; matrix products, arithmetic and copies ran while one was open for 26% of the time, Pallas kernels for 15%

profile of v12, /device:TPU:0, one launch (start us, length us, event | category | flops | bytes accessed | tf_op | source)
XLA Modules:
  0.0 192.5 jit_solution(14074587852689124992)
XLA Ops:
  0.7 2.9 %fusion.330 = (bf16[2,64,2048]{2,1,0:T(8,128)(2,1)}, f32[2,64,2048]{2,1,0:T(8,128)S(1)}) fusion(bf16[1,256,2048]{2,1,0:T(8,128)(2,1)} %bitcast.217, bf16[1,256,2048]{2,1,0:T(8,128)(2,1)} %bitcast.218, pred[64,256]{1,0:T(32,128)(4,1)S(1)} %slice_compare_fusion), kind=kOutput, calls=%fused_computation.423 | convolution fusion | flops 138706944 | bytes 3686400 | tf_op jit(solution)/shard_map/pr,krw->kpw/dot_general | solution.py:132
  3.6 3.0 %collective-permute-start = (bf16[2,64,2048]{2,1,0:T(8,128)(2,1)}, bf16[2,64,2048]{2,1,0:T(8,128)(2,1)}, u32[]{:S(2)}, u32[]{:S(2)}) collective-permute-start(bf16[2,64,2048]{2,1,0:T(8,128)(2,1)} %get-tuple-element.82), channel_id=1, source_target_pairs={{0,4},{4,0},{8,12},{12,8},{16,20},{20,16},{24,28},{28,24},{1,5},{5... | collective-permute-start | bytes 1572872 | tf_op jit(solution)/shard_map/ppermute | solution.py:22
  15.1 3.8 %collective-permute-done = bf16[2,64,2048]{2,1,0:T(8,128)(2,1)} collective-permute-done((bf16[2,64,2048]{2,1,0:T(8,128)(2,1)}, bf16[2,64,2048]{2,1,0:T(8,128)(2,1)}, u32[]{:S(2)}, u32[]{:S(2)}) %collective-permute-start) | collective-permute-done | bytes 524320 | tf_op jit(solution)/shard_map/ppermute | solution.py:22
  20.2 1.9 collective-permute-start.2
  25.0 1.9 collective-permute-start.12
  30.3 4.8 %collective-permute-done.6.refs_2_ = bf16[2,128,512]{2,1,0:T(8,128)(2,1)S(1)} collective-permute-done((bf16[2,128,512]{2,1,0:T(8,128)(2,1)S(1)}, bf16[2,128,512]{2,1,0:T(8,128)(2,1)S(1)}, u32[]{:S(2)}, u32[]{:S(2)}) %collective-permute-start.6) | collective-permute-done | bytes 262176 | tf_op jit(solution)/shard_map/ppermute | solution.py:22
  36.8 1.8 collective-permute-start.17
  38.7 2.1 %collective-permute-done.12.refs_2_ = bf16[2,128,512]{2,1,0:T(8,128)(2,1)S(1)} collective-permute-done((bf16[2,128,512]{2,1,0:T(8,128)(2,1)S(1)}, bf16[2,128,512]{2,1,0:T(8,128)(2,1)S(1)}, u32[]{:S(2)}, u32[]{:S(2)}) %collective-permute-start.12) | collective-permute-done | bytes 262176 | tf_op jit(solution)/shard_map/ppermute | solution.py:22
  40.7 1.7 collective-permute-start.5
  48.0 5.6 %collective-permute-done.8 = bf16[2,128,512]{2,1,0:T(8,128)(2,1)S(1)} collective-permute-done((bf16[2,128,512]{2,1,0:T(8,128)(2,1)S(1)}, bf16[2,128,512]{2,1,0:T(8,128)(2,1)S(1)}, u32[]{:S(2)}, u32[]{:S(2)}) %collective-permute-start.8) | collective-permute-done | bytes 262176 | tf_op jit(solution)/shard_map/ppermute | solution.py:160
  56.7 6.3 %collective-permute-done.5.refs_1_ = bf16[2,256,512]{2,1,0:T(8,128)(2,1)S(1)} collective-permute-done((bf16[2,256,512]{2,1,0:T(8,128)(2,1)S(1)}, bf16[2,256,512]{2,1,0:T(8,128)(2,1)S(1)}, u32[]{:S(2)}, u32[]{:S(2)}) %collective-permute-start.5) | collective-permute-done | bytes 524320 | tf_op jit(solution)/shard_map/ppermute | solution.py:22
  65.1 7.1 %shard_map.76 = (bf16[256,512]{1,0:T(8,128)(2,1)}, bf16[256,512]{1,0:T(8,128)(2,1)}, f32[2,256,512]{2,1,0:T(8,128)}, f32[2,256,512]{2,1,0:T(8,128)}, f32[2,128,512]{2,1,0:T(8,128)}, /*index=5*/f32[2,128,512]{2,1,0:T(8,128)}) custom-call(f32[1,768]{1,0:T(1,128)} %constant.97.clone.1.bias_ref, bf16[256,2048]{1,0:T(8,128)(2,1)} %q_ref.7, ...), custom_call_target="tpu_custom_call" | custom-call | flops 1207959552 | bytes 5767168 | tf_op jit(solution)/shard_map/pallas_call | solution.py:72
  74.6 1.8 collective-permute-start.11
  77.7 1.7 broadcast_select_fusion.1.refs_3_
  79.5 5.9 %collective-permute-start.15 = (bf16[2,128,512]{2,1,0:T(8,128)(2,1)S(1)}, bf16[2,128,512]{2,1,0:T(8,128)(2,1)S(1)}, u32[]{:S(2)}, u32[]{:S(2)}) collective-permute-start(bf16[2,128,512]{2,1,0:T(8,128)(2,1)S(1)} %convert_element_type.183), channel_id=1, source_target_pairs={{0,8},{4,12},{24,16},{28,20},{1,9},{5,13},{25,17},{29,21},{2,10},{... | collective-permute-start | bytes 786440 | tf_op jit(solution)/shard_map/ppermute | solution.py:186
  85.3 1.7 broadcast_select_fusion.3.refs_3_
  87.1 7.1 %shard_map.75 = (bf16[256,512]{1,0:T(8,128)(2,1)}, bf16[256,512]{1,0:T(8,128)(2,1)}, f32[2,256,512]{2,1,0:T(8,128)}, f32[2,256,512]{2,1,0:T(8,128)}, f32[2,128,512]{2,1,0:T(8,128)}, /*index=5*/f32[2,128,512]{2,1,0:T(8,128)}) custom-call(f32[1,768]{1,0:T(1,128)} %constant.97.clone.1.bias_ref, bf16[256,2048]{1,0:T(8,128)(2,1)} %q_ref.7, ...), custom_call_target="tpu_custom_call" | custom-call | flops 1207959552 | bytes 5767168 | tf_op jit(solution)/shard_map/pallas_call | solution.py:72
  98.6 2.1 %collective-permute-done.9 = bf16[2,128,512]{2,1,0:T(8,128)(2,1)S(1)} collective-permute-done((bf16[2,128,512]{2,1,0:T(8,128)(2,1)S(1)}, bf16[2,128,512]{2,1,0:T(8,128)(2,1)S(1)}, u32[]{:S(2)}, u32[]{:S(2)}) %collective-permute-start.9) | collective-permute-done | bytes 262176 | tf_op jit(solution)/shard_map/ppermute | solution.py:186
  100.6 2.0 %collective-permute-start.23 = (bf16[2,256,512]{2,1,0:T(8,128)(2,1)S(1)}, bf16[2,256,512]{2,1,0:T(8,128)(2,1)}, u32[]{:S(2)}, u32[]{:S(2)}) collective-permute-start(bf16[2,256,512]{2,1,0:T(8,128)(2,1)S(1)} %convert_element_type.187), channel_id=1, source_target_pairs={{0,4},{4,0},{8,12},{12,8},{16,20},{20,16},{24,28},{28,24},{1,5},{5... | collective-permute-start | bytes 1572872 | tf_op jit(solution)/shard_map/ppermute | solution.py:22
  104.0 9.4 %collective-permute-start.24 = (bf16[2,128,512]{2,1,0:T(8,128)(2,1)S(1)}, bf16[2,128,512]{2,1,0:T(8,128)(2,1)}, u32[]{:S(2)}, u32[]{:S(2)}) collective-permute-start(bf16[2,128,512]{2,1,0:T(8,128)(2,1)S(1)} %add_convert_fusion.8), channel_id=1, source_target_pairs={{0,8},{8,0},{4,12},{12,4},{16,24},{24,16},{20,28},{28,20},{1,9},{9... | collective-permute-start | bytes 786440 | tf_op jit(solution)/shard_map/ppermute | solution.py:22
  114.8 7.1 %shard_map.77 = (bf16[256,512]{1,0:T(8,128)(2,1)}, bf16[256,512]{1,0:T(8,128)(2,1)}, f32[2,256,512]{2,1,0:T(8,128)}, f32[2,256,512]{2,1,0:T(8,128)}, f32[2,128,512]{2,1,0:T(8,128)}, /*index=5*/f32[2,128,512]{2,1,0:T(8,128)}) custom-call(f32[1,768]{1,0:T(1,128)} %constant.97.clone.1.bias_ref, bf16[256,2048]{1,0:T(8,128)(2,1)} %q_ref.7, ...), custom_call_target="tpu_custom_call" | custom-call | flops 1207959552 | bytes 5767168 | tf_op jit(solution)/shard_map/pallas_call | solution.py:72
  123.0 4.8 %collective-permute-start.27 = (bf16[2,128,512]{2,1,0:T(8,128)(2,1)S(1)}, bf16[2,128,512]{2,1,0:T(8,128)(2,1)}, u32[]{:S(2)}, u32[]{:S(2)}) collective-permute-start(bf16[2,128,512]{2,1,0:T(8,128)(2,1)S(1)} %convert_element_type.200), channel_id=1, source_target_pairs={{0,8},{4,12},{24,16},{28,20},{1,9},{5,13},{25,17},{29,21},{2,10},{... | collective-permute-start | bytes 786440 | tf_op jit(solution)/shard_map/ppermute | solution.py:186
  127.8 7.1 %shard_map.78 = (bf16[256,512]{1,0:T(8,128)(2,1)}, bf16[256,512]{1,0:T(8,128)(2,1)}, f32[2,256,512]{2,1,0:T(8,128)}, f32[2,256,512]{2,1,0:T(8,128)}, f32[2,128,512]{2,1,0:T(8,128)}, /*index=5*/f32[2,128,512]{2,1,0:T(8,128)}) custom-call(f32[1,768]{1,0:T(1,128)} %constant.97.clone.1.bias_ref, bf16[256,2048]{1,0:T(8,128)(2,1)} %q_ref.7, ...), custom_call_target="tpu_custom_call" | custom-call | flops 1207959552 | bytes 5767168 | tf_op jit(solution)/shard_map/pallas_call | solution.py:72
  134.9 2.1 %pad_maximum_fusion = bf16[256,2048]{1,0:T(8,128)(2,1)} fusion(bf16[256,512]{1,0:T(8,128)(2,1)} %get-tuple-element.50, bf16[256,512]{1,0:T(8,128)(2,1)S(1)} %copy-done.37, bf16[256,512]{1,0:T(8,128)(2,1)S(1)} %copy-done.33, bf16[256,512]{1,0:T(8,128)(2,1)S(1)} %copy-done.35), kind=kLoop, calls=%fused_computation.52 | loop fusion | flops 4194304 | bytes 2097152 | tf_op jit(solution)/shard_map/concatenate | solution.py:204
  145.0 1.4 fusion.7
  152.4 7.5 %collective-permute-done.25 = bf16[2,64,512]{2,1,0:T(8,128)(2,1)S(1)} collective-permute-done((bf16[2,64,512]{2,1,0:T(8,128)(2,1)S(1)}, bf16[2,64,512]{2,1,0:T(8,128)(2,1)S(1)}, u32[]{:S(2)}, u32[]{:S(2)}) %collective-permute-start.25) | collective-permute-done | bytes 131104 | tf_op jit(solution)/shard_map/ppermute | solution.py:22
  160.9 4.0 %collective-permute-done.22 = bf16[2,64,512]{2,1,0:T(8,128)(2,1)S(1)} collective-permute-done((bf16[2,64,512]{2,1,0:T(8,128)(2,1)S(1)}, bf16[2,64,512]{2,1,0:T(8,128)(2,1)S(1)}, u32[]{:S(2)}, u32[]{:S(2)}) %collective-permute-start.22) | collective-permute-done | bytes 131104 | tf_op jit(solution)/shard_map/ppermute | solution.py:22
  167.1 1.6 add_convert_fusion.2
  168.7 1.5 add_convert_fusion.3
  171.4 3.5 %collective-permute-start.29 = (bf16[2,128,512]{2,1,0:T(8,128)(2,1)S(1)}, bf16[2,128,512]{2,1,0:T(8,128)(2,1)S(1)}, u32[]{:S(2)}, u32[]{:S(2)}) collective-permute-start(bf16[2,128,512]{2,1,0:T(8,128)(2,1)S(1)} %add_convert_fusion.6), channel_id=1, source_target_pairs={{0,8},{8,0},{4,12},{12,4},{16,24},{24,16},{20,28},{28,20},{1,9},{9... | collective-permute-start | bytes 786440 | tf_op jit(solution)/shard_map/ppermute | solution.py:22
  176.6 2.7 %collective-permute-done.29 = bf16[2,128,512]{2,1,0:T(8,128)(2,1)S(1)} collective-permute-done((bf16[2,128,512]{2,1,0:T(8,128)(2,1)S(1)}, bf16[2,128,512]{2,1,0:T(8,128)(2,1)S(1)}, u32[]{:S(2)}, u32[]{:S(2)}) %collective-permute-start.29) | collective-permute-done | bytes 262176 | tf_op jit(solution)/shard_map/ppermute | solution.py:22
  186.7 2.5 %collective-permute-done.35 = bf16[2,64,512]{2,1,0:T(8,128)(2,1)S(1)} collective-permute-done((bf16[2,64,512]{2,1,0:T(8,128)(2,1)S(1)}, bf16[2,64,512]{2,1,0:T(8,128)(2,1)S(1)}, u32[]{:S(2)}, u32[]{:S(2)}) %collective-permute-start.35) | collective-permute-done | bytes 131104 | tf_op jit(solution)/shard_map/ppermute | solution.py:22
  (211 shorter events, 70.3 us)
Async XLA Ops:
  3.6 15.2 %collective-permute-start = (bf16[2,64,2048]{2,1,0:T(8,128)(2,1)}, bf16[2,64,2048]{2,1,0:T(8,128)(2,1)}, u32[]{:S(2)}, u32[]{:S(2)}) collective-permute-start(bf16[2,64,2048]{2,1,0:T(8,128)(2,1)} %get-tuple-element.82), channel_id=1, source_target_pairs={{0,4},{4,0},{8,12},{12,8},{16,20},{20,16},{24,28},{28,24},{1,5},{5... | collective-permute-start | bytes 1572872 | tf_op jit(solution)/shard_map/ppermute | solution.py:22
  20.2 22.7 %collective-permute-start.2 = (bf16[2,128,512]{2,1,0:T(8,128)(2,1)S(1)}, bf16[2,128,512]{2,1,0:T(8,128)(2,1)S(1)}, u32[]{:S(2)}, u32[]{:S(2)}) collective-permute-start(bf16[2,128,512]{2,1,0:T(8,128)(2,1)S(1)} %get-tuple-element.86), channel_id=1, source_target_pairs={{0,8},{8,0},{4,12},{12,4},{16,24},{24,16},{20,28},{28,20},{1,9},{9... | collective-permute-start | bytes 786440 | tf_op jit(solution)/shard_map/ppermute | solution.py:22
  23.4 11.7 %collective-permute-start.6 = (bf16[2,128,512]{2,1,0:T(8,128)(2,1)S(1)}, bf16[2,128,512]{2,1,0:T(8,128)(2,1)S(1)}, u32[]{:S(2)}, u32[]{:S(2)}) collective-permute-start(bf16[2,128,512]{2,1,0:T(8,128)(2,1)S(1)} %get-tuple-element.84), channel_id=1, source_target_pairs={{0,8},{8,0},{4,12},{12,4},{16,24},{24,16},{20,28},{28,20},{1,9},{9... | collective-permute-start | bytes 786440 | tf_op jit(solution)/shard_map/ppermute | solution.py:22
  25.0 15.7 %collective-permute-start.12 = (bf16[2,128,512]{2,1,0:T(8,128)(2,1)S(1)}, bf16[2,128,512]{2,1,0:T(8,128)(2,1)S(1)}, u32[]{:S(2)}, u32[]{:S(2)}) collective-permute-start(bf16[2,128,512]{2,1,0:T(8,128)(2,1)S(1)} %get-tuple-element.90), channel_id=1, source_target_pairs={{0,8},{8,0},{4,12},{12,4},{16,24},{24,16},{20,28},{28,20},{1,9},{9... | collective-permute-start | bytes 786440 | tf_op jit(solution)/shard_map/ppermute | solution.py:22
  28.2 17.2 %collective-permute-start.18 = (bf16[2,128,512]{2,1,0:T(8,128)(2,1)S(1)}, bf16[2,128,512]{2,1,0:T(8,128)(2,1)S(1)}, u32[]{:S(2)}, u32[]{:S(2)}) collective-permute-start(bf16[2,128,512]{2,1,0:T(8,128)(2,1)S(1)} %get-tuple-element.88), channel_id=1, source_target_pairs={{0,8},{8,0},{4,12},{12,4},{16,24},{24,16},{20,28},{28,20},{1,9},{9... | collective-permute-start | bytes 786440 | tf_op jit(solution)/shard_map/ppermute | solution.py:22
  35.5 8.1 %collective-permute-start.7 = (bf16[2,128,512]{2,1,0:T(8,128)(2,1)S(1)}, bf16[2,128,512]{2,1,0:T(8,128)(2,1)S(1)}, u32[]{:S(2)}, u32[]{:S(2)}) collective-permute-start(bf16[2,128,512]{2,1,0:T(8,128)(2,1)S(1)} %fusion.17), channel_id=1, source_target_pairs={{8,16},{12,20},{16,8},{20,12},{9,17},{13,21},{17,9},{21,13},{10,18... | collective-permute-start | bytes 786440 | tf_op jit(solution)/shard_map/ppermute | solution.py:159
  36.8 86.2 %collective-permute-start.17 = (bf16[2,256,512]{2,1,0:T(8,128)(2,1)S(1)}, bf16[2,256,512]{2,1,0:T(8,128)(2,1)}, u32[]{:S(2)}, u32[]{:S(2)}) collective-permute-start(bf16[2,256,512]{2,1,0:T(8,128)(2,1)S(1)} %pad_maximum_fusion.7.refs_0_), channel_id=1, source_target_pairs={{0,4},{4,0},{8,12},{12,8},{16,20},{20,16},{24,28},{28,24},{1,5},{5... | collective-permute-start | bytes 1572872 | tf_op jit(solution)/shard_map/ppermute | solution.py:22
  40.7 22.3 %collective-permute-start.5 = (bf16[2,256,512]{2,1,0:T(8,128)(2,1)S(1)}, bf16[2,256,512]{2,1,0:T(8,128)(2,1)S(1)}, u32[]{:S(2)}, u32[]{:S(2)}) collective-permute-start(bf16[2,256,512]{2,1,0:T(8,128)(2,1)S(1)} %copy-done.23), channel_id=1, source_target_pairs={{0,4},{4,0},{8,12},{12,8},{16,20},{20,16},{24,28},{28,24},{1,5},{5... | collective-permute-start | bytes 1572872 | tf_op jit(solution)/shard_map/ppermute | solution.py:22
  43.6 10.0 %collective-permute-start.8 = (bf16[2,128,512]{2,1,0:T(8,128)(2,1)S(1)}, bf16[2,128,512]{2,1,0:T(8,128)(2,1)S(1)}, u32[]{:S(2)}, u32[]{:S(2)}) collective-permute-start(bf16[2,128,512]{2,1,0:T(8,128)(2,1)S(1)} %collective-permute-done.7), channel_id=1, source_target_pairs={{8,0},{12,4},{16,24},{20,28},{9,1},{13,5},{17,25},{21,29},{10,2},{... | collective-permute-start | bytes 786440 | tf_op jit(solution)/shard_map/ppermute | solution.py:160
  45.4 10.3 %collective-permute-start.3 = (bf16[2,128,512]{2,1,0:T(8,128)(2,1)S(1)}, bf16[2,128,512]{2,1,0:T(8,128)(2,1)S(1)}, u32[]{:S(2)}, u32[]{:S(2)}) collective-permute-start(bf16[2,128,512]{2,1,0:T(8,128)(2,1)S(1)} %fusion.18), channel_id=1, source_target_pairs={{8,16},{12,20},{16,8},{20,12},{9,17},{13,21},{17,9},{21,13},{10,18... | collective-permute-start | bytes 786440 | tf_op jit(solution)/shard_map/ppermute | solution.py:159
  47.3 27.3 %collective-permute-start.19 = (bf16[2,128,512]{2,1,0:T(8,128)(2,1)}, bf16[2,128,512]{2,1,0:T(8,128)(2,1)S(1)}, u32[]{:S(2)}, u32[]{:S(2)}) collective-permute-start(bf16[2,128,512]{2,1,0:T(8,128)(2,1)} %fusion.15), channel_id=1, source_target_pairs={{8,16},{12,20},{16,8},{20,12},{9,17},{13,21},{17,9},{21,13},{10,18... | collective-permute-start | bytes 786440 | tf_op jit(solution)/shard_map/ppermute | solution.py:159
  53.6 22.8 %collective-permute-start.14 = (bf16[2,128,512]{2,1,0:T(8,128)(2,1)S(1)}, bf16[2,128,512]{2,1,0:T(8,128)(2,1)}, u32[]{:S(2)}, u32[]{:S(2)}) collective-permute-start(bf16[2,128,512]{2,1,0:T(8,128)(2,1)S(1)} %collective-permute-done.13), channel_id=1, source_target_pairs={{8,0},{12,4},{16,24},{20,28},{9,1},{13,5},{17,25},{21,29},{10,2},{... | collective-permute-start | bytes 786440 | tf_op jit(solution)/shard_map/ppermute | solution.py:160
  55.7 31.4 %collective-permute-start.1 = (bf16[2,256,512]{2,1,0:T(8,128)(2,1)S(1)}, bf16[2,256,512]{2,1,0:T(8,128)(2,1)}, u32[]{:S(2)}, u32[]{:S(2)}) collective-permute-start(bf16[2,256,512]{2,1,0:T(8,128)(2,1)S(1)} %copy-done.22), channel_id=1, source_target_pairs={{0,4},{4,0},{8,12},{12,8},{16,20},{20,16},{24,28},{28,24},{1,5},{5... | collective-permute-start | bytes 1572872 | tf_op jit(solution)/shard_map/ppermute | solution.py:22
  63.8 15.7 %collective-permute-start.4 = (bf16[2,128,512]{2,1,0:T(8,128)(2,1)S(1)}, bf16[2,128,512]{2,1,0:T(8,128)(2,1)}, u32[]{:S(2)}, u32[]{:S(2)}) collective-permute-start(bf16[2,128,512]{2,1,0:T(8,128)(2,1)S(1)} %collective-permute-done.3), channel_id=1, source_target_pairs={{8,0},{12,4},{16,24},{20,28},{9,1},{13,5},{17,25},{21,29},{10,2},{... | collective-permute-start | bytes 786440 | tf_op jit(solution)/shard_map/ppermute | solution.py:160
  74.6 40.1 %collective-permute-start.11 = (bf16[2,256,512]{2,1,0:T(8,128)(2,1)S(1)}, bf16[2,256,512]{2,1,0:T(8,128)(2,1)}, u32[]{:S(2)}, u32[]{:S(2)}) collective-permute-start(bf16[2,256,512]{2,1,0:T(8,128)(2,1)S(1)} %pad_maximum_fusion.6.refs_0_), channel_id=1, source_target_pairs={{0,4},{4,0},{8,12},{12,8},{16,20},{20,16},{24,28},{28,24},{1,5},{5... | collective-permute-start | bytes 1572872 | tf_op jit(solution)/shard_map/ppermute | solution.py:22
  76.5 20.4 %collective-permute-start.20 = (bf16[2,128,512]{2,1,0:T(8,128)(2,1)S(1)}, bf16[2,128,512]{2,1,0:T(8,128)(2,1)S(1)}, u32[]{:S(2)}, u32[]{:S(2)}) collective-permute-start(bf16[2,128,512]{2,1,0:T(8,128)(2,1)S(1)} %collective-permute-done.19), channel_id=1, source_target_pairs={{8,0},{12,4},{16,24},{20,28},{9,1},{13,5},{17,25},{21,29},{10,2},{... | collective-permute-start | bytes 786440 | tf_op jit(solution)/shard_map/ppermute | solution.py:160
  79.5 15.9 %collective-permute-start.15 = (bf16[2,128,512]{2,1,0:T(8,128)(2,1)S(1)}, bf16[2,128,512]{2,1,0:T(8,128)(2,1)S(1)}, u32[]{:S(2)}, u32[]{:S(2)}) collective-permute-start(bf16[2,128,512]{2,1,0:T(8,128)(2,1)S(1)} %convert_element_type.183), channel_id=1, source_target_pairs={{0,8},{4,12},{24,16},{28,20},{1,9},{5,13},{25,17},{29,21},{2,10},{... | collective-permute-start | bytes 786440 | tf_op jit(solution)/shard_map/ppermute | solution.py:186
  87.0 79.1 %collective-permute-start.26 = (bf16[2,256,512]{2,1,0:T(8,128)(2,1)S(1)}, bf16[2,256,512]{2,1,0:T(8,128)(2,1)}, u32[]{:S(2)}, u32[]{:S(2)}) collective-permute-start(bf16[2,256,512]{2,1,0:T(8,128)(2,1)S(1)} %convert_element_type.198), channel_id=1, source_target_pairs={{0,4},{4,0},{8,12},{12,8},{16,20},{20,16},{24,28},{28,24},{1,5},{5... | collective-permute-start | bytes 1572872 | tf_op jit(solution)/shard_map/ppermute | solution.py:22
  96.9 5.8 %collective-permute-start.16 = (bf16[2,128,512]{2,1,0:T(8,128)(2,1)S(1)}, bf16[2,128,512]{2,1,0:T(8,128)(2,1)S(1)}, u32[]{:S(2)}, u32[]{:S(2)}) collective-permute-start(bf16[2,128,512]{2,1,0:T(8,128)(2,1)S(1)} %add_convert_fusion.9), channel_id=1, source_target_pairs={{8,16},{12,20},{16,8},{20,12},{9,17},{13,21},{17,9},{21,13},{10,18... | collective-permute-start | bytes 786440 | tf_op jit(solution)/shard_map/ppermute | solution.py:188
  100.6 68.0 %collective-permute-start.23 = (bf16[2,256,512]{2,1,0:T(8,128)(2,1)S(1)}, bf16[2,256,512]{2,1,0:T(8,128)(2,1)}, u32[]{:S(2)}, u32[]{:S(2)}) collective-permute-start(bf16[2,256,512]{2,1,0:T(8,128)(2,1)S(1)} %convert_element_type.187), channel_id=1, source_target_pairs={{0,4},{4,0},{8,12},{12,8},{16,20},{20,16},{24,28},{28,24},{1,5},{5... | collective-permute-start | bytes 1572872 | tf_op jit(solution)/shard_map/ppermute | solution.py:22
  104.0 36.4 %collective-permute-start.24 = (bf16[2,128,512]{2,1,0:T(8,128)(2,1)S(1)}, bf16[2,128,512]{2,1,0:T(8,128)(2,1)}, u32[]{:S(2)}, u32[]{:S(2)}) collective-permute-start(bf16[2,128,512]{2,1,0:T(8,128)(2,1)S(1)} %add_convert_fusion.8), channel_id=1, source_target_pairs={{0,8},{8,0},{4,12},{12,4},{16,24},{24,16},{20,28},{28,20},{1,9},{9... | collective-permute-start | bytes 786440 | tf_op jit(solution)/shard_map/ppermute | solution.py:22
  114.8 28.9 %collective-permute-start.21 = (bf16[2,128,512]{2,1,0:T(8,128)(2,1)}, bf16[2,128,512]{2,1,0:T(8,128)(2,1)}, u32[]{:S(2)}, u32[]{:S(2)}) collective-permute-start(bf16[2,128,512]{2,1,0:T(8,128)(2,1)} %add_convert_fusion.10), channel_id=1, source_target_pairs={{0,8},{8,0},{4,12},{12,4},{16,24},{24,16},{20,28},{28,20},{1,9},{9... | collective-permute-start | bytes 786440 | tf_op jit(solution)/shard_map/ppermute | solution.py:22
  123.0 24.5 %collective-permute-start.27 = (bf16[2,128,512]{2,1,0:T(8,128)(2,1)S(1)}, bf16[2,128,512]{2,1,0:T(8,128)(2,1)}, u32[]{:S(2)}, u32[]{:S(2)}) collective-permute-start(bf16[2,128,512]{2,1,0:T(8,128)(2,1)S(1)} %convert_element_type.200), channel_id=1, source_target_pairs={{0,8},{4,12},{24,16},{28,20},{1,9},{5,13},{25,17},{29,21},{2,10},{... | collective-permute-start | bytes 786440 | tf_op jit(solution)/shard_map/ppermute | solution.py:186
  140.5 45.7 %collective-permute-start.31 = (bf16[2,256,512]{2,1,0:T(8,128)(2,1)S(1)}, bf16[2,256,512]{2,1,0:T(8,128)(2,1)S(1)}, u32[]{:S(2)}, u32[]{:S(2)}) collective-permute-start(bf16[2,256,512]{2,1,0:T(8,128)(2,1)S(1)} %convert_element_type.207), channel_id=1, source_target_pairs={{0,4},{4,0},{8,12},{12,8},{16,20},{20,16},{24,28},{28,24},{1,5},{5... | collective-permute-start | bytes 1572872 | tf_op jit(solution)/shard_map/ppermute | solution.py:22
  143.7 6.8 %collective-permute-start.32 = (bf16[2,128,512]{2,1,0:T(8,128)(2,1)S(1)}, bf16[2,128,512]{2,1,0:T(8,128)(2,1)S(1)}, u32[]{:S(2)}, u32[]{:S(2)}) collective-permute-start(bf16[2,128,512]{2,1,0:T(8,128)(2,1)S(1)} %convert_element_type.209), channel_id=1, source_target_pairs={{0,8},{4,12},{24,16},{28,20},{1,9},{5,13},{25,17},{29,21},{2,10},{... | collective-permute-start | bytes 786440 | tf_op jit(solution)/shard_map/ppermute | solution.py:186
  147.5 42.3 %collective-permute-start.36 = (bf16[2,256,512]{2,1,0:T(8,128)(2,1)S(1)}, bf16[2,256,512]{2,1,0:T(8,128)(2,1)S(1)}, u32[]{:S(2)}, u32[]{:S(2)}) collective-permute-start(bf16[2,256,512]{2,1,0:T(8,128)(2,1)S(1)} %convert_element_type.216), channel_id=1, source_target_pairs={{0,4},{4,0},{8,12},{12,8},{16,20},{20,16},{24,28},{28,24},{1,5},{5... | collective-permute-start | bytes 1572872 | tf_op jit(solution)/shard_map/ppermute | solution.py:22
  150.5 9.4 %collective-permute-start.25 = (bf16[2,64,512]{2,1,0:T(8,128)(2,1)S(1)}, bf16[2,64,512]{2,1,0:T(8,128)(2,1)S(1)}, u32[]{:S(2)}, u32[]{:S(2)}) collective-permute-start(bf16[2,64,512]{2,1,0:T(8,128)(2,1)S(1)} %fusion.20), channel_id=1, source_target_pairs={{0,4},{4,0},{8,12},{12,8},{16,20},{20,16},{24,28},{28,24},{1,5},{5... | collective-permute-start | bytes 393224 | tf_op jit(solution)/shard_map/ppermute | solution.py:22
  164.8 5.5 %collective-permute-start.28 = (bf16[2,128,512]{2,1,0:T(8,128)(2,1)S(1)}, bf16[2,128,512]{2,1,0:T(8,128)(2,1)S(1)}, u32[]{:S(2)}, u32[]{:S(2)}) collective-permute-start(bf16[2,128,512]{2,1,0:T(8,128)(2,1)S(1)} %add_convert_fusion.7), channel_id=1, source_target_pairs={{8,16},{12,20},{16,8},{20,12},{9,17},{13,21},{17,9},{21,13},{10,18... | collective-permute-start | bytes 786440 | tf_op jit(solution)/shard_map/ppermute | solution.py:188
  166.2 8.8 %collective-permute-start.33 = (bf16[2,128,512]{2,1,0:T(8,128)(2,1)S(1)}, bf16[2,128,512]{2,1,0:T(8,128)(2,1)S(1)}, u32[]{:S(2)}, u32[]{:S(2)}) collective-permute-start(bf16[2,128,512]{2,1,0:T(8,128)(2,1)S(1)} %add_convert_fusion.5), channel_id=1, source_target_pairs={{8,16},{12,20},{16,8},{20,12},{9,17},{13,21},{17,9},{21,13},{10,18... | collective-permute-start | bytes 786440 | tf_op jit(solution)/shard_map/ppermute | solution.py:188
  171.4 7.9 %collective-permute-start.29 = (bf16[2,128,512]{2,1,0:T(8,128)(2,1)S(1)}, bf16[2,128,512]{2,1,0:T(8,128)(2,1)S(1)}, u32[]{:S(2)}, u32[]{:S(2)}) collective-permute-start(bf16[2,128,512]{2,1,0:T(8,128)(2,1)S(1)} %add_convert_fusion.6), channel_id=1, source_target_pairs={{0,8},{8,0},{4,12},{12,4},{16,24},{24,16},{20,28},{28,20},{1,9},{9... | collective-permute-start | bytes 786440 | tf_op jit(solution)/shard_map/ppermute | solution.py:22
  175.6 6.5 %collective-permute-start.34 = (bf16[2,128,512]{2,1,0:T(8,128)(2,1)S(1)}, bf16[2,128,512]{2,1,0:T(8,128)(2,1)S(1)}, u32[]{:S(2)}, u32[]{:S(2)}) collective-permute-start(bf16[2,128,512]{2,1,0:T(8,128)(2,1)S(1)} %add_convert_fusion.4), channel_id=1, source_target_pairs={{0,8},{8,0},{4,12},{12,4},{16,24},{24,16},{20,28},{28,20},{1,9},{9... | collective-permute-start | bytes 786440 | tf_op jit(solution)/shard_map/ppermute | solution.py:22
  180.2 5.3 %collective-permute-start.30 = (bf16[2,64,512]{2,1,0:T(8,128)(2,1)S(1)}, bf16[2,64,512]{2,1,0:T(8,128)(2,1)S(1)}, u32[]{:S(2)}, u32[]{:S(2)}) collective-permute-start(bf16[2,64,512]{2,1,0:T(8,128)(2,1)S(1)} %fusion.21), channel_id=1, source_target_pairs={{0,4},{4,0},{8,12},{12,8},{16,20},{20,16},{24,28},{28,24},{1,5},{5... | collective-permute-start | bytes 393224 | tf_op jit(solution)/shard_map/ppermute | solution.py:22
  (45 other events, 301.1 us)

commit v13 on v12

--- a/solution.py
+++ b/solution.py
@@ -190,12 +190,17 @@
                 grad = returned.astype(jnp.float32)
             else:
                 grad = apply(mine[step_level].T, grad) + returned
+        to_sibling = terms[1]
         own_total = terms[0]
-        sibling_send = terms[1].astype(jnp.bfloat16)
+        split = chunk == CHUNKS - 1 and grad is not None
+        if grad is not None:
+            if not split:
+                to_sibling = to_sibling + apply(other[0].T, grad)
+            own_total = own_total + apply(mine[0].T, grad)
+        sibling_send = to_sibling.astype(jnp.bfloat16)
         late.append((sibling_send, sends.get(1, sibling_send)))
         from_sibling = partner_2(sibling_send, "seq", 0)
-        if grad is not None:
-            own_total = own_total + apply(mine[0].T, grad)
+        if split:
             pooled_back = partner_2(apply(pick_other, grad).astype(jnp.bfloat16), "seq", 0)
             own_total = own_total + apply(spread_own, pooled_back)
         totals = own_total + from_sibling.astype(jnp.float32)

time: 194 us -> 171 us (0.88)
  waiting for transfers between devices: 41.7 us -> 25.4 us
  other arithmetic: 24.5 us -> 22 us
  starting transfers between devices: 59.7 us -> 57.5 us
    ppermute x21 -> x18, waiting for transfers between devices: 33.9 us -> 17.8 us  [partner_2(): return lax.ppermute(block, axis, route)]
    dot_general x36 -> x33, matrix products: 28.6 us -> 27.5 us  [apply(): jnp.einsum('pr,krw->kpw', matrix, rows.astype(jnp.float32), precision=lax...]
    ppermute x21 -> x18, starting transfers between devices: 35.3 us -> 34.4 us  [partner_2(): return lax.ppermute(block, axis, route)]
  transfers between devices with their start and end apart: 37 -> 34, of which waited for: 11 -> 8; matrix products, arithmetic and copies ran while one was open for 26% -> 28% of each run, Pallas kernels for 15% -> 17%
where the time goes in v13:
time: 171 us; the launch traced here: 170 us
  starting transfers between devices  57.5 us (34%)
  matrix products  30.4 us (18%)
  Pallas kernels  28.6 us (17%)
  waiting for transfers between devices  25.4 us (15%)
  other arithmetic  22 us (13%)
  local copies, waits for them, and re-layouts  4.27 us (2%)
    ppermute x18, starting transfers between devices, partner_2(): return lax.ppermute(block, axis, route)  34.4 us
    pallas_call x4, Pallas kernels, attention(): pl.pallas_call(functools.partial(attention_kernel, scale=score_scale, par...  28.6 us
    dot_general x33, matrix products, apply(): jnp.einsum('pr,krw->kpw', matrix, rows.astype(jnp.float32), precision=lax...  27.5 us
    ppermute x18, waiting for transfers between devices, partner_2(): return lax.ppermute(block, axis, route)  17.8 us
    ppermute x4, starting transfers between devices, body(): gathered = lax.ppermute(sends[step_level], 'seq', back)  12 us
    ppermute x4, waiting for transfers between devices, body(): passed = lax.ppermute(crossed, 'seq', outer_pairs(seq_count, step_level))  5.39 us
    ppermute x4, starting transfers between devices, body(): passed = lax.ppermute(crossed, 'seq', outer_pairs(seq_count, step_level))  5.15 us
    convert_element_type x8, other arithmetic, body(): sends[step_level] = outgoing.astype(jnp.bfloat16)  4.77 us
  transfers between devices with their start and end apart: 34, of which 8 were waited for; matrix products, arithmetic and copies ran while one was open for 28% of the time, Pallas kernels for 17%

profile of v13, /device:TPU:0, one launch (start us, length us, event | category | flops | bytes accessed | tf_op | source)
XLA Modules:
  0.0 169.8 jit_solution(14127018025212580923)
XLA Ops:
  0.7 2.9 %fusion.340 = (bf16[2,64,2048]{2,1,0:T(8,128)(2,1)}, f32[2,64,2048]{2,1,0:T(8,128)S(1)}) fusion(bf16[1,256,2048]{2,1,0:T(8,128)(2,1)} %bitcast.206, bf16[1,256,2048]{2,1,0:T(8,128)(2,1)} %bitcast.207, pred[64,256]{1,0:T(32,128)(4,1)S(1)} %slice_compare_fusion), kind=kOutput, calls=%fused_computation.434 | convolution fusion | flops 138706944 | bytes 3686400 | tf_op jit(solution)/shard_map/pr,krw->kpw/dot_general | solution.py:132
  3.6 3.0 %collective-permute-start = (bf16[2,64,2048]{2,1,0:T(8,128)(2,1)}, bf16[2,64,2048]{2,1,0:T(8,128)(2,1)}, u32[]{:S(2)}, u32[]{:S(2)}) collective-permute-start(bf16[2,64,2048]{2,1,0:T(8,128)(2,1)} %get-tuple-element.82), channel_id=1, source_target_pairs={{0,4},{4,0},{8,12},{12,8},{16,20},{20,16},{24,28},{28,24},{1,5},{5... | collective-permute-start | bytes 1572872 | tf_op jit(solution)/shard_map/ppermute | solution.py:22
  6.6 1.4 fusion.22
  8.1 1.4 fusion.24
  10.8 2.0 %pad_maximum_fusion.6.refs_0_ = bf16[2,256,512]{2,1,0:T(8,128)(2,1)} fusion(bf16[1,256,512]{2,1,0:T(8,128)(2,1)} %get-tuple-element.70, bf16[1,256,512]{2,1,0:T(8,128)(2,1)} %get-tuple-element.95), kind=kLoop, calls=%fused_computation.59 | loop fusion | flops 262144 | bytes 1048576 | tf_op jit(solution)/shard_map/stack | solution.py:149
  15.1 3.7 %collective-permute-done = bf16[2,64,2048]{2,1,0:T(8,128)(2,1)} collective-permute-done((bf16[2,64,2048]{2,1,0:T(8,128)(2,1)}, bf16[2,64,2048]{2,1,0:T(8,128)(2,1)}, u32[]{:S(2)}, u32[]{:S(2)}) %collective-permute-start) | collective-permute-done | bytes 524320 | tf_op jit(solution)/shard_map/ppermute | solution.py:22
  20.2 1.9 %collective-permute-start.2 = (bf16[2,128,512]{2,1,0:T(8,128)(2,1)S(1)}, bf16[2,128,512]{2,1,0:T(8,128)(2,1)S(1)}, u32[]{:S(2)}, u32[]{:S(2)}) collective-permute-start(bf16[2,128,512]{2,1,0:T(8,128)(2,1)S(1)} %get-tuple-element.86), channel_id=1, source_target_pairs={{0,8},{8,0},{4,12},{12,4},{16,24},{24,16},{20,28},{28,20},{1,9},{9... | collective-permute-start | bytes 786440 | tf_op jit(solution)/shard_map/ppermute | solution.py:22
  25.0 1.9 %collective-permute-start.12 = (bf16[2,128,512]{2,1,0:T(8,128)(2,1)S(1)}, bf16[2,128,512]{2,1,0:T(8,128)(2,1)S(1)}, u32[]{:S(2)}, u32[]{:S(2)}) collective-permute-start(bf16[2,128,512]{2,1,0:T(8,128)(2,1)S(1)} %get-tuple-element.90), channel_id=1, source_target_pairs={{0,8},{8,0},{4,12},{12,4},{16,24},{24,16},{20,28},{28,20},{1,9},{9... | collective-permute-start | bytes 786440 | tf_op jit(solution)/shard_map/ppermute | solution.py:22
  30.3 4.8 %collective-permute-done.6.refs_2_ = bf16[2,128,512]{2,1,0:T(8,128)(2,1)S(1)} collective-permute-done((bf16[2,128,512]{2,1,0:T(8,128)(2,1)S(1)}, bf16[2,128,512]{2,1,0:T(8,128)(2,1)S(1)}, u32[]{:S(2)}, u32[]{:S(2)}) %collective-permute-start.6) | collective-permute-done | bytes 262176 | tf_op jit(solution)/shard_map/ppermute | solution.py:22
  36.8 1.8 %collective-permute-start.1 = (bf16[2,256,512]{2,1,0:T(8,128)(2,1)S(1)}, bf16[2,256,512]{2,1,0:T(8,128)(2,1)}, u32[]{:S(2)}, u32[]{:S(2)}) collective-permute-start(bf16[2,256,512]{2,1,0:T(8,128)(2,1)S(1)} %pad_maximum_fusion.4.refs_0_), channel_id=1, source_target_pairs={{0,4},{4,0},{8,12},{12,8},{16,20},{20,16},{24,28},{28,24},{1,5},{5... | collective-permute-start | bytes 1572872 | tf_op jit(solution)/shard_map/ppermute | solution.py:22
  43.8 1.4 collective-permute-done.19.refs_2_
  47.8 5.4 %collective-permute-done.8 = bf16[2,128,512]{2,1,0:T(8,128)(2,1)S(1)} collective-permute-done((bf16[2,128,512]{2,1,0:T(8,128)(2,1)S(1)}, bf16[2,128,512]{2,1,0:T(8,128)(2,1)S(1)}, u32[]{:S(2)}, u32[]{:S(2)}) %collective-permute-start.8) | collective-permute-done | bytes 262176 | tf_op jit(solution)/shard_map/ppermute | solution.py:160
  55.2 4.2 %collective-permute-done.5.refs_1_ = bf16[2,256,512]{2,1,0:T(8,128)(2,1)S(1)} collective-permute-done((bf16[2,256,512]{2,1,0:T(8,128)(2,1)S(1)}, bf16[2,256,512]{2,1,0:T(8,128)(2,1)S(1)}, u32[]{:S(2)}, u32[]{:S(2)}) %collective-permute-start.5) | collective-permute-done | bytes 524320 | tf_op jit(solution)/shard_map/ppermute | solution.py:22
  60.2 1.8 %collective-permute-start.18 = (bf16[2,256,512]{2,1,0:T(8,128)(2,1)S(1)}, bf16[2,256,512]{2,1,0:T(8,128)(2,1)}, u32[]{:S(2)}, u32[]{:S(2)}) collective-permute-start(bf16[2,256,512]{2,1,0:T(8,128)(2,1)S(1)} %pad_maximum_fusion.7.refs_0_), channel_id=1, source_target_pairs={{0,4},{4,0},{8,12},{12,8},{16,20},{20,16},{24,28},{28,24},{1,5},{5... | collective-permute-start | bytes 1572872 | tf_op jit(solution)/shard_map/ppermute | solution.py:22
  62.0 7.1 %shard_map.76 = (bf16[256,512]{1,0:T(8,128)(2,1)}, bf16[256,512]{1,0:T(8,128)(2,1)}, f32[2,256,512]{2,1,0:T(8,128)}, f32[2,256,512]{2,1,0:T(8,128)}, f32[2,128,512]{2,1,0:T(8,128)}, /*index=5*/f32[2,128,512]{2,1,0:T(8,128)}) custom-call(f32[1,768]{1,0:T(1,128)} %constant.99.clone.1.bias_ref, bf16[256,2048]{1,0:T(8,128)(2,1)} %q_ref.7, ...), custom_call_target="tpu_custom_call" | custom-call | flops 1207959552 | bytes 5767168 | tf_op jit(solution)/shard_map/pallas_call | solution.py:72
  73.9 6.6 %collective-permute-start.15 = (bf16[2,128,512]{2,1,0:T(8,128)(2,1)S(1)}, bf16[2,128,512]{2,1,0:T(8,128)(2,1)S(1)}, u32[]{:S(2)}, u32[]{:S(2)}) collective-permute-start(bf16[2,128,512]{2,1,0:T(8,128)(2,1)S(1)} %convert_element_type.162), channel_id=1, source_target_pairs={{0,8},{4,12},{24,16},{28,20},{1,9},{5,13},{25,17},{29,21},{2,10},{... | collective-permute-start | bytes 786440 | tf_op jit(solution)/shard_map/ppermute | solution.py:186
  80.5 7.1 %shard_map.75 = (bf16[256,512]{1,0:T(8,128)(2,1)}, bf16[256,512]{1,0:T(8,128)(2,1)}, f32[2,256,512]{2,1,0:T(8,128)}, f32[2,256,512]{2,1,0:T(8,128)}, f32[2,128,512]{2,1,0:T(8,128)}, /*index=5*/f32[2,128,512]{2,1,0:T(8,128)}) custom-call(f32[1,768]{1,0:T(1,128)} %constant.99.clone.1.bias_ref, bf16[256,2048]{1,0:T(8,128)(2,1)} %q_ref.7, ...), custom_call_target="tpu_custom_call" | custom-call | flops 1207959552 | bytes 5767168 | tf_op jit(solution)/shard_map/pallas_call | solution.py:72
  88.7 1.5 collective-permute-start.9
  92.7 2.2 %collective-permute-done.9 = bf16[2,128,512]{2,1,0:T(8,128)(2,1)S(1)} collective-permute-done((bf16[2,128,512]{2,1,0:T(8,128)(2,1)S(1)}, bf16[2,128,512]{2,1,0:T(8,128)(2,1)S(1)}, u32[]{:S(2)}, u32[]{:S(2)}) %collective-permute-start.9) | collective-permute-done | bytes 262176 | tf_op jit(solution)/shard_map/ppermute | solution.py:186
  96.2 4.6 %collective-permute-start.23 = (bf16[2,128,512]{2,1,0:T(8,128)(2,1)S(1)}, bf16[2,128,512]{2,1,0:T(8,128)(2,1)S(1)}, u32[]{:S(2)}, u32[]{:S(2)}) collective-permute-start(bf16[2,128,512]{2,1,0:T(8,128)(2,1)S(1)} %add_convert_fusion.11), channel_id=1, source_target_pairs={{0,8},{8,0},{4,12},{12,4},{16,24},{24,16},{20,28},{28,20},{1,9},{9... | collective-permute-start | bytes 786440 | tf_op jit(solution)/shard_map/ppermute | solution.py:22
  101.4 4.9 %collective-permute-start.17 = (bf16[2,128,512]{2,1,0:T(8,128)(2,1)S(1)}, bf16[2,128,512]{2,1,0:T(8,128)(2,1)S(1)}, u32[]{:S(2)}, u32[]{:S(2)}) collective-permute-start(bf16[2,128,512]{2,1,0:T(8,128)(2,1)S(1)} %add_convert_fusion.13), channel_id=1, source_target_pairs={{0,8},{8,0},{4,12},{12,4},{16,24},{24,16},{20,28},{28,20},{1,9},{9... | collective-permute-start | bytes 786440 | tf_op jit(solution)/shard_map/ppermute | solution.py:22
  106.3 7.2 %shard_map.77 = (bf16[256,512]{1,0:T(8,128)(2,1)}, bf16[256,512]{1,0:T(8,128)(2,1)}, f32[2,256,512]{2,1,0:T(8,128)}, f32[2,256,512]{2,1,0:T(8,128)}, f32[2,128,512]{2,1,0:T(8,128)}, /*index=5*/f32[2,128,512]{2,1,0:T(8,128)}) custom-call(f32[1,768]{1,0:T(1,128)} %constant.99.clone.1.bias_ref, bf16[256,2048]{1,0:T(8,128)(2,1)} %q_ref.7, ...), custom_call_target="tpu_custom_call" | custom-call | flops 1207959552 | bytes 5767168 | tf_op jit(solution)/shard_map/pallas_call | solution.py:72
  114.6 2.7 %collective-permute-start.25 = (bf16[2,128,512]{2,1,0:T(8,128)(2,1)S(1)}, bf16[2,128,512]{2,1,0:T(8,128)(2,1)}, u32[]{:S(2)}, u32[]{:S(2)}) collective-permute-start(bf16[2,128,512]{2,1,0:T(8,128)(2,1)S(1)} %convert_element_type.175), channel_id=1, source_target_pairs={{0,8},{4,12},{24,16},{28,20},{1,9},{5,13},{25,17},{29,21},{2,10},{... | collective-permute-start | bytes 786440 | tf_op jit(solution)/shard_map/ppermute | solution.py:186
  119.2 1.6 collective-permute-start.24
  124.5 7.2 %shard_map.78 = (bf16[256,512]{1,0:T(8,128)(2,1)}, bf16[256,512]{1,0:T(8,128)(2,1)}, f32[2,256,512]{2,1,0:T(8,128)}, f32[2,256,512]{2,1,0:T(8,128)}, f32[2,128,512]{2,1,0:T(8,128)}, /*index=5*/f32[2,128,512]{2,1,0:T(8,128)}) custom-call(f32[1,768]{1,0:T(1,128)} %constant.99.clone.1.bias_ref, bf16[256,2048]{1,0:T(8,128)(2,1)} %q_ref.7, ...), custom_call_target="tpu_custom_call" | custom-call | flops 1207959552 | bytes 5767168 | tf_op jit(solution)/shard_map/pallas_call | solution.py:72
  135.4 1.6 collective-permute-start.33
  144.2 3.2 %collective-permute-start.27 = (bf16[2,128,512]{2,1,0:T(8,128)(2,1)S(1)}, bf16[2,128,512]{2,1,0:T(8,128)(2,1)S(1)}, u32[]{:S(2)}, u32[]{:S(2)}) collective-permute-start(bf16[2,128,512]{2,1,0:T(8,128)(2,1)S(1)} %add_convert_fusion.9), channel_id=1, source_target_pairs={{0,8},{8,0},{4,12},{12,4},{16,24},{24,16},{20,28},{28,20},{1,9},{9... | collective-permute-start | bytes 786440 | tf_op jit(solution)/shard_map/ppermute | solution.py:22
  148.0 4.3 %collective-permute-start.31 = (bf16[2,128,512]{2,1,0:T(8,128)(2,1)S(1)}, bf16[2,128,512]{2,1,0:T(8,128)(2,1)S(1)}, u32[]{:S(2)}, u32[]{:S(2)}) collective-permute-start(bf16[2,128,512]{2,1,0:T(8,128)(2,1)S(1)} %add_convert_fusion.7), channel_id=1, source_target_pairs={{0,8},{8,0},{4,12},{12,4},{16,24},{24,16},{20,28},{28,20},{1,9},{9... | collective-permute-start | bytes 786440 | tf_op jit(solution)/shard_map/ppermute | solution.py:22
  156.0 1.4 add_convert_fusion.3
  157.5 1.4 add_convert_fusion.5
  159.9 1.6 collective-permute-start.32
  162.6 2.4 %collective-permute-done.32 = bf16[2,64,512]{2,1,0:T(8,128)(2,1)S(1)} collective-permute-done((bf16[2,64,512]{2,1,0:T(8,128)(2,1)S(1)}, bf16[2,64,512]{2,1,0:T(8,128)(2,1)S(1)}, u32[]{:S(2)}, u32[]{:S(2)}) %collective-permute-start.32) | collective-permute-done | bytes 131104 | tf_op jit(solution)/shard_map/ppermute | solution.py:22
  (204 shorter events, 62.2 us)
Async XLA Ops:
  3.6 15.2 %collective-permute-start = (bf16[2,64,2048]{2,1,0:T(8,128)(2,1)}, bf16[2,64,2048]{2,1,0:T(8,128)(2,1)}, u32[]{:S(2)}, u32[]{:S(2)}) collective-permute-start(bf16[2,64,2048]{2,1,0:T(8,128)(2,1)} %get-tuple-element.82), channel_id=1, source_target_pairs={{0,4},{4,0},{8,12},{12,8},{16,20},{20,16},{24,28},{28,24},{1,5},{5... | collective-permute-start | bytes 1572872 | tf_op jit(solution)/shard_map/ppermute | solution.py:22
  20.2 18.5 %collective-permute-start.2 = (bf16[2,128,512]{2,1,0:T(8,128)(2,1)S(1)}, bf16[2,128,512]{2,1,0:T(8,128)(2,1)S(1)}, u32[]{:S(2)}, u32[]{:S(2)}) collective-permute-start(bf16[2,128,512]{2,1,0:T(8,128)(2,1)S(1)} %get-tuple-element.86), channel_id=1, source_target_pairs={{0,8},{8,0},{4,12},{12,4},{16,24},{24,16},{20,28},{28,20},{1,9},{9... | collective-permute-start | bytes 786440 | tf_op jit(solution)/shard_map/ppermute | solution.py:22
  23.4 11.7 %collective-permute-start.6 = (bf16[2,128,512]{2,1,0:T(8,128)(2,1)S(1)}, bf16[2,128,512]{2,1,0:T(8,128)(2,1)S(1)}, u32[]{:S(2)}, u32[]{:S(2)}) collective-permute-start(bf16[2,128,512]{2,1,0:T(8,128)(2,1)S(1)} %get-tuple-element.84), channel_id=1, source_target_pairs={{0,8},{8,0},{4,12},{12,4},{16,24},{24,16},{20,28},{28,20},{1,9},{9... | collective-permute-start | bytes 786440 | tf_op jit(solution)/shard_map/ppermute | solution.py:22
  25.0 15.7 %collective-permute-start.12 = (bf16[2,128,512]{2,1,0:T(8,128)(2,1)S(1)}, bf16[2,128,512]{2,1,0:T(8,128)(2,1)S(1)}, u32[]{:S(2)}, u32[]{:S(2)}) collective-permute-start(bf16[2,128,512]{2,1,0:T(8,128)(2,1)S(1)} %get-tuple-element.90), channel_id=1, source_target_pairs={{0,8},{8,0},{4,12},{12,4},{16,24},{24,16},{20,28},{28,20},{1,9},{9... | collective-permute-start | bytes 786440 | tf_op jit(solution)/shard_map/ppermute | solution.py:22
  28.2 17.1 %collective-permute-start.19 = (bf16[2,128,512]{2,1,0:T(8,128)(2,1)S(1)}, bf16[2,128,512]{2,1,0:T(8,128)(2,1)S(1)}, u32[]{:S(2)}, u32[]{:S(2)}) collective-permute-start(bf16[2,128,512]{2,1,0:T(8,128)(2,1)S(1)} %get-tuple-element.88), channel_id=1, source_target_pairs={{0,8},{8,0},{4,12},{12,4},{16,24},{24,16},{20,28},{28,20},{1,9},{9... | collective-permute-start | bytes 786440 | tf_op jit(solution)/shard_map/ppermute | solution.py:22
  35.5 5.9 %collective-permute-start.7 = (bf16[2,128,512]{2,1,0:T(8,128)(2,1)S(1)}, bf16[2,128,512]{2,1,0:T(8,128)(2,1)S(1)}, u32[]{:S(2)}, u32[]{:S(2)}) collective-permute-start(bf16[2,128,512]{2,1,0:T(8,128)(2,1)S(1)} %fusion.17), channel_id=1, source_target_pairs={{8,16},{12,20},{16,8},{20,12},{9,17},{13,21},{17,9},{21,13},{10,18... | collective-permute-start | bytes 786440 | tf_op jit(solution)/shard_map/ppermute | solution.py:159
  36.8 37.0 %collective-permute-start.1 = (bf16[2,256,512]{2,1,0:T(8,128)(2,1)S(1)}, bf16[2,256,512]{2,1,0:T(8,128)(2,1)}, u32[]{:S(2)}, u32[]{:S(2)}) collective-permute-start(bf16[2,256,512]{2,1,0:T(8,128)(2,1)S(1)} %pad_maximum_fusion.4.refs_0_), channel_id=1, source_target_pairs={{0,4},{4,0},{8,12},{12,8},{16,20},{20,16},{24,28},{28,24},{1,5},{5... | collective-permute-start | bytes 1572872 | tf_op jit(solution)/shard_map/ppermute | solution.py:22
  38.7 20.8 %collective-permute-start.5 = (bf16[2,256,512]{2,1,0:T(8,128)(2,1)S(1)}, bf16[2,256,512]{2,1,0:T(8,128)(2,1)S(1)}, u32[]{:S(2)}, u32[]{:S(2)}) collective-permute-start(bf16[2,256,512]{2,1,0:T(8,128)(2,1)S(1)} %copy-done.23), channel_id=1, source_target_pairs={{0,4},{4,0},{8,12},{12,8},{16,20},{20,16},{24,28},{28,24},{1,5},{5... | collective-permute-start | bytes 1572872 | tf_op jit(solution)/shard_map/ppermute | solution.py:22
  40.7 6.4 %collective-permute-start.3 = (bf16[2,128,512]{2,1,0:T(8,128)(2,1)S(1)}, bf16[2,128,512]{2,1,0:T(8,128)(2,1)S(1)}, u32[]{:S(2)}, u32[]{:S(2)}) collective-permute-start(bf16[2,128,512]{2,1,0:T(8,128)(2,1)S(1)} %fusion.18), channel_id=1, source_target_pairs={{8,16},{12,20},{16,8},{20,12},{9,17},{13,21},{17,9},{21,13},{10,18... | collective-permute-start | bytes 786440 | tf_op jit(solution)/shard_map/ppermute | solution.py:159
  41.4 11.7 %collective-permute-start.8 = (bf16[2,128,512]{2,1,0:T(8,128)(2,1)S(1)}, bf16[2,128,512]{2,1,0:T(8,128)(2,1)S(1)}, u32[]{:S(2)}, u32[]{:S(2)}) collective-permute-start(bf16[2,128,512]{2,1,0:T(8,128)(2,1)S(1)} %collective-permute-done.7), channel_id=1, source_target_pairs={{8,0},{12,4},{16,24},{20,28},{9,1},{13,5},{17,25},{21,29},{10,2},{... | collective-permute-start | bytes 786440 | tf_op jit(solution)/shard_map/ppermute | solution.py:160
  45.3 24.9 %collective-permute-start.13 = (bf16[2,128,512]{2,1,0:T(8,128)(2,1)}, bf16[2,128,512]{2,1,0:T(8,128)(2,1)S(1)}, u32[]{:S(2)}, u32[]{:S(2)}) collective-permute-start(bf16[2,128,512]{2,1,0:T(8,128)(2,1)} %fusion.16), channel_id=1, source_target_pairs={{8,16},{12,20},{16,8},{20,12},{9,17},{13,21},{17,9},{21,13},{10,18... | collective-permute-start | bytes 786440 | tf_op jit(solution)/shard_map/ppermute | solution.py:159
  47.1 23.5 %collective-permute-start.20 = (bf16[2,128,512]{2,1,0:T(8,128)(2,1)}, bf16[2,128,512]{2,1,0:T(8,128)(2,1)S(1)}, u32[]{:S(2)}, u32[]{:S(2)}) collective-permute-start(bf16[2,128,512]{2,1,0:T(8,128)(2,1)} %fusion.15), channel_id=1, source_target_pairs={{8,16},{12,20},{16,8},{20,12},{9,17},{13,21},{17,9},{21,13},{10,18... | collective-permute-start | bytes 786440 | tf_op jit(solution)/shard_map/ppermute | solution.py:159
  53.1 18.7 %collective-permute-start.4 = (bf16[2,128,512]{2,1,0:T(8,128)(2,1)S(1)}, bf16[2,128,512]{2,1,0:T(8,128)(2,1)S(1)}, u32[]{:S(2)}, u32[]{:S(2)}) collective-permute-start(bf16[2,128,512]{2,1,0:T(8,128)(2,1)S(1)} %collective-permute-done.3), channel_id=1, source_target_pairs={{8,0},{12,4},{16,24},{20,28},{9,1},{13,5},{17,25},{21,29},{10,2},{... | collective-permute-start | bytes 786440 | tf_op jit(solution)/shard_map/ppermute | solution.py:160
  60.2 64.2 %collective-permute-start.18 = (bf16[2,256,512]{2,1,0:T(8,128)(2,1)S(1)}, bf16[2,256,512]{2,1,0:T(8,128)(2,1)}, u32[]{:S(2)}, u32[]{:S(2)}) collective-permute-start(bf16[2,256,512]{2,1,0:T(8,128)(2,1)S(1)} %pad_maximum_fusion.7.refs_0_), channel_id=1, source_target_pairs={{0,4},{4,0},{8,12},{12,8},{16,20},{20,16},{24,28},{28,24},{1,5},{5... | collective-permute-start | bytes 1572872 | tf_op jit(solution)/shard_map/ppermute | solution.py:22
  70.2 36.1 %collective-permute-start.11 = (bf16[2,256,512]{2,1,0:T(8,128)(2,1)S(1)}, bf16[2,256,512]{2,1,0:T(8,128)(2,1)}, u32[]{:S(2)}, u32[]{:S(2)}) collective-permute-start(bf16[2,256,512]{2,1,0:T(8,128)(2,1)S(1)} %copy-done.21), channel_id=1, source_target_pairs={{0,4},{4,0},{8,12},{12,8},{16,20},{20,16},{24,28},{28,24},{1,5},{5... | collective-permute-start | bytes 1572872 | tf_op jit(solution)/shard_map/ppermute | solution.py:22
  70.6 18.2 %collective-permute-start.14 = (bf16[2,128,512]{2,1,0:T(8,128)(2,1)S(1)}, bf16[2,128,512]{2,1,0:T(8,128)(2,1)S(1)}, u32[]{:S(2)}, u32[]{:S(2)}) collective-permute-start(bf16[2,128,512]{2,1,0:T(8,128)(2,1)S(1)} %collective-permute-done.13), channel_id=1, source_target_pairs={{8,0},{12,4},{16,24},{20,28},{9,1},{13,5},{17,25},{21,29},{10,2},{... | collective-permute-start | bytes 786440 | tf_op jit(solution)/shard_map/ppermute | solution.py:160
  71.9 20.1 %collective-permute-start.21 = (bf16[2,128,512]{2,1,0:T(8,128)(2,1)S(1)}, bf16[2,128,512]{2,1,0:T(8,128)(2,1)S(1)}, u32[]{:S(2)}, u32[]{:S(2)}) collective-permute-start(bf16[2,128,512]{2,1,0:T(8,128)(2,1)S(1)} %collective-permute-done.20), channel_id=1, source_target_pairs={{8,0},{12,4},{16,24},{20,28},{9,1},{13,5},{17,25},{21,29},{10,2},{... | collective-permute-start | bytes 786440 | tf_op jit(solution)/shard_map/ppermute | solution.py:160
  73.9 17.1 %collective-permute-start.15 = (bf16[2,128,512]{2,1,0:T(8,128)(2,1)S(1)}, bf16[2,128,512]{2,1,0:T(8,128)(2,1)S(1)}, u32[]{:S(2)}, u32[]{:S(2)}) collective-permute-start(bf16[2,128,512]{2,1,0:T(8,128)(2,1)S(1)} %convert_element_type.162), channel_id=1, source_target_pairs={{0,8},{4,12},{24,16},{28,20},{1,9},{5,13},{25,17},{29,21},{2,10},{... | collective-permute-start | bytes 786440 | tf_op jit(solution)/shard_map/ppermute | solution.py:186
  88.7 6.1 %collective-permute-start.9 = (bf16[2,128,512]{2,1,0:T(8,128)(2,1)S(1)}, bf16[2,128,512]{2,1,0:T(8,128)(2,1)S(1)}, u32[]{:S(2)}, u32[]{:S(2)}) collective-permute-start(bf16[2,128,512]{2,1,0:T(8,128)(2,1)S(1)} %convert_element_type.155), channel_id=1, source_target_pairs={{0,8},{4,12},{24,16},{28,20},{1,9},{5,13},{25,17},{29,21},{2,10},{... | collective-permute-start | bytes 786440 | tf_op jit(solution)/shard_map/ppermute | solution.py:186
  94.9 5.9 %collective-permute-start.10 = (bf16[2,128,512]{2,1,0:T(8,128)(2,1)S(1)}, bf16[2,128,512]{2,1,0:T(8,128)(2,1)S(1)}, u32[]{:S(2)}, u32[]{:S(2)}) collective-permute-start(bf16[2,128,512]{2,1,0:T(8,128)(2,1)S(1)} %add_convert_fusion.14), channel_id=1, source_target_pairs={{8,16},{12,20},{16,8},{20,12},{9,17},{13,21},{17,9},{21,13},{10,18... | collective-permute-start | bytes 786440 | tf_op jit(solution)/shard_map/ppermute | solution.py:188
  96.2 21.0 %collective-permute-start.23 = (bf16[2,128,512]{2,1,0:T(8,128)(2,1)S(1)}, bf16[2,128,512]{2,1,0:T(8,128)(2,1)S(1)}, u32[]{:S(2)}, u32[]{:S(2)}) collective-permute-start(bf16[2,128,512]{2,1,0:T(8,128)(2,1)S(1)} %add_convert_fusion.11), channel_id=1, source_target_pairs={{0,8},{8,0},{4,12},{12,4},{16,24},{24,16},{20,28},{28,20},{1,9},{9... | collective-permute-start | bytes 786440 | tf_op jit(solution)/shard_map/ppermute | solution.py:22
  101.4 19.3 %collective-permute-start.17 = (bf16[2,128,512]{2,1,0:T(8,128)(2,1)S(1)}, bf16[2,128,512]{2,1,0:T(8,128)(2,1)S(1)}, u32[]{:S(2)}, u32[]{:S(2)}) collective-permute-start(bf16[2,128,512]{2,1,0:T(8,128)(2,1)S(1)} %add_convert_fusion.13), channel_id=1, source_target_pairs={{0,8},{8,0},{4,12},{12,4},{16,24},{24,16},{20,28},{28,20},{1,9},{9... | collective-permute-start | bytes 786440 | tf_op jit(solution)/shard_map/ppermute | solution.py:22
  114.6 23.5 %collective-permute-start.25 = (bf16[2,128,512]{2,1,0:T(8,128)(2,1)S(1)}, bf16[2,128,512]{2,1,0:T(8,128)(2,1)}, u32[]{:S(2)}, u32[]{:S(2)}) collective-permute-start(bf16[2,128,512]{2,1,0:T(8,128)(2,1)S(1)} %convert_element_type.175), channel_id=1, source_target_pairs={{0,8},{4,12},{24,16},{28,20},{1,9},{5,13},{25,17},{29,21},{2,10},{... | collective-permute-start | bytes 786440 | tf_op jit(solution)/shard_map/ppermute | solution.py:186
  119.2 36.8 %collective-permute-start.24 = (bf16[2,256,512]{2,1,0:T(8,128)(2,1)S(1)}, bf16[2,256,512]{2,1,0:T(8,128)(2,1)}, u32[]{:S(2)}, u32[]{:S(2)}) collective-permute-start(bf16[2,256,512]{2,1,0:T(8,128)(2,1)S(1)} %add_convert_fusion.4), channel_id=1, source_target_pairs={{0,4},{4,0},{8,12},{12,8},{16,20},{20,16},{24,28},{28,24},{1,5},{5... | collective-permute-start | bytes 1572872 | tf_op jit(solution)/shard_map/ppermute | solution.py:22
  122.8 34.7 %collective-permute-start.22 = (bf16[2,256,512]{2,1,0:T(8,128)(2,1)S(1)}, bf16[2,256,512]{2,1,0:T(8,128)(2,1)}, u32[]{:S(2)}, u32[]{:S(2)}) collective-permute-start(bf16[2,256,512]{2,1,0:T(8,128)(2,1)S(1)} %add_convert_fusion.6), channel_id=1, source_target_pairs={{0,4},{4,0},{8,12},{12,8},{16,20},{20,16},{24,28},{28,24},{1,5},{5... | collective-permute-start | bytes 1572872 | tf_op jit(solution)/shard_map/ppermute | solution.py:22
  132.7 9.7 %collective-permute-start.29 = (bf16[2,128,512]{2,1,0:T(8,128)(2,1)S(1)}, bf16[2,128,512]{2,1,0:T(8,128)(2,1)S(1)}, u32[]{:S(2)}, u32[]{:S(2)}) collective-permute-start(bf16[2,128,512]{2,1,0:T(8,128)(2,1)S(1)} %convert_element_type.182), channel_id=1, source_target_pairs={{0,8},{4,12},{24,16},{28,20},{1,9},{5,13},{25,17},{29,21},{2,10},{... | collective-permute-start | bytes 786440 | tf_op jit(solution)/shard_map/ppermute | solution.py:186
  135.4 30.2 %collective-permute-start.33 = (bf16[2,256,512]{2,1,0:T(8,128)(2,1)S(1)}, bf16[2,256,512]{2,1,0:T(8,128)(2,1)S(1)}, u32[]{:S(2)}, u32[]{:S(2)}) collective-permute-start(bf16[2,256,512]{2,1,0:T(8,128)(2,1)S(1)} %convert_element_type.189), channel_id=1, source_target_pairs={{0,4},{4,0},{8,12},{12,8},{16,20},{20,16},{24,28},{28,24},{1,5},{5... | collective-permute-start | bytes 1572872 | tf_op jit(solution)/shard_map/ppermute | solution.py:22
  142.5 4.9 %collective-permute-start.30 = (bf16[2,128,512]{2,1,0:T(8,128)(2,1)S(1)}, bf16[2,128,512]{2,1,0:T(8,128)(2,1)S(1)}, u32[]{:S(2)}, u32[]{:S(2)}) collective-permute-start(bf16[2,128,512]{2,1,0:T(8,128)(2,1)S(1)} %add_convert_fusion.8), channel_id=1, source_target_pairs={{8,16},{12,20},{16,8},{20,12},{9,17},{13,21},{17,9},{21,13},{10,18... | collective-permute-start | bytes 786440 | tf_op jit(solution)/shard_map/ppermute | solution.py:188
  144.2 8.2 %collective-permute-start.27 = (bf16[2,128,512]{2,1,0:T(8,128)(2,1)S(1)}, bf16[2,128,512]{2,1,0:T(8,128)(2,1)S(1)}, u32[]{:S(2)}, u32[]{:S(2)}) collective-permute-start(bf16[2,128,512]{2,1,0:T(8,128)(2,1)S(1)} %add_convert_fusion.9), channel_id=1, source_target_pairs={{0,8},{8,0},{4,12},{12,4},{16,24},{24,16},{20,28},{28,20},{1,9},{9... | collective-permute-start | bytes 786440 | tf_op jit(solution)/shard_map/ppermute | solution.py:22
  148.0 11.0 %collective-permute-start.31 = (bf16[2,128,512]{2,1,0:T(8,128)(2,1)S(1)}, bf16[2,128,512]{2,1,0:T(8,128)(2,1)S(1)}, u32[]{:S(2)}, u32[]{:S(2)}) collective-permute-start(bf16[2,128,512]{2,1,0:T(8,128)(2,1)S(1)} %add_convert_fusion.7), channel_id=1, source_target_pairs={{0,8},{8,0},{4,12},{12,4},{16,24},{24,16},{20,28},{28,20},{1,9},{9... | collective-permute-start | bytes 786440 | tf_op jit(solution)/shard_map/ppermute | solution.py:22
  154.3 11.8 %collective-permute-start.28 = (bf16[2,256,512]{2,1,0:T(8,128)(2,1)S(1)}, bf16[2,256,512]{2,1,0:T(8,128)(2,1)S(1)}, u32[]{:S(2)}, u32[]{:S(2)}) collective-permute-start(bf16[2,256,512]{2,1,0:T(8,128)(2,1)S(1)} %add_convert_fusion.2), channel_id=1, source_target_pairs={{0,4},{4,0},{8,12},{12,8},{16,20},{20,16},{24,28},{28,24},{1,5},{5... | collective-permute-start | bytes 1572872 | tf_op jit(solution)/shard_map/ppermute | solution.py:22
  159.9 5.1 %collective-permute-start.32 = (bf16[2,64,512]{2,1,0:T(8,128)(2,1)S(1)}, bf16[2,64,512]{2,1,0:T(8,128)(2,1)S(1)}, u32[]{:S(2)}, u32[]{:S(2)}) collective-permute-start(bf16[2,64,512]{2,1,0:T(8,128)(2,1)S(1)} %fusion.19), channel_id=1, source_target_pairs={{0,4},{4,0},{8,12},{12,8},{16,20},{20,16},{24,28},{28,24},{1,5},{5... | collective-permute-start | bytes 393224 | tf_op jit(solution)/shard_map/ppermute | solution.py:22
  (43 other events, 222.4 us)

commit v14 on v13

--- a/solution.py
+++ b/solution.py
@@ -192,7 +192,7 @@
                 grad = apply(mine[step_level].T, grad) + returned
         to_sibling = terms[1]
         own_total = terms[0]
-        split = chunk == CHUNKS - 1 and grad is not None
+        split = chunk >= CHUNKS - 2 and grad is not None
         if grad is not None:
             if not split:
                 to_sibling = to_sibling + apply(other[0].T, grad)

time: 171 us -> 181 us (1.058)
  waiting for transfers between devices: 25.4 us -> 31.3 us
  starting transfers between devices: 57.5 us -> 61.1 us
    ppermute x18 -> x19, waiting for transfers between devices: 17.8 us -> 23.7 us  [partner_2(): return lax.ppermute(block, axis, route)]
    ppermute x18 -> x19, starting transfers between devices: 34.4 us -> 38.1 us  [partner_2(): return lax.ppermute(block, axis, route)]
    dot_general x33 -> x34, matrix products: 27.5 us -> 27.5 us  [apply(): jnp.einsum('pr,krw->kpw', matrix, rows.astype(jnp.float32), precision=lax...]
  transfers between devices with their start and end apart: 34 -> 35, of which waited for: 8 -> 10; matrix products, arithmetic and copies ran while one was open for 28% -> 27% of each run, Pallas kernels for 17% -> 16%
where the time goes in v14:
time: 181 us; the launch traced here: 180 us
  starting transfers between devices  61.1 us (34%)
  waiting for transfers between devices  31.3 us (17%)
  matrix products  30.4 us (17%)
  Pallas kernels  28.5 us (16%)
  other arithmetic  23 us (13%)
  local copies, waits for them, and re-layouts  3.71 us (2%)
    ppermute x19, starting transfers between devices, partner_2(): return lax.ppermute(block, axis, route)  38.1 us
    pallas_call x4, Pallas kernels, attention(): pl.pallas_call(functools.partial(attention_kernel, scale=score_scale, par...  28.5 us
    dot_general x34, matrix products, apply(): jnp.einsum('pr,krw->kpw', matrix, rows.astype(jnp.float32), precision=lax...  27.5 us
    ppermute x19, waiting for transfers between devices, partner_2(): return lax.ppermute(block, axis, route)  23.7 us
    ppermute x4, starting transfers between devices, body(): gathered = lax.ppermute(sends[step_level], 'seq', back)  12.2 us
    ppermute x4, waiting for transfers between devices, body(): passed = lax.ppermute(crossed, 'seq', outer_pairs(seq_count, step_level))  5.39 us
    ppermute x4, starting transfers between devices, body(): passed = lax.ppermute(crossed, 'seq', outer_pairs(seq_count, step_level))  5.15 us
    convert_element_type x8, other arithmetic, body(): sends[step_level] = outgoing.astype(jnp.bfloat16)  4.81 us
  transfers between devices with their start and end apart: 35, of which 10 were waited for; matrix products, arithmetic and copies ran while one was open for 27% of the time, Pallas kernels for 16%

profile of v14, /device:TPU:0, one launch (start us, length us, event | category | flops | bytes accessed | tf_op | source)
XLA Modules:
  0.0 179.8 jit_solution(5640256314287528882)
XLA Ops:
  0.7 2.9 %fusion.342 = (bf16[2,64,2048]{2,1,0:T(8,128)(2,1)}, f32[2,64,2048]{2,1,0:T(8,128)S(1)}) fusion(bf16[1,256,2048]{2,1,0:T(8,128)(2,1)} %bitcast.210, bf16[1,256,2048]{2,1,0:T(8,128)(2,1)} %bitcast.211, pred[64,256]{1,0:T(32,128)(4,1)S(1)} %slice_compare_fusion), kind=kOutput, calls=%fused_computation.436 | convolution fusion | flops 138706944 | bytes 3686400 | tf_op jit(solution)/shard_map/pr,krw->kpw/dot_general | solution.py:132
  3.6 3.0 %collective-permute-start = (bf16[2,64,2048]{2,1,0:T(8,128)(2,1)}, bf16[2,64,2048]{2,1,0:T(8,128)(2,1)}, u32[]{:S(2)}, u32[]{:S(2)}) collective-permute-start(bf16[2,64,2048]{2,1,0:T(8,128)(2,1)} %get-tuple-element.82), channel_id=1, source_target_pairs={{0,4},{4,0},{8,12},{12,8},{16,20},{20,16},{24,28},{28,24},{1,5},{5... | collective-permute-start | bytes 1572872 | tf_op jit(solution)/shard_map/ppermute | solution.py:22
  8.1 1.4 fusion.25
  15.3 3.5 %collective-permute-done = bf16[2,64,2048]{2,1,0:T(8,128)(2,1)} collective-permute-done((bf16[2,64,2048]{2,1,0:T(8,128)(2,1)}, bf16[2,64,2048]{2,1,0:T(8,128)(2,1)}, u32[]{:S(2)}, u32[]{:S(2)}) %collective-permute-start) | collective-permute-done | bytes 524320 | tf_op jit(solution)/shard_map/ppermute | solution.py:22
  20.2 1.9 %collective-permute-start.2 = (bf16[2,128,512]{2,1,0:T(8,128)(2,1)S(1)}, bf16[2,128,512]{2,1,0:T(8,128)(2,1)S(1)}, u32[]{:S(2)}, u32[]{:S(2)}) collective-permute-start(bf16[2,128,512]{2,1,0:T(8,128)(2,1)S(1)} %get-tuple-element.86), channel_id=1, source_target_pairs={{0,8},{8,0},{4,12},{12,4},{16,24},{24,16},{20,28},{28,20},{1,9},{9... | collective-permute-start | bytes 786440 | tf_op jit(solution)/shard_map/ppermute | solution.py:22
  25.0 1.9 %collective-permute-start.12 = (bf16[2,128,512]{2,1,0:T(8,128)(2,1)S(1)}, bf16[2,128,512]{2,1,0:T(8,128)(2,1)S(1)}, u32[]{:S(2)}, u32[]{:S(2)}) collective-permute-start(bf16[2,128,512]{2,1,0:T(8,128)(2,1)S(1)} %get-tuple-element.90), channel_id=1, source_target_pairs={{0,8},{8,0},{4,12},{12,4},{16,24},{24,16},{20,28},{28,20},{1,9},{9... | collective-permute-start | bytes 786440 | tf_op jit(solution)/shard_map/ppermute | solution.py:22
  30.3 4.8 %collective-permute-done.6.refs_2_ = bf16[2,128,512]{2,1,0:T(8,128)(2,1)S(1)} collective-permute-done((bf16[2,128,512]{2,1,0:T(8,128)(2,1)S(1)}, bf16[2,128,512]{2,1,0:T(8,128)(2,1)S(1)}, u32[]{:S(2)}, u32[]{:S(2)}) %collective-permute-start.6) | collective-permute-done | bytes 262176 | tf_op jit(solution)/shard_map/ppermute | solution.py:22
  36.8 1.8 %collective-permute-start.1 = (bf16[2,256,512]{2,1,0:T(8,128)(2,1)S(1)}, bf16[2,256,512]{2,1,0:T(8,128)(2,1)}, u32[]{:S(2)}, u32[]{:S(2)}) collective-permute-start(bf16[2,256,512]{2,1,0:T(8,128)(2,1)S(1)} %pad_maximum_fusion.4.refs_0_), channel_id=1, source_target_pairs={{0,4},{4,0},{8,12},{12,8},{16,20},{20,16},{24,28},{28,24},{1,5},{5... | collective-permute-start | bytes 1572872 | tf_op jit(solution)/shard_map/ppermute | solution.py:22
  43.8 1.4 collective-permute-done.19.refs_2_
  47.8 5.4 %collective-permute-done.8 = bf16[2,128,512]{2,1,0:T(8,128)(2,1)S(1)} collective-permute-done((bf16[2,128,512]{2,1,0:T(8,128)(2,1)S(1)}, bf16[2,128,512]{2,1,0:T(8,128)(2,1)S(1)}, u32[]{:S(2)}, u32[]{:S(2)}) %collective-permute-start.8) | collective-permute-done | bytes 262176 | tf_op jit(solution)/shard_map/ppermute | solution.py:160
  55.2 4.1 %collective-permute-done.5.refs_1_ = bf16[2,256,512]{2,1,0:T(8,128)(2,1)S(1)} collective-permute-done((bf16[2,256,512]{2,1,0:T(8,128)(2,1)S(1)}, bf16[2,256,512]{2,1,0:T(8,128)(2,1)S(1)}, u32[]{:S(2)}, u32[]{:S(2)}) %collective-permute-start.5) | collective-permute-done | bytes 524320 | tf_op jit(solution)/shard_map/ppermute | solution.py:22
  60.0 1.7 collective-permute-start.18
  61.8 7.1 %shard_map.76 = (bf16[256,512]{1,0:T(8,128)(2,1)}, bf16[256,512]{1,0:T(8,128)(2,1)}, f32[2,256,512]{2,1,0:T(8,128)}, f32[2,256,512]{2,1,0:T(8,128)}, f32[2,128,512]{2,1,0:T(8,128)}, /*index=5*/f32[2,128,512]{2,1,0:T(8,128)}) custom-call(f32[1,768]{1,0:T(1,128)} %constant.99.clone.1.bias_ref, bf16[256,2048]{1,0:T(8,128)(2,1)} %q_ref.7, ...), custom_call_target="tpu_custom_call" | custom-call | flops 1207959552 | bytes 5767168 | tf_op jit(solution)/shard_map/pallas_call | solution.py:72
  73.7 6.6 %collective-permute-start.15 = (bf16[2,128,512]{2,1,0:T(8,128)(2,1)S(1)}, bf16[2,128,512]{2,1,0:T(8,128)(2,1)S(1)}, u32[]{:S(2)}, u32[]{:S(2)}) collective-permute-start(bf16[2,128,512]{2,1,0:T(8,128)(2,1)S(1)} %convert_element_type.169), channel_id=1, source_target_pairs={{0,8},{4,12},{24,16},{28,20},{1,9},{5,13},{25,17},{29,21},{2,10},{... | collective-permute-start | bytes 786440 | tf_op jit(solution)/shard_map/ppermute | solution.py:186
  80.3 7.1 %shard_map.75 = (bf16[256,512]{1,0:T(8,128)(2,1)}, bf16[256,512]{1,0:T(8,128)(2,1)}, f32[2,256,512]{2,1,0:T(8,128)}, f32[2,256,512]{2,1,0:T(8,128)}, f32[2,128,512]{2,1,0:T(8,128)}, /*index=5*/f32[2,128,512]{2,1,0:T(8,128)}) custom-call(f32[1,768]{1,0:T(1,128)} %constant.99.clone.1.bias_ref, bf16[256,2048]{1,0:T(8,128)(2,1)} %q_ref.7, ...), custom_call_target="tpu_custom_call" | custom-call | flops 1207959552 | bytes 5767168 | tf_op jit(solution)/shard_map/pallas_call | solution.py:72
  88.6 1.5 collective-permute-start.9
  92.5 2.2 %collective-permute-done.9 = bf16[2,128,512]{2,1,0:T(8,128)(2,1)S(1)} collective-permute-done((bf16[2,128,512]{2,1,0:T(8,128)(2,1)S(1)}, bf16[2,128,512]{2,1,0:T(8,128)(2,1)S(1)}, u32[]{:S(2)}, u32[]{:S(2)}) %collective-permute-start.9) | collective-permute-done | bytes 262176 | tf_op jit(solution)/shard_map/ppermute | solution.py:186
  96.1 4.6 %collective-permute-start.23 = (bf16[2,128,512]{2,1,0:T(8,128)(2,1)S(1)}, bf16[2,128,512]{2,1,0:T(8,128)(2,1)S(1)}, u32[]{:S(2)}, u32[]{:S(2)}) collective-permute-start(bf16[2,128,512]{2,1,0:T(8,128)(2,1)S(1)} %add_convert_fusion.10), channel_id=1, source_target_pairs={{0,8},{8,0},{4,12},{12,4},{16,24},{24,16},{20,28},{28,20},{1,9},{9... | collective-permute-start | bytes 786440 | tf_op jit(solution)/shard_map/ppermute | solution.py:22
  101.3 4.8 %collective-permute-start.17 = (bf16[2,128,512]{2,1,0:T(8,128)(2,1)S(1)}, bf16[2,128,512]{2,1,0:T(8,128)(2,1)S(1)}, u32[]{:S(2)}, u32[]{:S(2)}) collective-permute-start(bf16[2,128,512]{2,1,0:T(8,128)(2,1)S(1)} %add_convert_fusion.12), channel_id=1, source_target_pairs={{0,8},{8,0},{4,12},{12,4},{16,24},{24,16},{20,28},{28,20},{1,9},{9... | collective-permute-start | bytes 786440 | tf_op jit(solution)/shard_map/ppermute | solution.py:22
  106.2 7.1 %shard_map.77 = (bf16[256,512]{1,0:T(8,128)(2,1)}, bf16[256,512]{1,0:T(8,128)(2,1)}, f32[2,256,512]{2,1,0:T(8,128)}, f32[2,256,512]{2,1,0:T(8,128)}, f32[2,128,512]{2,1,0:T(8,128)}, /*index=5*/f32[2,128,512]{2,1,0:T(8,128)}) custom-call(f32[1,768]{1,0:T(1,128)} %constant.99.clone.1.bias_ref, bf16[256,2048]{1,0:T(8,128)(2,1)} %q_ref.7, ...), custom_call_target="tpu_custom_call" | custom-call | flops 1207959552 | bytes 5767168 | tf_op jit(solution)/shard_map/pallas_call | solution.py:72
  114.4 2.7 %collective-permute-start.25 = (bf16[2,128,512]{2,1,0:T(8,128)(2,1)S(1)}, bf16[2,128,512]{2,1,0:T(8,128)(2,1)}, u32[]{:S(2)}, u32[]{:S(2)}) collective-permute-start(bf16[2,128,512]{2,1,0:T(8,128)(2,1)S(1)} %convert_element_type.182), channel_id=1, source_target_pairs={{0,8},{4,12},{24,16},{28,20},{1,9},{5,13},{25,17},{29,21},{2,10},{... | collective-permute-start | bytes 786440 | tf_op jit(solution)/shard_map/ppermute | solution.py:186
  118.3 1.6 collective-permute-start.29
  124.5 1.6 collective-permute-start.22
  127.2 7.1 %shard_map.78 = (bf16[256,512]{1,0:T(8,128)(2,1)}, bf16[256,512]{1,0:T(8,128)(2,1)}, f32[2,256,512]{2,1,0:T(8,128)}, f32[2,256,512]{2,1,0:T(8,128)}, f32[2,128,512]{2,1,0:T(8,128)}, /*index=5*/f32[2,128,512]{2,1,0:T(8,128)}) custom-call(f32[1,768]{1,0:T(1,128)} %constant.99.clone.1.bias_ref, bf16[256,2048]{1,0:T(8,128)(2,1)} %q_ref.7, ...), custom_call_target="tpu_custom_call" | custom-call | flops 1207959552 | bytes 5767168 | tf_op jit(solution)/shard_map/pallas_call | solution.py:72
  135.5 1.4 collective-permute-start.30
  145.2 9.6 %collective-permute-start.27 = (bf16[2,128,512]{2,1,0:T(8,128)(2,1)S(1)}, bf16[2,128,512]{2,1,0:T(8,128)(2,1)S(1)}, u32[]{:S(2)}, u32[]{:S(2)}) collective-permute-start(bf16[2,128,512]{2,1,0:T(8,128)(2,1)S(1)} %add_convert_fusion.8), channel_id=1, source_target_pairs={{0,8},{8,0},{4,12},{12,4},{16,24},{24,16},{20,28},{28,20},{1,9},{9... | collective-permute-start | bytes 786440 | tf_op jit(solution)/shard_map/ppermute | solution.py:22
  155.4 3.7 %collective-permute-done.27 = bf16[2,128,512]{2,1,0:T(8,128)(2,1)S(1)} collective-permute-done((bf16[2,128,512]{2,1,0:T(8,128)(2,1)S(1)}, bf16[2,128,512]{2,1,0:T(8,128)(2,1)S(1)}, u32[]{:S(2)}, u32[]{:S(2)}) %collective-permute-start.27) | collective-permute-done | bytes 262176 | tf_op jit(solution)/shard_map/ppermute | solution.py:22
  159.2 2.0 %collective-permute-start.32 = (bf16[2,128,512]{2,1,0:T(8,128)(2,1)S(1)}, bf16[2,128,512]{2,1,0:T(8,128)(2,1)S(1)}, u32[]{:S(2)}, u32[]{:S(2)}) collective-permute-start(bf16[2,128,512]{2,1,0:T(8,128)(2,1)S(1)} %add_convert_fusion.6), channel_id=1, source_target_pairs={{0,8},{8,0},{4,12},{12,4},{16,24},{24,16},{20,28},{28,20},{1,9},{9... | collective-permute-start | bytes 786440 | tf_op jit(solution)/shard_map/ppermute | solution.py:22
  163.8 1.4 add_convert_fusion.2
  166.8 1.5 collective-permute-done.28
  168.9 1.5 add_convert_fusion.1
  173.1 3.3 %collective-permute-done.33 = bf16[2,64,512]{2,1,0:T(8,128)(2,1)S(1)} collective-permute-done((bf16[2,64,512]{2,1,0:T(8,128)(2,1)S(1)}, bf16[2,64,512]{2,1,0:T(8,128)(2,1)S(1)}, u32[]{:S(2)}, u32[]{:S(2)}) %collective-permute-start.33) | collective-permute-done | bytes 131104 | tf_op jit(solution)/shard_map/ppermute | solution.py:22
  (205 shorter events, 65.6 us)
Async XLA Ops:
  3.6 15.2 %collective-permute-start = (bf16[2,64,2048]{2,1,0:T(8,128)(2,1)}, bf16[2,64,2048]{2,1,0:T(8,128)(2,1)}, u32[]{:S(2)}, u32[]{:S(2)}) collective-permute-start(bf16[2,64,2048]{2,1,0:T(8,128)(2,1)} %get-tuple-element.82), channel_id=1, source_target_pairs={{0,4},{4,0},{8,12},{12,8},{16,20},{20,16},{24,28},{28,24},{1,5},{5... | collective-permute-start | bytes 1572872 | tf_op jit(solution)/shard_map/ppermute | solution.py:22
  20.2 18.5 %collective-permute-start.2 = (bf16[2,128,512]{2,1,0:T(8,128)(2,1)S(1)}, bf16[2,128,512]{2,1,0:T(8,128)(2,1)S(1)}, u32[]{:S(2)}, u32[]{:S(2)}) collective-permute-start(bf16[2,128,512]{2,1,0:T(8,128)(2,1)S(1)} %get-tuple-element.86), channel_id=1, source_target_pairs={{0,8},{8,0},{4,12},{12,4},{16,24},{24,16},{20,28},{28,20},{1,9},{9... | collective-permute-start | bytes 786440 | tf_op jit(solution)/shard_map/ppermute | solution.py:22
  23.4 11.7 %collective-permute-start.6 = (bf16[2,128,512]{2,1,0:T(8,128)(2,1)S(1)}, bf16[2,128,512]{2,1,0:T(8,128)(2,1)S(1)}, u32[]{:S(2)}, u32[]{:S(2)}) collective-permute-start(bf16[2,128,512]{2,1,0:T(8,128)(2,1)S(1)} %get-tuple-element.84), channel_id=1, source_target_pairs={{0,8},{8,0},{4,12},{12,4},{16,24},{24,16},{20,28},{28,20},{1,9},{9... | collective-permute-start | bytes 786440 | tf_op jit(solution)/shard_map/ppermute | solution.py:22
  25.0 15.7 %collective-permute-start.12 = (bf16[2,128,512]{2,1,0:T(8,128)(2,1)S(1)}, bf16[2,128,512]{2,1,0:T(8,128)(2,1)S(1)}, u32[]{:S(2)}, u32[]{:S(2)}) collective-permute-start(bf16[2,128,512]{2,1,0:T(8,128)(2,1)S(1)} %get-tuple-element.90), channel_id=1, source_target_pairs={{0,8},{8,0},{4,12},{12,4},{16,24},{24,16},{20,28},{28,20},{1,9},{9... | collective-permute-start | bytes 786440 | tf_op jit(solution)/shard_map/ppermute | solution.py:22
  28.2 17.1 %collective-permute-start.19 = (bf16[2,128,512]{2,1,0:T(8,128)(2,1)S(1)}, bf16[2,128,512]{2,1,0:T(8,128)(2,1)S(1)}, u32[]{:S(2)}, u32[]{:S(2)}) collective-permute-start(bf16[2,128,512]{2,1,0:T(8,128)(2,1)S(1)} %get-tuple-element.88), channel_id=1, source_target_pairs={{0,8},{8,0},{4,12},{12,4},{16,24},{24,16},{20,28},{28,20},{1,9},{9... | collective-permute-start | bytes 786440 | tf_op jit(solution)/shard_map/ppermute | solution.py:22
  35.5 5.9 %collective-permute-start.7 = (bf16[2,128,512]{2,1,0:T(8,128)(2,1)S(1)}, bf16[2,128,512]{2,1,0:T(8,128)(2,1)S(1)}, u32[]{:S(2)}, u32[]{:S(2)}) collective-permute-start(bf16[2,128,512]{2,1,0:T(8,128)(2,1)S(1)} %fusion.17), channel_id=1, source_target_pairs={{8,16},{12,20},{16,8},{20,12},{9,17},{13,21},{17,9},{21,13},{10,18... | collective-permute-start | bytes 786440 | tf_op jit(solution)/shard_map/ppermute | solution.py:159
  36.8 36.9 %collective-permute-start.1 = (bf16[2,256,512]{2,1,0:T(8,128)(2,1)S(1)}, bf16[2,256,512]{2,1,0:T(8,128)(2,1)}, u32[]{:S(2)}, u32[]{:S(2)}) collective-permute-start(bf16[2,256,512]{2,1,0:T(8,128)(2,1)S(1)} %pad_maximum_fusion.4.refs_0_), channel_id=1, source_target_pairs={{0,4},{4,0},{8,12},{12,8},{16,20},{20,16},{24,28},{28,24},{1,5},{5... | collective-permute-start | bytes 1572872 | tf_op jit(solution)/shard_map/ppermute | solution.py:22
  38.7 20.6 %collective-permute-start.5 = (bf16[2,256,512]{2,1,0:T(8,128)(2,1)S(1)}, bf16[2,256,512]{2,1,0:T(8,128)(2,1)S(1)}, u32[]{:S(2)}, u32[]{:S(2)}) collective-permute-start(bf16[2,256,512]{2,1,0:T(8,128)(2,1)S(1)} %copy-done.22), channel_id=1, source_target_pairs={{0,4},{4,0},{8,12},{12,8},{16,20},{20,16},{24,28},{28,24},{1,5},{5... | collective-permute-start | bytes 1572872 | tf_op jit(solution)/shard_map/ppermute | solution.py:22
  40.7 6.4 %collective-permute-start.3 = (bf16[2,128,512]{2,1,0:T(8,128)(2,1)S(1)}, bf16[2,128,512]{2,1,0:T(8,128)(2,1)S(1)}, u32[]{:S(2)}, u32[]{:S(2)}) collective-permute-start(bf16[2,128,512]{2,1,0:T(8,128)(2,1)S(1)} %fusion.18), channel_id=1, source_target_pairs={{8,16},{12,20},{16,8},{20,12},{9,17},{13,21},{17,9},{21,13},{10,18... | collective-permute-start | bytes 786440 | tf_op jit(solution)/shard_map/ppermute | solution.py:159
  41.4 11.7 %collective-permute-start.8 = (bf16[2,128,512]{2,1,0:T(8,128)(2,1)S(1)}, bf16[2,128,512]{2,1,0:T(8,128)(2,1)S(1)}, u32[]{:S(2)}, u32[]{:S(2)}) collective-permute-start(bf16[2,128,512]{2,1,0:T(8,128)(2,1)S(1)} %collective-permute-done.7), channel_id=1, source_target_pairs={{8,0},{12,4},{16,24},{20,28},{9,1},{13,5},{17,25},{21,29},{10,2},{... | collective-permute-start | bytes 786440 | tf_op jit(solution)/shard_map/ppermute | solution.py:160
  45.3 24.7 %collective-permute-start.13 = (bf16[2,128,512]{2,1,0:T(8,128)(2,1)}, bf16[2,128,512]{2,1,0:T(8,128)(2,1)S(1)}, u32[]{:S(2)}, u32[]{:S(2)}) collective-permute-start(bf16[2,128,512]{2,1,0:T(8,128)(2,1)} %fusion.16), channel_id=1, source_target_pairs={{8,16},{12,20},{16,8},{20,12},{9,17},{13,21},{17,9},{21,13},{10,18... | collective-permute-start | bytes 786440 | tf_op jit(solution)/shard_map/ppermute | solution.py:159
  47.1 23.3 %collective-permute-start.20 = (bf16[2,128,512]{2,1,0:T(8,128)(2,1)}, bf16[2,128,512]{2,1,0:T(8,128)(2,1)S(1)}, u32[]{:S(2)}, u32[]{:S(2)}) collective-permute-start(bf16[2,128,512]{2,1,0:T(8,128)(2,1)} %fusion.15), channel_id=1, source_target_pairs={{8,16},{12,20},{16,8},{20,12},{9,17},{13,21},{17,9},{21,13},{10,18... | collective-permute-start | bytes 786440 | tf_op jit(solution)/shard_map/ppermute | solution.py:159
  53.1 18.5 %collective-permute-start.4 = (bf16[2,128,512]{2,1,0:T(8,128)(2,1)S(1)}, bf16[2,128,512]{2,1,0:T(8,128)(2,1)S(1)}, u32[]{:S(2)}, u32[]{:S(2)}) collective-permute-start(bf16[2,128,512]{2,1,0:T(8,128)(2,1)S(1)} %collective-permute-done.3), channel_id=1, source_target_pairs={{8,0},{12,4},{16,24},{20,28},{9,1},{13,5},{17,25},{21,29},{10,2},{... | collective-permute-start | bytes 786440 | tf_op jit(solution)/shard_map/ppermute | solution.py:160
  60.0 67.1 %collective-permute-start.18 = (bf16[2,256,512]{2,1,0:T(8,128)(2,1)}, bf16[2,256,512]{2,1,0:T(8,128)(2,1)}, u32[]{:S(2)}, u32[]{:S(2)}) collective-permute-start(bf16[2,256,512]{2,1,0:T(8,128)(2,1)} %pad_maximum_fusion.7.refs_0_), channel_id=1, source_target_pairs={{0,4},{4,0},{8,12},{12,8},{16,20},{20,16},{24,28},{28,24},{1,5},{5... | collective-permute-start | bytes 1572872 | tf_op jit(solution)/shard_map/ppermute | solution.py:22
  70.0 36.1 %collective-permute-start.11 = (bf16[2,256,512]{2,1,0:T(8,128)(2,1)S(1)}, bf16[2,256,512]{2,1,0:T(8,128)(2,1)}, u32[]{:S(2)}, u32[]{:S(2)}) collective-permute-start(bf16[2,256,512]{2,1,0:T(8,128)(2,1)S(1)} %pad_maximum_fusion.6.refs_0_), channel_id=1, source_target_pairs={{0,4},{4,0},{8,12},{12,8},{16,20},{20,16},{24,28},{28,24},{1,5},{5... | collective-permute-start | bytes 1572872 | tf_op jit(solution)/shard_map/ppermute | solution.py:22
  70.4 18.2 %collective-permute-start.14 = (bf16[2,128,512]{2,1,0:T(8,128)(2,1)S(1)}, bf16[2,128,512]{2,1,0:T(8,128)(2,1)S(1)}, u32[]{:S(2)}, u32[]{:S(2)}) collective-permute-start(bf16[2,128,512]{2,1,0:T(8,128)(2,1)S(1)} %collective-permute-done.13), channel_id=1, source_target_pairs={{8,0},{12,4},{16,24},{20,28},{9,1},{13,5},{17,25},{21,29},{10,2},{... | collective-permute-start | bytes 786440 | tf_op jit(solution)/shard_map/ppermute | solution.py:160
  71.7 20.0 %collective-permute-start.21 = (bf16[2,128,512]{2,1,0:T(8,128)(2,1)S(1)}, bf16[2,128,512]{2,1,0:T(8,128)(2,1)S(1)}, u32[]{:S(2)}, u32[]{:S(2)}) collective-permute-start(bf16[2,128,512]{2,1,0:T(8,128)(2,1)S(1)} %collective-permute-done.20), channel_id=1, source_target_pairs={{8,0},{12,4},{16,24},{20,28},{9,1},{13,5},{17,25},{21,29},{10,2},{... | collective-permute-start | bytes 786440 | tf_op jit(solution)/shard_map/ppermute | solution.py:160
  73.7 17.1 %collective-permute-start.15 = (bf16[2,128,512]{2,1,0:T(8,128)(2,1)S(1)}, bf16[2,128,512]{2,1,0:T(8,128)(2,1)S(1)}, u32[]{:S(2)}, u32[]{:S(2)}) collective-permute-start(bf16[2,128,512]{2,1,0:T(8,128)(2,1)S(1)} %convert_element_type.169), channel_id=1, source_target_pairs={{0,8},{4,12},{24,16},{28,20},{1,9},{5,13},{25,17},{29,21},{2,10},{... | collective-permute-start | bytes 786440 | tf_op jit(solution)/shard_map/ppermute | solution.py:186
  88.6 6.1 %collective-permute-start.9 = (bf16[2,128,512]{2,1,0:T(8,128)(2,1)S(1)}, bf16[2,128,512]{2,1,0:T(8,128)(2,1)S(1)}, u32[]{:S(2)}, u32[]{:S(2)}) collective-permute-start(bf16[2,128,512]{2,1,0:T(8,128)(2,1)S(1)} %convert_element_type.162), channel_id=1, source_target_pairs={{0,8},{4,12},{24,16},{28,20},{1,9},{5,13},{25,17},{29,21},{2,10},{... | collective-permute-start | bytes 786440 | tf_op jit(solution)/shard_map/ppermute | solution.py:186
  94.7 6.0 %collective-permute-start.10 = (bf16[2,128,512]{2,1,0:T(8,128)(2,1)S(1)}, bf16[2,128,512]{2,1,0:T(8,128)(2,1)S(1)}, u32[]{:S(2)}, u32[]{:S(2)}) collective-permute-start(bf16[2,128,512]{2,1,0:T(8,128)(2,1)S(1)} %add_convert_fusion.13), channel_id=1, source_target_pairs={{8,16},{12,20},{16,8},{20,12},{9,17},{13,21},{17,9},{21,13},{10,18... | collective-permute-start | bytes 786440 | tf_op jit(solution)/shard_map/ppermute | solution.py:188
  96.1 23.9 %collective-permute-start.23 = (bf16[2,128,512]{2,1,0:T(8,128)(2,1)S(1)}, bf16[2,128,512]{2,1,0:T(8,128)(2,1)S(1)}, u32[]{:S(2)}, u32[]{:S(2)}) collective-permute-start(bf16[2,128,512]{2,1,0:T(8,128)(2,1)S(1)} %add_convert_fusion.10), channel_id=1, source_target_pairs={{0,8},{8,0},{4,12},{12,4},{16,24},{24,16},{20,28},{28,20},{1,9},{9... | collective-permute-start | bytes 786440 | tf_op jit(solution)/shard_map/ppermute | solution.py:22
  101.3 21.2 %collective-permute-start.17 = (bf16[2,128,512]{2,1,0:T(8,128)(2,1)S(1)}, bf16[2,128,512]{2,1,0:T(8,128)(2,1)S(1)}, u32[]{:S(2)}, u32[]{:S(2)}) collective-permute-start(bf16[2,128,512]{2,1,0:T(8,128)(2,1)S(1)} %add_convert_fusion.12), channel_id=1, source_target_pairs={{0,8},{8,0},{4,12},{12,4},{16,24},{24,16},{20,28},{28,20},{1,9},{9... | collective-permute-start | bytes 786440 | tf_op jit(solution)/shard_map/ppermute | solution.py:22
  114.4 23.7 %collective-permute-start.25 = (bf16[2,128,512]{2,1,0:T(8,128)(2,1)S(1)}, bf16[2,128,512]{2,1,0:T(8,128)(2,1)}, u32[]{:S(2)}, u32[]{:S(2)}) collective-permute-start(bf16[2,128,512]{2,1,0:T(8,128)(2,1)S(1)} %convert_element_type.182), channel_id=1, source_target_pairs={{0,8},{4,12},{24,16},{28,20},{1,9},{5,13},{25,17},{29,21},{2,10},{... | collective-permute-start | bytes 786440 | tf_op jit(solution)/shard_map/ppermute | solution.py:186
  118.3 50.6 %collective-permute-start.29 = (bf16[2,256,512]{2,1,0:T(8,128)(2,1)S(1)}, bf16[2,256,512]{2,1,0:T(8,128)(2,1)}, u32[]{:S(2)}, u32[]{:S(2)}) collective-permute-start(bf16[2,256,512]{2,1,0:T(8,128)(2,1)S(1)} %convert_element_type.189), channel_id=1, source_target_pairs={{0,4},{4,0},{8,12},{12,8},{16,20},{20,16},{24,28},{28,24},{1,5},{5... | collective-permute-start | bytes 1572872 | tf_op jit(solution)/shard_map/ppermute | solution.py:22
  121.9 41.3 %collective-permute-start.24 = (bf16[2,256,512]{2,1,0:T(8,128)(2,1)S(1)}, bf16[2,256,512]{2,1,0:T(8,128)(2,1)}, u32[]{:S(2)}, u32[]{:S(2)}) collective-permute-start(bf16[2,256,512]{2,1,0:T(8,128)(2,1)S(1)} %add_convert_fusion.3), channel_id=1, source_target_pairs={{0,4},{4,0},{8,12},{12,8},{16,20},{20,16},{24,28},{28,24},{1,5},{5... | collective-permute-start | bytes 1572872 | tf_op jit(solution)/shard_map/ppermute | solution.py:22
  124.5 40.8 %collective-permute-start.22 = (bf16[2,256,512]{2,1,0:T(8,128)(2,1)S(1)}, bf16[2,256,512]{2,1,0:T(8,128)(2,1)}, u32[]{:S(2)}, u32[]{:S(2)}) collective-permute-start(bf16[2,256,512]{2,1,0:T(8,128)(2,1)S(1)} %add_convert_fusion.5), channel_id=1, source_target_pairs={{0,4},{4,0},{8,12},{12,8},{16,20},{20,16},{24,28},{28,24},{1,5},{5... | collective-permute-start | bytes 1572872 | tf_op jit(solution)/shard_map/ppermute | solution.py:22
  135.5 7.5 %collective-permute-start.30 = (bf16[2,128,512]{2,1,0:T(8,128)(2,1)S(1)}, bf16[2,128,512]{2,1,0:T(8,128)(2,1)S(1)}, u32[]{:S(2)}, u32[]{:S(2)}) collective-permute-start(bf16[2,128,512]{2,1,0:T(8,128)(2,1)S(1)} %convert_element_type.191), channel_id=1, source_target_pairs={{0,8},{4,12},{24,16},{28,20},{1,9},{5,13},{25,17},{29,21},{2,10},{... | collective-permute-start | bytes 786440 | tf_op jit(solution)/shard_map/ppermute | solution.py:186
  143.0 34.1 %collective-permute-start.34 = (bf16[2,256,512]{2,1,0:T(8,128)(2,1)S(1)}, bf16[2,256,512]{2,1,0:T(8,128)(2,1)S(1)}, u32[]{:S(2)}, u32[]{:S(2)}) collective-permute-start(bf16[2,256,512]{2,1,0:T(8,128)(2,1)S(1)} %convert_element_type.198), channel_id=1, source_target_pairs={{0,4},{4,0},{8,12},{12,8},{16,20},{20,16},{24,28},{28,24},{1,5},{5... | collective-permute-start | bytes 1572872 | tf_op jit(solution)/shard_map/ppermute | solution.py:22
  145.2 13.9 %collective-permute-start.27 = (bf16[2,128,512]{2,1,0:T(8,128)(2,1)S(1)}, bf16[2,128,512]{2,1,0:T(8,128)(2,1)S(1)}, u32[]{:S(2)}, u32[]{:S(2)}) collective-permute-start(bf16[2,128,512]{2,1,0:T(8,128)(2,1)S(1)} %add_convert_fusion.8), channel_id=1, source_target_pairs={{0,8},{8,0},{4,12},{12,4},{16,24},{24,16},{20,28},{28,20},{1,9},{9... | collective-permute-start | bytes 786440 | tf_op jit(solution)/shard_map/ppermute | solution.py:22
  159.2 11.3 %collective-permute-start.32 = (bf16[2,128,512]{2,1,0:T(8,128)(2,1)S(1)}, bf16[2,128,512]{2,1,0:T(8,128)(2,1)S(1)}, u32[]{:S(2)}, u32[]{:S(2)}) collective-permute-start(bf16[2,128,512]{2,1,0:T(8,128)(2,1)S(1)} %add_convert_fusion.6), channel_id=1, source_target_pairs={{0,8},{8,0},{4,12},{12,4},{16,24},{24,16},{20,28},{28,20},{1,9},{9... | collective-permute-start | bytes 786440 | tf_op jit(solution)/shard_map/ppermute | solution.py:22
  163.2 5.0 %collective-permute-start.28 = (bf16[2,64,512]{2,1,0:T(8,128)(2,1)S(1)}, bf16[2,64,512]{2,1,0:T(8,128)(2,1)S(1)}, u32[]{:S(2)}, u32[]{:S(2)}) collective-permute-start(bf16[2,64,512]{2,1,0:T(8,128)(2,1)S(1)} %fusion.19), channel_id=1, source_target_pairs={{0,4},{4,0},{8,12},{12,8},{16,20},{20,16},{24,28},{28,24},{1,5},{5... | collective-permute-start | bytes 393224 | tf_op jit(solution)/shard_map/ppermute | solution.py:22
  171.5 5.0 %collective-permute-start.33 = (bf16[2,64,512]{2,1,0:T(8,128)(2,1)S(1)}, bf16[2,64,512]{2,1,0:T(8,128)(2,1)S(1)}, u32[]{:S(2)}, u32[]{:S(2)}) collective-permute-start(bf16[2,64,512]{2,1,0:T(8,128)(2,1)S(1)} %fusion.20), channel_id=1, source_target_pairs={{0,4},{4,0},{8,12},{12,8},{16,20},{20,16},{24,28},{28,24},{1,5},{5... | collective-permute-start | bytes 393224 | tf_op jit(solution)/shard_map/ppermute | solution.py:22
  (43 other events, 243.0 us)

commit v15 on v13

--- a/solution.py
+++ b/solution.py
@@ -129,10 +129,10 @@
     mine = [placed_pool(leaf_rows if s == 0 else POOLED, bits[s]) for s in range(levels)]
     other = [placed_pool(leaf_rows if s == 0 else POOLED, 1 - bits[s]) for s in range(levels)]
     pool_own = placed_pool(leaf_rows, 0)[: POOLED // 2]
-    own_pooled = jnp.einsum(
-        "pr,krw->kpw", pool_own.astype(jnp.bfloat16), jnp.stack((key_rows, value_rows)),
-        preferred_element_type=jnp.float32,
-    )
+    own_pooled = jnp.stack([
+        jnp.dot(pool_own.astype(jnp.bfloat16), rows, preferred_element_type=jnp.float32)
+        for rows in (key_rows, value_rows)
+    ])
     sibling_pooled = partner_2(own_pooled.astype(jnp.bfloat16), "seq", 0)
     pick_row = lax.broadcasted_iota(jnp.int32, (POOLED // 2, POOLED), 0)
     pick_col = lax.broadcasted_iota(jnp.int32, (POOLED // 2, POOLED), 1)

time: 171 us -> 171 us (level)
  other arithmetic: 22 us -> 25.3 us
  matrix products: 30.4 us -> 27.8 us
where the time goes in v15:
time: 171 us; the launch traced here: 170 us
  starting transfers between devices  56.5 us (33%)
  Pallas kernels  28.5 us (17%)
  matrix products  27.8 us (16%)
  other arithmetic  25.3 us (15%)
  waiting for transfers between devices  25 us (15%)
  local copies, waits for them, and re-layouts  4.79 us (3%)
    ppermute x18, starting transfers between devices, partner_2(): return lax.ppermute(block, axis, route)  34.5 us
    pallas_call x4, Pallas kernels, attention(): pl.pallas_call(functools.partial(attention_kernel, scale=score_scale, par...  28.5 us
    dot_general x33, matrix products, apply(): jnp.einsum('pr,krw->kpw', matrix, rows.astype(jnp.float32), precision=lax...  25.9 us
    ppermute x18, waiting for transfers between devices, partner_2(): return lax.ppermute(block, axis, route)  17.4 us
    ppermute x4, starting transfers between devices, body(): gathered = lax.ppermute(sends[step_level], 'seq', back)  11 us
    ppermute x4, waiting for transfers between devices, body(): passed = lax.ppermute(crossed, 'seq', outer_pairs(seq_count, step_level))  5.39 us
    ppermute x4, starting transfers between devices, body(): passed = lax.ppermute(crossed, 'seq', outer_pairs(seq_count, step_level))  5.15 us
    convert_element_type x8, other arithmetic, body(): sends[step_level] = outgoing.astype(jnp.bfloat16)  4.77 us
  transfers between devices with their start and end apart: 34, of which 8 were waited for; matrix products, arithmetic and copies ran while one was open for 28% of the time, Pallas kernels for 17%

profile of v15, /device:TPU:0, one launch (start us, length us, event | category | flops | bytes accessed | tf_op | source)
XLA Modules:
  0.0 169.7 jit_solution(3785655917754981702)
XLA Ops:
  0.7 1.6 convolution_bitcast_fusion
  3.5 3.0 %collective-permute-start = (bf16[2,64,2048]{2,1,0:T(8,128)(2,1)}, bf16[2,64,2048]{2,1,0:T(8,128)(2,1)}, u32[]{:S(2)}, u32[]{:S(2)}) collective-permute-start(bf16[2,64,2048]{2,1,0:T(8,128)(2,1)} %fusion.17), channel_id=1, source_target_pairs={{0,4},{4,0},{8,12},{12,8},{16,20},{20,16},{24,28},{28,24},{1,5},{5... | collective-permute-start | bytes 1572872 | tf_op jit(solution)/shard_map/ppermute | solution.py:22
  9.6 2.0 %pad_maximum_fusion.7.refs_0_ = bf16[2,256,512]{2,1,0:T(8,128)(2,1)} fusion(bf16[1,256,512]{2,1,0:T(8,128)(2,1)} %get-tuple-element.70, bf16[1,256,512]{2,1,0:T(8,128)(2,1)} %get-tuple-element.93), kind=kLoop, calls=%fused_computation.67 | loop fusion | flops 262144 | bytes 1048576 | tf_op jit(solution)/shard_map/stack | solution.py:149
  15.4 3.3 %collective-permute-done = bf16[2,64,2048]{2,1,0:T(8,128)(2,1)} collective-permute-done((bf16[2,64,2048]{2,1,0:T(8,128)(2,1)}, bf16[2,64,2048]{2,1,0:T(8,128)(2,1)}, u32[]{:S(2)}, u32[]{:S(2)}) %collective-permute-start) | collective-permute-done | bytes 524320 | tf_op jit(solution)/shard_map/ppermute | solution.py:22
  20.0 1.9 %collective-permute-start.2 = (bf16[2,128,512]{2,1,0:T(8,128)(2,1)S(1)}, bf16[2,128,512]{2,1,0:T(8,128)(2,1)S(1)}, u32[]{:S(2)}, u32[]{:S(2)}) collective-permute-start(bf16[2,128,512]{2,1,0:T(8,128)(2,1)S(1)} %get-tuple-element.84), channel_id=1, source_target_pairs={{0,8},{8,0},{4,12},{12,4},{16,24},{24,16},{20,28},{28,20},{1,9},{9... | collective-permute-start | bytes 786440 | tf_op jit(solution)/shard_map/ppermute | solution.py:22
  23.5 1.3 fusion.350
  24.9 1.9 %collective-permute-start.12 = (bf16[2,128,512]{2,1,0:T(8,128)(2,1)S(1)}, bf16[2,128,512]{2,1,0:T(8,128)(2,1)S(1)}, u32[]{:S(2)}, u32[]{:S(2)}) collective-permute-start(bf16[2,128,512]{2,1,0:T(8,128)(2,1)S(1)} %get-tuple-element.88), channel_id=1, source_target_pairs={{0,8},{8,0},{4,12},{12,4},{16,24},{24,16},{20,28},{28,20},{1,9},{9... | collective-permute-start | bytes 786440 | tf_op jit(solution)/shard_map/ppermute | solution.py:22
  30.2 4.7 %collective-permute-done.6.refs_2_ = bf16[2,128,512]{2,1,0:T(8,128)(2,1)S(1)} collective-permute-done((bf16[2,128,512]{2,1,0:T(8,128)(2,1)S(1)}, bf16[2,128,512]{2,1,0:T(8,128)(2,1)S(1)}, u32[]{:S(2)}, u32[]{:S(2)}) %collective-permute-start.6) | collective-permute-done | bytes 262176 | tf_op jit(solution)/shard_map/ppermute | solution.py:22
  36.7 1.8 %collective-permute-start.1 = (bf16[2,256,512]{2,1,0:T(8,128)(2,1)S(1)}, bf16[2,256,512]{2,1,0:T(8,128)(2,1)}, u32[]{:S(2)}, u32[]{:S(2)}) collective-permute-start(bf16[2,256,512]{2,1,0:T(8,128)(2,1)S(1)} %copy-done.20), channel_id=1, source_target_pairs={{0,4},{4,0},{8,12},{12,8},{16,20},{20,16},{24,28},{28,24},{1,5},{5... | collective-permute-start | bytes 1572872 | tf_op jit(solution)/shard_map/ppermute | solution.py:22
  43.7 1.4 collective-permute-done.19.refs_2_
  47.6 5.4 %collective-permute-done.8 = bf16[2,128,512]{2,1,0:T(8,128)(2,1)S(1)} collective-permute-done((bf16[2,128,512]{2,1,0:T(8,128)(2,1)S(1)}, bf16[2,128,512]{2,1,0:T(8,128)(2,1)S(1)}, u32[]{:S(2)}, u32[]{:S(2)}) %collective-permute-start.8) | collective-permute-done | bytes 262176 | tf_op jit(solution)/shard_map/ppermute | solution.py:160
  55.0 4.3 %collective-permute-done.5.refs_1_ = bf16[2,256,512]{2,1,0:T(8,128)(2,1)S(1)} collective-permute-done((bf16[2,256,512]{2,1,0:T(8,128)(2,1)S(1)}, bf16[2,256,512]{2,1,0:T(8,128)(2,1)S(1)}, u32[]{:S(2)}, u32[]{:S(2)}) %collective-permute-start.5) | collective-permute-done | bytes 524320 | tf_op jit(solution)/shard_map/ppermute | solution.py:22
  60.1 1.8 %collective-permute-start.18 = (bf16[2,256,512]{2,1,0:T(8,128)(2,1)S(1)}, bf16[2,256,512]{2,1,0:T(8,128)(2,1)}, u32[]{:S(2)}, u32[]{:S(2)}) collective-permute-start(bf16[2,256,512]{2,1,0:T(8,128)(2,1)S(1)} %copy-done.18), channel_id=1, source_target_pairs={{0,4},{4,0},{8,12},{12,8},{16,20},{20,16},{24,28},{28,24},{1,5},{5... | collective-permute-start | bytes 1572872 | tf_op jit(solution)/shard_map/ppermute | solution.py:22
  61.8 7.1 %shard_map.76 = (bf16[256,512]{1,0:T(8,128)(2,1)}, bf16[256,512]{1,0:T(8,128)(2,1)}, f32[2,256,512]{2,1,0:T(8,128)}, f32[2,256,512]{2,1,0:T(8,128)}, f32[2,128,512]{2,1,0:T(8,128)}, /*index=5*/f32[2,128,512]{2,1,0:T(8,128)}) custom-call(f32[1,768]{1,0:T(1,128)} %constant.99.clone.1.bias_ref, bf16[256,2048]{1,0:T(8,128)(2,1)} %q_ref.7, ...), custom_call_target="tpu_custom_call" | custom-call | flops 1207959552 | bytes 5767168 | tf_op jit(solution)/shard_map/pallas_call | solution.py:72
  73.0 1.7 broadcast_select_fusion.3.refs_3_
  74.7 5.6 %collective-permute-start.15 = (bf16[2,128,512]{2,1,0:T(8,128)(2,1)S(1)}, bf16[2,128,512]{2,1,0:T(8,128)(2,1)S(1)}, u32[]{:S(2)}, u32[]{:S(2)}) collective-permute-start(bf16[2,128,512]{2,1,0:T(8,128)(2,1)S(1)} %convert_element_type.165), channel_id=1, source_target_pairs={{0,8},{4,12},{24,16},{28,20},{1,9},{5,13},{25,17},{29,21},{2,10},{... | collective-permute-start | bytes 786440 | tf_op jit(solution)/shard_map/ppermute | solution.py:186
  80.3 7.1 %shard_map.75 = (bf16[256,512]{1,0:T(8,128)(2,1)}, bf16[256,512]{1,0:T(8,128)(2,1)}, f32[2,256,512]{2,1,0:T(8,128)}, f32[2,256,512]{2,1,0:T(8,128)}, f32[2,128,512]{2,1,0:T(8,128)}, /*index=5*/f32[2,128,512]{2,1,0:T(8,128)}) custom-call(f32[1,768]{1,0:T(1,128)} %constant.99.clone.1.bias_ref, bf16[256,2048]{1,0:T(8,128)(2,1)} %q_ref.7, ...), custom_call_target="tpu_custom_call" | custom-call | flops 1207959552 | bytes 5767168 | tf_op jit(solution)/shard_map/pallas_call | solution.py:72
  88.6 1.5 collective-permute-start.9
  92.5 2.2 %collective-permute-done.9 = bf16[2,128,512]{2,1,0:T(8,128)(2,1)S(1)} collective-permute-done((bf16[2,128,512]{2,1,0:T(8,128)(2,1)S(1)}, bf16[2,128,512]{2,1,0:T(8,128)(2,1)S(1)}, u32[]{:S(2)}, u32[]{:S(2)}) %collective-permute-start.9) | collective-permute-done | bytes 262176 | tf_op jit(solution)/shard_map/ppermute | solution.py:186
  96.0 4.6 %collective-permute-start.23 = (bf16[2,128,512]{2,1,0:T(8,128)(2,1)S(1)}, bf16[2,128,512]{2,1,0:T(8,128)(2,1)S(1)}, u32[]{:S(2)}, u32[]{:S(2)}) collective-permute-start(bf16[2,128,512]{2,1,0:T(8,128)(2,1)S(1)} %add_convert_fusion.11), channel_id=1, source_target_pairs={{0,8},{8,0},{4,12},{12,4},{16,24},{24,16},{20,28},{28,20},{1,9},{9... | collective-permute-start | bytes 786440 | tf_op jit(solution)/shard_map/ppermute | solution.py:22
  101.3 4.8 %collective-permute-start.17 = (bf16[2,128,512]{2,1,0:T(8,128)(2,1)S(1)}, bf16[2,128,512]{2,1,0:T(8,128)(2,1)S(1)}, u32[]{:S(2)}, u32[]{:S(2)}) collective-permute-start(bf16[2,128,512]{2,1,0:T(8,128)(2,1)S(1)} %add_convert_fusion.13), channel_id=1, source_target_pairs={{0,8},{8,0},{4,12},{12,4},{16,24},{24,16},{20,28},{28,20},{1,9},{9... | collective-permute-start | bytes 786440 | tf_op jit(solution)/shard_map/ppermute | solution.py:22
  106.2 7.2 %shard_map.77 = (bf16[256,512]{1,0:T(8,128)(2,1)}, bf16[256,512]{1,0:T(8,128)(2,1)}, f32[2,256,512]{2,1,0:T(8,128)}, f32[2,256,512]{2,1,0:T(8,128)}, f32[2,128,512]{2,1,0:T(8,128)}, /*index=5*/f32[2,128,512]{2,1,0:T(8,128)}) custom-call(f32[1,768]{1,0:T(1,128)} %constant.99.clone.1.bias_ref, bf16[256,2048]{1,0:T(8,128)(2,1)} %q_ref.7, ...), custom_call_target="tpu_custom_call" | custom-call | flops 1207959552 | bytes 5767168 | tf_op jit(solution)/shard_map/pallas_call | solution.py:72
  114.4 2.7 %collective-permute-start.25 = (bf16[2,128,512]{2,1,0:T(8,128)(2,1)S(1)}, bf16[2,128,512]{2,1,0:T(8,128)(2,1)}, u32[]{:S(2)}, u32[]{:S(2)}) collective-permute-start(bf16[2,128,512]{2,1,0:T(8,128)(2,1)S(1)} %convert_element_type.178), channel_id=1, source_target_pairs={{0,8},{4,12},{24,16},{28,20},{1,9},{5,13},{25,17},{29,21},{2,10},{... | collective-permute-start | bytes 786440 | tf_op jit(solution)/shard_map/ppermute | solution.py:186
  119.0 1.6 collective-permute-start.24
  124.3 7.2 %shard_map.78 = (bf16[256,512]{1,0:T(8,128)(2,1)}, bf16[256,512]{1,0:T(8,128)(2,1)}, f32[2,256,512]{2,1,0:T(8,128)}, f32[2,256,512]{2,1,0:T(8,128)}, f32[2,128,512]{2,1,0:T(8,128)}, /*index=5*/f32[2,128,512]{2,1,0:T(8,128)}) custom-call(f32[1,768]{1,0:T(1,128)} %constant.99.clone.1.bias_ref, bf16[256,2048]{1,0:T(8,128)(2,1)} %q_ref.7, ...), custom_call_target="tpu_custom_call" | custom-call | flops 1207959552 | bytes 5767168 | tf_op jit(solution)/shard_map/pallas_call | solution.py:72
  135.2 1.6 collective-permute-start.33
  144.0 3.2 %collective-permute-start.27 = (bf16[2,128,512]{2,1,0:T(8,128)(2,1)S(1)}, bf16[2,128,512]{2,1,0:T(8,128)(2,1)S(1)}, u32[]{:S(2)}, u32[]{:S(2)}) collective-permute-start(bf16[2,128,512]{2,1,0:T(8,128)(2,1)S(1)} %add_convert_fusion.9), channel_id=1, source_target_pairs={{0,8},{8,0},{4,12},{12,4},{16,24},{24,16},{20,28},{28,20},{1,9},{9... | collective-permute-start | bytes 786440 | tf_op jit(solution)/shard_map/ppermute | solution.py:22
  147.9 4.3 %collective-permute-start.31 = (bf16[2,128,512]{2,1,0:T(8,128)(2,1)S(1)}, bf16[2,128,512]{2,1,0:T(8,128)(2,1)S(1)}, u32[]{:S(2)}, u32[]{:S(2)}) collective-permute-start(bf16[2,128,512]{2,1,0:T(8,128)(2,1)S(1)} %add_convert_fusion.7), channel_id=1, source_target_pairs={{0,8},{8,0},{4,12},{12,4},{16,24},{24,16},{20,28},{28,20},{1,9},{9... | collective-permute-start | bytes 786440 | tf_op jit(solution)/shard_map/ppermute | solution.py:22
  155.9 1.4 add_convert_fusion.3
  157.3 1.4 add_convert_fusion.5
  159.8 1.6 collective-permute-start.32
  162.5 2.4 %collective-permute-done.32 = bf16[2,64,512]{2,1,0:T(8,128)(2,1)S(1)} collective-permute-done((bf16[2,64,512]{2,1,0:T(8,128)(2,1)S(1)}, bf16[2,64,512]{2,1,0:T(8,128)(2,1)S(1)}, u32[]{:S(2)}, u32[]{:S(2)}) %collective-permute-start.32) | collective-permute-done | bytes 131104 | tf_op jit(solution)/shard_map/ppermute | solution.py:22
  (202 shorter events, 64.6 us)
Async XLA Ops:
  3.5 15.2 %collective-permute-start = (bf16[2,64,2048]{2,1,0:T(8,128)(2,1)}, bf16[2,64,2048]{2,1,0:T(8,128)(2,1)}, u32[]{:S(2)}, u32[]{:S(2)}) collective-permute-start(bf16[2,64,2048]{2,1,0:T(8,128)(2,1)} %fusion.17), channel_id=1, source_target_pairs={{0,4},{4,0},{8,12},{12,8},{16,20},{20,16},{24,28},{28,24},{1,5},{5... | collective-permute-start | bytes 1572872 | tf_op jit(solution)/shard_map/ppermute | solution.py:22
  20.0 18.5 %collective-permute-start.2 = (bf16[2,128,512]{2,1,0:T(8,128)(2,1)S(1)}, bf16[2,128,512]{2,1,0:T(8,128)(2,1)S(1)}, u32[]{:S(2)}, u32[]{:S(2)}) collective-permute-start(bf16[2,128,512]{2,1,0:T(8,128)(2,1)S(1)} %get-tuple-element.84), channel_id=1, source_target_pairs={{0,8},{8,0},{4,12},{12,4},{16,24},{24,16},{20,28},{28,20},{1,9},{9... | collective-permute-start | bytes 786440 | tf_op jit(solution)/shard_map/ppermute | solution.py:22
  23.2 11.7 %collective-permute-start.6 = (bf16[2,128,512]{2,1,0:T(8,128)(2,1)S(1)}, bf16[2,128,512]{2,1,0:T(8,128)(2,1)S(1)}, u32[]{:S(2)}, u32[]{:S(2)}) collective-permute-start(bf16[2,128,512]{2,1,0:T(8,128)(2,1)S(1)} %get-tuple-element.82), channel_id=1, source_target_pairs={{0,8},{8,0},{4,12},{12,4},{16,24},{24,16},{20,28},{28,20},{1,9},{9... | collective-permute-start | bytes 786440 | tf_op jit(solution)/shard_map/ppermute | solution.py:22
  24.9 15.7 %collective-permute-start.12 = (bf16[2,128,512]{2,1,0:T(8,128)(2,1)S(1)}, bf16[2,128,512]{2,1,0:T(8,128)(2,1)S(1)}, u32[]{:S(2)}, u32[]{:S(2)}) collective-permute-start(bf16[2,128,512]{2,1,0:T(8,128)(2,1)S(1)} %get-tuple-element.88), channel_id=1, source_target_pairs={{0,8},{8,0},{4,12},{12,4},{16,24},{24,16},{20,28},{28,20},{1,9},{9... | collective-permute-start | bytes 786440 | tf_op jit(solution)/shard_map/ppermute | solution.py:22
  28.1 17.0 %collective-permute-start.19 = (bf16[2,128,512]{2,1,0:T(8,128)(2,1)S(1)}, bf16[2,128,512]{2,1,0:T(8,128)(2,1)S(1)}, u32[]{:S(2)}, u32[]{:S(2)}) collective-permute-start(bf16[2,128,512]{2,1,0:T(8,128)(2,1)S(1)} %get-tuple-element.86), channel_id=1, source_target_pairs={{0,8},{8,0},{4,12},{12,4},{16,24},{24,16},{20,28},{28,20},{1,9},{9... | collective-permute-start | bytes 786440 | tf_op jit(solution)/shard_map/ppermute | solution.py:22
  35.4 5.9 %collective-permute-start.7 = (bf16[2,128,512]{2,1,0:T(8,128)(2,1)S(1)}, bf16[2,128,512]{2,1,0:T(8,128)(2,1)S(1)}, u32[]{:S(2)}, u32[]{:S(2)}) collective-permute-start(bf16[2,128,512]{2,1,0:T(8,128)(2,1)S(1)} %fusion.14), channel_id=1, source_target_pairs={{8,16},{12,20},{16,8},{20,12},{9,17},{13,21},{17,9},{21,13},{10,18... | collective-permute-start | bytes 786440 | tf_op jit(solution)/shard_map/ppermute | solution.py:159
  36.7 38.0 %collective-permute-start.1 = (bf16[2,256,512]{2,1,0:T(8,128)(2,1)S(1)}, bf16[2,256,512]{2,1,0:T(8,128)(2,1)}, u32[]{:S(2)}, u32[]{:S(2)}) collective-permute-start(bf16[2,256,512]{2,1,0:T(8,128)(2,1)S(1)} %copy-done.20), channel_id=1, source_target_pairs={{0,4},{4,0},{8,12},{12,8},{16,20},{20,16},{24,28},{28,24},{1,5},{5... | collective-permute-start | bytes 1572872 | tf_op jit(solution)/shard_map/ppermute | solution.py:22
  38.5 20.8 %collective-permute-start.5 = (bf16[2,256,512]{2,1,0:T(8,128)(2,1)S(1)}, bf16[2,256,512]{2,1,0:T(8,128)(2,1)S(1)}, u32[]{:S(2)}, u32[]{:S(2)}) collective-permute-start(bf16[2,256,512]{2,1,0:T(8,128)(2,1)S(1)} %copy-done.21), channel_id=1, source_target_pairs={{0,4},{4,0},{8,12},{12,8},{16,20},{20,16},{24,28},{28,24},{1,5},{5... | collective-permute-start | bytes 1572872 | tf_op jit(solution)/shard_map/ppermute | solution.py:22
  40.6 6.3 %collective-permute-start.3 = (bf16[2,128,512]{2,1,0:T(8,128)(2,1)S(1)}, bf16[2,128,512]{2,1,0:T(8,128)(2,1)S(1)}, u32[]{:S(2)}, u32[]{:S(2)}) collective-permute-start(bf16[2,128,512]{2,1,0:T(8,128)(2,1)S(1)} %fusion.15), channel_id=1, source_target_pairs={{8,16},{12,20},{16,8},{20,12},{9,17},{13,21},{17,9},{21,13},{10,18... | collective-permute-start | bytes 786440 | tf_op jit(solution)/shard_map/ppermute | solution.py:159
  41.2 11.7 %collective-permute-start.8 = (bf16[2,128,512]{2,1,0:T(8,128)(2,1)S(1)}, bf16[2,128,512]{2,1,0:T(8,128)(2,1)S(1)}, u32[]{:S(2)}, u32[]{:S(2)}) collective-permute-start(bf16[2,128,512]{2,1,0:T(8,128)(2,1)S(1)} %collective-permute-done.7), channel_id=1, source_target_pairs={{8,0},{12,4},{16,24},{20,28},{9,1},{13,5},{17,25},{21,29},{10,2},{... | collective-permute-start | bytes 786440 | tf_op jit(solution)/shard_map/ppermute | solution.py:160
  45.1 24.9 %collective-permute-start.13 = (bf16[2,128,512]{2,1,0:T(8,128)(2,1)}, bf16[2,128,512]{2,1,0:T(8,128)(2,1)S(1)}, u32[]{:S(2)}, u32[]{:S(2)}) collective-permute-start(bf16[2,128,512]{2,1,0:T(8,128)(2,1)} %fusion.13), channel_id=1, source_target_pairs={{8,16},{12,20},{16,8},{20,12},{9,17},{13,21},{17,9},{21,13},{10,18... | collective-permute-start | bytes 786440 | tf_op jit(solution)/shard_map/ppermute | solution.py:159
  46.9 23.5 %collective-permute-start.20 = (bf16[2,128,512]{2,1,0:T(8,128)(2,1)}, bf16[2,128,512]{2,1,0:T(8,128)(2,1)S(1)}, u32[]{:S(2)}, u32[]{:S(2)}) collective-permute-start(bf16[2,128,512]{2,1,0:T(8,128)(2,1)} %fusion.12), channel_id=1, source_target_pairs={{8,16},{12,20},{16,8},{20,12},{9,17},{13,21},{17,9},{21,13},{10,18... | collective-permute-start | bytes 786440 | tf_op jit(solution)/shard_map/ppermute | solution.py:159
  53.0 18.7 %collective-permute-start.4 = (bf16[2,128,512]{2,1,0:T(8,128)(2,1)S(1)}, bf16[2,128,512]{2,1,0:T(8,128)(2,1)}, u32[]{:S(2)}, u32[]{:S(2)}) collective-permute-start(bf16[2,128,512]{2,1,0:T(8,128)(2,1)S(1)} %collective-permute-done.3), channel_id=1, source_target_pairs={{8,0},{12,4},{16,24},{20,28},{9,1},{13,5},{17,25},{21,29},{10,2},{... | collective-permute-start | bytes 786440 | tf_op jit(solution)/shard_map/ppermute | solution.py:160
  60.1 64.2 %collective-permute-start.18 = (bf16[2,256,512]{2,1,0:T(8,128)(2,1)S(1)}, bf16[2,256,512]{2,1,0:T(8,128)(2,1)}, u32[]{:S(2)}, u32[]{:S(2)}) collective-permute-start(bf16[2,256,512]{2,1,0:T(8,128)(2,1)S(1)} %copy-done.18), channel_id=1, source_target_pairs={{0,4},{4,0},{8,12},{12,8},{16,20},{20,16},{24,28},{28,24},{1,5},{5... | collective-permute-start | bytes 1572872 | tf_op jit(solution)/shard_map/ppermute | solution.py:22
  70.1 36.1 %collective-permute-start.11 = (bf16[2,256,512]{2,1,0:T(8,128)(2,1)S(1)}, bf16[2,256,512]{2,1,0:T(8,128)(2,1)}, u32[]{:S(2)}, u32[]{:S(2)}) collective-permute-start(bf16[2,256,512]{2,1,0:T(8,128)(2,1)S(1)} %copy-done.19), channel_id=1, source_target_pairs={{0,4},{4,0},{8,12},{12,8},{16,20},{20,16},{24,28},{28,24},{1,5},{5... | collective-permute-start | bytes 1572872 | tf_op jit(solution)/shard_map/ppermute | solution.py:22
  70.4 18.1 %collective-permute-start.14 = (bf16[2,128,512]{2,1,0:T(8,128)(2,1)S(1)}, bf16[2,128,512]{2,1,0:T(8,128)(2,1)S(1)}, u32[]{:S(2)}, u32[]{:S(2)}) collective-permute-start(bf16[2,128,512]{2,1,0:T(8,128)(2,1)S(1)} %collective-permute-done.13), channel_id=1, source_target_pairs={{8,0},{12,4},{16,24},{20,28},{9,1},{13,5},{17,25},{21,29},{10,2},{... | collective-permute-start | bytes 786440 | tf_op jit(solution)/shard_map/ppermute | solution.py:160
  71.7 20.0 %collective-permute-start.21 = (bf16[2,128,512]{2,1,0:T(8,128)(2,1)S(1)}, bf16[2,128,512]{2,1,0:T(8,128)(2,1)S(1)}, u32[]{:S(2)}, u32[]{:S(2)}) collective-permute-start(bf16[2,128,512]{2,1,0:T(8,128)(2,1)S(1)} %collective-permute-done.20), channel_id=1, source_target_pairs={{8,0},{12,4},{16,24},{20,28},{9,1},{13,5},{17,25},{21,29},{10,2},{... | collective-permute-start | bytes 786440 | tf_op jit(solution)/shard_map/ppermute | solution.py:160
  74.7 16.1 %collective-permute-start.15 = (bf16[2,128,512]{2,1,0:T(8,128)(2,1)S(1)}, bf16[2,128,512]{2,1,0:T(8,128)(2,1)S(1)}, u32[]{:S(2)}, u32[]{:S(2)}) collective-permute-start(bf16[2,128,512]{2,1,0:T(8,128)(2,1)S(1)} %convert_element_type.165), channel_id=1, source_target_pairs={{0,8},{4,12},{24,16},{28,20},{1,9},{5,13},{25,17},{29,21},{2,10},{... | collective-permute-start | bytes 786440 | tf_op jit(solution)/shard_map/ppermute | solution.py:186
  88.6 6.1 %collective-permute-start.9 = (bf16[2,128,512]{2,1,0:T(8,128)(2,1)S(1)}, bf16[2,128,512]{2,1,0:T(8,128)(2,1)S(1)}, u32[]{:S(2)}, u32[]{:S(2)}) collective-permute-start(bf16[2,128,512]{2,1,0:T(8,128)(2,1)S(1)} %convert_element_type.158), channel_id=1, source_target_pairs={{0,8},{4,12},{24,16},{28,20},{1,9},{5,13},{25,17},{29,21},{2,10},{... | collective-permute-start | bytes 786440 | tf_op jit(solution)/shard_map/ppermute | solution.py:186
  94.7 6.0 %collective-permute-start.10 = (bf16[2,128,512]{2,1,0:T(8,128)(2,1)S(1)}, bf16[2,128,512]{2,1,0:T(8,128)(2,1)S(1)}, u32[]{:S(2)}, u32[]{:S(2)}) collective-permute-start(bf16[2,128,512]{2,1,0:T(8,128)(2,1)S(1)} %add_convert_fusion.14), channel_id=1, source_target_pairs={{8,16},{12,20},{16,8},{20,12},{9,17},{13,21},{17,9},{21,13},{10,18... | collective-permute-start | bytes 786440 | tf_op jit(solution)/shard_map/ppermute | solution.py:188
  96.0 21.0 %collective-permute-start.23 = (bf16[2,128,512]{2,1,0:T(8,128)(2,1)S(1)}, bf16[2,128,512]{2,1,0:T(8,128)(2,1)S(1)}, u32[]{:S(2)}, u32[]{:S(2)}) collective-permute-start(bf16[2,128,512]{2,1,0:T(8,128)(2,1)S(1)} %add_convert_fusion.11), channel_id=1, source_target_pairs={{0,8},{8,0},{4,12},{12,4},{16,24},{24,16},{20,28},{28,20},{1,9},{9... | collective-permute-start | bytes 786440 | tf_op jit(solution)/shard_map/ppermute | solution.py:22
  101.3 19.3 %collective-permute-start.17 = (bf16[2,128,512]{2,1,0:T(8,128)(2,1)S(1)}, bf16[2,128,512]{2,1,0:T(8,128)(2,1)S(1)}, u32[]{:S(2)}, u32[]{:S(2)}) collective-permute-start(bf16[2,128,512]{2,1,0:T(8,128)(2,1)S(1)} %add_convert_fusion.13), channel_id=1, source_target_pairs={{0,8},{8,0},{4,12},{12,4},{16,24},{24,16},{20,28},{28,20},{1,9},{9... | collective-permute-start | bytes 786440 | tf_op jit(solution)/shard_map/ppermute | solution.py:22
  114.4 23.5 %collective-permute-start.25 = (bf16[2,128,512]{2,1,0:T(8,128)(2,1)S(1)}, bf16[2,128,512]{2,1,0:T(8,128)(2,1)}, u32[]{:S(2)}, u32[]{:S(2)}) collective-permute-start(bf16[2,128,512]{2,1,0:T(8,128)(2,1)S(1)} %convert_element_type.178), channel_id=1, source_target_pairs={{0,8},{4,12},{24,16},{28,20},{1,9},{5,13},{25,17},{29,21},{2,10},{... | collective-permute-start | bytes 786440 | tf_op jit(solution)/shard_map/ppermute | solution.py:186
  119.0 36.8 %collective-permute-start.24 = (bf16[2,256,512]{2,1,0:T(8,128)(2,1)S(1)}, bf16[2,256,512]{2,1,0:T(8,128)(2,1)}, u32[]{:S(2)}, u32[]{:S(2)}) collective-permute-start(bf16[2,256,512]{2,1,0:T(8,128)(2,1)S(1)} %add_convert_fusion.4), channel_id=1, source_target_pairs={{0,4},{4,0},{8,12},{12,8},{16,20},{20,16},{24,28},{28,24},{1,5},{5... | collective-permute-start | bytes 1572872 | tf_op jit(solution)/shard_map/ppermute | solution.py:22
  122.6 34.7 %collective-permute-start.22 = (bf16[2,256,512]{2,1,0:T(8,128)(2,1)S(1)}, bf16[2,256,512]{2,1,0:T(8,128)(2,1)}, u32[]{:S(2)}, u32[]{:S(2)}) collective-permute-start(bf16[2,256,512]{2,1,0:T(8,128)(2,1)S(1)} %add_convert_fusion.6), channel_id=1, source_target_pairs={{0,4},{4,0},{8,12},{12,8},{16,20},{20,16},{24,28},{28,24},{1,5},{5... | collective-permute-start | bytes 1572872 | tf_op jit(solution)/shard_map/ppermute | solution.py:22
  132.5 9.8 %collective-permute-start.29 = (bf16[2,128,512]{2,1,0:T(8,128)(2,1)S(1)}, bf16[2,128,512]{2,1,0:T(8,128)(2,1)S(1)}, u32[]{:S(2)}, u32[]{:S(2)}) collective-permute-start(bf16[2,128,512]{2,1,0:T(8,128)(2,1)S(1)} %convert_element_type.185), channel_id=1, source_target_pairs={{0,8},{4,12},{24,16},{28,20},{1,9},{5,13},{25,17},{29,21},{2,10},{... | collective-permute-start | bytes 786440 | tf_op jit(solution)/shard_map/ppermute | solution.py:186
  135.2 30.3 %collective-permute-start.33 = (bf16[2,256,512]{2,1,0:T(8,128)(2,1)S(1)}, bf16[2,256,512]{2,1,0:T(8,128)(2,1)S(1)}, u32[]{:S(2)}, u32[]{:S(2)}) collective-permute-start(bf16[2,256,512]{2,1,0:T(8,128)(2,1)S(1)} %convert_element_type.192), channel_id=1, source_target_pairs={{0,4},{4,0},{8,12},{12,8},{16,20},{20,16},{24,28},{28,24},{1,5},{5... | collective-permute-start | bytes 1572872 | tf_op jit(solution)/shard_map/ppermute | solution.py:22
  142.4 4.9 %collective-permute-start.30 = (bf16[2,128,512]{2,1,0:T(8,128)(2,1)S(1)}, bf16[2,128,512]{2,1,0:T(8,128)(2,1)S(1)}, u32[]{:S(2)}, u32[]{:S(2)}) collective-permute-start(bf16[2,128,512]{2,1,0:T(8,128)(2,1)S(1)} %add_convert_fusion.8), channel_id=1, source_target_pairs={{8,16},{12,20},{16,8},{20,12},{9,17},{13,21},{17,9},{21,13},{10,18... | collective-permute-start | bytes 786440 | tf_op jit(solution)/shard_map/ppermute | solution.py:188
  144.0 8.1 %collective-permute-start.27 = (bf16[2,128,512]{2,1,0:T(8,128)(2,1)S(1)}, bf16[2,128,512]{2,1,0:T(8,128)(2,1)S(1)}, u32[]{:S(2)}, u32[]{:S(2)}) collective-permute-start(bf16[2,128,512]{2,1,0:T(8,128)(2,1)S(1)} %add_convert_fusion.9), channel_id=1, source_target_pairs={{0,8},{8,0},{4,12},{12,4},{16,24},{24,16},{20,28},{28,20},{1,9},{9... | collective-permute-start | bytes 786440 | tf_op jit(solution)/shard_map/ppermute | solution.py:22
  147.9 10.9 %collective-permute-start.31 = (bf16[2,128,512]{2,1,0:T(8,128)(2,1)S(1)}, bf16[2,128,512]{2,1,0:T(8,128)(2,1)S(1)}, u32[]{:S(2)}, u32[]{:S(2)}) collective-permute-start(bf16[2,128,512]{2,1,0:T(8,128)(2,1)S(1)} %add_convert_fusion.7), channel_id=1, source_target_pairs={{0,8},{8,0},{4,12},{12,4},{16,24},{24,16},{20,28},{28,20},{1,9},{9... | collective-permute-start | bytes 786440 | tf_op jit(solution)/shard_map/ppermute | solution.py:22
  154.2 11.8 %collective-permute-start.28 = (bf16[2,256,512]{2,1,0:T(8,128)(2,1)S(1)}, bf16[2,256,512]{2,1,0:T(8,128)(2,1)S(1)}, u32[]{:S(2)}, u32[]{:S(2)}) collective-permute-start(bf16[2,256,512]{2,1,0:T(8,128)(2,1)S(1)} %add_convert_fusion.2), channel_id=1, source_target_pairs={{0,4},{4,0},{8,12},{12,8},{16,20},{20,16},{24,28},{28,24},{1,5},{5... | collective-permute-start | bytes 1572872 | tf_op jit(solution)/shard_map/ppermute | solution.py:22
  159.8 5.0 %collective-permute-start.32 = (bf16[2,64,512]{2,1,0:T(8,128)(2,1)S(1)}, bf16[2,64,512]{2,1,0:T(8,128)(2,1)S(1)}, u32[]{:S(2)}, u32[]{:S(2)}) collective-permute-start(bf16[2,64,512]{2,1,0:T(8,128)(2,1)S(1)} %fusion.16), channel_id=1, source_target_pairs={{0,4},{4,0},{8,12},{12,8},{16,20},{20,16},{24,28},{28,24},{1,5},{5... | collective-permute-start | bytes 393224 | tf_op jit(solution)/shard_map/ppermute | solution.py:22
  (41 other events, 169.3 us)

commit v16 on v15

--- a/solution.py
+++ b/solution.py
@@ -142,7 +142,8 @@
     spread_own = pool_own.T
     place_mine = placed_pool(POOLED // 2, bits[0])
     place_other = placed_pool(POOLED // 2, 1 - bits[0])
-    pieces = [[], [], [], []]
+    pieces = [[], []]
+    grads_out = [jnp.zeros((leaf_rows, model_width), jnp.bfloat16) for _ in range(2)]
     late = []
     for chunk in range(CHUNKS):
         columns = slice(chunk * chunk_width, (chunk + 1) * chunk_width)
@@ -204,9 +205,13 @@
             pooled_back = partner_2(apply(pick_other, grad).astype(jnp.bfloat16), "seq", 0)
             own_total = own_total + apply(spread_own, pooled_back)
         totals = own_total + from_sibling.astype(jnp.float32)
-        for slot, piece in enumerate((attended, query_grad, totals[0], totals[1])):
+        for slot, piece in enumerate((attended, query_grad)):
             pieces[slot].append(piece)
-    return tuple(jnp.concatenate(p, axis=1).astype(jnp.bfloat16) for p in pieces)
+        for slot in range(2):
+            grads_out[slot] = lax.dynamic_update_slice(
+                grads_out[slot], totals[slot].astype(jnp.bfloat16), (0, columns.start)
+            )
+    return tuple(jnp.concatenate(p, axis=1) for p in pieces[:2]) + tuple(grads_out)
 
 
 def solution(mesh):

time: 171 us -> 170 us (level)
  other arithmetic: 25.3 us -> 23.2 us
    concatenate x4 -> x2, other arithmetic: 4.39 us -> 2.2 us  [body(): jnp.concatenate(p, axis=1)]
    unnamed x78 -> x82, local copies, waits for them, and re-layouts: 3.4 us -> 4.34 us
  transfers between devices with their start and end apart: 34 -> 34, of which waited for: 8 -> 8; matrix products, arithmetic and copies ran while one was open for 28% -> 29% of each run, Pallas kernels for 17% -> 17%
where the time goes in v16:
time: 170 us; the launch traced here: 169 us
  starting transfers between devices  56.5 us (33%)
  Pallas kernels  28.6 us (17%)
  matrix products  27.8 us (16%)
  waiting for transfers between devices  24.9 us (15%)
  other arithmetic  23.2 us (14%)
  local copies, waits for them, and re-layouts  6.05 us (4%)
  between operations  1.71 us (1%)
    ppermute x18, starting transfers between devices, partner_2(): return lax.ppermute(block, axis, route)  34.5 us
    pallas_call x4, Pallas kernels, attention(): pl.pallas_call(functools.partial(attention_kernel, scale=score_scale, par...  28.6 us
    dot_general x33, matrix products, apply(): jnp.einsum('pr,krw->kpw', matrix, rows.astype(jnp.float32), precision=lax...  25.9 us
    ppermute x18, waiting for transfers between devices, partner_2(): return lax.ppermute(block, axis, route)  17.3 us
    ppermute x4, starting transfers between devices, body(): gathered = lax.ppermute(sends[step_level], 'seq', back)  11 us
    ppermute x4, waiting for transfers between devices, body(): passed = lax.ppermute(crossed, 'seq', outer_pairs(seq_count, step_level))  5.39 us
    ppermute x4, starting transfers between devices, body(): passed = lax.ppermute(crossed, 'seq', outer_pairs(seq_count, step_level))  5.15 us
    convert_element_type x8, other arithmetic, body(): sends[step_level] = outgoing.astype(jnp.bfloat16)  4.77 us
  transfers between devices with their start and end apart: 34, of which 8 were waited for; matrix products, arithmetic and copies ran while one was open for 29% of the time, Pallas kernels for 17%

profile of v16, /device:TPU:0, one launch (start us, length us, event | category | flops | bytes accessed | tf_op | source)
XLA Modules:
  0.0 168.8 jit_solution(1830237642649375863)
XLA Ops:
  0.7 1.6 convolution_bitcast_fusion
  3.5 3.0 %collective-permute-start = (bf16[2,64,2048]{2,1,0:T(8,128)(2,1)}, bf16[2,64,2048]{2,1,0:T(8,128)(2,1)}, u32[]{:S(2)}, u32[]{:S(2)}) collective-permute-start(bf16[2,64,2048]{2,1,0:T(8,128)(2,1)} %fusion.17), channel_id=1, source_target_pairs={{0,4},{4,0},{8,12},{12,8},{16,20},{20,16},{24,28},{28,24},{1,5},{5... | collective-permute-start | bytes 1572872 | tf_op jit(solution)/shard_map/ppermute | solution.py:22
  9.6 2.0 %pad_maximum_fusion.5.refs_0_ = bf16[2,256,512]{2,1,0:T(8,128)(2,1)} fusion(bf16[1,256,512]{2,1,0:T(8,128)(2,1)} %get-tuple-element.70, bf16[1,256,512]{2,1,0:T(8,128)(2,1)} %get-tuple-element.93), kind=kLoop, calls=%fused_computation.65 | loop fusion | flops 262144 | bytes 1048576 | tf_op jit(solution)/shard_map/stack | solution.py:150
  15.4 3.3 %collective-permute-done = bf16[2,64,2048]{2,1,0:T(8,128)(2,1)} collective-permute-done((bf16[2,64,2048]{2,1,0:T(8,128)(2,1)}, bf16[2,64,2048]{2,1,0:T(8,128)(2,1)}, u32[]{:S(2)}, u32[]{:S(2)}) %collective-permute-start) | collective-permute-done | bytes 524320 | tf_op jit(solution)/shard_map/ppermute | solution.py:22
  20.0 1.9 %collective-permute-start.2 = (bf16[2,128,512]{2,1,0:T(8,128)(2,1)S(1)}, bf16[2,128,512]{2,1,0:T(8,128)(2,1)S(1)}, u32[]{:S(2)}, u32[]{:S(2)}) collective-permute-start(bf16[2,128,512]{2,1,0:T(8,128)(2,1)S(1)} %get-tuple-element.84), channel_id=1, source_target_pairs={{0,8},{8,0},{4,12},{12,4},{16,24},{24,16},{20,28},{28,20},{1,9},{9... | collective-permute-start | bytes 786440 | tf_op jit(solution)/shard_map/ppermute | solution.py:22
  23.5 1.3 fusion.356
  24.9 1.9 %collective-permute-start.12 = (bf16[2,128,512]{2,1,0:T(8,128)(2,1)S(1)}, bf16[2,128,512]{2,1,0:T(8,128)(2,1)S(1)}, u32[]{:S(2)}, u32[]{:S(2)}) collective-permute-start(bf16[2,128,512]{2,1,0:T(8,128)(2,1)S(1)} %get-tuple-element.88), channel_id=1, source_target_pairs={{0,8},{8,0},{4,12},{12,4},{16,24},{24,16},{20,28},{28,20},{1,9},{9... | collective-permute-start | bytes 786440 | tf_op jit(solution)/shard_map/ppermute | solution.py:22
  30.2 4.7 %collective-permute-done.6.refs_2_ = bf16[2,128,512]{2,1,0:T(8,128)(2,1)S(1)} collective-permute-done((bf16[2,128,512]{2,1,0:T(8,128)(2,1)S(1)}, bf16[2,128,512]{2,1,0:T(8,128)(2,1)S(1)}, u32[]{:S(2)}, u32[]{:S(2)}) %collective-permute-start.6) | collective-permute-done | bytes 262176 | tf_op jit(solution)/shard_map/ppermute | solution.py:22
  36.7 1.8 %collective-permute-start.1 = (bf16[2,256,512]{2,1,0:T(8,128)(2,1)S(1)}, bf16[2,256,512]{2,1,0:T(8,128)(2,1)}, u32[]{:S(2)}, u32[]{:S(2)}) collective-permute-start(bf16[2,256,512]{2,1,0:T(8,128)(2,1)S(1)} %copy-done.22), channel_id=1, source_target_pairs={{0,4},{4,0},{8,12},{12,8},{16,20},{20,16},{24,28},{28,24},{1,5},{5... | collective-permute-start | bytes 1572872 | tf_op jit(solution)/shard_map/ppermute | solution.py:22
  43.7 1.4 collective-permute-done.19.refs_2_
  47.6 5.4 %collective-permute-done.8 = bf16[2,128,512]{2,1,0:T(8,128)(2,1)S(1)} collective-permute-done((bf16[2,128,512]{2,1,0:T(8,128)(2,1)S(1)}, bf16[2,128,512]{2,1,0:T(8,128)(2,1)S(1)}, u32[]{:S(2)}, u32[]{:S(2)}) %collective-permute-start.8) | collective-permute-done | bytes 262176 | tf_op jit(solution)/shard_map/ppermute | solution.py:161
  55.0 4.3 %collective-permute-done.5.refs_1_ = bf16[2,256,512]{2,1,0:T(8,128)(2,1)S(1)} collective-permute-done((bf16[2,256,512]{2,1,0:T(8,128)(2,1)S(1)}, bf16[2,256,512]{2,1,0:T(8,128)(2,1)S(1)}, u32[]{:S(2)}, u32[]{:S(2)}) %collective-permute-start.5) | collective-permute-done | bytes 524320 | tf_op jit(solution)/shard_map/ppermute | solution.py:22
  60.1 1.8 %collective-permute-start.18 = (bf16[2,256,512]{2,1,0:T(8,128)(2,1)S(1)}, bf16[2,256,512]{2,1,0:T(8,128)(2,1)}, u32[]{:S(2)}, u32[]{:S(2)}) collective-permute-start(bf16[2,256,512]{2,1,0:T(8,128)(2,1)S(1)} %copy-done.20), channel_id=1, source_target_pairs={{0,4},{4,0},{8,12},{12,8},{16,20},{20,16},{24,28},{28,24},{1,5},{5... | collective-permute-start | bytes 1572872 | tf_op jit(solution)/shard_map/ppermute | solution.py:22
  61.8 7.1 %shard_map.76 = (bf16[256,512]{1,0:T(8,128)(2,1)}, bf16[256,512]{1,0:T(8,128)(2,1)}, f32[2,256,512]{2,1,0:T(8,128)}, f32[2,256,512]{2,1,0:T(8,128)}, f32[2,128,512]{2,1,0:T(8,128)}, /*index=5*/f32[2,128,512]{2,1,0:T(8,128)}) custom-call(f32[1,768]{1,0:T(1,128)} %constant.104.clone.1.bias_ref, bf16[256,2048]{1,0:T(8,128)(2,1)} %q_ref.7, ...), custom_call_target="tpu_custom_call" | custom-call | flops 1207959552 | bytes 5767168 | tf_op jit(solution)/shard_map/pallas_call | solution.py:72
  73.0 1.7 broadcast_select_fusion.3.refs_3_
  74.7 5.6 %collective-permute-start.15 = (bf16[2,128,512]{2,1,0:T(8,128)(2,1)S(1)}, bf16[2,128,512]{2,1,0:T(8,128)(2,1)S(1)}, u32[]{:S(2)}, u32[]{:S(2)}) collective-permute-start(bf16[2,128,512]{2,1,0:T(8,128)(2,1)S(1)} %convert_element_type.195), channel_id=1, source_target_pairs={{0,8},{4,12},{24,16},{28,20},{1,9},{5,13},{25,17},{29,21},{2,10},{... | collective-permute-start | bytes 786440 | tf_op jit(solution)/shard_map/ppermute | solution.py:187
  80.3 7.1 %shard_map.75 = (bf16[256,512]{1,0:T(8,128)(2,1)}, bf16[256,512]{1,0:T(8,128)(2,1)}, f32[2,256,512]{2,1,0:T(8,128)}, f32[2,256,512]{2,1,0:T(8,128)}, f32[2,128,512]{2,1,0:T(8,128)}, /*index=5*/f32[2,128,512]{2,1,0:T(8,128)}) custom-call(f32[1,768]{1,0:T(1,128)} %constant.104.clone.1.bias_ref, bf16[256,2048]{1,0:T(8,128)(2,1)} %q_ref.7, ...), custom_call_target="tpu_custom_call" | custom-call | flops 1207959552 | bytes 5767168 | tf_op jit(solution)/shard_map/pallas_call | solution.py:72
  88.6 1.5 collective-permute-start.9
  92.5 2.2 %collective-permute-done.9 = bf16[2,128,512]{2,1,0:T(8,128)(2,1)S(1)} collective-permute-done((bf16[2,128,512]{2,1,0:T(8,128)(2,1)S(1)}, bf16[2,128,512]{2,1,0:T(8,128)(2,1)S(1)}, u32[]{:S(2)}, u32[]{:S(2)}) %collective-permute-start.9) | collective-permute-done | bytes 262176 | tf_op jit(solution)/shard_map/ppermute | solution.py:187
  96.1 4.6 %collective-permute-start.23 = (bf16[2,128,512]{2,1,0:T(8,128)(2,1)S(1)}, bf16[2,128,512]{2,1,0:T(8,128)(2,1)S(1)}, u32[]{:S(2)}, u32[]{:S(2)}) collective-permute-start(bf16[2,128,512]{2,1,0:T(8,128)(2,1)S(1)} %add_convert_fusion.11), channel_id=1, source_target_pairs={{0,8},{8,0},{4,12},{12,4},{16,24},{24,16},{20,28},{28,20},{1,9},{9... | collective-permute-start | bytes 786440 | tf_op jit(solution)/shard_map/ppermute | solution.py:22
  101.3 4.9 %collective-permute-start.17 = (bf16[2,128,512]{2,1,0:T(8,128)(2,1)S(1)}, bf16[2,128,512]{2,1,0:T(8,128)(2,1)S(1)}, u32[]{:S(2)}, u32[]{:S(2)}) collective-permute-start(bf16[2,128,512]{2,1,0:T(8,128)(2,1)S(1)} %add_convert_fusion.13), channel_id=1, source_target_pairs={{0,8},{8,0},{4,12},{12,4},{16,24},{24,16},{20,28},{28,20},{1,9},{9... | collective-permute-start | bytes 786440 | tf_op jit(solution)/shard_map/ppermute | solution.py:22
  106.2 7.2 %shard_map.77 = (bf16[256,512]{1,0:T(8,128)(2,1)}, bf16[256,512]{1,0:T(8,128)(2,1)}, f32[2,256,512]{2,1,0:T(8,128)}, f32[2,256,512]{2,1,0:T(8,128)}, f32[2,128,512]{2,1,0:T(8,128)}, /*index=5*/f32[2,128,512]{2,1,0:T(8,128)}) custom-call(f32[1,768]{1,0:T(1,128)} %constant.104.clone.1.bias_ref, bf16[256,2048]{1,0:T(8,128)(2,1)} %q_ref.7, ...), custom_call_target="tpu_custom_call" | custom-call | flops 1207959552 | bytes 5767168 | tf_op jit(solution)/shard_map/pallas_call | solution.py:72
  114.4 2.6 %collective-permute-start.25 = (bf16[2,128,512]{2,1,0:T(8,128)(2,1)S(1)}, bf16[2,128,512]{2,1,0:T(8,128)(2,1)}, u32[]{:S(2)}, u32[]{:S(2)}) collective-permute-start(bf16[2,128,512]{2,1,0:T(8,128)(2,1)S(1)} %convert_element_type.210), channel_id=1, source_target_pairs={{0,8},{4,12},{24,16},{28,20},{1,9},{5,13},{25,17},{29,21},{2,10},{... | collective-permute-start | bytes 786440 | tf_op jit(solution)/shard_map/ppermute | solution.py:187
  119.1 1.6 collective-permute-start.24
  124.3 7.2 %shard_map.78 = (bf16[256,512]{1,0:T(8,128)(2,1)}, bf16[256,512]{1,0:T(8,128)(2,1)}, f32[2,256,512]{2,1,0:T(8,128)}, f32[2,256,512]{2,1,0:T(8,128)}, f32[2,128,512]{2,1,0:T(8,128)}, /*index=5*/f32[2,128,512]{2,1,0:T(8,128)}) custom-call(f32[1,768]{1,0:T(1,128)} %constant.104.clone.1.bias_ref, bf16[256,2048]{1,0:T(8,128)(2,1)} %q_ref.7, ...), custom_call_target="tpu_custom_call" | custom-call | flops 1207959552 | bytes 5767168 | tf_op jit(solution)/shard_map/pallas_call | solution.py:72
  135.2 1.6 collective-permute-start.33
  144.0 3.2 %collective-permute-start.27 = (bf16[2,128,512]{2,1,0:T(8,128)(2,1)S(1)}, bf16[2,128,512]{2,1,0:T(8,128)(2,1)S(1)}, u32[]{:S(2)}, u32[]{:S(2)}) collective-permute-start(bf16[2,128,512]{2,1,0:T(8,128)(2,1)S(1)} %add_convert_fusion.9), channel_id=1, source_target_pairs={{0,8},{8,0},{4,12},{12,4},{16,24},{24,16},{20,28},{28,20},{1,9},{9... | collective-permute-start | bytes 786440 | tf_op jit(solution)/shard_map/ppermute | solution.py:22
  147.9 4.3 %collective-permute-start.31 = (bf16[2,128,512]{2,1,0:T(8,128)(2,1)S(1)}, bf16[2,128,512]{2,1,0:T(8,128)(2,1)S(1)}, u32[]{:S(2)}, u32[]{:S(2)}) collective-permute-start(bf16[2,128,512]{2,1,0:T(8,128)(2,1)S(1)} %add_convert_fusion.7), channel_id=1, source_target_pairs={{0,8},{8,0},{4,12},{12,4},{16,24},{24,16},{20,28},{28,20},{1,9},{9... | collective-permute-start | bytes 786440 | tf_op jit(solution)/shard_map/ppermute | solution.py:22
  155.9 1.4 add_convert_fusion.3
  157.4 1.4 add_convert_fusion.5
  160.1 1.6 collective-permute-start.32
  162.8 2.4 %collective-permute-done.32 = bf16[2,64,512]{2,1,0:T(8,128)(2,1)S(1)} collective-permute-done((bf16[2,64,512]{2,1,0:T(8,128)(2,1)S(1)}, bf16[2,64,512]{2,1,0:T(8,128)(2,1)S(1)}, u32[]{:S(2)}, u32[]{:S(2)}) %collective-permute-start.32) | collective-permute-done | bytes 131104 | tf_op jit(solution)/shard_map/ppermute | solution.py:22
  (206 shorter events, 63.7 us)
Async XLA Ops:
  3.5 15.2 %collective-permute-start = (bf16[2,64,2048]{2,1,0:T(8,128)(2,1)}, bf16[2,64,2048]{2,1,0:T(8,128)(2,1)}, u32[]{:S(2)}, u32[]{:S(2)}) collective-permute-start(bf16[2,64,2048]{2,1,0:T(8,128)(2,1)} %fusion.17), channel_id=1, source_target_pairs={{0,4},{4,0},{8,12},{12,8},{16,20},{20,16},{24,28},{28,24},{1,5},{5... | collective-permute-start | bytes 1572872 | tf_op jit(solution)/shard_map/ppermute | solution.py:22
  20.0 18.5 %collective-permute-start.2 = (bf16[2,128,512]{2,1,0:T(8,128)(2,1)S(1)}, bf16[2,128,512]{2,1,0:T(8,128)(2,1)S(1)}, u32[]{:S(2)}, u32[]{:S(2)}) collective-permute-start(bf16[2,128,512]{2,1,0:T(8,128)(2,1)S(1)} %get-tuple-element.84), channel_id=1, source_target_pairs={{0,8},{8,0},{4,12},{12,4},{16,24},{24,16},{20,28},{28,20},{1,9},{9... | collective-permute-start | bytes 786440 | tf_op jit(solution)/shard_map/ppermute | solution.py:22
  23.2 11.7 %collective-permute-start.6 = (bf16[2,128,512]{2,1,0:T(8,128)(2,1)S(1)}, bf16[2,128,512]{2,1,0:T(8,128)(2,1)S(1)}, u32[]{:S(2)}, u32[]{:S(2)}) collective-permute-start(bf16[2,128,512]{2,1,0:T(8,128)(2,1)S(1)} %get-tuple-element.82), channel_id=1, source_target_pairs={{0,8},{8,0},{4,12},{12,4},{16,24},{24,16},{20,28},{28,20},{1,9},{9... | collective-permute-start | bytes 786440 | tf_op jit(solution)/shard_map/ppermute | solution.py:22
  24.9 15.7 %collective-permute-start.12 = (bf16[2,128,512]{2,1,0:T(8,128)(2,1)S(1)}, bf16[2,128,512]{2,1,0:T(8,128)(2,1)S(1)}, u32[]{:S(2)}, u32[]{:S(2)}) collective-permute-start(bf16[2,128,512]{2,1,0:T(8,128)(2,1)S(1)} %get-tuple-element.88), channel_id=1, source_target_pairs={{0,8},{8,0},{4,12},{12,4},{16,24},{24,16},{20,28},{28,20},{1,9},{9... | collective-permute-start | bytes 786440 | tf_op jit(solution)/shard_map/ppermute | solution.py:22
  28.1 17.0 %collective-permute-start.19 = (bf16[2,128,512]{2,1,0:T(8,128)(2,1)S(1)}, bf16[2,128,512]{2,1,0:T(8,128)(2,1)S(1)}, u32[]{:S(2)}, u32[]{:S(2)}) collective-permute-start(bf16[2,128,512]{2,1,0:T(8,128)(2,1)S(1)} %get-tuple-element.86), channel_id=1, source_target_pairs={{0,8},{8,0},{4,12},{12,4},{16,24},{24,16},{20,28},{28,20},{1,9},{9... | collective-permute-start | bytes 786440 | tf_op jit(solution)/shard_map/ppermute | solution.py:22
  35.4 5.9 %collective-permute-start.7 = (bf16[2,128,512]{2,1,0:T(8,128)(2,1)S(1)}, bf16[2,128,512]{2,1,0:T(8,128)(2,1)S(1)}, u32[]{:S(2)}, u32[]{:S(2)}) collective-permute-start(bf16[2,128,512]{2,1,0:T(8,128)(2,1)S(1)} %fusion.14), channel_id=1, source_target_pairs={{8,16},{12,20},{16,8},{20,12},{9,17},{13,21},{17,9},{21,13},{10,18... | collective-permute-start | bytes 786440 | tf_op jit(solution)/shard_map/ppermute | solution.py:160
  36.7 38.0 %collective-permute-start.1 = (bf16[2,256,512]{2,1,0:T(8,128)(2,1)S(1)}, bf16[2,256,512]{2,1,0:T(8,128)(2,1)}, u32[]{:S(2)}, u32[]{:S(2)}) collective-permute-start(bf16[2,256,512]{2,1,0:T(8,128)(2,1)S(1)} %copy-done.22), channel_id=1, source_target_pairs={{0,4},{4,0},{8,12},{12,8},{16,20},{20,16},{24,28},{28,24},{1,5},{5... | collective-permute-start | bytes 1572872 | tf_op jit(solution)/shard_map/ppermute | solution.py:22
  38.5 20.8 %collective-permute-start.5 = (bf16[2,256,512]{2,1,0:T(8,128)(2,1)S(1)}, bf16[2,256,512]{2,1,0:T(8,128)(2,1)S(1)}, u32[]{:S(2)}, u32[]{:S(2)}) collective-permute-start(bf16[2,256,512]{2,1,0:T(8,128)(2,1)S(1)} %copy-done.23), channel_id=1, source_target_pairs={{0,4},{4,0},{8,12},{12,8},{16,20},{20,16},{24,28},{28,24},{1,5},{5... | collective-permute-start | bytes 1572872 | tf_op jit(solution)/shard_map/ppermute | solution.py:22
  40.6 6.4 %collective-permute-start.3 = (bf16[2,128,512]{2,1,0:T(8,128)(2,1)S(1)}, bf16[2,128,512]{2,1,0:T(8,128)(2,1)S(1)}, u32[]{:S(2)}, u32[]{:S(2)}) collective-permute-start(bf16[2,128,512]{2,1,0:T(8,128)(2,1)S(1)} %fusion.15), channel_id=1, source_target_pairs={{8,16},{12,20},{16,8},{20,12},{9,17},{13,21},{17,9},{21,13},{10,18... | collective-permute-start | bytes 786440 | tf_op jit(solution)/shard_map/ppermute | solution.py:160
  41.2 11.7 %collective-permute-start.8 = (bf16[2,128,512]{2,1,0:T(8,128)(2,1)S(1)}, bf16[2,128,512]{2,1,0:T(8,128)(2,1)S(1)}, u32[]{:S(2)}, u32[]{:S(2)}) collective-permute-start(bf16[2,128,512]{2,1,0:T(8,128)(2,1)S(1)} %collective-permute-done.7), channel_id=1, source_target_pairs={{8,0},{12,4},{16,24},{20,28},{9,1},{13,5},{17,25},{21,29},{10,2},{... | collective-permute-start | bytes 786440 | tf_op jit(solution)/shard_map/ppermute | solution.py:161
  45.1 24.9 %collective-permute-start.13 = (bf16[2,128,512]{2,1,0:T(8,128)(2,1)}, bf16[2,128,512]{2,1,0:T(8,128)(2,1)S(1)}, u32[]{:S(2)}, u32[]{:S(2)}) collective-permute-start(bf16[2,128,512]{2,1,0:T(8,128)(2,1)} %fusion.13), channel_id=1, source_target_pairs={{8,16},{12,20},{16,8},{20,12},{9,17},{13,21},{17,9},{21,13},{10,18... | collective-permute-start | bytes 786440 | tf_op jit(solution)/shard_map/ppermute | solution.py:160
  46.9 23.5 %collective-permute-start.20 = (bf16[2,128,512]{2,1,0:T(8,128)(2,1)}, bf16[2,128,512]{2,1,0:T(8,128)(2,1)S(1)}, u32[]{:S(2)}, u32[]{:S(2)}) collective-permute-start(bf16[2,128,512]{2,1,0:T(8,128)(2,1)} %fusion.12), channel_id=1, source_target_pairs={{8,16},{12,20},{16,8},{20,12},{9,17},{13,21},{17,9},{21,13},{10,18... | collective-permute-start | bytes 786440 | tf_op jit(solution)/shard_map/ppermute | solution.py:160
  53.0 18.7 %collective-permute-start.4 = (bf16[2,128,512]{2,1,0:T(8,128)(2,1)S(1)}, bf16[2,128,512]{2,1,0:T(8,128)(2,1)}, u32[]{:S(2)}, u32[]{:S(2)}) collective-permute-start(bf16[2,128,512]{2,1,0:T(8,128)(2,1)S(1)} %collective-permute-done.3), channel_id=1, source_target_pairs={{8,0},{12,4},{16,24},{20,28},{9,1},{13,5},{17,25},{21,29},{10,2},{... | collective-permute-start | bytes 786440 | tf_op jit(solution)/shard_map/ppermute | solution.py:161
  60.1 64.2 %collective-permute-start.18 = (bf16[2,256,512]{2,1,0:T(8,128)(2,1)S(1)}, bf16[2,256,512]{2,1,0:T(8,128)(2,1)}, u32[]{:S(2)}, u32[]{:S(2)}) collective-permute-start(bf16[2,256,512]{2,1,0:T(8,128)(2,1)S(1)} %copy-done.20), channel_id=1, source_target_pairs={{0,4},{4,0},{8,12},{12,8},{16,20},{20,16},{24,28},{28,24},{1,5},{5... | collective-permute-start | bytes 1572872 | tf_op jit(solution)/shard_map/ppermute | solution.py:22
  70.1 36.1 %collective-permute-start.11 = (bf16[2,256,512]{2,1,0:T(8,128)(2,1)S(1)}, bf16[2,256,512]{2,1,0:T(8,128)(2,1)}, u32[]{:S(2)}, u32[]{:S(2)}) collective-permute-start(bf16[2,256,512]{2,1,0:T(8,128)(2,1)S(1)} %copy-done.21), channel_id=1, source_target_pairs={{0,4},{4,0},{8,12},{12,8},{16,20},{20,16},{24,28},{28,24},{1,5},{5... | collective-permute-start | bytes 1572872 | tf_op jit(solution)/shard_map/ppermute | solution.py:22
  70.4 18.1 %collective-permute-start.14 = (bf16[2,128,512]{2,1,0:T(8,128)(2,1)S(1)}, bf16[2,128,512]{2,1,0:T(8,128)(2,1)S(1)}, u32[]{:S(2)}, u32[]{:S(2)}) collective-permute-start(bf16[2,128,512]{2,1,0:T(8,128)(2,1)S(1)} %collective-permute-done.13), channel_id=1, source_target_pairs={{8,0},{12,4},{16,24},{20,28},{9,1},{13,5},{17,25},{21,29},{10,2},{... | collective-permute-start | bytes 786440 | tf_op jit(solution)/shard_map/ppermute | solution.py:161
  71.7 20.0 %collective-permute-start.21 = (bf16[2,128,512]{2,1,0:T(8,128)(2,1)S(1)}, bf16[2,128,512]{2,1,0:T(8,128)(2,1)S(1)}, u32[]{:S(2)}, u32[]{:S(2)}) collective-permute-start(bf16[2,128,512]{2,1,0:T(8,128)(2,1)S(1)} %collective-permute-done.20), channel_id=1, source_target_pairs={{8,0},{12,4},{16,24},{20,28},{9,1},{13,5},{17,25},{21,29},{10,2},{... | collective-permute-start | bytes 786440 | tf_op jit(solution)/shard_map/ppermute | solution.py:161
  74.7 16.1 %collective-permute-start.15 = (bf16[2,128,512]{2,1,0:T(8,128)(2,1)S(1)}, bf16[2,128,512]{2,1,0:T(8,128)(2,1)S(1)}, u32[]{:S(2)}, u32[]{:S(2)}) collective-permute-start(bf16[2,128,512]{2,1,0:T(8,128)(2,1)S(1)} %convert_element_type.195), channel_id=1, source_target_pairs={{0,8},{4,12},{24,16},{28,20},{1,9},{5,13},{25,17},{29,21},{2,10},{... | collective-permute-start | bytes 786440 | tf_op jit(solution)/shard_map/ppermute | solution.py:187
  88.6 6.1 %collective-permute-start.9 = (bf16[2,128,512]{2,1,0:T(8,128)(2,1)S(1)}, bf16[2,128,512]{2,1,0:T(8,128)(2,1)S(1)}, u32[]{:S(2)}, u32[]{:S(2)}) collective-permute-start(bf16[2,128,512]{2,1,0:T(8,128)(2,1)S(1)} %convert_element_type.188), channel_id=1, source_target_pairs={{0,8},{4,12},{24,16},{28,20},{1,9},{5,13},{25,17},{29,21},{2,10},{... | collective-permute-start | bytes 786440 | tf_op jit(solution)/shard_map/ppermute | solution.py:187
  94.7 5.9 %collective-permute-start.10 = (bf16[2,128,512]{2,1,0:T(8,128)(2,1)S(1)}, bf16[2,128,512]{2,1,0:T(8,128)(2,1)S(1)}, u32[]{:S(2)}, u32[]{:S(2)}) collective-permute-start(bf16[2,128,512]{2,1,0:T(8,128)(2,1)S(1)} %add_convert_fusion.14), channel_id=1, source_target_pairs={{8,16},{12,20},{16,8},{20,12},{9,17},{13,21},{17,9},{21,13},{10,18... | collective-permute-start | bytes 786440 | tf_op jit(solution)/shard_map/ppermute | solution.py:189
  96.1 21.0 %collective-permute-start.23 = (bf16[2,128,512]{2,1,0:T(8,128)(2,1)S(1)}, bf16[2,128,512]{2,1,0:T(8,128)(2,1)S(1)}, u32[]{:S(2)}, u32[]{:S(2)}) collective-permute-start(bf16[2,128,512]{2,1,0:T(8,128)(2,1)S(1)} %add_convert_fusion.11), channel_id=1, source_target_pairs={{0,8},{8,0},{4,12},{12,4},{16,24},{24,16},{20,28},{28,20},{1,9},{9... | collective-permute-start | bytes 786440 | tf_op jit(solution)/shard_map/ppermute | solution.py:22
  101.3 19.4 %collective-permute-start.17 = (bf16[2,128,512]{2,1,0:T(8,128)(2,1)S(1)}, bf16[2,128,512]{2,1,0:T(8,128)(2,1)S(1)}, u32[]{:S(2)}, u32[]{:S(2)}) collective-permute-start(bf16[2,128,512]{2,1,0:T(8,128)(2,1)S(1)} %add_convert_fusion.13), channel_id=1, source_target_pairs={{0,8},{8,0},{4,12},{12,4},{16,24},{24,16},{20,28},{28,20},{1,9},{9... | collective-permute-start | bytes 786440 | tf_op jit(solution)/shard_map/ppermute | solution.py:22
  114.4 23.5 %collective-permute-start.25 = (bf16[2,128,512]{2,1,0:T(8,128)(2,1)S(1)}, bf16[2,128,512]{2,1,0:T(8,128)(2,1)}, u32[]{:S(2)}, u32[]{:S(2)}) collective-permute-start(bf16[2,128,512]{2,1,0:T(8,128)(2,1)S(1)} %convert_element_type.210), channel_id=1, source_target_pairs={{0,8},{4,12},{24,16},{28,20},{1,9},{5,13},{25,17},{29,21},{2,10},{... | collective-permute-start | bytes 786440 | tf_op jit(solution)/shard_map/ppermute | solution.py:187
  119.1 36.8 %collective-permute-start.24 = (bf16[2,256,512]{2,1,0:T(8,128)(2,1)S(1)}, bf16[2,256,512]{2,1,0:T(8,128)(2,1)}, u32[]{:S(2)}, u32[]{:S(2)}) collective-permute-start(bf16[2,256,512]{2,1,0:T(8,128)(2,1)S(1)} %add_convert_fusion.4), channel_id=1, source_target_pairs={{0,4},{4,0},{8,12},{12,8},{16,20},{20,16},{24,28},{28,24},{1,5},{5... | collective-permute-start | bytes 1572872 | tf_op jit(solution)/shard_map/ppermute | solution.py:22
  122.6 34.7 %collective-permute-start.22 = (bf16[2,256,512]{2,1,0:T(8,128)(2,1)S(1)}, bf16[2,256,512]{2,1,0:T(8,128)(2,1)}, u32[]{:S(2)}, u32[]{:S(2)}) collective-permute-start(bf16[2,256,512]{2,1,0:T(8,128)(2,1)S(1)} %add_convert_fusion.6), channel_id=1, source_target_pairs={{0,4},{4,0},{8,12},{12,8},{16,20},{20,16},{24,28},{28,24},{1,5},{5... | collective-permute-start | bytes 1572872 | tf_op jit(solution)/shard_map/ppermute | solution.py:22
  132.5 9.8 %collective-permute-start.29 = (bf16[2,128,512]{2,1,0:T(8,128)(2,1)S(1)}, bf16[2,128,512]{2,1,0:T(8,128)(2,1)S(1)}, u32[]{:S(2)}, u32[]{:S(2)}) collective-permute-start(bf16[2,128,512]{2,1,0:T(8,128)(2,1)S(1)} %convert_element_type.218), channel_id=1, source_target_pairs={{0,8},{4,12},{24,16},{28,20},{1,9},{5,13},{25,17},{29,21},{2,10},{... | collective-permute-start | bytes 786440 | tf_op jit(solution)/shard_map/ppermute | solution.py:187
  135.2 30.5 %collective-permute-start.33 = (bf16[2,256,512]{2,1,0:T(8,128)(2,1)S(1)}, bf16[2,256,512]{2,1,0:T(8,128)(2,1)S(1)}, u32[]{:S(2)}, u32[]{:S(2)}) collective-permute-start(bf16[2,256,512]{2,1,0:T(8,128)(2,1)S(1)} %convert_element_type.225), channel_id=1, source_target_pairs={{0,4},{4,0},{8,12},{12,8},{16,20},{20,16},{24,28},{28,24},{1,5},{5... | collective-permute-start | bytes 1572872 | tf_op jit(solution)/shard_map/ppermute | solution.py:22
  142.4 4.9 %collective-permute-start.30 = (bf16[2,128,512]{2,1,0:T(8,128)(2,1)S(1)}, bf16[2,128,512]{2,1,0:T(8,128)(2,1)S(1)}, u32[]{:S(2)}, u32[]{:S(2)}) collective-permute-start(bf16[2,128,512]{2,1,0:T(8,128)(2,1)S(1)} %add_convert_fusion.8), channel_id=1, source_target_pairs={{8,16},{12,20},{16,8},{20,12},{9,17},{13,21},{17,9},{21,13},{10,18... | collective-permute-start | bytes 786440 | tf_op jit(solution)/shard_map/ppermute | solution.py:189
  144.0 8.2 %collective-permute-start.27 = (bf16[2,128,512]{2,1,0:T(8,128)(2,1)S(1)}, bf16[2,128,512]{2,1,0:T(8,128)(2,1)S(1)}, u32[]{:S(2)}, u32[]{:S(2)}) collective-permute-start(bf16[2,128,512]{2,1,0:T(8,128)(2,1)S(1)} %add_convert_fusion.9), channel_id=1, source_target_pairs={{0,8},{8,0},{4,12},{12,4},{16,24},{24,16},{20,28},{28,20},{1,9},{9... | collective-permute-start | bytes 786440 | tf_op jit(solution)/shard_map/ppermute | solution.py:22
  147.9 11.2 %collective-permute-start.31 = (bf16[2,128,512]{2,1,0:T(8,128)(2,1)S(1)}, bf16[2,128,512]{2,1,0:T(8,128)(2,1)S(1)}, u32[]{:S(2)}, u32[]{:S(2)}) collective-permute-start(bf16[2,128,512]{2,1,0:T(8,128)(2,1)S(1)} %add_convert_fusion.7), channel_id=1, source_target_pairs={{0,8},{8,0},{4,12},{12,4},{16,24},{24,16},{20,28},{28,20},{1,9},{9... | collective-permute-start | bytes 786440 | tf_op jit(solution)/shard_map/ppermute | solution.py:22
  154.2 12.0 %collective-permute-start.28 = (bf16[2,256,512]{2,1,0:T(8,128)(2,1)S(1)}, bf16[2,256,512]{2,1,0:T(8,128)(2,1)S(1)}, u32[]{:S(2)}, u32[]{:S(2)}) collective-permute-start(bf16[2,256,512]{2,1,0:T(8,128)(2,1)S(1)} %add_convert_fusion.2), channel_id=1, source_target_pairs={{0,4},{4,0},{8,12},{12,8},{16,20},{20,16},{24,28},{28,24},{1,5},{5... | collective-permute-start | bytes 1572872 | tf_op jit(solution)/shard_map/ppermute | solution.py:22
  160.1 5.0 %collective-permute-start.32 = (bf16[2,64,512]{2,1,0:T(8,128)(2,1)S(1)}, bf16[2,64,512]{2,1,0:T(8,128)(2,1)S(1)}, u32[]{:S(2)}, u32[]{:S(2)}) collective-permute-start(bf16[2,64,512]{2,1,0:T(8,128)(2,1)S(1)} %fusion.16), channel_id=1, source_target_pairs={{0,4},{4,0},{8,12},{12,8},{16,20},{20,16},{24,28},{28,24},{1,5},{5... | collective-permute-start | bytes 393224 | tf_op jit(solution)/shard_map/ppermute | solution.py:22
  (43 other events, 171.6 us)

commit v17 on v16

--- a/solution.py
+++ b/solution.py
@@ -26,10 +26,16 @@
     part_refs = refs[:parts]
     o_ref, dq_ref = refs[parts:parts + 2]
     grad_refs = refs[parts + 2:]
-    q = q_ref[...]
-    do = do_ref[...]
-    k = jnp.concatenate([r[0] for r in part_refs], axis=0)
-    v = jnp.concatenate([r[1] for r in part_refs], axis=0)
+    for head in range(q_ref.shape[1] // HEAD_DIM):
+        cols = slice(head * HEAD_DIM, (head + 1) * HEAD_DIM)
+        head_block(bias_ref, q_ref, do_ref, part_refs, o_ref, dq_ref, grad_refs, cols, scale)
+
+
+def head_block(bias_ref, q_ref, do_ref, part_refs, o_ref, dq_ref, grad_refs, cols, scale):
+    q = q_ref[:, cols]
+    do = do_ref[:, cols]
+    k = jnp.concatenate([r[0, :, cols] for r in part_refs], axis=0)
+    v = jnp.concatenate([r[1, :, cols] for r in part_refs], axis=0)
     scores = (
         lax.dot_general(q, k, (((1,), (1,)), ((), ())), preferred_element_type=jnp.float32) * scale
         + bias_ref[...]
@@ -39,13 +45,13 @@
     weights = shifted * (1.0 / jnp.sum(shifted, axis=-1, keepdims=True))
     weights_low = weights.astype(jnp.bfloat16)
     attended = jnp.dot(weights_low, v, preferred_element_type=jnp.float32).astype(jnp.bfloat16)
-    o_ref[...] = attended
+    o_ref[:, cols] = attended
     row_dot = jnp.sum(
         do.astype(jnp.float32) * attended.astype(jnp.float32), axis=-1, keepdims=True
     )
     weight_grad = lax.dot_general(do, v, (((1,), (1,)), ((), ())), preferred_element_type=jnp.float32)
     score_grad = (weights * (weight_grad - row_dot)).astype(jnp.bfloat16)
-    dq_ref[...] = (
+    dq_ref[:, cols] = (
         jnp.dot(score_grad, k, preferred_element_type=jnp.float32) * scale
     ).astype(jnp.bfloat16)
     by_query = (((0,), (0,)), ((), ()))
@@ -54,8 +60,8 @@
     first = 0
     for r in grad_refs:
         rows = r.shape[1]
-        r[0] = dk[first:first + rows]
-        r[1] = dv[first:first + rows]
+        r[0, :, cols] = dk[first:first + rows]
+        r[1, :, cols] = dv[first:first + rows]
         first += rows
 
 
@@ -64,14 +70,15 @@
     width = parts[0].shape[2]
     key_count = sum(p.shape[1] for p in parts)
     heads = width // HEAD_DIM
-    row_in = pl.BlockSpec((leaf_rows, HEAD_DIM), lambda h: (0, h + head_offset))
-    row_out = pl.BlockSpec((leaf_rows, HEAD_DIM), lambda h: (0, h))
-    part_specs = [pl.BlockSpec((2, p.shape[1], HEAD_DIM), lambda h: (0, 0, h)) for p in parts]
+    step = HEAD_DIM * (2 if heads % 2 == 0 and head_offset % 2 == 0 else 1)
+    row_in = pl.BlockSpec((leaf_rows, step), lambda h: (0, h + head_offset * HEAD_DIM // step))
+    row_out = pl.BlockSpec((leaf_rows, step), lambda h: (0, h))
+    part_specs = [pl.BlockSpec((2, p.shape[1], step), lambda h: (0, 0, h)) for p in parts]
     flops = 12 * leaf_rows * key_count * width
     io_bytes = 2 * (4 * leaf_rows + 2 * key_count) * width + 8 * key_count * width
     return pl.pallas_call(
         functools.partial(attention_kernel, scale=score_scale, parts=len(parts)),
-        grid=(heads,),
+        grid=(width // step,),
         in_specs=[pl.BlockSpec((1, key_count), lambda h: (0, 0)), row_in, row_in] + part_specs,
         out_specs=[row_out, row_out] + part_specs,
         out_shape=[

time: 170 us -> 170 us (level)
  no operation moved by 1% of the time
where the time goes in v17:
time: 170 us; the launch traced here: 169 us
  starting transfers between devices  56.5 us (33%)
  Pallas kernels  28.3 us (17%)
  matrix products  27.9 us (16%)
  waiting for transfers between devices  25.2 us (15%)
  other arithmetic  23.2 us (14%)
  local copies, waits for them, and re-layouts  6.05 us (4%)
  between operations  1.71 us (1%)
    ppermute x18, starting transfers between devices, partner_2(): return lax.ppermute(block, axis, route)  34.5 us
    pallas_call x4, Pallas kernels, attention(): pl.pallas_call(functools.partial(attention_kernel, scale=score_scale, par...  28.3 us
    dot_general x33, matrix products, apply(): jnp.einsum('pr,krw->kpw', matrix, rows.astype(jnp.float32), precision=lax...  26 us
    ppermute x18, waiting for transfers between devices, partner_2(): return lax.ppermute(block, axis, route)  17.3 us
    ppermute x4, starting transfers between devices, body(): gathered = lax.ppermute(sends[step_level], 'seq', back)  11 us
    ppermute x4, waiting for transfers between devices, body(): passed = lax.ppermute(crossed, 'seq', outer_pairs(seq_count, step_level))  5.39 us
    ppermute x4, starting transfers between devices, body(): passed = lax.ppermute(crossed, 'seq', outer_pairs(seq_count, step_level))  5.15 us
    convert_element_type x8, other arithmetic, body(): sends[step_level] = outgoing.astype(jnp.bfloat16)  4.77 us
  transfers between devices with their start and end apart: 34, of which 8 were waited for; matrix products, arithmetic and copies ran while one was open for 29% of the time, Pallas kernels for 17%

profile of v17, /device:TPU:0, one launch (start us, length us, event | category | flops | bytes accessed | tf_op | source)
XLA Modules:
  0.0 168.8 jit_solution(17882230912896276397)
XLA Ops:
  0.7 1.6 convolution_bitcast_fusion
  3.5 3.0 %collective-permute-start = (bf16[2,64,2048]{2,1,0:T(8,128)(2,1)}, bf16[2,64,2048]{2,1,0:T(8,128)(2,1)}, u32[]{:S(2)}, u32[]{:S(2)}) collective-permute-start(bf16[2,64,2048]{2,1,0:T(8,128)(2,1)} %fusion.17), channel_id=1, source_target_pairs={{0,4},{4,0},{8,12},{12,8},{16,20},{20,16},{24,28},{28,24},{1,5},{5... | collective-permute-start | bytes 1572872 | tf_op jit(solution)/shard_map/ppermute | solution.py:22
  9.6 2.0 %pad_maximum_fusion.5.refs_0_ = bf16[2,256,512]{2,1,0:T(8,128)(2,1)} fusion(bf16[1,256,512]{2,1,0:T(8,128)(2,1)} %get-tuple-element.70, bf16[1,256,512]{2,1,0:T(8,128)(2,1)} %get-tuple-element.93), kind=kLoop, calls=%fused_computation.65 | loop fusion | flops 262144 | bytes 1048576 | tf_op jit(solution)/shard_map/stack | solution.py:157
  15.4 3.3 %collective-permute-done = bf16[2,64,2048]{2,1,0:T(8,128)(2,1)} collective-permute-done((bf16[2,64,2048]{2,1,0:T(8,128)(2,1)}, bf16[2,64,2048]{2,1,0:T(8,128)(2,1)}, u32[]{:S(2)}, u32[]{:S(2)}) %collective-permute-start) | collective-permute-done | bytes 524320 | tf_op jit(solution)/shard_map/ppermute | solution.py:22
  18.7 1.3 fusion.354
  20.0 1.9 %collective-permute-start.2 = (bf16[2,128,512]{2,1,0:T(8,128)(2,1)S(1)}, bf16[2,128,512]{2,1,0:T(8,128)(2,1)S(1)}, u32[]{:S(2)}, u32[]{:S(2)}) collective-permute-start(bf16[2,128,512]{2,1,0:T(8,128)(2,1)S(1)} %get-tuple-element.84), channel_id=1, source_target_pairs={{0,8},{8,0},{4,12},{12,4},{16,24},{24,16},{20,28},{28,20},{1,9},{9... | collective-permute-start | bytes 786440 | tf_op jit(solution)/shard_map/ppermute | solution.py:22
  23.5 1.3 fusion.356
  24.9 1.9 %collective-permute-start.12 = (bf16[2,128,512]{2,1,0:T(8,128)(2,1)S(1)}, bf16[2,128,512]{2,1,0:T(8,128)(2,1)S(1)}, u32[]{:S(2)}, u32[]{:S(2)}) collective-permute-start(bf16[2,128,512]{2,1,0:T(8,128)(2,1)S(1)} %get-tuple-element.88), channel_id=1, source_target_pairs={{0,8},{8,0},{4,12},{12,4},{16,24},{24,16},{20,28},{28,20},{1,9},{9... | collective-permute-start | bytes 786440 | tf_op jit(solution)/shard_map/ppermute | solution.py:22
  30.2 4.7 %collective-permute-done.6.refs_2_ = bf16[2,128,512]{2,1,0:T(8,128)(2,1)S(1)} collective-permute-done((bf16[2,128,512]{2,1,0:T(8,128)(2,1)S(1)}, bf16[2,128,512]{2,1,0:T(8,128)(2,1)S(1)}, u32[]{:S(2)}, u32[]{:S(2)}) %collective-permute-start.6) | collective-permute-done | bytes 262176 | tf_op jit(solution)/shard_map/ppermute | solution.py:22
  36.7 1.8 %collective-permute-start.1 = (bf16[2,256,512]{2,1,0:T(8,128)(2,1)S(1)}, bf16[2,256,512]{2,1,0:T(8,128)(2,1)}, u32[]{:S(2)}, u32[]{:S(2)}) collective-permute-start(bf16[2,256,512]{2,1,0:T(8,128)(2,1)S(1)} %copy-done.22), channel_id=1, source_target_pairs={{0,4},{4,0},{8,12},{12,8},{16,20},{20,16},{24,28},{28,24},{1,5},{5... | collective-permute-start | bytes 1572872 | tf_op jit(solution)/shard_map/ppermute | solution.py:22
  43.7 1.4 collective-permute-done.19.refs_2_
  47.6 5.4 %collective-permute-done.8 = bf16[2,128,512]{2,1,0:T(8,128)(2,1)S(1)} collective-permute-done((bf16[2,128,512]{2,1,0:T(8,128)(2,1)S(1)}, bf16[2,128,512]{2,1,0:T(8,128)(2,1)S(1)}, u32[]{:S(2)}, u32[]{:S(2)}) %collective-permute-start.8) | collective-permute-done | bytes 262176 | tf_op jit(solution)/shard_map/ppermute | solution.py:168
  55.0 4.3 %collective-permute-done.5.refs_1_ = bf16[2,256,512]{2,1,0:T(8,128)(2,1)S(1)} collective-permute-done((bf16[2,256,512]{2,1,0:T(8,128)(2,1)S(1)}, bf16[2,256,512]{2,1,0:T(8,128)(2,1)S(1)}, u32[]{:S(2)}, u32[]{:S(2)}) %collective-permute-start.5) | collective-permute-done | bytes 524320 | tf_op jit(solution)/shard_map/ppermute | solution.py:22
  60.1 1.8 %collective-permute-start.18 = (bf16[2,256,512]{2,1,0:T(8,128)(2,1)S(1)}, bf16[2,256,512]{2,1,0:T(8,128)(2,1)}, u32[]{:S(2)}, u32[]{:S(2)}) collective-permute-start(bf16[2,256,512]{2,1,0:T(8,128)(2,1)S(1)} %copy-done.20), channel_id=1, source_target_pairs={{0,4},{4,0},{8,12},{12,8},{16,20},{20,16},{24,28},{28,24},{1,5},{5... | collective-permute-start | bytes 1572872 | tf_op jit(solution)/shard_map/ppermute | solution.py:22
  61.8 7.1 %shard_map.76 = (bf16[256,512]{1,0:T(8,128)(2,1)}, bf16[256,512]{1,0:T(8,128)(2,1)}, f32[2,256,512]{2,1,0:T(8,128)}, f32[2,256,512]{2,1,0:T(8,128)}, f32[2,128,512]{2,1,0:T(8,128)}, /*index=5*/f32[2,128,512]{2,1,0:T(8,128)}) custom-call(f32[1,768]{1,0:T(1,128)} %constant.104.clone.1.bias_ref, bf16[256,2048]{1,0:T(8,128)(2,1)} %q_ref.7, ...), custom_call_target="tpu_custom_call" | custom-call | flops 1207959552 | bytes 5767168 | tf_op jit(solution)/shard_map/pallas_call | solution.py:79
  73.0 1.7 broadcast_select_fusion.3.refs_3_
  74.6 5.8 %collective-permute-start.15 = (bf16[2,128,512]{2,1,0:T(8,128)(2,1)S(1)}, bf16[2,128,512]{2,1,0:T(8,128)(2,1)S(1)}, u32[]{:S(2)}, u32[]{:S(2)}) collective-permute-start(bf16[2,128,512]{2,1,0:T(8,128)(2,1)S(1)} %convert_element_type.195), channel_id=1, source_target_pairs={{0,8},{4,12},{24,16},{28,20},{1,9},{5,13},{25,17},{29,21},{2,10},{... | collective-permute-start | bytes 786440 | tf_op jit(solution)/shard_map/ppermute | solution.py:194
  80.4 7.0 %shard_map.75 = (bf16[256,512]{1,0:T(8,128)(2,1)}, bf16[256,512]{1,0:T(8,128)(2,1)}, f32[2,256,512]{2,1,0:T(8,128)}, f32[2,256,512]{2,1,0:T(8,128)}, f32[2,128,512]{2,1,0:T(8,128)}, /*index=5*/f32[2,128,512]{2,1,0:T(8,128)}) custom-call(f32[1,768]{1,0:T(1,128)} %constant.104.clone.1.bias_ref, bf16[256,2048]{1,0:T(8,128)(2,1)} %q_ref.7, ...), custom_call_target="tpu_custom_call" | custom-call | flops 1207959552 | bytes 5767168 | tf_op jit(solution)/shard_map/pallas_call | solution.py:79
  92.4 2.5 %collective-permute-done.9 = bf16[2,128,512]{2,1,0:T(8,128)(2,1)S(1)} collective-permute-done((bf16[2,128,512]{2,1,0:T(8,128)(2,1)S(1)}, bf16[2,128,512]{2,1,0:T(8,128)(2,1)S(1)}, u32[]{:S(2)}, u32[]{:S(2)}) %collective-permute-start.9) | collective-permute-done | bytes 262176 | tf_op jit(solution)/shard_map/ppermute | solution.py:194
  96.2 4.6 %collective-permute-start.23 = (bf16[2,128,512]{2,1,0:T(8,128)(2,1)S(1)}, bf16[2,128,512]{2,1,0:T(8,128)(2,1)S(1)}, u32[]{:S(2)}, u32[]{:S(2)}) collective-permute-start(bf16[2,128,512]{2,1,0:T(8,128)(2,1)S(1)} %add_convert_fusion.11), channel_id=1, source_target_pairs={{0,8},{8,0},{4,12},{12,4},{16,24},{24,16},{20,28},{28,20},{1,9},{9... | collective-permute-start | bytes 786440 | tf_op jit(solution)/shard_map/ppermute | solution.py:22
  101.5 4.9 %collective-permute-start.17 = (bf16[2,128,512]{2,1,0:T(8,128)(2,1)S(1)}, bf16[2,128,512]{2,1,0:T(8,128)(2,1)S(1)}, u32[]{:S(2)}, u32[]{:S(2)}) collective-permute-start(bf16[2,128,512]{2,1,0:T(8,128)(2,1)S(1)} %add_convert_fusion.13), channel_id=1, source_target_pairs={{0,8},{8,0},{4,12},{12,4},{16,24},{24,16},{20,28},{28,20},{1,9},{9... | collective-permute-start | bytes 786440 | tf_op jit(solution)/shard_map/ppermute | solution.py:22
  106.3 7.1 %shard_map.77 = (bf16[256,512]{1,0:T(8,128)(2,1)}, bf16[256,512]{1,0:T(8,128)(2,1)}, f32[2,256,512]{2,1,0:T(8,128)}, f32[2,256,512]{2,1,0:T(8,128)}, f32[2,128,512]{2,1,0:T(8,128)}, /*index=5*/f32[2,128,512]{2,1,0:T(8,128)}) custom-call(f32[1,768]{1,0:T(1,128)} %constant.104.clone.1.bias_ref, bf16[256,2048]{1,0:T(8,128)(2,1)} %q_ref.7, ...), custom_call_target="tpu_custom_call" | custom-call | flops 1207959552 | bytes 5767168 | tf_op jit(solution)/shard_map/pallas_call | solution.py:79
  114.5 2.6 %collective-permute-start.25 = (bf16[2,128,512]{2,1,0:T(8,128)(2,1)S(1)}, bf16[2,128,512]{2,1,0:T(8,128)(2,1)}, u32[]{:S(2)}, u32[]{:S(2)}) collective-permute-start(bf16[2,128,512]{2,1,0:T(8,128)(2,1)S(1)} %convert_element_type.210), channel_id=1, source_target_pairs={{0,8},{4,12},{24,16},{28,20},{1,9},{5,13},{25,17},{29,21},{2,10},{... | collective-permute-start | bytes 786440 | tf_op jit(solution)/shard_map/ppermute | solution.py:194
  119.2 1.6 collective-permute-start.24
  124.4 7.1 %shard_map.78 = (bf16[256,512]{1,0:T(8,128)(2,1)}, bf16[256,512]{1,0:T(8,128)(2,1)}, f32[2,256,512]{2,1,0:T(8,128)}, f32[2,256,512]{2,1,0:T(8,128)}, f32[2,128,512]{2,1,0:T(8,128)}, /*index=5*/f32[2,128,512]{2,1,0:T(8,128)}) custom-call(f32[1,768]{1,0:T(1,128)} %constant.104.clone.1.bias_ref, bf16[256,2048]{1,0:T(8,128)(2,1)} %q_ref.7, ...), custom_call_target="tpu_custom_call" | custom-call | flops 1207959552 | bytes 5767168 | tf_op jit(solution)/shard_map/pallas_call | solution.py:79
  135.3 1.6 collective-permute-start.33
  144.1 3.2 %collective-permute-start.27 = (bf16[2,128,512]{2,1,0:T(8,128)(2,1)S(1)}, bf16[2,128,512]{2,1,0:T(8,128)(2,1)S(1)}, u32[]{:S(2)}, u32[]{:S(2)}) collective-permute-start(bf16[2,128,512]{2,1,0:T(8,128)(2,1)S(1)} %add_convert_fusion.9), channel_id=1, source_target_pairs={{0,8},{8,0},{4,12},{12,4},{16,24},{24,16},{20,28},{28,20},{1,9},{9... | collective-permute-start | bytes 786440 | tf_op jit(solution)/shard_map/ppermute | solution.py:22
  147.9 4.3 %collective-permute-start.31 = (bf16[2,128,512]{2,1,0:T(8,128)(2,1)S(1)}, bf16[2,128,512]{2,1,0:T(8,128)(2,1)S(1)}, u32[]{:S(2)}, u32[]{:S(2)}) collective-permute-start(bf16[2,128,512]{2,1,0:T(8,128)(2,1)S(1)} %add_convert_fusion.7), channel_id=1, source_target_pairs={{0,8},{8,0},{4,12},{12,4},{16,24},{24,16},{20,28},{28,20},{1,9},{9... | collective-permute-start | bytes 786440 | tf_op jit(solution)/shard_map/ppermute | solution.py:22
  156.0 1.4 add_convert_fusion.3
  157.4 1.4 add_convert_fusion.5
  160.1 1.6 collective-permute-start.32
  162.8 2.4 %collective-permute-done.32 = bf16[2,64,512]{2,1,0:T(8,128)(2,1)S(1)} collective-permute-done((bf16[2,64,512]{2,1,0:T(8,128)(2,1)S(1)}, bf16[2,64,512]{2,1,0:T(8,128)(2,1)S(1)}, u32[]{:S(2)}, u32[]{:S(2)}) %collective-permute-start.32) | collective-permute-done | bytes 131104 | tf_op jit(solution)/shard_map/ppermute | solution.py:22
  (206 shorter events, 63.7 us)
Async XLA Ops:
  3.5 15.2 %collective-permute-start = (bf16[2,64,2048]{2,1,0:T(8,128)(2,1)}, bf16[2,64,2048]{2,1,0:T(8,128)(2,1)}, u32[]{:S(2)}, u32[]{:S(2)}) collective-permute-start(bf16[2,64,2048]{2,1,0:T(8,128)(2,1)} %fusion.17), channel_id=1, source_target_pairs={{0,4},{4,0},{8,12},{12,8},{16,20},{20,16},{24,28},{28,24},{1,5},{5... | collective-permute-start | bytes 1572872 | tf_op jit(solution)/shard_map/ppermute | solution.py:22
  20.0 18.5 %collective-permute-start.2 = (bf16[2,128,512]{2,1,0:T(8,128)(2,1)S(1)}, bf16[2,128,512]{2,1,0:T(8,128)(2,1)S(1)}, u32[]{:S(2)}, u32[]{:S(2)}) collective-permute-start(bf16[2,128,512]{2,1,0:T(8,128)(2,1)S(1)} %get-tuple-element.84), channel_id=1, source_target_pairs={{0,8},{8,0},{4,12},{12,4},{16,24},{24,16},{20,28},{28,20},{1,9},{9... | collective-permute-start | bytes 786440 | tf_op jit(solution)/shard_map/ppermute | solution.py:22
  23.2 11.7 %collective-permute-start.6 = (bf16[2,128,512]{2,1,0:T(8,128)(2,1)S(1)}, bf16[2,128,512]{2,1,0:T(8,128)(2,1)S(1)}, u32[]{:S(2)}, u32[]{:S(2)}) collective-permute-start(bf16[2,128,512]{2,1,0:T(8,128)(2,1)S(1)} %get-tuple-element.82), channel_id=1, source_target_pairs={{0,8},{8,0},{4,12},{12,4},{16,24},{24,16},{20,28},{28,20},{1,9},{9... | collective-permute-start | bytes 786440 | tf_op jit(solution)/shard_map/ppermute | solution.py:22
  24.9 15.7 %collective-permute-start.12 = (bf16[2,128,512]{2,1,0:T(8,128)(2,1)S(1)}, bf16[2,128,512]{2,1,0:T(8,128)(2,1)S(1)}, u32[]{:S(2)}, u32[]{:S(2)}) collective-permute-start(bf16[2,128,512]{2,1,0:T(8,128)(2,1)S(1)} %get-tuple-element.88), channel_id=1, source_target_pairs={{0,8},{8,0},{4,12},{12,4},{16,24},{24,16},{20,28},{28,20},{1,9},{9... | collective-permute-start | bytes 786440 | tf_op jit(solution)/shard_map/ppermute | solution.py:22
  28.1 17.0 %collective-permute-start.19 = (bf16[2,128,512]{2,1,0:T(8,128)(2,1)S(1)}, bf16[2,128,512]{2,1,0:T(8,128)(2,1)S(1)}, u32[]{:S(2)}, u32[]{:S(2)}) collective-permute-start(bf16[2,128,512]{2,1,0:T(8,128)(2,1)S(1)} %get-tuple-element.86), channel_id=1, source_target_pairs={{0,8},{8,0},{4,12},{12,4},{16,24},{24,16},{20,28},{28,20},{1,9},{9... | collective-permute-start | bytes 786440 | tf_op jit(solution)/shard_map/ppermute | solution.py:22
  35.4 5.9 %collective-permute-start.7 = (bf16[2,128,512]{2,1,0:T(8,128)(2,1)S(1)}, bf16[2,128,512]{2,1,0:T(8,128)(2,1)S(1)}, u32[]{:S(2)}, u32[]{:S(2)}) collective-permute-start(bf16[2,128,512]{2,1,0:T(8,128)(2,1)S(1)} %fusion.14), channel_id=1, source_target_pairs={{8,16},{12,20},{16,8},{20,12},{9,17},{13,21},{17,9},{21,13},{10,18... | collective-permute-start | bytes 786440 | tf_op jit(solution)/shard_map/ppermute | solution.py:167
  36.7 37.9 %collective-permute-start.1 = (bf16[2,256,512]{2,1,0:T(8,128)(2,1)S(1)}, bf16[2,256,512]{2,1,0:T(8,128)(2,1)}, u32[]{:S(2)}, u32[]{:S(2)}) collective-permute-start(bf16[2,256,512]{2,1,0:T(8,128)(2,1)S(1)} %copy-done.22), channel_id=1, source_target_pairs={{0,4},{4,0},{8,12},{12,8},{16,20},{20,16},{24,28},{28,24},{1,5},{5... | collective-permute-start | bytes 1572872 | tf_op jit(solution)/shard_map/ppermute | solution.py:22
  38.5 20.8 %collective-permute-start.5 = (bf16[2,256,512]{2,1,0:T(8,128)(2,1)S(1)}, bf16[2,256,512]{2,1,0:T(8,128)(2,1)S(1)}, u32[]{:S(2)}, u32[]{:S(2)}) collective-permute-start(bf16[2,256,512]{2,1,0:T(8,128)(2,1)S(1)} %copy-done.23), channel_id=1, source_target_pairs={{0,4},{4,0},{8,12},{12,8},{16,20},{20,16},{24,28},{28,24},{1,5},{5... | collective-permute-start | bytes 1572872 | tf_op jit(solution)/shard_map/ppermute | solution.py:22
  40.6 6.4 %collective-permute-start.3 = (bf16[2,128,512]{2,1,0:T(8,128)(2,1)S(1)}, bf16[2,128,512]{2,1,0:T(8,128)(2,1)S(1)}, u32[]{:S(2)}, u32[]{:S(2)}) collective-permute-start(bf16[2,128,512]{2,1,0:T(8,128)(2,1)S(1)} %fusion.15), channel_id=1, source_target_pairs={{8,16},{12,20},{16,8},{20,12},{9,17},{13,21},{17,9},{21,13},{10,18... | collective-permute-start | bytes 786440 | tf_op jit(solution)/shard_map/ppermute | solution.py:167
  41.2 11.7 %collective-permute-start.8 = (bf16[2,128,512]{2,1,0:T(8,128)(2,1)S(1)}, bf16[2,128,512]{2,1,0:T(8,128)(2,1)S(1)}, u32[]{:S(2)}, u32[]{:S(2)}) collective-permute-start(bf16[2,128,512]{2,1,0:T(8,128)(2,1)S(1)} %collective-permute-done.7), channel_id=1, source_target_pairs={{8,0},{12,4},{16,24},{20,28},{9,1},{13,5},{17,25},{21,29},{10,2},{... | collective-permute-start | bytes 786440 | tf_op jit(solution)/shard_map/ppermute | solution.py:168
  45.1 24.9 %collective-permute-start.13 = (bf16[2,128,512]{2,1,0:T(8,128)(2,1)}, bf16[2,128,512]{2,1,0:T(8,128)(2,1)S(1)}, u32[]{:S(2)}, u32[]{:S(2)}) collective-permute-start(bf16[2,128,512]{2,1,0:T(8,128)(2,1)} %fusion.13), channel_id=1, source_target_pairs={{8,16},{12,20},{16,8},{20,12},{9,17},{13,21},{17,9},{21,13},{10,18... | collective-permute-start | bytes 786440 | tf_op jit(solution)/shard_map/ppermute | solution.py:167
  46.9 23.4 %collective-permute-start.20 = (bf16[2,128,512]{2,1,0:T(8,128)(2,1)}, bf16[2,128,512]{2,1,0:T(8,128)(2,1)S(1)}, u32[]{:S(2)}, u32[]{:S(2)}) collective-permute-start(bf16[2,128,512]{2,1,0:T(8,128)(2,1)} %fusion.12), channel_id=1, source_target_pairs={{8,16},{12,20},{16,8},{20,12},{9,17},{13,21},{17,9},{21,13},{10,18... | collective-permute-start | bytes 786440 | tf_op jit(solution)/shard_map/ppermute | solution.py:167
  53.0 18.7 %collective-permute-start.4 = (bf16[2,128,512]{2,1,0:T(8,128)(2,1)S(1)}, bf16[2,128,512]{2,1,0:T(8,128)(2,1)}, u32[]{:S(2)}, u32[]{:S(2)}) collective-permute-start(bf16[2,128,512]{2,1,0:T(8,128)(2,1)S(1)} %collective-permute-done.3), channel_id=1, source_target_pairs={{8,0},{12,4},{16,24},{20,28},{9,1},{13,5},{17,25},{21,29},{10,2},{... | collective-permute-start | bytes 786440 | tf_op jit(solution)/shard_map/ppermute | solution.py:168
  60.1 64.3 %collective-permute-start.18 = (bf16[2,256,512]{2,1,0:T(8,128)(2,1)S(1)}, bf16[2,256,512]{2,1,0:T(8,128)(2,1)}, u32[]{:S(2)}, u32[]{:S(2)}) collective-permute-start(bf16[2,256,512]{2,1,0:T(8,128)(2,1)S(1)} %copy-done.20), channel_id=1, source_target_pairs={{0,4},{4,0},{8,12},{12,8},{16,20},{20,16},{24,28},{28,24},{1,5},{5... | collective-permute-start | bytes 1572872 | tf_op jit(solution)/shard_map/ppermute | solution.py:22
  70.0 36.3 %collective-permute-start.11 = (bf16[2,256,512]{2,1,0:T(8,128)(2,1)S(1)}, bf16[2,256,512]{2,1,0:T(8,128)(2,1)}, u32[]{:S(2)}, u32[]{:S(2)}) collective-permute-start(bf16[2,256,512]{2,1,0:T(8,128)(2,1)S(1)} %copy-done.21), channel_id=1, source_target_pairs={{0,4},{4,0},{8,12},{12,8},{16,20},{20,16},{24,28},{28,24},{1,5},{5... | collective-permute-start | bytes 1572872 | tf_op jit(solution)/shard_map/ppermute | solution.py:22
  70.4 18.3 %collective-permute-start.14 = (bf16[2,128,512]{2,1,0:T(8,128)(2,1)S(1)}, bf16[2,128,512]{2,1,0:T(8,128)(2,1)S(1)}, u32[]{:S(2)}, u32[]{:S(2)}) collective-permute-start(bf16[2,128,512]{2,1,0:T(8,128)(2,1)S(1)} %collective-permute-done.13), channel_id=1, source_target_pairs={{8,0},{12,4},{16,24},{20,28},{9,1},{13,5},{17,25},{21,29},{10,2},{... | collective-permute-start | bytes 786440 | tf_op jit(solution)/shard_map/ppermute | solution.py:168
  71.7 20.0 %collective-permute-start.21 = (bf16[2,128,512]{2,1,0:T(8,128)(2,1)S(1)}, bf16[2,128,512]{2,1,0:T(8,128)(2,1)S(1)}, u32[]{:S(2)}, u32[]{:S(2)}) collective-permute-start(bf16[2,128,512]{2,1,0:T(8,128)(2,1)S(1)} %collective-permute-done.20), channel_id=1, source_target_pairs={{8,0},{12,4},{16,24},{20,28},{9,1},{13,5},{17,25},{21,29},{10,2},{... | collective-permute-start | bytes 786440 | tf_op jit(solution)/shard_map/ppermute | solution.py:168
  74.6 16.1 %collective-permute-start.15 = (bf16[2,128,512]{2,1,0:T(8,128)(2,1)S(1)}, bf16[2,128,512]{2,1,0:T(8,128)(2,1)S(1)}, u32[]{:S(2)}, u32[]{:S(2)}) collective-permute-start(bf16[2,128,512]{2,1,0:T(8,128)(2,1)S(1)} %convert_element_type.195), channel_id=1, source_target_pairs={{0,8},{4,12},{24,16},{28,20},{1,9},{5,13},{25,17},{29,21},{2,10},{... | collective-permute-start | bytes 786440 | tf_op jit(solution)/shard_map/ppermute | solution.py:194
  88.6 6.2 %collective-permute-start.9 = (bf16[2,128,512]{2,1,0:T(8,128)(2,1)S(1)}, bf16[2,128,512]{2,1,0:T(8,128)(2,1)S(1)}, u32[]{:S(2)}, u32[]{:S(2)}) collective-permute-start(bf16[2,128,512]{2,1,0:T(8,128)(2,1)S(1)} %convert_element_type.188), channel_id=1, source_target_pairs={{0,8},{4,12},{24,16},{28,20},{1,9},{5,13},{25,17},{29,21},{2,10},{... | collective-permute-start | bytes 786440 | tf_op jit(solution)/shard_map/ppermute | solution.py:194
  94.9 5.9 %collective-permute-start.10 = (bf16[2,128,512]{2,1,0:T(8,128)(2,1)S(1)}, bf16[2,128,512]{2,1,0:T(8,128)(2,1)S(1)}, u32[]{:S(2)}, u32[]{:S(2)}) collective-permute-start(bf16[2,128,512]{2,1,0:T(8,128)(2,1)S(1)} %add_convert_fusion.14), channel_id=1, source_target_pairs={{8,16},{12,20},{16,8},{20,12},{9,17},{13,21},{17,9},{21,13},{10,18... | collective-permute-start | bytes 786440 | tf_op jit(solution)/shard_map/ppermute | solution.py:196
  96.2 20.9 %collective-permute-start.23 = (bf16[2,128,512]{2,1,0:T(8,128)(2,1)S(1)}, bf16[2,128,512]{2,1,0:T(8,128)(2,1)S(1)}, u32[]{:S(2)}, u32[]{:S(2)}) collective-permute-start(bf16[2,128,512]{2,1,0:T(8,128)(2,1)S(1)} %add_convert_fusion.11), channel_id=1, source_target_pairs={{0,8},{8,0},{4,12},{12,4},{16,24},{24,16},{20,28},{28,20},{1,9},{9... | collective-permute-start | bytes 786440 | tf_op jit(solution)/shard_map/ppermute | solution.py:22
  101.5 19.3 %collective-permute-start.17 = (bf16[2,128,512]{2,1,0:T(8,128)(2,1)S(1)}, bf16[2,128,512]{2,1,0:T(8,128)(2,1)S(1)}, u32[]{:S(2)}, u32[]{:S(2)}) collective-permute-start(bf16[2,128,512]{2,1,0:T(8,128)(2,1)S(1)} %add_convert_fusion.13), channel_id=1, source_target_pairs={{0,8},{8,0},{4,12},{12,4},{16,24},{24,16},{20,28},{28,20},{1,9},{9... | collective-permute-start | bytes 786440 | tf_op jit(solution)/shard_map/ppermute | solution.py:22
  114.5 23.4 %collective-permute-start.25 = (bf16[2,128,512]{2,1,0:T(8,128)(2,1)S(1)}, bf16[2,128,512]{2,1,0:T(8,128)(2,1)}, u32[]{:S(2)}, u32[]{:S(2)}) collective-permute-start(bf16[2,128,512]{2,1,0:T(8,128)(2,1)S(1)} %convert_element_type.210), channel_id=1, source_target_pairs={{0,8},{4,12},{24,16},{28,20},{1,9},{5,13},{25,17},{29,21},{2,10},{... | collective-permute-start | bytes 786440 | tf_op jit(solution)/shard_map/ppermute | solution.py:194
  119.2 36.8 %collective-permute-start.24 = (bf16[2,256,512]{2,1,0:T(8,128)(2,1)S(1)}, bf16[2,256,512]{2,1,0:T(8,128)(2,1)}, u32[]{:S(2)}, u32[]{:S(2)}) collective-permute-start(bf16[2,256,512]{2,1,0:T(8,128)(2,1)S(1)} %add_convert_fusion.4), channel_id=1, source_target_pairs={{0,4},{4,0},{8,12},{12,8},{16,20},{20,16},{24,28},{28,24},{1,5},{5... | collective-permute-start | bytes 1572872 | tf_op jit(solution)/shard_map/ppermute | solution.py:22
  122.7 34.7 %collective-permute-start.22 = (bf16[2,256,512]{2,1,0:T(8,128)(2,1)S(1)}, bf16[2,256,512]{2,1,0:T(8,128)(2,1)}, u32[]{:S(2)}, u32[]{:S(2)}) collective-permute-start(bf16[2,256,512]{2,1,0:T(8,128)(2,1)S(1)} %add_convert_fusion.6), channel_id=1, source_target_pairs={{0,4},{4,0},{8,12},{12,8},{16,20},{20,16},{24,28},{28,24},{1,5},{5... | collective-permute-start | bytes 1572872 | tf_op jit(solution)/shard_map/ppermute | solution.py:22
  132.6 9.8 %collective-permute-start.29 = (bf16[2,128,512]{2,1,0:T(8,128)(2,1)S(1)}, bf16[2,128,512]{2,1,0:T(8,128)(2,1)S(1)}, u32[]{:S(2)}, u32[]{:S(2)}) collective-permute-start(bf16[2,128,512]{2,1,0:T(8,128)(2,1)S(1)} %convert_element_type.218), channel_id=1, source_target_pairs={{0,8},{4,12},{24,16},{28,20},{1,9},{5,13},{25,17},{29,21},{2,10},{... | collective-permute-start | bytes 786440 | tf_op jit(solution)/shard_map/ppermute | solution.py:194
  135.3 30.5 %collective-permute-start.33 = (bf16[2,256,512]{2,1,0:T(8,128)(2,1)S(1)}, bf16[2,256,512]{2,1,0:T(8,128)(2,1)S(1)}, u32[]{:S(2)}, u32[]{:S(2)}) collective-permute-start(bf16[2,256,512]{2,1,0:T(8,128)(2,1)S(1)} %convert_element_type.225), channel_id=1, source_target_pairs={{0,4},{4,0},{8,12},{12,8},{16,20},{20,16},{24,28},{28,24},{1,5},{5... | collective-permute-start | bytes 1572872 | tf_op jit(solution)/shard_map/ppermute | solution.py:22
  142.4 4.9 %collective-permute-start.30 = (bf16[2,128,512]{2,1,0:T(8,128)(2,1)S(1)}, bf16[2,128,512]{2,1,0:T(8,128)(2,1)S(1)}, u32[]{:S(2)}, u32[]{:S(2)}) collective-permute-start(bf16[2,128,512]{2,1,0:T(8,128)(2,1)S(1)} %add_convert_fusion.8), channel_id=1, source_target_pairs={{8,16},{12,20},{16,8},{20,12},{9,17},{13,21},{17,9},{21,13},{10,18... | collective-permute-start | bytes 786440 | tf_op jit(solution)/shard_map/ppermute | solution.py:196
  144.1 8.2 %collective-permute-start.27 = (bf16[2,128,512]{2,1,0:T(8,128)(2,1)S(1)}, bf16[2,128,512]{2,1,0:T(8,128)(2,1)S(1)}, u32[]{:S(2)}, u32[]{:S(2)}) collective-permute-start(bf16[2,128,512]{2,1,0:T(8,128)(2,1)S(1)} %add_convert_fusion.9), channel_id=1, source_target_pairs={{0,8},{8,0},{4,12},{12,4},{16,24},{24,16},{20,28},{28,20},{1,9},{9... | collective-permute-start | bytes 786440 | tf_op jit(solution)/shard_map/ppermute | solution.py:22
  147.9 11.2 %collective-permute-start.31 = (bf16[2,128,512]{2,1,0:T(8,128)(2,1)S(1)}, bf16[2,128,512]{2,1,0:T(8,128)(2,1)S(1)}, u32[]{:S(2)}, u32[]{:S(2)}) collective-permute-start(bf16[2,128,512]{2,1,0:T(8,128)(2,1)S(1)} %add_convert_fusion.7), channel_id=1, source_target_pairs={{0,8},{8,0},{4,12},{12,4},{16,24},{24,16},{20,28},{28,20},{1,9},{9... | collective-permute-start | bytes 786440 | tf_op jit(solution)/shard_map/ppermute | solution.py:22
  154.3 12.0 %collective-permute-start.28 = (bf16[2,256,512]{2,1,0:T(8,128)(2,1)S(1)}, bf16[2,256,512]{2,1,0:T(8,128)(2,1)S(1)}, u32[]{:S(2)}, u32[]{:S(2)}) collective-permute-start(bf16[2,256,512]{2,1,0:T(8,128)(2,1)S(1)} %add_convert_fusion.2), channel_id=1, source_target_pairs={{0,4},{4,0},{8,12},{12,8},{16,20},{20,16},{24,28},{28,24},{1,5},{5... | collective-permute-start | bytes 1572872 | tf_op jit(solution)/shard_map/ppermute | solution.py:22
  160.1 5.0 %collective-permute-start.32 = (bf16[2,64,512]{2,1,0:T(8,128)(2,1)S(1)}, bf16[2,64,512]{2,1,0:T(8,128)(2,1)S(1)}, u32[]{:S(2)}, u32[]{:S(2)}) collective-permute-start(bf16[2,64,512]{2,1,0:T(8,128)(2,1)S(1)} %fusion.16), channel_id=1, source_target_pairs={{0,4},{4,0},{8,12},{12,8},{16,20},{20,16},{24,28},{28,24},{1,5},{5... | collective-permute-start | bytes 393224 | tf_op jit(solution)/shard_map/ppermute | solution.py:22
  (43 other events, 172.2 us)

commit v18 on v16

--- a/solution.py
+++ b/solution.py
@@ -166,8 +166,6 @@
         held = own
         if chunk >= 2:
             held = after(held, late[chunk - 2][1])
-        if chunk >= 3:
-            held = after(held, late[chunk - 3][0])
         outs = attention(
             query_rows, out_grad, [held, sibling] + far, key_bias, score_scale,
             chunk * (chunk_width // HEAD_DIM),

time: 170 us -> 174 us (1.024)
  waiting for transfers between devices: 24.9 us -> 32.2 us
  other arithmetic: 23.2 us -> 18.3 us
    ppermute x18, waiting for transfers between devices: 17.3 us -> 27 us  [partner_2(): return lax.ppermute(block, axis, route)]
    another operation x4, other arithmetic: 3.56 us -> 1.33 us
  transfers between devices with their start and end apart: 34 -> 34, of which waited for: 8 -> 10; matrix products, arithmetic and copies ran while one was open for 29% -> 25% of each run, Pallas kernels for 17% -> 17%
where the time goes in v18:
time: 174 us; the launch traced here: 173 us
  starting transfers between devices  57.4 us (33%)
  waiting for transfers between devices  32.2 us (19%)
  Pallas kernels  28.7 us (16%)
  matrix products  27.9 us (16%)
  other arithmetic  18.3 us (11%)
  local copies, waits for them, and re-layouts  6.33 us (4%)
    ppermute x18, starting transfers between devices, partner_2(): return lax.ppermute(block, axis, route)  35.7 us
    pallas_call x4, Pallas kernels, attention(): pl.pallas_call(functools.partial(attention_kernel, scale=score_scale, par...  28.7 us
    ppermute x18, waiting for transfers between devices, partner_2(): return lax.ppermute(block, axis, route)  27 us
    dot_general x33, matrix products, apply(): jnp.einsum('pr,krw->kpw', matrix, rows.astype(jnp.float32), precision=lax...  26 us
    ppermute x4, starting transfers between devices, body(): gathered = lax.ppermute(sends[step_level], 'seq', back)  10.7 us
    ppermute x4, starting transfers between devices, body(): passed = lax.ppermute(crossed, 'seq', outer_pairs(seq_count, step_level))  5.15 us
    convert_element_type x8, other arithmetic, body(): sends[step_level] = outgoing.astype(jnp.bfloat16)  4.84 us
    unnamed x82, local copies, waits for them, and re-layouts  4.64 us
  transfers between devices with their start and end apart: 34, of which 10 were waited for; matrix products, arithmetic and copies ran while one was open for 25% of the time, Pallas kernels for 17%

profile of v18, /device:TPU:0, one launch (start us, length us, event | category | flops | bytes accessed | tf_op | source)
XLA Modules:
  0.0 172.5 jit_solution(15130847070516081984)
XLA Ops:
  0.7 1.6 convolution_bitcast_fusion
  3.5 3.0 %collective-permute-start = (bf16[2,64,2048]{2,1,0:T(8,128)(2,1)}, bf16[2,64,2048]{2,1,0:T(8,128)(2,1)}, u32[]{:S(2)}, u32[]{:S(2)}) collective-permute-start(bf16[2,64,2048]{2,1,0:T(8,128)(2,1)} %fusion.17), channel_id=1, source_target_pairs={{0,4},{4,0},{8,12},{12,8},{16,20},{20,16},{24,28},{28,24},{1,5},{5... | collective-permute-start | bytes 1572872 | tf_op jit(solution)/shard_map/ppermute | solution.py:22
  9.6 2.0 %pad_maximum_fusion.3.refs_0_ = bf16[2,256,512]{2,1,0:T(8,128)(2,1)} fusion(bf16[1,256,512]{2,1,0:T(8,128)(2,1)} %get-tuple-element.68, bf16[1,256,512]{2,1,0:T(8,128)(2,1)} %get-tuple-element.91), kind=kLoop, calls=%fused_computation.63 | loop fusion | flops 262144 | bytes 1048576 | tf_op jit(solution)/shard_map/stack | solution.py:150
  14.7 4.0 %collective-permute-done = bf16[2,64,2048]{2,1,0:T(8,128)(2,1)} collective-permute-done((bf16[2,64,2048]{2,1,0:T(8,128)(2,1)}, bf16[2,64,2048]{2,1,0:T(8,128)(2,1)}, u32[]{:S(2)}, u32[]{:S(2)}) %collective-permute-start) | collective-permute-done | bytes 524320 | tf_op jit(solution)/shard_map/ppermute | solution.py:22
  18.7 1.3 fusion.355
  20.0 1.9 %collective-permute-start.2 = (bf16[2,128,512]{2,1,0:T(8,128)(2,1)S(1)}, bf16[2,128,512]{2,1,0:T(8,128)(2,1)S(1)}, u32[]{:S(2)}, u32[]{:S(2)}) collective-permute-start(bf16[2,128,512]{2,1,0:T(8,128)(2,1)S(1)} %get-tuple-element.84), channel_id=1, source_target_pairs={{0,8},{8,0},{4,12},{12,4},{16,24},{24,16},{20,28},{28,20},{1,9},{9... | collective-permute-start | bytes 786440 | tf_op jit(solution)/shard_map/ppermute | solution.py:22
  23.5 1.3 fusion.356
  24.9 1.9 %collective-permute-start.12 = (bf16[2,128,512]{2,1,0:T(8,128)(2,1)S(1)}, bf16[2,128,512]{2,1,0:T(8,128)(2,1)S(1)}, u32[]{:S(2)}, u32[]{:S(2)}) collective-permute-start(bf16[2,128,512]{2,1,0:T(8,128)(2,1)S(1)} %get-tuple-element.86), channel_id=1, source_target_pairs={{0,8},{8,0},{4,12},{12,4},{16,24},{24,16},{20,28},{28,20},{1,9},{9... | collective-permute-start | bytes 786440 | tf_op jit(solution)/shard_map/ppermute | solution.py:22
  32.0 1.8 %collective-permute-start.5 = (bf16[2,256,512]{2,1,0:T(8,128)(2,1)S(1)}, bf16[2,256,512]{2,1,0:T(8,128)(2,1)}, u32[]{:S(2)}, u32[]{:S(2)}) collective-permute-start(bf16[2,256,512]{2,1,0:T(8,128)(2,1)S(1)} %copy-done.22), channel_id=1, source_target_pairs={{0,4},{4,0},{8,12},{12,8},{16,20},{20,16},{24,28},{28,24},{1,5},{5... | collective-permute-start | bytes 1572872 | tf_op jit(solution)/shard_map/ppermute | solution.py:22
  35.0 1.8 %collective-permute-start.1 = (bf16[2,256,512]{2,1,0:T(8,128)(2,1)S(1)}, bf16[2,256,512]{2,1,0:T(8,128)(2,1)S(1)}, u32[]{:S(2)}, u32[]{:S(2)}) collective-permute-start(bf16[2,256,512]{2,1,0:T(8,128)(2,1)S(1)} %copy-done.23), channel_id=1, source_target_pairs={{0,4},{4,0},{8,12},{12,8},{16,20},{20,16},{24,28},{28,24},{1,5},{5... | collective-permute-start | bytes 1572872 | tf_op jit(solution)/shard_map/ppermute | solution.py:22
  37.1 3.4 %collective-permute-done.12.refs_2_ = bf16[2,128,512]{2,1,0:T(8,128)(2,1)S(1)} collective-permute-done((bf16[2,128,512]{2,1,0:T(8,128)(2,1)S(1)}, bf16[2,128,512]{2,1,0:T(8,128)(2,1)S(1)}, u32[]{:S(2)}, u32[]{:S(2)}) %collective-permute-start.12) | collective-permute-done | bytes 262176 | tf_op jit(solution)/shard_map/ppermute | solution.py:22
  43.7 1.4 collective-permute-done.18.refs_2_
  47.6 3.9 %collective-permute-done.4 = bf16[2,128,512]{2,1,0:T(8,128)(2,1)S(1)} collective-permute-done((bf16[2,128,512]{2,1,0:T(8,128)(2,1)S(1)}, bf16[2,128,512]{2,1,0:T(8,128)(2,1)S(1)}, u32[]{:S(2)}, u32[]{:S(2)}) %collective-permute-start.4) | collective-permute-done | bytes 262176 | tf_op jit(solution)/shard_map/ppermute | solution.py:161
  53.5 1.7 %collective-permute-done.1.refs_1_ = bf16[2,256,512]{2,1,0:T(8,128)(2,1)S(1)} collective-permute-done((bf16[2,256,512]{2,1,0:T(8,128)(2,1)S(1)}, bf16[2,256,512]{2,1,0:T(8,128)(2,1)S(1)}, u32[]{:S(2)}, u32[]{:S(2)}) %collective-permute-start.1) | collective-permute-done | bytes 524320 | tf_op jit(solution)/shard_map/ppermute | solution.py:22
  56.1 1.4 collective-permute-start.11
  57.5 7.2 %shard_map.75 = (bf16[256,512]{1,0:T(8,128)(2,1)}, bf16[256,512]{1,0:T(8,128)(2,1)}, f32[2,256,512]{2,1,0:T(8,128)}, f32[2,256,512]{2,1,0:T(8,128)}, f32[2,128,512]{2,1,0:T(8,128)}, /*index=5*/f32[2,128,512]{2,1,0:T(8,128)}) custom-call(f32[1,768]{1,0:T(1,128)} %constant.104.clone.1.bias_ref, bf16[256,2048]{1,0:T(8,128)(2,1)} %q_ref.7, ...), custom_call_target="tpu_custom_call" | custom-call | flops 1207959552 | bytes 5767168 | tf_op jit(solution)/shard_map/pallas_call | solution.py:72
  69.8 6.0 %collective-permute-start.9 = (bf16[2,128,512]{2,1,0:T(8,128)(2,1)S(1)}, bf16[2,128,512]{2,1,0:T(8,128)(2,1)S(1)}, u32[]{:S(2)}, u32[]{:S(2)}) collective-permute-start(bf16[2,128,512]{2,1,0:T(8,128)(2,1)S(1)} %convert_element_type.188), channel_id=1, source_target_pairs={{0,8},{4,12},{24,16},{28,20},{1,9},{5,13},{25,17},{29,21},{2,10},{... | collective-permute-start | bytes 786440 | tf_op jit(solution)/shard_map/ppermute | solution.py:185
  75.8 7.1 %shard_map.76 = (bf16[256,512]{1,0:T(8,128)(2,1)}, bf16[256,512]{1,0:T(8,128)(2,1)}, f32[2,256,512]{2,1,0:T(8,128)}, f32[2,256,512]{2,1,0:T(8,128)}, f32[2,128,512]{2,1,0:T(8,128)}, /*index=5*/f32[2,128,512]{2,1,0:T(8,128)}) custom-call(f32[1,768]{1,0:T(1,128)} %constant.104.clone.1.bias_ref, bf16[256,2048]{1,0:T(8,128)(2,1)} %q_ref.7, ...), custom_call_target="tpu_custom_call" | custom-call | flops 1207959552 | bytes 5767168 | tf_op jit(solution)/shard_map/pallas_call | solution.py:72
  84.1 1.5 collective-permute-start.15
  90.7 6.9 %collective-permute-start.21 = (bf16[2,128,512]{2,1,0:T(8,128)(2,1)S(1)}, bf16[2,128,512]{2,1,0:T(8,128)(2,1)S(1)}, u32[]{:S(2)}, u32[]{:S(2)}) collective-permute-start(bf16[2,128,512]{2,1,0:T(8,128)(2,1)S(1)} %add_convert_fusion.13), channel_id=1, source_target_pairs={{0,8},{8,0},{4,12},{12,4},{16,24},{24,16},{20,28},{28,20},{1,9},{9... | collective-permute-start | bytes 786440 | tf_op jit(solution)/shard_map/ppermute | solution.py:22
  98.2 2.6 %collective-permute-start.23 = (bf16[2,128,512]{2,1,0:T(8,128)(2,1)S(1)}, bf16[2,128,512]{2,1,0:T(8,128)(2,1)S(1)}, u32[]{:S(2)}, u32[]{:S(2)}) collective-permute-start(bf16[2,128,512]{2,1,0:T(8,128)(2,1)S(1)} %add_convert_fusion.11), channel_id=1, source_target_pairs={{0,8},{8,0},{4,12},{12,4},{16,24},{24,16},{20,28},{28,20},{1,9},{9... | collective-permute-start | bytes 786440 | tf_op jit(solution)/shard_map/ppermute | solution.py:22
  100.8 7.2 %shard_map.77 = (bf16[256,512]{1,0:T(8,128)(2,1)}, bf16[256,512]{1,0:T(8,128)(2,1)}, f32[2,256,512]{2,1,0:T(8,128)}, f32[2,256,512]{2,1,0:T(8,128)}, f32[2,128,512]{2,1,0:T(8,128)}, /*index=5*/f32[2,128,512]{2,1,0:T(8,128)}) custom-call(f32[1,768]{1,0:T(1,128)} %constant.104.clone.1.bias_ref, bf16[256,2048]{1,0:T(8,128)(2,1)} %q_ref.7, ...), custom_call_target="tpu_custom_call" | custom-call | flops 1207959552 | bytes 5767168 | tf_op jit(solution)/shard_map/pallas_call | solution.py:72
  109.0 2.0 %collective-permute-start.25 = (bf16[2,128,512]{2,1,0:T(8,128)(2,1)S(1)}, bf16[2,128,512]{2,1,0:T(8,128)(2,1)S(1)}, u32[]{:S(2)}, u32[]{:S(2)}) collective-permute-start(bf16[2,128,512]{2,1,0:T(8,128)(2,1)S(1)} %convert_element_type.210), channel_id=1, source_target_pairs={{0,8},{4,12},{24,16},{28,20},{1,9},{5,13},{25,17},{29,21},{2,10},{... | collective-permute-start | bytes 786440 | tf_op jit(solution)/shard_map/ppermute | solution.py:185
  111.0 7.1 %shard_map.78 = (bf16[256,512]{1,0:T(8,128)(2,1)}, bf16[256,512]{1,0:T(8,128)(2,1)}, f32[2,256,512]{2,1,0:T(8,128)}, f32[2,256,512]{2,1,0:T(8,128)}, f32[2,128,512]{2,1,0:T(8,128)}, /*index=5*/f32[2,128,512]{2,1,0:T(8,128)}) custom-call(f32[1,768]{1,0:T(1,128)} %constant.104.clone.1.bias_ref, bf16[256,2048]{1,0:T(8,128)(2,1)} %q_ref.7, ...), custom_call_target="tpu_custom_call" | custom-call | flops 1207959552 | bytes 5767168 | tf_op jit(solution)/shard_map/pallas_call | solution.py:72
  122.0 1.6 collective-permute-start.33
  131.7 1.4 collective-permute-start.24
  137.1 3.9 %collective-permute-start.27 = (bf16[2,128,512]{2,1,0:T(8,128)(2,1)S(1)}, bf16[2,128,512]{2,1,0:T(8,128)(2,1)S(1)}, u32[]{:S(2)}, u32[]{:S(2)}) collective-permute-start(bf16[2,128,512]{2,1,0:T(8,128)(2,1)S(1)} %add_convert_fusion.9), channel_id=1, source_target_pairs={{0,8},{8,0},{4,12},{12,4},{16,24},{24,16},{20,28},{28,20},{1,9},{9... | collective-permute-start | bytes 786440 | tf_op jit(solution)/shard_map/ppermute | solution.py:22
  141.6 3.6 %collective-permute-start.31 = (bf16[2,128,512]{2,1,0:T(8,128)(2,1)S(1)}, bf16[2,128,512]{2,1,0:T(8,128)(2,1)S(1)}, u32[]{:S(2)}, u32[]{:S(2)}) collective-permute-start(bf16[2,128,512]{2,1,0:T(8,128)(2,1)S(1)} %add_convert_fusion.7), channel_id=1, source_target_pairs={{0,8},{8,0},{4,12},{12,4},{16,24},{24,16},{20,28},{28,20},{1,9},{9... | collective-permute-start | bytes 786440 | tf_op jit(solution)/shard_map/ppermute | solution.py:22
  145.2 1.5 collective-permute-done.27
  148.7 1.4 collective-permute-start.28
  154.5 4.9 %collective-permute-done.24 = bf16[2,256,512]{2,1,0:T(8,128)(2,1)S(1)} collective-permute-done((bf16[2,256,512]{2,1,0:T(8,128)(2,1)S(1)}, bf16[2,256,512]{2,1,0:T(8,128)(2,1)S(1)}, u32[]{:S(2)}, u32[]{:S(2)}) %collective-permute-start.24) | collective-permute-done | bytes 524320 | tf_op jit(solution)/shard_map/ppermute | solution.py:22
  160.0 8.9 %collective-permute-done.32 = bf16[2,64,512]{2,1,0:T(8,128)(2,1)S(1)} collective-permute-done((bf16[2,64,512]{2,1,0:T(8,128)(2,1)S(1)}, bf16[2,64,512]{2,1,0:T(8,128)(2,1)S(1)}, u32[]{:S(2)}, u32[]{:S(2)}) %collective-permute-start.32) | collective-permute-done | bytes 131104 | tf_op jit(solution)/shard_map/ppermute | solution.py:22
  (206 shorter events, 63.7 us)
Async XLA Ops:
  3.5 15.2 %collective-permute-start = (bf16[2,64,2048]{2,1,0:T(8,128)(2,1)}, bf16[2,64,2048]{2,1,0:T(8,128)(2,1)}, u32[]{:S(2)}, u32[]{:S(2)}) collective-permute-start(bf16[2,64,2048]{2,1,0:T(8,128)(2,1)} %fusion.17), channel_id=1, source_target_pairs={{0,4},{4,0},{8,12},{12,8},{16,20},{20,16},{24,28},{28,24},{1,5},{5... | collective-permute-start | bytes 1572872 | tf_op jit(solution)/shard_map/ppermute | solution.py:22
  20.0 10.2 %collective-permute-start.2 = (bf16[2,128,512]{2,1,0:T(8,128)(2,1)S(1)}, bf16[2,128,512]{2,1,0:T(8,128)(2,1)S(1)}, u32[]{:S(2)}, u32[]{:S(2)}) collective-permute-start(bf16[2,128,512]{2,1,0:T(8,128)(2,1)S(1)} %get-tuple-element.84), channel_id=1, source_target_pairs={{0,8},{8,0},{4,12},{12,4},{16,24},{24,16},{20,28},{28,20},{1,9},{9... | collective-permute-start | bytes 786440 | tf_op jit(solution)/shard_map/ppermute | solution.py:22
  23.2 11.7 %collective-permute-start.6 = (bf16[2,128,512]{2,1,0:T(8,128)(2,1)S(1)}, bf16[2,128,512]{2,1,0:T(8,128)(2,1)S(1)}, u32[]{:S(2)}, u32[]{:S(2)}) collective-permute-start(bf16[2,128,512]{2,1,0:T(8,128)(2,1)S(1)} %get-tuple-element.80), channel_id=1, source_target_pairs={{0,8},{8,0},{4,12},{12,4},{16,24},{24,16},{20,28},{28,20},{1,9},{9... | collective-permute-start | bytes 786440 | tf_op jit(solution)/shard_map/ppermute | solution.py:22
  24.9 15.7 %collective-permute-start.12 = (bf16[2,128,512]{2,1,0:T(8,128)(2,1)S(1)}, bf16[2,128,512]{2,1,0:T(8,128)(2,1)S(1)}, u32[]{:S(2)}, u32[]{:S(2)}) collective-permute-start(bf16[2,128,512]{2,1,0:T(8,128)(2,1)S(1)} %get-tuple-element.86), channel_id=1, source_target_pairs={{0,8},{8,0},{4,12},{12,4},{16,24},{24,16},{20,28},{28,20},{1,9},{9... | collective-permute-start | bytes 786440 | tf_op jit(solution)/shard_map/ppermute | solution.py:22
  28.1 17.0 %collective-permute-start.18 = (bf16[2,128,512]{2,1,0:T(8,128)(2,1)S(1)}, bf16[2,128,512]{2,1,0:T(8,128)(2,1)S(1)}, u32[]{:S(2)}, u32[]{:S(2)}) collective-permute-start(bf16[2,128,512]{2,1,0:T(8,128)(2,1)S(1)} %get-tuple-element.82), channel_id=1, source_target_pairs={{0,8},{8,0},{4,12},{12,4},{16,24},{24,16},{20,28},{28,20},{1,9},{9... | collective-permute-start | bytes 786440 | tf_op jit(solution)/shard_map/ppermute | solution.py:22
  30.7 10.6 %collective-permute-start.3 = (bf16[2,128,512]{2,1,0:T(8,128)(2,1)S(1)}, bf16[2,128,512]{2,1,0:T(8,128)(2,1)S(1)}, u32[]{:S(2)}, u32[]{:S(2)}) collective-permute-start(bf16[2,128,512]{2,1,0:T(8,128)(2,1)S(1)} %fusion.15), channel_id=1, source_target_pairs={{8,16},{12,20},{16,8},{20,12},{9,17},{13,21},{17,9},{21,13},{10,18... | collective-permute-start | bytes 786440 | tf_op jit(solution)/shard_map/ppermute | solution.py:160
  32.0 37.9 %collective-permute-start.5 = (bf16[2,256,512]{2,1,0:T(8,128)(2,1)S(1)}, bf16[2,256,512]{2,1,0:T(8,128)(2,1)}, u32[]{:S(2)}, u32[]{:S(2)}) collective-permute-start(bf16[2,256,512]{2,1,0:T(8,128)(2,1)S(1)} %copy-done.22), channel_id=1, source_target_pairs={{0,4},{4,0},{8,12},{12,8},{16,20},{20,16},{24,28},{28,24},{1,5},{5... | collective-permute-start | bytes 1572872 | tf_op jit(solution)/shard_map/ppermute | solution.py:22
  35.0 20.3 %collective-permute-start.1 = (bf16[2,256,512]{2,1,0:T(8,128)(2,1)S(1)}, bf16[2,256,512]{2,1,0:T(8,128)(2,1)S(1)}, u32[]{:S(2)}, u32[]{:S(2)}) collective-permute-start(bf16[2,256,512]{2,1,0:T(8,128)(2,1)S(1)} %copy-done.23), channel_id=1, source_target_pairs={{0,4},{4,0},{8,12},{12,8},{16,20},{20,16},{24,28},{28,24},{1,5},{5... | collective-permute-start | bytes 1572872 | tf_op jit(solution)/shard_map/ppermute | solution.py:22
  40.6 6.4 %collective-permute-start.7 = (bf16[2,128,512]{2,1,0:T(8,128)(2,1)S(1)}, bf16[2,128,512]{2,1,0:T(8,128)(2,1)S(1)}, u32[]{:S(2)}, u32[]{:S(2)}) collective-permute-start(bf16[2,128,512]{2,1,0:T(8,128)(2,1)S(1)} %fusion.14), channel_id=1, source_target_pairs={{8,16},{12,20},{16,8},{20,12},{9,17},{13,21},{17,9},{21,13},{10,18... | collective-permute-start | bytes 786440 | tf_op jit(solution)/shard_map/ppermute | solution.py:160
  41.2 10.2 %collective-permute-start.4 = (bf16[2,128,512]{2,1,0:T(8,128)(2,1)S(1)}, bf16[2,128,512]{2,1,0:T(8,128)(2,1)S(1)}, u32[]{:S(2)}, u32[]{:S(2)}) collective-permute-start(bf16[2,128,512]{2,1,0:T(8,128)(2,1)S(1)} %collective-permute-done.3), channel_id=1, source_target_pairs={{8,0},{12,4},{16,24},{20,28},{9,1},{13,5},{17,25},{21,29},{10,2},{... | collective-permute-start | bytes 786440 | tf_op jit(solution)/shard_map/ppermute | solution.py:161
  45.1 20.7 %collective-permute-start.13 = (bf16[2,128,512]{2,1,0:T(8,128)(2,1)}, bf16[2,128,512]{2,1,0:T(8,128)(2,1)S(1)}, u32[]{:S(2)}, u32[]{:S(2)}) collective-permute-start(bf16[2,128,512]{2,1,0:T(8,128)(2,1)} %fusion.13), channel_id=1, source_target_pairs={{8,16},{12,20},{16,8},{20,12},{9,17},{13,21},{17,9},{21,13},{10,18... | collective-permute-start | bytes 786440 | tf_op jit(solution)/shard_map/ppermute | solution.py:160
  46.9 19.6 %collective-permute-start.19 = (bf16[2,128,512]{2,1,0:T(8,128)(2,1)}, bf16[2,128,512]{2,1,0:T(8,128)(2,1)S(1)}, u32[]{:S(2)}, u32[]{:S(2)}) collective-permute-start(bf16[2,128,512]{2,1,0:T(8,128)(2,1)} %fusion.12), channel_id=1, source_target_pairs={{8,16},{12,20},{16,8},{20,12},{9,17},{13,21},{17,9},{21,13},{10,18... | collective-permute-start | bytes 786440 | tf_op jit(solution)/shard_map/ppermute | solution.py:160
  51.5 16.3 %collective-permute-start.8 = (bf16[2,128,512]{2,1,0:T(8,128)(2,1)S(1)}, bf16[2,128,512]{2,1,0:T(8,128)(2,1)S(1)}, u32[]{:S(2)}, u32[]{:S(2)}) collective-permute-start(bf16[2,128,512]{2,1,0:T(8,128)(2,1)S(1)} %collective-permute-done.7), channel_id=1, source_target_pairs={{8,0},{12,4},{16,24},{20,28},{9,1},{13,5},{17,25},{21,29},{10,2},{... | collective-permute-start | bytes 786440 | tf_op jit(solution)/shard_map/ppermute | solution.py:161
  56.1 44.7 %collective-permute-start.11 = (bf16[2,256,512]{2,1,0:T(8,128)(2,1)S(1)}, bf16[2,256,512]{2,1,0:T(8,128)(2,1)}, u32[]{:S(2)}, u32[]{:S(2)}) collective-permute-start(bf16[2,256,512]{2,1,0:T(8,128)(2,1)S(1)} %pad_maximum_fusion.5.refs_0_), channel_id=1, source_target_pairs={{0,4},{4,0},{8,12},{12,8},{16,20},{20,16},{24,28},{28,24},{1,5},{5... | collective-permute-start | bytes 1572872 | tf_op jit(solution)/shard_map/ppermute | solution.py:22
  65.8 45.2 %collective-permute-start.17 = (bf16[2,256,512]{2,1,0:T(8,128)(2,1)S(1)}, bf16[2,256,512]{2,1,0:T(8,128)(2,1)}, u32[]{:S(2)}, u32[]{:S(2)}) collective-permute-start(bf16[2,256,512]{2,1,0:T(8,128)(2,1)S(1)} %copy-done.20), channel_id=1, source_target_pairs={{0,4},{4,0},{8,12},{12,8},{16,20},{20,16},{24,28},{28,24},{1,5},{5... | collective-permute-start | bytes 1572872 | tf_op jit(solution)/shard_map/ppermute | solution.py:22
  66.5 17.6 %collective-permute-start.14 = (bf16[2,128,512]{2,1,0:T(8,128)(2,1)S(1)}, bf16[2,128,512]{2,1,0:T(8,128)(2,1)S(1)}, u32[]{:S(2)}, u32[]{:S(2)}) collective-permute-start(bf16[2,128,512]{2,1,0:T(8,128)(2,1)S(1)} %collective-permute-done.13), channel_id=1, source_target_pairs={{8,0},{12,4},{16,24},{20,28},{9,1},{13,5},{17,25},{21,29},{10,2},{... | collective-permute-start | bytes 786440 | tf_op jit(solution)/shard_map/ppermute | solution.py:161
  67.8 19.4 %collective-permute-start.20 = (bf16[2,128,512]{2,1,0:T(8,128)(2,1)S(1)}, bf16[2,128,512]{2,1,0:T(8,128)(2,1)S(1)}, u32[]{:S(2)}, u32[]{:S(2)}) collective-permute-start(bf16[2,128,512]{2,1,0:T(8,128)(2,1)S(1)} %collective-permute-done.19), channel_id=1, source_target_pairs={{8,0},{12,4},{16,24},{20,28},{9,1},{13,5},{17,25},{21,29},{10,2},{... | collective-permute-start | bytes 786440 | tf_op jit(solution)/shard_map/ppermute | solution.py:161
  69.8 16.5 %collective-permute-start.9 = (bf16[2,128,512]{2,1,0:T(8,128)(2,1)S(1)}, bf16[2,128,512]{2,1,0:T(8,128)(2,1)S(1)}, u32[]{:S(2)}, u32[]{:S(2)}) collective-permute-start(bf16[2,128,512]{2,1,0:T(8,128)(2,1)S(1)} %convert_element_type.188), channel_id=1, source_target_pairs={{0,8},{4,12},{24,16},{28,20},{1,9},{5,13},{25,17},{29,21},{2,10},{... | collective-permute-start | bytes 786440 | tf_op jit(solution)/shard_map/ppermute | solution.py:185
  89.4 8.2 %collective-permute-start.16 = (bf16[2,128,512]{2,1,0:T(8,128)(2,1)S(1)}, bf16[2,128,512]{2,1,0:T(8,128)(2,1)S(1)}, u32[]{:S(2)}, u32[]{:S(2)}) collective-permute-start(bf16[2,128,512]{2,1,0:T(8,128)(2,1)S(1)} %add_convert_fusion.12), channel_id=1, source_target_pairs={{8,16},{12,20},{16,8},{20,12},{9,17},{13,21},{17,9},{21,13},{10,18... | collective-permute-start | bytes 786440 | tf_op jit(solution)/shard_map/ppermute | solution.py:187
  90.7 35.5 %collective-permute-start.21 = (bf16[2,128,512]{2,1,0:T(8,128)(2,1)S(1)}, bf16[2,128,512]{2,1,0:T(8,128)(2,1)S(1)}, u32[]{:S(2)}, u32[]{:S(2)}) collective-permute-start(bf16[2,128,512]{2,1,0:T(8,128)(2,1)S(1)} %add_convert_fusion.13), channel_id=1, source_target_pairs={{0,8},{8,0},{4,12},{12,4},{16,24},{24,16},{20,28},{28,20},{1,9},{9... | collective-permute-start | bytes 786440 | tf_op jit(solution)/shard_map/ppermute | solution.py:22
  98.2 31.5 %collective-permute-start.23 = (bf16[2,128,512]{2,1,0:T(8,128)(2,1)S(1)}, bf16[2,128,512]{2,1,0:T(8,128)(2,1)S(1)}, u32[]{:S(2)}, u32[]{:S(2)}) collective-permute-start(bf16[2,128,512]{2,1,0:T(8,128)(2,1)S(1)} %add_convert_fusion.11), channel_id=1, source_target_pairs={{0,8},{8,0},{4,12},{12,4},{16,24},{24,16},{20,28},{28,20},{1,9},{9... | collective-permute-start | bytes 786440 | tf_op jit(solution)/shard_map/ppermute | solution.py:22
  109.0 19.7 %collective-permute-start.25 = (bf16[2,128,512]{2,1,0:T(8,128)(2,1)S(1)}, bf16[2,128,512]{2,1,0:T(8,128)(2,1)S(1)}, u32[]{:S(2)}, u32[]{:S(2)}) collective-permute-start(bf16[2,128,512]{2,1,0:T(8,128)(2,1)S(1)} %convert_element_type.210), channel_id=1, source_target_pairs={{0,8},{4,12},{24,16},{28,20},{1,9},{5,13},{25,17},{29,21},{2,10},{... | collective-permute-start | bytes 786440 | tf_op jit(solution)/shard_map/ppermute | solution.py:185
  119.3 14.8 %collective-permute-start.29 = (bf16[2,128,512]{2,1,0:T(8,128)(2,1)S(1)}, bf16[2,128,512]{2,1,0:T(8,128)(2,1)S(1)}, u32[]{:S(2)}, u32[]{:S(2)}) collective-permute-start(bf16[2,128,512]{2,1,0:T(8,128)(2,1)S(1)} %convert_element_type.218), channel_id=1, source_target_pairs={{0,8},{4,12},{24,16},{28,20},{1,9},{5,13},{25,17},{29,21},{2,10},{... | collective-permute-start | bytes 786440 | tf_op jit(solution)/shard_map/ppermute | solution.py:185
  122.0 47.6 %collective-permute-start.33 = (bf16[2,256,512]{2,1,0:T(8,128)(2,1)S(1)}, bf16[2,256,512]{2,1,0:T(8,128)(2,1)S(1)}, u32[]{:S(2)}, u32[]{:S(2)}) collective-permute-start(bf16[2,256,512]{2,1,0:T(8,128)(2,1)S(1)} %convert_element_type.225), channel_id=1, source_target_pairs={{0,4},{4,0},{8,12},{12,8},{16,20},{20,16},{24,28},{28,24},{1,5},{5... | collective-permute-start | bytes 1572872 | tf_op jit(solution)/shard_map/ppermute | solution.py:22
  128.2 25.9 %collective-permute-start.22 = (bf16[2,256,512]{2,1,0:T(8,128)(2,1)S(1)}, bf16[2,256,512]{2,1,0:T(8,128)(2,1)S(1)}, u32[]{:S(2)}, u32[]{:S(2)}) collective-permute-start(bf16[2,256,512]{2,1,0:T(8,128)(2,1)S(1)} %add_convert_fusion.6), channel_id=1, source_target_pairs={{0,4},{4,0},{8,12},{12,8},{16,20},{20,16},{24,28},{28,24},{1,5},{5... | collective-permute-start | bytes 1572872 | tf_op jit(solution)/shard_map/ppermute | solution.py:22
  129.0 7.4 %collective-permute-start.26 = (bf16[2,128,512]{2,1,0:T(8,128)(2,1)S(1)}, bf16[2,128,512]{2,1,0:T(8,128)(2,1)S(1)}, u32[]{:S(2)}, u32[]{:S(2)}) collective-permute-start(bf16[2,128,512]{2,1,0:T(8,128)(2,1)S(1)} %add_convert_fusion.10), channel_id=1, source_target_pairs={{8,16},{12,20},{16,8},{20,12},{9,17},{13,21},{17,9},{21,13},{10,18... | collective-permute-start | bytes 786440 | tf_op jit(solution)/shard_map/ppermute | solution.py:187
  131.7 27.7 %collective-permute-start.24 = (bf16[2,256,512]{2,1,0:T(8,128)(2,1)S(1)}, bf16[2,256,512]{2,1,0:T(8,128)(2,1)S(1)}, u32[]{:S(2)}, u32[]{:S(2)}) collective-permute-start(bf16[2,256,512]{2,1,0:T(8,128)(2,1)S(1)} %add_convert_fusion.4), channel_id=1, source_target_pairs={{0,4},{4,0},{8,12},{12,8},{16,20},{20,16},{24,28},{28,24},{1,5},{5... | collective-permute-start | bytes 1572872 | tf_op jit(solution)/shard_map/ppermute | solution.py:22
  134.3 6.7 %collective-permute-start.30 = (bf16[2,128,512]{2,1,0:T(8,128)(2,1)S(1)}, bf16[2,128,512]{2,1,0:T(8,128)(2,1)S(1)}, u32[]{:S(2)}, u32[]{:S(2)}) collective-permute-start(bf16[2,128,512]{2,1,0:T(8,128)(2,1)S(1)} %add_convert_fusion.8), channel_id=1, source_target_pairs={{8,16},{12,20},{16,8},{20,12},{9,17},{13,21},{17,9},{21,13},{10,18... | collective-permute-start | bytes 786440 | tf_op jit(solution)/shard_map/ppermute | solution.py:187
  137.1 9.6 %collective-permute-start.27 = (bf16[2,128,512]{2,1,0:T(8,128)(2,1)S(1)}, bf16[2,128,512]{2,1,0:T(8,128)(2,1)S(1)}, u32[]{:S(2)}, u32[]{:S(2)}) collective-permute-start(bf16[2,128,512]{2,1,0:T(8,128)(2,1)S(1)} %add_convert_fusion.9), channel_id=1, source_target_pairs={{0,8},{8,0},{4,12},{12,4},{16,24},{24,16},{20,28},{28,20},{1,9},{9... | collective-permute-start | bytes 786440 | tf_op jit(solution)/shard_map/ppermute | solution.py:22
  141.6 8.5 %collective-permute-start.31 = (bf16[2,128,512]{2,1,0:T(8,128)(2,1)S(1)}, bf16[2,128,512]{2,1,0:T(8,128)(2,1)S(1)}, u32[]{:S(2)}, u32[]{:S(2)}) collective-permute-start(bf16[2,128,512]{2,1,0:T(8,128)(2,1)S(1)} %add_convert_fusion.7), channel_id=1, source_target_pairs={{0,8},{8,0},{4,12},{12,4},{16,24},{24,16},{20,28},{28,20},{1,9},{9... | collective-permute-start | bytes 786440 | tf_op jit(solution)/shard_map/ppermute | solution.py:22
  148.7 21.3 %collective-permute-start.28 = (bf16[2,256,512]{2,1,0:T(8,128)(2,1)S(1)}, bf16[2,256,512]{2,1,0:T(8,128)(2,1)S(1)}, u32[]{:S(2)}, u32[]{:S(2)}) collective-permute-start(bf16[2,256,512]{2,1,0:T(8,128)(2,1)S(1)} %add_convert_fusion.2), channel_id=1, source_target_pairs={{0,4},{4,0},{8,12},{12,8},{16,20},{20,16},{24,28},{28,24},{1,5},{5... | collective-permute-start | bytes 1572872 | tf_op jit(solution)/shard_map/ppermute | solution.py:22
  151.0 17.9 %collective-permute-start.32 = (bf16[2,64,512]{2,1,0:T(8,128)(2,1)S(1)}, bf16[2,64,512]{2,1,0:T(8,128)(2,1)S(1)}, u32[]{:S(2)}, u32[]{:S(2)}) collective-permute-start(bf16[2,64,512]{2,1,0:T(8,128)(2,1)S(1)} %fusion.16), channel_id=1, source_target_pairs={{0,4},{4,0},{8,12},{12,8},{16,20},{20,16},{24,28},{28,24},{1,5},{5... | collective-permute-start | bytes 393224 | tf_op jit(solution)/shard_map/ppermute | solution.py:22
  (43 other events, 197.9 us)

commit v19 on v16

--- a/solution.py
+++ b/solution.py
@@ -107,7 +107,7 @@
 
 def apply(matrix, rows):
     return jnp.einsum(
-        "pr,krw->kpw", matrix, rows.astype(jnp.float32), precision=lax.Precision.HIGHEST,
+        "pr,krw->kpw", matrix, rows.astype(jnp.float32), precision=lax.Precision.HIGH,
         preferred_element_type=jnp.float32,
     )
 

time: 170 us -> 168 us (0.988)
  matrix products: 27.8 us -> 21.9 us
  waiting for transfers between devices: 24.9 us -> 27.4 us
    dot_general x33, matrix products: 25.9 us -> 20 us  [apply(): jnp.einsum('pr,krw->kpw', matrix, rows.astype(jnp.float32), precision=lax...]
    ppermute x18, waiting for transfers between devices: 17.3 us -> 19.5 us  [partner_2(): return lax.ppermute(block, axis, route)]
  transfers between devices with their start and end apart: 34 -> 34, of which waited for: 8 -> 8; matrix products, arithmetic and copies ran while one was open for 29% -> 25% of each run, Pallas kernels for 17% -> 17%
where the time goes in v19:
time: 168 us; the launch traced here: 167 us
  starting transfers between devices  56.5 us (34%)
  Pallas kernels  28.6 us (17%)
  waiting for transfers between devices  27.4 us (16%)
  other arithmetic  23.2 us (14%)
  matrix products  21.9 us (13%)
  local copies, waits for them, and re-layouts  7.48 us (4%)
  between operations  1.7 us (1%)
    ppermute x18, starting transfers between devices, partner_2(): return lax.ppermute(block, axis, route)  34.4 us
    pallas_call x4, Pallas kernels, attention(): pl.pallas_call(functools.partial(attention_kernel, scale=score_scale, par...  28.6 us
    dot_general x33, matrix products, apply(): jnp.einsum('pr,krw->kpw', matrix, rows.astype(jnp.float32), precision=lax...  20 us
    ppermute x18, waiting for transfers between devices, partner_2(): return lax.ppermute(block, axis, route)  19.5 us
    ppermute x4, starting transfers between devices, body(): gathered = lax.ppermute(sends[step_level], 'seq', back)  10.9 us
    unnamed x82, local copies, waits for them, and re-layouts  5.77 us
    ppermute x4, waiting for transfers between devices, body(): passed = lax.ppermute(crossed, 'seq', outer_pairs(seq_count, step_level))  5.7 us
    ppermute x4, starting transfers between devices, body(): passed = lax.ppermute(crossed, 'seq', outer_pairs(seq_count, step_level))  5.15 us
  transfers between devices with their start and end apart: 34, of which 8 were waited for; matrix products, arithmetic and copies ran while one was open for 25% of the time, Pallas kernels for 17%

profile of v19, /device:TPU:0, one launch (start us, length us, event | category | flops | bytes accessed | tf_op | source)
XLA Modules:
  0.0 166.8 jit_solution(9752397505219731051)
XLA Ops:
  0.7 1.6 convolution_bitcast_fusion
  3.5 3.0 %collective-permute-start = (bf16[2,64,2048]{2,1,0:T(8,128)(2,1)}, bf16[2,64,2048]{2,1,0:T(8,128)(2,1)}, u32[]{:S(2)}, u32[]{:S(2)}) collective-permute-start(bf16[2,64,2048]{2,1,0:T(8,128)(2,1)} %fusion.17), channel_id=1, source_target_pairs={{0,4},{4,0},{8,12},{12,8},{16,20},{20,16},{24,28},{28,24},{1,5},{5... | collective-permute-start | bytes 1572872 | tf_op jit(solution)/shard_map/ppermute | solution.py:22
  9.4 2.0 %pad_maximum_fusion.5.refs_0_ = bf16[2,256,512]{2,1,0:T(8,128)(2,1)} fusion(bf16[1,256,512]{2,1,0:T(8,128)(2,1)} %get-tuple-element.70, bf16[1,256,512]{2,1,0:T(8,128)(2,1)} %get-tuple-element.93), kind=kLoop, calls=%fused_computation.65 | loop fusion | flops 262144 | bytes 1048576 | tf_op jit(solution)/shard_map/stack | solution.py:150
  14.8 3.9 %collective-permute-done = bf16[2,64,2048]{2,1,0:T(8,128)(2,1)} collective-permute-done((bf16[2,64,2048]{2,1,0:T(8,128)(2,1)}, bf16[2,64,2048]{2,1,0:T(8,128)(2,1)}, u32[]{:S(2)}, u32[]{:S(2)}) %collective-permute-start) | collective-permute-done | bytes 524320 | tf_op jit(solution)/shard_map/ppermute | solution.py:22
  20.0 1.9 %collective-permute-start.2 = (bf16[2,128,512]{2,1,0:T(8,128)(2,1)S(1)}, bf16[2,128,512]{2,1,0:T(8,128)(2,1)S(1)}, u32[]{:S(2)}, u32[]{:S(2)}) collective-permute-start(bf16[2,128,512]{2,1,0:T(8,128)(2,1)S(1)} %get-tuple-element.84), channel_id=1, source_target_pairs={{0,8},{8,0},{4,12},{12,4},{16,24},{24,16},{20,28},{28,20},{1,9},{9... | collective-permute-start | bytes 786440 | tf_op jit(solution)/shard_map/ppermute | solution.py:22
  24.6 1.9 %collective-permute-start.12 = (bf16[2,128,512]{2,1,0:T(8,128)(2,1)S(1)}, bf16[2,128,512]{2,1,0:T(8,128)(2,1)S(1)}, u32[]{:S(2)}, u32[]{:S(2)}) collective-permute-start(bf16[2,128,512]{2,1,0:T(8,128)(2,1)S(1)} %get-tuple-element.88), channel_id=1, source_target_pairs={{0,8},{8,0},{4,12},{12,4},{16,24},{24,16},{20,28},{28,20},{1,9},{9... | collective-permute-start | bytes 786440 | tf_op jit(solution)/shard_map/ppermute | solution.py:22
  29.3 5.6 %collective-permute-done.6.refs_2_ = bf16[2,128,512]{2,1,0:T(8,128)(2,1)S(1)} collective-permute-done((bf16[2,128,512]{2,1,0:T(8,128)(2,1)S(1)}, bf16[2,128,512]{2,1,0:T(8,128)(2,1)S(1)}, u32[]{:S(2)}, u32[]{:S(2)}) %collective-permute-start.6) | collective-permute-done | bytes 262176 | tf_op jit(solution)/shard_map/ppermute | solution.py:22
  36.4 1.8 %collective-permute-start.1 = (bf16[2,256,512]{2,1,0:T(8,128)(2,1)S(1)}, bf16[2,256,512]{2,1,0:T(8,128)(2,1)}, u32[]{:S(2)}, u32[]{:S(2)}) collective-permute-start(bf16[2,256,512]{2,1,0:T(8,128)(2,1)S(1)} %copy-done.22), channel_id=1, source_target_pairs={{0,4},{4,0},{8,12},{12,8},{16,20},{20,16},{24,28},{28,24},{1,5},{5... | collective-permute-start | bytes 1572872 | tf_op jit(solution)/shard_map/ppermute | solution.py:22
  38.9 1.6 collective-permute-done.12.refs_2_
  43.6 1.5 collective-permute-done.19.refs_2_
  47.5 5.7 %collective-permute-done.8 = bf16[2,128,512]{2,1,0:T(8,128)(2,1)S(1)} collective-permute-done((bf16[2,128,512]{2,1,0:T(8,128)(2,1)S(1)}, bf16[2,128,512]{2,1,0:T(8,128)(2,1)S(1)}, u32[]{:S(2)}, u32[]{:S(2)}) %collective-permute-start.8) | collective-permute-done | bytes 262176 | tf_op jit(solution)/shard_map/ppermute | solution.py:161
  55.2 3.8 %collective-permute-done.5.refs_1_ = bf16[2,256,512]{2,1,0:T(8,128)(2,1)S(1)} collective-permute-done((bf16[2,256,512]{2,1,0:T(8,128)(2,1)S(1)}, bf16[2,256,512]{2,1,0:T(8,128)(2,1)S(1)}, u32[]{:S(2)}, u32[]{:S(2)}) %collective-permute-start.5) | collective-permute-done | bytes 524320 | tf_op jit(solution)/shard_map/ppermute | solution.py:22
  59.7 1.7 %collective-permute-start.18 = (bf16[2,256,512]{2,1,0:T(8,128)(2,1)S(1)}, bf16[2,256,512]{2,1,0:T(8,128)(2,1)}, u32[]{:S(2)}, u32[]{:S(2)}) collective-permute-start(bf16[2,256,512]{2,1,0:T(8,128)(2,1)S(1)} %copy-done.20), channel_id=1, source_target_pairs={{0,4},{4,0},{8,12},{12,8},{16,20},{20,16},{24,28},{28,24},{1,5},{5... | collective-permute-start | bytes 1572872 | tf_op jit(solution)/shard_map/ppermute | solution.py:22
  61.5 7.1 %shard_map.76 = (bf16[256,512]{1,0:T(8,128)(2,1)}, bf16[256,512]{1,0:T(8,128)(2,1)}, f32[2,256,512]{2,1,0:T(8,128)}, f32[2,256,512]{2,1,0:T(8,128)}, f32[2,128,512]{2,1,0:T(8,128)}, /*index=5*/f32[2,128,512]{2,1,0:T(8,128)}) custom-call(f32[1,768]{1,0:T(1,128)} %constant.104.clone.1.bias_ref, bf16[256,2048]{1,0:T(8,128)(2,1)} %q_ref.7, ...), custom_call_target="tpu_custom_call" | custom-call | flops 1207959552 | bytes 5767168 | tf_op jit(solution)/shard_map/pallas_call | solution.py:72
  72.7 1.7 %broadcast_select_fusion.3.refs_3_ = bf16[2,128,512]{2,1,0:T(8,128)(2,1)} fusion(bf16[2,128,512]{2,1,0:T(8,128)(2,1)S(1)} %collective-permute-done.3, bf16[2,128,512]{2,1,0:T(8,128)(2,1)} %collective-permute-done.4, pred[]{:T(512)S(6)} %ne.121), kind=kLoop, calls=%fused_computation.108 | loop fusion | flops 131072 | bytes 786433 | tf_op jit(solution)/shard_map/jit(_where)/select_n | solution.py:162
  74.4 5.6 %collective-permute-start.15 = (bf16[2,128,512]{2,1,0:T(8,128)(2,1)S(1)}, bf16[2,128,512]{2,1,0:T(8,128)(2,1)S(1)}, u32[]{:S(2)}, u32[]{:S(2)}) collective-permute-start(bf16[2,128,512]{2,1,0:T(8,128)(2,1)S(1)} %convert_element_type.195), channel_id=1, source_target_pairs={{0,8},{4,12},{24,16},{28,20},{1,9},{5,13},{25,17},{29,21},{2,10},{... | collective-permute-start | bytes 786440 | tf_op jit(solution)/shard_map/ppermute | solution.py:187
  80.0 7.1 %shard_map.75 = (bf16[256,512]{1,0:T(8,128)(2,1)}, bf16[256,512]{1,0:T(8,128)(2,1)}, f32[2,256,512]{2,1,0:T(8,128)}, f32[2,256,512]{2,1,0:T(8,128)}, f32[2,128,512]{2,1,0:T(8,128)}, /*index=5*/f32[2,128,512]{2,1,0:T(8,128)}) custom-call(f32[1,768]{1,0:T(1,128)} %constant.104.clone.1.bias_ref, bf16[256,2048]{1,0:T(8,128)(2,1)} %q_ref.7, ...), custom_call_target="tpu_custom_call" | custom-call | flops 1207959552 | bytes 5767168 | tf_op jit(solution)/shard_map/pallas_call | solution.py:72
  92.0 2.2 %collective-permute-done.9 = bf16[2,128,512]{2,1,0:T(8,128)(2,1)S(1)} collective-permute-done((bf16[2,128,512]{2,1,0:T(8,128)(2,1)S(1)}, bf16[2,128,512]{2,1,0:T(8,128)(2,1)S(1)}, u32[]{:S(2)}, u32[]{:S(2)}) %collective-permute-start.9) | collective-permute-done | bytes 262176 | tf_op jit(solution)/shard_map/ppermute | solution.py:187
  95.7 4.6 %collective-permute-start.23 = (bf16[2,128,512]{2,1,0:T(8,128)(2,1)S(1)}, bf16[2,128,512]{2,1,0:T(8,128)(2,1)S(1)}, u32[]{:S(2)}, u32[]{:S(2)}) collective-permute-start(bf16[2,128,512]{2,1,0:T(8,128)(2,1)S(1)} %add_convert_fusion.11), channel_id=1, source_target_pairs={{0,8},{8,0},{4,12},{12,4},{16,24},{24,16},{20,28},{28,20},{1,9},{9... | collective-permute-start | bytes 786440 | tf_op jit(solution)/shard_map/ppermute | solution.py:22
  100.9 4.7 %collective-permute-start.17 = (bf16[2,128,512]{2,1,0:T(8,128)(2,1)S(1)}, bf16[2,128,512]{2,1,0:T(8,128)(2,1)S(1)}, u32[]{:S(2)}, u32[]{:S(2)}) collective-permute-start(bf16[2,128,512]{2,1,0:T(8,128)(2,1)S(1)} %add_convert_fusion.13), channel_id=1, source_target_pairs={{0,8},{8,0},{4,12},{12,4},{16,24},{24,16},{20,28},{28,20},{1,9},{9... | collective-permute-start | bytes 786440 | tf_op jit(solution)/shard_map/ppermute | solution.py:22
  105.6 7.2 %shard_map.77 = (bf16[256,512]{1,0:T(8,128)(2,1)}, bf16[256,512]{1,0:T(8,128)(2,1)}, f32[2,256,512]{2,1,0:T(8,128)}, f32[2,256,512]{2,1,0:T(8,128)}, f32[2,128,512]{2,1,0:T(8,128)}, /*index=5*/f32[2,128,512]{2,1,0:T(8,128)}) custom-call(f32[1,768]{1,0:T(1,128)} %constant.104.clone.1.bias_ref, bf16[256,2048]{1,0:T(8,128)(2,1)} %q_ref.7, ...), custom_call_target="tpu_custom_call" | custom-call | flops 1207959552 | bytes 5767168 | tf_op jit(solution)/shard_map/pallas_call | solution.py:72
  113.9 2.6 %collective-permute-start.25 = (bf16[2,128,512]{2,1,0:T(8,128)(2,1)S(1)}, bf16[2,128,512]{2,1,0:T(8,128)(2,1)}, u32[]{:S(2)}, u32[]{:S(2)}) collective-permute-start(bf16[2,128,512]{2,1,0:T(8,128)(2,1)S(1)} %convert_element_type.210), channel_id=1, source_target_pairs={{0,8},{4,12},{24,16},{28,20},{1,9},{5,13},{25,17},{29,21},{2,10},{... | collective-permute-start | bytes 786440 | tf_op jit(solution)/shard_map/ppermute | solution.py:187
  118.5 1.6 collective-permute-start.24
  123.2 7.2 %shard_map.78 = (bf16[256,512]{1,0:T(8,128)(2,1)}, bf16[256,512]{1,0:T(8,128)(2,1)}, f32[2,256,512]{2,1,0:T(8,128)}, f32[2,256,512]{2,1,0:T(8,128)}, f32[2,128,512]{2,1,0:T(8,128)}, /*index=5*/f32[2,128,512]{2,1,0:T(8,128)}) custom-call(f32[1,768]{1,0:T(1,128)} %constant.104.clone.1.bias_ref, bf16[256,2048]{1,0:T(8,128)(2,1)} %q_ref.7, ...), custom_call_target="tpu_custom_call" | custom-call | flops 1207959552 | bytes 5767168 | tf_op jit(solution)/shard_map/pallas_call | solution.py:72
  131.5 1.3 collective-permute-start.29
  134.1 1.6 collective-permute-start.33
  142.5 3.2 %collective-permute-start.27 = (bf16[2,128,512]{2,1,0:T(8,128)(2,1)S(1)}, bf16[2,128,512]{2,1,0:T(8,128)(2,1)S(1)}, u32[]{:S(2)}, u32[]{:S(2)}) collective-permute-start(bf16[2,128,512]{2,1,0:T(8,128)(2,1)S(1)} %add_convert_fusion.9), channel_id=1, source_target_pairs={{0,8},{8,0},{4,12},{12,4},{16,24},{24,16},{20,28},{28,20},{1,9},{9... | collective-permute-start | bytes 786440 | tf_op jit(solution)/shard_map/ppermute | solution.py:22
  146.3 4.4 %collective-permute-start.31 = (bf16[2,128,512]{2,1,0:T(8,128)(2,1)S(1)}, bf16[2,128,512]{2,1,0:T(8,128)(2,1)S(1)}, u32[]{:S(2)}, u32[]{:S(2)}) collective-permute-start(bf16[2,128,512]{2,1,0:T(8,128)(2,1)S(1)} %add_convert_fusion.7), channel_id=1, source_target_pairs={{0,8},{8,0},{4,12},{12,4},{16,24},{24,16},{20,28},{28,20},{1,9},{9... | collective-permute-start | bytes 786440 | tf_op jit(solution)/shard_map/ppermute | solution.py:22
  153.9 1.4 add_convert_fusion.3
  155.4 1.4 add_convert_fusion.5
  157.9 1.6 collective-permute-start.32
  160.2 3.1 %collective-permute-done.32 = bf16[2,64,512]{2,1,0:T(8,128)(2,1)S(1)} collective-permute-done((bf16[2,64,512]{2,1,0:T(8,128)(2,1)S(1)}, bf16[2,64,512]{2,1,0:T(8,128)(2,1)S(1)}, u32[]{:S(2)}, u32[]{:S(2)}) %collective-permute-start.32) | collective-permute-done | bytes 131104 | tf_op jit(solution)/shard_map/ppermute | solution.py:22
  (206 shorter events, 59.5 us)
Async XLA Ops:
  3.5 15.2 %collective-permute-start = (bf16[2,64,2048]{2,1,0:T(8,128)(2,1)}, bf16[2,64,2048]{2,1,0:T(8,128)(2,1)}, u32[]{:S(2)}, u32[]{:S(2)}) collective-permute-start(bf16[2,64,2048]{2,1,0:T(8,128)(2,1)} %fusion.17), channel_id=1, source_target_pairs={{0,4},{4,0},{8,12},{12,8},{16,20},{20,16},{24,28},{28,24},{1,5},{5... | collective-permute-start | bytes 1572872 | tf_op jit(solution)/shard_map/ppermute | solution.py:22
  20.0 18.2 %collective-permute-start.2 = (bf16[2,128,512]{2,1,0:T(8,128)(2,1)S(1)}, bf16[2,128,512]{2,1,0:T(8,128)(2,1)S(1)}, u32[]{:S(2)}, u32[]{:S(2)}) collective-permute-start(bf16[2,128,512]{2,1,0:T(8,128)(2,1)S(1)} %get-tuple-element.84), channel_id=1, source_target_pairs={{0,8},{8,0},{4,12},{12,4},{16,24},{24,16},{20,28},{28,20},{1,9},{9... | collective-permute-start | bytes 786440 | tf_op jit(solution)/shard_map/ppermute | solution.py:22
  23.1 11.8 %collective-permute-start.6 = (bf16[2,128,512]{2,1,0:T(8,128)(2,1)S(1)}, bf16[2,128,512]{2,1,0:T(8,128)(2,1)S(1)}, u32[]{:S(2)}, u32[]{:S(2)}) collective-permute-start(bf16[2,128,512]{2,1,0:T(8,128)(2,1)S(1)} %get-tuple-element.82), channel_id=1, source_target_pairs={{0,8},{8,0},{4,12},{12,4},{16,24},{24,16},{20,28},{28,20},{1,9},{9... | collective-permute-start | bytes 786440 | tf_op jit(solution)/shard_map/ppermute | solution.py:22
  24.6 15.9 %collective-permute-start.12 = (bf16[2,128,512]{2,1,0:T(8,128)(2,1)S(1)}, bf16[2,128,512]{2,1,0:T(8,128)(2,1)S(1)}, u32[]{:S(2)}, u32[]{:S(2)}) collective-permute-start(bf16[2,128,512]{2,1,0:T(8,128)(2,1)S(1)} %get-tuple-element.88), channel_id=1, source_target_pairs={{0,8},{8,0},{4,12},{12,4},{16,24},{24,16},{20,28},{28,20},{1,9},{9... | collective-permute-start | bytes 786440 | tf_op jit(solution)/shard_map/ppermute | solution.py:22
  27.8 17.3 %collective-permute-start.19 = (bf16[2,128,512]{2,1,0:T(8,128)(2,1)S(1)}, bf16[2,128,512]{2,1,0:T(8,128)(2,1)S(1)}, u32[]{:S(2)}, u32[]{:S(2)}) collective-permute-start(bf16[2,128,512]{2,1,0:T(8,128)(2,1)S(1)} %get-tuple-element.86), channel_id=1, source_target_pairs={{0,8},{8,0},{4,12},{12,4},{16,24},{24,16},{20,28},{28,20},{1,9},{9... | collective-permute-start | bytes 786440 | tf_op jit(solution)/shard_map/ppermute | solution.py:22
  35.2 5.9 %collective-permute-start.7 = (bf16[2,128,512]{2,1,0:T(8,128)(2,1)S(1)}, bf16[2,128,512]{2,1,0:T(8,128)(2,1)S(1)}, u32[]{:S(2)}, u32[]{:S(2)}) collective-permute-start(bf16[2,128,512]{2,1,0:T(8,128)(2,1)S(1)} %fusion.14), channel_id=1, source_target_pairs={{8,16},{12,20},{16,8},{20,12},{9,17},{13,21},{17,9},{21,13},{10,18... | collective-permute-start | bytes 786440 | tf_op jit(solution)/shard_map/ppermute | solution.py:160
  36.4 38.0 %collective-permute-start.1 = (bf16[2,256,512]{2,1,0:T(8,128)(2,1)S(1)}, bf16[2,256,512]{2,1,0:T(8,128)(2,1)}, u32[]{:S(2)}, u32[]{:S(2)}) collective-permute-start(bf16[2,256,512]{2,1,0:T(8,128)(2,1)S(1)} %copy-done.22), channel_id=1, source_target_pairs={{0,4},{4,0},{8,12},{12,8},{16,20},{20,16},{24,28},{28,24},{1,5},{5... | collective-permute-start | bytes 1572872 | tf_op jit(solution)/shard_map/ppermute | solution.py:22
  38.2 20.8 %collective-permute-start.5 = (bf16[2,256,512]{2,1,0:T(8,128)(2,1)S(1)}, bf16[2,256,512]{2,1,0:T(8,128)(2,1)S(1)}, u32[]{:S(2)}, u32[]{:S(2)}) collective-permute-start(bf16[2,256,512]{2,1,0:T(8,128)(2,1)S(1)} %copy-done.23), channel_id=1, source_target_pairs={{0,4},{4,0},{8,12},{12,8},{16,20},{20,16},{24,28},{28,24},{1,5},{5... | collective-permute-start | bytes 1572872 | tf_op jit(solution)/shard_map/ppermute | solution.py:22
  40.5 6.3 %collective-permute-start.3 = (bf16[2,128,512]{2,1,0:T(8,128)(2,1)S(1)}, bf16[2,128,512]{2,1,0:T(8,128)(2,1)S(1)}, u32[]{:S(2)}, u32[]{:S(2)}) collective-permute-start(bf16[2,128,512]{2,1,0:T(8,128)(2,1)S(1)} %fusion.15), channel_id=1, source_target_pairs={{8,16},{12,20},{16,8},{20,12},{9,17},{13,21},{17,9},{21,13},{10,18... | collective-permute-start | bytes 786440 | tf_op jit(solution)/shard_map/ppermute | solution.py:160
  41.2 12.0 %collective-permute-start.8 = (bf16[2,128,512]{2,1,0:T(8,128)(2,1)S(1)}, bf16[2,128,512]{2,1,0:T(8,128)(2,1)S(1)}, u32[]{:S(2)}, u32[]{:S(2)}) collective-permute-start(bf16[2,128,512]{2,1,0:T(8,128)(2,1)S(1)} %collective-permute-done.7), channel_id=1, source_target_pairs={{8,0},{12,4},{16,24},{20,28},{9,1},{13,5},{17,25},{21,29},{10,2},{... | collective-permute-start | bytes 786440 | tf_op jit(solution)/shard_map/ppermute | solution.py:161
  45.1 24.6 %collective-permute-start.13 = (bf16[2,128,512]{2,1,0:T(8,128)(2,1)}, bf16[2,128,512]{2,1,0:T(8,128)(2,1)S(1)}, u32[]{:S(2)}, u32[]{:S(2)}) collective-permute-start(bf16[2,128,512]{2,1,0:T(8,128)(2,1)} %fusion.13), channel_id=1, source_target_pairs={{8,16},{12,20},{16,8},{20,12},{9,17},{13,21},{17,9},{21,13},{10,18... | collective-permute-start | bytes 786440 | tf_op jit(solution)/shard_map/ppermute | solution.py:160
  46.8 23.3 %collective-permute-start.20 = (bf16[2,128,512]{2,1,0:T(8,128)(2,1)}, bf16[2,128,512]{2,1,0:T(8,128)(2,1)S(1)}, u32[]{:S(2)}, u32[]{:S(2)}) collective-permute-start(bf16[2,128,512]{2,1,0:T(8,128)(2,1)} %fusion.12), channel_id=1, source_target_pairs={{8,16},{12,20},{16,8},{20,12},{9,17},{13,21},{17,9},{21,13},{10,18... | collective-permute-start | bytes 786440 | tf_op jit(solution)/shard_map/ppermute | solution.py:160
  53.2 18.2 %collective-permute-start.4 = (bf16[2,128,512]{2,1,0:T(8,128)(2,1)S(1)}, bf16[2,128,512]{2,1,0:T(8,128)(2,1)}, u32[]{:S(2)}, u32[]{:S(2)}) collective-permute-start(bf16[2,128,512]{2,1,0:T(8,128)(2,1)S(1)} %collective-permute-done.3), channel_id=1, source_target_pairs={{8,0},{12,4},{16,24},{20,28},{9,1},{13,5},{17,25},{21,29},{10,2},{... | collective-permute-start | bytes 786440 | tf_op jit(solution)/shard_map/ppermute | solution.py:161
  59.7 63.5 %collective-permute-start.18 = (bf16[2,256,512]{2,1,0:T(8,128)(2,1)S(1)}, bf16[2,256,512]{2,1,0:T(8,128)(2,1)}, u32[]{:S(2)}, u32[]{:S(2)}) collective-permute-start(bf16[2,256,512]{2,1,0:T(8,128)(2,1)S(1)} %copy-done.20), channel_id=1, source_target_pairs={{0,4},{4,0},{8,12},{12,8},{16,20},{20,16},{24,28},{28,24},{1,5},{5... | collective-permute-start | bytes 1572872 | tf_op jit(solution)/shard_map/ppermute | solution.py:22
  69.7 35.9 %collective-permute-start.11 = (bf16[2,256,512]{2,1,0:T(8,128)(2,1)S(1)}, bf16[2,256,512]{2,1,0:T(8,128)(2,1)}, u32[]{:S(2)}, u32[]{:S(2)}) collective-permute-start(bf16[2,256,512]{2,1,0:T(8,128)(2,1)S(1)} %copy-done.21), channel_id=1, source_target_pairs={{0,4},{4,0},{8,12},{12,8},{16,20},{20,16},{24,28},{28,24},{1,5},{5... | collective-permute-start | bytes 1572872 | tf_op jit(solution)/shard_map/ppermute | solution.py:22
  70.1 18.1 %collective-permute-start.14 = (bf16[2,128,512]{2,1,0:T(8,128)(2,1)S(1)}, bf16[2,128,512]{2,1,0:T(8,128)(2,1)S(1)}, u32[]{:S(2)}, u32[]{:S(2)}) collective-permute-start(bf16[2,128,512]{2,1,0:T(8,128)(2,1)S(1)} %collective-permute-done.13), channel_id=1, source_target_pairs={{8,0},{12,4},{16,24},{20,28},{9,1},{13,5},{17,25},{21,29},{10,2},{... | collective-permute-start | bytes 786440 | tf_op jit(solution)/shard_map/ppermute | solution.py:161
  71.4 19.8 %collective-permute-start.21 = (bf16[2,128,512]{2,1,0:T(8,128)(2,1)S(1)}, bf16[2,128,512]{2,1,0:T(8,128)(2,1)S(1)}, u32[]{:S(2)}, u32[]{:S(2)}) collective-permute-start(bf16[2,128,512]{2,1,0:T(8,128)(2,1)S(1)} %collective-permute-done.20), channel_id=1, source_target_pairs={{8,0},{12,4},{16,24},{20,28},{9,1},{13,5},{17,25},{21,29},{10,2},{... | collective-permute-start | bytes 786440 | tf_op jit(solution)/shard_map/ppermute | solution.py:161
  74.4 16.0 %collective-permute-start.15 = (bf16[2,128,512]{2,1,0:T(8,128)(2,1)S(1)}, bf16[2,128,512]{2,1,0:T(8,128)(2,1)S(1)}, u32[]{:S(2)}, u32[]{:S(2)}) collective-permute-start(bf16[2,128,512]{2,1,0:T(8,128)(2,1)S(1)} %convert_element_type.195), channel_id=1, source_target_pairs={{0,8},{4,12},{24,16},{28,20},{1,9},{5,13},{25,17},{29,21},{2,10},{... | collective-permute-start | bytes 786440 | tf_op jit(solution)/shard_map/ppermute | solution.py:187
  88.2 6.0 %collective-permute-start.9 = (bf16[2,128,512]{2,1,0:T(8,128)(2,1)S(1)}, bf16[2,128,512]{2,1,0:T(8,128)(2,1)S(1)}, u32[]{:S(2)}, u32[]{:S(2)}) collective-permute-start(bf16[2,128,512]{2,1,0:T(8,128)(2,1)S(1)} %convert_element_type.188), channel_id=1, source_target_pairs={{0,8},{4,12},{24,16},{28,20},{1,9},{5,13},{25,17},{29,21},{2,10},{... | collective-permute-start | bytes 786440 | tf_op jit(solution)/shard_map/ppermute | solution.py:187
  94.3 6.1 %collective-permute-start.10 = (bf16[2,128,512]{2,1,0:T(8,128)(2,1)S(1)}, bf16[2,128,512]{2,1,0:T(8,128)(2,1)S(1)}, u32[]{:S(2)}, u32[]{:S(2)}) collective-permute-start(bf16[2,128,512]{2,1,0:T(8,128)(2,1)S(1)} %add_convert_fusion.14), channel_id=1, source_target_pairs={{8,16},{12,20},{16,8},{20,12},{9,17},{13,21},{17,9},{21,13},{10,18... | collective-permute-start | bytes 786440 | tf_op jit(solution)/shard_map/ppermute | solution.py:189
  95.7 20.8 %collective-permute-start.23 = (bf16[2,128,512]{2,1,0:T(8,128)(2,1)S(1)}, bf16[2,128,512]{2,1,0:T(8,128)(2,1)S(1)}, u32[]{:S(2)}, u32[]{:S(2)}) collective-permute-start(bf16[2,128,512]{2,1,0:T(8,128)(2,1)S(1)} %add_convert_fusion.11), channel_id=1, source_target_pairs={{0,8},{8,0},{4,12},{12,4},{16,24},{24,16},{20,28},{28,20},{1,9},{9... | collective-permute-start | bytes 786440 | tf_op jit(solution)/shard_map/ppermute | solution.py:22
  100.9 19.1 %collective-permute-start.17 = (bf16[2,128,512]{2,1,0:T(8,128)(2,1)S(1)}, bf16[2,128,512]{2,1,0:T(8,128)(2,1)S(1)}, u32[]{:S(2)}, u32[]{:S(2)}) collective-permute-start(bf16[2,128,512]{2,1,0:T(8,128)(2,1)S(1)} %add_convert_fusion.13), channel_id=1, source_target_pairs={{0,8},{8,0},{4,12},{12,4},{16,24},{24,16},{20,28},{28,20},{1,9},{9... | collective-permute-start | bytes 786440 | tf_op jit(solution)/shard_map/ppermute | solution.py:22
  113.9 22.5 %collective-permute-start.25 = (bf16[2,128,512]{2,1,0:T(8,128)(2,1)S(1)}, bf16[2,128,512]{2,1,0:T(8,128)(2,1)}, u32[]{:S(2)}, u32[]{:S(2)}) collective-permute-start(bf16[2,128,512]{2,1,0:T(8,128)(2,1)S(1)} %convert_element_type.210), channel_id=1, source_target_pairs={{0,8},{4,12},{24,16},{28,20},{1,9},{5,13},{25,17},{29,21},{2,10},{... | collective-permute-start | bytes 786440 | tf_op jit(solution)/shard_map/ppermute | solution.py:187
  118.5 35.4 %collective-permute-start.24 = (bf16[2,256,512]{2,1,0:T(8,128)(2,1)S(1)}, bf16[2,256,512]{2,1,0:T(8,128)(2,1)}, u32[]{:S(2)}, u32[]{:S(2)}) collective-permute-start(bf16[2,256,512]{2,1,0:T(8,128)(2,1)S(1)} %add_convert_fusion.4), channel_id=1, source_target_pairs={{0,4},{4,0},{8,12},{12,8},{16,20},{20,16},{24,28},{28,24},{1,5},{5... | collective-permute-start | bytes 1572872 | tf_op jit(solution)/shard_map/ppermute | solution.py:22
  122.0 33.4 %collective-permute-start.22 = (bf16[2,256,512]{2,1,0:T(8,128)(2,1)S(1)}, bf16[2,256,512]{2,1,0:T(8,128)(2,1)}, u32[]{:S(2)}, u32[]{:S(2)}) collective-permute-start(bf16[2,256,512]{2,1,0:T(8,128)(2,1)S(1)} %add_convert_fusion.6), channel_id=1, source_target_pairs={{0,4},{4,0},{8,12},{12,8},{16,20},{20,16},{24,28},{28,24},{1,5},{5... | collective-permute-start | bytes 1572872 | tf_op jit(solution)/shard_map/ppermute | solution.py:22
  131.5 9.3 %collective-permute-start.29 = (bf16[2,128,512]{2,1,0:T(8,128)(2,1)S(1)}, bf16[2,128,512]{2,1,0:T(8,128)(2,1)S(1)}, u32[]{:S(2)}, u32[]{:S(2)}) collective-permute-start(bf16[2,128,512]{2,1,0:T(8,128)(2,1)S(1)} %convert_element_type.218), channel_id=1, source_target_pairs={{0,8},{4,12},{24,16},{28,20},{1,9},{5,13},{25,17},{29,21},{2,10},{... | collective-permute-start | bytes 786440 | tf_op jit(solution)/shard_map/ppermute | solution.py:187
  134.1 29.6 %collective-permute-start.33 = (bf16[2,256,512]{2,1,0:T(8,128)(2,1)S(1)}, bf16[2,256,512]{2,1,0:T(8,128)(2,1)S(1)}, u32[]{:S(2)}, u32[]{:S(2)}) collective-permute-start(bf16[2,256,512]{2,1,0:T(8,128)(2,1)S(1)} %convert_element_type.225), channel_id=1, source_target_pairs={{0,4},{4,0},{8,12},{12,8},{16,20},{20,16},{24,28},{28,24},{1,5},{5... | collective-permute-start | bytes 1572872 | tf_op jit(solution)/shard_map/ppermute | solution.py:22
  140.9 4.8 %collective-permute-start.30 = (bf16[2,128,512]{2,1,0:T(8,128)(2,1)S(1)}, bf16[2,128,512]{2,1,0:T(8,128)(2,1)S(1)}, u32[]{:S(2)}, u32[]{:S(2)}) collective-permute-start(bf16[2,128,512]{2,1,0:T(8,128)(2,1)S(1)} %add_convert_fusion.8), channel_id=1, source_target_pairs={{8,16},{12,20},{16,8},{20,12},{9,17},{13,21},{17,9},{21,13},{10,18... | collective-permute-start | bytes 786440 | tf_op jit(solution)/shard_map/ppermute | solution.py:189
  142.5 8.2 %collective-permute-start.27 = (bf16[2,128,512]{2,1,0:T(8,128)(2,1)S(1)}, bf16[2,128,512]{2,1,0:T(8,128)(2,1)S(1)}, u32[]{:S(2)}, u32[]{:S(2)}) collective-permute-start(bf16[2,128,512]{2,1,0:T(8,128)(2,1)S(1)} %add_convert_fusion.9), channel_id=1, source_target_pairs={{0,8},{8,0},{4,12},{12,4},{16,24},{24,16},{20,28},{28,20},{1,9},{9... | collective-permute-start | bytes 786440 | tf_op jit(solution)/shard_map/ppermute | solution.py:22
  146.3 10.8 %collective-permute-start.31 = (bf16[2,128,512]{2,1,0:T(8,128)(2,1)S(1)}, bf16[2,128,512]{2,1,0:T(8,128)(2,1)S(1)}, u32[]{:S(2)}, u32[]{:S(2)}) collective-permute-start(bf16[2,128,512]{2,1,0:T(8,128)(2,1)S(1)} %add_convert_fusion.7), channel_id=1, source_target_pairs={{0,8},{8,0},{4,12},{12,4},{16,24},{24,16},{20,28},{28,20},{1,9},{9... | collective-permute-start | bytes 786440 | tf_op jit(solution)/shard_map/ppermute | solution.py:22
  152.6 11.6 %collective-permute-start.28 = (bf16[2,256,512]{2,1,0:T(8,128)(2,1)S(1)}, bf16[2,256,512]{2,1,0:T(8,128)(2,1)S(1)}, u32[]{:S(2)}, u32[]{:S(2)}) collective-permute-start(bf16[2,256,512]{2,1,0:T(8,128)(2,1)S(1)} %add_convert_fusion.2), channel_id=1, source_target_pairs={{0,4},{4,0},{8,12},{12,8},{16,20},{20,16},{24,28},{28,24},{1,5},{5... | collective-permute-start | bytes 1572872 | tf_op jit(solution)/shard_map/ppermute | solution.py:22
  157.9 5.4 %collective-permute-start.32 = (bf16[2,64,512]{2,1,0:T(8,128)(2,1)S(1)}, bf16[2,64,512]{2,1,0:T(8,128)(2,1)S(1)}, u32[]{:S(2)}, u32[]{:S(2)}) collective-permute-start(bf16[2,64,512]{2,1,0:T(8,128)(2,1)S(1)} %fusion.16), channel_id=1, source_target_pairs={{0,4},{4,0},{8,12},{12,8},{16,20},{20,16},{24,28},{28,24},{1,5},{5... | collective-permute-start | bytes 393224 | tf_op jit(solution)/shard_map/ppermute | solution.py:22
  (43 other events, 169.4 us)

commit v20 on v19

--- a/solution.py
+++ b/solution.py
@@ -142,7 +142,7 @@
     spread_own = pool_own.T
     place_mine = placed_pool(POOLED // 2, bits[0])
     place_other = placed_pool(POOLED // 2, 1 - bits[0])
-    pieces = [[], []]
+    rows_out = [jnp.zeros((leaf_rows, model_width), jnp.bfloat16) for _ in range(2)]
     grads_out = [jnp.zeros((leaf_rows, model_width), jnp.bfloat16) for _ in range(2)]
     late = []
     for chunk in range(CHUNKS):
@@ -206,12 +206,12 @@
             own_total = own_total + apply(spread_own, pooled_back)
         totals = own_total + from_sibling.astype(jnp.float32)
         for slot, piece in enumerate((attended, query_grad)):
-            pieces[slot].append(piece)
+            rows_out[slot] = lax.dynamic_update_slice(rows_out[slot], piece, (0, columns.start))
         for slot in range(2):
             grads_out[slot] = lax.dynamic_update_slice(
                 grads_out[slot], totals[slot].astype(jnp.bfloat16), (0, columns.start)
             )
-    return tuple(jnp.concatenate(p, axis=1) for p in pieces[:2]) + tuple(grads_out)
+    return tuple(rows_out) + tuple(grads_out)
 
 
 def solution(mesh):

time: 168 us -> 180 us (1.071)
  starting transfers between devices: 56.5 us -> 63.6 us
  local copies, waits for them, and re-layouts: 7.48 us -> 11.8 us
    unnamed x82 -> x84, local copies, waits for them, and re-layouts: 5.77 us -> 9.03 us
    ppermute x18, starting transfers between devices: 34.4 us -> 37.5 us  [partner_2(): return lax.ppermute(block, axis, route)]
    ppermute x4, starting transfers between devices: 10.9 us -> 13.2 us  [body(): gathered = lax.ppermute(sends[step_level], 'seq', back)]
    concatenate x2 -> x0, other arithmetic: 2.2 us -> none  [body(): jnp.concatenate(p, axis=1)]
  transfers between devices with their start and end apart: 34 -> 34, of which waited for: 8 -> 9; matrix products, arithmetic and copies ran while one was open for 25% -> 25% of each run, Pallas kernels for 17% -> 16%
where the time goes in v20:
time: 180 us; the launch traced here: 178 us
  starting transfers between devices  63.6 us (35%)
  Pallas kernels  28.6 us (16%)
  waiting for transfers between devices  25.8 us (14%)
  other arithmetic  24.1 us (13%)
  matrix products  22.4 us (12%)
  local copies, waits for them, and re-layouts  11.8 us (7%)
    ppermute x18, starting transfers between devices, partner_2(): return lax.ppermute(block, axis, route)  37.5 us
    pallas_call x4, Pallas kernels, attention(): pl.pallas_call(functools.partial(attention_kernel, scale=score_scale, par...  28.6 us
    dot_general x33, matrix products, apply(): jnp.einsum('pr,krw->kpw', matrix, rows.astype(jnp.float32), precision=lax...  20.5 us
    ppermute x18, waiting for transfers between devices, partner_2(): return lax.ppermute(block, axis, route)  20.4 us
    ppermute x4, starting transfers between devices, body(): gathered = lax.ppermute(sends[step_level], 'seq', back)  13.2 us
    unnamed x84, local copies, waits for them, and re-layouts  9.03 us
    convert_element_type x8, other arithmetic, body(): sends[step_level] = outgoing.astype(jnp.bfloat16)  6.16 us
    ppermute x4, starting transfers between devices, body(): passed = lax.ppermute(crossed, 'seq', outer_pairs(seq_count, step_level))  5.15 us
  transfers between devices with their start and end apart: 34, of which 9 were waited for; matrix products, arithmetic and copies ran while one was open for 25% of the time, Pallas kernels for 16%

profile of v20, /device:TPU:0, one launch (start us, length us, event | category | flops | bytes accessed | tf_op | source)
XLA Modules:
  0.0 178.0 jit_solution(3765623057892575205)
XLA Ops:
  0.7 1.6 convolution_bitcast_fusion
  3.5 3.0 %collective-permute-start = (bf16[2,64,2048]{2,1,0:T(8,128)(2,1)}, bf16[2,64,2048]{2,1,0:T(8,128)(2,1)}, u32[]{:S(2)}, u32[]{:S(2)}) collective-permute-start(bf16[2,64,2048]{2,1,0:T(8,128)(2,1)} %fusion.17), channel_id=1, source_target_pairs={{0,4},{4,0},{8,12},{12,8},{16,20},{20,16},{24,28},{28,24},{1,5},{5... | collective-permute-start | bytes 1572872 | tf_op jit(solution)/shard_map/ppermute | solution.py:22
  9.4 1.9 %pad_maximum_fusion.4.refs_0_ = bf16[2,256,512]{2,1,0:T(8,128)(2,1)} fusion(bf16[1,256,512]{2,1,0:T(8,128)(2,1)} %get-tuple-element.70, bf16[1,256,512]{2,1,0:T(8,128)(2,1)} %get-tuple-element.93), kind=kLoop, calls=%fused_computation.64 | loop fusion | flops 262144 | bytes 1048576 | tf_op jit(solution)/shard_map/stack | solution.py:150
  15.2 3.5 %collective-permute-done = bf16[2,64,2048]{2,1,0:T(8,128)(2,1)} collective-permute-done((bf16[2,64,2048]{2,1,0:T(8,128)(2,1)}, bf16[2,64,2048]{2,1,0:T(8,128)(2,1)}, u32[]{:S(2)}, u32[]{:S(2)}) %collective-permute-start) | collective-permute-done | bytes 524320 | tf_op jit(solution)/shard_map/ppermute | solution.py:22
  20.0 1.9 %collective-permute-start.2 = (bf16[2,128,512]{2,1,0:T(8,128)(2,1)S(1)}, bf16[2,128,512]{2,1,0:T(8,128)(2,1)S(1)}, u32[]{:S(2)}, u32[]{:S(2)}) collective-permute-start(bf16[2,128,512]{2,1,0:T(8,128)(2,1)S(1)} %get-tuple-element.82), channel_id=1, source_target_pairs={{0,8},{8,0},{4,12},{12,4},{16,24},{24,16},{20,28},{28,20},{1,9},{9... | collective-permute-start | bytes 786440 | tf_op jit(solution)/shard_map/ppermute | solution.py:22
  24.6 1.9 %collective-permute-start.12 = (bf16[2,128,512]{2,1,0:T(8,128)(2,1)S(1)}, bf16[2,128,512]{2,1,0:T(8,128)(2,1)S(1)}, u32[]{:S(2)}, u32[]{:S(2)}) collective-permute-start(bf16[2,128,512]{2,1,0:T(8,128)(2,1)S(1)} %get-tuple-element.86), channel_id=1, source_target_pairs={{0,8},{8,0},{4,12},{12,4},{16,24},{24,16},{20,28},{28,20},{1,9},{9... | collective-permute-start | bytes 786440 | tf_op jit(solution)/shard_map/ppermute | solution.py:22
  29.3 5.6 %collective-permute-done.6.refs_2_ = bf16[2,128,512]{2,1,0:T(8,128)(2,1)S(1)} collective-permute-done((bf16[2,128,512]{2,1,0:T(8,128)(2,1)S(1)}, bf16[2,128,512]{2,1,0:T(8,128)(2,1)S(1)}, u32[]{:S(2)}, u32[]{:S(2)}) %collective-permute-start.6) | collective-permute-done | bytes 262176 | tf_op jit(solution)/shard_map/ppermute | solution.py:22
  37.3 1.7 collective-permute-start.1
  42.8 2.1 %collective-permute-done.19.refs_2_ = bf16[2,128,512]{2,1,0:T(8,128)(2,1)S(1)} collective-permute-done((bf16[2,128,512]{2,1,0:T(8,128)(2,1)S(1)}, bf16[2,128,512]{2,1,0:T(8,128)(2,1)S(1)}, u32[]{:S(2)}, u32[]{:S(2)}) %collective-permute-start.19) | collective-permute-done | bytes 262176 | tf_op jit(solution)/shard_map/ppermute | solution.py:22
  44.9 1.4 collective-permute-start.13
  46.7 1.5 collective-permute-start.20
  48.2 4.9 %collective-permute-done.8 = bf16[2,128,512]{2,1,0:T(8,128)(2,1)S(1)} collective-permute-done((bf16[2,128,512]{2,1,0:T(8,128)(2,1)S(1)}, bf16[2,128,512]{2,1,0:T(8,128)(2,1)S(1)}, u32[]{:S(2)}, u32[]{:S(2)}) %collective-permute-start.8) | collective-permute-done | bytes 262176 | tf_op jit(solution)/shard_map/ppermute | solution.py:161
  55.1 4.7 %collective-permute-done.5.refs_1_ = bf16[2,256,512]{2,1,0:T(8,128)(2,1)S(1)} collective-permute-done((bf16[2,256,512]{2,1,0:T(8,128)(2,1)S(1)}, bf16[2,256,512]{2,1,0:T(8,128)(2,1)S(1)}, u32[]{:S(2)}, u32[]{:S(2)}) %collective-permute-start.5) | collective-permute-done | bytes 524320 | tf_op jit(solution)/shard_map/ppermute | solution.py:22
  60.6 1.7 collective-permute-start.11
  62.4 7.1 %shard_map.76 = (bf16[256,512]{1,0:T(8,128)(2,1)}, bf16[256,512]{1,0:T(8,128)(2,1)}, f32[2,256,512]{2,1,0:T(8,128)}, f32[2,256,512]{2,1,0:T(8,128)}, f32[2,128,512]{2,1,0:T(8,128)}, /*index=5*/f32[2,128,512]{2,1,0:T(8,128)}) custom-call(f32[1,768]{1,0:T(1,128)} %constant.104.clone.1.bias_ref, bf16[256,2048]{1,0:T(8,128)(2,1)} %q_ref.7, ...), custom_call_target="tpu_custom_call" | custom-call | flops 1207959552 | bytes 5767168 | tf_op jit(solution)/shard_map/pallas_call | solution.py:72
  74.3 7.8 %collective-permute-start.15 = (bf16[2,128,512]{2,1,0:T(8,128)(2,1)S(1)}, bf16[2,128,512]{2,1,0:T(8,128)(2,1)}, u32[]{:S(2)}, u32[]{:S(2)}) collective-permute-start(bf16[2,128,512]{2,1,0:T(8,128)(2,1)S(1)} %convert_element_type.195), channel_id=1, source_target_pairs={{0,8},{4,12},{24,16},{28,20},{1,9},{5,13},{25,17},{29,21},{2,10},{... | collective-permute-start | bytes 786440 | tf_op jit(solution)/shard_map/ppermute | solution.py:187
  82.1 7.1 %shard_map.75 = (bf16[256,512]{1,0:T(8,128)(2,1)}, bf16[256,512]{1,0:T(8,128)(2,1)}, f32[2,256,512]{2,1,0:T(8,128)}, f32[2,256,512]{2,1,0:T(8,128)}, f32[2,128,512]{2,1,0:T(8,128)}, /*index=5*/f32[2,128,512]{2,1,0:T(8,128)}) custom-call(f32[1,768]{1,0:T(1,128)} %constant.104.clone.1.bias_ref, bf16[256,2048]{1,0:T(8,128)(2,1)} %q_ref.7, ...), custom_call_target="tpu_custom_call" | custom-call | flops 1207959552 | bytes 5767168 | tf_op jit(solution)/shard_map/pallas_call | solution.py:72
  90.5 1.4 collective-permute-start.9
  93.8 1.7 broadcast_select_fusion.refs_3_
  100.2 7.8 %collective-permute-start.17 = (bf16[2,128,512]{2,1,0:T(8,128)(2,1)}, bf16[2,128,512]{2,1,0:T(8,128)(2,1)}, u32[]{:S(2)}, u32[]{:S(2)}) collective-permute-start(bf16[2,128,512]{2,1,0:T(8,128)(2,1)} %add_convert_fusion.13), channel_id=1, source_target_pairs={{0,8},{8,0},{4,12},{12,4},{16,24},{24,16},{20,28},{28,20},{1,9},{9... | collective-permute-start | bytes 786440 | tf_op jit(solution)/shard_map/ppermute | solution.py:22
  108.5 3.1 %collective-permute-start.23 = (bf16[2,128,512]{2,1,0:T(8,128)(2,1)S(1)}, bf16[2,128,512]{2,1,0:T(8,128)(2,1)}, u32[]{:S(2)}, u32[]{:S(2)}) collective-permute-start(bf16[2,128,512]{2,1,0:T(8,128)(2,1)S(1)} %add_convert_fusion.11), channel_id=1, source_target_pairs={{0,8},{8,0},{4,12},{12,4},{16,24},{24,16},{20,28},{28,20},{1,9},{9... | collective-permute-start | bytes 786440 | tf_op jit(solution)/shard_map/ppermute | solution.py:22
  111.6 7.2 %shard_map.77 = (bf16[256,512]{1,0:T(8,128)(2,1)}, bf16[256,512]{1,0:T(8,128)(2,1)}, f32[2,256,512]{2,1,0:T(8,128)}, f32[2,256,512]{2,1,0:T(8,128)}, f32[2,128,512]{2,1,0:T(8,128)}, /*index=5*/f32[2,128,512]{2,1,0:T(8,128)}) custom-call(f32[1,768]{1,0:T(1,128)} %constant.104.clone.1.bias_ref, bf16[256,2048]{1,0:T(8,128)(2,1)} %q_ref.7, ...), custom_call_target="tpu_custom_call" | custom-call | flops 1207959552 | bytes 5767168 | tf_op jit(solution)/shard_map/pallas_call | solution.py:72
  118.8 1.8 %convert_element_type.210 = bf16[2,128,512]{2,1,0:T(8,128)(2,1)} convert(f32[2,128,512]{2,1,0:T(8,128)} %get-tuple-element.59) | non-fusion elementwise | flops 131072 | bytes 786432 | tf_op jit(solution)/shard_map/convert_element_type | solution.py:182
  120.6 2.6 %collective-permute-start.25 = (bf16[2,128,512]{2,1,0:T(8,128)(2,1)}, bf16[2,128,512]{2,1,0:T(8,128)(2,1)}, u32[]{:S(2)}, u32[]{:S(2)}) collective-permute-start(bf16[2,128,512]{2,1,0:T(8,128)(2,1)} %convert_element_type.210), channel_id=1, source_target_pairs={{0,8},{4,12},{24,16},{28,20},{1,9},{5,13},{25,17},{29,21},{2,10},{... | collective-permute-start | bytes 786440 | tf_op jit(solution)/shard_map/ppermute | solution.py:187
  127.1 1.6 collective-permute-start.24
  133.5 7.2 %shard_map.78 = (bf16[256,512]{1,0:T(8,128)(2,1)}, bf16[256,512]{1,0:T(8,128)(2,1)}, f32[2,256,512]{2,1,0:T(8,128)}, f32[2,256,512]{2,1,0:T(8,128)}, f32[2,128,512]{2,1,0:T(8,128)}, /*index=5*/f32[2,128,512]{2,1,0:T(8,128)}) custom-call(f32[1,768]{1,0:T(1,128)} %constant.104.clone.1.bias_ref, bf16[256,2048]{1,0:T(8,128)(2,1)} %q_ref.7, ...), custom_call_target="tpu_custom_call" | custom-call | flops 1207959552 | bytes 5767168 | tf_op jit(solution)/shard_map/pallas_call | solution.py:72
  144.4 1.6 collective-permute-start.33
  151.3 4.6 %collective-permute-start.27 = (bf16[2,128,512]{2,1,0:T(8,128)(2,1)S(1)}, bf16[2,128,512]{2,1,0:T(8,128)(2,1)S(1)}, u32[]{:S(2)}, u32[]{:S(2)}) collective-permute-start(bf16[2,128,512]{2,1,0:T(8,128)(2,1)S(1)} %add_convert_fusion.9), channel_id=1, source_target_pairs={{0,8},{8,0},{4,12},{12,4},{16,24},{24,16},{20,28},{28,20},{1,9},{9... | collective-permute-start | bytes 786440 | tf_op jit(solution)/shard_map/ppermute | solution.py:22
  156.4 4.6 %collective-permute-start.31 = (bf16[2,128,512]{2,1,0:T(8,128)(2,1)S(1)}, bf16[2,128,512]{2,1,0:T(8,128)(2,1)S(1)}, u32[]{:S(2)}, u32[]{:S(2)}) collective-permute-start(bf16[2,128,512]{2,1,0:T(8,128)(2,1)S(1)} %add_convert_fusion.7), channel_id=1, source_target_pairs={{0,8},{8,0},{4,12},{12,4},{16,24},{24,16},{20,28},{28,20},{1,9},{9... | collective-permute-start | bytes 786440 | tf_op jit(solution)/shard_map/ppermute | solution.py:22
  162.9 1.8 %collective-permute-start.28 = (bf16[2,256,512]{2,1,0:T(8,128)(2,1)S(1)}, bf16[2,256,512]{2,1,0:T(8,128)(2,1)S(1)}, u32[]{:S(2)}, u32[]{:S(2)}) collective-permute-start(bf16[2,256,512]{2,1,0:T(8,128)(2,1)S(1)} %add_convert_fusion.2), channel_id=1, source_target_pairs={{0,4},{4,0},{8,12},{12,8},{16,20},{20,16},{24,28},{28,24},{1,5},{5... | collective-permute-start | bytes 1572872 | tf_op jit(solution)/shard_map/ppermute | solution.py:22
  165.5 1.4 add_convert_fusion.3
  170.6 3.9 %collective-permute-done.32 = bf16[2,64,512]{2,1,0:T(8,128)(2,1)S(1)} collective-permute-done((bf16[2,64,512]{2,1,0:T(8,128)(2,1)S(1)}, bf16[2,64,512]{2,1,0:T(8,128)(2,1)S(1)}, u32[]{:S(2)}, u32[]{:S(2)}) %collective-permute-start.32) | collective-permute-done | bytes 131104 | tf_op jit(solution)/shard_map/ppermute | solution.py:22
  (214 shorter events, 64.6 us)
Async XLA Ops:
  3.5 15.2 %collective-permute-start = (bf16[2,64,2048]{2,1,0:T(8,128)(2,1)}, bf16[2,64,2048]{2,1,0:T(8,128)(2,1)}, u32[]{:S(2)}, u32[]{:S(2)}) collective-permute-start(bf16[2,64,2048]{2,1,0:T(8,128)(2,1)} %fusion.17), channel_id=1, source_target_pairs={{0,4},{4,0},{8,12},{12,8},{16,20},{20,16},{24,28},{28,24},{1,5},{5... | collective-permute-start | bytes 1572872 | tf_op jit(solution)/shard_map/ppermute | solution.py:22
  20.0 19.1 %collective-permute-start.2 = (bf16[2,128,512]{2,1,0:T(8,128)(2,1)S(1)}, bf16[2,128,512]{2,1,0:T(8,128)(2,1)S(1)}, u32[]{:S(2)}, u32[]{:S(2)}) collective-permute-start(bf16[2,128,512]{2,1,0:T(8,128)(2,1)S(1)} %get-tuple-element.82), channel_id=1, source_target_pairs={{0,8},{8,0},{4,12},{12,4},{16,24},{24,16},{20,28},{28,20},{1,9},{9... | collective-permute-start | bytes 786440 | tf_op jit(solution)/shard_map/ppermute | solution.py:22
  23.1 11.8 %collective-permute-start.6 = (bf16[2,128,512]{2,1,0:T(8,128)(2,1)S(1)}, bf16[2,128,512]{2,1,0:T(8,128)(2,1)S(1)}, u32[]{:S(2)}, u32[]{:S(2)}) collective-permute-start(bf16[2,128,512]{2,1,0:T(8,128)(2,1)S(1)} %get-tuple-element.84), channel_id=1, source_target_pairs={{0,8},{8,0},{4,12},{12,4},{16,24},{24,16},{20,28},{28,20},{1,9},{9... | collective-permute-start | bytes 786440 | tf_op jit(solution)/shard_map/ppermute | solution.py:22
  24.6 15.9 %collective-permute-start.12 = (bf16[2,128,512]{2,1,0:T(8,128)(2,1)S(1)}, bf16[2,128,512]{2,1,0:T(8,128)(2,1)S(1)}, u32[]{:S(2)}, u32[]{:S(2)}) collective-permute-start(bf16[2,128,512]{2,1,0:T(8,128)(2,1)S(1)} %get-tuple-element.86), channel_id=1, source_target_pairs={{0,8},{8,0},{4,12},{12,4},{16,24},{24,16},{20,28},{28,20},{1,9},{9... | collective-permute-start | bytes 786440 | tf_op jit(solution)/shard_map/ppermute | solution.py:22
  27.8 17.1 %collective-permute-start.19 = (bf16[2,128,512]{2,1,0:T(8,128)(2,1)S(1)}, bf16[2,128,512]{2,1,0:T(8,128)(2,1)S(1)}, u32[]{:S(2)}, u32[]{:S(2)}) collective-permute-start(bf16[2,128,512]{2,1,0:T(8,128)(2,1)S(1)} %get-tuple-element.88), channel_id=1, source_target_pairs={{0,8},{8,0},{4,12},{12,4},{16,24},{24,16},{20,28},{28,20},{1,9},{9... | collective-permute-start | bytes 786440 | tf_op jit(solution)/shard_map/ppermute | solution.py:22
  35.6 5.6 %collective-permute-start.7 = (bf16[2,128,512]{2,1,0:T(8,128)(2,1)S(1)}, bf16[2,128,512]{2,1,0:T(8,128)(2,1)S(1)}, u32[]{:S(2)}, u32[]{:S(2)}) collective-permute-start(bf16[2,128,512]{2,1,0:T(8,128)(2,1)S(1)} %fusion.14), channel_id=1, source_target_pairs={{8,16},{12,20},{16,8},{20,12},{9,17},{13,21},{17,9},{21,13},{10,18... | collective-permute-start | bytes 786440 | tf_op jit(solution)/shard_map/ppermute | solution.py:160
  37.3 37.0 %collective-permute-start.1 = (bf16[2,256,512]{2,1,0:T(8,128)(2,1)S(1)}, bf16[2,256,512]{2,1,0:T(8,128)(2,1)}, u32[]{:S(2)}, u32[]{:S(2)}) collective-permute-start(bf16[2,256,512]{2,1,0:T(8,128)(2,1)S(1)} %copy-done.23), channel_id=1, source_target_pairs={{0,4},{4,0},{8,12},{12,8},{16,20},{20,16},{24,28},{28,24},{1,5},{5... | collective-permute-start | bytes 1572872 | tf_op jit(solution)/shard_map/ppermute | solution.py:22
  39.0 20.8 %collective-permute-start.5 = (bf16[2,256,512]{2,1,0:T(8,128)(2,1)S(1)}, bf16[2,256,512]{2,1,0:T(8,128)(2,1)S(1)}, u32[]{:S(2)}, u32[]{:S(2)}) collective-permute-start(bf16[2,256,512]{2,1,0:T(8,128)(2,1)S(1)} %copy-done.24), channel_id=1, source_target_pairs={{0,4},{4,0},{8,12},{12,8},{16,20},{20,16},{24,28},{28,24},{1,5},{5... | collective-permute-start | bytes 1572872 | tf_op jit(solution)/shard_map/ppermute | solution.py:22
  40.5 6.2 %collective-permute-start.3 = (bf16[2,128,512]{2,1,0:T(8,128)(2,1)S(1)}, bf16[2,128,512]{2,1,0:T(8,128)(2,1)S(1)}, u32[]{:S(2)}, u32[]{:S(2)}) collective-permute-start(bf16[2,128,512]{2,1,0:T(8,128)(2,1)S(1)} %fusion.15), channel_id=1, source_target_pairs={{8,16},{12,20},{16,8},{20,12},{9,17},{13,21},{17,9},{21,13},{10,18... | collective-permute-start | bytes 786440 | tf_op jit(solution)/shard_map/ppermute | solution.py:160
  41.2 11.9 %collective-permute-start.8 = (bf16[2,128,512]{2,1,0:T(8,128)(2,1)S(1)}, bf16[2,128,512]{2,1,0:T(8,128)(2,1)S(1)}, u32[]{:S(2)}, u32[]{:S(2)}) collective-permute-start(bf16[2,128,512]{2,1,0:T(8,128)(2,1)S(1)} %collective-permute-done.7), channel_id=1, source_target_pairs={{8,0},{12,4},{16,24},{20,28},{9,1},{13,5},{17,25},{21,29},{10,2},{... | collective-permute-start | bytes 786440 | tf_op jit(solution)/shard_map/ppermute | solution.py:161
  44.9 25.6 %collective-permute-start.13 = (bf16[2,128,512]{2,1,0:T(8,128)(2,1)S(1)}, bf16[2,128,512]{2,1,0:T(8,128)(2,1)}, u32[]{:S(2)}, u32[]{:S(2)}) collective-permute-start(bf16[2,128,512]{2,1,0:T(8,128)(2,1)S(1)} %fusion.13), channel_id=1, source_target_pairs={{8,16},{12,20},{16,8},{20,12},{9,17},{13,21},{17,9},{21,13},{10,18... | collective-permute-start | bytes 786440 | tf_op jit(solution)/shard_map/ppermute | solution.py:160
  46.7 24.2 %collective-permute-start.20 = (bf16[2,128,512]{2,1,0:T(8,128)(2,1)S(1)}, bf16[2,128,512]{2,1,0:T(8,128)(2,1)}, u32[]{:S(2)}, u32[]{:S(2)}) collective-permute-start(bf16[2,128,512]{2,1,0:T(8,128)(2,1)S(1)} %fusion.12), channel_id=1, source_target_pairs={{8,16},{12,20},{16,8},{20,12},{9,17},{13,21},{17,9},{21,13},{10,18... | collective-permute-start | bytes 786440 | tf_op jit(solution)/shard_map/ppermute | solution.py:160
  53.1 19.1 %collective-permute-start.4 = (bf16[2,128,512]{2,1,0:T(8,128)(2,1)S(1)}, bf16[2,128,512]{2,1,0:T(8,128)(2,1)S(1)}, u32[]{:S(2)}, u32[]{:S(2)}) collective-permute-start(bf16[2,128,512]{2,1,0:T(8,128)(2,1)S(1)} %collective-permute-done.3), channel_id=1, source_target_pairs={{8,0},{12,4},{16,24},{20,28},{9,1},{13,5},{17,25},{21,29},{10,2},{... | collective-permute-start | bytes 786440 | tf_op jit(solution)/shard_map/ppermute | solution.py:161
  60.6 51.0 %collective-permute-start.11 = (bf16[2,256,512]{2,1,0:T(8,128)(2,1)S(1)}, bf16[2,256,512]{2,1,0:T(8,128)(2,1)}, u32[]{:S(2)}, u32[]{:S(2)}) collective-permute-start(bf16[2,256,512]{2,1,0:T(8,128)(2,1)S(1)} %copy-done.22), channel_id=1, source_target_pairs={{0,4},{4,0},{8,12},{12,8},{16,20},{20,16},{24,28},{28,24},{1,5},{5... | collective-permute-start | bytes 1572872 | tf_op jit(solution)/shard_map/ppermute | solution.py:22
  70.6 62.9 %collective-permute-start.18 = (bf16[2,256,512]{2,1,0:T(8,128)(2,1)}, bf16[2,256,512]{2,1,0:T(8,128)(2,1)}, u32[]{:S(2)}, u32[]{:S(2)}) collective-permute-start(bf16[2,256,512]{2,1,0:T(8,128)(2,1)} %pad_maximum_fusion.4.refs_0_), channel_id=1, source_target_pairs={{0,4},{4,0},{8,12},{12,8},{16,20},{20,16},{24,28},{28,24},{1,5},{5... | collective-permute-start | bytes 1572872 | tf_op jit(solution)/shard_map/ppermute | solution.py:22
  70.9 19.6 %collective-permute-start.14 = (bf16[2,128,512]{2,1,0:T(8,128)(2,1)}, bf16[2,128,512]{2,1,0:T(8,128)(2,1)S(1)}, u32[]{:S(2)}, u32[]{:S(2)}) collective-permute-start(bf16[2,128,512]{2,1,0:T(8,128)(2,1)} %collective-permute-done.13), channel_id=1, source_target_pairs={{8,0},{12,4},{16,24},{20,28},{9,1},{13,5},{17,25},{21,29},{10,2},{... | collective-permute-start | bytes 786440 | tf_op jit(solution)/shard_map/ppermute | solution.py:161
  72.2 21.5 %collective-permute-start.21 = (bf16[2,128,512]{2,1,0:T(8,128)(2,1)}, bf16[2,128,512]{2,1,0:T(8,128)(2,1)}, u32[]{:S(2)}, u32[]{:S(2)}) collective-permute-start(bf16[2,128,512]{2,1,0:T(8,128)(2,1)} %collective-permute-done.20), channel_id=1, source_target_pairs={{8,0},{12,4},{16,24},{20,28},{9,1},{13,5},{17,25},{21,29},{10,2},{... | collective-permute-start | bytes 786440 | tf_op jit(solution)/shard_map/ppermute | solution.py:161
  74.3 22.5 %collective-permute-start.15 = (bf16[2,128,512]{2,1,0:T(8,128)(2,1)S(1)}, bf16[2,128,512]{2,1,0:T(8,128)(2,1)}, u32[]{:S(2)}, u32[]{:S(2)}) collective-permute-start(bf16[2,128,512]{2,1,0:T(8,128)(2,1)S(1)} %convert_element_type.195), channel_id=1, source_target_pairs={{0,8},{4,12},{24,16},{28,20},{1,9},{5,13},{25,17},{29,21},{2,10},{... | collective-permute-start | bytes 786440 | tf_op jit(solution)/shard_map/ppermute | solution.py:187
  90.5 5.3 %collective-permute-start.9 = (bf16[2,128,512]{2,1,0:T(8,128)(2,1)S(1)}, bf16[2,128,512]{2,1,0:T(8,128)(2,1)S(1)}, u32[]{:S(2)}, u32[]{:S(2)}) collective-permute-start(bf16[2,128,512]{2,1,0:T(8,128)(2,1)S(1)} %convert_element_type.188), channel_id=1, source_target_pairs={{0,8},{4,12},{24,16},{28,20},{1,9},{5,13},{25,17},{29,21},{2,10},{... | collective-permute-start | bytes 786440 | tf_op jit(solution)/shard_map/ppermute | solution.py:187
  98.0 10.0 %collective-permute-start.16 = (bf16[2,128,512]{2,1,0:T(8,128)(2,1)S(1)}, bf16[2,128,512]{2,1,0:T(8,128)(2,1)S(1)}, u32[]{:S(2)}, u32[]{:S(2)}) collective-permute-start(bf16[2,128,512]{2,1,0:T(8,128)(2,1)S(1)} %add_convert_fusion.12), channel_id=1, source_target_pairs={{8,16},{12,20},{16,8},{20,12},{9,17},{13,21},{17,9},{21,13},{10,18... | collective-permute-start | bytes 786440 | tf_op jit(solution)/shard_map/ppermute | solution.py:189
  100.2 28.5 %collective-permute-start.17 = (bf16[2,128,512]{2,1,0:T(8,128)(2,1)}, bf16[2,128,512]{2,1,0:T(8,128)(2,1)}, u32[]{:S(2)}, u32[]{:S(2)}) collective-permute-start(bf16[2,128,512]{2,1,0:T(8,128)(2,1)} %add_convert_fusion.13), channel_id=1, source_target_pairs={{0,8},{8,0},{4,12},{12,4},{16,24},{24,16},{20,28},{28,20},{1,9},{9... | collective-permute-start | bytes 786440 | tf_op jit(solution)/shard_map/ppermute | solution.py:22
  108.5 15.8 %collective-permute-start.23 = (bf16[2,128,512]{2,1,0:T(8,128)(2,1)S(1)}, bf16[2,128,512]{2,1,0:T(8,128)(2,1)}, u32[]{:S(2)}, u32[]{:S(2)}) collective-permute-start(bf16[2,128,512]{2,1,0:T(8,128)(2,1)S(1)} %add_convert_fusion.11), channel_id=1, source_target_pairs={{0,8},{8,0},{4,12},{12,4},{16,24},{24,16},{20,28},{28,20},{1,9},{9... | collective-permute-start | bytes 786440 | tf_op jit(solution)/shard_map/ppermute | solution.py:22
  120.6 26.1 %collective-permute-start.25 = (bf16[2,128,512]{2,1,0:T(8,128)(2,1)}, bf16[2,128,512]{2,1,0:T(8,128)(2,1)}, u32[]{:S(2)}, u32[]{:S(2)}) collective-permute-start(bf16[2,128,512]{2,1,0:T(8,128)(2,1)} %convert_element_type.210), channel_id=1, source_target_pairs={{0,8},{4,12},{24,16},{28,20},{1,9},{5,13},{25,17},{29,21},{2,10},{... | collective-permute-start | bytes 786440 | tf_op jit(solution)/shard_map/ppermute | solution.py:187
  127.1 38.3 %collective-permute-start.24 = (bf16[2,256,512]{2,1,0:T(8,128)(2,1)S(1)}, bf16[2,256,512]{2,1,0:T(8,128)(2,1)}, u32[]{:S(2)}, u32[]{:S(2)}) collective-permute-start(bf16[2,256,512]{2,1,0:T(8,128)(2,1)S(1)} %add_convert_fusion.4), channel_id=1, source_target_pairs={{0,4},{4,0},{8,12},{12,8},{16,20},{20,16},{24,28},{28,24},{1,5},{5... | collective-permute-start | bytes 1572872 | tf_op jit(solution)/shard_map/ppermute | solution.py:22
  132.3 34.6 %collective-permute-start.22 = (bf16[2,256,512]{2,1,0:T(8,128)(2,1)}, bf16[2,256,512]{2,1,0:T(8,128)(2,1)}, u32[]{:S(2)}, u32[]{:S(2)}) collective-permute-start(bf16[2,256,512]{2,1,0:T(8,128)(2,1)} %add_convert_fusion.6), channel_id=1, source_target_pairs={{0,4},{4,0},{8,12},{12,8},{16,20},{20,16},{24,28},{28,24},{1,5},{5... | collective-permute-start | bytes 1572872 | tf_op jit(solution)/shard_map/ppermute | solution.py:22
  141.7 7.7 %collective-permute-start.29 = (bf16[2,128,512]{2,1,0:T(8,128)(2,1)S(1)}, bf16[2,128,512]{2,1,0:T(8,128)(2,1)S(1)}, u32[]{:S(2)}, u32[]{:S(2)}) collective-permute-start(bf16[2,128,512]{2,1,0:T(8,128)(2,1)S(1)} %convert_element_type.218), channel_id=1, source_target_pairs={{0,8},{4,12},{24,16},{28,20},{1,9},{5,13},{25,17},{29,21},{2,10},{... | collective-permute-start | bytes 786440 | tf_op jit(solution)/shard_map/ppermute | solution.py:187
  144.4 30.6 %collective-permute-start.33 = (bf16[2,256,512]{2,1,0:T(8,128)(2,1)S(1)}, bf16[2,256,512]{2,1,0:T(8,128)(2,1)S(1)}, u32[]{:S(2)}, u32[]{:S(2)}) collective-permute-start(bf16[2,256,512]{2,1,0:T(8,128)(2,1)S(1)} %convert_element_type.225), channel_id=1, source_target_pairs={{0,4},{4,0},{8,12},{12,8},{16,20},{20,16},{24,28},{28,24},{1,5},{5... | collective-permute-start | bytes 1572872 | tf_op jit(solution)/shard_map/ppermute | solution.py:22
  149.7 6.2 %collective-permute-start.30 = (bf16[2,128,512]{2,1,0:T(8,128)(2,1)S(1)}, bf16[2,128,512]{2,1,0:T(8,128)(2,1)S(1)}, u32[]{:S(2)}, u32[]{:S(2)}) collective-permute-start(bf16[2,128,512]{2,1,0:T(8,128)(2,1)S(1)} %add_convert_fusion.8), channel_id=1, source_target_pairs={{8,16},{12,20},{16,8},{20,12},{9,17},{13,21},{17,9},{21,13},{10,18... | collective-permute-start | bytes 786440 | tf_op jit(solution)/shard_map/ppermute | solution.py:189
  151.3 9.7 %collective-permute-start.27 = (bf16[2,128,512]{2,1,0:T(8,128)(2,1)S(1)}, bf16[2,128,512]{2,1,0:T(8,128)(2,1)S(1)}, u32[]{:S(2)}, u32[]{:S(2)}) collective-permute-start(bf16[2,128,512]{2,1,0:T(8,128)(2,1)S(1)} %add_convert_fusion.9), channel_id=1, source_target_pairs={{0,8},{8,0},{4,12},{12,4},{16,24},{24,16},{20,28},{28,20},{1,9},{9... | collective-permute-start | bytes 786440 | tf_op jit(solution)/shard_map/ppermute | solution.py:22
  156.4 12.3 %collective-permute-start.31 = (bf16[2,128,512]{2,1,0:T(8,128)(2,1)S(1)}, bf16[2,128,512]{2,1,0:T(8,128)(2,1)S(1)}, u32[]{:S(2)}, u32[]{:S(2)}) collective-permute-start(bf16[2,128,512]{2,1,0:T(8,128)(2,1)S(1)} %add_convert_fusion.7), channel_id=1, source_target_pairs={{0,8},{8,0},{4,12},{12,4},{16,24},{24,16},{20,28},{28,20},{1,9},{9... | collective-permute-start | bytes 786440 | tf_op jit(solution)/shard_map/ppermute | solution.py:22
  162.9 12.5 %collective-permute-start.28 = (bf16[2,256,512]{2,1,0:T(8,128)(2,1)S(1)}, bf16[2,256,512]{2,1,0:T(8,128)(2,1)S(1)}, u32[]{:S(2)}, u32[]{:S(2)}) collective-permute-start(bf16[2,256,512]{2,1,0:T(8,128)(2,1)S(1)} %add_convert_fusion.2), channel_id=1, source_target_pairs={{0,4},{4,0},{8,12},{12,8},{16,20},{20,16},{24,28},{28,24},{1,5},{5... | collective-permute-start | bytes 1572872 | tf_op jit(solution)/shard_map/ppermute | solution.py:22
  169.5 5.0 %collective-permute-start.32 = (bf16[2,64,512]{2,1,0:T(8,128)(2,1)S(1)}, bf16[2,64,512]{2,1,0:T(8,128)(2,1)S(1)}, u32[]{:S(2)}, u32[]{:S(2)}) collective-permute-start(bf16[2,64,512]{2,1,0:T(8,128)(2,1)S(1)} %fusion.16), channel_id=1, source_target_pairs={{0,4},{4,0},{8,12},{12,8},{16,20},{20,16},{24,28},{28,24},{1,5},{5... | collective-permute-start | bytes 393224 | tf_op jit(solution)/shard_map/ppermute | solution.py:22
  (44 other events, 99.9 us)

commit v21 on v19

--- a/solution.py
+++ b/solution.py
@@ -107,7 +107,7 @@
 
 def apply(matrix, rows):
     return jnp.einsum(
-        "pr,krw->kpw", matrix, rows.astype(jnp.float32), precision=lax.Precision.HIGH,
+        "pr,krw->kpw", matrix, rows.astype(jnp.float32), precision=lax.Precision.DEFAULT,
         preferred_element_type=jnp.float32,
     )
 

time: 168 us -> 166 us (0.988)
  matrix products: 21.9 us -> 15.8 us
  waiting for transfers between devices: 27.4 us -> 32.7 us
  other arithmetic: 23.2 us -> 20.6 us
  starting transfers between devices: 56.5 us -> 58.2 us
    dot_general x33, matrix products: 20 us -> 13.9 us  [apply(): jnp.einsum('pr,krw->kpw', matrix, rows.astype(jnp.float32), precision=lax...]
    ppermute x18, waiting for transfers between devices: 19.5 us -> 23.5 us  [partner_2(): return lax.ppermute(block, axis, route)]
    another operation x4, other arithmetic: 3.56 us -> 1.38 us
    unnamed x82 -> x76, local copies, waits for them, and re-layouts: 5.77 us -> 5.2 us
  transfers between devices with their start and end apart: 34 -> 34, of which waited for: 8 -> 8; matrix products, arithmetic and copies ran while one was open for 25% -> 20% of each run, Pallas kernels for 17% -> 17%
where the time goes in v21:
time: 166 us; the launch traced here: 164 us
  starting transfers between devices  58.2 us (35%)
  waiting for transfers between devices  32.7 us (20%)
  Pallas kernels  28.7 us (17%)
  other arithmetic  20.6 us (12%)
  matrix products  15.8 us (10%)
  local copies, waits for them, and re-layouts  6.73 us (4%)
  between operations  1.7 us (1%)
    ppermute x18, starting transfers between devices, partner_2(): return lax.ppermute(block, axis, route)  35 us
    pallas_call x4, Pallas kernels, attention(): pl.pallas_call(functools.partial(attention_kernel, scale=score_scale, par...  28.7 us
    ppermute x18, waiting for transfers between devices, partner_2(): return lax.ppermute(block, axis, route)  23.5 us
    dot_general x33, matrix products, apply(): jnp.einsum('pr,krw->kpw', matrix, rows.astype(jnp.float32), precision=lax...  13.9 us
    ppermute x4, starting transfers between devices, body(): gathered = lax.ppermute(sends[step_level], 'seq', back)  12.4 us
    ppermute x4, waiting for transfers between devices, body(): passed = lax.ppermute(crossed, 'seq', outer_pairs(seq_count, step_level))  6.65 us
    convert_element_type x8, other arithmetic, body(): sends[step_level] = outgoing.astype(jnp.bfloat16)  5.44 us
    unnamed x76, local copies, waits for them, and re-layouts  5.2 us
  transfers between devices with their start and end apart: 34, of which 8 were waited for; matrix products, arithmetic and copies ran while one was open for 20% of the time, Pallas kernels for 17%

profile of v21, /device:TPU:0, one launch (start us, length us, event | category | flops | bytes accessed | tf_op | source)
XLA Modules:
  0.0 164.4 jit_solution(18362027433543485286)
XLA Ops:
  0.7 1.6 convolution_bitcast_fusion
  3.5 3.0 %collective-permute-start = (bf16[2,64,2048]{2,1,0:T(8,128)(2,1)}, bf16[2,64,2048]{2,1,0:T(8,128)(2,1)}, u32[]{:S(2)}, u32[]{:S(2)}) collective-permute-start(bf16[2,64,2048]{2,1,0:T(8,128)(2,1)} %fusion.17), channel_id=1, source_target_pairs={{0,4},{4,0},{8,12},{12,8},{16,20},{20,16},{24,28},{28,24},{1,5},{5... | collective-permute-start | bytes 1572872 | tf_op jit(solution)/shard_map/ppermute | solution.py:22
  8.8 1.9 %pad_maximum_fusion.5.refs_0_ = bf16[2,256,512]{2,1,0:T(8,128)(2,1)} fusion(bf16[1,256,512]{2,1,0:T(8,128)(2,1)} %get-tuple-element.70, bf16[1,256,512]{2,1,0:T(8,128)(2,1)} %get-tuple-element.85), kind=kLoop, calls=%fused_computation.65 | loop fusion | flops 262144 | bytes 1048576 | tf_op jit(solution)/shard_map/stack | solution.py:150
  13.8 4.8 %collective-permute-done = bf16[2,64,2048]{2,1,0:T(8,128)(2,1)} collective-permute-done((bf16[2,64,2048]{2,1,0:T(8,128)(2,1)}, bf16[2,64,2048]{2,1,0:T(8,128)(2,1)}, u32[]{:S(2)}, u32[]{:S(2)}) %collective-permute-start) | collective-permute-done | bytes 524320 | tf_op jit(solution)/shard_map/ppermute | solution.py:22
  19.9 1.9 %collective-permute-start.2 = (bf16[2,128,512]{2,1,0:T(8,128)(2,1)S(1)}, bf16[2,128,512]{2,1,0:T(8,128)(2,1)S(1)}, u32[]{:S(2)}, u32[]{:S(2)}) collective-permute-start(bf16[2,128,512]{2,1,0:T(8,128)(2,1)S(1)} %fusion.3), channel_id=1, source_target_pairs={{0,8},{8,0},{4,12},{12,4},{16,24},{24,16},{20,28},{28,20},{1,9},{9... | collective-permute-start | bytes 786440 | tf_op jit(solution)/shard_map/ppermute | solution.py:22
  24.4 1.9 %collective-permute-start.19 = (bf16[2,128,512]{2,1,0:T(8,128)(2,1)S(1)}, bf16[2,128,512]{2,1,0:T(8,128)(2,1)S(1)}, u32[]{:S(2)}, u32[]{:S(2)}) collective-permute-start(bf16[2,128,512]{2,1,0:T(8,128)(2,1)S(1)} %fusion), channel_id=1, source_target_pairs={{0,8},{8,0},{4,12},{12,4},{16,24},{24,16},{20,28},{28,20},{1,9},{9... | collective-permute-start | bytes 786440 | tf_op jit(solution)/shard_map/ppermute | solution.py:22
  28.5 6.3 %collective-permute-done.6.refs_2_ = bf16[2,128,512]{2,1,0:T(8,128)(2,1)S(1)} collective-permute-done((bf16[2,128,512]{2,1,0:T(8,128)(2,1)S(1)}, bf16[2,128,512]{2,1,0:T(8,128)(2,1)S(1)}, u32[]{:S(2)}, u32[]{:S(2)}) %collective-permute-start.6) | collective-permute-done | bytes 262176 | tf_op jit(solution)/shard_map/ppermute | solution.py:22
  36.0 1.8 %collective-permute-start.1 = (bf16[2,256,512]{2,1,0:T(8,128)(2,1)}, bf16[2,256,512]{2,1,0:T(8,128)(2,1)S(1)}, u32[]{:S(2)}, u32[]{:S(2)}) collective-permute-start(bf16[2,256,512]{2,1,0:T(8,128)(2,1)} %pad_maximum_fusion.3.refs_0_), channel_id=1, source_target_pairs={{0,4},{4,0},{8,12},{12,8},{16,20},{20,16},{24,28},{28,24},{1,5},{5... | collective-permute-start | bytes 1572872 | tf_op jit(solution)/shard_map/ppermute | solution.py:22
  38.5 5.8 %collective-permute-done.12.refs_2_ = bf16[2,128,512]{2,1,0:T(8,128)(2,1)S(1)} collective-permute-done((bf16[2,128,512]{2,1,0:T(8,128)(2,1)S(1)}, bf16[2,128,512]{2,1,0:T(8,128)(2,1)S(1)}, u32[]{:S(2)}, u32[]{:S(2)}) %collective-permute-start.12) | collective-permute-done | bytes 262176 | tf_op jit(solution)/shard_map/ppermute | solution.py:22
  44.9 1.3 collective-permute-start.8
  48.2 6.6 %collective-permute-done.8 = bf16[2,128,512]{2,1,0:T(8,128)(2,1)S(1)} collective-permute-done((bf16[2,128,512]{2,1,0:T(8,128)(2,1)S(1)}, bf16[2,128,512]{2,1,0:T(8,128)(2,1)S(1)}, u32[]{:S(2)}, u32[]{:S(2)}) %collective-permute-start.8) | collective-permute-done | bytes 262176 | tf_op jit(solution)/shard_map/ppermute | solution.py:161
  54.9 1.3 collective-permute-start.4
  59.9 7.2 %shard_map.76 = (bf16[256,512]{1,0:T(8,128)(2,1)}, bf16[256,512]{1,0:T(8,128)(2,1)}, f32[2,256,512]{2,1,0:T(8,128)}, f32[2,256,512]{2,1,0:T(8,128)}, f32[2,128,512]{2,1,0:T(8,128)}, /*index=5*/f32[2,128,512]{2,1,0:T(8,128)}) custom-call(f32[1,768]{1,0:T(1,128)} %constant.104.clone.1.bias_ref, bf16[256,2048]{1,0:T(8,128)(2,1)} %q_ref.7, ...), custom_call_target="tpu_custom_call" | custom-call | flops 1207959552 | bytes 5767168 | tf_op jit(solution)/shard_map/pallas_call | solution.py:72
  69.4 1.3 collective-permute-start.14
  70.7 1.3 collective-permute-start.21
  72.7 6.9 %collective-permute-start.15 = (bf16[2,128,512]{2,1,0:T(8,128)(2,1)S(1)}, bf16[2,128,512]{2,1,0:T(8,128)(2,1)S(1)}, u32[]{:S(2)}, u32[]{:S(2)}) collective-permute-start(bf16[2,128,512]{2,1,0:T(8,128)(2,1)S(1)} %convert_element_type.195), channel_id=1, source_target_pairs={{0,8},{4,12},{24,16},{28,20},{1,9},{5,13},{25,17},{29,21},{2,10},{... | collective-permute-start | bytes 786440 | tf_op jit(solution)/shard_map/ppermute | solution.py:187
  79.7 7.1 %shard_map.75 = (bf16[256,512]{1,0:T(8,128)(2,1)}, bf16[256,512]{1,0:T(8,128)(2,1)}, f32[2,256,512]{2,1,0:T(8,128)}, f32[2,256,512]{2,1,0:T(8,128)}, f32[2,128,512]{2,1,0:T(8,128)}, /*index=5*/f32[2,128,512]{2,1,0:T(8,128)}) custom-call(f32[1,768]{1,0:T(1,128)} %constant.104.clone.1.bias_ref, bf16[256,2048]{1,0:T(8,128)(2,1)} %q_ref.7, ...), custom_call_target="tpu_custom_call" | custom-call | flops 1207959552 | bytes 5767168 | tf_op jit(solution)/shard_map/pallas_call | solution.py:72
  88.0 1.3 collective-permute-start.9
  91.7 2.5 %collective-permute-done.9 = bf16[2,128,512]{2,1,0:T(8,128)(2,1)S(1)} collective-permute-done((bf16[2,128,512]{2,1,0:T(8,128)(2,1)S(1)}, bf16[2,128,512]{2,1,0:T(8,128)(2,1)S(1)}, u32[]{:S(2)}, u32[]{:S(2)}) %collective-permute-start.9) | collective-permute-done | bytes 262176 | tf_op jit(solution)/shard_map/ppermute | solution.py:187
  95.4 4.8 %collective-permute-start.23 = (bf16[2,128,512]{2,1,0:T(8,128)(2,1)S(1)}, bf16[2,128,512]{2,1,0:T(8,128)(2,1)S(1)}, u32[]{:S(2)}, u32[]{:S(2)}) collective-permute-start(bf16[2,128,512]{2,1,0:T(8,128)(2,1)S(1)} %add_convert_fusion.11), channel_id=1, source_target_pairs={{0,8},{8,0},{4,12},{12,4},{16,24},{24,16},{20,28},{28,20},{1,9},{9... | collective-permute-start | bytes 786440 | tf_op jit(solution)/shard_map/ppermute | solution.py:22
  100.7 4.8 %collective-permute-start.17 = (bf16[2,128,512]{2,1,0:T(8,128)(2,1)S(1)}, bf16[2,128,512]{2,1,0:T(8,128)(2,1)S(1)}, u32[]{:S(2)}, u32[]{:S(2)}) collective-permute-start(bf16[2,128,512]{2,1,0:T(8,128)(2,1)S(1)} %add_convert_fusion.13), channel_id=1, source_target_pairs={{0,8},{8,0},{4,12},{12,4},{16,24},{24,16},{20,28},{28,20},{1,9},{9... | collective-permute-start | bytes 786440 | tf_op jit(solution)/shard_map/ppermute | solution.py:22
  105.5 7.2 %shard_map.77 = (bf16[256,512]{1,0:T(8,128)(2,1)}, bf16[256,512]{1,0:T(8,128)(2,1)}, f32[2,256,512]{2,1,0:T(8,128)}, f32[2,256,512]{2,1,0:T(8,128)}, f32[2,128,512]{2,1,0:T(8,128)}, /*index=5*/f32[2,128,512]{2,1,0:T(8,128)}) custom-call(f32[1,768]{1,0:T(1,128)} %constant.104.clone.1.bias_ref, bf16[256,2048]{1,0:T(8,128)(2,1)} %q_ref.7, ...), custom_call_target="tpu_custom_call" | custom-call | flops 1207959552 | bytes 5767168 | tf_op jit(solution)/shard_map/pallas_call | solution.py:72
  112.7 1.8 %convert_element_type.210 = bf16[2,128,512]{2,1,0:T(8,128)(2,1)} convert(f32[2,128,512]{2,1,0:T(8,128)} %get-tuple-element.59) | non-fusion elementwise | flops 131072 | bytes 786432 | tf_op jit(solution)/shard_map/convert_element_type | solution.py:182
  114.5 2.8 %collective-permute-start.25 = (bf16[2,128,512]{2,1,0:T(8,128)(2,1)}, bf16[2,128,512]{2,1,0:T(8,128)(2,1)}, u32[]{:S(2)}, u32[]{:S(2)}) collective-permute-start(bf16[2,128,512]{2,1,0:T(8,128)(2,1)} %convert_element_type.210), channel_id=1, source_target_pairs={{0,8},{4,12},{24,16},{28,20},{1,9},{5,13},{25,17},{29,21},{2,10},{... | collective-permute-start | bytes 786440 | tf_op jit(solution)/shard_map/ppermute | solution.py:187
  118.3 1.6 collective-permute-start.24
  121.9 7.1 %shard_map.78 = (bf16[256,512]{1,0:T(8,128)(2,1)}, bf16[256,512]{1,0:T(8,128)(2,1)}, f32[2,256,512]{2,1,0:T(8,128)}, f32[2,256,512]{2,1,0:T(8,128)}, f32[2,128,512]{2,1,0:T(8,128)}, /*index=5*/f32[2,128,512]{2,1,0:T(8,128)}) custom-call(f32[1,768]{1,0:T(1,128)} %constant.104.clone.1.bias_ref, bf16[256,2048]{1,0:T(8,128)(2,1)} %q_ref.7, ...), custom_call_target="tpu_custom_call" | custom-call | flops 1207959552 | bytes 5767168 | tf_op jit(solution)/shard_map/pallas_call | solution.py:72
  130.1 1.3 collective-permute-start.29
  131.5 1.3 convert_element_type.225
  132.8 1.6 collective-permute-start.33
  140.6 3.4 %collective-permute-start.27 = (bf16[2,128,512]{2,1,0:T(8,128)(2,1)S(1)}, bf16[2,128,512]{2,1,0:T(8,128)(2,1)S(1)}, u32[]{:S(2)}, u32[]{:S(2)}) collective-permute-start(bf16[2,128,512]{2,1,0:T(8,128)(2,1)S(1)} %add_convert_fusion.9), channel_id=1, source_target_pairs={{0,8},{8,0},{4,12},{12,4},{16,24},{24,16},{20,28},{28,20},{1,9},{9... | collective-permute-start | bytes 786440 | tf_op jit(solution)/shard_map/ppermute | solution.py:22
  144.4 4.9 %collective-permute-start.31 = (bf16[2,128,512]{2,1,0:T(8,128)(2,1)S(1)}, bf16[2,128,512]{2,1,0:T(8,128)(2,1)S(1)}, u32[]{:S(2)}, u32[]{:S(2)}) collective-permute-start(bf16[2,128,512]{2,1,0:T(8,128)(2,1)S(1)} %add_convert_fusion.7), channel_id=1, source_target_pairs={{0,8},{8,0},{4,12},{12,4},{16,24},{24,16},{20,28},{28,20},{1,9},{9... | collective-permute-start | bytes 786440 | tf_op jit(solution)/shard_map/ppermute | solution.py:22
  155.9 5.1 %collective-permute-done.32 = bf16[2,64,512]{2,1,0:T(8,128)(2,1)S(1)} collective-permute-done((bf16[2,64,512]{2,1,0:T(8,128)(2,1)S(1)}, bf16[2,64,512]{2,1,0:T(8,128)(2,1)S(1)}, u32[]{:S(2)}, u32[]{:S(2)}) %collective-permute-start.32) | collective-permute-done | bytes 131104 | tf_op jit(solution)/shard_map/ppermute | solution.py:22
  (200 shorter events, 49.1 us)
Async XLA Ops:
  3.5 15.2 %collective-permute-start = (bf16[2,64,2048]{2,1,0:T(8,128)(2,1)}, bf16[2,64,2048]{2,1,0:T(8,128)(2,1)}, u32[]{:S(2)}, u32[]{:S(2)}) collective-permute-start(bf16[2,64,2048]{2,1,0:T(8,128)(2,1)} %fusion.17), channel_id=1, source_target_pairs={{0,4},{4,0},{8,12},{12,8},{16,20},{20,16},{24,28},{28,24},{1,5},{5... | collective-permute-start | bytes 1572872 | tf_op jit(solution)/shard_map/ppermute | solution.py:22
  19.9 18.0 %collective-permute-start.2 = (bf16[2,128,512]{2,1,0:T(8,128)(2,1)S(1)}, bf16[2,128,512]{2,1,0:T(8,128)(2,1)S(1)}, u32[]{:S(2)}, u32[]{:S(2)}) collective-permute-start(bf16[2,128,512]{2,1,0:T(8,128)(2,1)S(1)} %fusion.3), channel_id=1, source_target_pairs={{0,8},{8,0},{4,12},{12,4},{16,24},{24,16},{20,28},{28,20},{1,9},{9... | collective-permute-start | bytes 786440 | tf_op jit(solution)/shard_map/ppermute | solution.py:22
  22.9 11.9 %collective-permute-start.6 = (bf16[2,128,512]{2,1,0:T(8,128)(2,1)S(1)}, bf16[2,128,512]{2,1,0:T(8,128)(2,1)S(1)}, u32[]{:S(2)}, u32[]{:S(2)}) collective-permute-start(bf16[2,128,512]{2,1,0:T(8,128)(2,1)S(1)} %fusion.2), channel_id=1, source_target_pairs={{0,8},{8,0},{4,12},{12,4},{16,24},{24,16},{20,28},{28,20},{1,9},{9... | collective-permute-start | bytes 786440 | tf_op jit(solution)/shard_map/ppermute | solution.py:22
  24.4 22.2 %collective-permute-start.19 = (bf16[2,128,512]{2,1,0:T(8,128)(2,1)S(1)}, bf16[2,128,512]{2,1,0:T(8,128)(2,1)S(1)}, u32[]{:S(2)}, u32[]{:S(2)}) collective-permute-start(bf16[2,128,512]{2,1,0:T(8,128)(2,1)S(1)} %fusion), channel_id=1, source_target_pairs={{0,8},{8,0},{4,12},{12,4},{16,24},{24,16},{20,28},{28,20},{1,9},{9... | collective-permute-start | bytes 786440 | tf_op jit(solution)/shard_map/ppermute | solution.py:22
  28.0 16.3 %collective-permute-start.12 = (bf16[2,128,512]{2,1,0:T(8,128)(2,1)S(1)}, bf16[2,128,512]{2,1,0:T(8,128)(2,1)S(1)}, u32[]{:S(2)}, u32[]{:S(2)}) collective-permute-start(bf16[2,128,512]{2,1,0:T(8,128)(2,1)S(1)} %fusion.1), channel_id=1, source_target_pairs={{0,8},{8,0},{4,12},{12,4},{16,24},{24,16},{20,28},{28,20},{1,9},{9... | collective-permute-start | bytes 786440 | tf_op jit(solution)/shard_map/ppermute | solution.py:22
  35.1 9.9 %collective-permute-start.7 = (bf16[2,128,512]{2,1,0:T(8,128)(2,1)S(1)}, bf16[2,128,512]{2,1,0:T(8,128)(2,1)S(1)}, u32[]{:S(2)}, u32[]{:S(2)}) collective-permute-start(bf16[2,128,512]{2,1,0:T(8,128)(2,1)S(1)} %fusion.14), channel_id=1, source_target_pairs={{8,16},{12,20},{16,8},{20,12},{9,17},{13,21},{17,9},{21,13},{10,18... | collective-permute-start | bytes 786440 | tf_op jit(solution)/shard_map/ppermute | solution.py:160
  36.0 36.7 %collective-permute-start.1 = (bf16[2,256,512]{2,1,0:T(8,128)(2,1)}, bf16[2,256,512]{2,1,0:T(8,128)(2,1)S(1)}, u32[]{:S(2)}, u32[]{:S(2)}) collective-permute-start(bf16[2,256,512]{2,1,0:T(8,128)(2,1)} %pad_maximum_fusion.3.refs_0_), channel_id=1, source_target_pairs={{0,4},{4,0},{8,12},{12,8},{16,20},{20,16},{24,28},{28,24},{1,5},{5... | collective-permute-start | bytes 1572872 | tf_op jit(solution)/shard_map/ppermute | solution.py:22
  37.8 20.3 %collective-permute-start.5 = (bf16[2,256,512]{2,1,0:T(8,128)(2,1)S(1)}, bf16[2,256,512]{2,1,0:T(8,128)(2,1)S(1)}, u32[]{:S(2)}, u32[]{:S(2)}) collective-permute-start(bf16[2,256,512]{2,1,0:T(8,128)(2,1)S(1)} %copy-done.19), channel_id=1, source_target_pairs={{0,4},{4,0},{8,12},{12,8},{16,20},{20,16},{24,28},{28,24},{1,5},{5... | collective-permute-start | bytes 1572872 | tf_op jit(solution)/shard_map/ppermute | solution.py:22
  44.9 9.9 %collective-permute-start.8 = (bf16[2,128,512]{2,1,0:T(8,128)(2,1)S(1)}, bf16[2,128,512]{2,1,0:T(8,128)(2,1)S(1)}, u32[]{:S(2)}, u32[]{:S(2)}) collective-permute-start(bf16[2,128,512]{2,1,0:T(8,128)(2,1)S(1)} %collective-permute-done.7), channel_id=1, source_target_pairs={{8,0},{12,4},{16,24},{20,28},{9,1},{13,5},{17,25},{21,29},{10,2},{... | collective-permute-start | bytes 786440 | tf_op jit(solution)/shard_map/ppermute | solution.py:161
  46.6 21.6 %collective-permute-start.13 = (bf16[2,128,512]{2,1,0:T(8,128)(2,1)S(1)}, bf16[2,128,512]{2,1,0:T(8,128)(2,1)S(1)}, u32[]{:S(2)}, u32[]{:S(2)}) collective-permute-start(bf16[2,128,512]{2,1,0:T(8,128)(2,1)S(1)} %fusion.13), channel_id=1, source_target_pairs={{8,16},{12,20},{16,8},{20,12},{9,17},{13,21},{17,9},{21,13},{10,18... | collective-permute-start | bytes 786440 | tf_op jit(solution)/shard_map/ppermute | solution.py:160
  47.5 21.8 %collective-permute-start.20 = (bf16[2,128,512]{2,1,0:T(8,128)(2,1)S(1)}, bf16[2,128,512]{2,1,0:T(8,128)(2,1)S(1)}, u32[]{:S(2)}, u32[]{:S(2)}) collective-permute-start(bf16[2,128,512]{2,1,0:T(8,128)(2,1)S(1)} %fusion.12), channel_id=1, source_target_pairs={{8,16},{12,20},{16,8},{20,12},{9,17},{13,21},{17,9},{21,13},{10,18... | collective-permute-start | bytes 786440 | tf_op jit(solution)/shard_map/ppermute | solution.py:160
  54.9 15.8 %collective-permute-start.4 = (bf16[2,128,512]{2,1,0:T(8,128)(2,1)S(1)}, bf16[2,128,512]{2,1,0:T(8,128)(2,1)S(1)}, u32[]{:S(2)}, u32[]{:S(2)}) collective-permute-start(bf16[2,128,512]{2,1,0:T(8,128)(2,1)S(1)} %collective-permute-done.3), channel_id=1, source_target_pairs={{8,0},{12,4},{16,24},{20,28},{9,1},{13,5},{17,25},{21,29},{10,2},{... | collective-permute-start | bytes 786440 | tf_op jit(solution)/shard_map/ppermute | solution.py:161
  59.0 63.0 %collective-permute-start.18 = (bf16[2,256,512]{2,1,0:T(8,128)(2,1)}, bf16[2,256,512]{2,1,0:T(8,128)(2,1)}, u32[]{:S(2)}, u32[]{:S(2)}) collective-permute-start(bf16[2,256,512]{2,1,0:T(8,128)(2,1)} %pad_maximum_fusion.6.refs_0_), channel_id=1, source_target_pairs={{0,4},{4,0},{8,12},{12,8},{16,20},{20,16},{24,28},{28,24},{1,5},{5... | collective-permute-start | bytes 1572872 | tf_op jit(solution)/shard_map/ppermute | solution.py:22
  68.2 37.3 %collective-permute-start.11 = (bf16[2,256,512]{2,1,0:T(8,128)(2,1)S(1)}, bf16[2,256,512]{2,1,0:T(8,128)(2,1)}, u32[]{:S(2)}, u32[]{:S(2)}) collective-permute-start(bf16[2,256,512]{2,1,0:T(8,128)(2,1)S(1)} %copy-done.18), channel_id=1, source_target_pairs={{0,4},{4,0},{8,12},{12,8},{16,20},{20,16},{24,28},{28,24},{1,5},{5... | collective-permute-start | bytes 1572872 | tf_op jit(solution)/shard_map/ppermute | solution.py:22
  69.4 18.6 %collective-permute-start.14 = (bf16[2,128,512]{2,1,0:T(8,128)(2,1)S(1)}, bf16[2,128,512]{2,1,0:T(8,128)(2,1)S(1)}, u32[]{:S(2)}, u32[]{:S(2)}) collective-permute-start(bf16[2,128,512]{2,1,0:T(8,128)(2,1)S(1)} %collective-permute-done.13), channel_id=1, source_target_pairs={{8,0},{12,4},{16,24},{20,28},{9,1},{13,5},{17,25},{21,29},{10,2},{... | collective-permute-start | bytes 786440 | tf_op jit(solution)/shard_map/ppermute | solution.py:161
  70.7 20.2 %collective-permute-start.21 = (bf16[2,128,512]{2,1,0:T(8,128)(2,1)S(1)}, bf16[2,128,512]{2,1,0:T(8,128)(2,1)S(1)}, u32[]{:S(2)}, u32[]{:S(2)}) collective-permute-start(bf16[2,128,512]{2,1,0:T(8,128)(2,1)S(1)} %collective-permute-done.20), channel_id=1, source_target_pairs={{8,0},{12,4},{16,24},{20,28},{9,1},{13,5},{17,25},{21,29},{10,2},{... | collective-permute-start | bytes 786440 | tf_op jit(solution)/shard_map/ppermute | solution.py:161
  72.7 17.3 %collective-permute-start.15 = (bf16[2,128,512]{2,1,0:T(8,128)(2,1)S(1)}, bf16[2,128,512]{2,1,0:T(8,128)(2,1)S(1)}, u32[]{:S(2)}, u32[]{:S(2)}) collective-permute-start(bf16[2,128,512]{2,1,0:T(8,128)(2,1)S(1)} %convert_element_type.195), channel_id=1, source_target_pairs={{0,8},{4,12},{24,16},{28,20},{1,9},{5,13},{25,17},{29,21},{2,10},{... | collective-permute-start | bytes 786440 | tf_op jit(solution)/shard_map/ppermute | solution.py:187
  88.0 6.2 %collective-permute-start.9 = (bf16[2,128,512]{2,1,0:T(8,128)(2,1)S(1)}, bf16[2,128,512]{2,1,0:T(8,128)(2,1)S(1)}, u32[]{:S(2)}, u32[]{:S(2)}) collective-permute-start(bf16[2,128,512]{2,1,0:T(8,128)(2,1)S(1)} %convert_element_type.188), channel_id=1, source_target_pairs={{0,8},{4,12},{24,16},{28,20},{1,9},{5,13},{25,17},{29,21},{2,10},{... | collective-permute-start | bytes 786440 | tf_op jit(solution)/shard_map/ppermute | solution.py:187
  90.1 4.8 %collective-permute-start.16 = (bf16[2,128,512]{2,1,0:T(8,128)(2,1)S(1)}, bf16[2,128,512]{2,1,0:T(8,128)(2,1)S(1)}, u32[]{:S(2)}, u32[]{:S(2)}) collective-permute-start(bf16[2,128,512]{2,1,0:T(8,128)(2,1)S(1)} %add_convert_fusion.12), channel_id=1, source_target_pairs={{8,16},{12,20},{16,8},{20,12},{9,17},{13,21},{17,9},{21,13},{10,18... | collective-permute-start | bytes 786440 | tf_op jit(solution)/shard_map/ppermute | solution.py:189
  94.2 6.0 %collective-permute-start.10 = (bf16[2,128,512]{2,1,0:T(8,128)(2,1)S(1)}, bf16[2,128,512]{2,1,0:T(8,128)(2,1)S(1)}, u32[]{:S(2)}, u32[]{:S(2)}) collective-permute-start(bf16[2,128,512]{2,1,0:T(8,128)(2,1)S(1)} %add_convert_fusion.14), channel_id=1, source_target_pairs={{8,16},{12,20},{16,8},{20,12},{9,17},{13,21},{17,9},{21,13},{10,18... | collective-permute-start | bytes 786440 | tf_op jit(solution)/shard_map/ppermute | solution.py:189
  95.4 21.9 %collective-permute-start.23 = (bf16[2,128,512]{2,1,0:T(8,128)(2,1)S(1)}, bf16[2,128,512]{2,1,0:T(8,128)(2,1)S(1)}, u32[]{:S(2)}, u32[]{:S(2)}) collective-permute-start(bf16[2,128,512]{2,1,0:T(8,128)(2,1)S(1)} %add_convert_fusion.11), channel_id=1, source_target_pairs={{0,8},{8,0},{4,12},{12,4},{16,24},{24,16},{20,28},{28,20},{1,9},{9... | collective-permute-start | bytes 786440 | tf_op jit(solution)/shard_map/ppermute | solution.py:22
  100.7 19.2 %collective-permute-start.17 = (bf16[2,128,512]{2,1,0:T(8,128)(2,1)S(1)}, bf16[2,128,512]{2,1,0:T(8,128)(2,1)S(1)}, u32[]{:S(2)}, u32[]{:S(2)}) collective-permute-start(bf16[2,128,512]{2,1,0:T(8,128)(2,1)S(1)} %add_convert_fusion.13), channel_id=1, source_target_pairs={{0,8},{8,0},{4,12},{12,4},{16,24},{24,16},{20,28},{28,20},{1,9},{9... | collective-permute-start | bytes 786440 | tf_op jit(solution)/shard_map/ppermute | solution.py:22
  114.5 20.3 %collective-permute-start.25 = (bf16[2,128,512]{2,1,0:T(8,128)(2,1)}, bf16[2,128,512]{2,1,0:T(8,128)(2,1)}, u32[]{:S(2)}, u32[]{:S(2)}) collective-permute-start(bf16[2,128,512]{2,1,0:T(8,128)(2,1)} %convert_element_type.210), channel_id=1, source_target_pairs={{0,8},{4,12},{24,16},{28,20},{1,9},{5,13},{25,17},{29,21},{2,10},{... | collective-permute-start | bytes 786440 | tf_op jit(solution)/shard_map/ppermute | solution.py:187
  118.3 33.0 %collective-permute-start.24 = (bf16[2,256,512]{2,1,0:T(8,128)(2,1)S(1)}, bf16[2,256,512]{2,1,0:T(8,128)(2,1)S(1)}, u32[]{:S(2)}, u32[]{:S(2)}) collective-permute-start(bf16[2,256,512]{2,1,0:T(8,128)(2,1)S(1)} %add_convert_fusion.4), channel_id=1, source_target_pairs={{0,4},{4,0},{8,12},{12,8},{16,20},{20,16},{24,28},{28,24},{1,5},{5... | collective-permute-start | bytes 1572872 | tf_op jit(solution)/shard_map/ppermute | solution.py:22
  120.9 31.0 %collective-permute-start.22 = (bf16[2,256,512]{2,1,0:T(8,128)(2,1)S(1)}, bf16[2,256,512]{2,1,0:T(8,128)(2,1)S(1)}, u32[]{:S(2)}, u32[]{:S(2)}) collective-permute-start(bf16[2,256,512]{2,1,0:T(8,128)(2,1)S(1)} %add_convert_fusion.6), channel_id=1, source_target_pairs={{0,4},{4,0},{8,12},{12,8},{16,20},{20,16},{24,28},{28,24},{1,5},{5... | collective-permute-start | bytes 1572872 | tf_op jit(solution)/shard_map/ppermute | solution.py:22
  130.1 9.0 %collective-permute-start.29 = (bf16[2,128,512]{2,1,0:T(8,128)(2,1)S(1)}, bf16[2,128,512]{2,1,0:T(8,128)(2,1)S(1)}, u32[]{:S(2)}, u32[]{:S(2)}) collective-permute-start(bf16[2,128,512]{2,1,0:T(8,128)(2,1)S(1)} %convert_element_type.218), channel_id=1, source_target_pairs={{0,8},{4,12},{24,16},{28,20},{1,9},{5,13},{25,17},{29,21},{2,10},{... | collective-permute-start | bytes 786440 | tf_op jit(solution)/shard_map/ppermute | solution.py:187
  132.8 28.5 %collective-permute-start.33 = (bf16[2,256,512]{2,1,0:T(8,128)(2,1)S(1)}, bf16[2,256,512]{2,1,0:T(8,128)(2,1)S(1)}, u32[]{:S(2)}, u32[]{:S(2)}) collective-permute-start(bf16[2,256,512]{2,1,0:T(8,128)(2,1)S(1)} %convert_element_type.225), channel_id=1, source_target_pairs={{0,4},{4,0},{8,12},{12,8},{16,20},{20,16},{24,28},{28,24},{1,5},{5... | collective-permute-start | bytes 1572872 | tf_op jit(solution)/shard_map/ppermute | solution.py:22
  139.3 4.7 %collective-permute-start.30 = (bf16[2,128,512]{2,1,0:T(8,128)(2,1)S(1)}, bf16[2,128,512]{2,1,0:T(8,128)(2,1)S(1)}, u32[]{:S(2)}, u32[]{:S(2)}) collective-permute-start(bf16[2,128,512]{2,1,0:T(8,128)(2,1)S(1)} %add_convert_fusion.8), channel_id=1, source_target_pairs={{8,16},{12,20},{16,8},{20,12},{9,17},{13,21},{17,9},{21,13},{10,18... | collective-permute-start | bytes 786440 | tf_op jit(solution)/shard_map/ppermute | solution.py:189
  140.6 8.8 %collective-permute-start.27 = (bf16[2,128,512]{2,1,0:T(8,128)(2,1)S(1)}, bf16[2,128,512]{2,1,0:T(8,128)(2,1)S(1)}, u32[]{:S(2)}, u32[]{:S(2)}) collective-permute-start(bf16[2,128,512]{2,1,0:T(8,128)(2,1)S(1)} %add_convert_fusion.9), channel_id=1, source_target_pairs={{0,8},{8,0},{4,12},{12,4},{16,24},{24,16},{20,28},{28,20},{1,9},{9... | collective-permute-start | bytes 786440 | tf_op jit(solution)/shard_map/ppermute | solution.py:22
  144.4 9.3 %collective-permute-start.31 = (bf16[2,128,512]{2,1,0:T(8,128)(2,1)S(1)}, bf16[2,128,512]{2,1,0:T(8,128)(2,1)S(1)}, u32[]{:S(2)}, u32[]{:S(2)}) collective-permute-start(bf16[2,128,512]{2,1,0:T(8,128)(2,1)S(1)} %add_convert_fusion.7), channel_id=1, source_target_pairs={{0,8},{8,0},{4,12},{12,4},{16,24},{24,16},{20,28},{28,20},{1,9},{9... | collective-permute-start | bytes 786440 | tf_op jit(solution)/shard_map/ppermute | solution.py:22
  150.4 11.5 %collective-permute-start.28 = (bf16[2,256,512]{2,1,0:T(8,128)(2,1)S(1)}, bf16[2,256,512]{2,1,0:T(8,128)(2,1)S(1)}, u32[]{:S(2)}, u32[]{:S(2)}) collective-permute-start(bf16[2,256,512]{2,1,0:T(8,128)(2,1)S(1)} %add_convert_fusion.2), channel_id=1, source_target_pairs={{0,4},{4,0},{8,12},{12,8},{16,20},{20,16},{24,28},{28,24},{1,5},{5... | collective-permute-start | bytes 1572872 | tf_op jit(solution)/shard_map/ppermute | solution.py:22
  154.3 6.7 %collective-permute-start.32 = (bf16[2,64,512]{2,1,0:T(8,128)(2,1)S(1)}, bf16[2,64,512]{2,1,0:T(8,128)(2,1)S(1)}, u32[]{:S(2)}, u32[]{:S(2)}) collective-permute-start(bf16[2,64,512]{2,1,0:T(8,128)(2,1)S(1)} %fusion.16), channel_id=1, source_target_pairs={{0,4},{4,0},{8,12},{12,8},{16,20},{20,16},{24,28},{28,24},{1,5},{5... | collective-permute-start | bytes 393224 | tf_op jit(solution)/shard_map/ppermute | solution.py:22
  (40 other events, 142.0 us)

commit v22 on v21

--- a/solution.py
+++ b/solution.py
@@ -164,6 +164,8 @@
             if step_level + 1 < levels:
                 summary = apply(mine[step_level], summary) + apply(other[step_level], partner)
         held = own
+        if chunk >= 1:
+            held = after(held, late[chunk - 1][2])
         if chunk >= 2:
             held = after(held, late[chunk - 2][1])
         if chunk >= 3:
@@ -199,7 +201,7 @@
                 to_sibling = to_sibling + apply(other[0].T, grad)
             own_total = own_total + apply(mine[0].T, grad)
         sibling_send = to_sibling.astype(jnp.bfloat16)
-        late.append((sibling_send, sends.get(1, sibling_send)))
+        late.append((sibling_send, sends.get(1, sibling_send), sends.get(levels - 1, sibling_send)))
         from_sibling = partner_2(sibling_send, "seq", 0)
         if split:
             pooled_back = partner_2(apply(pick_other, grad).astype(jnp.bfloat16), "seq", 0)

time: 166 us -> 166 us (level)
  waiting for transfers between devices: 32.7 us -> 39.7 us
  starting transfers between devices: 58.2 us -> 51.3 us
    ppermute x18, starting transfers between devices: 35 us -> 25.6 us  [partner_2(): return lax.ppermute(block, axis, route)]
    ppermute x18, waiting for transfers between devices: 23.5 us -> 32.3 us  [partner_2(): return lax.ppermute(block, axis, route)]
    ppermute x4, starting transfers between devices: 12.4 us -> 14.6 us  [body(): gathered = lax.ppermute(sends[step_level], 'seq', back)]
    another operation x4, other arithmetic: 1.38 us -> 3.56 us
    another operation x4 -> x3, other arithmetic: 4.47 us -> 2.79 us  [body(): own = jnp.stack((key_rows[:, columns], value_rows[:, columns]))]
    unnamed x76 -> x74, local copies, waits for them, and re-layouts: 5.2 us -> 5.53 us
  transfers between devices with their start and end apart: 34 -> 34, of which waited for: 8 -> 10; matrix products, arithmetic and copies ran while one was open for 20% -> 21% of each run, Pallas kernels for 17% -> 17%
where the time goes in v22:
time: 166 us; the launch traced here: 165 us
  starting transfers between devices  51.3 us (31%)
  waiting for transfers between devices  39.7 us (24%)
  Pallas kernels  28.5 us (17%)
  other arithmetic  19.7 us (12%)
  matrix products  16.5 us (10%)
  local copies, waits for them, and re-layouts  7.59 us (5%)
    ppermute x18, waiting for transfers between devices, partner_2(): return lax.ppermute(block, axis, route)  32.3 us
    pallas_call x4, Pallas kernels, attention(): pl.pallas_call(functools.partial(attention_kernel, scale=score_scale, par...  28.5 us
    ppermute x18, starting transfers between devices, partner_2(): return lax.ppermute(block, axis, route)  25.6 us
    dot_general x33, matrix products, apply(): jnp.einsum('pr,krw->kpw', matrix, rows.astype(jnp.float32), precision=lax...  14.6 us
    ppermute x4, starting transfers between devices, body(): gathered = lax.ppermute(sends[step_level], 'seq', back)  14.6 us
    ppermute x4, waiting for transfers between devices, body(): passed = lax.ppermute(crossed, 'seq', outer_pairs(seq_count, step_level))  5.84 us
    unnamed x74, local copies, waits for them, and re-layouts  5.53 us
    ppermute x4, starting transfers between devices, body(): passed = lax.ppermute(crossed, 'seq', outer_pairs(seq_count, step_level))  5.15 us
  transfers between devices with their start and end apart: 34, of which 10 were waited for; matrix products, arithmetic and copies ran while one was open for 21% of the time, Pallas kernels for 17%

profile of v22, /device:TPU:0, one launch (start us, length us, event | category | flops | bytes accessed | tf_op | source)
XLA Modules:
  0.0 164.9 jit_solution(18214088864701340248)
XLA Ops:
  0.7 1.6 convolution_bitcast_fusion
  3.5 3.0 %collective-permute-start = (bf16[2,64,2048]{2,1,0:T(8,128)(2,1)}, bf16[2,64,2048]{2,1,0:T(8,128)(2,1)}, u32[]{:S(2)}, u32[]{:S(2)}) collective-permute-start(bf16[2,64,2048]{2,1,0:T(8,128)(2,1)} %fusion.17), channel_id=1, source_target_pairs={{0,4},{4,0},{8,12},{12,8},{16,20},{20,16},{24,28},{28,24},{1,5},{5... | collective-permute-start | bytes 1572872 | tf_op jit(solution)/shard_map/ppermute | solution.py:22
  12.5 6.2 %collective-permute-done = bf16[2,64,2048]{2,1,0:T(8,128)(2,1)} collective-permute-done((bf16[2,64,2048]{2,1,0:T(8,128)(2,1)}, bf16[2,64,2048]{2,1,0:T(8,128)(2,1)}, u32[]{:S(2)}, u32[]{:S(2)}) %collective-permute-start) | collective-permute-done | bytes 524320 | tf_op jit(solution)/shard_map/ppermute | solution.py:22
  19.9 1.9 %collective-permute-start.2 = (bf16[2,128,512]{2,1,0:T(8,128)(2,1)S(1)}, bf16[2,128,512]{2,1,0:T(8,128)(2,1)S(1)}, u32[]{:S(2)}, u32[]{:S(2)}) collective-permute-start(bf16[2,128,512]{2,1,0:T(8,128)(2,1)S(1)} %fusion.3), channel_id=1, source_target_pairs={{0,8},{8,0},{4,12},{12,4},{16,24},{24,16},{20,28},{28,20},{1,9},{9... | collective-permute-start | bytes 786440 | tf_op jit(solution)/shard_map/ppermute | solution.py:22
  24.9 1.9 %collective-permute-start.6 = (bf16[2,128,512]{2,1,0:T(8,128)(2,1)S(1)}, bf16[2,128,512]{2,1,0:T(8,128)(2,1)S(1)}, u32[]{:S(2)}, u32[]{:S(2)}) collective-permute-start(bf16[2,128,512]{2,1,0:T(8,128)(2,1)S(1)} %fusion.2), channel_id=1, source_target_pairs={{0,8},{8,0},{4,12},{12,4},{16,24},{24,16},{20,28},{28,20},{1,9},{9... | collective-permute-start | bytes 786440 | tf_op jit(solution)/shard_map/ppermute | solution.py:22
  30.8 1.8 %collective-permute-start.5 = (bf16[2,256,512]{2,1,0:T(8,128)(2,1)}, bf16[2,256,512]{2,1,0:T(8,128)(2,1)}, u32[]{:S(2)}, u32[]{:S(2)}) collective-permute-start(bf16[2,256,512]{2,1,0:T(8,128)(2,1)} %get-tuple-element.42.refs_0_), channel_id=1, source_target_pairs={{0,4},{4,0},{8,12},{12,8},{16,20},{20,16},{24,28},{28,24},{1,5},{5... | collective-permute-start | bytes 1572872 | tf_op jit(solution)/shard_map/ppermute | solution.py:22
  32.6 7.8 %collective-permute-done.6.refs_2_ = bf16[2,128,512]{2,1,0:T(8,128)(2,1)S(1)} collective-permute-done((bf16[2,128,512]{2,1,0:T(8,128)(2,1)S(1)}, bf16[2,128,512]{2,1,0:T(8,128)(2,1)S(1)}, u32[]{:S(2)}, u32[]{:S(2)}) %collective-permute-start.6) | collective-permute-done | bytes 262176 | tf_op jit(solution)/shard_map/ppermute | solution.py:22
  40.4 1.7 %collective-permute-start.1 = (bf16[2,256,512]{2,1,0:T(8,128)(2,1)S(1)}, bf16[2,256,512]{2,1,0:T(8,128)(2,1)S(1)}, u32[]{:S(2)}, u32[]{:S(2)}) collective-permute-start(bf16[2,256,512]{2,1,0:T(8,128)(2,1)S(1)} %copy-done.18), channel_id=1, source_target_pairs={{0,4},{4,0},{8,12},{12,8},{16,20},{20,16},{24,28},{28,24},{1,5},{5... | collective-permute-start | bytes 1572872 | tf_op jit(solution)/shard_map/ppermute | solution.py:22
  42.4 1.8 %collective-permute-done.12.refs_2_ = bf16[2,128,512]{2,1,0:T(8,128)(2,1)S(1)} collective-permute-done((bf16[2,128,512]{2,1,0:T(8,128)(2,1)S(1)}, bf16[2,128,512]{2,1,0:T(8,128)(2,1)S(1)}, u32[]{:S(2)}, u32[]{:S(2)}) %collective-permute-start.12) | collective-permute-done | bytes 262176 | tf_op jit(solution)/shard_map/ppermute | solution.py:22
  44.9 1.3 collective-permute-start.4
  49.0 5.8 %collective-permute-done.4 = bf16[2,128,512]{2,1,0:T(8,128)(2,1)S(1)} collective-permute-done((bf16[2,128,512]{2,1,0:T(8,128)(2,1)S(1)}, bf16[2,128,512]{2,1,0:T(8,128)(2,1)S(1)}, u32[]{:S(2)}, u32[]{:S(2)}) %collective-permute-start.4) | collective-permute-done | bytes 262176 | tf_op jit(solution)/shard_map/ppermute | solution.py:161
  57.7 1.5 collective-permute-start.11
  59.2 7.1 %shard_map.75 = (bf16[256,512]{1,0:T(8,128)(2,1)}, bf16[256,512]{1,0:T(8,128)(2,1)}, f32[2,256,512]{2,1,0:T(8,128)}, f32[2,256,512]{2,1,0:T(8,128)}, f32[2,128,512]{2,1,0:T(8,128)}, /*index=5*/f32[2,128,512]{2,1,0:T(8,128)}) custom-call(f32[1,768]{1,0:T(1,128)} %constant.104.clone.1.bias_ref, bf16[256,2048]{1,0:T(8,128)(2,1)} %q_ref.7, ...), custom_call_target="tpu_custom_call" | custom-call | flops 1207959552 | bytes 5767168 | tf_op jit(solution)/shard_map/pallas_call | solution.py:72
  71.4 4.9 %collective-permute-start.9 = (bf16[2,128,512]{2,1,0:T(8,128)(2,1)S(1)}, bf16[2,128,512]{2,1,0:T(8,128)(2,1)S(1)}, u32[]{:S(2)}, u32[]{:S(2)}) collective-permute-start(bf16[2,128,512]{2,1,0:T(8,128)(2,1)S(1)} %convert_element_type.185), channel_id=1, source_target_pairs={{0,8},{4,12},{24,16},{28,20},{1,9},{5,13},{25,17},{29,21},{2,10},{... | collective-permute-start | bytes 786440 | tf_op jit(solution)/shard_map/ppermute | solution.py:189
  76.3 7.1 %shard_map.76 = (bf16[256,512]{1,0:T(8,128)(2,1)}, bf16[256,512]{1,0:T(8,128)(2,1)}, f32[2,256,512]{2,1,0:T(8,128)}, f32[2,256,512]{2,1,0:T(8,128)}, f32[2,128,512]{2,1,0:T(8,128)}, /*index=5*/f32[2,128,512]{2,1,0:T(8,128)}) custom-call(f32[1,768]{1,0:T(1,128)} %constant.104.clone.1.bias_ref, bf16[256,2048]{1,0:T(8,128)(2,1)} %q_ref.7, ...), custom_call_target="tpu_custom_call" | custom-call | flops 1207959552 | bytes 5767168 | tf_op jit(solution)/shard_map/pallas_call | solution.py:72
  84.6 1.3 collective-permute-start.15
  88.3 1.4 collective-permute-done.15
  91.0 6.2 %collective-permute-start.17 = (bf16[2,128,512]{2,1,0:T(8,128)(2,1)S(1)}, bf16[2,128,512]{2,1,0:T(8,128)(2,1)S(1)}, u32[]{:S(2)}, u32[]{:S(2)}) collective-permute-start(bf16[2,128,512]{2,1,0:T(8,128)(2,1)S(1)} %add_convert_fusion.13), channel_id=1, source_target_pairs={{0,8},{8,0},{4,12},{12,4},{16,24},{24,16},{20,28},{28,20},{1,9},{9... | collective-permute-start | bytes 786440 | tf_op jit(solution)/shard_map/ppermute | solution.py:22
  97.2 7.1 %shard_map.77 = (bf16[256,512]{1,0:T(8,128)(2,1)}, bf16[256,512]{1,0:T(8,128)(2,1)}, f32[2,256,512]{2,1,0:T(8,128)}, f32[2,256,512]{2,1,0:T(8,128)}, f32[2,128,512]{2,1,0:T(8,128)}, /*index=5*/f32[2,128,512]{2,1,0:T(8,128)}) custom-call(f32[1,768]{1,0:T(1,128)} %constant.104.clone.1.bias_ref, bf16[256,2048]{1,0:T(8,128)(2,1)} %q_ref.7, ...), custom_call_target="tpu_custom_call" | custom-call | flops 1207959552 | bytes 5767168 | tf_op jit(solution)/shard_map/pallas_call | solution.py:72
  105.5 2.0 %collective-permute-start.25 = (bf16[2,128,512]{2,1,0:T(8,128)(2,1)S(1)}, bf16[2,128,512]{2,1,0:T(8,128)(2,1)S(1)}, u32[]{:S(2)}, u32[]{:S(2)}) collective-permute-start(bf16[2,128,512]{2,1,0:T(8,128)(2,1)S(1)} %convert_element_type.196), channel_id=1, source_target_pairs={{0,8},{4,12},{24,16},{28,20},{1,9},{5,13},{25,17},{29,21},{2,10},{... | collective-permute-start | bytes 786440 | tf_op jit(solution)/shard_map/ppermute | solution.py:189
  109.4 1.6 collective-permute-start.22
  111.0 3.4 %collective-permute-done.23 = bf16[2,128,512]{2,1,0:T(8,128)(2,1)S(1)} collective-permute-done((bf16[2,128,512]{2,1,0:T(8,128)(2,1)S(1)}, bf16[2,128,512]{2,1,0:T(8,128)(2,1)S(1)}, u32[]{:S(2)}, u32[]{:S(2)}) %collective-permute-start.23) | collective-permute-done | bytes 262176 | tf_op jit(solution)/shard_map/ppermute | solution.py:22
  115.4 1.6 collective-permute-start.24
  118.3 7.2 %shard_map.78 = (bf16[256,512]{1,0:T(8,128)(2,1)}, bf16[256,512]{1,0:T(8,128)(2,1)}, f32[2,256,512]{2,1,0:T(8,128)}, f32[2,256,512]{2,1,0:T(8,128)}, f32[2,128,512]{2,1,0:T(8,128)}, /*index=5*/f32[2,128,512]{2,1,0:T(8,128)}) custom-call(f32[1,768]{1,0:T(1,128)} %constant.104.clone.1.bias_ref, bf16[256,2048]{1,0:T(8,128)(2,1)} %q_ref.7, ...), custom_call_target="tpu_custom_call" | custom-call | flops 1207959552 | bytes 5767168 | tf_op jit(solution)/shard_map/pallas_call | solution.py:72
  126.7 6.4 %collective-permute-start.29 = (bf16[2,128,512]{2,1,0:T(8,128)(2,1)S(1)}, bf16[2,128,512]{2,1,0:T(8,128)(2,1)S(1)}, u32[]{:S(2)}, u32[]{:S(2)}) collective-permute-start(bf16[2,128,512]{2,1,0:T(8,128)(2,1)S(1)} %convert_element_type.218), channel_id=1, source_target_pairs={{0,8},{4,12},{24,16},{28,20},{1,9},{5,13},{25,17},{29,21},{2,10},{... | collective-permute-start | bytes 786440 | tf_op jit(solution)/shard_map/ppermute | solution.py:189
  133.1 1.3 convert_element_type.225
  139.9 6.4 %collective-permute-done.27 = bf16[2,128,512]{2,1,0:T(8,128)(2,1)S(1)} collective-permute-done((bf16[2,128,512]{2,1,0:T(8,128)(2,1)S(1)}, bf16[2,128,512]{2,1,0:T(8,128)(2,1)S(1)}, u32[]{:S(2)}, u32[]{:S(2)}) %collective-permute-start.27) | collective-permute-done | bytes 262176 | tf_op jit(solution)/shard_map/ppermute | solution.py:22
  147.3 1.7 %collective-permute-start.28 = (bf16[2,256,512]{2,1,0:T(8,128)(2,1)S(1)}, bf16[2,256,512]{2,1,0:T(8,128)(2,1)S(1)}, u32[]{:S(2)}, u32[]{:S(2)}) collective-permute-start(bf16[2,256,512]{2,1,0:T(8,128)(2,1)S(1)} %add_convert_fusion.2), channel_id=1, source_target_pairs={{0,4},{4,0},{8,12},{12,8},{16,20},{20,16},{24,28},{28,24},{1,5},{5... | collective-permute-start | bytes 1572872 | tf_op jit(solution)/shard_map/ppermute | solution.py:22
  150.6 1.4 add_convert_fusion.5
  152.1 1.4 add_convert_fusion.3
  153.8 2.1 %collective-permute-done.31 = bf16[2,128,512]{2,1,0:T(8,128)(2,1)S(1)} collective-permute-done((bf16[2,128,512]{2,1,0:T(8,128)(2,1)S(1)}, bf16[2,128,512]{2,1,0:T(8,128)(2,1)S(1)}, u32[]{:S(2)}, u32[]{:S(2)}) %collective-permute-start.31) | collective-permute-done | bytes 262176 | tf_op jit(solution)/shard_map/ppermute | solution.py:22
  157.6 4.0 %collective-permute-done.32 = bf16[2,64,512]{2,1,0:T(8,128)(2,1)S(1)} collective-permute-done((bf16[2,64,512]{2,1,0:T(8,128)(2,1)S(1)}, bf16[2,64,512]{2,1,0:T(8,128)(2,1)S(1)}, u32[]{:S(2)}, u32[]{:S(2)}) %collective-permute-start.32) | collective-permute-done | bytes 131104 | tf_op jit(solution)/shard_map/ppermute | solution.py:22
  (198 shorter events, 51.4 us)
Async XLA Ops:
  3.5 15.2 %collective-permute-start = (bf16[2,64,2048]{2,1,0:T(8,128)(2,1)}, bf16[2,64,2048]{2,1,0:T(8,128)(2,1)}, u32[]{:S(2)}, u32[]{:S(2)}) collective-permute-start(bf16[2,64,2048]{2,1,0:T(8,128)(2,1)} %fusion.17), channel_id=1, source_target_pairs={{0,4},{4,0},{8,12},{12,8},{16,20},{20,16},{24,28},{28,24},{1,5},{5... | collective-permute-start | bytes 1572872 | tf_op jit(solution)/shard_map/ppermute | solution.py:22
  19.9 9.3 %collective-permute-start.2 = (bf16[2,128,512]{2,1,0:T(8,128)(2,1)S(1)}, bf16[2,128,512]{2,1,0:T(8,128)(2,1)S(1)}, u32[]{:S(2)}, u32[]{:S(2)}) collective-permute-start(bf16[2,128,512]{2,1,0:T(8,128)(2,1)S(1)} %fusion.3), channel_id=1, source_target_pairs={{0,8},{8,0},{4,12},{12,4},{16,24},{24,16},{20,28},{28,20},{1,9},{9... | collective-permute-start | bytes 786440 | tf_op jit(solution)/shard_map/ppermute | solution.py:22
  22.9 24.3 %collective-permute-start.19 = (bf16[2,128,512]{2,1,0:T(8,128)(2,1)S(1)}, bf16[2,128,512]{2,1,0:T(8,128)(2,1)S(1)}, u32[]{:S(2)}, u32[]{:S(2)}) collective-permute-start(bf16[2,128,512]{2,1,0:T(8,128)(2,1)S(1)} %fusion), channel_id=1, source_target_pairs={{0,8},{8,0},{4,12},{12,4},{16,24},{24,16},{20,28},{28,20},{1,9},{9... | collective-permute-start | bytes 786440 | tf_op jit(solution)/shard_map/ppermute | solution.py:22
  24.9 15.5 %collective-permute-start.6 = (bf16[2,128,512]{2,1,0:T(8,128)(2,1)S(1)}, bf16[2,128,512]{2,1,0:T(8,128)(2,1)S(1)}, u32[]{:S(2)}, u32[]{:S(2)}) collective-permute-start(bf16[2,128,512]{2,1,0:T(8,128)(2,1)S(1)} %fusion.2), channel_id=1, source_target_pairs={{0,8},{8,0},{4,12},{12,4},{16,24},{24,16},{20,28},{28,20},{1,9},{9... | collective-permute-start | bytes 786440 | tf_op jit(solution)/shard_map/ppermute | solution.py:22
  27.9 16.3 %collective-permute-start.12 = (bf16[2,128,512]{2,1,0:T(8,128)(2,1)S(1)}, bf16[2,128,512]{2,1,0:T(8,128)(2,1)S(1)}, u32[]{:S(2)}, u32[]{:S(2)}) collective-permute-start(bf16[2,128,512]{2,1,0:T(8,128)(2,1)S(1)} %fusion.1), channel_id=1, source_target_pairs={{0,8},{8,0},{4,12},{12,4},{16,24},{24,16},{20,28},{28,20},{1,9},{9... | collective-permute-start | bytes 786440 | tf_op jit(solution)/shard_map/ppermute | solution.py:22
  29.9 15.1 %collective-permute-start.3 = (bf16[2,128,512]{2,1,0:T(8,128)(2,1)S(1)}, bf16[2,128,512]{2,1,0:T(8,128)(2,1)S(1)}, u32[]{:S(2)}, u32[]{:S(2)}) collective-permute-start(bf16[2,128,512]{2,1,0:T(8,128)(2,1)S(1)} %fusion.15), channel_id=1, source_target_pairs={{8,16},{12,20},{16,8},{20,12},{9,17},{13,21},{17,9},{21,13},{10,18... | collective-permute-start | bytes 786440 | tf_op jit(solution)/shard_map/ppermute | solution.py:160
  30.8 40.6 %collective-permute-start.5 = (bf16[2,256,512]{2,1,0:T(8,128)(2,1)}, bf16[2,256,512]{2,1,0:T(8,128)(2,1)}, u32[]{:S(2)}, u32[]{:S(2)}) collective-permute-start(bf16[2,256,512]{2,1,0:T(8,128)(2,1)} %get-tuple-element.42.refs_0_), channel_id=1, source_target_pairs={{0,4},{4,0},{8,12},{12,8},{16,20},{20,16},{24,28},{28,24},{1,5},{5... | collective-permute-start | bytes 1572872 | tf_op jit(solution)/shard_map/ppermute | solution.py:22
  40.4 16.5 %collective-permute-start.1 = (bf16[2,256,512]{2,1,0:T(8,128)(2,1)S(1)}, bf16[2,256,512]{2,1,0:T(8,128)(2,1)S(1)}, u32[]{:S(2)}, u32[]{:S(2)}) collective-permute-start(bf16[2,256,512]{2,1,0:T(8,128)(2,1)S(1)} %copy-done.18), channel_id=1, source_target_pairs={{0,4},{4,0},{8,12},{12,8},{16,20},{20,16},{24,28},{28,24},{1,5},{5... | collective-permute-start | bytes 1572872 | tf_op jit(solution)/shard_map/ppermute | solution.py:22
  44.9 9.9 %collective-permute-start.4 = (bf16[2,128,512]{2,1,0:T(8,128)(2,1)S(1)}, bf16[2,128,512]{2,1,0:T(8,128)(2,1)S(1)}, u32[]{:S(2)}, u32[]{:S(2)}) collective-permute-start(bf16[2,128,512]{2,1,0:T(8,128)(2,1)S(1)} %collective-permute-done.3), channel_id=1, source_target_pairs={{8,0},{12,4},{16,24},{20,28},{9,1},{13,5},{17,25},{21,29},{10,2},{... | collective-permute-start | bytes 786440 | tf_op jit(solution)/shard_map/ppermute | solution.py:161
  47.2 20.2 %collective-permute-start.13 = (bf16[2,128,512]{2,1,0:T(8,128)(2,1)}, bf16[2,128,512]{2,1,0:T(8,128)(2,1)S(1)}, u32[]{:S(2)}, u32[]{:S(2)}) collective-permute-start(bf16[2,128,512]{2,1,0:T(8,128)(2,1)} %fusion.13), channel_id=1, source_target_pairs={{8,16},{12,20},{16,8},{20,12},{9,17},{13,21},{17,9},{21,13},{10,18... | collective-permute-start | bytes 786440 | tf_op jit(solution)/shard_map/ppermute | solution.py:160
  48.4 19.7 %collective-permute-start.20 = (bf16[2,128,512]{2,1,0:T(8,128)(2,1)S(1)}, bf16[2,128,512]{2,1,0:T(8,128)(2,1)S(1)}, u32[]{:S(2)}, u32[]{:S(2)}) collective-permute-start(bf16[2,128,512]{2,1,0:T(8,128)(2,1)S(1)} %fusion.12), channel_id=1, source_target_pairs={{8,16},{12,20},{16,8},{20,12},{9,17},{13,21},{17,9},{21,13},{10,18... | collective-permute-start | bytes 786440 | tf_op jit(solution)/shard_map/ppermute | solution.py:160
  54.9 14.5 %collective-permute-start.8 = (bf16[2,128,512]{2,1,0:T(8,128)(2,1)S(1)}, bf16[2,128,512]{2,1,0:T(8,128)(2,1)S(1)}, u32[]{:S(2)}, u32[]{:S(2)}) collective-permute-start(bf16[2,128,512]{2,1,0:T(8,128)(2,1)S(1)} %collective-permute-done.7), channel_id=1, source_target_pairs={{8,0},{12,4},{16,24},{20,28},{9,1},{13,5},{17,25},{21,29},{10,2},{... | collective-permute-start | bytes 786440 | tf_op jit(solution)/shard_map/ppermute | solution.py:161
  57.7 39.5 %collective-permute-start.11 = (bf16[2,256,512]{2,1,0:T(8,128)(2,1)S(1)}, bf16[2,256,512]{2,1,0:T(8,128)(2,1)}, u32[]{:S(2)}, u32[]{:S(2)}) collective-permute-start(bf16[2,256,512]{2,1,0:T(8,128)(2,1)S(1)} %copy-done.23), channel_id=1, source_target_pairs={{0,4},{4,0},{8,12},{12,8},{16,20},{20,16},{24,28},{28,24},{1,5},{5... | collective-permute-start | bytes 1572872 | tf_op jit(solution)/shard_map/ppermute | solution.py:22
  67.5 50.9 %collective-permute-start.18 = (bf16[2,256,512]{2,1,0:T(8,128)(2,1)S(1)}, bf16[2,256,512]{2,1,0:T(8,128)(2,1)}, u32[]{:S(2)}, u32[]{:S(2)}) collective-permute-start(bf16[2,256,512]{2,1,0:T(8,128)(2,1)S(1)} %copy-done.17), channel_id=1, source_target_pairs={{0,4},{4,0},{8,12},{12,8},{16,20},{20,16},{24,28},{28,24},{1,5},{5... | collective-permute-start | bytes 1572872 | tf_op jit(solution)/shard_map/ppermute | solution.py:22
  68.0 16.6 %collective-permute-start.14 = (bf16[2,128,512]{2,1,0:T(8,128)(2,1)S(1)}, bf16[2,128,512]{2,1,0:T(8,128)(2,1)S(1)}, u32[]{:S(2)}, u32[]{:S(2)}) collective-permute-start(bf16[2,128,512]{2,1,0:T(8,128)(2,1)S(1)} %collective-permute-done.13), channel_id=1, source_target_pairs={{8,0},{12,4},{16,24},{20,28},{9,1},{13,5},{17,25},{21,29},{10,2},{... | collective-permute-start | bytes 786440 | tf_op jit(solution)/shard_map/ppermute | solution.py:161
  69.3 18.2 %collective-permute-start.21 = (bf16[2,128,512]{2,1,0:T(8,128)(2,1)S(1)}, bf16[2,128,512]{2,1,0:T(8,128)(2,1)S(1)}, u32[]{:S(2)}, u32[]{:S(2)}) collective-permute-start(bf16[2,128,512]{2,1,0:T(8,128)(2,1)S(1)} %collective-permute-done.20), channel_id=1, source_target_pairs={{8,0},{12,4},{16,24},{20,28},{9,1},{13,5},{17,25},{21,29},{10,2},{... | collective-permute-start | bytes 786440 | tf_op jit(solution)/shard_map/ppermute | solution.py:161
  71.4 15.3 %collective-permute-start.9 = (bf16[2,128,512]{2,1,0:T(8,128)(2,1)S(1)}, bf16[2,128,512]{2,1,0:T(8,128)(2,1)S(1)}, u32[]{:S(2)}, u32[]{:S(2)}) collective-permute-start(bf16[2,128,512]{2,1,0:T(8,128)(2,1)S(1)} %convert_element_type.185), channel_id=1, source_target_pairs={{0,8},{4,12},{24,16},{28,20},{1,9},{5,13},{25,17},{29,21},{2,10},{... | collective-permute-start | bytes 786440 | tf_op jit(solution)/shard_map/ppermute | solution.py:189
  84.6 5.2 %collective-permute-start.15 = (bf16[2,128,512]{2,1,0:T(8,128)(2,1)S(1)}, bf16[2,128,512]{2,1,0:T(8,128)(2,1)S(1)}, u32[]{:S(2)}, u32[]{:S(2)}) collective-permute-start(bf16[2,128,512]{2,1,0:T(8,128)(2,1)S(1)} %convert_element_type.189), channel_id=1, source_target_pairs={{0,8},{4,12},{24,16},{28,20},{1,9},{5,13},{25,17},{29,21},{2,10},{... | collective-permute-start | bytes 786440 | tf_op jit(solution)/shard_map/ppermute | solution.py:189
  89.8 17.6 %collective-permute-start.16 = (bf16[2,128,512]{2,1,0:T(8,128)(2,1)S(1)}, bf16[2,128,512]{2,1,0:T(8,128)(2,1)S(1)}, u32[]{:S(2)}, u32[]{:S(2)}) collective-permute-start(bf16[2,128,512]{2,1,0:T(8,128)(2,1)S(1)} %add_convert_fusion.12), channel_id=1, source_target_pairs={{8,16},{12,20},{16,8},{20,12},{9,17},{13,21},{17,9},{21,13},{10,18... | collective-permute-start | bytes 786440 | tf_op jit(solution)/shard_map/ppermute | solution.py:191
  91.0 17.0 %collective-permute-start.17 = (bf16[2,128,512]{2,1,0:T(8,128)(2,1)S(1)}, bf16[2,128,512]{2,1,0:T(8,128)(2,1)S(1)}, u32[]{:S(2)}, u32[]{:S(2)}) collective-permute-start(bf16[2,128,512]{2,1,0:T(8,128)(2,1)S(1)} %add_convert_fusion.13), channel_id=1, source_target_pairs={{0,8},{8,0},{4,12},{12,4},{16,24},{24,16},{20,28},{28,20},{1,9},{9... | collective-permute-start | bytes 786440 | tf_op jit(solution)/shard_map/ppermute | solution.py:22
  105.5 11.5 %collective-permute-start.25 = (bf16[2,128,512]{2,1,0:T(8,128)(2,1)S(1)}, bf16[2,128,512]{2,1,0:T(8,128)(2,1)S(1)}, u32[]{:S(2)}, u32[]{:S(2)}) collective-permute-start(bf16[2,128,512]{2,1,0:T(8,128)(2,1)S(1)} %convert_element_type.196), channel_id=1, source_target_pairs={{0,8},{4,12},{24,16},{28,20},{1,9},{5,13},{25,17},{29,21},{2,10},{... | collective-permute-start | bytes 786440 | tf_op jit(solution)/shard_map/ppermute | solution.py:189
  107.9 6.4 %collective-permute-start.23 = (bf16[2,128,512]{2,1,0:T(8,128)(2,1)S(1)}, bf16[2,128,512]{2,1,0:T(8,128)(2,1)S(1)}, u32[]{:S(2)}, u32[]{:S(2)}) collective-permute-start(bf16[2,128,512]{2,1,0:T(8,128)(2,1)S(1)} %add_convert_fusion.11), channel_id=1, source_target_pairs={{0,8},{8,0},{4,12},{12,4},{16,24},{24,16},{20,28},{28,20},{1,9},{9... | collective-permute-start | bytes 786440 | tf_op jit(solution)/shard_map/ppermute | solution.py:22
  109.4 40.6 %collective-permute-start.22 = (bf16[2,256,512]{2,1,0:T(8,128)(2,1)S(1)}, bf16[2,256,512]{2,1,0:T(8,128)(2,1)}, u32[]{:S(2)}, u32[]{:S(2)}) collective-permute-start(bf16[2,256,512]{2,1,0:T(8,128)(2,1)S(1)} %add_convert_fusion.6), channel_id=1, source_target_pairs={{0,4},{4,0},{8,12},{12,8},{16,20},{20,16},{24,28},{28,24},{1,5},{5... | collective-permute-start | bytes 1572872 | tf_op jit(solution)/shard_map/ppermute | solution.py:22
  115.4 36.7 %collective-permute-start.24 = (bf16[2,256,512]{2,1,0:T(8,128)(2,1)S(1)}, bf16[2,256,512]{2,1,0:T(8,128)(2,1)}, u32[]{:S(2)}, u32[]{:S(2)}) collective-permute-start(bf16[2,256,512]{2,1,0:T(8,128)(2,1)S(1)} %add_convert_fusion.4), channel_id=1, source_target_pairs={{0,4},{4,0},{8,12},{12,8},{16,20},{20,16},{24,28},{28,24},{1,5},{5... | collective-permute-start | bytes 1572872 | tf_op jit(solution)/shard_map/ppermute | solution.py:22
  117.0 19.6 %collective-permute-start.26 = (bf16[2,128,512]{2,1,0:T(8,128)(2,1)S(1)}, bf16[2,128,512]{2,1,0:T(8,128)(2,1)S(1)}, u32[]{:S(2)}, u32[]{:S(2)}) collective-permute-start(bf16[2,128,512]{2,1,0:T(8,128)(2,1)S(1)} %add_convert_fusion.10), channel_id=1, source_target_pairs={{8,16},{12,20},{16,8},{20,12},{9,17},{13,21},{17,9},{21,13},{10,18... | collective-permute-start | bytes 786440 | tf_op jit(solution)/shard_map/ppermute | solution.py:191
  126.7 12.3 %collective-permute-start.29 = (bf16[2,128,512]{2,1,0:T(8,128)(2,1)S(1)}, bf16[2,128,512]{2,1,0:T(8,128)(2,1)S(1)}, u32[]{:S(2)}, u32[]{:S(2)}) collective-permute-start(bf16[2,128,512]{2,1,0:T(8,128)(2,1)S(1)} %convert_element_type.218), channel_id=1, source_target_pairs={{0,8},{4,12},{24,16},{28,20},{1,9},{5,13},{25,17},{29,21},{2,10},{... | collective-permute-start | bytes 786440 | tf_op jit(solution)/shard_map/ppermute | solution.py:189
  134.4 27.5 %collective-permute-start.33 = (bf16[2,256,512]{2,1,0:T(8,128)(2,1)S(1)}, bf16[2,256,512]{2,1,0:T(8,128)(2,1)S(1)}, u32[]{:S(2)}, u32[]{:S(2)}) collective-permute-start(bf16[2,256,512]{2,1,0:T(8,128)(2,1)S(1)} %convert_element_type.225), channel_id=1, source_target_pairs={{0,4},{4,0},{8,12},{12,8},{16,20},{20,16},{24,28},{28,24},{1,5},{5... | collective-permute-start | bytes 1572872 | tf_op jit(solution)/shard_map/ppermute | solution.py:22
  137.4 8.9 %collective-permute-start.27 = (bf16[2,128,512]{2,1,0:T(8,128)(2,1)S(1)}, bf16[2,128,512]{2,1,0:T(8,128)(2,1)S(1)}, u32[]{:S(2)}, u32[]{:S(2)}) collective-permute-start(bf16[2,128,512]{2,1,0:T(8,128)(2,1)S(1)} %add_convert_fusion.9), channel_id=1, source_target_pairs={{0,8},{8,0},{4,12},{12,4},{16,24},{24,16},{20,28},{28,20},{1,9},{9... | collective-permute-start | bytes 786440 | tf_op jit(solution)/shard_map/ppermute | solution.py:22
  139.1 10.0 %collective-permute-start.30 = (bf16[2,128,512]{2,1,0:T(8,128)(2,1)S(1)}, bf16[2,128,512]{2,1,0:T(8,128)(2,1)S(1)}, u32[]{:S(2)}, u32[]{:S(2)}) collective-permute-start(bf16[2,128,512]{2,1,0:T(8,128)(2,1)S(1)} %add_convert_fusion.8), channel_id=1, source_target_pairs={{8,16},{12,20},{16,8},{20,12},{9,17},{13,21},{17,9},{21,13},{10,18... | collective-permute-start | bytes 786440 | tf_op jit(solution)/shard_map/ppermute | solution.py:191
  147.3 15.0 %collective-permute-start.28 = (bf16[2,256,512]{2,1,0:T(8,128)(2,1)S(1)}, bf16[2,256,512]{2,1,0:T(8,128)(2,1)S(1)}, u32[]{:S(2)}, u32[]{:S(2)}) collective-permute-start(bf16[2,256,512]{2,1,0:T(8,128)(2,1)S(1)} %add_convert_fusion.2), channel_id=1, source_target_pairs={{0,4},{4,0},{8,12},{12,8},{16,20},{20,16},{24,28},{28,24},{1,5},{5... | collective-permute-start | bytes 1572872 | tf_op jit(solution)/shard_map/ppermute | solution.py:22
  149.5 6.4 %collective-permute-start.31 = (bf16[2,128,512]{2,1,0:T(8,128)(2,1)S(1)}, bf16[2,128,512]{2,1,0:T(8,128)(2,1)S(1)}, u32[]{:S(2)}, u32[]{:S(2)}) collective-permute-start(bf16[2,128,512]{2,1,0:T(8,128)(2,1)S(1)} %add_convert_fusion.7), channel_id=1, source_target_pairs={{0,8},{8,0},{4,12},{12,4},{16,24},{24,16},{20,28},{28,20},{1,9},{9... | collective-permute-start | bytes 786440 | tf_op jit(solution)/shard_map/ppermute | solution.py:22
  156.5 5.0 %collective-permute-start.32 = (bf16[2,64,512]{2,1,0:T(8,128)(2,1)S(1)}, bf16[2,64,512]{2,1,0:T(8,128)(2,1)S(1)}, u32[]{:S(2)}, u32[]{:S(2)}) collective-permute-start(bf16[2,64,512]{2,1,0:T(8,128)(2,1)S(1)} %fusion.16), channel_id=1, source_target_pairs={{0,4},{4,0},{8,12},{12,8},{16,20},{20,16},{24,28},{28,24},{1,5},{5... | collective-permute-start | bytes 393224 | tf_op jit(solution)/shard_map/ppermute | solution.py:22
  (39 other events, 166.6 us)

commit v23 on v21

--- a/solution.py
+++ b/solution.py
@@ -54,8 +54,8 @@
     first = 0
     for r in grad_refs:
         rows = r.shape[1]
-        r[0] = dk[first:first + rows]
-        r[1] = dv[first:first + rows]
+        r[0] = dk[first:first + rows].astype(r.dtype)
+        r[1] = dv[first:first + rows].astype(r.dtype)
         first += rows
 
 
@@ -77,7 +77,8 @@
         out_shape=[
             jax.ShapeDtypeStruct((leaf_rows, width), jnp.bfloat16),
             jax.ShapeDtypeStruct((leaf_rows, width), jnp.bfloat16),
-        ] + [jax.ShapeDtypeStruct(p.shape, jnp.float32) for p in parts],
+        ] + [jax.ShapeDtypeStruct(p.shape, jnp.float32) for p in parts[:-1]]
+        + [jax.ShapeDtypeStruct(parts[-1].shape, jnp.bfloat16)],
         cost_estimate=pl.CostEstimate(
             flops=flops, transcendentals=2 * leaf_rows * key_count * heads, bytes_accessed=io_bytes
         ),

time: 166 us -> 166 us (level)
  other arithmetic: 20.6 us -> 15.6 us
  starting transfers between devices: 58.2 us -> 61.7 us
  waiting for transfers between devices: 32.7 us -> 34.6 us
    convert_element_type x8 -> x4, other arithmetic: 5.44 us -> 0.37 us  [body(): sends[step_level] = outgoing.astype(jnp.bfloat16)]
    ppermute x18, starting transfers between devices: 35 us -> 37.1 us  [partner_2(): return lax.ppermute(block, axis, route)]
    ppermute x4, waiting for transfers between devices: 6.65 us -> 8.49 us  [body(): passed = lax.ppermute(crossed, 'seq', outer_pairs(seq_count, step_level))]
    unnamed x76 -> x80, local copies, waits for them, and re-layouts: 5.2 us -> 5.76 us
  transfers between devices with their start and end apart: 34 -> 34, of which waited for: 8 -> 8; matrix products, arithmetic and copies ran while one was open for 20% -> 17% of each run, Pallas kernels for 17% -> 17%
where the time goes in v23:
time: 166 us; the launch traced here: 165 us
  starting transfers between devices  61.7 us (37%)
  waiting for transfers between devices  34.6 us (21%)
  Pallas kernels  28.6 us (17%)
  matrix products  15.8 us (10%)
  other arithmetic  15.6 us (9%)
  local copies, waits for them, and re-layouts  7.26 us (4%)
  between operations  1.76 us (1%)
    ppermute x18, starting transfers between devices, partner_2(): return lax.ppermute(block, axis, route)  37.1 us
    pallas_call x4, Pallas kernels, attention(): pl.pallas_call(functools.partial(attention_kernel, scale=score_scale, par...  28.6 us
    ppermute x18, waiting for transfers between devices, partner_2(): return lax.ppermute(block, axis, route)  24.3 us
    dot_general x33, matrix products, apply(): jnp.einsum('pr,krw->kpw', matrix, rows.astype(jnp.float32), precision=lax...  13.9 us
    ppermute x4, starting transfers between devices, body(): gathered = lax.ppermute(sends[step_level], 'seq', back)  13.7 us
    ppermute x4, waiting for transfers between devices, body(): passed = lax.ppermute(crossed, 'seq', outer_pairs(seq_count, step_level))  8.49 us
    unnamed x80, local copies, waits for them, and re-layouts  5.76 us
    ppermute x4, starting transfers between devices, body(): passed = lax.ppermute(crossed, 'seq', outer_pairs(seq_count, step_level))  5.13 us
  transfers between devices with their start and end apart: 34, of which 8 were waited for; matrix products, arithmetic and copies ran while one was open for 17% of the time, Pallas kernels for 17%

profile of v23, /device:TPU:0, one launch (start us, length us, event | category | flops | bytes accessed | tf_op | source)
XLA Modules:
  0.0 165.3 jit_solution(3403174327175087681)
XLA Ops:
  0.7 1.6 convolution_bitcast_fusion
  3.5 3.0 %collective-permute-start = (bf16[2,64,2048]{2,1,0:T(8,128)(2,1)}, bf16[2,64,2048]{2,1,0:T(8,128)(2,1)}, u32[]{:S(2)}, u32[]{:S(2)}) collective-permute-start(bf16[2,64,2048]{2,1,0:T(8,128)(2,1)} %fusion.17), channel_id=1, source_target_pairs={{0,4},{4,0},{8,12},{12,8},{16,20},{20,16},{24,28},{28,24},{1,5},{5... | collective-permute-start | bytes 1572872 | tf_op jit(solution)/shard_map/ppermute | solution.py:22
  8.8 1.9 %pad_maximum_fusion.5.refs_0_ = bf16[2,256,512]{2,1,0:T(8,128)(2,1)} fusion(bf16[1,256,512]{2,1,0:T(8,128)(2,1)} %get-tuple-element.70, bf16[1,256,512]{2,1,0:T(8,128)(2,1)} %get-tuple-element.85), kind=kLoop, calls=%fused_computation.65 | loop fusion | flops 262144 | bytes 1048576 | tf_op jit(solution)/shard_map/stack | solution.py:151
  13.8 4.9 %collective-permute-done = bf16[2,64,2048]{2,1,0:T(8,128)(2,1)} collective-permute-done((bf16[2,64,2048]{2,1,0:T(8,128)(2,1)}, bf16[2,64,2048]{2,1,0:T(8,128)(2,1)}, u32[]{:S(2)}, u32[]{:S(2)}) %collective-permute-start) | collective-permute-done | bytes 524320 | tf_op jit(solution)/shard_map/ppermute | solution.py:22
  19.9 1.9 %collective-permute-start.2 = (bf16[2,128,512]{2,1,0:T(8,128)(2,1)S(1)}, bf16[2,128,512]{2,1,0:T(8,128)(2,1)S(1)}, u32[]{:S(2)}, u32[]{:S(2)}) collective-permute-start(bf16[2,128,512]{2,1,0:T(8,128)(2,1)S(1)} %fusion.3), channel_id=1, source_target_pairs={{0,8},{8,0},{4,12},{12,4},{16,24},{24,16},{20,28},{28,20},{1,9},{9... | collective-permute-start | bytes 786440 | tf_op jit(solution)/shard_map/ppermute | solution.py:22
  24.4 1.9 %collective-permute-start.19 = (bf16[2,128,512]{2,1,0:T(8,128)(2,1)S(1)}, bf16[2,128,512]{2,1,0:T(8,128)(2,1)S(1)}, u32[]{:S(2)}, u32[]{:S(2)}) collective-permute-start(bf16[2,128,512]{2,1,0:T(8,128)(2,1)S(1)} %fusion), channel_id=1, source_target_pairs={{0,8},{8,0},{4,12},{12,4},{16,24},{24,16},{20,28},{28,20},{1,9},{9... | collective-permute-start | bytes 786440 | tf_op jit(solution)/shard_map/ppermute | solution.py:22
  28.5 6.3 %collective-permute-done.6.refs_2_ = bf16[2,128,512]{2,1,0:T(8,128)(2,1)S(1)} collective-permute-done((bf16[2,128,512]{2,1,0:T(8,128)(2,1)S(1)}, bf16[2,128,512]{2,1,0:T(8,128)(2,1)S(1)}, u32[]{:S(2)}, u32[]{:S(2)}) %collective-permute-start.6) | collective-permute-done | bytes 262176 | tf_op jit(solution)/shard_map/ppermute | solution.py:22
  37.2 1.8 %collective-permute-start.1 = (bf16[2,256,512]{2,1,0:T(8,128)(2,1)S(1)}, bf16[2,256,512]{2,1,0:T(8,128)(2,1)S(1)}, u32[]{:S(2)}, u32[]{:S(2)}) collective-permute-start(bf16[2,256,512]{2,1,0:T(8,128)(2,1)S(1)} %copy-done.15), channel_id=1, source_target_pairs={{0,4},{4,0},{8,12},{12,8},{16,20},{20,16},{24,28},{28,24},{1,5},{5... | collective-permute-start | bytes 1572872 | tf_op jit(solution)/shard_map/ppermute | solution.py:22
  39.0 5.3 %collective-permute-done.12.refs_2_ = bf16[2,128,512]{2,1,0:T(8,128)(2,1)S(1)} collective-permute-done((bf16[2,128,512]{2,1,0:T(8,128)(2,1)S(1)}, bf16[2,128,512]{2,1,0:T(8,128)(2,1)S(1)}, u32[]{:S(2)}, u32[]{:S(2)}) %collective-permute-start.12) | collective-permute-done | bytes 262176 | tf_op jit(solution)/shard_map/ppermute | solution.py:22
  44.3 1.4 collective-permute-start.5
  45.7 1.3 collective-permute-start.8
  48.0 1.3 collective-permute-start.4
  49.6 4.4 %collective-permute-done.8 = bf16[2,128,512]{2,1,0:T(8,128)(2,1)S(1)} collective-permute-done((bf16[2,128,512]{2,1,0:T(8,128)(2,1)S(1)}, bf16[2,128,512]{2,1,0:T(8,128)(2,1)S(1)}, u32[]{:S(2)}, u32[]{:S(2)}) %collective-permute-start.8) | collective-permute-done | bytes 262176 | tf_op jit(solution)/shard_map/ppermute | solution.py:162
  56.1 4.1 %collective-permute-done.4 = bf16[2,128,512]{2,1,0:T(8,128)(2,1)S(1)} collective-permute-done((bf16[2,128,512]{2,1,0:T(8,128)(2,1)S(1)}, bf16[2,128,512]{2,1,0:T(8,128)(2,1)S(1)}, u32[]{:S(2)}, u32[]{:S(2)}) %collective-permute-start.4) | collective-permute-done | bytes 262176 | tf_op jit(solution)/shard_map/ppermute | solution.py:162
  64.9 7.1 %shard_map.76 = (bf16[256,512]{1,0:T(8,128)(2,1)}, bf16[256,512]{1,0:T(8,128)(2,1)}, f32[2,256,512]{2,1,0:T(8,128)}, f32[2,256,512]{2,1,0:T(8,128)}, f32[2,128,5...) custom-call(f32[1,768]{1,0:T(1,128)} %constant.104.clone.1.bias_ref, bf16[256,2048]{1,0:T(8,128)(2,1)} %q_ref.7, ...), custom_call_target="tpu_custom_call" | custom-call | flops 1207959552 | bytes 5767168 | tf_op jit(solution)/shard_map/pallas_call | solution.py:72
  72.1 8.2 %collective-permute-start.15 = (bf16[2,128,512]{2,1,0:T(8,128)(2,1)}, bf16[2,128,512]{2,1,0:T(8,128)(2,1)S(1)}, u32[]{:S(2)}, u32[]{:S(2)}) collective-permute-start(bf16[2,128,512]{2,1,0:T(8,128)(2,1)} %get-tuple-element.45), channel_id=1, source_target_pairs={{0,8},{4,12},{24,16},{28,20},{1,9},{5,13},{25,17},{29,21},{2,10},{... | collective-permute-start | bytes 786440 | tf_op jit(solution)/shard_map/ppermute | solution.py:188
  80.3 7.1 %shard_map.75 = (bf16[256,512]{1,0:T(8,128)(2,1)}, bf16[256,512]{1,0:T(8,128)(2,1)}, f32[2,256,512]{2,1,0:T(8,128)}, f32[2,256,512]{2,1,0:T(8,128)}, f32[2,128,5...) custom-call(f32[1,768]{1,0:T(1,128)} %constant.104.clone.1.bias_ref, bf16[256,2048]{1,0:T(8,128)(2,1)} %q_ref.7, ...), custom_call_target="tpu_custom_call" | custom-call | flops 1207959552 | bytes 5767168 | tf_op jit(solution)/shard_map/pallas_call | solution.py:72
  87.4 1.4 collective-permute-start.9
  91.2 1.8 %collective-permute-done.9 = bf16[2,128,512]{2,1,0:T(8,128)(2,1)S(1)} collective-permute-done((bf16[2,128,512]{2,1,0:T(8,128)(2,1)}, bf16[2,128,512]{2,1,0:T(8,128)(2,1)S(1)}, u32[]{:S(2)}, u32[]{:S(2)}) %collective-permute-start.9) | collective-permute-done | bytes 262176 | tf_op jit(solution)/shard_map/ppermute | solution.py:188
  94.2 5.9 %collective-permute-start.23 = (bf16[2,128,512]{2,1,0:T(8,128)(2,1)S(1)}, bf16[2,128,512]{2,1,0:T(8,128)(2,1)S(1)}, u32[]{:S(2)}, u32[]{:S(2)}) collective-permute-start(bf16[2,128,512]{2,1,0:T(8,128)(2,1)S(1)} %add_convert_fusion.11), channel_id=1, source_target_pairs={{0,8},{8,0},{4,12},{12,4},{16,24},{24,16},{20,28},{28,20},{1,9},{9... | collective-permute-start | bytes 786440 | tf_op jit(solution)/shard_map/ppermute | solution.py:22
  100.6 3.6 %collective-permute-start.17 = (bf16[2,128,512]{2,1,0:T(8,128)(2,1)S(1)}, bf16[2,128,512]{2,1,0:T(8,128)(2,1)S(1)}, u32[]{:S(2)}, u32[]{:S(2)}) collective-permute-start(bf16[2,128,512]{2,1,0:T(8,128)(2,1)S(1)} %add_convert_fusion.13), channel_id=1, source_target_pairs={{0,8},{8,0},{4,12},{12,4},{16,24},{24,16},{20,28},{28,20},{1,9},{9... | collective-permute-start | bytes 786440 | tf_op jit(solution)/shard_map/ppermute | solution.py:22
  105.0 7.2 %shard_map.77 = (bf16[256,512]{1,0:T(8,128)(2,1)}, bf16[256,512]{1,0:T(8,128)(2,1)}, f32[2,256,512]{2,1,0:T(8,128)}, f32[2,256,512]{2,1,0:T(8,128)}, f32[2,128,5...) custom-call(f32[1,768]{1,0:T(1,128)} %constant.104.clone.1.bias_ref, bf16[256,2048]{1,0:T(8,128)(2,1)} %q_ref.7, ...), custom_call_target="tpu_custom_call" | custom-call | flops 1207959552 | bytes 5767168 | tf_op jit(solution)/shard_map/pallas_call | solution.py:72
  112.2 2.8 %collective-permute-start.25 = (bf16[2,128,512]{2,1,0:T(8,128)(2,1)}, bf16[2,128,512]{2,1,0:T(8,128)(2,1)}, u32[]{:S(2)}, u32[]{:S(2)}) collective-permute-start(bf16[2,128,512]{2,1,0:T(8,128)(2,1)} %get-tuple-element.59), channel_id=1, source_target_pairs={{0,8},{4,12},{24,16},{28,20},{1,9},{5,13},{25,17},{29,21},{2,10},{... | collective-permute-start | bytes 786440 | tf_op jit(solution)/shard_map/ppermute | solution.py:188
  116.0 2.3 %collective-permute-start.24 = (bf16[2,256,512]{2,1,0:T(8,128)(2,1)S(1)}, bf16[2,256,512]{2,1,0:T(8,128)(2,1)S(1)}, u32[]{:S(2)}, u32[]{:S(2)}) collective-permute-start(bf16[2,256,512]{2,1,0:T(8,128)(2,1)S(1)} %add_convert_fusion.4), channel_id=1, source_target_pairs={{0,4},{4,0},{8,12},{12,8},{16,20},{20,16},{24,28},{28,24},{1,5},{5... | collective-permute-start | bytes 1572872 | tf_op jit(solution)/shard_map/ppermute | solution.py:22
  120.2 7.1 %shard_map.78 = (bf16[256,512]{1,0:T(8,128)(2,1)}, bf16[256,512]{1,0:T(8,128)(2,1)}, f32[2,256,512]{2,1,0:T(8,128)}, f32[2,256,512]{2,1,0:T(8,128)}, f32[2,128,5...) custom-call(f32[1,768]{1,0:T(1,128)} %constant.104.clone.1.bias_ref, bf16[256,2048]{1,0:T(8,128)(2,1)} %q_ref.7, ...), custom_call_target="tpu_custom_call" | custom-call | flops 1207959552 | bytes 5767168 | tf_op jit(solution)/shard_map/pallas_call | solution.py:72
  127.4 1.3 collective-permute-start.29
  128.7 1.3 convert_element_type.225
  130.0 1.7 %collective-permute-start.33 = (bf16[2,256,512]{2,1,0:T(8,128)(2,1)S(1)}, bf16[2,256,512]{2,1,0:T(8,128)(2,1)S(1)}, u32[]{:S(2)}, u32[]{:S(2)}) collective-permute-start(bf16[2,256,512]{2,1,0:T(8,128)(2,1)S(1)} %convert_element_type.225), channel_id=1, source_target_pairs={{0,4},{4,0},{8,12},{12,8},{16,20},{20,16},{24,28},{28,24},{1,5},{5... | collective-permute-start | bytes 1572872 | tf_op jit(solution)/shard_map/ppermute | solution.py:22
  137.9 5.4 %collective-permute-start.27 = (bf16[2,128,512]{2,1,0:T(8,128)(2,1)S(1)}, bf16[2,128,512]{2,1,0:T(8,128)(2,1)S(1)}, u32[]{:S(2)}, u32[]{:S(2)}) collective-permute-start(bf16[2,128,512]{2,1,0:T(8,128)(2,1)S(1)} %add_convert_fusion.9), channel_id=1, source_target_pairs={{0,8},{8,0},{4,12},{12,4},{16,24},{24,16},{20,28},{28,20},{1,9},{9... | collective-permute-start | bytes 786440 | tf_op jit(solution)/shard_map/ppermute | solution.py:22
  143.8 3.7 %collective-permute-start.31 = (bf16[2,128,512]{2,1,0:T(8,128)(2,1)S(1)}, bf16[2,128,512]{2,1,0:T(8,128)(2,1)S(1)}, u32[]{:S(2)}, u32[]{:S(2)}) collective-permute-start(bf16[2,128,512]{2,1,0:T(8,128)(2,1)S(1)} %add_convert_fusion.7), channel_id=1, source_target_pairs={{0,8},{8,0},{4,12},{12,4},{16,24},{24,16},{20,28},{28,20},{1,9},{9... | collective-permute-start | bytes 786440 | tf_op jit(solution)/shard_map/ppermute | solution.py:22
  147.5 2.1 %collective-permute-done.27 = bf16[2,128,512]{2,1,0:T(8,128)(2,1)S(1)} collective-permute-done((bf16[2,128,512]{2,1,0:T(8,128)(2,1)S(1)}, bf16[2,128,512]{2,1,0:T(8,128)(2,1)S(1)}, u32[]{:S(2)}, u32[]{:S(2)}) %collective-permute-start.27) | collective-permute-done | bytes 262176 | tf_op jit(solution)/shard_map/ppermute | solution.py:22
  156.1 5.8 %collective-permute-done.32 = bf16[2,64,512]{2,1,0:T(8,128)(2,1)S(1)} collective-permute-done((bf16[2,64,512]{2,1,0:T(8,128)(2,1)S(1)}, bf16[2,64,512]{2,1,0:T(8,128)(2,1)S(1)}, u32[]{:S(2)}, u32[]{:S(2)}) %collective-permute-start.32) | collective-permute-done | bytes 131104 | tf_op jit(solution)/shard_map/ppermute | solution.py:22
  (200 shorter events, 46.7 us)
Async XLA Ops:
  3.5 15.2 %collective-permute-start = (bf16[2,64,2048]{2,1,0:T(8,128)(2,1)}, bf16[2,64,2048]{2,1,0:T(8,128)(2,1)}, u32[]{:S(2)}, u32[]{:S(2)}) collective-permute-start(bf16[2,64,2048]{2,1,0:T(8,128)(2,1)} %fusion.17), channel_id=1, source_target_pairs={{0,4},{4,0},{8,12},{12,8},{16,20},{20,16},{24,28},{28,24},{1,5},{5... | collective-permute-start | bytes 1572872 | tf_op jit(solution)/shard_map/ppermute | solution.py:22
  19.9 16.1 %collective-permute-start.2 = (bf16[2,128,512]{2,1,0:T(8,128)(2,1)S(1)}, bf16[2,128,512]{2,1,0:T(8,128)(2,1)S(1)}, u32[]{:S(2)}, u32[]{:S(2)}) collective-permute-start(bf16[2,128,512]{2,1,0:T(8,128)(2,1)S(1)} %fusion.3), channel_id=1, source_target_pairs={{0,8},{8,0},{4,12},{12,4},{16,24},{24,16},{20,28},{28,20},{1,9},{9... | collective-permute-start | bytes 786440 | tf_op jit(solution)/shard_map/ppermute | solution.py:22
  22.9 11.9 %collective-permute-start.6 = (bf16[2,128,512]{2,1,0:T(8,128)(2,1)S(1)}, bf16[2,128,512]{2,1,0:T(8,128)(2,1)S(1)}, u32[]{:S(2)}, u32[]{:S(2)}) collective-permute-start(bf16[2,128,512]{2,1,0:T(8,128)(2,1)S(1)} %fusion.2), channel_id=1, source_target_pairs={{0,8},{8,0},{4,12},{12,4},{16,24},{24,16},{20,28},{28,20},{1,9},{9... | collective-permute-start | bytes 786440 | tf_op jit(solution)/shard_map/ppermute | solution.py:22
  24.4 22.9 %collective-permute-start.19 = (bf16[2,128,512]{2,1,0:T(8,128)(2,1)S(1)}, bf16[2,128,512]{2,1,0:T(8,128)(2,1)S(1)}, u32[]{:S(2)}, u32[]{:S(2)}) collective-permute-start(bf16[2,128,512]{2,1,0:T(8,128)(2,1)S(1)} %fusion), channel_id=1, source_target_pairs={{0,8},{8,0},{4,12},{12,4},{16,24},{24,16},{20,28},{28,20},{1,9},{9... | collective-permute-start | bytes 786440 | tf_op jit(solution)/shard_map/ppermute | solution.py:22
  28.2 16.0 %collective-permute-start.12 = (bf16[2,128,512]{2,1,0:T(8,128)(2,1)S(1)}, bf16[2,128,512]{2,1,0:T(8,128)(2,1)S(1)}, u32[]{:S(2)}, u32[]{:S(2)}) collective-permute-start(bf16[2,128,512]{2,1,0:T(8,128)(2,1)S(1)} %fusion.1), channel_id=1, source_target_pairs={{0,8},{8,0},{4,12},{12,4},{16,24},{24,16},{20,28},{28,20},{1,9},{9... | collective-permute-start | bytes 786440 | tf_op jit(solution)/shard_map/ppermute | solution.py:22
  35.1 10.6 %collective-permute-start.7 = (bf16[2,128,512]{2,1,0:T(8,128)(2,1)S(1)}, bf16[2,128,512]{2,1,0:T(8,128)(2,1)S(1)}, u32[]{:S(2)}, u32[]{:S(2)}) collective-permute-start(bf16[2,128,512]{2,1,0:T(8,128)(2,1)S(1)} %fusion.14), channel_id=1, source_target_pairs={{8,16},{12,20},{16,8},{20,12},{9,17},{13,21},{17,9},{21,13},{10,18... | collective-permute-start | bytes 786440 | tf_op jit(solution)/shard_map/ppermute | solution.py:161
  36.2 11.8 %collective-permute-start.3 = (bf16[2,128,512]{2,1,0:T(8,128)(2,1)S(1)}, bf16[2,128,512]{2,1,0:T(8,128)(2,1)S(1)}, u32[]{:S(2)}, u32[]{:S(2)}) collective-permute-start(bf16[2,128,512]{2,1,0:T(8,128)(2,1)S(1)} %fusion.15), channel_id=1, source_target_pairs={{8,16},{12,20},{16,8},{20,12},{9,17},{13,21},{17,9},{21,13},{10,18... | collective-permute-start | bytes 786440 | tf_op jit(solution)/shard_map/ppermute | solution.py:161
  37.2 34.9 %collective-permute-start.1 = (bf16[2,256,512]{2,1,0:T(8,128)(2,1)S(1)}, bf16[2,256,512]{2,1,0:T(8,128)(2,1)S(1)}, u32[]{:S(2)}, u32[]{:S(2)}) collective-permute-start(bf16[2,256,512]{2,1,0:T(8,128)(2,1)S(1)} %copy-done.15), channel_id=1, source_target_pairs={{0,4},{4,0},{8,12},{12,8},{16,20},{20,16},{24,28},{28,24},{1,5},{5... | collective-permute-start | bytes 1572872 | tf_op jit(solution)/shard_map/ppermute | solution.py:22
  44.3 18.6 %collective-permute-start.5 = (bf16[2,256,512]{2,1,0:T(8,128)(2,1)S(1)}, bf16[2,256,512]{2,1,0:T(8,128)(2,1)S(1)}, u32[]{:S(2)}, u32[]{:S(2)}) collective-permute-start(bf16[2,256,512]{2,1,0:T(8,128)(2,1)S(1)} %copy-done.16), channel_id=1, source_target_pairs={{0,4},{4,0},{8,12},{12,8},{16,20},{20,16},{24,28},{28,24},{1,5},{5... | collective-permute-start | bytes 1572872 | tf_op jit(solution)/shard_map/ppermute | solution.py:22
  45.7 8.3 %collective-permute-start.8 = (bf16[2,128,512]{2,1,0:T(8,128)(2,1)S(1)}, bf16[2,128,512]{2,1,0:T(8,128)(2,1)S(1)}, u32[]{:S(2)}, u32[]{:S(2)}) collective-permute-start(bf16[2,128,512]{2,1,0:T(8,128)(2,1)S(1)} %collective-permute-done.7), channel_id=1, source_target_pairs={{8,0},{12,4},{16,24},{20,28},{9,1},{13,5},{17,25},{21,29},{10,2},{... | collective-permute-start | bytes 786440 | tf_op jit(solution)/shard_map/ppermute | solution.py:162
  47.3 8.1 %collective-permute-start.13 = (bf16[2,128,512]{2,1,0:T(8,128)(2,1)S(1)}, bf16[2,128,512]{2,1,0:T(8,128)(2,1)S(1)}, u32[]{:S(2)}, u32[]{:S(2)}) collective-permute-start(bf16[2,128,512]{2,1,0:T(8,128)(2,1)S(1)} %fusion.13), channel_id=1, source_target_pairs={{8,16},{12,20},{16,8},{20,12},{9,17},{13,21},{17,9},{21,13},{10,18... | collective-permute-start | bytes 786440 | tf_op jit(solution)/shard_map/ppermute | solution.py:161
  48.0 12.2 %collective-permute-start.4 = (bf16[2,128,512]{2,1,0:T(8,128)(2,1)S(1)}, bf16[2,128,512]{2,1,0:T(8,128)(2,1)S(1)}, u32[]{:S(2)}, u32[]{:S(2)}) collective-permute-start(bf16[2,128,512]{2,1,0:T(8,128)(2,1)S(1)} %collective-permute-done.3), channel_id=1, source_target_pairs={{8,0},{12,4},{16,24},{20,28},{9,1},{13,5},{17,25},{21,29},{10,2},{... | collective-permute-start | bytes 786440 | tf_op jit(solution)/shard_map/ppermute | solution.py:162
  53.9 8.3 %collective-permute-start.20 = (bf16[2,128,512]{2,1,0:T(8,128)(2,1)S(1)}, bf16[2,128,512]{2,1,0:T(8,128)(2,1)S(1)}, u32[]{:S(2)}, u32[]{:S(2)}) collective-permute-start(bf16[2,128,512]{2,1,0:T(8,128)(2,1)S(1)} %fusion.12), channel_id=1, source_target_pairs={{8,16},{12,20},{16,8},{20,12},{9,17},{13,21},{17,9},{21,13},{10,18... | collective-permute-start | bytes 786440 | tf_op jit(solution)/shard_map/ppermute | solution.py:161
  55.4 64.8 %collective-permute-start.18 = (bf16[2,256,512]{2,1,0:T(8,128)(2,1)}, bf16[2,256,512]{2,1,0:T(8,128)(2,1)}, u32[]{:S(2)}, u32[]{:S(2)}) collective-permute-start(bf16[2,256,512]{2,1,0:T(8,128)(2,1)} %pad_maximum_fusion.6.refs_0_), channel_id=1, source_target_pairs={{0,4},{4,0},{8,12},{12,8},{16,20},{20,16},{24,28},{28,24},{1,5},{5... | collective-permute-start | bytes 1572872 | tf_op jit(solution)/shard_map/ppermute | solution.py:22
  60.2 27.2 %collective-permute-start.14 = (bf16[2,128,512]{2,1,0:T(8,128)(2,1)S(1)}, bf16[2,128,512]{2,1,0:T(8,128)(2,1)S(1)}, u32[]{:S(2)}, u32[]{:S(2)}) collective-permute-start(bf16[2,128,512]{2,1,0:T(8,128)(2,1)S(1)} %collective-permute-done.13), channel_id=1, source_target_pairs={{8,0},{12,4},{16,24},{20,28},{9,1},{13,5},{17,25},{21,29},{10,2},{... | collective-permute-start | bytes 786440 | tf_op jit(solution)/shard_map/ppermute | solution.py:162
  62.3 42.0 %collective-permute-start.11 = (bf16[2,256,512]{2,1,0:T(8,128)(2,1)S(1)}, bf16[2,256,512]{2,1,0:T(8,128)(2,1)S(1)}, u32[]{:S(2)}, u32[]{:S(2)}) collective-permute-start(bf16[2,256,512]{2,1,0:T(8,128)(2,1)S(1)} %copy-done.14), channel_id=1, source_target_pairs={{0,4},{4,0},{8,12},{12,8},{16,20},{20,16},{24,28},{28,24},{1,5},{5... | collective-permute-start | bytes 1572872 | tf_op jit(solution)/shard_map/ppermute | solution.py:22
  63.6 26.8 %collective-permute-start.21 = (bf16[2,128,512]{2,1,0:T(8,128)(2,1)S(1)}, bf16[2,128,512]{2,1,0:T(8,128)(2,1)S(1)}, u32[]{:S(2)}, u32[]{:S(2)}) collective-permute-start(bf16[2,128,512]{2,1,0:T(8,128)(2,1)S(1)} %collective-permute-done.20), channel_id=1, source_target_pairs={{8,0},{12,4},{16,24},{20,28},{9,1},{13,5},{17,25},{21,29},{10,2},{... | collective-permute-start | bytes 786440 | tf_op jit(solution)/shard_map/ppermute | solution.py:162
  72.1 17.5 %collective-permute-start.15 = (bf16[2,128,512]{2,1,0:T(8,128)(2,1)}, bf16[2,128,512]{2,1,0:T(8,128)(2,1)S(1)}, u32[]{:S(2)}, u32[]{:S(2)}) collective-permute-start(bf16[2,128,512]{2,1,0:T(8,128)(2,1)} %get-tuple-element.45), channel_id=1, source_target_pairs={{0,8},{4,12},{24,16},{28,20},{1,9},{5,13},{25,17},{29,21},{2,10},{... | collective-permute-start | bytes 786440 | tf_op jit(solution)/shard_map/ppermute | solution.py:188
  87.4 5.6 %collective-permute-start.9 = (bf16[2,128,512]{2,1,0:T(8,128)(2,1)}, bf16[2,128,512]{2,1,0:T(8,128)(2,1)S(1)}, u32[]{:S(2)}, u32[]{:S(2)}) collective-permute-start(bf16[2,128,512]{2,1,0:T(8,128)(2,1)} %get-tuple-element.40), channel_id=1, source_target_pairs={{0,8},{4,12},{24,16},{28,20},{1,9},{5,13},{25,17},{29,21},{2,10},{... | collective-permute-start | bytes 786440 | tf_op jit(solution)/shard_map/ppermute | solution.py:188
  93.1 7.1 %collective-permute-start.10 = (bf16[2,128,512]{2,1,0:T(8,128)(2,1)S(1)}, bf16[2,128,512]{2,1,0:T(8,128)(2,1)S(1)}, u32[]{:S(2)}, u32[]{:S(2)}) collective-permute-start(bf16[2,128,512]{2,1,0:T(8,128)(2,1)S(1)} %add_convert_fusion.14), channel_id=1, source_target_pairs={{8,16},{12,20},{16,8},{20,12},{9,17},{13,21},{17,9},{21,13},{10,18... | collective-permute-start | bytes 786440 | tf_op jit(solution)/shard_map/ppermute | solution.py:190
  94.2 20.8 %collective-permute-start.23 = (bf16[2,128,512]{2,1,0:T(8,128)(2,1)S(1)}, bf16[2,128,512]{2,1,0:T(8,128)(2,1)S(1)}, u32[]{:S(2)}, u32[]{:S(2)}) collective-permute-start(bf16[2,128,512]{2,1,0:T(8,128)(2,1)S(1)} %add_convert_fusion.11), channel_id=1, source_target_pairs={{0,8},{8,0},{4,12},{12,4},{16,24},{24,16},{20,28},{28,20},{1,9},{9... | collective-permute-start | bytes 786440 | tf_op jit(solution)/shard_map/ppermute | solution.py:22
  100.6 17.8 %collective-permute-start.17 = (bf16[2,128,512]{2,1,0:T(8,128)(2,1)S(1)}, bf16[2,128,512]{2,1,0:T(8,128)(2,1)S(1)}, u32[]{:S(2)}, u32[]{:S(2)}) collective-permute-start(bf16[2,128,512]{2,1,0:T(8,128)(2,1)S(1)} %add_convert_fusion.13), channel_id=1, source_target_pairs={{0,8},{8,0},{4,12},{12,4},{16,24},{24,16},{20,28},{28,20},{1,9},{9... | collective-permute-start | bytes 786440 | tf_op jit(solution)/shard_map/ppermute | solution.py:22
  112.2 19.9 %collective-permute-start.25 = (bf16[2,128,512]{2,1,0:T(8,128)(2,1)}, bf16[2,128,512]{2,1,0:T(8,128)(2,1)}, u32[]{:S(2)}, u32[]{:S(2)}) collective-permute-start(bf16[2,128,512]{2,1,0:T(8,128)(2,1)} %get-tuple-element.59), channel_id=1, source_target_pairs={{0,8},{4,12},{24,16},{28,20},{1,9},{5,13},{25,17},{29,21},{2,10},{... | collective-permute-start | bytes 786440 | tf_op jit(solution)/shard_map/ppermute | solution.py:188
  116.0 36.0 %collective-permute-start.24 = (bf16[2,256,512]{2,1,0:T(8,128)(2,1)S(1)}, bf16[2,256,512]{2,1,0:T(8,128)(2,1)S(1)}, u32[]{:S(2)}, u32[]{:S(2)}) collective-permute-start(bf16[2,256,512]{2,1,0:T(8,128)(2,1)S(1)} %add_convert_fusion.4), channel_id=1, source_target_pairs={{0,4},{4,0},{8,12},{12,8},{16,20},{20,16},{24,28},{28,24},{1,5},{5... | collective-permute-start | bytes 1572872 | tf_op jit(solution)/shard_map/ppermute | solution.py:22
  119.4 33.1 %collective-permute-start.22 = (bf16[2,256,512]{2,1,0:T(8,128)(2,1)S(1)}, bf16[2,256,512]{2,1,0:T(8,128)(2,1)S(1)}, u32[]{:S(2)}, u32[]{:S(2)}) collective-permute-start(bf16[2,256,512]{2,1,0:T(8,128)(2,1)S(1)} %add_convert_fusion.6), channel_id=1, source_target_pairs={{0,4},{4,0},{8,12},{12,8},{16,20},{20,16},{24,28},{28,24},{1,5},{5... | collective-permute-start | bytes 1572872 | tf_op jit(solution)/shard_map/ppermute | solution.py:22
  127.4 9.2 %collective-permute-start.29 = (bf16[2,128,512]{2,1,0:T(8,128)(2,1)}, bf16[2,128,512]{2,1,0:T(8,128)(2,1)S(1)}, u32[]{:S(2)}, u32[]{:S(2)}) collective-permute-start(bf16[2,128,512]{2,1,0:T(8,128)(2,1)} %get-tuple-element.63), channel_id=1, source_target_pairs={{0,8},{4,12},{24,16},{28,20},{1,9},{5,13},{25,17},{29,21},{2,10},{... | collective-permute-start | bytes 786440 | tf_op jit(solution)/shard_map/ppermute | solution.py:188
  130.0 32.2 %collective-permute-start.33 = (bf16[2,256,512]{2,1,0:T(8,128)(2,1)S(1)}, bf16[2,256,512]{2,1,0:T(8,128)(2,1)S(1)}, u32[]{:S(2)}, u32[]{:S(2)}) collective-permute-start(bf16[2,256,512]{2,1,0:T(8,128)(2,1)S(1)} %convert_element_type.225), channel_id=1, source_target_pairs={{0,4},{4,0},{8,12},{12,8},{16,20},{20,16},{24,28},{28,24},{1,5},{5... | collective-permute-start | bytes 1572872 | tf_op jit(solution)/shard_map/ppermute | solution.py:22
  136.6 6.7 %collective-permute-start.30 = (bf16[2,128,512]{2,1,0:T(8,128)(2,1)S(1)}, bf16[2,128,512]{2,1,0:T(8,128)(2,1)S(1)}, u32[]{:S(2)}, u32[]{:S(2)}) collective-permute-start(bf16[2,128,512]{2,1,0:T(8,128)(2,1)S(1)} %add_convert_fusion.8), channel_id=1, source_target_pairs={{8,16},{12,20},{16,8},{20,12},{9,17},{13,21},{17,9},{21,13},{10,18... | collective-permute-start | bytes 786440 | tf_op jit(solution)/shard_map/ppermute | solution.py:190
  137.9 11.7 %collective-permute-start.27 = (bf16[2,128,512]{2,1,0:T(8,128)(2,1)S(1)}, bf16[2,128,512]{2,1,0:T(8,128)(2,1)S(1)}, u32[]{:S(2)}, u32[]{:S(2)}) collective-permute-start(bf16[2,128,512]{2,1,0:T(8,128)(2,1)S(1)} %add_convert_fusion.9), channel_id=1, source_target_pairs={{0,8},{8,0},{4,12},{12,4},{16,24},{24,16},{20,28},{28,20},{1,9},{9... | collective-permute-start | bytes 786440 | tf_op jit(solution)/shard_map/ppermute | solution.py:22
  143.8 10.2 %collective-permute-start.31 = (bf16[2,128,512]{2,1,0:T(8,128)(2,1)S(1)}, bf16[2,128,512]{2,1,0:T(8,128)(2,1)S(1)}, u32[]{:S(2)}, u32[]{:S(2)}) collective-permute-start(bf16[2,128,512]{2,1,0:T(8,128)(2,1)S(1)} %add_convert_fusion.7), channel_id=1, source_target_pairs={{0,8},{8,0},{4,12},{12,4},{16,24},{24,16},{20,28},{28,20},{1,9},{9... | collective-permute-start | bytes 786440 | tf_op jit(solution)/shard_map/ppermute | solution.py:22
  150.6 12.1 %collective-permute-start.28 = (bf16[2,256,512]{2,1,0:T(8,128)(2,1)S(1)}, bf16[2,256,512]{2,1,0:T(8,128)(2,1)S(1)}, u32[]{:S(2)}, u32[]{:S(2)}) collective-permute-start(bf16[2,256,512]{2,1,0:T(8,128)(2,1)S(1)} %add_convert_fusion.2), channel_id=1, source_target_pairs={{0,4},{4,0},{8,12},{12,8},{16,20},{20,16},{24,28},{28,24},{1,5},{5... | collective-permute-start | bytes 1572872 | tf_op jit(solution)/shard_map/ppermute | solution.py:22
  154.6 7.3 %collective-permute-start.32 = (bf16[2,64,512]{2,1,0:T(8,128)(2,1)S(1)}, bf16[2,64,512]{2,1,0:T(8,128)(2,1)S(1)}, u32[]{:S(2)}, u32[]{:S(2)}) collective-permute-start(bf16[2,64,512]{2,1,0:T(8,128)(2,1)S(1)} %fusion.16), channel_id=1, source_target_pairs={{0,4},{4,0},{8,12},{12,8},{16,20},{20,16},{24,28},{28,24},{1,5},{5... | collective-permute-start | bytes 393224 | tf_op jit(solution)/shard_map/ppermute | solution.py:22
  (42 other events, 176.8 us)
